TPU v7x, 32 devices: a whole 2x2x4 slice. The times are simulated.
32 devices in a mesh: groups: 2 (over y), cand: 4 (over z), query: 2 (over x), mp: 2 (over core).
Axes of the slice: x: 2, y: 2, z: 4, core: 2. Of those that a mesh axis runs over, the one named last changes fastest.
Arguments:
- tokens: bfloat16 [4, 4, 256, 1024], P(('groups', 'query'), 'cand'), parts along dimension 0, may hold values from -6 to 6
- lengths: int32 [4, 4], P(('groups', 'query'), 'cand'), parts along dimension 0, may hold values from 64 to 256, as said below
- teacher: float32 [4, 4], P(('groups', 'query'), 'cand'), parts along dimension 0, may hold values from -15 to 291, as said below
- w_first: bfloat16 [3, 1024, 512], P(None, None, 'mp'), may hold values from -0.1875 to 0.1875
- w_out_first: bfloat16 [512, 1024], P('mp'), may hold values from -0.25 to 0.25
- gain_first: float32 [1024], replicated, may hold values from 0.5 to 1.5
- w_last: bfloat16 [3, 1024, 512], P(None, None, 'mp'), may hold values from -0.1875 to 0.1875
- w_out_last: bfloat16 [512, 1024], P('mp'), may hold values from -0.25 to 0.25
- gain_last: float32 [1024], replicated, may hold values from 0.5 to 1.5
- w_score: float32 [1024], replicated, may hold values from -0.5 to 0.5
Outputs:
- grad_first: float32 [2048, 3, 512], P(('groups', 'cand'), None, 'mp'), parts along dimension 0
There are 2 independent parts, one for each index of `groups`. A program takes and returns all parts, laid end to end along the dimension named above; an argument that names none is the same for every part. Nothing has to cross between parts.
Inputs may be any that keep to these rules, and one draw needn't show every extreme that they name: `lengths`: valid tokens of each pair; in every list some pair fills all 256 positions. Within each list the teacher's scores span at most 30.
All inputs are finite; a program needn't handle non-finite values.
Results may differ from a plain program's by a relative error of at most 0.012.
Values may be sent and summed in bfloat16 or wider, within the bound.
No kernel may reach another device: no remote copies, remote signals or barrier semaphores. Data moves between devices by JAX's collectives and lax.ppermute only.
A program may use at most 64 MiB of HBM per device.

v0:
```python
import jax
import jax.numpy as jnp
from jax import lax
from jax.sharding import PartitionSpec as P

HEAD_DIM = 64


EPSILON = 1e-05
LOSS_SCALE = 1024.0
NEGATIVE = -1e30


def mixed(pattern, former, latter):
    return jnp.einsum(pattern, former, latter, preferred_element_type=jnp.float32)


def norm_forward(matrix, scales):
    center = matrix - jnp.mean(matrix, -1, keepdims=True)
    inverse = lax.rsqrt(jnp.mean(center * center, -1, keepdims=True) + EPSILON)
    normed = center * inverse
    return (normed * scales, normed, inverse)


def norm_backward(incoming, normed, inverse, scales):
    scaled = incoming * scales
    return inverse * (
        scaled
        - jnp.mean(scaled, -1, keepdims=True)
        - normed * jnp.mean(scaled * normed, -1, keepdims=True)
    )


def split_softmax(own_scores, cross_scores, first_mask):
    own_peak = jnp.max(own_scores, -1)
    row_peak = jnp.maximum(own_peak[..., 0], jnp.max(cross_scores, -1))
    peak = jnp.where(first_mask, row_peak[..., None], own_peak)
    own_exp = jnp.exp(own_scores - peak[..., None])
    cross_exp = jnp.exp(cross_scores - row_peak[..., None])
    own_totals = jnp.sum(own_exp, -1)
    row_totals = own_totals[..., 0] + jnp.sum(cross_exp, -1)
    totals = jnp.where(first_mask, row_totals[..., None], own_totals)
    return (own_exp / totals[..., None], cross_exp / row_totals[..., None])


def row_softmax(own_scores, cross_scores):
    peak = jnp.maximum(jnp.max(own_scores, -1), jnp.max(cross_scores, -1))[..., None]
    own_exp = jnp.exp(own_scores - peak)
    cross_exp = jnp.exp(cross_scores - peak)
    totals = (jnp.sum(own_exp, -1) + jnp.sum(cross_exp, -1))[..., None]
    return (own_exp / totals, cross_exp / totals)


def local(
    tokens,
    lengths,
    teacher,
    w_first,
    w_out_first,
    gain_first,
    w_last,
    w_out_last,
    gain_last,
    w_score,
):
    lists, local_cands, seq_len, model_width = tokens.shape
    local_width = w_first.shape[2]
    local_heads = local_width // HEAD_DIM
    cand_count = local_cands * lax.axis_size("cand")
    query_count = lists * lax.axis_size("query")
    score_scale = HEAD_DIM ** (-0.5)
    positions = jnp.arange(seq_len)
    first_mask = positions == 0
    own_valid = positions[None, None, :] < lengths[:, :, None]
    local_ids = lax.axis_index("cand") * local_cands + jnp.arange(local_cands)
    cross_valid = local_ids[:, None] != jnp.arange(cand_count)[None, :]
    head_shape = (lists, local_cands, seq_len, local_heads, HEAD_DIM)
    cls_shape = (lists, cand_count, local_heads, HEAD_DIM)
    projected = mixed("qcsd,kdf->kqcsf", tokens, w_first).astype(jnp.bfloat16)
    gathered_keys, gathered_vals = (
        lax.all_gather(projected[1][:, :, 0], "cand", axis=1, tiled=True),
        lax.all_gather(projected[2][:, :, 0], "cand", axis=1, tiled=True),
    )
    first_query = projected[0].reshape(head_shape)
    first_keys = projected[1].reshape(head_shape)
    first_vals = projected[2].reshape(head_shape)
    cls_keys = gathered_keys.reshape(cls_shape)
    cls_vals = gathered_vals.reshape(cls_shape)
    own_scores = mixed("qcshe,qcthe->qchst", first_query, first_keys) * score_scale
    own_scores = jnp.where(own_valid[:, :, None, None, :], own_scores, NEGATIVE)
    cross_scores = mixed("qche,qdhe->qchd", first_query[:, :, 0], cls_keys) * score_scale
    cross_scores = jnp.where(cross_valid[None, :, None, :], cross_scores, NEGATIVE)
    own_prob, cross_prob = split_softmax(own_scores, cross_scores, first_mask)
    own_weight = own_prob.astype(jnp.bfloat16)
    cross_weight = cross_prob.astype(jnp.bfloat16)
    attended = mixed("qchst,qcthe->qcshe", own_weight, first_vals)
    attended_cls = mixed("qchd,qdhe->qche", cross_weight, cls_vals)
    attended = jnp.where(
        first_mask[None, None, :, None, None], attended + attended_cls[:, :, None], attended
    )
    first_mixed = attended.reshape(lists, local_cands, seq_len, local_width).astype(jnp.bfloat16)
    partial_first = mixed("qcsf,fd->qcsd", first_mixed, w_out_first)
    residual_first = tokens.astype(jnp.float32) + lax.psum(partial_first, "mp")
    normed_first, unit_first, inverse_first = norm_forward(residual_first, gain_first)
    hidden = normed_first.astype(jnp.bfloat16)
    last_query = mixed("qcd,df->qcf", hidden[:, :, 0], w_last[0]).astype(jnp.bfloat16)
    last_kv = mixed("qcsd,kdf->kqcsf", hidden, w_last[1:]).astype(jnp.bfloat16)
    gathered_keys_last, gathered_vals_last = (
        lax.all_gather(last_kv[0][:, :, 0], "cand", axis=1, tiled=True),
        lax.all_gather(last_kv[1][:, :, 0], "cand", axis=1, tiled=True),
    )
    last_heads = last_query.reshape(lists, local_cands, local_heads, HEAD_DIM)
    last_keys = last_kv[0].reshape(head_shape)
    last_vals = last_kv[1].reshape(head_shape)
    cls_keys_last = gathered_keys_last.reshape(cls_shape)
    cls_vals_last = gathered_vals_last.reshape(cls_shape)
    own_last = mixed("qche,qcthe->qcht", last_heads, last_keys) * score_scale
    own_last = jnp.where(own_valid[:, :, None, :], own_last, NEGATIVE)
    cross_last = mixed("qche,qdhe->qchd", last_heads, cls_keys_last) * score_scale
    cross_last = jnp.where(cross_valid[None, :, None, :], cross_last, NEGATIVE)
    own_last_prob, cross_last_prob = row_softmax(own_last, cross_last)
    own_last_weight = own_last_prob.astype(jnp.bfloat16)
    cross_last_weight = cross_last_prob.astype(jnp.bfloat16)
    attended_last = mixed("qcht,qcthe->qche", own_last_weight, last_vals) + mixed(
        "qchd,qdhe->qche", cross_last_weight, cls_vals_last
    )
    last_mixed = attended_last.reshape(lists, local_cands, local_width).astype(jnp.bfloat16)
    partial_last = mixed("qcf,fd->qcd", last_mixed, w_out_last)
    residual_last = hidden[:, :, 0].astype(jnp.float32) + lax.psum(partial_last, "mp")
    normed_last, unit_last, inverse_last = norm_forward(residual_last, gain_last)
    scores = jnp.einsum("qcd,d->qc", normed_last, w_score, precision=lax.Precision.HIGHEST)
    score_exp = jnp.exp(scores)
    teacher_peak = lax.pmax(jnp.max(teacher, 1), "cand")
    teacher_exp = jnp.exp(teacher - teacher_peak[:, None])
    score_totals, teacher_totals = lax.psum(
        (jnp.sum(score_exp, 1), jnp.sum(teacher_exp, 1)), "cand"
    )
    student_prob = score_exp / score_totals[:, None]
    teacher_prob = teacher_exp / teacher_totals[:, None]
    score_grad = LOSS_SCALE * (student_prob - teacher_prob) / query_count
    grad_last = norm_backward(score_grad[..., None] * w_score, unit_last, inverse_last, gain_last)
    grad_last_low = grad_last.astype(jnp.bfloat16)
    grad_mixed_last = (
        mixed("qcd,fd->qcf", grad_last_low, w_out_last)
        .astype(jnp.bfloat16)
        .reshape(lists, local_cands, local_heads, HEAD_DIM)
    )
    own_dot = mixed("qche,qcthe->qcht", grad_mixed_last, last_vals)
    cross_dot = mixed("qche,qdhe->qchd", grad_mixed_last, cls_vals_last)
    centre = jnp.sum(own_last_prob * own_dot, -1, keepdims=True) + jnp.sum(
        cross_last_prob * cross_dot, -1, keepdims=True
    )
    own_slope = (own_last_prob * (own_dot - centre)).astype(jnp.bfloat16)
    cross_slope = (cross_last_prob * (cross_dot - centre)).astype(jnp.bfloat16)
    grad_query_last = (
        (
            (
                mixed("qcht,qcthe->qche", own_slope, last_keys)
                + mixed("qchd,qdhe->qche", cross_slope, cls_keys_last)
            )
            * score_scale
        )
        .astype(jnp.bfloat16)
        .reshape(lists, local_cands, local_width)
    )
    own_key_grad = (mixed("qcht,qche->qcthe", own_slope, last_heads) * score_scale).reshape(
        lists, local_cands, seq_len, local_width
    )
    own_val_grad = mixed("qcht,qche->qcthe", own_last_weight, grad_mixed_last).reshape(
        lists, local_cands, seq_len, local_width
    )
    cls_key_terms = (mixed("qchd,qche->qdhe", cross_slope, last_heads) * score_scale).reshape(
        lists, cand_count, local_width
    )
    cls_val_terms = mixed("qchd,qche->qdhe", cross_last_weight, grad_mixed_last).reshape(
        lists, cand_count, local_width
    )
    back_keys, back_vals = (
        lax.psum_scatter(cls_key_terms, "cand", scatter_dimension=1, tiled=True),
        lax.psum_scatter(cls_val_terms, "cand", scatter_dimension=1, tiled=True),
    )
    first_cols = first_mask[None, None, :, None]
    key_grad = jnp.where(first_cols, own_key_grad + back_keys[:, :, None], own_key_grad).astype(
        jnp.bfloat16
    )
    val_grad = jnp.where(first_cols, own_val_grad + back_vals[:, :, None], own_val_grad).astype(
        jnp.bfloat16
    )
    partial_term = mixed("qcsf,df->qcsd", key_grad, w_last[1]) + mixed(
        "qcsf,df->qcsd", val_grad, w_last[2]
    )
    query_term = mixed("qcf,df->qcd", grad_query_last, w_last[0])
    partial_term = jnp.where(first_cols, partial_term + query_term[:, :, None], partial_term)
    summed_term = lax.psum(partial_term, "mp")
    grad_hidden = jnp.where(first_cols, summed_term + grad_last[:, :, None], summed_term)
    grad_first = norm_backward(grad_hidden, unit_first, inverse_first, gain_first).astype(
        jnp.bfloat16
    )
    grad_mixed_first = (
        mixed("qcsd,fd->qcsf", grad_first, w_out_first).astype(jnp.bfloat16).reshape(head_shape)
    )
    own_dot_first = mixed("qcshe,qcthe->qchst", grad_mixed_first, first_vals)
    cross_dot_first = mixed("qche,qdhe->qchd", grad_mixed_first[:, :, 0], cls_vals)
    own_part = jnp.sum(own_prob * own_dot_first, -1)
    row_part = own_part[..., 0] + jnp.sum(cross_prob * cross_dot_first, -1)
    centre_first = jnp.where(first_mask, row_part[..., None], own_part)
    own_slope_first = (own_prob * (own_dot_first - centre_first[..., None])).astype(jnp.bfloat16)
    cross_slope_first = (cross_prob * (cross_dot_first - row_part[..., None])).astype(jnp.bfloat16)
    query_grad = mixed("qchst,qcthe->qcshe", own_slope_first, first_keys)
    query_cls = mixed("qchd,qdhe->qche", cross_slope_first, cls_keys)
    query_grad = jnp.where(
        first_mask[None, None, :, None, None], query_grad + query_cls[:, :, None], query_grad
    )
    query_grad = (
        (query_grad * score_scale)
        .astype(jnp.bfloat16)
        .reshape(lists, local_cands, seq_len, local_width)
    )
    key_first = (mixed("qchst,qcshe->qcthe", own_slope_first, first_query) * score_scale).reshape(
        lists, local_cands, seq_len, local_width
    )
    val_first = mixed("qchst,qcshe->qcthe", own_weight, grad_mixed_first).reshape(
        lists, local_cands, seq_len, local_width
    )
    cls_key_first = (
        mixed("qchd,qche->qdhe", cross_slope_first, first_query[:, :, 0]) * score_scale
    ).reshape(lists, cand_count, local_width)
    cls_val_first = mixed("qchd,qche->qdhe", cross_weight, grad_mixed_first[:, :, 0]).reshape(
        lists, cand_count, local_width
    )
    back_key_first, back_val_first = (
        lax.psum_scatter(cls_key_first, "cand", scatter_dimension=1, tiled=True),
        lax.psum_scatter(cls_val_first, "cand", scatter_dimension=1, tiled=True),
    )
    key_first = jnp.where(first_cols, key_first + back_key_first[:, :, None], key_first).astype(
        jnp.bfloat16
    )
    val_first = jnp.where(first_cols, val_first + back_val_first[:, :, None], val_first).astype(
        jnp.bfloat16
    )
    row_count = lists * local_cands * seq_len
    stacked = jnp.stack([query_grad, key_first, val_first], 3).reshape(row_count, 3, local_width)
    flat_tokens = tokens.reshape(row_count, model_width)
    partial_grad = lax.psum_scatter(
        mixed("rd,rkf->dkf", flat_tokens, stacked), "cand", scatter_dimension=0, tiled=True
    )
    result = lax.psum(partial_grad, "query")
    return result


def solution(mesh):
    return jax.shard_map(
        local,
        mesh=mesh,
        in_specs=(
            P(("groups", "query"), "cand", None, None),
            P(("groups", "query"), "cand"),
            P(("groups", "query"), "cand"),
            P(None, None, "mp"),
            P("mp", None),
            P(),
            P(None, None, "mp"),
            P("mp", None),
            P(),
            P(),
        ),
        out_specs=P(("groups", "cand"), None, "mp"),
        check_vma=False,
    )
```

profile of v0, /device:TPU:8, one launch (start us, length us, event | category | flops | bytes accessed | tf_op | source)
XLA Modules:
  0.0 305.8 jit_solution(17431305689464585126)
XLA Ops:
  6.5 1.4 copy-done
  7.9 1.7 fusion.2
  9.9 8.2 %all-gather = bf16[1,4,1,256]{3,2,0,1:T(2,128)(2,1)S(1)} all-gather(bf16[1,1,1,256]{3,2,0,1:T(2,128)(2,1)S(1)} %copy.68), channel_id=2, replica_groups=mesh['groups'=2,'cand'=4,'query'=2,'mp'=2] {'cand'}, dimensions={1}, use_global_device_ids=true | all-gather | bytes 2560 | tf_op jit(solution)/shard_map/all_gather | solution.py:81
  21.9 10.9 %all-gather.1 = bf16[1,4,1,256]{3,2,0,1:T(2,128)(2,1)S(1)} all-gather(bf16[1,1,1,256]{3,2,0,1:T(2,128)(2,1)S(1)} %copy.73), channel_id=3, replica_groups=mesh['groups'=2,'cand'=4,'query'=2,'mp'=2] {'cand'}, dimensions={1}, use_global_device_ids=true | all-gather | bytes 2560 | tf_op jit(solution)/shard_map/all_gather | solution.py:82
  35.5 9.0 %pmax.7 = f32[1,1]{1,0:T(1,128)} all-reduce(f32[1,1]{1,0:T(1,128)} %param.12), channel_id=1, replica_groups=mesh['groups'=2,'cand'=4,'query'=2,'mp'=2] {'cand'}, use_global_device_ids=true, to_apply=%region_15.16 | all-reduce | flops 1 | bytes 8 | tf_op jit(solution)/shard_map/pmax | solution.py:133
  46.4 8.2 %all-reduce.11.cloned.1.call-done = f32[1,1,256,1024]{3,2,1,0:T(8,128)} async-done(((f32[1,1,256,1024]{3,2,1,0:T(8,128)}), f32[1,1,256,1024]{3,2,1,0:T(8,128)}) %all-reduce.11.cloned.1.call-update) | async-done | bytes 1048592 | tf_op jit(solution)/shard_map/psum | solution.py:103
  54.7 1.5 fusion.99
  59.0 8.1 %all-gather.2 = bf16[1,4,1,256]{3,2,0,1:T(2,128)(2,1)S(1)} all-gather(bf16[1,1,1,256]{3,2,0,1:T(2,128)(2,1)S(1)} %slice_bitcast_fusion.1), channel_id=4, replica_groups=mesh['groups'=2,'cand'=4,'query'=2,'mp'=2] {'cand'}, dimensions={1}, use_global_device_ids=true | all-gather | bytes 2560 | tf_op jit(solution)/shard_map/all_gather | solution.py:109
  73.0 1.4 convert_convert_fusion
  75.7 10.8 %all-gather.3 = bf16[1,4,1,256]{3,2,0,1:T(2,128)(2,1)S(1)} all-gather(bf16[1,1,1,256]{3,2,0,1:T(2,128)(2,1)S(1)} %slice_bitcast_fusion), channel_id=5, replica_groups=mesh['groups'=2,'cand'=4,'query'=2,'mp'=2] {'cand'}, dimensions={1}, use_global_device_ids=true | all-gather | bytes 2560 | tf_op jit(solution)/shard_map/all_gather | solution.py:110
  88.5 1.7 copy.76
  93.9 3.0 psum.43
  96.9 1.4 fusion.112
  102.9 9.4 %all-reduce.6 = (f32[1,1]{1,0:T(1,128)}, f32[1,1]{1,0:T(1,128)}) all-reduce(f32[1,1]{1,0:T(1,128)} %bitcast.54, f32[1,1]{1,0:T(1,128)S(6)} %exp.31), channel_id=1, replica_groups=mesh['groups'=2,'cand'=4,'query'=2,'mp'=2] {'cand'}, use_global_device_ids=true, to_apply=%region_14.15 | all-reduce | flops 2 | bytes 16 | tf_op jit(solution)/shard_map/psum | solution.py:135
  113.8 1.4 fusion.111
  121.6 1.4 fusion.60
  124.0 1.3 copy.105
  133.9 1.5 broadcast_multiply_fusion
  137.7 1.5 multiply_multiply_fusion
  139.2 10.5 %all-reduce.5 = (f32[1,4,256]{2,1,0:T(4,128)S(1)}, f32[1,4,256]{2,1,0:T(4,128)S(1)}) all-reduce(f32[1,4,256]{2,1,0:T(4,128)S(1)} %reshape.1078, f32[1,4,256]{2,1,0:T(4,128)S(1)} %reshape.1080), channel_id=6, replica_groups=mesh['groups'=2,'cand'=4,'query'=2,'mp'=2] {'cand'}, use_global_device_ids=true, to_apply=%region_21.22.clone | all-reduce | flops 2048 | bytes 16384
  150.3 1.6 fusion.14
  151.9 2.5 fusion
  155.1 18.5 %all-reduce.13.cloned.1.call-done = f32[1,1,256,1024]{3,2,1,0:T(8,128)} async-done(((f32[1,1,256,1024]{3,2,1,0:T(8,128)}), f32[1,1,256,1024]{3,2,1,0:T(8,128)}) %all-reduce.13.cloned.1.call-update) | async-done | bytes 1048592 | tf_op jit(solution)/shard_map/psum | solution.py:194
  173.6 1.9 fusion.8
  175.6 1.4 convolution_convert_fusion.2
  180.0 2.8 multiply_reduce_fusion
  184.3 1.5 multiply_convert_fusion
  186.6 9.0 %all-reduce.4 = (f32[1,4,256]{2,1,0:T(4,128)S(1)}, f32[1,4,256]{2,1,0:T(4,128)S(1)}) all-reduce(f32[1,4,256]{2,1,0:T(4,128)S(1)} %reshape.1089, f32[1,4,256]{2,1,0:T(4,128)S(1)} %reshape.1087), channel_id=9, replica_groups=mesh['groups'=2,'cand'=4,'query'=2,'mp'=2] {'cand'}, use_global_device_ids=true, to_apply=%region_29.30.clone | all-reduce | flops 2048 | bytes 16384
  196.9 2.2 convolution_bitcast_fusion
  199.2 60.8 %reduce-scatter.6.cloned.1.call-done = f32[256,3,256]{0,2,1:T(8,128)} async-done(((f32[1024,3,256]{0,2,1:T(8,128)}), f32[256,3,256]{0,2,1:T(8,128)}) %reduce-scatter.6.cloned.1.call-update) | async-done | bytes 786448 | tf_op jit(solution)/shard_map/reduce_scatter | solution.py:244
  260.0 37.0 %all-reduce.15.cloned.1.call-done = f32[256,3,256]{0,2,1:T(8,128)} async-done(((f32[256,3,256]{0,2,1:T(8,128)}), f32[256,3,256]{0,2,1:T(8,128)}) %all-reduce.15.cloned.1.call-update) | async-done | bytes 786448 | tf_op jit(solution)/shard_map/psum | solution.py:247
  297.0 2.3 copy.83
  (225 shorter events, 49.7 us)
Async XLA Ops:
  6.5 48.1 %all-reduce.11.cloned.1.call-start = ((), (), s32[]{:S(2)}) async-start(), calls=%async_computation.1 | async-start | bytes 2097152 | tf_op jit(solution)/shard_map/psum | solution.py:103
  7.9 25.2 %copy-start.19 = (pred[256]{0:T(512)(128)(4,1)}, pred[256]{0:T(512)(128)(4,1)S(1)}, u32[]{:S(2)}) copy-start(pred[256]{0:T(512)(128)(4,1)S(1)} %iota_compare_fusion.1) | copy-start | bytes 772
  9.7 23.8 %copy-start.12 = (bf16[1,1,1,256,256]{3,4,0,2,1:T(8,128)(2,1)}, bf16[1,1,1,256,256]{3,4,0,2,1:T(8,128)(2,1)S(1)}, u32[]{:S(2)}) copy-start(bf16[1,1,1,256,256]{3,4,0,2,1:T(8,128)(2,1)S(1)} %get-tuple-element.31) | copy-start | bytes 393220
  9.8 11.0 %copy-start.37 = (bf16[1,1,1,4,64]{4,3,2,1,0:T(4,128)(2,1)}, bf16[1,1,1,4,64]{4,3,2,1,0:T(4,128)(2,1)S(1)}, u32[]{:S(2)}) copy-start(bf16[1,1,1,4,64]{4,3,2,1,0:T(4,128)(2,1)S(1)} %copy.125) | copy-start | bytes 1540
  19.1 2.8 copy-start.21
  20.3 13.1 %copy-start.3 = (f32[4,256,256]{1,2,0:T(8,128)}, f32[4,256,256]{1,2,0:T(8,128)S(1)}, u32[]{:S(2)}) copy-start(f32[4,256,256]{1,2,0:T(8,128)S(1)} %get-tuple-element.41) | copy-start | bytes 3145732
  21.0 12.1 %copy-start.27 = (f32[4,256]{1,0:T(4,128)}, f32[4,256]{1,0:T(4,128)S(1)}, u32[]{:S(2)}) copy-start(f32[4,256]{1,0:T(4,128)S(1)} %broadcast_select_fusion.1) | copy-start | bytes 12292
  21.7 11.7 %copy-start.16 = (f32[4,4]{0,1:T(4,128)}, f32[4,4]{0,1:T(4,128)S(1)}, u32[]{:S(2)}) copy-start(f32[4,4]{0,1:T(4,128)S(1)} %get-tuple-element.16) | copy-start | bytes 196
  33.6 12.3 %copy-start.47 = (u32[32]{0:T(128)S(1)}, u32[32]{0:T(128)}, u32[]{:S(2)}) copy-start(u32[32]{0:T(128)} %constant.50) | copy-start | bytes 388
  33.6 21.1 %copy-start.2 = (bf16[1,1,256,1024]{3,2,1,0:T(8,128)(2,1)S(1)}, bf16[1,1,256,1024]{3,2,1,0:T(8,128)(2,1)}, u32[]{:S(2)}) copy-start(bf16[1,1,256,1024]{3,2,1,0:T(8,128)(2,1)} %param.10) | copy-start | bytes 1572868
  35.5 138.1 %all-reduce.13.cloned.1.call-start = ((), (), s32[]{:S(2)}) async-start(), calls=%async_computation.2 | async-start | bytes 2097152 | tf_op jit(solution)/shard_map/psum | solution.py:194
  46.4 10.1 %copy-start.25 = (f32[1024]{0:T(1024)S(1)}, f32[1024]{0:T(1024)}, u32[]{:S(2)}) copy-start(f32[1024]{0:T(1024)} %param.15) | copy-start | bytes 12292
  57.6 10.5 %copy-start.22 = (pred[4]{0:T(512)(128)(4,1)S(1)}, pred[4]{0:T(512)(128)(4,1)}, u32[]{:S(2)}) copy-start(pred[4]{0:T(512)(128)(4,1)} %copy-done.21) | copy-start | bytes 16
  73.0 40.8 %copy-start.18 = (f32[4,4]{0,1:T(4,128)}, f32[4,4]{0,1:T(4,128)S(1)}, u32[]{:S(2)}) copy-start(f32[4,4]{0,1:T(4,128)S(1)} %get-tuple-element.20) | copy-start | bytes 196
  87.9 4.1 %copy-start.45 = (bf16[4,4,64]{2,1,0:T(4,128)(2,1)}, bf16[4,4,64]{2,1,0:T(4,128)(2,1)S(1)}, u32[]{:S(2)}) copy-start(bf16[4,4,64]{2,1,0:T(4,128)(2,1)S(1)} %reshape.1073) | copy-start | bytes 6148
  131.7 20.2 %copy-start.20 = (pred[256]{0:T(512)(128)(4,1)S(1)}, pred[256]{0:T(512)(128)(4,1)}, u32[]{:S(2)}) copy-start(pred[256]{0:T(512)(128)(4,1)} %copy-done.19) | copy-start | bytes 772
  149.7 2.2 copy-start.6
  151.9 2.6 copy-start.38
  151.9 21.7 %copy-start.24 = (f32[256]{0:T(256)S(1)}, f32[256]{0:T(256)}, u32[]{:S(2)}) copy-start(f32[256]{0:T(256)} %copy-done.23) | copy-start | bytes 3076
  151.9 21.7 %copy-start.26 = (f32[1024]{0:T(1024)S(1)}, f32[1024]{0:T(1024)}, u32[]{:S(2)}) copy-start(f32[1024]{0:T(1024)} %param.15) | copy-start | bytes 12292
  151.9 21.7 %copy-start.31 = (f32[256]{0:T(256)S(1)}, f32[256]{0:T(256)}, u32[]{:S(2)}) copy-start(f32[256]{0:T(256)} %copy-done.30) | copy-start | bytes 3076
  154.4 105.6 %reduce-scatter.6.cloned.1.call-start = ((), (), s32[]{:S(2)}) async-start(), calls=%async_computation.3 | async-start | bytes 3932160 | tf_op jit(solution)/shard_map/reduce_scatter | solution.py:244
  175.5 3.7 %copy-start.17 = (f32[4,4]{0,1:T(4,128)S(1)}, f32[4,4]{0,1:T(4,128)}, u32[]{:S(2)}) copy-start(f32[4,4]{0,1:T(4,128)} %copy-done.16) | copy-start | bytes 196
  175.5 4.4 %copy-start.13 = (bf16[1,1,1,256,256]{3,4,0,2,1:T(8,128)(2,1)S(1)}, bf16[1,1,1,256,256]{3,4,0,2,1:T(8,128)(2,1)}, u32[]{:S(2)}) copy-start(bf16[1,1,1,256,256]{3,4,0,2,1:T(8,128)(2,1)} %copy-done.12) | copy-start | bytes 393220
  180.0 2.8 copy-start.34
  180.0 3.0 copy-start.4
  180.0 3.0 copy-start.15
  180.0 3.0 copy-start.28
  184.3 2.0 copy-start.35
  184.3 2.2 copy-start.36
  185.7 11.0 %copy-start.11 = (f32[4,64,256]{2,1,0:T(8,128)S(1)}, f32[4,64,256]{2,1,0:T(8,128)}, u32[]{:S(2)}) copy-start(f32[4,64,256]{2,1,0:T(8,128)} %fusion.35) | copy-start | bytes 786436
  199.1 97.9 %all-reduce.15.cloned.1.call-start = ((), (), s32[]{:S(2)}) async-start(), calls=%async_computation.4 | async-start | bytes 1572864 | tf_op jit(solution)/shard_map/psum | solution.py:247
  (20 other events, 23.3 us)
Sparse Core Ops, SparseCore 0:
  35.6 19.0 all-reduce.10
  154.5 19.0 all-reduce.12
  199.3 60.7 reduce-scatter.5
  262.2 34.8 all-reduce.14
where the time goes:
time: 309 us; the launch traced here: 306 us
  waiting for transfers between devices  125 us (40%)
  blocking collectives  79 us (26%)
  other arithmetic  29.3 us (9%)
  matrix products  27.3 us (9%)
  local copies, waits for them, and re-layouts  25 us (8%)
  between operations  20.4 us (7%)
    reduce_scatter x1, waiting for transfers between devices, local(): lax.psum_scatter(mixed('rd,rkf->dkf', flat_tokens, stacked), 'cand', scat...  60.8 us
    psum x1, waiting for transfers between devices, local(): result = lax.psum(partial_grad, 'query')  37 us
    dot_general x29, matrix products, mixed(): jnp.einsum(pattern, former, latter, preferred_element_type=jnp.float32)  27.3 us
    unnamed x2, blocking collectives  19.4 us
    psum x1, waiting for transfers between devices, local(): summed_term = lax.psum(partial_term, 'mp')  18.5 us
    all_gather x1, blocking collectives, local(): lax.all_gather(projected[2][:, :, 0], 'cand', axis=1, tiled=True)  10.9 us
    all_gather x1, blocking collectives, local(): lax.all_gather(last_kv[1][:, :, 0], 'cand', axis=1, tiled=True)  10.8 us
    psum x1, blocking collectives, local(): lax.psum((jnp.sum(score_exp, 1), jnp.sum(teacher_exp, 1)), 'cand')  9.44 us
  transfers between devices with their start and end apart: 4, of which 4 were waited for; matrix products, arithmetic and copies ran while one was open for 0% of the time, Pallas kernels for 0%

commit v1 on v0

--- a/solution.py
+++ b/solution.py
@@ -76,11 +76,19 @@
     cross_valid = local_ids[:, None] != jnp.arange(cand_count)[None, :]
     head_shape = (lists, local_cands, seq_len, local_heads, HEAD_DIM)
     cls_shape = (lists, cand_count, local_heads, HEAD_DIM)
+    out_first_full = lax.all_gather(w_out_first, "mp", axis=0, tiled=True)
+    last_full = lax.all_gather(w_last, "mp", axis=2, tiled=True)
+    out_last_full = lax.all_gather(w_out_last, "mp", axis=0, tiled=True)
+    teacher_all = lax.all_gather(teacher, "cand", axis=1, tiled=True)
     projected = mixed("qcsd,kdf->kqcsf", tokens, w_first).astype(jnp.bfloat16)
-    gathered_keys, gathered_vals = (
-        lax.all_gather(projected[1][:, :, 0], "cand", axis=1, tiled=True),
-        lax.all_gather(projected[2][:, :, 0], "cand", axis=1, tiled=True),
-    )
+    gathered_kv = lax.all_gather(
+        jnp.concatenate([projected[1][:, :, 0], projected[2][:, :, 0]], -1),
+        "cand",
+        axis=1,
+        tiled=True,
+    )
+    gathered_keys = gathered_kv[..., :local_width]
+    gathered_vals = gathered_kv[..., local_width:]
     first_query = projected[0].reshape(head_shape)
     first_keys = projected[1].reshape(head_shape)
     first_vals = projected[2].reshape(head_shape)
@@ -99,16 +107,22 @@
         first_mask[None, None, :, None, None], attended + attended_cls[:, :, None], attended
     )
     first_mixed = attended.reshape(lists, local_cands, seq_len, local_width).astype(jnp.bfloat16)
-    partial_first = mixed("qcsf,fd->qcsd", first_mixed, w_out_first)
-    residual_first = tokens.astype(jnp.float32) + lax.psum(partial_first, "mp")
+    first_joined = lax.all_gather(first_mixed, "mp", axis=3, tiled=True)
+    residual_first = tokens.astype(jnp.float32) + mixed(
+        "qcsf,fd->qcsd", first_joined, out_first_full
+    )
     normed_first, unit_first, inverse_first = norm_forward(residual_first, gain_first)
     hidden = normed_first.astype(jnp.bfloat16)
     last_query = mixed("qcd,df->qcf", hidden[:, :, 0], w_last[0]).astype(jnp.bfloat16)
     last_kv = mixed("qcsd,kdf->kqcsf", hidden, w_last[1:]).astype(jnp.bfloat16)
-    gathered_keys_last, gathered_vals_last = (
-        lax.all_gather(last_kv[0][:, :, 0], "cand", axis=1, tiled=True),
-        lax.all_gather(last_kv[1][:, :, 0], "cand", axis=1, tiled=True),
-    )
+    gathered_kv_last = lax.all_gather(
+        jnp.concatenate([last_kv[0][:, :, 0], last_kv[1][:, :, 0]], -1),
+        "cand",
+        axis=1,
+        tiled=True,
+    )
+    gathered_keys_last = gathered_kv_last[..., :local_width]
+    gathered_vals_last = gathered_kv_last[..., local_width:]
     last_heads = last_query.reshape(lists, local_cands, local_heads, HEAD_DIM)
     last_keys = last_kv[0].reshape(head_shape)
     last_vals = last_kv[1].reshape(head_shape)
@@ -125,16 +139,17 @@
         "qchd,qdhe->qche", cross_last_weight, cls_vals_last
     )
     last_mixed = attended_last.reshape(lists, local_cands, local_width).astype(jnp.bfloat16)
-    partial_last = mixed("qcf,fd->qcd", last_mixed, w_out_last)
-    residual_last = hidden[:, :, 0].astype(jnp.float32) + lax.psum(partial_last, "mp")
+    last_joined = lax.all_gather(last_mixed, "mp", axis=2, tiled=True)
+    residual_last = hidden[:, :, 0].astype(jnp.float32) + mixed(
+        "qcf,fd->qcd", last_joined, out_last_full
+    )
     normed_last, unit_last, inverse_last = norm_forward(residual_last, gain_last)
     scores = jnp.einsum("qcd,d->qc", normed_last, w_score, precision=lax.Precision.HIGHEST)
     score_exp = jnp.exp(scores)
-    teacher_peak = lax.pmax(jnp.max(teacher, 1), "cand")
+    teacher_peak = jnp.max(teacher_all, 1)
     teacher_exp = jnp.exp(teacher - teacher_peak[:, None])
-    score_totals, teacher_totals = lax.psum(
-        (jnp.sum(score_exp, 1), jnp.sum(teacher_exp, 1)), "cand"
-    )
+    teacher_totals = jnp.sum(jnp.exp(teacher_all - teacher_peak[:, None]), 1)
+    score_totals = lax.psum(jnp.sum(score_exp, 1), "cand")
     student_prob = score_exp / score_totals[:, None]
     teacher_prob = teacher_exp / teacher_totals[:, None]
     score_grad = LOSS_SCALE * (student_prob - teacher_prob) / query_count
@@ -186,12 +201,20 @@
     val_grad = jnp.where(first_cols, own_val_grad + back_vals[:, :, None], own_val_grad).astype(
         jnp.bfloat16
     )
-    partial_term = mixed("qcsf,df->qcsd", key_grad, w_last[1]) + mixed(
-        "qcsf,df->qcsd", val_grad, w_last[2]
-    )
-    query_term = mixed("qcf,df->qcd", grad_query_last, w_last[0])
-    partial_term = jnp.where(first_cols, partial_term + query_term[:, :, None], partial_term)
-    summed_term = lax.psum(partial_term, "mp")
+    joined = lax.all_gather(
+        jnp.concatenate([key_grad, val_grad, grad_query_last[:, :, None]], 2),
+        "mp",
+        axis=3,
+        tiled=True,
+    )
+    key_joined = joined[:, :, :seq_len]
+    val_joined = joined[:, :, seq_len : 2 * seq_len]
+    query_joined = joined[:, :, 2 * seq_len]
+    summed_term = mixed("qcsf,df->qcsd", key_joined, last_full[1]) + mixed(
+        "qcsf,df->qcsd", val_joined, last_full[2]
+    )
+    query_term = mixed("qcf,df->qcd", query_joined, last_full[0])
+    summed_term = jnp.where(first_cols, summed_term + query_term[:, :, None], summed_term)
     grad_hidden = jnp.where(first_cols, summed_term + grad_last[:, :, None], summed_term)
     grad_first = norm_backward(grad_hidden, unit_first, inverse_first, gain_first).astype(
         jnp.bfloat16
@@ -242,10 +265,13 @@
     stacked = jnp.stack([query_grad, key_first, val_first], 3).reshape(row_count, 3, local_width)
     flat_tokens = tokens.reshape(row_count, model_width)
     partial_grad = lax.psum_scatter(
-        mixed("rd,rkf->dkf", flat_tokens, stacked), "cand", scatter_dimension=0, tiled=True
+        mixed("rd,rkf->dkf", flat_tokens, stacked).astype(jnp.bfloat16),
+        "cand",
+        scatter_dimension=0,
+        tiled=True,
     )
     result = lax.psum(partial_grad, "query")
-    return result
+    return result.astype(jnp.float32)
 
 
 def solution(mesh):

time: 309 us -> 237 us (0.77)
  waiting for transfers between devices: 125 us -> 63.7 us
  blocking collectives: 79 us -> 60.3 us
  local copies, waits for them, and re-layouts: 25 us -> 29.8 us
  other arithmetic: 29.3 us -> 33.3 us
    reduce_scatter x1, waiting for transfers between devices: 60.8 us -> 33.6 us  [local(): lax.psum_scatter(mixed('rd,rkf->dkf', flat_tokens, stacked).astype(jnp.bf...]
    psum x2 -> x0, waiting for transfers between devices: 26.8 us -> none  [the longest x1 18.5 us: local(): summed_term = lax.psum(partial_term, 'mp')]
    psum x1, waiting for transfers between devices: 37 us -> 27.9 us  [local(): result = lax.psum(partial_grad, 'query')]
    pmax x1 -> x0, blocking collectives: 8.97 us -> none  [local(): teacher_peak = lax.pmax(jnp.max(teacher, 1), 'cand')]
    all_gather x4 -> x5, blocking collectives: 38.1 us -> 30.3 us  [the longest x1 12.1 us: local(): lax.all_gather(jnp.concatenate([projected[1][:, :, 0], projected[2][:, :,...]
    psum x2 -> x1, blocking collectives: 12.5 us -> 11 us  [local(): score_totals = lax.psum(jnp.sum(score_exp, 1), 'cand')]
    unnamed x102 -> x103, local copies, waits for them, and re-layouts: 8.67 us -> 9.49 us
  transfers between devices with their start and end apart: 4 -> 5, of which waited for: 4 -> 2; matrix products, arithmetic and copies ran while one was open for 0% -> 28% of each run, Pallas kernels for 0% -> 0%
where the time goes in v1:
time: 237 us; the launch traced here: 234 us
  waiting for transfers between devices  63.7 us (27%)
  blocking collectives  60.3 us (25%)
  other arithmetic  33.3 us (14%)
  local copies, waits for them, and re-layouts  29.8 us (13%)
  matrix products  25.8 us (11%)
  between operations  20.6 us (9%)
    reduce_scatter x1, waiting for transfers between devices, local(): lax.psum_scatter(mixed('rd,rkf->dkf', flat_tokens, stacked).astype(jnp.bf...  33.6 us
    psum x1, waiting for transfers between devices, local(): result = lax.psum(partial_grad, 'query')  27.9 us
    dot_general x29, matrix products, mixed(): jnp.einsum(pattern, former, latter, preferred_element_type=jnp.float32)  25.8 us
    unnamed x2, blocking collectives  19 us
    all_gather x1, blocking collectives, local(): lax.all_gather(jnp.concatenate([projected[1][:, :, 0], projected[2][:, :,...  12.1 us
    psum x1, blocking collectives, local(): score_totals = lax.psum(jnp.sum(score_exp, 1), 'cand')  11 us
    all_gather x1, blocking collectives, local(): lax.all_gather(jnp.concatenate([last_kv[0][:, :, 0], last_kv[1][:, :, 0]]...  10.7 us
    unnamed x103, local copies, waits for them, and re-layouts  9.49 us
  transfers between devices with their start and end apart: 5, of which 2 were waited for; matrix products, arithmetic and copies ran while one was open for 28% of the time, Pallas kernels for 0%

profile of v1, /device:TPU:8, one launch (start us, length us, event | category | flops | bytes accessed | tf_op | source)
XLA Modules:
  0.0 233.5 jit_solution(6001374203612047564)
XLA Ops:
  10.9 12.1 %all_gather.27 = bf16[1,4,512]{2,0,1:T(2,128)(2,1)S(1)} all-gather(bf16[1,1,512]{2,0,1:T(2,128)(2,1)S(1)} %maximum_bitcast_fusion.2), channel_id=1, replica_groups=mesh['groups'=2,'cand'=4,'query'=2,'mp'=2] {'cand'}, dimensions={1}, use_global_device_ids=true | all-gather | bytes 5120 | tf_op jit(solution)/shard_map/all_gather | solution.py:84
  27.9 1.3 copy.69
  37.2 2.1 all_gather.28
  40.0 1.3 fusion.108
  41.9 1.9 bitcast_dynamic-update-slice_fusion
  43.8 1.9 fusion.110
  52.4 10.7 %all_gather.30 = bf16[1,4,512]{2,0,1:T(2,128)(2,1)S(1)} all-gather(bf16[1,1,512]{2,0,1:T(2,128)(2,1)S(1)} %pad_maximum_fusion.1), channel_id=1, replica_groups=mesh['groups'=2,'cand'=4,'query'=2,'mp'=2] {'cand'}, dimensions={1}, use_global_device_ids=true | all-gather | bytes 5120 | tf_op jit(solution)/shard_map/all_gather | solution.py:118
  68.9 1.4 convert_convert_fusion
  72.3 1.7 copy.72
  75.1 1.4 copy.95
  76.5 1.3 reshape.1029
  80.3 1.3 convert_element_type.190
  81.6 3.0 %all_gather.31 = bf16[1,1,512]{2,1,0:T(2,128)(2,1)} all-gather(bf16[1,1,256]{2,1,0:T(2,128)(2,1)} %convert_element_type.190), channel_id=1, replica_groups=mesh['groups'=2,'cand'=4,'query'=2,'mp'=2] {'mp'}, dimensions={2}, use_global_device_ids=true | all-gather | bytes 1536 | tf_op jit(solution)/shard_map/all_gather | solution.py:142
  84.6 1.5 fusion.72
  88.9 1.4 multiply_reduce_fusion.2
  91.1 11.0 %all-reduce.7 = (f32[1,1]{1,0:T(1,128)}, f32[4]{0:T(128)}) all-reduce(f32[1,1]{1,0:T(1,128)} %bitcast.52, f32[4]{0:T(128)} %bitcast_dynamic-update-slice_fusion), channel_id=1, replica_groups=mesh['groups'=2,'cand'=4,'query'=2,'mp'=2] {'cand'}, use_global_device_ids=true, to_apply=%region_12.13 | all-reduce | flops 5 | bytes 40 | tf_op jit(solution)/shard_map/psum | solution.py:152
  102.8 1.4 reduce_max.55
  104.2 2.0 exponential_reduce_fusion
  107.5 1.9 fusion.95
  118.7 9.5 %all-reduce.6 = (f32[1,4,256]{2,1,0:T(4,128)S(1)}, f32[1,4,256]{2,1,0:T(4,128)S(1)}) all-reduce(f32[1,4,256]{2,1,0:T(4,128)S(1)} %reshape.1035, f32[1,4,256]{2,1,0:T(4,128)S(1)} %reshape.1033), channel_id=3, replica_groups=mesh['groups'=2,'cand'=4,'query'=2,'mp'=2] {'cand'}, use_global_device_ids=true, to_apply=%region_20.21.clone | all-reduce | flops 2048 | bytes 16384
  131.2 2.3 all_gather.34
  134.3 1.7 fusion.7
  136.1 1.6 fusion.6
  137.7 3.1 %fusion.8 = (f32[256]{0:T(256)S(1)}, f32[256,1024]{1,0:T(8,128)}) fusion(f32[1,1,256,1024]{3,2,1,0:T(8,128)S(1)} %get-tuple-element.50, f32[256]{0:T(256)S(1)} %copy-done.26, f32[256]{0:T(256)S(1)} %copy-done.24, f32[1024]{0:T(1024)S(1)} %copy-done.37, f32[1024]{0:T(1024)S(1)} %copy-done.45, f32[1024]{0:T(1024)S(1)} %bitcast.339, ...), kind=kOutput, calls=%fused_computation.24 | convolution fusion | flops 271056640 | bytes 4472064 | tf_op jit(solution)/shard_map/qcsf,df->qcsd/dot_general | solution.py:15
  141.4 1.4 reduce_sum.183
  142.8 1.9 convolution_convert_fusion.3
  144.7 1.4 multiply_reduce_fusion
  150.2 9.5 %all-reduce.5 = (f32[1,4,256]{2,1,0:T(4,128)S(1)}, f32[1,4,256]{2,1,0:T(4,128)S(1)}) all-reduce(f32[1,4,256]{2,1,0:T(4,128)S(1)} %reshape.1046, f32[1,4,256]{2,1,0:T(4,128)S(1)} %reshape.1044), channel_id=5, replica_groups=mesh['groups'=2,'cand'=4,'query'=2,'mp'=2] {'cand'}, use_global_device_ids=true, to_apply=%region_26.27.clone | all-reduce | flops 2048 | bytes 16384
  161.6 1.7 fusion
  163.4 33.6 %reduce-scatter.6.cloned.1.call-done = bf16[256,3,256]{0,2,1:T(8,128)(2,1)} async-done(((bf16[1024,3,256]{0,2,1:T(8,128)(2,1)}), bf16[256,3,256]{0,2,1:T(8,128)(2,1)}) %reduce-scatter.6.cloned.1.call-update) | async-done | bytes 393232 | tf_op jit(solution)/shard_map/reduce_scatter | solution.py:267
  197.0 27.9 %all-reduce.10.cloned.1.call-done = bf16[256,3,256]{0,2,1:T(8,128)(2,1)} async-done(((bf16[256,3,256]{0,2,1:T(8,128)(2,1)}), bf16[256,3,256]{0,2,1:T(8,128)(2,1)}) %all-reduce.10.cloned.1.call-update) | async-done | bytes 393232 | tf_op jit(solution)/shard_map/psum | solution.py:273
  225.0 2.0 copy.79
  (231 shorter events, 54.8 us)
Async XLA Ops:
  6.5 2.8 %copy-start = (bf16[3,1024,256]{2,1,0:T(8,128)(2,1)S(1)}, bf16[3,1024,256]{2,1,0:T(8,128)(2,1)}, u32[]{:S(2)}) copy-start(bf16[3,1024,256]{2,1,0:T(8,128)(2,1)} %param.13) | copy-start | bytes 4718596
  6.5 2.8 %copy-start.6 = (bf16[1,1,256,1024]{3,2,1,0:T(8,128)(2,1)S(1)}, bf16[1,1,256,1024]{3,2,1,0:T(8,128)(2,1)}, u32[]{:S(2)}) copy-start(bf16[1,1,256,1024]{3,2,1,0:T(8,128)(2,1)} %param.10) | copy-start | bytes 1572868
  6.5 37.3 %all-gather.4.cloned.1.call-start = ((), (), s32[]{:S(2)}) async-start(), calls=%async_computation.1 | async-start | bytes 1572864 | tf_op jit(solution)/shard_map/all_gather | solution.py:79
  7.3 77.4 %all-gather.6.cloned.1.call-start = ((), (), s32[]{:S(2)}) async-start(), calls=%async_computation.2 | async-start | bytes 1572864 | tf_op jit(solution)/shard_map/all_gather | solution.py:81
  8.0 126.3 %all-gather.8.cloned.1.call-start = ((), (), s32[]{:S(2)}) async-start(), calls=%async_computation.3 | async-start | bytes 4718592 | tf_op jit(solution)/shard_map/all_gather | solution.py:80
  8.7 188.3 %reduce-scatter.6.cloned.1.call-start = ((), (), s32[]{:S(2)}) async-start(), calls=%async_computation.4 | async-start | bytes 1966080 | tf_op jit(solution)/shard_map/reduce_scatter | solution.py:267
  10.0 27.2 %copy-start.13 = (bf16[1,1,1,256,256]{3,4,0,2,1:T(8,128)(2,1)}, bf16[1,1,1,256,256]{3,4,0,2,1:T(8,128)(2,1)S(1)}, u32[]{:S(2)}) copy-start(bf16[1,1,1,256,256]{3,4,0,2,1:T(8,128)(2,1)S(1)} %get-tuple-element.35) | copy-start | bytes 393220
  10.7 15.8 %copy-start.29 = (pred[256]{0:T(512)(128)(4,1)}, pred[256]{0:T(512)(128)(4,1)S(1)}, u32[]{:S(2)}) copy-start(pred[256]{0:T(512)(128)(4,1)S(1)} %iota_compare_fusion) | copy-start | bytes 772
  24.6 12.6 %copy-start.18 = (pred[4]{0:T(512)(128)(4,1)}, pred[4]{0:T(512)(128)(4,1)S(1)}, u32[]{:S(2)}) copy-start(pred[4]{0:T(512)(128)(4,1)S(1)} %iota_compare_fusion.2) | copy-start | bytes 16
  25.7 11.5 %copy-start.1 = (f32[4,256,256]{1,2,0:T(8,128)}, f32[4,256,256]{1,2,0:T(8,128)S(1)}, u32[]{:S(2)}) copy-start(f32[4,256,256]{1,2,0:T(8,128)S(1)} %get-tuple-element.48) | copy-start | bytes 3145732
  32.7 4.5 %copy-start.15 = (f32[4,4]{0,1:T(4,128)}, f32[4,4]{0,1:T(4,128)S(1)}, u32[]{:S(2)}) copy-start(f32[4,4]{0,1:T(4,128)S(1)} %get-tuple-element.20) | copy-start | bytes 196
  43.8 2.2 copy-start.36
  47.2 3.1 %copy-start.30 = (pred[256]{0:T(512)(128)(4,1)S(1)}, pred[256]{0:T(512)(128)(4,1)}, u32[]{:S(2)}) copy-start(pred[256]{0:T(512)(128)(4,1)} %copy-done.29) | copy-start | bytes 772
  47.8 64.0 %copy-start.5 = (bf16[256,1024]{1,0:T(8,128)(2,1)S(1)}, bf16[256,1024]{1,0:T(8,128)(2,1)}, u32[]{:S(2)}) copy-start(bf16[256,1024]{1,0:T(8,128)(2,1)} %param.17) | copy-start | bytes 1572868
  49.2 3.2 %copy-start.27 = (bf16[4,64,1]{1,2,0:T(2,128)(2,1)}, bf16[4,64,1]{1,2,0:T(2,128)(2,1)S(1)}, u32[]{:S(2)}) copy-start(bf16[4,64,1]{1,2,0:T(2,128)(2,1)S(1)} %reshape.1094) | copy-start | bytes 1540
  71.6 13.1 %copy-start.17 = (f32[4,4]{0,1:T(4,128)}, f32[4,4]{0,1:T(4,128)S(1)}, u32[]{:S(2)}) copy-start(f32[4,4]{0,1:T(4,128)S(1)} %get-tuple-element.26) | copy-start | bytes 196
  133.5 4.2 %copy-start.9 = (bf16[1,1,513,512]{2,3,1,0:T(8,128)(2,1)}, bf16[1,1,513,512]{2,3,1,0:T(8,128)(2,1)S(1)}, u32[]{:S(2)}) copy-start(bf16[1,1,513,512]{2,3,1,0:T(8,128)(2,1)S(1)} %all_gather.34) | copy-start | bytes 1575940
  134.3 3.4 %copy-start.19 = (pred[256]{0:T(512)(128)(4,1)S(1)}, pred[256]{0:T(512)(128)(4,1)}, u32[]{:S(2)}) copy-start(pred[256]{0:T(512)(128)(4,1)} %iota_compare_fusion.1) | copy-start | bytes 772
  134.3 3.4 %copy-start.24 = (f32[256]{0:T(256)S(1)}, f32[256]{0:T(256)}, u32[]{:S(2)}) copy-start(f32[256]{0:T(256)} %copy-done.23) | copy-start | bytes 3076
  134.3 3.4 %copy-start.26 = (f32[256]{0:T(256)S(1)}, f32[256]{0:T(256)}, u32[]{:S(2)}) copy-start(f32[256]{0:T(256)} %copy-done.25) | copy-start | bytes 3076
  134.3 3.4 %copy-start.37 = (f32[1024]{0:T(1024)S(1)}, f32[1024]{0:T(1024)}, u32[]{:S(2)}) copy-start(f32[1024]{0:T(1024)} %param.15) | copy-start | bytes 12292
  134.3 3.4 %copy-start.45 = (f32[1024]{0:T(1024)S(1)}, f32[1024]{0:T(1024)}, u32[]{:S(2)}) copy-start(f32[1024]{0:T(1024)} %get-tuple-element.30) | copy-start | bytes 12292
  137.7 5.1 %copy-start.8 = (bf16[256,1024]{1,0:T(8,128)(2,1)S(1)}, bf16[256,1024]{1,0:T(8,128)(2,1)}, u32[]{:S(2)}) copy-start(bf16[256,1024]{1,0:T(8,128)(2,1)} %param.14) | copy-start | bytes 1572868
  144.7 2.1 copy-start.43
  144.7 2.3 copy-start.16
  144.7 3.2 %copy-start.3 = (f32[4,256,256]{1,2,0:T(8,128)S(1)}, f32[4,256,256]{1,2,0:T(8,128)}, u32[]{:S(2)}) copy-start(f32[4,256,256]{1,2,0:T(8,128)} %copy-done.1) | copy-start | bytes 3145732
  144.7 3.2 %copy-start.21 = (f32[4,256]{1,0:T(4,128)S(1)}, f32[4,256]{1,0:T(4,128)}, u32[]{:S(2)}) copy-start(f32[4,256]{1,0:T(4,128)} %broadcast_select_fusion.1) | copy-start | bytes 12292
  149.2 11.8 %copy-start.39 = (bf16[4,4]{0,1:T(4,128)(2,1)S(1)}, bf16[4,4]{0,1:T(4,128)(2,1)}, u32[]{:S(2)}) copy-start(bf16[4,4]{0,1:T(4,128)(2,1)} %get-tuple-element.18) | copy-start | bytes 100
  149.2 11.9 %copy-start.41 = (bf16[4,4,64]{2,1,0:T(4,128)(2,1)S(1)}, bf16[4,4,64]{2,1,0:T(4,128)(2,1)}, u32[]{:S(2)}) copy-start(bf16[4,4,64]{2,1,0:T(4,128)(2,1)} %copy-done.40) | copy-start | bytes 6148
  149.5 11.9 %copy-start.12 = (f32[4,64,256]{2,1,0:T(8,128)S(1)}, f32[4,64,256]{2,1,0:T(8,128)}, u32[]{:S(2)}) copy-start(f32[4,64,256]{2,1,0:T(8,128)} %fusion.38) | copy-start | bytes 786436
  149.5 12.1 %copy-start.7 = (bf16[1,1,256,1024]{3,2,1,0:T(8,128)(2,1)S(1)}, bf16[1,1,256,1024]{3,2,1,0:T(8,128)(2,1)}, u32[]{:S(2)}) copy-start(bf16[1,1,256,1024]{3,2,1,0:T(8,128)(2,1)} %param.10) | copy-start | bytes 1572868
  163.3 61.6 %all-reduce.10.cloned.1.call-start = ((), (), s32[]{:S(2)}) async-start(), calls=%async_computation.5 | async-start | bytes 786432 | tf_op jit(solution)/shard_map/psum | solution.py:273
  (20 other events, 25.9 us)
Sparse Core Ops, SparseCore 0:
  8.9 10.4 all-gather.3
  20.9 10.1 all-gather.5
  32.7 12.8 all-gather.7
  163.5 33.4 reduce-scatter.5
  199.1 25.7 all-reduce.9

commit v2 on v1

--- a/solution.py
+++ b/solution.py
@@ -49,6 +49,28 @@
     cross_exp = jnp.exp(cross_scores - peak)
     totals = (jnp.sum(own_exp, -1) + jnp.sum(cross_exp, -1))[..., None]
     return (own_exp / totals, cross_exp / totals)
+
+
+def gather_cand(block, axis):
+    count = lax.axis_size("cand")
+    if count > 8:
+        return lax.all_gather(block, "cand", axis=axis, tiled=True)
+    me = lax.axis_index("cand")
+    parts = [block] + [
+        lax.ppermute(block, "cand", [(j, (j + k) % count) for j in range(count)])
+        for k in range(1, count)
+    ]
+    ordered = jnp.take(jnp.stack(parts, 0), (me - jnp.arange(count)) % count, axis=0)
+    ordered = jnp.moveaxis(ordered, 0, axis)
+    shape = block.shape[:axis] + (count * block.shape[axis],) + block.shape[axis + 1 :]
+    return ordered.reshape(shape)
+
+
+def sum_query(block):
+    if lax.axis_size("query") != 2:
+        return lax.psum(block, "query")
+    other = lax.ppermute(block, "query", [(0, 1), (1, 0)])
+    return block.astype(jnp.float32) + other.astype(jnp.float32)
 
 
 def local(
@@ -80,15 +102,11 @@
     last_full = lax.all_gather(w_last, "mp", axis=2, tiled=True)
     out_last_full = lax.all_gather(w_out_last, "mp", axis=0, tiled=True)
     teacher_all = lax.all_gather(teacher, "cand", axis=1, tiled=True)
+    cls_tokens = gather_cand(tokens[:, :, 0], 1)
     projected = mixed("qcsd,kdf->kqcsf", tokens, w_first).astype(jnp.bfloat16)
-    gathered_kv = lax.all_gather(
-        jnp.concatenate([projected[1][:, :, 0], projected[2][:, :, 0]], -1),
-        "cand",
-        axis=1,
-        tiled=True,
-    )
-    gathered_keys = gathered_kv[..., :local_width]
-    gathered_vals = gathered_kv[..., local_width:]
+    cls_projected = mixed("qcd,kdf->kqcf", cls_tokens, w_first[1:]).astype(jnp.bfloat16)
+    gathered_keys = cls_projected[0]
+    gathered_vals = cls_projected[1]
     first_query = projected[0].reshape(head_shape)
     first_keys = projected[1].reshape(head_shape)
     first_vals = projected[2].reshape(head_shape)
@@ -251,27 +269,27 @@
     cls_val_first = mixed("qchd,qche->qdhe", cross_weight, grad_mixed_first[:, :, 0]).reshape(
         lists, cand_count, local_width
     )
-    back_key_first, back_val_first = (
-        lax.psum_scatter(cls_key_first, "cand", scatter_dimension=1, tiled=True),
-        lax.psum_scatter(cls_val_first, "cand", scatter_dimension=1, tiled=True),
-    )
-    key_first = jnp.where(first_cols, key_first + back_key_first[:, :, None], key_first).astype(
-        jnp.bfloat16
-    )
-    val_first = jnp.where(first_cols, val_first + back_val_first[:, :, None], val_first).astype(
-        jnp.bfloat16
-    )
+    key_first = key_first.astype(jnp.bfloat16)
+    val_first = val_first.astype(jnp.bfloat16)
     row_count = lists * local_cands * seq_len
     stacked = jnp.stack([query_grad, key_first, val_first], 3).reshape(row_count, 3, local_width)
-    flat_tokens = tokens.reshape(row_count, model_width)
+    cross_rows = lists * cand_count
+    cross_stacked = jnp.stack(
+        [jnp.zeros_like(cls_key_first), cls_key_first, cls_val_first], 2
+    ).astype(jnp.bfloat16)
+    all_rows = jnp.concatenate(
+        [stacked, cross_stacked.reshape(cross_rows, 3, local_width)], 0
+    )
+    all_tokens = jnp.concatenate(
+        [tokens.reshape(row_count, model_width), cls_tokens.reshape(cross_rows, model_width)], 0
+    )
     partial_grad = lax.psum_scatter(
-        mixed("rd,rkf->dkf", flat_tokens, stacked).astype(jnp.bfloat16),
+        mixed("rd,rkf->dkf", all_tokens, all_rows).astype(jnp.bfloat16),
         "cand",
         scatter_dimension=0,
         tiled=True,
     )
-    result = lax.psum(partial_grad, "query")
-    return result.astype(jnp.float32)
+    return sum_query(partial_grad).astype(jnp.float32)
 
 
 def solution(mesh):

time: 237 us -> 177 us (0.75)
  the two profiles are of different devices: /device:TPU:8 before, /device:TPU:0 now
where the time goes in v2:
time: 177 us; the launch traced here: 176 us
  waiting for transfers between devices  45.5 us (26%)
  blocking collectives  38.1 us (22%)
  other arithmetic  25.1 us (14%)
  matrix products  20.8 us (12%)
  between operations  20.7 us (12%)
  local copies, waits for them, and re-layouts  17.9 us (10%)
  starting transfers between devices  7.66 us (4%)
    reduce_scatter x1, waiting for transfers between devices, local(): lax.psum_scatter(mixed('rd,rkf->dkf', all_tokens, all_rows).astype(jnp.bf...  34.7 us
    dot_general x30, matrix products, mixed(): jnp.einsum(pattern, former, latter, preferred_element_type=jnp.float32)  20.8 us
    all_gather x1, blocking collectives, local(): lax.all_gather(jnp.concatenate([last_kv[0][:, :, 0], last_kv[1][:, :, 0]]...  11.9 us
    psum x1, blocking collectives, local(): score_totals = lax.psum(jnp.sum(score_exp, 1), 'cand')  11.2 us
    ppermute x1, waiting for transfers between devices, sum_query(): other = lax.ppermute(block, 'query', [(0, 1), (1, 0)])  9.41 us
    unnamed x1, blocking collectives  8.94 us
    unnamed x86, local copies, waits for them, and re-layouts  6.25 us
    ppermute x3, starting transfers between devices, gather_cand(): lax.ppermute(block, 'cand', [(j, (j + k) % count) for j in range(count)])  6.06 us
  transfers between devices with their start and end apart: 8, of which 2 were waited for; matrix products, arithmetic and copies ran while one was open for 27% of the time, Pallas kernels for 0%

profile of v2, /device:TPU:0, one launch (start us, length us, event | category | flops | bytes accessed | tf_op | source)
XLA Modules:
  0.0 175.8 jit_solution(16031980861146810389)
XLA Ops:
  8.8 5.0 %collective-permute-start.2 = (bf16[1,1,1024]{2,1,0:T(2,128)(2,1)S(1)}, bf16[1,1,1024]{2,1,0:T(2,128)(2,1)}, u32[]{:S(2)}, u32[]{:S(2)}) collective-permute-start(bf16[1,1,1024]{2,1,0:T(2,128)(2,1)S(1)} %get-tuple-element.29), channel_id=1, source_target_pairs={{0,12},{4,0},{8,4},{12,8},{1,13},{5,1},{9,5},{13,9},{2,14},{6,2},{... | collective-permute-start | bytes 6152 | tf_op jit(solution)/shard_map/ppermute | solution.py:60
  13.8 1.0 collective-permute-start
  18.2 0.9 fusion.119
  21.0 1.4 fusion.118
  32.1 0.9 fusion.37
  33.1 2.0 %all_gather.24 = bf16[1,1,256,512]{2,3,1,0:T(8,128)(2,1)S(1)} all-gather(bf16[1,1,256,256]{2,3,1,0:T(8,128)(2,1)S(1)} %bitcast.344), channel_id=1, replica_groups=mesh['groups'=2,'cand'=4,'query'=2,'mp'=2] {'mp'}, dimensions={3}, use_global_device_ids=true | all-gather | bytes 393216 | tf_op jit(solution)/shard_map/all_gather | solution.py:128
  35.1 1.8 %fusion.120 = (f32[256]{0:T(256)S(1)}, f32[1,1,256,1024]{3,2,1,0:T(8,128)S(1)}) fusion(bf16[512,1024]{1,0:T(8,128)(2,1)} %all-gather.4.cloned.1.call-done, bf16[1,1,256,512]{2,3,1,0:T(8,128)(2,1)S(1)} %all_gather.24, bf16[1,1,256,1024]{3,2,1,0:T(8,128)(2,1)S(1)} %copy-done.4), kind=kOutput, calls=%fused_computation.222 | convolution fusion | flops 269221632 | bytes 2884608 | tf_op jit(solution)/shard_map/qcsf,fd->qcsd/dot_general | solution.py:15
  40.2 1.0 copy.83
  41.4 1.2 fusion.96
  44.0 11.9 %all_gather.26 = bf16[1,4,512]{2,0,1:T(2,128)(2,1)S(1)} all-gather(bf16[1,1,512]{2,0,1:T(2,128)(2,1)S(1)} %pad_maximum_fusion.1), channel_id=1, replica_groups=mesh['groups'=2,'cand'=4,'query'=2,'mp'=2] {'cand'}, dimensions={1}, use_global_device_ids=true | all-gather | bytes 5120 | tf_op jit(solution)/shard_map/all_gather | solution.py:136
  56.5 1.3 reshape.969
  57.8 1.4 fusion.64
  61.6 1.3 convert_convert_fusion
  62.8 1.3 convert_convert_fusion.1
  64.3 1.0 copy.84
  67.2 1.8 %all_gather.27 = bf16[1,1,512]{2,1,0:T(2,128)(2,1)S(1)} all-gather(bf16[1,1,256]{2,1,0:T(2,128)(2,1)S(1)} %convert_element_type.228), channel_id=1, replica_groups=mesh['groups'=2,'cand'=4,'query'=2,'mp'=2] {'mp'}, dimensions={2}, use_global_device_ids=true | all-gather | bytes 1536 | tf_op jit(solution)/shard_map/all_gather | solution.py:160
  69.0 1.5 fusion.78
  73.0 1.3 multiply_reduce_fusion.2
  75.0 11.2 %all-reduce.4 = (f32[1,1]{1,0:T(1,128)}, f32[4]{0:T(128)S(1)}) all-reduce(f32[1,1]{1,0:T(1,128)} %bitcast.62, f32[4]{0:T(128)} %copy-done.38), channel_id=1, replica_groups=mesh['groups'=2,'cand'=4,'query'=2,'mp'=2] {'cand'}, use_global_device_ids=true, to_apply=%region_12.13 | all-reduce | flops 5 | bytes 40 | tf_op jit(solution)/shard_map/psum | solution.py:170
  87.5 1.3 exponential_reduce_fusion
  90.3 1.4 fusion.104
  95.7 8.9 %all-reduce.3 = (f32[1,4,256]{2,1,0:T(4,128)S(1)}, f32[1,4,256]{2,1,0:T(4,128)S(1)}) all-reduce(f32[1,4,256]{2,1,0:T(4,128)S(1)} %reshape.977, f32[1,4,256]{2,1,0:T(4,128)S(1)} %reshape.975), channel_id=3, replica_groups=mesh['groups'=2,'cand'=4,'query'=2,'mp'=2] {'cand'}, use_global_device_ids=true, to_apply=%region_20.21.clone | all-reduce | flops 2048 | bytes 16384
  106.2 2.3 %all_gather.30 = bf16[1,1,513,512]{2,3,1,0:T(8,128)(2,1)S(1)} all-gather(bf16[1,1,513,256]{2,3,1,0:T(8,128)(2,1)S(1)} %pad_maximum_fusion), channel_id=1, replica_groups=mesh['groups'=2,'cand'=4,'query'=2,'mp'=2] {'mp'}, dimensions={3}, use_global_device_ids=true | all-gather | bytes 787968 | tf_op jit(solution)/shard_map/all_gather | solution.py:222
  108.6 1.8 %fusion.8 = f32[256,1024]{1,0:T(8,128)S(1)} fusion(bf16[3,1024,512]{2,1,0:T(8,128)(2,1)} %all-gather.8.cloned.1.call-done, bf16[1,1,513,512]{2,3,1,0:T(8,128)(2,1)S(1)} %all_gather.30), kind=kOutput, calls=%fused_computation.26 | convolution fusion | flops 268435456 | bytes 2359296 | tf_op jit(solution)/shard_map/qcsf,df->qcsd/dot_general | solution.py:15
  110.4 1.6 fusion.7
  112.1 2.2 %fusion.9 = (f32[256]{0:T(256)S(1)}, f32[256,1024]{1,0:T(8,128)S(1)}) fusion(f32[1,1,256,1024]{3,2,1,0:T(8,128)S(1)} %get-tuple-element.47, f32[256]{0:T(256)S(1)} %copy-done.22, f32[256]{0:T(256)S(1)} %copy-done.18, f32[1024]{0:T(1024)S(1)} %copy-done.27, f32[1024]{0:T(1024)S(1)} %copy-done.34, f32[1024]{0:T(1024)S(1)} %bitcast.351, ...), kind=kOutput, calls=%fused_computation.28 | convolution fusion | flops 271056640 | bytes 4472064 | tf_op jit(solution)/shard_map/qcsf,df->qcsd/dot_general | solution.py:15
  114.4 1.6 convolution_convert_fusion.4
  119.4 2.3 %convolution_convert_fusion = bf16[1024,3,256]{2,0,1:T(8,128)(2,1)} fusion(bf16[4,1024]{1,0:T(4,128)(2,1)S(1)} %copy-done.9, bf16[256,1024]{1,0:T(8,128)(2,1)S(1)} %bitcast.329, bf16[4,1,256]{2,0,1:T(4,128)(2,1)S(1)} %stack.30, bf16[4,1,256]{2,0,1:T(4,128)(2,1)S(1)} %stack.29, bf16[256,3,256]{2,0,1:T(8,128)(2,1)S(1)} %maximum_bitcast_fusion.2, ...), kind=kOutput, calls=%fused_computation.1 | convolution fusion | flops 412393472 | bytes 2504216 | tf_op jit(solution)/shard_map/rd,rkf->dkf/dot_general | solution.py:15
  121.7 34.7 %reduce-scatter.4.cloned.1.call-done = bf16[256,3,256]{2,0,1:T(8,128)(2,1)} async-done(((bf16[1024,3,256]{2,0,1:T(8,128)(2,1)}), bf16[256,3,256]{2,0,1:T(8,128)(2,1)}) %reduce-scatter.4.cloned.1.call-update) | async-done | bytes 393232 | tf_op jit(solution)/shard_map/reduce_scatter | solution.py:286
  156.4 1.5 collective-permute-start.3
  157.9 9.4 %collective-permute-done.3 = bf16[256,3,256]{2,0,1:T(8,128)(2,1)S(1)} collective-permute-done((bf16[256,3,256]{2,0,1:T(8,128)(2,1)}, bf16[256,3,256]{2,0,1:T(8,128)(2,1)S(1)}, u32[]{:S(2)}, u32[]{:S(2)}) %collective-permute-start.3) | collective-permute-done | bytes 393248 | tf_op jit(solution)/shard_map/ppermute | solution.py:72
  167.3 2.0 %convert_add_fusion = f32[256,3,256]{2,0,1:T(8,128)} fusion(bf16[256,3,256]{2,0,1:T(8,128)(2,1)S(1)} %collective-permute-done.3, bf16[256,3,256]{2,0,1:T(8,128)(2,1)} %reduce-scatter.4.cloned.1.call-done), kind=kLoop, calls=%fused_computation.42 | loop fusion | flops 589824 | bytes 1572864 | tf_op jit(solution)/shard_map/add | solution.py:73
  (223 shorter events, 34.8 us)
Async XLA Ops:
  6.5 9.6 %copy-start.4 = (bf16[1,1,256,1024]{3,2,1,0:T(8,128)(2,1)S(1)}, bf16[1,1,256,1024]{3,2,1,0:T(8,128)(2,1)}, u32[]{:S(2)}) copy-start(bf16[1,1,256,1024]{3,2,1,0:T(8,128)(2,1)} %param.10) | copy-start | bytes 1572868
  6.5 9.6 %copy-start.3 = (bf16[3,1024,256]{2,1,0:T(8,128)(2,1)S(1)}, bf16[3,1024,256]{2,1,0:T(8,128)(2,1)}, u32[]{:S(2)}) copy-start(bf16[3,1024,256]{2,1,0:T(8,128)(2,1)} %param.13) | copy-start | bytes 4718596
  6.5 28.6 %all-gather.4.cloned.1.call-start = ((), (), s32[]{:S(2)}) async-start(), calls=%async_computation.1 | async-start | bytes 1572864 | tf_op jit(solution)/shard_map/all_gather | solution.py:101
  7.3 61.7 %all-gather.6.cloned.1.call-start = ((), (), s32[]{:S(2)}) async-start(), calls=%async_computation.2 | async-start | bytes 1572864 | tf_op jit(solution)/shard_map/all_gather | solution.py:103
  8.0 100.6 %all-gather.8.cloned.1.call-start = ((), (), s32[]{:S(2)}) async-start(), calls=%async_computation.3 | async-start | bytes 4718592 | tf_op jit(solution)/shard_map/all_gather | solution.py:102
  8.8 14.2 %collective-permute-start.2 = (bf16[1,1,1024]{2,1,0:T(2,128)(2,1)S(1)}, bf16[1,1,1024]{2,1,0:T(2,128)(2,1)}, u32[]{:S(2)}, u32[]{:S(2)}) collective-permute-start(bf16[1,1,1024]{2,1,0:T(2,128)(2,1)S(1)} %get-tuple-element.29), channel_id=1, source_target_pairs={{0,12},{4,0},{8,4},{12,8},{1,13},{5,1},{9,5},{13,9},{2,14},{6,2},{... | collective-permute-start | bytes 6152 | tf_op jit(solution)/shard_map/ppermute | solution.py:60
  13.8 9.2 %collective-permute-start.1 = (bf16[1,1,1024]{2,1,0:T(2,128)(2,1)S(1)}, bf16[1,1,1024]{2,1,0:T(2,128)(2,1)}, u32[]{:S(2)}, u32[]{:S(2)}) collective-permute-start(bf16[1,1,1024]{2,1,0:T(2,128)(2,1)S(1)} %get-tuple-element.29), channel_id=1, source_target_pairs={{0,8},{4,12},{8,0},{12,4},{1,9},{5,13},{9,1},{13,5},{2,10},{6,14},... | collective-permute-start | bytes 6152 | tf_op jit(solution)/shard_map/ppermute | solution.py:60
  13.8 9.2 %collective-permute-start = (bf16[1,1,1024]{2,1,0:T(2,128)(2,1)S(1)}, bf16[1,1,1024]{2,1,0:T(2,128)(2,1)}, u32[]{:S(2)}, u32[]{:S(2)}) collective-permute-start(bf16[1,1,1024]{2,1,0:T(2,128)(2,1)S(1)} %get-tuple-element.29), channel_id=1, source_target_pairs={{0,4},{4,8},{8,12},{12,0},{1,5},{5,9},{9,13},{13,1},{2,6},{6,10},{... | collective-permute-start | bytes 6152 | tf_op jit(solution)/shard_map/ppermute | solution.py:60
  14.9 141.5 %reduce-scatter.4.cloned.1.call-start = ((), (), s32[]{:S(2)}) async-start(), calls=%async_computation.4 | async-start | bytes 1966080 | tf_op jit(solution)/shard_map/reduce_scatter | solution.py:286
  16.8 15.3 %copy-start.6 = (bf16[1,1,1,256,256]{3,4,0,2,1:T(8,128)(2,1)}, bf16[1,1,1,256,256]{3,4,0,2,1:T(8,128)(2,1)S(1)}, u32[]{:S(2)}) copy-start(bf16[1,1,1,256,256]{3,4,0,2,1:T(8,128)(2,1)S(1)} %get-tuple-element.30) | copy-start | bytes 393220
  17.0 6.1 %copy-start.28 = (bf16[1,1,1,4,64]{4,3,2,1,0:T(4,128)(2,1)}, bf16[1,1,1,4,64]{4,3,2,1,0:T(4,128)(2,1)S(1)}, u32[]{:S(2)}) copy-start(bf16[1,1,1,4,64]{4,3,2,1,0:T(4,128)(2,1)S(1)} %copy.132) | copy-start | bytes 1540
  17.6 5.4 %copy-start.23 = (pred[256]{0:T(512)(128)(4,1)}, pred[256]{0:T(512)(128)(4,1)S(1)}, u32[]{:S(2)}) copy-start(pred[256]{0:T(512)(128)(4,1)S(1)} %iota_compare_fusion) | copy-start | bytes 772
  25.7 7.3 %copy-start.8 = (bf16[4,1024]{1,0:T(4,128)(2,1)}, bf16[4,1024]{1,0:T(4,128)(2,1)S(1)}, u32[]{:S(2)}) copy-start(bf16[4,1024]{1,0:T(4,128)(2,1)S(1)} %broadcast_select_fusion) | copy-start | bytes 24580
  25.7 4.7 %copy-start.12 = (pred[4]{0:T(512)(128)(4,1)S(1)}, pred[4]{0:T(512)(128)(4,1)}, u32[]{:S(2)}) copy-start(pred[4]{0:T(512)(128)(4,1)} %get-tuple-element.53) | copy-start | bytes 16
  35.1 2.1 %copy-start.26 = (f32[1024]{0:T(1024)S(1)}, f32[1024]{0:T(1024)}, u32[]{:S(2)}) copy-start(f32[1024]{0:T(1024)} %param.15) | copy-start | bytes 12292
  36.9 1.8 %copy-start.17 = (f32[256]{0:T(256)}, f32[256]{0:T(256)S(1)}, u32[]{:S(2)}) copy-start(f32[256]{0:T(256)S(1)} %broadcast_multiply_fusion.3) | copy-start | bytes 3076
  38.3 21.7 %copy-start.13 = (pred[4]{0:T(512)(128)(4,1)S(1)}, pred[4]{0:T(512)(128)(4,1)}, u32[]{:S(2)}) copy-start(pred[4]{0:T(512)(128)(4,1)} %get-tuple-element.53) | copy-start | bytes 16
  38.9 54.7 %copy-start.1 = (bf16[256,1024]{1,0:T(8,128)(2,1)S(1)}, bf16[256,1024]{1,0:T(8,128)(2,1)}, u32[]{:S(2)}) copy-start(bf16[256,1024]{1,0:T(8,128)(2,1)} %param.17) | copy-start | bytes 1572868
  64.2 30.3 %copy-start.10 = (f32[4,4]{0,1:T(4,128)S(1)}, f32[4,4]{0,1:T(4,128)}, u32[]{:S(2)}) copy-start(f32[4,4]{0,1:T(4,128)} %get-tuple-element.20) | copy-start | bytes 196
  64.2 30.0 %copy-start.37 = (bf16[256]{0:T(256)(128)(2,1)S(1)}, bf16[256]{0:T(256)(128)(2,1)}, u32[]{:S(2)}) copy-start(bf16[256]{0:T(256)(128)(2,1)} %copy-done.36) | copy-start | bytes 1540
  64.2 30.6 %copy-start.33 = (bf16[4,4,64]{2,1,0:T(4,128)(2,1)S(1)}, bf16[4,4,64]{2,1,0:T(4,128)(2,1)}, u32[]{:S(2)}) copy-start(bf16[4,4,64]{2,1,0:T(4,128)(2,1)} %reshape.969) | copy-start | bytes 6148
  64.2 31.1 %copy-start.25 = (f32[4,4]{0,1:T(4,128)S(1)}, f32[4,4]{0,1:T(4,128)}, u32[]{:S(2)}) copy-start(f32[4,4]{0,1:T(4,128)} %get-tuple-element.19) | copy-start | bytes 196
  64.2 41.6 %copy-start.14 = (f32[4,256]{1,0:T(4,128)S(1)}, f32[4,256]{1,0:T(4,128)}, u32[]{:S(2)}) copy-start(f32[4,256]{1,0:T(4,128)} %get-tuple-element.21) | copy-start | bytes 12292
  64.2 41.7 %copy-start.19 = (pred[256]{0:T(512)(128)(4,1)S(1)}, pred[256]{0:T(512)(128)(4,1)}, u32[]{:S(2)}) copy-start(pred[256]{0:T(512)(128)(4,1)} %iota_compare_fusion.1) | copy-start | bytes 772
  108.4 3.6 %copy-start.2 = (bf16[1,1,513,512]{2,3,1,0:T(8,128)(2,1)}, bf16[1,1,513,512]{2,3,1,0:T(8,128)(2,1)S(1)}, u32[]{:S(2)}) copy-start(bf16[1,1,513,512]{2,3,1,0:T(8,128)(2,1)S(1)} %all_gather.30) | copy-start | bytes 1575940
  108.6 3.5 %copy-start.18 = (f32[256]{0:T(256)S(1)}, f32[256]{0:T(256)}, u32[]{:S(2)}) copy-start(f32[256]{0:T(256)} %copy-done.17) | copy-start | bytes 3076
  108.6 3.5 %copy-start.20 = (pred[256]{0:T(512)(128)(4,1)S(1)}, pred[256]{0:T(512)(128)(4,1)}, u32[]{:S(2)}) copy-start(pred[256]{0:T(512)(128)(4,1)} %iota_compare_fusion.1) | copy-start | bytes 772
  108.6 3.5 %copy-start.22 = (f32[256]{0:T(256)S(1)}, f32[256]{0:T(256)}, u32[]{:S(2)}) copy-start(f32[256]{0:T(256)} %copy-done.21) | copy-start | bytes 3076
  108.6 3.5 %copy-start.27 = (f32[1024]{0:T(1024)S(1)}, f32[1024]{0:T(1024)}, u32[]{:S(2)}) copy-start(f32[1024]{0:T(1024)} %param.15) | copy-start | bytes 12292
  108.6 3.5 %copy-start.34 = (f32[1024]{0:T(1024)S(1)}, f32[1024]{0:T(1024)}, u32[]{:S(2)}) copy-start(f32[1024]{0:T(1024)} %get-tuple-element.24) | copy-start | bytes 12292
  114.4 1.6 copy-start.16
  156.4 10.9 %collective-permute-start.3 = (bf16[256,3,256]{2,0,1:T(8,128)(2,1)}, bf16[256,3,256]{2,0,1:T(8,128)(2,1)S(1)}, u32[]{:S(2)}, u32[]{:S(2)}) collective-permute-start(bf16[256,3,256]{2,0,1:T(8,128)(2,1)} %reduce-scatter.4.cloned.1.call-done), channel_id=1, source_target_pairs={{0,2},{2,0},{1,3},{3,1},{4,6},{6,4},{5,7},{7,5},{8,10},{10,8},{9,1... | collective-permute-start | bytes 1179656 | tf_op jit(solution)/shard_map/ppermute | solution.py:72
  (15 other events, 16.6 us)
Sparse Core Ops, SparseCore 0:
  8.9 11.7 all-gather.3
  22.2 10.1 all-gather.5
  34.0 12.8 all-gather.7
  121.8 34.4 reduce-scatter.3

commit v3 on v2

--- a/solution.py
+++ b/solution.py
@@ -64,6 +64,29 @@
     ordered = jnp.moveaxis(ordered, 0, axis)
     shape = block.shape[:axis] + (count * block.shape[axis],) + block.shape[axis + 1 :]
     return ordered.reshape(shape)
+
+
+def sum_cand(block):
+    count = lax.axis_size("cand")
+    if count > 8:
+        return lax.psum(block, "cand")
+    total = block
+    for k in range(1, count):
+        total = total + lax.ppermute(block, "cand", [(j, (j + k) % count) for j in range(count)])
+    return total
+
+
+def scatter_cand(block, axis):
+    count = lax.axis_size("cand")
+    if count > 8:
+        return lax.psum_scatter(block, "cand", scatter_dimension=axis, tiled=True)
+    me = lax.axis_index("cand")
+    width = block.shape[axis] // count
+    total = lax.dynamic_slice_in_dim(block, me * width, width, axis)
+    for k in range(1, count):
+        piece = lax.dynamic_slice_in_dim(block, ((me + k) % count) * width, width, axis)
+        total = total + lax.ppermute(piece, "cand", [(j, (j + k) % count) for j in range(count)])
+    return total
 
 
 def sum_query(block):
@@ -101,7 +124,7 @@
     out_first_full = lax.all_gather(w_out_first, "mp", axis=0, tiled=True)
     last_full = lax.all_gather(w_last, "mp", axis=2, tiled=True)
     out_last_full = lax.all_gather(w_out_last, "mp", axis=0, tiled=True)
-    teacher_all = lax.all_gather(teacher, "cand", axis=1, tiled=True)
+    teacher_all = gather_cand(teacher, 1)
     cls_tokens = gather_cand(tokens[:, :, 0], 1)
     projected = mixed("qcsd,kdf->kqcsf", tokens, w_first).astype(jnp.bfloat16)
     cls_projected = mixed("qcd,kdf->kqcf", cls_tokens, w_first[1:]).astype(jnp.bfloat16)
@@ -133,11 +156,8 @@
     hidden = normed_first.astype(jnp.bfloat16)
     last_query = mixed("qcd,df->qcf", hidden[:, :, 0], w_last[0]).astype(jnp.bfloat16)
     last_kv = mixed("qcsd,kdf->kqcsf", hidden, w_last[1:]).astype(jnp.bfloat16)
-    gathered_kv_last = lax.all_gather(
-        jnp.concatenate([last_kv[0][:, :, 0], last_kv[1][:, :, 0]], -1),
-        "cand",
-        axis=1,
-        tiled=True,
+    gathered_kv_last = gather_cand(
+        jnp.concatenate([last_kv[0][:, :, 0], last_kv[1][:, :, 0]], -1), 1
     )
     gathered_keys_last = gathered_kv_last[..., :local_width]
     gathered_vals_last = gathered_kv_last[..., local_width:]
@@ -167,7 +187,7 @@
     teacher_peak = jnp.max(teacher_all, 1)
     teacher_exp = jnp.exp(teacher - teacher_peak[:, None])
     teacher_totals = jnp.sum(jnp.exp(teacher_all - teacher_peak[:, None]), 1)
-    score_totals = lax.psum(jnp.sum(score_exp, 1), "cand")
+    score_totals = sum_cand(jnp.sum(score_exp, 1))
     student_prob = score_exp / score_totals[:, None]
     teacher_prob = teacher_exp / teacher_totals[:, None]
     score_grad = LOSS_SCALE * (student_prob - teacher_prob) / query_count
@@ -208,10 +228,9 @@
     cls_val_terms = mixed("qchd,qche->qdhe", cross_last_weight, grad_mixed_last).reshape(
         lists, cand_count, local_width
     )
-    back_keys, back_vals = (
-        lax.psum_scatter(cls_key_terms, "cand", scatter_dimension=1, tiled=True),
-        lax.psum_scatter(cls_val_terms, "cand", scatter_dimension=1, tiled=True),
-    )
+    back_terms = scatter_cand(jnp.concatenate([cls_key_terms, cls_val_terms], -1), 1)
+    back_keys = back_terms[..., :local_width]
+    back_vals = back_terms[..., local_width:]
     first_cols = first_mask[None, None, :, None]
     key_grad = jnp.where(first_cols, own_key_grad + back_keys[:, :, None], own_key_grad).astype(
         jnp.bfloat16

time: 177 us -> 163 us (0.921)
  blocking collectives: 38.1 us -> 6.06 us
  starting transfers between devices: 7.66 us -> 25.6 us
  waiting for transfers between devices: 45.5 us -> 57.3 us
  local copies, waits for them, and re-layouts: 17.9 us -> 9.65 us
  other arithmetic: 25.1 us -> 22.7 us
    ppermute x0 -> x6, starting transfers between devices: none -> 11.9 us  [the longest x3 7.77 us: sum_cand(): lax.ppermute(block, 'cand', [(j, (j + k) % count) for j in range(count)])]
    all_gather x1 -> x0, blocking collectives: 11.9 us -> none  [local(): lax.all_gather(jnp.concatenate([last_kv[0][:, :, 0], last_kv[1][:, :, 0]]...]
    psum x1 -> x0, blocking collectives: 11.2 us -> none  [local(): score_totals = lax.psum(jnp.sum(score_exp, 1), 'cand')]
    unnamed x1 -> x0, blocking collectives: 8.94 us -> none
    ppermute x3 -> x9, waiting for transfers between devices: 0.01 us -> 8.81 us  [gather_cand(): lax.ppermute(block, 'cand', [(j, (j + k) % count) for j in range(count)])]
    ppermute x3 -> x9, starting transfers between devices: 6.06 us -> 12.1 us  [gather_cand(): lax.ppermute(block, 'cand', [(j, (j + k) % count) for j in range(count)])]
    ppermute x0 -> x6, waiting for transfers between devices: none -> 3.61 us  [the longest x3 3.61 us: scatter_cand(): lax.ppermute(piece, 'cand', [(j, (j + k) % count) for j in range(count)])]
    unnamed x86 -> x66, local copies, waits for them, and re-layouts: 6.25 us -> 2.78 us
  transfers between devices with their start and end apart: 8 -> 20, of which waited for: 2 -> 8; matrix products, arithmetic and copies ran while one was open for 27% -> 21% of each run, Pallas kernels for 0% -> 0%
where the time goes in v3:
time: 163 us; the launch traced here: 162 us
  waiting for transfers between devices  57.3 us (35%)
  starting transfers between devices  25.6 us (16%)
  other arithmetic  22.7 us (14%)
  between operations  21.8 us (13%)
  matrix products  19.1 us (12%)
  local copies, waits for them, and re-layouts  9.65 us (6%)
  blocking collectives  6.06 us (4%)
    reduce_scatter x1, waiting for transfers between devices, local(): lax.psum_scatter(mixed('rd,rkf->dkf', all_tokens, all_rows).astype(jnp.bf...  34 us
    dot_general x30, matrix products, mixed(): jnp.einsum(pattern, former, latter, preferred_element_type=jnp.float32)  19.1 us
    ppermute x9, starting transfers between devices, gather_cand(): lax.ppermute(block, 'cand', [(j, (j + k) % count) for j in range(count)])  12.1 us
    ppermute x1, waiting for transfers between devices, sum_query(): other = lax.ppermute(block, 'query', [(0, 1), (1, 0)])  9.43 us
    ppermute x9, waiting for transfers between devices, gather_cand(): lax.ppermute(block, 'cand', [(j, (j + k) % count) for j in range(count)])  8.81 us
    ppermute x3, starting transfers between devices, sum_cand(): lax.ppermute(block, 'cand', [(j, (j + k) % count) for j in range(count)])  7.77 us
    ppermute x3, starting transfers between devices, scatter_cand(): lax.ppermute(piece, 'cand', [(j, (j + k) % count) for j in range(count)])  4.1 us
    ppermute x3, waiting for transfers between devices, scatter_cand(): lax.ppermute(piece, 'cand', [(j, (j + k) % count) for j in range(count)])  3.61 us
  transfers between devices with their start and end apart: 20, of which 8 were waited for; matrix products, arithmetic and copies ran while one was open for 21% of the time, Pallas kernels for 0%

profile of v3, /device:TPU:0, one launch (start us, length us, event | category | flops | bytes accessed | tf_op | source)
XLA Modules:
  0.0 162.2 jit_solution(13944407680088185383)
XLA Ops:
  8.1 1.3 slice_bitcast_fusion.11
  9.4 5.0 %collective-permute-start.2 = (bf16[1,1,1024]{2,1,0:T(2,128)(2,1)}, bf16[1,1,1024]{2,1,0:T(2,128)(2,1)}, u32[]{:S(2)}, u32[]{:S(2)}) collective-permute-start(bf16[1,1,1024]{2,1,0:T(2,128)(2,1)} %get-tuple-element.23), channel_id=1, source_target_pairs={{0,12},{4,0},{8,4},{12,8},{1,13},{5,1},{9,5},{13,9},{2,14},{6,2},{... | collective-permute-start | bytes 6152 | tf_op jit(solution)/shard_map/ppermute | solution.py:60
  15.4 2.8 %collective-permute-start.11 = (f32[1,1]{1,0:T(1,128)}, f32[1,1]{1,0:T(1,128)}, u32[]{:S(2)}, u32[]{:S(2)}) collective-permute-start(f32[1,1]{1,0:T(1,128)} %param.12), channel_id=1, source_target_pairs={{0,12},{4,0},{8,4},{12,8},{1,13},{5,1},{9,5},{13,9},{2,14},{6,2},{... | collective-permute-start | bytes 20 | tf_op jit(solution)/shard_map/ppermute | solution.py:60
  18.3 1.1 collective-permute-start.10
  24.5 5.5 %collective-permute-done.9 = f32[1,1]{1,0:T(1,128)} collective-permute-done((f32[1,1]{1,0:T(1,128)}, f32[1,1]{1,0:T(1,128)}, u32[]{:S(2)}, u32[]{:S(2)}) %collective-permute-start.9) | collective-permute-done | bytes 36 | tf_op jit(solution)/shard_map/ppermute | solution.py:60
  30.1 1.9 %maximum_bitcast_fusion.5 = f32[4]{0:T(128)S(1)} fusion(f32[1,1,1]{0,2,1:T(1,128)} %bitcast.74, f32[1,1,1]{0,2,1:T(1,128)} %bitcast.73, f32[1,1,1]{0,2,1:T(1,128)} %bitcast.72, f32[1,1,1]{0,2,1:T(1,128)} %bitcast.337), kind=kLoop, calls=%fused_computation.210 | loop fusion | flops 12 | bytes 32 | tf_op jit(solution)/shard_map/stack | solution.py:63
  33.1 1.2 fusion.102
  34.3 1.8 %exponential_reduce_fusion = f32[]{:T(128)} fusion(f32[]{:T(128)} %fusion.102, f32[4]{0:T(128)} %gather_fusion.2, s32[]{:T(128)S(6)} %axis_index.11), kind=kLoop, calls=%fused_computation.211 | loop fusion | flops 83 | bytes 28 | tf_op jit(solution)/shard_map/reduce_sum | solution.py:189
  38.3 1.3 gather_fusion
  44.5 1.3 convert_bitcast_fusion.2
  47.9 2.0 %all_gather.18 = bf16[1,1,256,512]{2,3,1,0:T(8,128)(2,1)S(1)} all-gather(bf16[1,1,256,256]{2,3,1,0:T(8,128)(2,1)S(1)} %bitcast.360), channel_id=1, replica_groups=mesh['groups'=2,'cand'=4,'query'=2,'mp'=2] {'mp'}, dimensions={3}, use_global_device_ids=true | all-gather | bytes 393216 | tf_op jit(solution)/shard_map/all_gather | solution.py:151
  49.9 1.8 %fusion.123 = (f32[256]{0:T(256)S(1)}, f32[1,1,256,1024]{3,2,1,0:T(8,128)S(1)}) fusion(bf16[512,1024]{1,0:T(8,128)(2,1)} %all-gather.4.cloned.1.call-done, bf16[1,1,256,512]{2,3,1,0:T(8,128)(2,1)S(1)} %all_gather.18, bf16[1,1,256,1024]{3,2,1,0:T(8,128)(2,1)S(1)} %copy-done.4), kind=kOutput, calls=%fused_computation.236 | convolution fusion | flops 269221632 | bytes 2884608 | tf_op jit(solution)/shard_map/qcsf,fd->qcsd/dot_general | solution.py:15
  53.9 1.9 %collective-permute-start.3 = (bf16[1,1,512]{2,1,0:T(2,128)(2,1)S(1)}, bf16[1,1,512]{2,1,0:T(2,128)(2,1)S(1)}, u32[]{:S(2)}, u32[]{:S(2)}) collective-permute-start(bf16[1,1,512]{2,1,0:T(2,128)(2,1)S(1)} %pad_maximum_fusion.1), channel_id=1, source_target_pairs={{0,4},{4,8},{8,12},{12,0},{1,5},{5,9},{9,13},{13,1},{2,6},{6,10},{... | collective-permute-start | bytes 3080 | tf_op jit(solution)/shard_map/ppermute | solution.py:60
  58.4 1.4 collective-permute-done.3
  62.0 1.8 %all_gather.20 = bf16[1,1,512]{2,1,0:T(2,128)(2,1)S(1)} all-gather(bf16[1,1,256]{2,1,0:T(2,128)(2,1)S(1)} %convert_element_type.228), channel_id=1, replica_groups=mesh['groups'=2,'cand'=4,'query'=2,'mp'=2] {'mp'}, dimensions={2}, use_global_device_ids=true | all-gather | bytes 1536 | tf_op jit(solution)/shard_map/all_gather | solution.py:180
  63.8 1.5 fusion.78
  69.2 1.9 %collective-permute-start.6 = (f32[1]{0:T(128)}, f32[1]{0:T(128)}, u32[]{:S(2)}, u32[]{:S(2)}) collective-permute-start(f32[1]{0:T(128)} %bitcast.69), channel_id=1, source_target_pairs={{0,4},{4,8},{8,12},{12,0},{1,5},{5,9},{9,13},{13,1},{2,6},{6,10},{... | collective-permute-start | bytes 20 | tf_op jit(solution)/shard_map/ppermute | solution.py:75
  71.1 3.3 %collective-permute-start.7 = (f32[1]{0:T(128)}, f32[1]{0:T(128)}, u32[]{:S(2)}, u32[]{:S(2)}) collective-permute-start(f32[1]{0:T(128)} %bitcast.69), channel_id=1, source_target_pairs={{0,8},{4,12},{8,0},{12,4},{1,9},{5,13},{9,1},{13,5},{2,10},{6,14},... | collective-permute-start | bytes 20 | tf_op jit(solution)/shard_map/ppermute | solution.py:75
  74.4 2.6 %collective-permute-start.8 = (f32[1]{0:T(128)}, f32[1]{0:T(128)}, u32[]{:S(2)}, u32[]{:S(2)}) collective-permute-start(f32[1]{0:T(128)} %bitcast.69), channel_id=1, source_target_pairs={{0,12},{4,0},{8,4},{12,8},{1,13},{5,1},{9,5},{13,9},{2,14},{6,2},{... | collective-permute-start | bytes 20 | tf_op jit(solution)/shard_map/ppermute | solution.py:75
  82.9 2.8 %collective-permute-start.14 = (f32[1,1,512]{2,1,0:T(1,128)S(1)}, f32[1,1,512]{2,1,0:T(1,128)S(1)}, u32[]{:S(2)}, u32[]{:S(2)}) collective-permute-start(f32[1,1,512]{2,1,0:T(1,128)S(1)} %get-tuple-element.32), channel_id=1, source_target_pairs={{0,12},{4,0},{8,4},{12,8},{1,13},{5,1},{9,5},{13,9},{2,14},{6,2},{... | collective-permute-start | bytes 6152 | tf_op jit(solution)/shard_map/ppermute | solution.py:88
  87.7 2.5 %collective-permute-done.13 = f32[1,1,512]{2,1,0:T(1,128)S(1)} collective-permute-done((f32[1,1,512]{2,1,0:T(1,128)S(1)}, f32[1,1,512]{2,1,0:T(1,128)S(1)}, u32[]{:S(2)}, u32[]{:S(2)}) %collective-permute-start.13) | collective-permute-done | bytes 2080 | tf_op jit(solution)/shard_map/ppermute | solution.py:88
  90.2 1.1 collective-permute-done.12
  91.5 2.3 %all_gather.22 = bf16[1,1,513,512]{2,3,1,0:T(8,128)(2,1)S(1)} all-gather(bf16[1,1,513,256]{2,3,1,0:T(8,128)(2,1)S(1)} %pad_maximum_fusion), channel_id=1, replica_groups=mesh['groups'=2,'cand'=4,'query'=2,'mp'=2] {'mp'}, dimensions={3}, use_global_device_ids=true | all-gather | bytes 787968 | tf_op jit(solution)/shard_map/all_gather | solution.py:241
  94.0 1.8 %fusion.8 = f32[256,1024]{1,0:T(8,128)S(1)} fusion(bf16[3,1024,512]{2,1,0:T(8,128)(2,1)} %all-gather.8.cloned.1.call-done, bf16[1,1,513,512]{2,3,1,0:T(8,128)(2,1)S(1)} %all_gather.22), kind=kOutput, calls=%fused_computation.28 | convolution fusion | flops 268435456 | bytes 2359296 | tf_op jit(solution)/shard_map/qcsf,df->qcsd/dot_general | solution.py:15
  95.8 1.6 fusion.7
  97.4 2.2 %fusion.9 = (f32[256]{0:T(256)S(1)}, f32[256,1024]{1,0:T(8,128)S(1)}) fusion(f32[1,1,256,1024]{3,2,1,0:T(8,128)S(1)} %get-tuple-element.46, f32[256]{0:T(256)S(1)} %add_rsqrt_fusion, f32[256]{0:T(256)S(1)} %broadcast_multiply_fusion.3, f32[1024]{0:T(1024)S(1)} %copy-done.22, f32[1024]{0:T(1024)S(1)} %copy-done.28, f32[1024]{0:T(1024)S(1)} %bitcast.367, ...), kind=kOutput, calls=%fused_computation.30 | convolution fusion | flops 271056640 | bytes 4472064 | tf_op jit(solution)/shard_map/qcsf,df->qcsd/dot_general | solution.py:15
  101.6 1.6 convolution_convert_fusion.4
  106.5 2.3 %convolution_convert_fusion = bf16[1024,3,256]{2,0,1:T(8,128)(2,1)} fusion(bf16[4,1024]{1,0:T(4,128)(2,1)S(1)} %copy-done.7, bf16[256,1024]{1,0:T(8,128)(2,1)S(1)} %bitcast.345, bf16[4,1,256]{2,0,1:T(4,128)(2,1)S(1)} %stack.70, bf16[4,1,256]{2,0,1:T(4,128)(2,1)S(1)} %stack.69, bf16[256,3,256]{2,0,1:T(8,128)(2,1)S(1)} %maximum_bitcast_fusion.2, ...), kind=kOutput, calls=%fused_computation.3 | convolution fusion | flops 412393472 | bytes 2504216 | tf_op jit(solution)/shard_map/rd,rkf->dkf/dot_general | solution.py:15
  108.8 34.0 %reduce-scatter.2.cloned.1.call-done = bf16[256,3,256]{2,0,1:T(8,128)(2,1)} async-done(((bf16[1024,3,256]{2,0,1:T(8,128)(2,1)}), bf16[256,3,256]{2,0,1:T(8,128)(2,1)}) %reduce-scatter.2.cloned.1.call-update) | async-done | bytes 393232 | tf_op jit(solution)/shard_map/reduce_scatter | solution.py:305
  142.8 1.5 collective-permute-start.15
  144.3 9.4 %collective-permute-done.15 = bf16[256,3,256]{2,0,1:T(8,128)(2,1)S(1)} collective-permute-done((bf16[256,3,256]{2,0,1:T(8,128)(2,1)}, bf16[256,3,256]{2,0,1:T(8,128)(2,1)S(1)}, u32[]{:S(2)}, u32[]{:S(2)}) %collective-permute-start.15) | collective-permute-done | bytes 393248 | tf_op jit(solution)/shard_map/ppermute | solution.py:95
  153.7 2.0 %convert_add_fusion = f32[256,3,256]{2,0,1:T(8,128)} fusion(bf16[256,3,256]{2,0,1:T(8,128)(2,1)S(1)} %collective-permute-done.15, bf16[256,3,256]{2,0,1:T(8,128)(2,1)} %reduce-scatter.2.cloned.1.call-done), kind=kLoop, calls=%fused_computation.44 | loop fusion | flops 589824 | bytes 1572864 | tf_op jit(solution)/shard_map/add | solution.py:96
  (234 shorter events, 33.9 us)
Async XLA Ops:
  6.5 14.8 %copy-start.4 = (bf16[1,1,256,1024]{3,2,1,0:T(8,128)(2,1)S(1)}, bf16[1,1,256,1024]{3,2,1,0:T(8,128)(2,1)}, u32[]{:S(2)}) copy-start(bf16[1,1,256,1024]{3,2,1,0:T(8,128)(2,1)} %param.10) | copy-start | bytes 1572868
  6.5 14.8 %copy-start.3 = (bf16[3,1024,256]{2,1,0:T(8,128)(2,1)S(1)}, bf16[3,1024,256]{2,1,0:T(8,128)(2,1)}, u32[]{:S(2)}) copy-start(bf16[3,1024,256]{2,1,0:T(8,128)(2,1)} %param.13) | copy-start | bytes 4718596
  6.5 43.3 %all-gather.4.cloned.1.call-start = ((), (), s32[]{:S(2)}) async-start(), calls=%async_computation.1 | async-start | bytes 1572864 | tf_op jit(solution)/shard_map/all_gather | solution.py:124
  7.3 56.6 %all-gather.6.cloned.1.call-start = ((), (), s32[]{:S(2)}) async-start(), calls=%async_computation.2 | async-start | bytes 1572864 | tf_op jit(solution)/shard_map/all_gather | solution.py:126
  8.0 85.9 %all-gather.8.cloned.1.call-start = ((), (), s32[]{:S(2)}) async-start(), calls=%async_computation.3 | async-start | bytes 4718592 | tf_op jit(solution)/shard_map/all_gather | solution.py:125
  9.4 28.1 %collective-permute-start.2 = (bf16[1,1,1024]{2,1,0:T(2,128)(2,1)}, bf16[1,1,1024]{2,1,0:T(2,128)(2,1)}, u32[]{:S(2)}, u32[]{:S(2)}) collective-permute-start(bf16[1,1,1024]{2,1,0:T(2,128)(2,1)} %get-tuple-element.23), channel_id=1, source_target_pairs={{0,12},{4,0},{8,4},{12,8},{1,13},{5,1},{9,5},{13,9},{2,14},{6,2},{... | collective-permute-start | bytes 6152 | tf_op jit(solution)/shard_map/ppermute | solution.py:60
  14.4 23.1 %collective-permute-start.1 = (bf16[1,1,1024]{2,1,0:T(2,128)(2,1)}, bf16[1,1,1024]{2,1,0:T(2,128)(2,1)}, u32[]{:S(2)}, u32[]{:S(2)}) collective-permute-start(bf16[1,1,1024]{2,1,0:T(2,128)(2,1)} %get-tuple-element.23), channel_id=1, source_target_pairs={{0,8},{4,12},{8,0},{12,4},{1,9},{5,13},{9,1},{13,5},{2,10},{6,14},... | collective-permute-start | bytes 6152 | tf_op jit(solution)/shard_map/ppermute | solution.py:60
  14.4 23.1 %collective-permute-start = (bf16[1,1,1024]{2,1,0:T(2,128)(2,1)}, bf16[1,1,1024]{2,1,0:T(2,128)(2,1)}, u32[]{:S(2)}, u32[]{:S(2)}) collective-permute-start(bf16[1,1,1024]{2,1,0:T(2,128)(2,1)} %get-tuple-element.23), channel_id=1, source_target_pairs={{0,4},{4,8},{8,12},{12,0},{1,5},{5,9},{9,13},{13,1},{2,6},{6,10},{... | collective-permute-start | bytes 6152 | tf_op jit(solution)/shard_map/ppermute | solution.py:60
  15.4 9.0 %collective-permute-start.11 = (f32[1,1]{1,0:T(1,128)}, f32[1,1]{1,0:T(1,128)}, u32[]{:S(2)}, u32[]{:S(2)}) collective-permute-start(f32[1,1]{1,0:T(1,128)} %param.12), channel_id=1, source_target_pairs={{0,12},{4,0},{8,4},{12,8},{1,13},{5,1},{9,5},{13,9},{2,14},{6,2},{... | collective-permute-start | bytes 20 | tf_op jit(solution)/shard_map/ppermute | solution.py:60
  18.3 6.3 %collective-permute-start.10 = (f32[1,1]{1,0:T(1,128)}, f32[1,1]{1,0:T(1,128)}, u32[]{:S(2)}, u32[]{:S(2)}) collective-permute-start(f32[1,1]{1,0:T(1,128)} %param.12), channel_id=1, source_target_pairs={{0,8},{4,12},{8,0},{12,4},{1,9},{5,13},{9,1},{13,5},{2,10},{6,14},... | collective-permute-start | bytes 20 | tf_op jit(solution)/shard_map/ppermute | solution.py:60
  19.4 123.4 %reduce-scatter.2.cloned.1.call-start = ((), (), s32[]{:S(2)}) async-start(), calls=%async_computation.4 | async-start | bytes 1966080 | tf_op jit(solution)/shard_map/reduce_scatter | solution.py:305
  21.4 10.6 %copy-start.20 = (s32[1024]{0:T(1024)}, s32[1024]{0:T(1024)S(1)}, u32[]{:S(2)}) copy-start(s32[1024]{0:T(1024)S(1)} %pad_clamp_fusion) | copy-start | bytes 12292
  22.2 15.3 %copy-start.23 = (bf16[1,1,1,4,64]{4,3,2,1,0:T(4,128)(2,1)}, bf16[1,1,1,4,64]{4,3,2,1,0:T(4,128)(2,1)S(1)}, u32[]{:S(2)}) copy-start(bf16[1,1,1,4,64]{4,3,2,1,0:T(4,128)(2,1)S(1)} %copy.127) | copy-start | bytes 1540
  24.4 18.9 %copy-start.8 = (f32[4,256]{1,0:T(4,128)}, f32[4,256]{1,0:T(4,128)S(1)}, u32[]{:S(2)}) copy-start(f32[4,256]{1,0:T(4,128)S(1)} %get-tuple-element.43) | copy-start | bytes 12292
  24.4 5.6 %collective-permute-start.9 = (f32[1,1]{1,0:T(1,128)}, f32[1,1]{1,0:T(1,128)}, u32[]{:S(2)}, u32[]{:S(2)}) collective-permute-start(f32[1,1]{1,0:T(1,128)} %param.12), channel_id=1, source_target_pairs={{0,4},{4,8},{8,12},{12,0},{1,5},{5,9},{9,13},{13,1},{2,6},{6,10},{... | collective-permute-start | bytes 20 | tf_op jit(solution)/shard_map/ppermute | solution.py:60
  40.3 7.5 %copy-start.6 = (bf16[4,1024]{1,0:T(4,128)(2,1)}, bf16[4,1024]{1,0:T(4,128)(2,1)S(1)}, u32[]{:S(2)}) copy-start(bf16[4,1024]{1,0:T(4,128)(2,1)S(1)} %broadcast_select_fusion) | copy-start | bytes 24580
  51.9 45.4 %copy-start.16 = (f32[256]{0:T(256)}, f32[256]{0:T(256)S(1)}, u32[]{:S(2)}) copy-start(f32[256]{0:T(256)S(1)} %add_rsqrt_fusion) | copy-start | bytes 3076
  53.5 7.4 %copy-start.10 = (pred[4]{0:T(512)(128)(4,1)S(1)}, pred[4]{0:T(512)(128)(4,1)}, u32[]{:S(2)}) copy-start(pred[4]{0:T(512)(128)(4,1)} %get-tuple-element.52) | copy-start | bytes 16
  53.7 14.2 %copy-start.13 = (f32[1024]{0:T(1024)S(1)}, f32[1024]{0:T(1024)}, u32[]{:S(2)}) copy-start(f32[1024]{0:T(1024)} %param.18) | copy-start | bytes 12292
  53.7 14.2 %copy-start.14 = (f32[1024]{0:T(1024)S(1)}, f32[1024]{0:T(1024)}, u32[]{:S(2)}) copy-start(f32[1024]{0:T(1024)} %param.19) | copy-start | bytes 12292
  53.7 27.7 %copy-start.1 = (bf16[256,1024]{1,0:T(8,128)(2,1)S(1)}, bf16[256,1024]{1,0:T(8,128)(2,1)}, u32[]{:S(2)}) copy-start(bf16[256,1024]{1,0:T(8,128)(2,1)} %param.17) | copy-start | bytes 1572868
  53.8 3.6 %collective-permute-start.5 = (bf16[1,1,512]{2,1,0:T(2,128)(2,1)S(1)}, bf16[1,1,512]{2,1,0:T(2,128)(2,1)S(1)}, u32[]{:S(2)}, u32[]{:S(2)}) collective-permute-start(bf16[1,1,512]{2,1,0:T(2,128)(2,1)S(1)} %pad_maximum_fusion.1), channel_id=1, source_target_pairs={{0,12},{4,0},{8,4},{12,8},{1,13},{5,1},{9,5},{13,9},{2,14},{6,2},{... | collective-permute-start | bytes 3080 | tf_op jit(solution)/shard_map/ppermute | solution.py:60
  53.9 4.5 %collective-permute-start.4 = (bf16[1,1,512]{2,1,0:T(2,128)(2,1)S(1)}, bf16[1,1,512]{2,1,0:T(2,128)(2,1)S(1)}, u32[]{:S(2)}, u32[]{:S(2)}) collective-permute-start(bf16[1,1,512]{2,1,0:T(2,128)(2,1)S(1)} %pad_maximum_fusion.1), channel_id=1, source_target_pairs={{0,8},{4,12},{8,0},{12,4},{1,9},{5,13},{9,1},{13,5},{2,10},{6,14},... | collective-permute-start | bytes 3080 | tf_op jit(solution)/shard_map/ppermute | solution.py:60
  53.9 5.9 %collective-permute-start.3 = (bf16[1,1,512]{2,1,0:T(2,128)(2,1)S(1)}, bf16[1,1,512]{2,1,0:T(2,128)(2,1)S(1)}, u32[]{:S(2)}, u32[]{:S(2)}) collective-permute-start(bf16[1,1,512]{2,1,0:T(2,128)(2,1)S(1)} %pad_maximum_fusion.1), channel_id=1, source_target_pairs={{0,4},{4,8},{8,12},{12,0},{1,5},{5,9},{9,13},{13,1},{2,6},{6,10},{... | collective-permute-start | bytes 3080 | tf_op jit(solution)/shard_map/ppermute | solution.py:60
  56.6 34.8 %copy-start.15 = (pred[256]{0:T(512)(128)(4,1)S(1)}, pred[256]{0:T(512)(128)(4,1)}, u32[]{:S(2)}) copy-start(pred[256]{0:T(512)(128)(4,1)} %iota_compare_fusion.1) | copy-start | bytes 772
  69.2 7.8 %collective-permute-start.6 = (f32[1]{0:T(128)}, f32[1]{0:T(128)}, u32[]{:S(2)}, u32[]{:S(2)}) collective-permute-start(f32[1]{0:T(128)} %bitcast.69), channel_id=1, source_target_pairs={{0,4},{4,8},{8,12},{12,0},{1,5},{5,9},{9,13},{13,1},{2,6},{6,10},{... | collective-permute-start | bytes 20 | tf_op jit(solution)/shard_map/ppermute | solution.py:75
  71.1 6.5 %collective-permute-start.7 = (f32[1]{0:T(128)}, f32[1]{0:T(128)}, u32[]{:S(2)}, u32[]{:S(2)}) collective-permute-start(f32[1]{0:T(128)} %bitcast.69), channel_id=1, source_target_pairs={{0,8},{4,12},{8,0},{12,4},{1,9},{5,13},{9,1},{13,5},{2,10},{6,14},... | collective-permute-start | bytes 20 | tf_op jit(solution)/shard_map/ppermute | solution.py:75
  74.4 3.8 %collective-permute-start.8 = (f32[1]{0:T(128)}, f32[1]{0:T(128)}, u32[]{:S(2)}, u32[]{:S(2)}) collective-permute-start(f32[1]{0:T(128)} %bitcast.69), channel_id=1, source_target_pairs={{0,12},{4,0},{8,4},{12,8},{1,13},{5,1},{9,5},{13,9},{2,14},{6,2},{... | collective-permute-start | bytes 20 | tf_op jit(solution)/shard_map/ppermute | solution.py:75
  82.9 4.8 %collective-permute-start.14 = (f32[1,1,512]{2,1,0:T(1,128)S(1)}, f32[1,1,512]{2,1,0:T(1,128)S(1)}, u32[]{:S(2)}, u32[]{:S(2)}) collective-permute-start(f32[1,1,512]{2,1,0:T(1,128)S(1)} %get-tuple-element.32), channel_id=1, source_target_pairs={{0,12},{4,0},{8,4},{12,8},{1,13},{5,1},{9,5},{13,9},{2,14},{6,2},{... | collective-permute-start | bytes 6152 | tf_op jit(solution)/shard_map/ppermute | solution.py:88
  85.7 4.5 %collective-permute-start.13 = (f32[1,1,512]{2,1,0:T(1,128)S(1)}, f32[1,1,512]{2,1,0:T(1,128)S(1)}, u32[]{:S(2)}, u32[]{:S(2)}) collective-permute-start(f32[1,1,512]{2,1,0:T(1,128)S(1)} %get-tuple-element.33), channel_id=1, source_target_pairs={{0,8},{4,12},{8,0},{12,4},{1,9},{5,13},{9,1},{13,5},{2,10},{6,14},... | collective-permute-start | bytes 6152 | tf_op jit(solution)/shard_map/ppermute | solution.py:88
  85.9 5.4 %collective-permute-start.12 = (f32[1,1,512]{2,1,0:T(1,128)S(1)}, f32[1,1,512]{2,1,0:T(1,128)S(1)}, u32[]{:S(2)}, u32[]{:S(2)}) collective-permute-start(f32[1,1,512]{2,1,0:T(1,128)S(1)} %get-tuple-element.31), channel_id=1, source_target_pairs={{0,4},{4,8},{8,12},{12,0},{1,5},{5,9},{9,13},{13,1},{2,6},{6,10},{... | collective-permute-start | bytes 6152 | tf_op jit(solution)/shard_map/ppermute | solution.py:88
  142.8 10.9 %collective-permute-start.15 = (bf16[256,3,256]{2,0,1:T(8,128)(2,1)}, bf16[256,3,256]{2,0,1:T(8,128)(2,1)S(1)}, u32[]{:S(2)}, u32[]{:S(2)}) collective-permute-start(bf16[256,3,256]{2,0,1:T(8,128)(2,1)} %reduce-scatter.2.cloned.1.call-done), channel_id=1, source_target_pairs={{0,2},{2,0},{1,3},{3,1},{4,6},{6,4},{5,7},{7,5},{8,10},{10,8},{9,1... | collective-permute-start | bytes 1179656 | tf_op jit(solution)/shard_map/ppermute | solution.py:95
  (19 other events, 44.7 us)
Sparse Core Ops, SparseCore 0:
  8.9 11.7 all-gather.3
  22.2 10.1 all-gather.5
  34.0 12.9 all-gather.7
  108.9 33.8 reduce-scatter.1

commit v4 on v3

--- a/solution.py
+++ b/solution.py
@@ -302,13 +302,33 @@
     all_tokens = jnp.concatenate(
         [tokens.reshape(row_count, model_width), cls_tokens.reshape(cross_rows, model_width)], 0
     )
-    partial_grad = lax.psum_scatter(
-        mixed("rd,rkf->dkf", all_tokens, all_rows).astype(jnp.bfloat16),
-        "cand",
-        scatter_dimension=0,
-        tiled=True,
-    )
-    return sum_query(partial_grad).astype(jnp.float32)
+    if lax.axis_size("query") != 2:
+        partial_grad = lax.psum_scatter(
+            mixed("rd,rkf->dkf", all_tokens, all_rows).astype(jnp.bfloat16),
+            "cand",
+            scatter_dimension=0,
+            tiled=True,
+        )
+        return sum_query(partial_grad).astype(jnp.float32)
+    swap = [(0, 1), (1, 0)]
+    half = 3 * local_width // 2
+    side = lax.axis_index("query")
+    other_tokens = lax.ppermute(all_tokens, "query", swap)
+    flat_rows = all_rows.reshape(all_rows.shape[0], 3 * local_width)
+    other_rows = lax.ppermute(flat_rows, "query", swap)
+    own_half = lax.dynamic_slice_in_dim(flat_rows, side * half, half, 1)
+    other_half = lax.dynamic_slice_in_dim(other_rows, side * half, half, 1)
+    paired = mixed("rd,rf->df", all_tokens, own_half) + mixed("rd,rf->df", other_tokens, other_half)
+    reduced = lax.psum_scatter(
+        paired.astype(jnp.bfloat16), "cand", scatter_dimension=0, tiled=True
+    )
+    partner = lax.ppermute(reduced, "query", swap)
+    joined = jnp.where(
+        side == 0,
+        jnp.concatenate([reduced, partner], 1),
+        jnp.concatenate([partner, reduced], 1),
+    )
+    return joined.reshape(joined.shape[0], 3, local_width).astype(jnp.float32)
 
 
 def solution(mesh):

time: 163 us -> 196 us (1.20)
  other arithmetic: 22.7 us -> 38.6 us
  local copies, waits for them, and re-layouts: 9.65 us -> 24.2 us
  waiting for transfers between devices: 57.3 us -> 44.9 us
  matrix products: 19.1 us -> 28.1 us
  starting transfers between devices: 25.6 us -> 29.1 us
    reduce_scatter x1, waiting for transfers between devices: 34 us -> 22 us  [local(): lax.psum_scatter(paired.astype(jnp.bfloat16), 'cand', scatter_dimension=0...]
    dot_general x30 -> x31, matrix products: 19.1 us -> 28.1 us  [mixed(): jnp.einsum(pattern, former, latter, preferred_element_type=jnp.float32)]
    another operation x9 -> x12, other arithmetic: 0.84 us -> 7.94 us
    ppermute x1 -> x3, waiting for transfers between devices: 9.43 us -> 14.3 us  [the longest x1 9.94 us: local(): other_rows = lax.ppermute(flat_rows, 'query', swap)]
    another operation x10 -> x9, local copies, waits for them, and re-layouts: 0.79 us -> 5.03 us
    ppermute x9, waiting for transfers between devices: 8.81 us -> 5.42 us  [gather_cand(): lax.ppermute(block, 'cand', [(j, (j + k) % count) for j in range(count)])]
    ppermute x1 -> x3, starting transfers between devices: 1.45 us -> 3.78 us  [the longest x1 1.49 us: local(): other_tokens = lax.ppermute(all_tokens, 'query', swap)]
    slice x2, local copies, waits for them, and re-layouts: 0.14 us -> 2.4 us  [local(): last_kv[1][:, :, 0]]
  transfers between devices with their start and end apart: 20 -> 22, of which waited for: 8 -> 6; matrix products, arithmetic and copies ran while one was open for 21% -> 43% of each run, Pallas kernels for 0% -> 0%
where the time goes in v4:
time: 196 us; the launch traced here: 194 us
  waiting for transfers between devices  44.9 us (23%)
  other arithmetic  38.6 us (20%)
  starting transfers between devices  29.1 us (15%)
  matrix products  28.1 us (14%)
  local copies, waits for them, and re-layouts  24.2 us (12%)
  between operations  21.9 us (11%)
  blocking collectives  7.24 us (4%)
    dot_general x31, matrix products, mixed(): jnp.einsum(pattern, former, latter, preferred_element_type=jnp.float32)  28.1 us
    reduce_scatter x1, waiting for transfers between devices, local(): lax.psum_scatter(paired.astype(jnp.bfloat16), 'cand', scatter_dimension=0...  22 us
    ppermute x9, starting transfers between devices, gather_cand(): lax.ppermute(block, 'cand', [(j, (j + k) % count) for j in range(count)])  12.2 us
    ppermute x1, waiting for transfers between devices, local(): other_rows = lax.ppermute(flat_rows, 'query', swap)  9.94 us
    ppermute x3, starting transfers between devices, sum_cand(): lax.ppermute(block, 'cand', [(j, (j + k) % count) for j in range(count)])  9.64 us
    another operation x10, other arithmetic  7.82 us
    ppermute x9, waiting for transfers between devices, gather_cand(): lax.ppermute(block, 'cand', [(j, (j + k) % count) for j in range(count)])  5.42 us
    another operation x9, local copies, waits for them, and re-layouts  5.03 us
  transfers between devices with their start and end apart: 22, of which 6 were waited for; matrix products, arithmetic and copies ran while one was open for 43% of the time, Pallas kernels for 0%

profile of v4, /device:TPU:0, one launch (start us, length us, event | category | flops | bytes accessed | tf_op | source)
XLA Modules:
  0.0 194.0 jit_solution(7297623915869044211)
XLA Ops:
  8.8 5.0 %collective-permute-start.2 = (bf16[1,1,1024]{2,1,0:T(2,128)(2,1)S(1)}, bf16[1,1,1024]{2,1,0:T(2,128)(2,1)S(1)}, u32[]{:S(2)}, u32[]{:S(2)}) collective-permute-start(bf16[1,1,1024]{2,1,0:T(2,128)(2,1)S(1)} %get-tuple-element.23), channel_id=1, source_target_pairs={{0,12},{4,0},{8,4},{12,8},{1,13},{5,1},{9,5},{13,9},{2,14},{6,2},{... | collective-permute-start | bytes 6152 | tf_op jit(solution)/shard_map/ppermute | solution.py:60
  14.8 2.8 %collective-permute-start.11 = (f32[1,1]{1,0:T(1,128)}, f32[1,1]{1,0:T(1,128)}, u32[]{:S(2)}, u32[]{:S(2)}) collective-permute-start(f32[1,1]{1,0:T(1,128)} %param.12), channel_id=1, source_target_pairs={{0,12},{4,0},{8,4},{12,8},{1,13},{5,1},{9,5},{13,9},{2,14},{6,2},{... | collective-permute-start | bytes 20 | tf_op jit(solution)/shard_map/ppermute | solution.py:60
  23.3 5.4 %collective-permute-done.9 = f32[1,1]{1,0:T(1,128)} collective-permute-done((f32[1,1]{1,0:T(1,128)}, f32[1,1]{1,0:T(1,128)}, u32[]{:S(2)}, u32[]{:S(2)}) %collective-permute-start.9) | collective-permute-done | bytes 36 | tf_op jit(solution)/shard_map/ppermute | solution.py:60
  28.7 2.0 %maximum_bitcast_fusion.2 = f32[4]{0:T(128)S(1)} fusion(f32[1,1,1]{0,2,1:T(1,128)} %bitcast.73, f32[1,1,1]{0,2,1:T(1,128)} %bitcast.72, f32[1,1,1]{0,2,1:T(1,128)} %bitcast.71, f32[1,1,1]{0,2,1:T(1,128)} %bitcast.337), kind=kLoop, calls=%fused_computation.211 | loop fusion | flops 12 | bytes 32 | tf_op jit(solution)/shard_map/stack | solution.py:63
  39.0 2.0 %all_gather.18 = bf16[1,1,256,512]{2,3,1,0:T(8,128)(2,1)S(1)} all-gather(bf16[1,1,256,256]{2,3,1,0:T(8,128)(2,1)S(1)} %bitcast.364), channel_id=1, replica_groups=mesh['groups'=2,'cand'=4,'query'=2,'mp'=2] {'mp'}, dimensions={3}, use_global_device_ids=true | all-gather | bytes 393216 | tf_op jit(solution)/shard_map/all_gather | solution.py:151
  41.9 1.5 collective-permute-start.15
  43.4 2.0 %fusion.121 = (f32[256]{0:T(256)S(1)}, f32[1,1,256,1024]{3,2,1,0:T(8,128)S(1)}) fusion(bf16[512,1024]{1,0:T(8,128)(2,1)} %all-gather.4.cloned.1.call-done, bf16[1,1,256,512]{2,3,1,0:T(8,128)(2,1)S(1)} %all_gather.18, bf16[1,1,256,1024]{3,2,1,0:T(8,128)(2,1)S(1)} %copy-done), kind=kOutput, calls=%fused_computation.237 | convolution fusion | flops 269221632 | bytes 2884608 | tf_op jit(solution)/shard_map/qcsf,fd->qcsd/dot_general | solution.py:15
  48.9 2.0 %collective-permute-start.3 = (bf16[1,1,512]{2,1,0:T(2,128)(2,1)}, bf16[1,1,512]{2,1,0:T(2,128)(2,1)}, u32[]{:S(2)}, u32[]{:S(2)}) collective-permute-start(bf16[1,1,512]{2,1,0:T(2,128)(2,1)} %pad_maximum_fusion.5), channel_id=1, source_target_pairs={{0,4},{4,8},{8,12},{12,0},{1,5},{5,9},{9,13},{13,1},{2,6},{6,10},{... | collective-permute-start | bytes 3080 | tf_op jit(solution)/shard_map/ppermute | solution.py:60
  57.2 1.7 copy.81
  64.9 1.4 fusion.60
  71.4 1.4 convert_convert_fusion.1
  75.2 1.4 reshape.1099
  79.1 1.4 convert_element_type.232
  80.4 2.8 %all_gather.20 = bf16[1,1,512]{2,1,0:T(2,128)(2,1)} all-gather(bf16[1,1,256]{2,1,0:T(2,128)(2,1)} %convert_element_type.232), channel_id=1, replica_groups=mesh['groups'=2,'cand'=4,'query'=2,'mp'=2] {'mp'}, dimensions={2}, use_global_device_ids=true | all-gather | bytes 1536 | tf_op jit(solution)/shard_map/all_gather | solution.py:180
  83.2 1.5 fusion.74
  87.5 1.4 multiply_reduce_fusion.2
  89.6 2.7 %collective-permute-start.6 = (f32[1]{0:T(128)}, f32[1]{0:T(128)}, u32[]{:S(2)}, u32[]{:S(2)}) collective-permute-start(f32[1]{0:T(128)} %bitcast.68), channel_id=1, source_target_pairs={{0,4},{4,8},{8,12},{12,0},{1,5},{5,9},{9,13},{13,1},{2,6},{6,10},{... | collective-permute-start | bytes 20 | tf_op jit(solution)/shard_map/ppermute | solution.py:75
  92.2 2.8 %collective-permute-start.7 = (f32[1]{0:T(128)}, f32[1]{0:T(128)}, u32[]{:S(2)}, u32[]{:S(2)}) collective-permute-start(f32[1]{0:T(128)} %bitcast.68), channel_id=1, source_target_pairs={{0,8},{4,12},{8,0},{12,4},{1,9},{5,13},{9,1},{13,5},{2,10},{6,14},... | collective-permute-start | bytes 20 | tf_op jit(solution)/shard_map/ppermute | solution.py:75
  95.0 4.2 %collective-permute-start.8 = (f32[1]{0:T(128)}, f32[1]{0:T(128)}, u32[]{:S(2)}, u32[]{:S(2)}) collective-permute-start(f32[1]{0:T(128)} %bitcast.68), channel_id=1, source_target_pairs={{0,12},{4,0},{8,4},{12,8},{1,13},{5,1},{9,5},{13,9},{2,14},{6,2},{... | collective-permute-start | bytes 20 | tf_op jit(solution)/shard_map/ppermute | solution.py:75
  101.2 2.0 %fusion.104 = (f32[]{:T(128)}, f32[]{:T(128)}, f32[1024]{0:T(1024)}) fusion(f32[]{:T(128)S(6)} %rsqrt.13, f32[]{:T(128)S(6)} %div.79, f32[1024]{0:T(1024)S(1)} %bitcast.362, bf16[1024]{0:T(1024)(128)(2,1)S(1)} %slice_reduce_fusion.1, f32[1024]{0:T(1024)} %param.18, f32[1024]{0:T(1024)} %param.19, f32[]{:T(128)} %bitcast.78), kind=kLoop, calls=%fused_computation.226 | loop fusion | flops 9214 | bytes 18452 | tf_op jit(solution)/shard_map/reduce_sum | solution.py:29
  112.6 2.8 %collective-permute-start.14 = (f32[1,1,512]{2,1,0:T(1,128)}, f32[1,1,512]{2,1,0:T(1,128)}, u32[]{:S(2)}, u32[]{:S(2)}) collective-permute-start(f32[1,1,512]{2,1,0:T(1,128)} %get-tuple-element.32), channel_id=1, source_target_pairs={{0,12},{4,0},{8,4},{12,8},{1,13},{5,1},{9,5},{13,9},{2,14},{6,2},{... | collective-permute-start | bytes 6152 | tf_op jit(solution)/shard_map/ppermute | solution.py:88
  122.7 2.5 %all_gather.22 = bf16[1,1,513,512]{2,3,1,0:T(8,128)(2,1)S(1)} all-gather(bf16[1,1,513,256]{2,3,1,0:T(8,128)(2,1)S(1)} %pad_maximum_fusion.3), channel_id=1, replica_groups=mesh['groups'=2,'cand'=4,'query'=2,'mp'=2] {'mp'}, dimensions={3}, use_global_device_ids=true | all-gather | bytes 787968 | tf_op jit(solution)/shard_map/all_gather | solution.py:241
  126.0 1.7 fusion.8
  127.7 1.6 fusion.7
  129.4 3.1 %fusion.9 = (f32[256]{0:T(256)S(1)}, f32[256,1024]{1,0:T(8,128)}) fusion(f32[1,1,256,1024]{3,2,1,0:T(8,128)S(1)} %get-tuple-element.45, f32[256]{0:T(256)S(1)} %copy-done.26, f32[256]{0:T(256)S(1)} %copy-done.20, f32[1024]{0:T(1024)S(1)} %copy-done.38, f32[1024]{0:T(1024)S(1)} %copy-done.43, f32[1024]{0:T(1024)S(1)} %bitcast.372, ...), kind=kOutput, calls=%fused_computation.30 | convolution fusion | flops 271056640 | bytes 4472064 | tf_op jit(solution)/shard_map/qcsf,df->qcsd/dot_general | solution.py:15
  132.5 1.4 reduce_sum.183
  133.9 1.7 convolution_convert_fusion.3
  144.5 9.9 %collective-permute-done.16 = bf16[260,768]{1,0:T(8,128)(2,1)S(1)} collective-permute-done((bf16[260,768]{1,0:T(8,128)(2,1)S(1)}, bf16[260,768]{1,0:T(8,128)(2,1)S(1)}, u32[]{:S(2)}, u32[]{:S(2)}) %collective-permute-start.16) | collective-permute-done | bytes 399392 | tf_op jit(solution)/shard_map/ppermute | solution.py:318
  154.4 2.6 %add_convert_fusion = bf16[1024,384]{1,0:T(8,128)(2,1)} fusion(f32[1024,384]{1,0:T(8,128)S(1)} %fusion.32, bf16[260,1024]{1,0:T(8,128)(2,1)} %collective-permute-done.15, bf16[260,768]{1,0:T(8,128)(2,1)S(1)} %collective-permute-done.16, s32[]{:T(128)S(6)} %select_n.270), kind=kOutput, calls=%fused_computation.3 | convolution fusion | flops 205258752 | bytes 3094532 | tf_op jit(solution)/shard_map/rd,rf->df/dot_general | solution.py:15
  157.1 22.0 %reduce-scatter.2.cloned.1.call-done = bf16[256,384]{1,0:T(8,128)(2,1)} async-done(((bf16[1024,384]{1,0:T(8,128)(2,1)}), bf16[256,384]{1,0:T(8,128)(2,1)}) %reduce-scatter.2.cloned.1.call-update) | async-done | bytes 196624 | tf_op jit(solution)/shard_map/reduce_scatter | solution.py:322
  179.1 1.5 collective-permute-start.17
  180.6 4.4 %collective-permute-done.17 = bf16[256,384]{1,0:T(8,128)(2,1)S(1)} collective-permute-done((bf16[256,384]{1,0:T(8,128)(2,1)}, bf16[256,384]{1,0:T(8,128)(2,1)S(1)}, u32[]{:S(2)}, u32[]{:S(2)}) %collective-permute-start.17) | collective-permute-done | bytes 196640 | tf_op jit(solution)/shard_map/ppermute | solution.py:325
  (275 shorter events, 69.8 us)
Async XLA Ops:
  6.5 13.1 %copy-start = (bf16[1,1,256,1024]{3,2,1,0:T(8,128)(2,1)S(1)}, bf16[1,1,256,1024]{3,2,1,0:T(8,128)(2,1)}, u32[]{:S(2)}) copy-start(bf16[1,1,256,1024]{3,2,1,0:T(8,128)(2,1)} %param.10) | copy-start | bytes 1572868
  6.5 13.1 %copy-start.5 = (bf16[3,1024,256]{2,1,0:T(8,128)(2,1)S(1)}, bf16[3,1024,256]{2,1,0:T(8,128)(2,1)}, u32[]{:S(2)}) copy-start(bf16[3,1024,256]{2,1,0:T(8,128)(2,1)} %param.13) | copy-start | bytes 4718596
  6.5 36.9 %all-gather.4.cloned.1.call-start = ((), (), s32[]{:S(2)}) async-start(), calls=%async_computation.1 | async-start | bytes 1572864 | tf_op jit(solution)/shard_map/all_gather | solution.py:124
  7.3 76.0 %all-gather.6.cloned.1.call-start = ((), (), s32[]{:S(2)}) async-start(), calls=%async_computation.2 | async-start | bytes 1572864 | tf_op jit(solution)/shard_map/all_gather | solution.py:126
  8.0 117.9 %all-gather.8.cloned.1.call-start = ((), (), s32[]{:S(2)}) async-start(), calls=%async_computation.3 | async-start | bytes 4718592 | tf_op jit(solution)/shard_map/all_gather | solution.py:125
  8.8 25.8 %collective-permute-start.2 = (bf16[1,1,1024]{2,1,0:T(2,128)(2,1)S(1)}, bf16[1,1,1024]{2,1,0:T(2,128)(2,1)S(1)}, u32[]{:S(2)}, u32[]{:S(2)}) collective-permute-start(bf16[1,1,1024]{2,1,0:T(2,128)(2,1)S(1)} %get-tuple-element.23), channel_id=1, source_target_pairs={{0,12},{4,0},{8,4},{12,8},{1,13},{5,1},{9,5},{13,9},{2,14},{6,2},{... | collective-permute-start | bytes 6152 | tf_op jit(solution)/shard_map/ppermute | solution.py:60
  13.8 20.8 %collective-permute-start.1 = (bf16[1,1,1024]{2,1,0:T(2,128)(2,1)S(1)}, bf16[1,1,1024]{2,1,0:T(2,128)(2,1)S(1)}, u32[]{:S(2)}, u32[]{:S(2)}) collective-permute-start(bf16[1,1,1024]{2,1,0:T(2,128)(2,1)S(1)} %get-tuple-element.23), channel_id=1, source_target_pairs={{0,8},{4,12},{8,0},{12,4},{1,9},{5,13},{9,1},{13,5},{2,10},{6,14},... | collective-permute-start | bytes 6152 | tf_op jit(solution)/shard_map/ppermute | solution.py:60
  13.8 20.8 %collective-permute-start = (bf16[1,1,1024]{2,1,0:T(2,128)(2,1)S(1)}, bf16[1,1,1024]{2,1,0:T(2,128)(2,1)S(1)}, u32[]{:S(2)}, u32[]{:S(2)}) collective-permute-start(bf16[1,1,1024]{2,1,0:T(2,128)(2,1)S(1)} %get-tuple-element.23), channel_id=1, source_target_pairs={{0,4},{4,8},{8,12},{12,0},{1,5},{5,9},{9,13},{13,1},{2,6},{6,10},{... | collective-permute-start | bytes 6152 | tf_op jit(solution)/shard_map/ppermute | solution.py:60
  14.8 8.4 %collective-permute-start.11 = (f32[1,1]{1,0:T(1,128)}, f32[1,1]{1,0:T(1,128)}, u32[]{:S(2)}, u32[]{:S(2)}) collective-permute-start(f32[1,1]{1,0:T(1,128)} %param.12), channel_id=1, source_target_pairs={{0,12},{4,0},{8,4},{12,8},{1,13},{5,1},{9,5},{13,9},{2,14},{6,2},{... | collective-permute-start | bytes 20 | tf_op jit(solution)/shard_map/ppermute | solution.py:60
  17.7 5.7 %collective-permute-start.10 = (f32[1,1]{1,0:T(1,128)}, f32[1,1]{1,0:T(1,128)}, u32[]{:S(2)}, u32[]{:S(2)}) collective-permute-start(f32[1,1]{1,0:T(1,128)} %param.12), channel_id=1, source_target_pairs={{0,8},{4,12},{8,0},{12,4},{1,9},{5,13},{9,1},{13,5},{2,10},{6,14},... | collective-permute-start | bytes 20 | tf_op jit(solution)/shard_map/ppermute | solution.py:60
  18.8 160.3 %reduce-scatter.2.cloned.1.call-start = ((), (), s32[]{:S(2)}) async-start(), calls=%async_computation.4 | async-start | bytes 983040 | tf_op jit(solution)/shard_map/reduce_scatter | solution.py:322
  18.9 16.3 %copy-start.44 = (pred[4]{0:T(512)(128)(4,1)}, pred[4]{0:T(512)(128)(4,1)S(1)}, u32[]{:S(2)}) copy-start(pred[4]{0:T(512)(128)(4,1)S(1)} %get-tuple-element.50) | copy-start | bytes 16
  18.9 17.8 %copy-start.16 = (pred[4]{0:T(512)(128)(4,1)}, pred[4]{0:T(512)(128)(4,1)S(1)}, u32[]{:S(2)}) copy-start(pred[4]{0:T(512)(128)(4,1)S(1)} %get-tuple-element.51) | copy-start | bytes 16
  18.9 18.8 %copy-start.22 = (pred[256]{0:T(512)(128)(4,1)}, pred[256]{0:T(512)(128)(4,1)S(1)}, u32[]{:S(2)}) copy-start(pred[256]{0:T(512)(128)(4,1)S(1)} %iota_compare_fusion.1) | copy-start | bytes 772
  21.0 14.3 %copy-start.36 = (s32[1024]{0:T(1024)}, s32[1024]{0:T(1024)S(1)}, u32[]{:S(2)}) copy-start(s32[1024]{0:T(1024)S(1)} %pad_clamp_fusion) | copy-start | bytes 12292
  21.8 7.0 %copy-start.31 = (pred[256]{0:T(512)(128)(4,1)}, pred[256]{0:T(512)(128)(4,1)S(1)}, u32[]{:S(2)}) copy-start(pred[256]{0:T(512)(128)(4,1)S(1)} %iota_compare_fusion) | copy-start | bytes 772
  23.3 5.5 %collective-permute-start.9 = (f32[1,1]{1,0:T(1,128)}, f32[1,1]{1,0:T(1,128)}, u32[]{:S(2)}, u32[]{:S(2)}) collective-permute-start(f32[1,1]{1,0:T(1,128)} %param.12), channel_id=1, source_target_pairs={{0,4},{4,8},{8,12},{12,0},{1,5},{5,9},{9,13},{13,1},{2,6},{6,10},{... | collective-permute-start | bytes 20 | tf_op jit(solution)/shard_map/ppermute | solution.py:60
  41.9 102.6 %collective-permute-start.15 = (bf16[260,1024]{1,0:T(8,128)(2,1)}, bf16[260,1024]{1,0:T(8,128)(2,1)}, u32[]{:S(2)}, u32[]{:S(2)}) collective-permute-start(bf16[260,1024]{1,0:T(8,128)(2,1)} %pad_maximum_fusion.1), channel_id=1, source_target_pairs={{0,2},{2,0},{1,3},{3,1},{4,6},{6,4},{5,7},{7,5},{8,10},{10,8},{9,1... | collective-permute-start | bytes 1597448 | tf_op jit(solution)/shard_map/ppermute | solution.py:316
  47.4 58.3 %copy-start.2 = (bf16[256,1024]{1,0:T(8,128)(2,1)S(1)}, bf16[256,1024]{1,0:T(8,128)(2,1)}, u32[]{:S(2)}) copy-start(bf16[256,1024]{1,0:T(8,128)(2,1)} %param.17) | copy-start | bytes 1572868
  48.8 11.3 %collective-permute-start.5 = (bf16[1,1,512]{2,1,0:T(2,128)(2,1)}, bf16[1,1,512]{2,1,0:T(2,128)(2,1)}, u32[]{:S(2)}, u32[]{:S(2)}) collective-permute-start(bf16[1,1,512]{2,1,0:T(2,128)(2,1)} %pad_maximum_fusion.5), channel_id=1, source_target_pairs={{0,12},{4,0},{8,4},{12,8},{1,13},{5,1},{9,5},{13,9},{2,14},{6,2},{... | collective-permute-start | bytes 3080 | tf_op jit(solution)/shard_map/ppermute | solution.py:60
  48.8 11.3 %collective-permute-start.4 = (bf16[1,1,512]{2,1,0:T(2,128)(2,1)}, bf16[1,1,512]{2,1,0:T(2,128)(2,1)}, u32[]{:S(2)}, u32[]{:S(2)}) collective-permute-start(bf16[1,1,512]{2,1,0:T(2,128)(2,1)} %pad_maximum_fusion.5), channel_id=1, source_target_pairs={{0,8},{4,12},{8,0},{12,4},{1,9},{5,13},{9,1},{13,5},{2,10},{6,14},... | collective-permute-start | bytes 3080 | tf_op jit(solution)/shard_map/ppermute | solution.py:60
  48.9 11.2 %collective-permute-start.3 = (bf16[1,1,512]{2,1,0:T(2,128)(2,1)}, bf16[1,1,512]{2,1,0:T(2,128)(2,1)}, u32[]{:S(2)}, u32[]{:S(2)}) collective-permute-start(bf16[1,1,512]{2,1,0:T(2,128)(2,1)} %pad_maximum_fusion.5), channel_id=1, source_target_pairs={{0,4},{4,8},{8,12},{12,0},{1,5},{5,9},{9,13},{13,1},{2,6},{6,10},{... | collective-permute-start | bytes 3080 | tf_op jit(solution)/shard_map/ppermute | solution.py:60
  53.5 6.7 %copy-start.7 = (f32[4,1,256]{2,1,0:T(1,128)}, f32[4,1,256]{2,1,0:T(1,128)S(1)}, u32[]{:S(2)}) copy-start(f32[4,1,256]{2,1,0:T(1,128)S(1)} %fusion.122) | copy-start | bytes 12292
  71.4 11.8 %copy-start.8 = (f32[4,256]{1,0:T(4,128)}, f32[4,256]{1,0:T(4,128)S(1)}, u32[]{:S(2)}) copy-start(f32[4,256]{1,0:T(4,128)S(1)} %get-tuple-element.18) | copy-start | bytes 12292
  89.6 9.6 %collective-permute-start.6 = (f32[1]{0:T(128)}, f32[1]{0:T(128)}, u32[]{:S(2)}, u32[]{:S(2)}) collective-permute-start(f32[1]{0:T(128)} %bitcast.68), channel_id=1, source_target_pairs={{0,4},{4,8},{8,12},{12,0},{1,5},{5,9},{9,13},{13,1},{2,6},{6,10},{... | collective-permute-start | bytes 20 | tf_op jit(solution)/shard_map/ppermute | solution.py:75
  92.2 7.5 %collective-permute-start.7 = (f32[1]{0:T(128)}, f32[1]{0:T(128)}, u32[]{:S(2)}, u32[]{:S(2)}) collective-permute-start(f32[1]{0:T(128)} %bitcast.68), channel_id=1, source_target_pairs={{0,8},{4,12},{8,0},{12,4},{1,9},{5,13},{9,1},{13,5},{2,10},{6,14},... | collective-permute-start | bytes 20 | tf_op jit(solution)/shard_map/ppermute | solution.py:75
  95.0 5.4 %collective-permute-start.8 = (f32[1]{0:T(128)}, f32[1]{0:T(128)}, u32[]{:S(2)}, u32[]{:S(2)}) collective-permute-start(f32[1]{0:T(128)} %bitcast.68), channel_id=1, source_target_pairs={{0,12},{4,0},{8,4},{12,8},{1,13},{5,1},{9,5},{13,9},{2,14},{6,2},{... | collective-permute-start | bytes 20 | tf_op jit(solution)/shard_map/ppermute | solution.py:75
  112.6 6.8 %collective-permute-start.14 = (f32[1,1,512]{2,1,0:T(1,128)}, f32[1,1,512]{2,1,0:T(1,128)}, u32[]{:S(2)}, u32[]{:S(2)}) collective-permute-start(f32[1,1,512]{2,1,0:T(1,128)} %get-tuple-element.32), channel_id=1, source_target_pairs={{0,12},{4,0},{8,4},{12,8},{1,13},{5,1},{9,5},{13,9},{2,14},{6,2},{... | collective-permute-start | bytes 6152 | tf_op jit(solution)/shard_map/ppermute | solution.py:88
  115.4 4.8 %collective-permute-start.13 = (f32[1,1,512]{2,1,0:T(1,128)}, f32[1,1,512]{2,1,0:T(1,128)}, u32[]{:S(2)}, u32[]{:S(2)}) collective-permute-start(f32[1,1,512]{2,1,0:T(1,128)} %get-tuple-element.33), channel_id=1, source_target_pairs={{0,8},{4,12},{8,0},{12,4},{1,9},{5,13},{9,1},{13,5},{2,10},{6,14},... | collective-permute-start | bytes 6152 | tf_op jit(solution)/shard_map/ppermute | solution.py:88
  115.4 5.7 %collective-permute-start.12 = (f32[1,1,512]{2,1,0:T(1,128)}, f32[1,1,512]{2,1,0:T(1,128)}, u32[]{:S(2)}, u32[]{:S(2)}) collective-permute-start(f32[1,1,512]{2,1,0:T(1,128)} %get-tuple-element.31), channel_id=1, source_target_pairs={{0,4},{4,8},{8,12},{12,0},{1,5},{5,9},{9,13},{13,1},{2,6},{6,10},{... | collective-permute-start | bytes 6152 | tf_op jit(solution)/shard_map/ppermute | solution.py:88
  143.0 11.5 %collective-permute-start.16 = (bf16[260,768]{1,0:T(8,128)(2,1)S(1)}, bf16[260,768]{1,0:T(8,128)(2,1)S(1)}, u32[]{:S(2)}, u32[]{:S(2)}) collective-permute-start(bf16[260,768]{1,0:T(8,128)(2,1)S(1)} %copy.89), channel_id=1, source_target_pairs={{0,2},{2,0},{1,3},{3,1},{4,6},{6,4},{5,7},{7,5},{8,10},{10,8},{9,1... | collective-permute-start | bytes 1198088 | tf_op jit(solution)/shard_map/ppermute | solution.py:318
  179.1 5.9 %collective-permute-start.17 = (bf16[256,384]{1,0:T(8,128)(2,1)}, bf16[256,384]{1,0:T(8,128)(2,1)S(1)}, u32[]{:S(2)}, u32[]{:S(2)}) collective-permute-start(bf16[256,384]{1,0:T(8,128)(2,1)} %reduce-scatter.2.cloned.1.call-done), channel_id=1, source_target_pairs={{0,2},{2,0},{1,3},{3,1},{4,6},{6,4},{5,7},{7,5},{8,10},{10,8},{9,1... | collective-permute-start | bytes 589832 | tf_op jit(solution)/shard_map/ppermute | solution.py:325
  (37 other events, 94.8 us)
Sparse Core Ops, SparseCore 0:
  8.9 11.7 all-gather.3
  22.2 10.1 all-gather.5
  34.0 12.8 all-gather.7
  157.2 21.8 reduce-scatter.1

commit v5 on v4

--- a/solution.py
+++ b/solution.py
@@ -126,6 +126,11 @@
     out_last_full = lax.all_gather(w_out_last, "mp", axis=0, tiled=True)
     teacher_all = gather_cand(teacher, 1)
     cls_tokens = gather_cand(tokens[:, :, 0], 1)
+    row_count = lists * local_cands * seq_len
+    swap = [(0, 1), (1, 0)]
+    paired_lists = lax.axis_size("query") == 2
+    if paired_lists:
+        other_tokens = lax.ppermute(tokens.reshape(row_count, model_width), "query", swap)
     projected = mixed("qcsd,kdf->kqcsf", tokens, w_first).astype(jnp.bfloat16)
     cls_projected = mixed("qcd,kdf->kqcf", cls_tokens, w_first[1:]).astype(jnp.bfloat16)
     gathered_keys = cls_projected[0]
@@ -290,7 +295,6 @@
     )
     key_first = key_first.astype(jnp.bfloat16)
     val_first = val_first.astype(jnp.bfloat16)
-    row_count = lists * local_cands * seq_len
     stacked = jnp.stack([query_grad, key_first, val_first], 3).reshape(row_count, 3, local_width)
     cross_rows = lists * cand_count
     cross_stacked = jnp.stack(
@@ -302,7 +306,7 @@
     all_tokens = jnp.concatenate(
         [tokens.reshape(row_count, model_width), cls_tokens.reshape(cross_rows, model_width)], 0
     )
-    if lax.axis_size("query") != 2:
+    if not paired_lists:
         partial_grad = lax.psum_scatter(
             mixed("rd,rkf->dkf", all_tokens, all_rows).astype(jnp.bfloat16),
             "cand",
@@ -310,15 +314,22 @@
             tiled=True,
         )
         return sum_query(partial_grad).astype(jnp.float32)
-    swap = [(0, 1), (1, 0)]
     half = 3 * local_width // 2
     side = lax.axis_index("query")
-    other_tokens = lax.ppermute(all_tokens, "query", swap)
     flat_rows = all_rows.reshape(all_rows.shape[0], 3 * local_width)
-    other_rows = lax.ppermute(flat_rows, "query", swap)
+    cls_flat = cls_tokens.reshape(cross_rows, model_width)
+    sent = lax.ppermute(
+        jnp.concatenate([flat_rows.reshape(-1), cls_flat.reshape(-1)]), "query", swap
+    )
+    other_rows = sent[: flat_rows.size].reshape(flat_rows.shape)
+    other_cls = sent[flat_rows.size :].reshape(cls_flat.shape)
     own_half = lax.dynamic_slice_in_dim(flat_rows, side * half, half, 1)
     other_half = lax.dynamic_slice_in_dim(other_rows, side * half, half, 1)
-    paired = mixed("rd,rf->df", all_tokens, own_half) + mixed("rd,rf->df", other_tokens, other_half)
+    paired = (
+        mixed("rd,rf->df", all_tokens, own_half)
+        + mixed("rd,rf->df", other_tokens, other_half[:row_count])
+        + mixed("rd,rf->df", other_cls, other_half[row_count:])
+    )
     reduced = lax.psum_scatter(
         paired.astype(jnp.bfloat16), "cand", scatter_dimension=0, tiled=True
     )

time: 196 us -> 153 us (0.78)
  other arithmetic: 38.6 us -> 15.7 us
  local copies, waits for them, and re-layouts: 24.2 us -> 11.6 us
  matrix products: 28.1 us -> 21.5 us
    dot_general x31 -> x32, matrix products: 28.1 us -> 21.5 us  [mixed(): jnp.einsum(pattern, former, latter, preferred_element_type=jnp.float32)]
    another operation x12 -> x10, other arithmetic: 7.94 us -> 1.49 us
    another operation x9 -> x10, local copies, waits for them, and re-layouts: 5.03 us -> 1.03 us
    slice x2, local copies, waits for them, and re-layouts: 2.4 us -> 0.14 us  [local(): last_kv[1][:, :, 0]]
    another operation x4, other arithmetic: 3.98 us -> 1.99 us  [gather_cand(): jnp.stack(parts, 0)]
    ppermute x3, waiting for transfers between devices: 1.68 us -> 3.66 us  [scatter_cand(): lax.ppermute(piece, 'cand', [(j, (j + k) % count) for j in range(count)])]
  transfers between devices with their start and end apart: 22 -> 22, of which waited for: 6 -> 9; matrix products, arithmetic and copies ran while one was open for 43% -> 27% of each run, Pallas kernels for 0% -> 0%
where the time goes in v5:
time: 153 us; the launch traced here: 152 us
  waiting for transfers between devices  46.8 us (31%)
  starting transfers between devices  28.6 us (19%)
  between operations  21.9 us (14%)
  matrix products  21.5 us (14%)
  other arithmetic  15.7 us (10%)
  local copies, waits for them, and re-layouts  11.6 us (8%)
  blocking collectives  6.23 us (4%)
    reduce_scatter x1, waiting for transfers between devices, local(): lax.psum_scatter(paired.astype(jnp.bfloat16), 'cand', scatter_dimension=0...  22 us
    dot_general x32, matrix products, mixed(): jnp.einsum(pattern, former, latter, preferred_element_type=jnp.float32)  21.5 us
    ppermute x9, starting transfers between devices, gather_cand(): lax.ppermute(block, 'cand', [(j, (j + k) % count) for j in range(count)])  12.2 us
    ppermute x1, waiting for transfers between devices, local(): lax.ppermute(jnp.concatenate([flat_rows.reshape(-1), cls_flat.reshape(-1)...  8.01 us
    ppermute x3, starting transfers between devices, sum_cand(): lax.ppermute(block, 'cand', [(j, (j + k) % count) for j in range(count)])  7.77 us
    ppermute x9, waiting for transfers between devices, gather_cand(): lax.ppermute(block, 'cand', [(j, (j + k) % count) for j in range(count)])  7.11 us
    ppermute x1, waiting for transfers between devices, local(): partner = lax.ppermute(reduced, 'query', swap)  4.48 us
    ppermute x3, starting transfers between devices, scatter_cand(): lax.ppermute(piece, 'cand', [(j, (j + k) % count) for j in range(count)])  4.1 us
  transfers between devices with their start and end apart: 22, of which 9 were waited for; matrix products, arithmetic and copies ran while one was open for 27% of the time, Pallas kernels for 0%

profile of v5, /device:TPU:0, one launch (start us, length us, event | category | flops | bytes accessed | tf_op | source)
XLA Modules:
  0.0 152.2 jit_solution(5445848692927797432)
XLA Ops:
  8.8 5.0 %collective-permute-start.2 = (bf16[1,1,1024]{2,1,0:T(2,128)(2,1)S(1)}, bf16[1,1,1024]{2,1,0:T(2,128)(2,1)S(1)}, u32[]{:S(2)}, u32[]{:S(2)}) collective-permute-start(bf16[1,1,1024]{2,1,0:T(2,128)(2,1)S(1)} %get-tuple-element.23), channel_id=1, source_target_pairs={{0,12},{4,0},{8,4},{12,8},{1,13},{5,1},{9,5},{13,9},{2,14},{6,2},{... | collective-permute-start | bytes 6152 | tf_op jit(solution)/shard_map/ppermute | solution.py:60
  14.8 2.8 %collective-permute-start.11 = (f32[1,1]{1,0:T(1,128)}, f32[1,1]{1,0:T(1,128)}, u32[]{:S(2)}, u32[]{:S(2)}) collective-permute-start(f32[1,1]{1,0:T(1,128)} %param.12), channel_id=1, source_target_pairs={{0,12},{4,0},{8,4},{12,8},{1,13},{5,1},{9,5},{13,9},{2,14},{6,2},{... | collective-permute-start | bytes 20 | tf_op jit(solution)/shard_map/ppermute | solution.py:60
  19.6 1.7 %fusion.5 = bf16[3,1,1,256,256]{3,4,0,2,1:T(8,128)(2,1)S(1)} fusion(bf16[3,1024,256]{2,1,0:T(8,128)(2,1)S(1)} %copy-done.3, bf16[1,1,256,1024]{3,2,1,0:T(8,128)(2,1)} %param.10), kind=kOutput, calls=%fused_computation.15 | convolution fusion | flops 402849792 | bytes 2490368 | tf_op jit(solution)/shard_map/qcsd,kdf->kqcsf/dot_general | solution.py:15
  23.9 1.5 %collective-permute-start.16 = (bf16[256,1024]{1,0:T(8,128)(2,1)}, bf16[256,1024]{1,0:T(8,128)(2,1)}, u32[]{:S(2)}, u32[]{:S(2)}) collective-permute-start(bf16[256,1024]{1,0:T(8,128)(2,1)} %bitcast), channel_id=1, source_target_pairs={{0,2},{2,0},{1,3},{3,1},{4,6},{6,4},{5,7},{7,5},{8,10},{10,8},{9,1... | collective-permute-start | bytes 1572872 | tf_op jit(solution)/shard_map/ppermute | solution.py:133
  25.4 3.8 %collective-permute-done.9 = f32[1,1]{1,0:T(1,128)} collective-permute-done((f32[1,1]{1,0:T(1,128)}, f32[1,1]{1,0:T(1,128)}, u32[]{:S(2)}, u32[]{:S(2)}) %collective-permute-start.9) | collective-permute-done | bytes 36 | tf_op jit(solution)/shard_map/ppermute | solution.py:60
  29.2 1.9 %maximum_bitcast_fusion.2 = f32[4]{0:T(128)S(1)} fusion(f32[1,1,1]{0,2,1:T(1,128)} %bitcast.73, f32[1,1,1]{0,2,1:T(1,128)} %bitcast.72, f32[1,1,1]{0,2,1:T(1,128)} %bitcast.71, f32[1,1,1]{0,2,1:T(1,128)} %bitcast.354), kind=kLoop, calls=%fused_computation.218 | loop fusion | flops 12 | bytes 32 | tf_op jit(solution)/shard_map/stack | solution.py:63
  32.4 1.3 exponential_reduce_fusion
  39.5 2.0 %all_gather.18 = bf16[1,1,256,512]{2,3,1,0:T(8,128)(2,1)S(1)} all-gather(bf16[1,1,256,256]{2,3,1,0:T(8,128)(2,1)S(1)} %bitcast.379), channel_id=1, replica_groups=mesh['groups'=2,'cand'=4,'query'=2,'mp'=2] {'mp'}, dimensions={3}, use_global_device_ids=true | all-gather | bytes 393216 | tf_op jit(solution)/shard_map/all_gather | solution.py:156
  42.0 2.1 %fusion.127 = (f32[256]{0:T(256)S(1)}, f32[1,1,256,1024]{3,2,1,0:T(8,128)S(1)}) fusion(bf16[512,1024]{1,0:T(8,128)(2,1)} %all-gather.4.cloned.1.call-done, bf16[1,1,256,512]{2,3,1,0:T(8,128)(2,1)S(1)} %all_gather.18, bf16[1,1,256,1024]{3,2,1,0:T(8,128)(2,1)} %param.10), kind=kOutput, calls=%fused_computation.245 | convolution fusion | flops 269221632 | bytes 2884608 | tf_op jit(solution)/shard_map/qcsf,fd->qcsd/dot_general | solution.py:15
  44.7 1.1 copy-done
  46.7 1.9 %collective-permute-start.3 = (bf16[1,1,512]{2,1,0:T(2,128)(2,1)S(1)}, bf16[1,1,512]{2,1,0:T(2,128)(2,1)S(1)}, u32[]{:S(2)}, u32[]{:S(2)}) collective-permute-start(bf16[1,1,512]{2,1,0:T(2,128)(2,1)S(1)} %pad_maximum_fusion.4), channel_id=1, source_target_pairs={{0,4},{4,8},{8,12},{12,0},{1,5},{5,9},{9,13},{13,1},{2,6},{6,10},{... | collective-permute-start | bytes 3080 | tf_op jit(solution)/shard_map/ppermute | solution.py:60
  51.2 1.4 collective-permute-done.3
  54.7 1.8 %all_gather.20 = bf16[1,1,512]{2,1,0:T(2,128)(2,1)S(1)} all-gather(bf16[1,1,256]{2,1,0:T(2,128)(2,1)S(1)} %convert_element_type.234), channel_id=1, replica_groups=mesh['groups'=2,'cand'=4,'query'=2,'mp'=2] {'mp'}, dimensions={2}, use_global_device_ids=true | all-gather | bytes 1536 | tf_op jit(solution)/shard_map/all_gather | solution.py:185
  56.5 1.5 fusion.79
  61.8 1.9 %collective-permute-start.6 = (f32[1]{0:T(128)}, f32[1]{0:T(128)}, u32[]{:S(2)}, u32[]{:S(2)}) collective-permute-start(f32[1]{0:T(128)} %bitcast.68), channel_id=1, source_target_pairs={{0,4},{4,8},{8,12},{12,0},{1,5},{5,9},{9,13},{13,1},{2,6},{6,10},{... | collective-permute-start | bytes 20 | tf_op jit(solution)/shard_map/ppermute | solution.py:75
  63.7 3.3 %collective-permute-start.7 = (f32[1]{0:T(128)}, f32[1]{0:T(128)}, u32[]{:S(2)}, u32[]{:S(2)}) collective-permute-start(f32[1]{0:T(128)} %bitcast.68), channel_id=1, source_target_pairs={{0,8},{4,12},{8,0},{12,4},{1,9},{5,13},{9,1},{13,5},{2,10},{6,14},... | collective-permute-start | bytes 20 | tf_op jit(solution)/shard_map/ppermute | solution.py:75
  67.1 2.6 %collective-permute-start.8 = (f32[1]{0:T(128)}, f32[1]{0:T(128)}, u32[]{:S(2)}, u32[]{:S(2)}) collective-permute-start(f32[1]{0:T(128)} %bitcast.68), channel_id=1, source_target_pairs={{0,12},{4,0},{8,4},{12,8},{1,13},{5,1},{9,5},{13,9},{2,14},{6,2},{... | collective-permute-start | bytes 20 | tf_op jit(solution)/shard_map/ppermute | solution.py:75
  75.5 2.9 %collective-permute-start.14 = (f32[1,1,512]{2,1,0:T(1,128)S(1)}, f32[1,1,512]{2,1,0:T(1,128)S(1)}, u32[]{:S(2)}, u32[]{:S(2)}) collective-permute-start(f32[1,1,512]{2,1,0:T(1,128)S(1)} %get-tuple-element.34), channel_id=1, source_target_pairs={{0,12},{4,0},{8,4},{12,8},{1,13},{5,1},{9,5},{13,9},{2,14},{6,2},{... | collective-permute-start | bytes 6152 | tf_op jit(solution)/shard_map/ppermute | solution.py:88
  80.3 2.5 %collective-permute-done.13 = f32[1,1,512]{2,1,0:T(1,128)S(1)} collective-permute-done((f32[1,1,512]{2,1,0:T(1,128)S(1)}, f32[1,1,512]{2,1,0:T(1,128)S(1)}, u32[]{:S(2)}, u32[]{:S(2)}) %collective-permute-start.13) | collective-permute-done | bytes 2080 | tf_op jit(solution)/shard_map/ppermute | solution.py:88
  84.2 2.5 %all_gather.22 = bf16[1,1,513,512]{2,3,1,0:T(8,128)(2,1)S(1)} all-gather(bf16[1,1,513,256]{2,3,1,0:T(8,128)(2,1)S(1)} %pad_maximum_fusion.3), channel_id=1, replica_groups=mesh['groups'=2,'cand'=4,'query'=2,'mp'=2] {'mp'}, dimensions={3}, use_global_device_ids=true | all-gather | bytes 787968 | tf_op jit(solution)/shard_map/all_gather | solution.py:246
  86.8 1.8 %fusion.10 = f32[256,1024]{1,0:T(8,128)S(1)} fusion(bf16[3,1024,512]{2,1,0:T(8,128)(2,1)} %all-gather.8.cloned.1.call-done, bf16[1,1,513,512]{2,3,1,0:T(8,128)(2,1)S(1)} %all_gather.22), kind=kOutput, calls=%fused_computation.30 | convolution fusion | flops 268435456 | bytes 2359296 | tf_op jit(solution)/shard_map/qcsf,df->qcsd/dot_general | solution.py:15
  88.6 1.6 %fusion.9 = f32[1,1024]{1,0:T(1,128)S(1)} fusion(bf16[512,1]{0,1:T(2,128)(2,1)S(1)} %reshape.1205, bf16[3,1024,512]{2,1,0:T(8,128)(2,1)} %all-gather.8.cloned.1.call-done), kind=kOutput, calls=%fused_computation.27 | convolution fusion | flops 1048576 | bytes 1053696 | tf_op jit(solution)/shard_map/qcf,df->qcd/dot_general | solution.py:15
  90.3 2.2 %fusion.11 = (f32[256]{0:T(256)S(1)}, f32[256,1024]{1,0:T(8,128)S(1)}) fusion(f32[1,1,256,1024]{3,2,1,0:T(8,128)S(1)} %get-tuple-element.47, f32[256]{0:T(256)S(1)} %copy-done.16, f32[256]{0:T(256)S(1)} %copy-done.11, f32[1024]{0:T(1024)S(1)} %copy-done.20, f32[1024]{0:T(1024)S(1)} %copy-done.25, f32[1024]{0:T(1024)S(1)} %bitcast.387, ...), kind=kOutput, calls=%fused_computation.32 | convolution fusion | flops 271056640 | bytes 4472064 | tf_op jit(solution)/shard_map/qcsf,df->qcsd/dot_general | solution.py:15
  94.4 1.6 %convolution_convert_fusion.3 = bf16[256,256]{0,1:T(8,128)(2,1)S(1)} fusion(bf16[256,1024]{1,0:T(8,128)(2,1)} %param.14, f32[1,1,256,1024]{3,2,1,0:T(8,128)S(1)} %get-tuple-element.47, f32[256,1024]{1,0:T(8,128)S(1)} %get-tuple-element.49, f32[256]{0:T(256)} %broadcast_multiply_fusion.1, f32[256]{0:T(256)S(1)} %broadcast_multiply_fusion.2, ...), kind=kOutput, calls=%fused_computation.23 | convolution fusion | flops 136118272 | bytes 2756608 | tf_op jit(solution)/shard_map/qcsd,fd->qcsf/dot_general | solution.py:15
  100.4 1.6 %collective-permute-start.15 = (bf16[203776]{0:T(1024)(128)(2,1)S(1)}, bf16[203776]{0:T(1024)(128)(2,1)S(1)}, u32[]{:S(2)}, u32[]{:S(2)}) collective-permute-start(bf16[203776]{0:T(1024)(128)(2,1)S(1)} %pad_maximum_fusion.1), channel_id=1, source_target_pairs={{0,2},{2,0},{1,3},{3,1},{4,6},{6,4},{5,7},{7,5},{8,10},{10,8},{9,1... | collective-permute-start | bytes 1222664 | tf_op jit(solution)/shard_map/ppermute | solution.py:321
  102.2 1.8 %fusion.18 = f32[1024,384]{1,0:T(8,128)S(1)} fusion(bf16[4,1024]{1,0:T(4,128)(2,1)S(1)} %broadcast_select_fusion, bf16[256,1024]{1,0:T(8,128)(2,1)} %bitcast, s32[]{:T(128)S(6)} %select_n.273, bf16[256,768]{0,1:T(8,128)(2,1)S(1)} %bitcast.359, bf16[4,768]{0,1:T(8,128)(2,1)S(1)} %copy.122), kind=kOutput, calls=%fused_computation.49 | convolution fusion | flops 205936640 | bytes 2504708 | tf_op jit(solution)/shard_map/rd,rf->df/dot_general | solution.py:15
  103.9 8.0 %collective-permute-done.15 = bf16[203776]{0:T(1024)(128)(2,1)S(1)} collective-permute-done((bf16[203776]{0:T(1024)(128)(2,1)S(1)}, bf16[203776]{0:T(1024)(128)(2,1)S(1)}, u32[]{:S(2)}, u32[]{:S(2)}) %collective-permute-start.15) | collective-permute-done | bytes 407584 | tf_op jit(solution)/shard_map/ppermute | solution.py:321
  112.4 1.5 %fusion.44 = f32[384,1024]{0,1:T(8,128)S(1)} fusion(bf16[256,1024]{1,0:T(8,128)(2,1)} %collective-permute-done.16, bf16[260,768]{1,0:T(8,128)(2,1)S(1)} %reshape.1127, s32[]{:T(128)S(6)} %select_n.273), kind=kOutput, calls=%fused_computation.84 | convolution fusion | flops 201326592 | bytes 2293764 | tf_op jit(solution)/shard_map/rd,rf->df/dot_general | solution.py:15
  113.9 1.3 fusion.1
  115.3 22.0 %reduce-scatter.2.cloned.1.call-done = bf16[256,384]{1,0:T(8,128)(2,1)} async-done(((bf16[1024,384]{1,0:T(8,128)(2,1)}), bf16[256,384]{1,0:T(8,128)(2,1)}) %reduce-scatter.2.cloned.1.call-update) | async-done | bytes 196624 | tf_op jit(solution)/shard_map/reduce_scatter | solution.py:333
  137.3 1.4 collective-permute-start.17
  138.7 4.5 %collective-permute-done.17 = bf16[256,384]{1,0:T(8,128)(2,1)S(1)} collective-permute-done((bf16[256,384]{1,0:T(8,128)(2,1)}, bf16[256,384]{1,0:T(8,128)(2,1)S(1)}, u32[]{:S(2)}, u32[]{:S(2)}) %collective-permute-start.17) | collective-permute-done | bytes 196640 | tf_op jit(solution)/shard_map/ppermute | solution.py:336
  (244 shorter events, 35.4 us)
Async XLA Ops:
  6.5 13.1 %copy-start.3 = (bf16[3,1024,256]{2,1,0:T(8,128)(2,1)S(1)}, bf16[3,1024,256]{2,1,0:T(8,128)(2,1)}, u32[]{:S(2)}) copy-start(bf16[3,1024,256]{2,1,0:T(8,128)(2,1)} %param.13) | copy-start | bytes 4718596
  6.5 35.5 %all-gather.4.cloned.1.call-start = ((), (), s32[]{:S(2)}) async-start(), calls=%async_computation.1 | async-start | bytes 1572864 | tf_op jit(solution)/shard_map/all_gather | solution.py:124
  7.3 49.2 %all-gather.6.cloned.1.call-start = ((), (), s32[]{:S(2)}) async-start(), calls=%async_computation.2 | async-start | bytes 1572864 | tf_op jit(solution)/shard_map/all_gather | solution.py:126
  8.0 78.8 %all-gather.8.cloned.1.call-start = ((), (), s32[]{:S(2)}) async-start(), calls=%async_computation.3 | async-start | bytes 4718592 | tf_op jit(solution)/shard_map/all_gather | solution.py:125
  8.8 26.4 %collective-permute-start.2 = (bf16[1,1,1024]{2,1,0:T(2,128)(2,1)S(1)}, bf16[1,1,1024]{2,1,0:T(2,128)(2,1)S(1)}, u32[]{:S(2)}, u32[]{:S(2)}) collective-permute-start(bf16[1,1,1024]{2,1,0:T(2,128)(2,1)S(1)} %get-tuple-element.23), channel_id=1, source_target_pairs={{0,12},{4,0},{8,4},{12,8},{1,13},{5,1},{9,5},{13,9},{2,14},{6,2},{... | collective-permute-start | bytes 6152 | tf_op jit(solution)/shard_map/ppermute | solution.py:60
  13.8 21.4 %collective-permute-start.1 = (bf16[1,1,1024]{2,1,0:T(2,128)(2,1)S(1)}, bf16[1,1,1024]{2,1,0:T(2,128)(2,1)S(1)}, u32[]{:S(2)}, u32[]{:S(2)}) collective-permute-start(bf16[1,1,1024]{2,1,0:T(2,128)(2,1)S(1)} %get-tuple-element.23), channel_id=1, source_target_pairs={{0,8},{4,12},{8,0},{12,4},{1,9},{5,13},{9,1},{13,5},{2,10},{6,14},... | collective-permute-start | bytes 6152 | tf_op jit(solution)/shard_map/ppermute | solution.py:60
  13.8 21.4 %collective-permute-start = (bf16[1,1,1024]{2,1,0:T(2,128)(2,1)S(1)}, bf16[1,1,1024]{2,1,0:T(2,128)(2,1)S(1)}, u32[]{:S(2)}, u32[]{:S(2)}) collective-permute-start(bf16[1,1,1024]{2,1,0:T(2,128)(2,1)S(1)} %get-tuple-element.23), channel_id=1, source_target_pairs={{0,4},{4,8},{8,12},{12,0},{1,5},{5,9},{9,13},{13,1},{2,6},{6,10},{... | collective-permute-start | bytes 6152 | tf_op jit(solution)/shard_map/ppermute | solution.py:60
  14.8 8.9 %collective-permute-start.11 = (f32[1,1]{1,0:T(1,128)}, f32[1,1]{1,0:T(1,128)}, u32[]{:S(2)}, u32[]{:S(2)}) collective-permute-start(f32[1,1]{1,0:T(1,128)} %param.12), channel_id=1, source_target_pairs={{0,12},{4,0},{8,4},{12,8},{1,13},{5,1},{9,5},{13,9},{2,14},{6,2},{... | collective-permute-start | bytes 20 | tf_op jit(solution)/shard_map/ppermute | solution.py:60
  17.7 6.2 %collective-permute-start.10 = (f32[1,1]{1,0:T(1,128)}, f32[1,1]{1,0:T(1,128)}, u32[]{:S(2)}, u32[]{:S(2)}) collective-permute-start(f32[1,1]{1,0:T(1,128)} %param.12), channel_id=1, source_target_pairs={{0,8},{4,12},{8,0},{12,4},{1,9},{5,13},{9,1},{13,5},{2,10},{6,14},... | collective-permute-start | bytes 20 | tf_op jit(solution)/shard_map/ppermute | solution.py:60
  18.8 118.5 %reduce-scatter.2.cloned.1.call-start = ((), (), s32[]{:S(2)}) async-start(), calls=%async_computation.4 | async-start | bytes 983040 | tf_op jit(solution)/shard_map/reduce_scatter | solution.py:333
  18.9 65.1 %copy-start.12 = (pred[256]{0:T(512)(128)(4,1)}, pred[256]{0:T(512)(128)(4,1)S(1)}, u32[]{:S(2)}) copy-start(pred[256]{0:T(512)(128)(4,1)S(1)} %iota_compare_fusion.1) | copy-start | bytes 772
  23.8 5.5 %collective-permute-start.9 = (f32[1,1]{1,0:T(1,128)}, f32[1,1]{1,0:T(1,128)}, u32[]{:S(2)}, u32[]{:S(2)}) collective-permute-start(f32[1,1]{1,0:T(1,128)} %param.12), channel_id=1, source_target_pairs={{0,4},{4,8},{8,12},{12,0},{1,5},{5,9},{9,13},{13,1},{2,6},{6,10},{... | collective-permute-start | bytes 20 | tf_op jit(solution)/shard_map/ppermute | solution.py:60
  23.9 88.5 %collective-permute-start.16 = (bf16[256,1024]{1,0:T(8,128)(2,1)}, bf16[256,1024]{1,0:T(8,128)(2,1)}, u32[]{:S(2)}, u32[]{:S(2)}) collective-permute-start(bf16[256,1024]{1,0:T(8,128)(2,1)} %bitcast), channel_id=1, source_target_pairs={{0,2},{2,0},{1,3},{3,1},{4,6},{6,4},{5,7},{7,5},{8,10},{10,8},{9,1... | collective-permute-start | bytes 1572872 | tf_op jit(solution)/shard_map/ppermute | solution.py:133
  46.5 14.0 %copy-start.8 = (f32[1024]{0:T(1024)S(1)}, f32[1024]{0:T(1024)}, u32[]{:S(2)}) copy-start(f32[1024]{0:T(1024)} %param.18) | copy-start | bytes 12292
  46.5 14.0 %copy-start.9 = (f32[1024]{0:T(1024)S(1)}, f32[1024]{0:T(1024)}, u32[]{:S(2)}) copy-start(f32[1024]{0:T(1024)} %param.19) | copy-start | bytes 12292
  46.5 27.6 %copy-start.1 = (bf16[256,1024]{1,0:T(8,128)(2,1)S(1)}, bf16[256,1024]{1,0:T(8,128)(2,1)}, u32[]{:S(2)}) copy-start(bf16[256,1024]{1,0:T(8,128)(2,1)} %param.17) | copy-start | bytes 1572868
  46.6 3.6 %collective-permute-start.5 = (bf16[1,1,512]{2,1,0:T(2,128)(2,1)S(1)}, bf16[1,1,512]{2,1,0:T(2,128)(2,1)S(1)}, u32[]{:S(2)}, u32[]{:S(2)}) collective-permute-start(bf16[1,1,512]{2,1,0:T(2,128)(2,1)S(1)} %pad_maximum_fusion.4), channel_id=1, source_target_pairs={{0,12},{4,0},{8,4},{12,8},{1,13},{5,1},{9,5},{13,9},{2,14},{6,2},{... | collective-permute-start | bytes 3080 | tf_op jit(solution)/shard_map/ppermute | solution.py:60
  46.7 4.5 %collective-permute-start.4 = (bf16[1,1,512]{2,1,0:T(2,128)(2,1)S(1)}, bf16[1,1,512]{2,1,0:T(2,128)(2,1)S(1)}, u32[]{:S(2)}, u32[]{:S(2)}) collective-permute-start(bf16[1,1,512]{2,1,0:T(2,128)(2,1)S(1)} %pad_maximum_fusion.4), channel_id=1, source_target_pairs={{0,8},{4,12},{8,0},{12,4},{1,9},{5,13},{9,1},{13,5},{2,10},{6,14},... | collective-permute-start | bytes 3080 | tf_op jit(solution)/shard_map/ppermute | solution.py:60
  46.7 5.9 %collective-permute-start.3 = (bf16[1,1,512]{2,1,0:T(2,128)(2,1)S(1)}, bf16[1,1,512]{2,1,0:T(2,128)(2,1)S(1)}, u32[]{:S(2)}, u32[]{:S(2)}) collective-permute-start(bf16[1,1,512]{2,1,0:T(2,128)(2,1)S(1)} %pad_maximum_fusion.4), channel_id=1, source_target_pairs={{0,4},{4,8},{8,12},{12,0},{1,5},{5,9},{9,13},{13,1},{2,6},{6,10},{... | collective-permute-start | bytes 3080 | tf_op jit(solution)/shard_map/ppermute | solution.py:60
  61.8 7.8 %collective-permute-start.6 = (f32[1]{0:T(128)}, f32[1]{0:T(128)}, u32[]{:S(2)}, u32[]{:S(2)}) collective-permute-start(f32[1]{0:T(128)} %bitcast.68), channel_id=1, source_target_pairs={{0,4},{4,8},{8,12},{12,0},{1,5},{5,9},{9,13},{13,1},{2,6},{6,10},{... | collective-permute-start | bytes 20 | tf_op jit(solution)/shard_map/ppermute | solution.py:75
  63.7 6.5 %collective-permute-start.7 = (f32[1]{0:T(128)}, f32[1]{0:T(128)}, u32[]{:S(2)}, u32[]{:S(2)}) collective-permute-start(f32[1]{0:T(128)} %bitcast.68), channel_id=1, source_target_pairs={{0,8},{4,12},{8,0},{12,4},{1,9},{5,13},{9,1},{13,5},{2,10},{6,14},... | collective-permute-start | bytes 20 | tf_op jit(solution)/shard_map/ppermute | solution.py:75
  67.1 3.7 %collective-permute-start.8 = (f32[1]{0:T(128)}, f32[1]{0:T(128)}, u32[]{:S(2)}, u32[]{:S(2)}) collective-permute-start(f32[1]{0:T(128)} %bitcast.68), channel_id=1, source_target_pairs={{0,12},{4,0},{8,4},{12,8},{1,13},{5,1},{9,5},{13,9},{2,14},{6,2},{... | collective-permute-start | bytes 20 | tf_op jit(solution)/shard_map/ppermute | solution.py:75
  75.5 4.8 %collective-permute-start.14 = (f32[1,1,512]{2,1,0:T(1,128)S(1)}, f32[1,1,512]{2,1,0:T(1,128)S(1)}, u32[]{:S(2)}, u32[]{:S(2)}) collective-permute-start(f32[1,1,512]{2,1,0:T(1,128)S(1)} %get-tuple-element.34), channel_id=1, source_target_pairs={{0,12},{4,0},{8,4},{12,8},{1,13},{5,1},{9,5},{13,9},{2,14},{6,2},{... | collective-permute-start | bytes 6152 | tf_op jit(solution)/shard_map/ppermute | solution.py:88
  78.4 4.5 %collective-permute-start.13 = (f32[1,1,512]{2,1,0:T(1,128)S(1)}, f32[1,1,512]{2,1,0:T(1,128)S(1)}, u32[]{:S(2)}, u32[]{:S(2)}) collective-permute-start(f32[1,1,512]{2,1,0:T(1,128)S(1)} %get-tuple-element.35), channel_id=1, source_target_pairs={{0,8},{4,12},{8,0},{12,4},{1,9},{5,13},{9,1},{13,5},{2,10},{6,14},... | collective-permute-start | bytes 6152 | tf_op jit(solution)/shard_map/ppermute | solution.py:88
  78.6 5.4 %collective-permute-start.12 = (f32[1,1,512]{2,1,0:T(1,128)S(1)}, f32[1,1,512]{2,1,0:T(1,128)S(1)}, u32[]{:S(2)}, u32[]{:S(2)}) collective-permute-start(f32[1,1,512]{2,1,0:T(1,128)S(1)} %get-tuple-element.33), channel_id=1, source_target_pairs={{0,4},{4,8},{8,12},{12,0},{1,5},{5,9},{9,13},{13,1},{2,6},{6,10},{... | collective-permute-start | bytes 6152 | tf_op jit(solution)/shard_map/ppermute | solution.py:88
  86.6 3.6 %copy-start.2 = (bf16[1,1,513,512]{2,3,1,0:T(8,128)(2,1)}, bf16[1,1,513,512]{2,3,1,0:T(8,128)(2,1)S(1)}, u32[]{:S(2)}) copy-start(bf16[1,1,513,512]{2,3,1,0:T(8,128)(2,1)S(1)} %all_gather.22) | copy-start | bytes 1575940
  86.8 3.4 %copy-start.13 = (pred[256]{0:T(512)(128)(4,1)S(1)}, pred[256]{0:T(512)(128)(4,1)}, u32[]{:S(2)}) copy-start(pred[256]{0:T(512)(128)(4,1)} %copy-done.12) | copy-start | bytes 772
  86.8 3.4 %copy-start.16 = (f32[256]{0:T(256)S(1)}, f32[256]{0:T(256)}, u32[]{:S(2)}) copy-start(f32[256]{0:T(256)} %copy-done.15) | copy-start | bytes 3076
  86.8 3.4 %copy-start.20 = (f32[1024]{0:T(1024)S(1)}, f32[1024]{0:T(1024)}, u32[]{:S(2)}) copy-start(f32[1024]{0:T(1024)} %param.15) | copy-start | bytes 12292
  86.8 3.4 %copy-start.25 = (f32[1024]{0:T(1024)S(1)}, f32[1024]{0:T(1024)}, u32[]{:S(2)}) copy-start(f32[1024]{0:T(1024)} %get-tuple-element.20) | copy-start | bytes 12292
  100.4 11.5 %collective-permute-start.15 = (bf16[203776]{0:T(1024)(128)(2,1)S(1)}, bf16[203776]{0:T(1024)(128)(2,1)S(1)}, u32[]{:S(2)}, u32[]{:S(2)}) collective-permute-start(bf16[203776]{0:T(1024)(128)(2,1)S(1)} %pad_maximum_fusion.1), channel_id=1, source_target_pairs={{0,2},{2,0},{1,3},{3,1},{4,6},{6,4},{5,7},{7,5},{8,10},{10,8},{9,1... | collective-permute-start | bytes 1222664 | tf_op jit(solution)/shard_map/ppermute | solution.py:321
  137.3 5.9 %collective-permute-start.17 = (bf16[256,384]{1,0:T(8,128)(2,1)}, bf16[256,384]{1,0:T(8,128)(2,1)S(1)}, u32[]{:S(2)}, u32[]{:S(2)}) collective-permute-start(bf16[256,384]{1,0:T(8,128)(2,1)} %reduce-scatter.2.cloned.1.call-done), channel_id=1, source_target_pairs={{0,2},{2,0},{1,3},{3,1},{4,6},{6,4},{5,7},{7,5},{8,10},{10,8},{9,1... | collective-permute-start | bytes 589832 | tf_op jit(solution)/shard_map/ppermute | solution.py:336
  (17 other events, 23.9 us)
Sparse Core Ops, SparseCore 0:
  8.9 11.7 all-gather.3
  22.2 10.1 all-gather.5
  34.0 12.8 all-gather.7
  115.4 21.8 reduce-scatter.1

commit v6 on v5

--- a/solution.py
+++ b/solution.py
@@ -124,8 +124,11 @@
     out_first_full = lax.all_gather(w_out_first, "mp", axis=0, tiled=True)
     last_full = lax.all_gather(w_last, "mp", axis=2, tiled=True)
     out_last_full = lax.all_gather(w_out_last, "mp", axis=0, tiled=True)
-    teacher_all = gather_cand(teacher, 1)
-    cls_tokens = gather_cand(tokens[:, :, 0], 1)
+    cls_and_teacher = gather_cand(
+        jnp.concatenate([tokens[:, :, 0].astype(jnp.float32), teacher[..., None]], -1), 1
+    )
+    cls_tokens = cls_and_teacher[..., :model_width].astype(jnp.bfloat16)
+    teacher_all = cls_and_teacher[..., model_width]
     row_count = lists * local_cands * seq_len
     swap = [(0, 1), (1, 0)]
     paired_lists = lax.axis_size("query") == 2
@@ -318,13 +321,13 @@
     side = lax.axis_index("query")
     flat_rows = all_rows.reshape(all_rows.shape[0], 3 * local_width)
     cls_flat = cls_tokens.reshape(cross_rows, model_width)
+    own_half = lax.dynamic_slice_in_dim(flat_rows, side * half, half, 1)
+    given_half = lax.dynamic_slice_in_dim(flat_rows, (1 - side) * half, half, 1)
     sent = lax.ppermute(
-        jnp.concatenate([flat_rows.reshape(-1), cls_flat.reshape(-1)]), "query", swap
-    )
-    other_rows = sent[: flat_rows.size].reshape(flat_rows.shape)
-    other_cls = sent[flat_rows.size :].reshape(cls_flat.shape)
-    own_half = lax.dynamic_slice_in_dim(flat_rows, side * half, half, 1)
-    other_half = lax.dynamic_slice_in_dim(other_rows, side * half, half, 1)
+        jnp.concatenate([given_half.reshape(-1), cls_flat.reshape(-1)]), "query", swap
+    )
+    other_half = sent[: given_half.size].reshape(given_half.shape)
+    other_cls = sent[given_half.size :].reshape(cls_flat.shape)
     paired = (
         mixed("rd,rf->df", all_tokens, own_half)
         + mixed("rd,rf->df", other_tokens, other_half[:row_count])

time: 153 us -> 145 us (0.948)
  waiting for transfers between devices: 46.8 us -> 39.2 us
  other arithmetic: 15.7 us -> 19.1 us
  starting transfers between devices: 28.6 us -> 25.7 us
    ppermute x9 -> x6, waiting for transfers between devices: 7.11 us -> 2.77 us  [gather_cand(): lax.ppermute(block, 'cand', [(j, (j + k) % count) for j in range(count)])]
    ppermute x1, waiting for transfers between devices: 8.01 us -> 5.9 us  [local(): lax.ppermute(jnp.concatenate([given_half.reshape(-1), cls_flat.reshape(-1...]
    ppermute x9 -> x6, starting transfers between devices: 12.2 us -> 10.1 us  [gather_cand(): lax.ppermute(block, 'cand', [(j, (j + k) % count) for j in range(count)])]
    unnamed x59 -> x73, local copies, waits for them, and re-layouts: 3.15 us -> 3.31 us
  transfers between devices with their start and end apart: 22 -> 19, of which waited for: 9 -> 7; matrix products, arithmetic and copies ran while one was open for 27% -> 30% of each run, Pallas kernels for 0% -> 0%
where the time goes in v6:
time: 145 us; the launch traced here: 144 us
  waiting for transfers between devices  39.2 us (27%)
  starting transfers between devices  25.7 us (18%)
  between operations  22 us (15%)
  matrix products  20.2 us (14%)
  other arithmetic  19.1 us (13%)
  local copies, waits for them, and re-layouts  11.6 us (8%)
  blocking collectives  6.23 us (4%)
    reduce_scatter x1, waiting for transfers between devices, local(): lax.psum_scatter(paired.astype(jnp.bfloat16), 'cand', scatter_dimension=0...  21.1 us
    dot_general x32, matrix products, mixed(): jnp.einsum(pattern, former, latter, preferred_element_type=jnp.float32)  20.2 us
    ppermute x6, starting transfers between devices, gather_cand(): lax.ppermute(block, 'cand', [(j, (j + k) % count) for j in range(count)])  10.1 us
    ppermute x3, starting transfers between devices, sum_cand(): lax.ppermute(block, 'cand', [(j, (j + k) % count) for j in range(count)])  7.77 us
    ppermute x1, waiting for transfers between devices, local(): lax.ppermute(jnp.concatenate([given_half.reshape(-1), cls_flat.reshape(-1...  5.9 us
    ppermute x1, waiting for transfers between devices, local(): partner = lax.ppermute(reduced, 'query', swap)  4.41 us
    ppermute x3, starting transfers between devices, scatter_cand(): lax.ppermute(piece, 'cand', [(j, (j + k) % count) for j in range(count)])  4.1 us
    ppermute x3, waiting for transfers between devices, scatter_cand(): lax.ppermute(piece, 'cand', [(j, (j + k) % count) for j in range(count)])  3.57 us
  transfers between devices with their start and end apart: 19, of which 7 were waited for; matrix products, arithmetic and copies ran while one was open for 30% of the time, Pallas kernels for 0%

profile of v6, /device:TPU:0, one launch (start us, length us, event | category | flops | bytes accessed | tf_op | source)
XLA Modules:
  0.0 144.0 jit_solution(18103175890588558430)
XLA Ops:
  9.4 5.1 %collective-permute-start.2 = (f32[1,1,1025]{2,1,0:T(1,128)S(1)}, f32[1,1,1025]{2,1,0:T(1,128)S(1)}, u32[]{:S(2)}, u32[]{:S(2)}) collective-permute-start(f32[1,1,1025]{2,1,0:T(1,128)S(1)} %pad_maximum_fusion.4), channel_id=1, source_target_pairs={{0,12},{4,0},{8,4},{12,8},{1,13},{5,1},{9,5},{13,9},{2,14},{6,2},{... | collective-permute-start | bytes 12308 | tf_op jit(solution)/shard_map/ppermute | solution.py:60
  15.6 1.5 %collective-permute-start.13 = (bf16[256,1024]{1,0:T(8,128)(2,1)}, bf16[256,1024]{1,0:T(8,128)(2,1)}, u32[]{:S(2)}, u32[]{:S(2)}) collective-permute-start(bf16[256,1024]{1,0:T(8,128)(2,1)} %bitcast.349), channel_id=1, source_target_pairs={{0,2},{2,0},{1,3},{3,1},{4,6},{6,4},{5,7},{7,5},{8,10},{10,8},{9,1... | collective-permute-start | bytes 1572872 | tf_op jit(solution)/shard_map/ppermute | solution.py:136
  21.0 1.5 %fusion.8 = bf16[2,1,4,256]{3,2,0,1:T(4,128)(2,1)S(1)} fusion(bf16[3,1024,256]{2,1,0:T(8,128)(2,1)} %param.13, f32[1,4,1025]{2,1,0:T(4,128)S(1)} %bitcast_select_fusion), kind=kOutput, calls=%fused_computation.24 | convolution fusion | flops 4196352 | bytes 1060864 | tf_op jit(solution)/shard_map/qcd,kdf->kqcf/dot_general | solution.py:15
  26.4 2.0 %all_gather.18 = bf16[1,1,256,512]{2,3,1,0:T(8,128)(2,1)S(1)} all-gather(bf16[1,1,256,256]{2,3,1,0:T(8,128)(2,1)S(1)} %bitcast.372), channel_id=1, replica_groups=mesh['groups'=2,'cand'=4,'query'=2,'mp'=2] {'mp'}, dimensions={3}, use_global_device_ids=true | all-gather | bytes 393216 | tf_op jit(solution)/shard_map/all_gather | solution.py:159
  28.4 1.3 exponential_reduce_fusion
  31.8 1.8 %fusion.125 = (f32[256]{0:T(256)S(1)}, f32[1,1,256,1024]{3,2,1,0:T(8,128)S(1)}) fusion(bf16[512,1024]{1,0:T(8,128)(2,1)} %all-gather.4.cloned.1.call-done, bf16[1,1,256,512]{2,3,1,0:T(8,128)(2,1)S(1)} %all_gather.18, bf16[1,1,256,1024]{3,2,1,0:T(8,128)(2,1)S(1)} %copy-done.1), kind=kOutput, calls=%fused_computation.238 | convolution fusion | flops 269221632 | bytes 2884608 | tf_op jit(solution)/shard_map/qcsf,fd->qcsd/dot_general | solution.py:15
  36.9 2.8 %collective-permute-start.5 = (bf16[1,1,512]{2,1,0:T(2,128)(2,1)}, bf16[1,1,512]{2,1,0:T(2,128)(2,1)}, u32[]{:S(2)}, u32[]{:S(2)}) collective-permute-start(bf16[1,1,512]{2,1,0:T(2,128)(2,1)} %pad_maximum_fusion.5), channel_id=1, source_target_pairs={{0,12},{4,0},{8,4},{12,8},{1,13},{5,1},{9,5},{13,9},{2,14},{6,2},{... | collective-permute-start | bytes 3080 | tf_op jit(solution)/shard_map/ppermute | solution.py:60
  39.8 1.1 collective-permute-start.4
  44.6 2.0 %collective-permute-done.3 = bf16[1,1,512]{2,1,0:T(2,128)(2,1)} collective-permute-done((bf16[1,1,512]{2,1,0:T(2,128)(2,1)}, bf16[1,1,512]{2,1,0:T(2,128)(2,1)}, u32[]{:S(2)}, u32[]{:S(2)}) %collective-permute-start.3) | collective-permute-done | bytes 1056 | tf_op jit(solution)/shard_map/ppermute | solution.py:60
  53.1 1.8 %all_gather.20 = bf16[1,1,512]{2,1,0:T(2,128)(2,1)S(1)} all-gather(bf16[1,1,256]{2,1,0:T(2,128)(2,1)S(1)} %convert_element_type.249), channel_id=1, replica_groups=mesh['groups'=2,'cand'=4,'query'=2,'mp'=2] {'mp'}, dimensions={2}, use_global_device_ids=true | all-gather | bytes 1536 | tf_op jit(solution)/shard_map/all_gather | solution.py:188
  54.9 1.5 %fusion.79 = f32[1,1024]{1,0:T(1,128)S(1)} fusion(bf16[512,1024]{1,0:T(8,128)(2,1)} %all-gather.6.cloned.1.call-done, bf16[1,1,512]{2,1,0:T(2,128)(2,1)S(1)} %all_gather.20), kind=kOutput, calls=%fused_computation.159 | convolution fusion | flops 1048576 | bytes 1053696 | tf_op jit(solution)/shard_map/qcf,fd->qcd/dot_general | solution.py:15
  59.0 1.3 multiply_reduce_fusion.2
  61.0 1.4 collective-permute-start.6
  62.3 2.9 %collective-permute-start.7 = (f32[1]{0:T(128)}, f32[1]{0:T(128)}, u32[]{:S(2)}, u32[]{:S(2)}) collective-permute-start(f32[1]{0:T(128)} %bitcast.72), channel_id=1, source_target_pairs={{0,8},{4,12},{8,0},{12,4},{1,9},{5,13},{9,1},{13,5},{2,10},{6,14},... | collective-permute-start | bytes 20 | tf_op jit(solution)/shard_map/ppermute | solution.py:75
  65.2 3.5 %collective-permute-start.8 = (f32[1]{0:T(128)}, f32[1]{0:T(128)}, u32[]{:S(2)}, u32[]{:S(2)}) collective-permute-start(f32[1]{0:T(128)} %bitcast.72), channel_id=1, source_target_pairs={{0,12},{4,0},{8,4},{12,8},{1,13},{5,1},{9,5},{13,9},{2,14},{6,2},{... | collective-permute-start | bytes 20 | tf_op jit(solution)/shard_map/ppermute | solution.py:75
  70.7 1.4 fusion.108
  74.9 2.8 %collective-permute-start.11 = (f32[1,1,512]{2,1,0:T(1,128)S(1)}, f32[1,1,512]{2,1,0:T(1,128)S(1)}, u32[]{:S(2)}, u32[]{:S(2)}) collective-permute-start(f32[1,1,512]{2,1,0:T(1,128)S(1)} %get-tuple-element.32), channel_id=1, source_target_pairs={{0,12},{4,0},{8,4},{12,8},{1,13},{5,1},{9,5},{13,9},{2,14},{6,2},{... | collective-permute-start | bytes 6152 | tf_op jit(solution)/shard_map/ppermute | solution.py:88
  79.7 2.4 %collective-permute-done.10 = f32[1,1,512]{2,1,0:T(1,128)S(1)} collective-permute-done((f32[1,1,512]{2,1,0:T(1,128)S(1)}, f32[1,1,512]{2,1,0:T(1,128)S(1)}, u32[]{:S(2)}, u32[]{:S(2)}) %collective-permute-start.10) | collective-permute-done | bytes 2080 | tf_op jit(solution)/shard_map/ppermute | solution.py:88
  82.1 1.1 collective-permute-done.9
  83.5 2.5 %all_gather.22 = bf16[1,1,513,512]{2,3,1,0:T(8,128)(2,1)S(1)} all-gather(bf16[1,1,513,256]{2,3,1,0:T(8,128)(2,1)S(1)} %pad_maximum_fusion.1), channel_id=1, replica_groups=mesh['groups'=2,'cand'=4,'query'=2,'mp'=2] {'mp'}, dimensions={3}, use_global_device_ids=true | all-gather | bytes 787968 | tf_op jit(solution)/shard_map/all_gather | solution.py:249
  86.1 1.8 %fusion.10 = f32[256,1024]{1,0:T(8,128)S(1)} fusion(bf16[3,1024,512]{2,1,0:T(8,128)(2,1)} %all-gather.8.cloned.1.call-done, bf16[1,1,513,512]{2,3,1,0:T(8,128)(2,1)S(1)} %all_gather.22), kind=kOutput, calls=%fused_computation.29 | convolution fusion | flops 268435456 | bytes 2359296 | tf_op jit(solution)/shard_map/qcsf,df->qcsd/dot_general | solution.py:15
  87.9 1.6 %fusion.9 = f32[1,1024]{1,0:T(1,128)S(1)} fusion(bf16[512,1]{0,1:T(2,128)(2,1)S(1)} %reshape.1155, bf16[3,1024,512]{2,1,0:T(8,128)(2,1)} %all-gather.8.cloned.1.call-done), kind=kOutput, calls=%fused_computation.26 | convolution fusion | flops 1048576 | bytes 1053696 | tf_op jit(solution)/shard_map/qcf,df->qcd/dot_general | solution.py:15
  89.6 2.2 %fusion.11 = (f32[256]{0:T(256)S(1)}, f32[256,1024]{1,0:T(8,128)S(1)}) fusion(f32[1,1,256,1024]{3,2,1,0:T(8,128)S(1)} %get-tuple-element.45, f32[256]{0:T(256)S(1)} %copy-done.19, f32[256]{0:T(256)S(1)} %copy-done.15, f32[1024]{0:T(1024)S(1)} %copy-done.27, f32[1024]{0:T(1024)S(1)} %get-tuple-element.20, f32[1024]{0:T(1024)S(1)} %bitcast.384, ...), kind=kOutput, calls=%fused_computation.31 | convolution fusion | flops 271056640 | bytes 4472064 | tf_op jit(solution)/shard_map/qcsf,df->qcsd/dot_general | solution.py:15
  91.9 1.6 %convolution_convert_fusion.3 = bf16[256,256]{0,1:T(8,128)(2,1)S(1)} fusion(bf16[256,1024]{1,0:T(8,128)(2,1)} %param.14, f32[1,1,256,1024]{3,2,1,0:T(8,128)S(1)} %get-tuple-element.45, f32[256,1024]{1,0:T(8,128)S(1)} %get-tuple-element.47, f32[256]{0:T(256)S(1)} %broadcast_multiply_fusion.1, f32[256]{0:T(256)S(1)} %broadcast_multiply_fusion.2, ...), kind=kOutput, calls=%fused_computation.22 | convolution fusion | flops 136118272 | bytes 2756608 | tf_op jit(solution)/shard_map/qcsd,fd->qcsf/dot_general | solution.py:15
  99.0 5.9 %collective-permute-done.12 = bf16[103936]{0:T(1024)(128)(2,1)S(1)} collective-permute-done((bf16[103936]{0:T(1024)(128)(2,1)S(1)}, bf16[103936]{0:T(1024)(128)(2,1)S(1)}, u32[]{:S(2)}, u32[]{:S(2)}) %collective-permute-start.12) | collective-permute-done | bytes 207904 | tf_op jit(solution)/shard_map/ppermute | solution.py:326
  105.1 1.5 %fusion.129 = f32[384,1024]{0,1:T(8,128)S(1)} fusion(bf16[256,384]{1,0:T(8,128)(2,1)S(1)} %slice.153, bf16[256,1024]{1,0:T(8,128)(2,1)} %collective-permute-done.13), kind=kOutput, calls=%fused_computation.242 | convolution fusion | flops 201326592 | bytes 2293760 | tf_op jit(solution)/shard_map/rd,rf->df/dot_general | solution.py:15
  106.7 1.3 fusion.1
  108.0 21.1 %reduce-scatter.2.cloned.1.call-done = bf16[256,384]{1,0:T(8,128)(2,1)} async-done(((bf16[1024,384]{1,0:T(8,128)(2,1)}), bf16[256,384]{1,0:T(8,128)(2,1)}) %reduce-scatter.2.cloned.1.call-update) | async-done | bytes 196624 | tf_op jit(solution)/shard_map/reduce_scatter | solution.py:336
  129.1 1.5 %collective-permute-start.14 = (bf16[256,384]{1,0:T(8,128)(2,1)}, bf16[256,384]{1,0:T(8,128)(2,1)S(1)}, u32[]{:S(2)}, u32[]{:S(2)}) collective-permute-start(bf16[256,384]{1,0:T(8,128)(2,1)} %reduce-scatter.2.cloned.1.call-done), channel_id=1, source_target_pairs={{0,2},{2,0},{1,3},{3,1},{4,6},{6,4},{5,7},{7,5},{8,10},{10,8},{9,1... | collective-permute-start | bytes 589832 | tf_op jit(solution)/shard_map/ppermute | solution.py:339
  130.5 4.4 %collective-permute-done.14 = bf16[256,384]{1,0:T(8,128)(2,1)S(1)} collective-permute-done((bf16[256,384]{1,0:T(8,128)(2,1)}, bf16[256,384]{1,0:T(8,128)(2,1)S(1)}, u32[]{:S(2)}, u32[]{:S(2)}) %collective-permute-start.14) | collective-permute-done | bytes 196640 | tf_op jit(solution)/shard_map/ppermute | solution.py:339
  135.0 1.1 fusion.33
  136.3 1.1 copy.93
  (253 shorter events, 35.3 us)
Async XLA Ops:
  6.5 10.7 %copy-start.1 = (bf16[1,1,256,1024]{3,2,1,0:T(8,128)(2,1)S(1)}, bf16[1,1,256,1024]{3,2,1,0:T(8,128)(2,1)}, u32[]{:S(2)}) copy-start(bf16[1,1,256,1024]{3,2,1,0:T(8,128)(2,1)} %param.10) | copy-start | bytes 1572868
  6.5 10.7 %copy-start.5 = (bf16[3,1024,256]{2,1,0:T(8,128)(2,1)S(1)}, bf16[3,1024,256]{2,1,0:T(8,128)(2,1)}, u32[]{:S(2)}) copy-start(bf16[3,1024,256]{2,1,0:T(8,128)(2,1)} %param.13) | copy-start | bytes 4718596
  6.5 25.2 %all-gather.4.cloned.1.call-start = ((), (), s32[]{:S(2)}) async-start(), calls=%async_computation.1 | async-start | bytes 1572864 | tf_op jit(solution)/shard_map/all_gather | solution.py:124
  7.3 47.7 %all-gather.6.cloned.1.call-start = ((), (), s32[]{:S(2)}) async-start(), calls=%async_computation.2 | async-start | bytes 1572864 | tf_op jit(solution)/shard_map/all_gather | solution.py:126
  8.0 78.1 %all-gather.8.cloned.1.call-start = ((), (), s32[]{:S(2)}) async-start(), calls=%async_computation.3 | async-start | bytes 4718592 | tf_op jit(solution)/shard_map/all_gather | solution.py:125
  9.4 10.8 %collective-permute-start.2 = (f32[1,1,1025]{2,1,0:T(1,128)S(1)}, f32[1,1,1025]{2,1,0:T(1,128)S(1)}, u32[]{:S(2)}, u32[]{:S(2)}) collective-permute-start(f32[1,1,1025]{2,1,0:T(1,128)S(1)} %pad_maximum_fusion.4), channel_id=1, source_target_pairs={{0,12},{4,0},{8,4},{12,8},{1,13},{5,1},{9,5},{13,9},{2,14},{6,2},{... | collective-permute-start | bytes 12308 | tf_op jit(solution)/shard_map/ppermute | solution.py:60
  14.6 5.7 %collective-permute-start.1 = (f32[1,1,1025]{2,1,0:T(1,128)S(1)}, f32[1,1,1025]{2,1,0:T(1,128)S(1)}, u32[]{:S(2)}, u32[]{:S(2)}) collective-permute-start(f32[1,1,1025]{2,1,0:T(1,128)S(1)} %pad_maximum_fusion.4), channel_id=1, source_target_pairs={{0,8},{4,12},{8,0},{12,4},{1,9},{5,13},{9,1},{13,5},{2,10},{6,14},... | collective-permute-start | bytes 12308 | tf_op jit(solution)/shard_map/ppermute | solution.py:60
  14.6 5.7 %collective-permute-start = (f32[1,1,1025]{2,1,0:T(1,128)S(1)}, f32[1,1,1025]{2,1,0:T(1,128)S(1)}, u32[]{:S(2)}, u32[]{:S(2)}) collective-permute-start(f32[1,1,1025]{2,1,0:T(1,128)S(1)} %pad_maximum_fusion.4), channel_id=1, source_target_pairs={{0,4},{4,8},{8,12},{12,0},{1,5},{5,9},{9,13},{13,1},{2,6},{6,10},{... | collective-permute-start | bytes 12308 | tf_op jit(solution)/shard_map/ppermute | solution.py:60
  15.6 89.6 %collective-permute-start.13 = (bf16[256,1024]{1,0:T(8,128)(2,1)}, bf16[256,1024]{1,0:T(8,128)(2,1)}, u32[]{:S(2)}, u32[]{:S(2)}) collective-permute-start(bf16[256,1024]{1,0:T(8,128)(2,1)} %bitcast.349), channel_id=1, source_target_pairs={{0,2},{2,0},{1,3},{3,1},{4,6},{6,4},{5,7},{7,5},{8,10},{10,8},{9,1... | collective-permute-start | bytes 1572872 | tf_op jit(solution)/shard_map/ppermute | solution.py:136
  17.1 112.0 %reduce-scatter.2.cloned.1.call-start = ((), (), s32[]{:S(2)}) async-start(), calls=%async_computation.4 | async-start | bytes 983040 | tf_op jit(solution)/shard_map/reduce_scatter | solution.py:336
  17.2 3.7 %copy-start.32 = (pred[4]{0:T(512)(128)(4,1)}, pred[4]{0:T(512)(128)(4,1)S(1)}, u32[]{:S(2)}) copy-start(pred[4]{0:T(512)(128)(4,1)S(1)} %get-tuple-element.50) | copy-start | bytes 16
  17.2 7.0 %copy-start.11 = (pred[4]{0:T(512)(128)(4,1)}, pred[4]{0:T(512)(128)(4,1)S(1)}, u32[]{:S(2)}) copy-start(pred[4]{0:T(512)(128)(4,1)S(1)} %get-tuple-element.51) | copy-start | bytes 16
  17.9 8.1 %copy-start.6 = (bf16[1,1,1,256,256]{3,4,0,2,1:T(8,128)(2,1)}, bf16[1,1,1,256,256]{3,4,0,2,1:T(8,128)(2,1)S(1)}, u32[]{:S(2)}) copy-start(bf16[1,1,1,256,256]{3,4,0,2,1:T(8,128)(2,1)S(1)} %get-tuple-element.23) | copy-start | bytes 393220
  19.7 6.6 %copy-start.16 = (pred[256]{0:T(512)(128)(4,1)}, pred[256]{0:T(512)(128)(4,1)S(1)}, u32[]{:S(2)}) copy-start(pred[256]{0:T(512)(128)(4,1)S(1)} %iota_compare_fusion.1) | copy-start | bytes 772
  35.6 37.8 %copy-start.3 = (bf16[256,1024]{1,0:T(8,128)(2,1)S(1)}, bf16[256,1024]{1,0:T(8,128)(2,1)}, u32[]{:S(2)}) copy-start(bf16[256,1024]{1,0:T(8,128)(2,1)} %param.17) | copy-start | bytes 1572868
  36.3 4.5 %copy-start.20 = (bf16[1,1,256]{2,1,0:T(2,128)(2,1)}, bf16[1,1,256]{2,1,0:T(2,128)(2,1)S(1)}, u32[]{:S(2)}) copy-start(bf16[1,1,256]{2,1,0:T(2,128)(2,1)S(1)} %slice_bitcast_fusion.10) | copy-start | bytes 1540
  36.3 4.6 %copy-start.21 = (bf16[1,1,256]{2,1,0:T(2,128)(2,1)}, bf16[1,1,256]{2,1,0:T(2,128)(2,1)S(1)}, u32[]{:S(2)}) copy-start(bf16[1,1,256]{2,1,0:T(2,128)(2,1)S(1)} %slice_bitcast_fusion.11) | copy-start | bytes 1540
  36.9 6.9 %collective-permute-start.5 = (bf16[1,1,512]{2,1,0:T(2,128)(2,1)}, bf16[1,1,512]{2,1,0:T(2,128)(2,1)}, u32[]{:S(2)}, u32[]{:S(2)}) collective-permute-start(bf16[1,1,512]{2,1,0:T(2,128)(2,1)} %pad_maximum_fusion.5), channel_id=1, source_target_pairs={{0,12},{4,0},{8,4},{12,8},{1,13},{5,1},{9,5},{13,9},{2,14},{6,2},{... | collective-permute-start | bytes 3080 | tf_op jit(solution)/shard_map/ppermute | solution.py:60
  39.8 4.8 %collective-permute-start.4 = (bf16[1,1,512]{2,1,0:T(2,128)(2,1)}, bf16[1,1,512]{2,1,0:T(2,128)(2,1)}, u32[]{:S(2)}, u32[]{:S(2)}) collective-permute-start(bf16[1,1,512]{2,1,0:T(2,128)(2,1)} %pad_maximum_fusion.5), channel_id=1, source_target_pairs={{0,8},{4,12},{8,0},{12,4},{1,9},{5,13},{9,1},{13,5},{2,10},{6,14},... | collective-permute-start | bytes 3080 | tf_op jit(solution)/shard_map/ppermute | solution.py:60
  40.8 5.7 %collective-permute-start.3 = (bf16[1,1,512]{2,1,0:T(2,128)(2,1)}, bf16[1,1,512]{2,1,0:T(2,128)(2,1)}, u32[]{:S(2)}, u32[]{:S(2)}) collective-permute-start(bf16[1,1,512]{2,1,0:T(2,128)(2,1)} %pad_maximum_fusion.5), channel_id=1, source_target_pairs={{0,4},{4,8},{8,12},{12,0},{1,5},{5,9},{9,13},{13,1},{2,6},{6,10},{... | collective-permute-start | bytes 3080 | tf_op jit(solution)/shard_map/ppermute | solution.py:60
  43.8 39.5 %copy-start.17 = (pred[256]{0:T(512)(128)(4,1)S(1)}, pred[256]{0:T(512)(128)(4,1)}, u32[]{:S(2)}) copy-start(pred[256]{0:T(512)(128)(4,1)} %copy-done.16) | copy-start | bytes 772
  61.0 7.8 %collective-permute-start.6 = (f32[1]{0:T(128)}, f32[1]{0:T(128)}, u32[]{:S(2)}, u32[]{:S(2)}) collective-permute-start(f32[1]{0:T(128)} %bitcast.72), channel_id=1, source_target_pairs={{0,4},{4,8},{8,12},{12,0},{1,5},{5,9},{9,13},{13,1},{2,6},{6,10},{... | collective-permute-start | bytes 20 | tf_op jit(solution)/shard_map/ppermute | solution.py:75
  62.3 7.0 %collective-permute-start.7 = (f32[1]{0:T(128)}, f32[1]{0:T(128)}, u32[]{:S(2)}, u32[]{:S(2)}) collective-permute-start(f32[1]{0:T(128)} %bitcast.72), channel_id=1, source_target_pairs={{0,8},{4,12},{8,0},{12,4},{1,9},{5,13},{9,1},{13,5},{2,10},{6,14},... | collective-permute-start | bytes 20 | tf_op jit(solution)/shard_map/ppermute | solution.py:75
  65.2 4.7 %collective-permute-start.8 = (f32[1]{0:T(128)}, f32[1]{0:T(128)}, u32[]{:S(2)}, u32[]{:S(2)}) collective-permute-start(f32[1]{0:T(128)} %bitcast.72), channel_id=1, source_target_pairs={{0,12},{4,0},{8,4},{12,8},{1,13},{5,1},{9,5},{13,9},{2,14},{6,2},{... | collective-permute-start | bytes 20 | tf_op jit(solution)/shard_map/ppermute | solution.py:75
  74.9 4.8 %collective-permute-start.11 = (f32[1,1,512]{2,1,0:T(1,128)S(1)}, f32[1,1,512]{2,1,0:T(1,128)S(1)}, u32[]{:S(2)}, u32[]{:S(2)}) collective-permute-start(f32[1,1,512]{2,1,0:T(1,128)S(1)} %get-tuple-element.32), channel_id=1, source_target_pairs={{0,12},{4,0},{8,4},{12,8},{1,13},{5,1},{9,5},{13,9},{2,14},{6,2},{... | collective-permute-start | bytes 6152 | tf_op jit(solution)/shard_map/ppermute | solution.py:88
  77.7 4.5 %collective-permute-start.10 = (f32[1,1,512]{2,1,0:T(1,128)S(1)}, f32[1,1,512]{2,1,0:T(1,128)S(1)}, u32[]{:S(2)}, u32[]{:S(2)}) collective-permute-start(f32[1,1,512]{2,1,0:T(1,128)S(1)} %get-tuple-element.33), channel_id=1, source_target_pairs={{0,8},{4,12},{8,0},{12,4},{1,9},{5,13},{9,1},{13,5},{2,10},{6,14},... | collective-permute-start | bytes 6152 | tf_op jit(solution)/shard_map/ppermute | solution.py:88
  77.9 5.4 %collective-permute-start.9 = (f32[1,1,512]{2,1,0:T(1,128)S(1)}, f32[1,1,512]{2,1,0:T(1,128)S(1)}, u32[]{:S(2)}, u32[]{:S(2)}) collective-permute-start(f32[1,1,512]{2,1,0:T(1,128)S(1)} %get-tuple-element.31), channel_id=1, source_target_pairs={{0,4},{4,8},{8,12},{12,0},{1,5},{5,9},{9,13},{13,1},{2,6},{6,10},{... | collective-permute-start | bytes 6152 | tf_op jit(solution)/shard_map/ppermute | solution.py:88
  85.9 3.6 %copy-start.4 = (bf16[1,1,513,512]{2,3,1,0:T(8,128)(2,1)}, bf16[1,1,513,512]{2,3,1,0:T(8,128)(2,1)S(1)}, u32[]{:S(2)}) copy-start(bf16[1,1,513,512]{2,3,1,0:T(8,128)(2,1)S(1)} %all_gather.22) | copy-start | bytes 1575940
  86.1 3.5 %copy-start.19 = (f32[256]{0:T(256)S(1)}, f32[256]{0:T(256)}, u32[]{:S(2)}) copy-start(f32[256]{0:T(256)} %copy-done.18) | copy-start | bytes 3076
  86.1 3.5 %copy-start.27 = (f32[1024]{0:T(1024)S(1)}, f32[1024]{0:T(1024)}, u32[]{:S(2)}) copy-start(f32[1024]{0:T(1024)} %param.15) | copy-start | bytes 12292
  97.7 7.3 %collective-permute-start.12 = (bf16[103936]{0:T(1024)(128)(2,1)S(1)}, bf16[103936]{0:T(1024)(128)(2,1)S(1)}, u32[]{:S(2)}, u32[]{:S(2)}) collective-permute-start(bf16[103936]{0:T(1024)(128)(2,1)S(1)} %pad_maximum_fusion.2), channel_id=1, source_target_pairs={{0,2},{2,0},{1,3},{3,1},{4,6},{6,4},{5,7},{7,5},{8,10},{10,8},{9,1... | collective-permute-start | bytes 623624 | tf_op jit(solution)/shard_map/ppermute | solution.py:326
  129.1 5.9 %collective-permute-start.14 = (bf16[256,384]{1,0:T(8,128)(2,1)}, bf16[256,384]{1,0:T(8,128)(2,1)S(1)}, u32[]{:S(2)}, u32[]{:S(2)}) collective-permute-start(bf16[256,384]{1,0:T(8,128)(2,1)} %reduce-scatter.2.cloned.1.call-done), channel_id=1, source_target_pairs={{0,2},{2,0},{1,3},{3,1},{4,6},{6,4},{5,7},{7,5},{8,10},{10,8},{9,1... | collective-permute-start | bytes 589832 | tf_op jit(solution)/shard_map/ppermute | solution.py:339
  (21 other events, 30.2 us)
Sparse Core Ops, SparseCore 0:
  8.9 11.7 all-gather.3
  22.2 10.2 all-gather.5
  34.1 12.8 all-gather.7
  108.1 20.9 reduce-scatter.1

commit v7 on v6

--- a/solution.py
+++ b/solution.py
@@ -76,16 +76,18 @@
     return total
 
 
-def scatter_cand(block, axis):
+def scatter_cand(block, axis, total_type=None):
     count = lax.axis_size("cand")
     if count > 8:
         return lax.psum_scatter(block, "cand", scatter_dimension=axis, tiled=True)
+    total_type = total_type or block.dtype
     me = lax.axis_index("cand")
     width = block.shape[axis] // count
-    total = lax.dynamic_slice_in_dim(block, me * width, width, axis)
+    total = lax.dynamic_slice_in_dim(block, me * width, width, axis).astype(total_type)
     for k in range(1, count):
         piece = lax.dynamic_slice_in_dim(block, ((me + k) % count) * width, width, axis)
-        total = total + lax.ppermute(piece, "cand", [(j, (j + k) % count) for j in range(count)])
+        moved = lax.ppermute(piece, "cand", [(j, (j + k) % count) for j in range(count)])
+        total = total + moved.astype(total_type)
     return total
 
 
@@ -333,9 +335,7 @@
         + mixed("rd,rf->df", other_tokens, other_half[:row_count])
         + mixed("rd,rf->df", other_cls, other_half[row_count:])
     )
-    reduced = lax.psum_scatter(
-        paired.astype(jnp.bfloat16), "cand", scatter_dimension=0, tiled=True
-    )
+    reduced = scatter_cand(paired.astype(jnp.bfloat16), 0, jnp.float32).astype(jnp.bfloat16)
     partner = lax.ppermute(reduced, "query", swap)
     joined = jnp.where(
         side == 0,

time: 145 us -> 139 us (0.959)
  the two profiles are of different devices: /device:TPU:0 before, /device:TPU:8 now
where the time goes in v7:
time: 139 us; the launch traced here: 137 us
  starting transfers between devices  30.4 us (22%)
  waiting for transfers between devices  29.6 us (21%)
  between operations  22 us (16%)
  matrix products  19.1 us (14%)
  other arithmetic  18.3 us (13%)
  local copies, waits for them, and re-layouts  11.3 us (8%)
  blocking collectives  6.23 us (4%)
    dot_general x32, matrix products, mixed(): jnp.einsum(pattern, former, latter, preferred_element_type=jnp.float32)  19.1 us
    ppermute x6, waiting for transfers between devices, scatter_cand(): lax.ppermute(piece, 'cand', [(j, (j + k) % count) for j in range(count)])  14.9 us
    ppermute x6, starting transfers between devices, gather_cand(): lax.ppermute(block, 'cand', [(j, (j + k) % count) for j in range(count)])  9.46 us
    ppermute x6, starting transfers between devices, scatter_cand(): lax.ppermute(piece, 'cand', [(j, (j + k) % count) for j in range(count)])  9.38 us
    ppermute x3, starting transfers between devices, sum_cand(): lax.ppermute(block, 'cand', [(j, (j + k) % count) for j in range(count)])  8.67 us
    ppermute x1, waiting for transfers between devices, local(): partner = lax.ppermute(reduced, 'query', swap)  6.23 us
    ppermute x1, waiting for transfers between devices, local(): lax.ppermute(jnp.concatenate([given_half.reshape(-1), cls_flat.reshape(-1...  6.03 us
    unnamed x73, local copies, waits for them, and re-layouts  3.31 us
  transfers between devices with their start and end apart: 21, of which 6 were waited for; matrix products, arithmetic and copies ran while one was open for 31% of the time, Pallas kernels for 0%

profile of v7, /device:TPU:8, one launch (start us, length us, event | category | flops | bytes accessed | tf_op | source)
XLA Modules:
  0.0 136.9 jit_solution(1775410940563906798)
XLA Ops:
  9.5 3.0 %collective-permute-start.1 = (f32[1,1,1025]{2,1,0:T(1,128)S(1)}, f32[1,1,1025]{2,1,0:T(1,128)S(1)}, u32[]{:S(2)}, u32[]{:S(2)}) collective-permute-start(f32[1,1,1025]{2,1,0:T(1,128)S(1)} %pad_maximum_fusion.4), channel_id=1, source_target_pairs={{0,8},{4,12},{8,0},{12,4},{1,9},{5,13},{9,1},{13,5},{2,10},{6,14},... | collective-permute-start | bytes 12308 | tf_op jit(solution)/shard_map/ppermute | solution.py:60
  12.5 2.5 %collective-permute-start = (f32[1,1,1025]{2,1,0:T(1,128)S(1)}, f32[1,1,1025]{2,1,0:T(1,128)S(1)}, u32[]{:S(2)}, u32[]{:S(2)}) collective-permute-start(f32[1,1,1025]{2,1,0:T(1,128)S(1)} %pad_maximum_fusion.4), channel_id=1, source_target_pairs={{0,4},{4,8},{8,12},{12,0},{1,5},{5,9},{9,13},{13,1},{2,6},{6,10},{... | collective-permute-start | bytes 12308 | tf_op jit(solution)/shard_map/ppermute | solution.py:60
  15.0 1.5 %collective-permute-start.13 = (bf16[256,1024]{1,0:T(8,128)(2,1)}, bf16[256,1024]{1,0:T(8,128)(2,1)}, u32[]{:S(2)}, u32[]{:S(2)}) collective-permute-start(bf16[256,1024]{1,0:T(8,128)(2,1)} %bitcast.349), channel_id=1, source_target_pairs={{0,2},{2,0},{1,3},{3,1},{4,6},{6,4},{5,7},{7,5},{8,10},{10,8},{9,1... | collective-permute-start | bytes 1572872 | tf_op jit(solution)/shard_map/ppermute | solution.py:138
  20.4 1.5 %fusion.8 = bf16[2,1,4,256]{3,2,0,1:T(4,128)(2,1)S(1)} fusion(bf16[3,1024,256]{2,1,0:T(8,128)(2,1)} %param.13, f32[1,4,1025]{2,1,0:T(4,128)S(1)} %bitcast_select_fusion), kind=kOutput, calls=%fused_computation.24 | convolution fusion | flops 4196352 | bytes 1060864 | tf_op jit(solution)/shard_map/qcd,kdf->kqcf/dot_general | solution.py:15
  25.8 2.0 %all_gather.18 = bf16[1,1,256,512]{2,3,1,0:T(8,128)(2,1)S(1)} all-gather(bf16[1,1,256,256]{2,3,1,0:T(8,128)(2,1)S(1)} %bitcast.373), channel_id=1, replica_groups=mesh['groups'=2,'cand'=4,'query'=2,'mp'=2] {'mp'}, dimensions={3}, use_global_device_ids=true | all-gather | bytes 393216 | tf_op jit(solution)/shard_map/all_gather | solution.py:161
  27.8 1.3 exponential_reduce_fusion
  31.2 1.8 %fusion.127 = (f32[256]{0:T(256)S(1)}, f32[1,1,256,1024]{3,2,1,0:T(8,128)S(1)}) fusion(bf16[512,1024]{1,0:T(8,128)(2,1)} %all-gather.4.cloned.1.call-done, bf16[1,1,256,512]{2,3,1,0:T(8,128)(2,1)S(1)} %all_gather.18, bf16[1,1,256,1024]{3,2,1,0:T(8,128)(2,1)S(1)} %copy-done.1), kind=kOutput, calls=%fused_computation.244 | convolution fusion | flops 269221632 | bytes 2884608 | tf_op jit(solution)/shard_map/qcsf,fd->qcsd/dot_general | solution.py:15
  36.3 1.5 %collective-permute-start.4 = (bf16[1,1,512]{2,1,0:T(2,128)(2,1)}, bf16[1,1,512]{2,1,0:T(2,128)(2,1)}, u32[]{:S(2)}, u32[]{:S(2)}) collective-permute-start(bf16[1,1,512]{2,1,0:T(2,128)(2,1)} %pad_maximum_fusion.5), channel_id=1, source_target_pairs={{0,8},{4,12},{8,0},{12,4},{1,9},{5,13},{9,1},{13,5},{2,10},{6,14},... | collective-permute-start | bytes 3080 | tf_op jit(solution)/shard_map/ppermute | solution.py:60
  37.8 2.4 %collective-permute-start.3 = (bf16[1,1,512]{2,1,0:T(2,128)(2,1)}, bf16[1,1,512]{2,1,0:T(2,128)(2,1)}, u32[]{:S(2)}, u32[]{:S(2)}) collective-permute-start(bf16[1,1,512]{2,1,0:T(2,128)(2,1)} %pad_maximum_fusion.5), channel_id=1, source_target_pairs={{0,4},{4,8},{8,12},{12,0},{1,5},{5,9},{9,13},{13,1},{2,6},{6,10},{... | collective-permute-start | bytes 3080 | tf_op jit(solution)/shard_map/ppermute | solution.py:60
  40.3 1.0 copy.74
  49.7 1.8 %all_gather.20 = bf16[1,1,512]{2,1,0:T(2,128)(2,1)S(1)} all-gather(bf16[1,1,256]{2,1,0:T(2,128)(2,1)S(1)} %convert_element_type.264), channel_id=1, replica_groups=mesh['groups'=2,'cand'=4,'query'=2,'mp'=2] {'mp'}, dimensions={2}, use_global_device_ids=true | all-gather | bytes 1536 | tf_op jit(solution)/shard_map/all_gather | solution.py:190
  51.5 1.5 %fusion.82 = f32[1,1024]{1,0:T(1,128)S(1)} fusion(bf16[512,1024]{1,0:T(8,128)(2,1)} %all-gather.6.cloned.1.call-done, bf16[1,1,512]{2,1,0:T(2,128)(2,1)S(1)} %all_gather.20), kind=kOutput, calls=%fused_computation.170 | convolution fusion | flops 1048576 | bytes 1053696 | tf_op jit(solution)/shard_map/qcf,fd->qcd/dot_general | solution.py:15
  55.6 1.3 multiply_reduce_fusion.2
  57.6 2.3 %collective-permute-start.6 = (f32[1]{0:T(128)}, f32[1]{0:T(128)}, u32[]{:S(2)}, u32[]{:S(2)}) collective-permute-start(f32[1]{0:T(128)} %bitcast.72), channel_id=1, source_target_pairs={{0,4},{4,8},{8,12},{12,0},{1,5},{5,9},{9,13},{13,1},{2,6},{6,10},{... | collective-permute-start | bytes 20 | tf_op jit(solution)/shard_map/ppermute | solution.py:75
  59.9 5.1 %collective-permute-start.7 = (f32[1]{0:T(128)}, f32[1]{0:T(128)}, u32[]{:S(2)}, u32[]{:S(2)}) collective-permute-start(f32[1]{0:T(128)} %bitcast.72), channel_id=1, source_target_pairs={{0,8},{4,12},{8,0},{12,4},{1,9},{5,13},{9,1},{13,5},{2,10},{6,14},... | collective-permute-start | bytes 20 | tf_op jit(solution)/shard_map/ppermute | solution.py:75
  64.9 1.3 collective-permute-start.8
  67.5 1.0 collective-permute-done.8
  69.2 1.4 %fusion.110 = (f32[]{:T(128)}, f32[]{:T(128)}, f32[1024]{0:T(1024)S(1)}) fusion(f32[]{:T(128)S(6)} %rsqrt.13, f32[]{:T(128)S(6)} %div.79, f32[1024]{0:T(1024)S(1)} %bitcast.371, bf16[1024]{0:T(1024)(128)(2,1)S(1)} %slice_reduce_fusion.1, f32[1024]{0:T(1024)} %param.18, f32[1024]{0:T(1024)} %param.19, f32[]{:T(128)} %bitcast.76), kind=kLoop, calls=%fused_computation.233 | loop fusion | flops 9214 | bytes 18452 | tf_op jit(solution)/shard_map/reduce_sum | solution.py:29
  73.9 2.0 %collective-permute-start.10 = (f32[1,1,512]{2,1,0:T(1,128)S(1)}, f32[1,1,512]{2,1,0:T(1,128)S(1)}, u32[]{:S(2)}, u32[]{:S(2)}) collective-permute-start(f32[1,1,512]{2,1,0:T(1,128)S(1)} %get-tuple-element.36), channel_id=1, source_target_pairs={{0,8},{4,12},{8,0},{12,4},{1,9},{5,13},{9,1},{13,5},{2,10},{6,14},... | collective-permute-start | bytes 6152 | tf_op jit(solution)/shard_map/ppermute | solution.py:89
  75.9 2.2 %collective-permute-start.9 = (f32[1,1,512]{2,1,0:T(1,128)S(1)}, f32[1,1,512]{2,1,0:T(1,128)S(1)}, u32[]{:S(2)}, u32[]{:S(2)}) collective-permute-start(f32[1,1,512]{2,1,0:T(1,128)S(1)} %get-tuple-element.34), channel_id=1, source_target_pairs={{0,4},{4,8},{8,12},{12,0},{1,5},{5,9},{9,13},{13,1},{2,6},{6,10},{... | collective-permute-start | bytes 6152 | tf_op jit(solution)/shard_map/ppermute | solution.py:89
  79.7 2.5 %all_gather.22 = bf16[1,1,513,512]{2,3,1,0:T(8,128)(2,1)S(1)} all-gather(bf16[1,1,513,256]{2,3,1,0:T(8,128)(2,1)S(1)} %pad_maximum_fusion.1), channel_id=1, replica_groups=mesh['groups'=2,'cand'=4,'query'=2,'mp'=2] {'mp'}, dimensions={3}, use_global_device_ids=true | all-gather | bytes 787968 | tf_op jit(solution)/shard_map/all_gather | solution.py:251
  82.3 1.8 %fusion.10 = f32[256,1024]{1,0:T(8,128)S(1)} fusion(bf16[3,1024,512]{2,1,0:T(8,128)(2,1)} %all-gather.8.cloned.1.call-done, bf16[1,1,513,512]{2,3,1,0:T(8,128)(2,1)S(1)} %all_gather.22), kind=kOutput, calls=%fused_computation.29 | convolution fusion | flops 268435456 | bytes 2359296 | tf_op jit(solution)/shard_map/qcsf,df->qcsd/dot_general | solution.py:15
  84.1 1.6 %fusion.9 = f32[1,1024]{1,0:T(1,128)S(1)} fusion(bf16[512,1]{0,1:T(2,128)(2,1)S(1)} %reshape.1155, bf16[3,1024,512]{2,1,0:T(8,128)(2,1)} %all-gather.8.cloned.1.call-done), kind=kOutput, calls=%fused_computation.26 | convolution fusion | flops 1048576 | bytes 1053696 | tf_op jit(solution)/shard_map/qcf,df->qcd/dot_general | solution.py:15
  85.8 2.2 %fusion.11 = (f32[256]{0:T(256)S(1)}, f32[256,1024]{1,0:T(8,128)S(1)}) fusion(f32[1,1,256,1024]{3,2,1,0:T(8,128)S(1)} %get-tuple-element.48, f32[256]{0:T(256)S(1)} %copy-done.19, f32[256]{0:T(256)S(1)} %copy-done.15, f32[1024]{0:T(1024)S(1)} %copy-done.27, f32[1024]{0:T(1024)S(1)} %get-tuple-element.20, f32[1024]{0:T(1024)S(1)} %bitcast.385, ...), kind=kOutput, calls=%fused_computation.31 | convolution fusion | flops 271056640 | bytes 4472064 | tf_op jit(solution)/shard_map/qcsf,df->qcsd/dot_general | solution.py:15
  88.1 1.6 %convolution_convert_fusion.3 = bf16[256,256]{0,1:T(8,128)(2,1)S(1)} fusion(bf16[256,1024]{1,0:T(8,128)(2,1)} %param.14, f32[1,1,256,1024]{3,2,1,0:T(8,128)S(1)} %get-tuple-element.48, f32[256,1024]{1,0:T(8,128)S(1)} %get-tuple-element.50, f32[256]{0:T(256)S(1)} %broadcast_multiply_fusion.1, f32[256]{0:T(256)S(1)} %broadcast_multiply_fusion.2, ...), kind=kOutput, calls=%fused_computation.22 | convolution fusion | flops 136118272 | bytes 2756608 | tf_op jit(solution)/shard_map/qcsd,fd->qcsf/dot_general | solution.py:15
  95.1 6.0 %collective-permute-done.12 = bf16[103936]{0:T(1024)(128)(2,1)S(1)} collective-permute-done((bf16[103936]{0:T(1024)(128)(2,1)S(1)}, bf16[103936]{0:T(1024)(128)(2,1)S(1)}, u32[]{:S(2)}, u32[]{:S(2)}) %collective-permute-start.12) | collective-permute-done | bytes 207904 | tf_op jit(solution)/shard_map/ppermute | solution.py:328
  101.3 1.4 %fusion.131 = f32[384,1024]{1,0:T(8,128)S(1)} fusion(bf16[256,384]{1,0:T(8,128)(2,1)S(1)} %slice.153, bf16[256,1024]{1,0:T(8,128)(2,1)} %collective-permute-done.13), kind=kOutput, calls=%fused_computation.248 | convolution fusion | flops 201326592 | bytes 2293760 | tf_op jit(solution)/shard_map/rd,rf->df/dot_general | solution.py:15
  103.3 2.8 %collective-permute-start.16 = (bf16[256,384]{0,1:T(8,128)(2,1)S(1)}, bf16[256,384]{0,1:T(8,128)(2,1)S(1)}, u32[]{:S(2)}, u32[]{:S(2)}) collective-permute-start(bf16[256,384]{0,1:T(8,128)(2,1)S(1)} %get-tuple-element.23), channel_id=1, source_target_pairs={{0,12},{4,0},{8,4},{12,8},{1,13},{5,1},{9,5},{13,9},{2,14},{6,2},{... | collective-permute-start | bytes 589832 | tf_op jit(solution)/shard_map/ppermute | solution.py:89
  107.9 11.9 %collective-permute-done.16 = bf16[256,384]{0,1:T(8,128)(2,1)S(1)} collective-permute-done((bf16[256,384]{0,1:T(8,128)(2,1)S(1)}, bf16[256,384]{0,1:T(8,128)(2,1)S(1)}, u32[]{:S(2)}, u32[]{:S(2)}) %collective-permute-start.16) | collective-permute-done | bytes 196640 | tf_op jit(solution)/shard_map/ppermute | solution.py:89
  119.7 2.4 %collective-permute-done.14 = bf16[256,384]{0,1:T(8,128)(2,1)S(1)} collective-permute-done((bf16[256,384]{0,1:T(8,128)(2,1)S(1)}, bf16[256,384]{0,1:T(8,128)(2,1)S(1)}, u32[]{:S(2)}, u32[]{:S(2)}) %collective-permute-start.14) | collective-permute-done | bytes 196640 | tf_op jit(solution)/shard_map/ppermute | solution.py:89
  122.9 6.2 %collective-permute-done.17 = bf16[256,384]{0,1:T(8,128)(2,1)S(1)} collective-permute-done((bf16[256,384]{0,1:T(8,128)(2,1)S(1)}, bf16[256,384]{0,1:T(8,128)(2,1)S(1)}, u32[]{:S(2)}, u32[]{:S(2)}) %collective-permute-start.17) | collective-permute-done | bytes 196640 | tf_op jit(solution)/shard_map/ppermute | solution.py:339
  129.3 1.1 copy.84
  (257 shorter events, 35.2 us)
Async XLA Ops:
  6.5 10.1 %copy-start.1 = (bf16[1,1,256,1024]{3,2,1,0:T(8,128)(2,1)S(1)}, bf16[1,1,256,1024]{3,2,1,0:T(8,128)(2,1)}, u32[]{:S(2)}) copy-start(bf16[1,1,256,1024]{3,2,1,0:T(8,128)(2,1)} %param.10) | copy-start | bytes 1572868
  6.5 10.1 %copy-start.5 = (bf16[3,1024,256]{2,1,0:T(8,128)(2,1)S(1)}, bf16[3,1024,256]{2,1,0:T(8,128)(2,1)}, u32[]{:S(2)}) copy-start(bf16[3,1024,256]{2,1,0:T(8,128)(2,1)} %param.13) | copy-start | bytes 4718596
  6.5 24.6 %all-gather.4.cloned.1.call-start = ((), (), s32[]{:S(2)}) async-start(), calls=%async_computation | async-start | bytes 1572864 | tf_op jit(solution)/shard_map/all_gather | solution.py:126
  7.3 44.3 %all-gather.6.cloned.1.call-start = ((), (), s32[]{:S(2)}) async-start(), calls=%async_computation.1 | async-start | bytes 1572864 | tf_op jit(solution)/shard_map/all_gather | solution.py:128
  8.0 74.3 %all-gather.8.cloned.1.call-start = ((), (), s32[]{:S(2)}) async-start(), calls=%async_computation.2 | async-start | bytes 4718592 | tf_op jit(solution)/shard_map/all_gather | solution.py:127
  9.4 10.2 %collective-permute-start.2 = (f32[1,1,1025]{2,1,0:T(1,128)S(1)}, f32[1,1,1025]{2,1,0:T(1,128)S(1)}, u32[]{:S(2)}, u32[]{:S(2)}) collective-permute-start(f32[1,1,1025]{2,1,0:T(1,128)S(1)} %pad_maximum_fusion.4), channel_id=1, source_target_pairs={{0,12},{4,0},{8,4},{12,8},{1,13},{5,1},{9,5},{13,9},{2,14},{6,2},{... | collective-permute-start | bytes 12308 | tf_op jit(solution)/shard_map/ppermute | solution.py:60
  9.5 10.2 %collective-permute-start.1 = (f32[1,1,1025]{2,1,0:T(1,128)S(1)}, f32[1,1,1025]{2,1,0:T(1,128)S(1)}, u32[]{:S(2)}, u32[]{:S(2)}) collective-permute-start(f32[1,1,1025]{2,1,0:T(1,128)S(1)} %pad_maximum_fusion.4), channel_id=1, source_target_pairs={{0,8},{4,12},{8,0},{12,4},{1,9},{5,13},{9,1},{13,5},{2,10},{6,14},... | collective-permute-start | bytes 12308 | tf_op jit(solution)/shard_map/ppermute | solution.py:60
  12.5 7.1 %collective-permute-start = (f32[1,1,1025]{2,1,0:T(1,128)S(1)}, f32[1,1,1025]{2,1,0:T(1,128)S(1)}, u32[]{:S(2)}, u32[]{:S(2)}) collective-permute-start(f32[1,1,1025]{2,1,0:T(1,128)S(1)} %pad_maximum_fusion.4), channel_id=1, source_target_pairs={{0,4},{4,8},{8,12},{12,0},{1,5},{5,9},{9,13},{13,1},{2,6},{6,10},{... | collective-permute-start | bytes 12308 | tf_op jit(solution)/shard_map/ppermute | solution.py:60
  15.0 86.3 %collective-permute-start.13 = (bf16[256,1024]{1,0:T(8,128)(2,1)}, bf16[256,1024]{1,0:T(8,128)(2,1)}, u32[]{:S(2)}, u32[]{:S(2)}) collective-permute-start(bf16[256,1024]{1,0:T(8,128)(2,1)} %bitcast.349), channel_id=1, source_target_pairs={{0,2},{2,0},{1,3},{3,1},{4,6},{6,4},{5,7},{7,5},{8,10},{10,8},{9,1... | collective-permute-start | bytes 1572872 | tf_op jit(solution)/shard_map/ppermute | solution.py:138
  16.6 3.7 %copy-start.32 = (pred[4]{0:T(512)(128)(4,1)}, pred[4]{0:T(512)(128)(4,1)S(1)}, u32[]{:S(2)}) copy-start(pred[4]{0:T(512)(128)(4,1)S(1)} %get-tuple-element.53) | copy-start | bytes 16
  16.6 7.0 %copy-start.11 = (pred[4]{0:T(512)(128)(4,1)}, pred[4]{0:T(512)(128)(4,1)S(1)}, u32[]{:S(2)}) copy-start(pred[4]{0:T(512)(128)(4,1)S(1)} %get-tuple-element.54) | copy-start | bytes 16
  17.3 8.1 %copy-start.6 = (bf16[1,1,1,256,256]{3,4,0,2,1:T(8,128)(2,1)}, bf16[1,1,1,256,256]{3,4,0,2,1:T(8,128)(2,1)S(1)}, u32[]{:S(2)}) copy-start(bf16[1,1,1,256,256]{3,4,0,2,1:T(8,128)(2,1)S(1)} %get-tuple-element.26) | copy-start | bytes 393220
  19.1 6.6 %copy-start.16 = (pred[256]{0:T(512)(128)(4,1)}, pred[256]{0:T(512)(128)(4,1)S(1)}, u32[]{:S(2)}) copy-start(pred[256]{0:T(512)(128)(4,1)S(1)} %iota_compare_fusion.1) | copy-start | bytes 772
  35.0 36.9 %copy-start.3 = (bf16[256,1024]{1,0:T(8,128)(2,1)S(1)}, bf16[256,1024]{1,0:T(8,128)(2,1)}, u32[]{:S(2)}) copy-start(bf16[256,1024]{1,0:T(8,128)(2,1)} %param.17) | copy-start | bytes 1572868
  35.7 4.5 %copy-start.21 = (bf16[1,1,256]{2,1,0:T(2,128)(2,1)}, bf16[1,1,256]{2,1,0:T(2,128)(2,1)S(1)}, u32[]{:S(2)}) copy-start(bf16[1,1,256]{2,1,0:T(2,128)(2,1)S(1)} %slice_bitcast_fusion.11) | copy-start | bytes 1540
  36.3 6.8 %collective-permute-start.5 = (bf16[1,1,512]{2,1,0:T(2,128)(2,1)}, bf16[1,1,512]{2,1,0:T(2,128)(2,1)}, u32[]{:S(2)}, u32[]{:S(2)}) collective-permute-start(bf16[1,1,512]{2,1,0:T(2,128)(2,1)} %pad_maximum_fusion.5), channel_id=1, source_target_pairs={{0,12},{4,0},{8,4},{12,8},{1,13},{5,1},{9,5},{13,9},{2,14},{6,2},{... | collective-permute-start | bytes 3080 | tf_op jit(solution)/shard_map/ppermute | solution.py:60
  36.3 6.8 %collective-permute-start.4 = (bf16[1,1,512]{2,1,0:T(2,128)(2,1)}, bf16[1,1,512]{2,1,0:T(2,128)(2,1)}, u32[]{:S(2)}, u32[]{:S(2)}) collective-permute-start(bf16[1,1,512]{2,1,0:T(2,128)(2,1)} %pad_maximum_fusion.5), channel_id=1, source_target_pairs={{0,8},{4,12},{8,0},{12,4},{1,9},{5,13},{9,1},{13,5},{2,10},{6,14},... | collective-permute-start | bytes 3080 | tf_op jit(solution)/shard_map/ppermute | solution.py:60
  37.8 5.3 %collective-permute-start.3 = (bf16[1,1,512]{2,1,0:T(2,128)(2,1)}, bf16[1,1,512]{2,1,0:T(2,128)(2,1)}, u32[]{:S(2)}, u32[]{:S(2)}) collective-permute-start(bf16[1,1,512]{2,1,0:T(2,128)(2,1)} %pad_maximum_fusion.5), channel_id=1, source_target_pairs={{0,4},{4,8},{8,12},{12,0},{1,5},{5,9},{9,13},{13,1},{2,6},{6,10},{... | collective-permute-start | bytes 3080 | tf_op jit(solution)/shard_map/ppermute | solution.py:60
  43.1 36.4 %copy-start.17 = (pred[256]{0:T(512)(128)(4,1)S(1)}, pred[256]{0:T(512)(128)(4,1)}, u32[]{:S(2)}) copy-start(pred[256]{0:T(512)(128)(4,1)} %copy-done.16) | copy-start | bytes 772
  57.6 8.7 %collective-permute-start.6 = (f32[1]{0:T(128)}, f32[1]{0:T(128)}, u32[]{:S(2)}, u32[]{:S(2)}) collective-permute-start(f32[1]{0:T(128)} %bitcast.72), channel_id=1, source_target_pairs={{0,4},{4,8},{8,12},{12,0},{1,5},{5,9},{9,13},{13,1},{2,6},{6,10},{... | collective-permute-start | bytes 20 | tf_op jit(solution)/shard_map/ppermute | solution.py:75
  59.9 7.0 %collective-permute-start.7 = (f32[1]{0:T(128)}, f32[1]{0:T(128)}, u32[]{:S(2)}, u32[]{:S(2)}) collective-permute-start(f32[1]{0:T(128)} %bitcast.72), channel_id=1, source_target_pairs={{0,8},{4,12},{8,0},{12,4},{1,9},{5,13},{9,1},{13,5},{2,10},{6,14},... | collective-permute-start | bytes 20 | tf_op jit(solution)/shard_map/ppermute | solution.py:75
  64.9 3.5 %collective-permute-start.8 = (f32[1]{0:T(128)}, f32[1]{0:T(128)}, u32[]{:S(2)}, u32[]{:S(2)}) collective-permute-start(f32[1]{0:T(128)} %bitcast.72), channel_id=1, source_target_pairs={{0,12},{4,0},{8,4},{12,8},{1,13},{5,1},{9,5},{13,9},{2,14},{6,2},{... | collective-permute-start | bytes 20 | tf_op jit(solution)/shard_map/ppermute | solution.py:75
  73.3 5.5 %collective-permute-start.11 = (f32[1,1,512]{2,1,0:T(1,128)S(1)}, f32[1,1,512]{2,1,0:T(1,128)S(1)}, u32[]{:S(2)}, u32[]{:S(2)}) collective-permute-start(f32[1,1,512]{2,1,0:T(1,128)S(1)} %get-tuple-element.35), channel_id=1, source_target_pairs={{0,12},{4,0},{8,4},{12,8},{1,13},{5,1},{9,5},{13,9},{2,14},{6,2},{... | collective-permute-start | bytes 6152 | tf_op jit(solution)/shard_map/ppermute | solution.py:89
  73.9 5.0 %collective-permute-start.10 = (f32[1,1,512]{2,1,0:T(1,128)S(1)}, f32[1,1,512]{2,1,0:T(1,128)S(1)}, u32[]{:S(2)}, u32[]{:S(2)}) collective-permute-start(f32[1,1,512]{2,1,0:T(1,128)S(1)} %get-tuple-element.36), channel_id=1, source_target_pairs={{0,8},{4,12},{8,0},{12,4},{1,9},{5,13},{9,1},{13,5},{2,10},{6,14},... | collective-permute-start | bytes 6152 | tf_op jit(solution)/shard_map/ppermute | solution.py:89
  75.9 3.6 %collective-permute-start.9 = (f32[1,1,512]{2,1,0:T(1,128)S(1)}, f32[1,1,512]{2,1,0:T(1,128)S(1)}, u32[]{:S(2)}, u32[]{:S(2)}) collective-permute-start(f32[1,1,512]{2,1,0:T(1,128)S(1)} %get-tuple-element.34), channel_id=1, source_target_pairs={{0,4},{4,8},{8,12},{12,0},{1,5},{5,9},{9,13},{13,1},{2,6},{6,10},{... | collective-permute-start | bytes 6152 | tf_op jit(solution)/shard_map/ppermute | solution.py:89
  82.1 3.6 %copy-start.4 = (bf16[1,1,513,512]{2,3,1,0:T(8,128)(2,1)}, bf16[1,1,513,512]{2,3,1,0:T(8,128)(2,1)S(1)}, u32[]{:S(2)}) copy-start(bf16[1,1,513,512]{2,3,1,0:T(8,128)(2,1)S(1)} %all_gather.22) | copy-start | bytes 1575940
  82.3 3.5 %copy-start.19 = (f32[256]{0:T(256)S(1)}, f32[256]{0:T(256)}, u32[]{:S(2)}) copy-start(f32[256]{0:T(256)} %copy-done.18) | copy-start | bytes 3076
  93.9 7.3 %collective-permute-start.12 = (bf16[103936]{0:T(1024)(128)(2,1)S(1)}, bf16[103936]{0:T(1024)(128)(2,1)S(1)}, u32[]{:S(2)}, u32[]{:S(2)}) collective-permute-start(bf16[103936]{0:T(1024)(128)(2,1)S(1)} %pad_maximum_fusion.2), channel_id=1, source_target_pairs={{0,2},{2,0},{1,3},{3,1},{4,6},{6,4},{5,7},{7,5},{8,10},{10,8},{9,1... | collective-permute-start | bytes 623624 | tf_op jit(solution)/shard_map/ppermute | solution.py:328
  103.3 16.5 %collective-permute-start.16 = (bf16[256,384]{0,1:T(8,128)(2,1)S(1)}, bf16[256,384]{0,1:T(8,128)(2,1)S(1)}, u32[]{:S(2)}, u32[]{:S(2)}) collective-permute-start(bf16[256,384]{0,1:T(8,128)(2,1)S(1)} %get-tuple-element.23), channel_id=1, source_target_pairs={{0,12},{4,0},{8,4},{12,8},{1,13},{5,1},{9,5},{13,9},{2,14},{6,2},{... | collective-permute-start | bytes 589832 | tf_op jit(solution)/shard_map/ppermute | solution.py:89
  106.1 13.7 %collective-permute-start.15 = (bf16[256,384]{0,1:T(8,128)(2,1)S(1)}, bf16[256,384]{0,1:T(8,128)(2,1)S(1)}, u32[]{:S(2)}, u32[]{:S(2)}) collective-permute-start(bf16[256,384]{0,1:T(8,128)(2,1)S(1)} %get-tuple-element.24), channel_id=1, source_target_pairs={{0,8},{4,12},{8,0},{12,4},{1,9},{5,13},{9,1},{13,5},{2,10},{6,14},... | collective-permute-start | bytes 589832 | tf_op jit(solution)/shard_map/ppermute | solution.py:89
  107.0 15.2 %collective-permute-start.14 = (bf16[256,384]{0,1:T(8,128)(2,1)S(1)}, bf16[256,384]{0,1:T(8,128)(2,1)S(1)}, u32[]{:S(2)}, u32[]{:S(2)}) collective-permute-start(bf16[256,384]{0,1:T(8,128)(2,1)S(1)} %get-tuple-element.22), channel_id=1, source_target_pairs={{0,4},{4,8},{8,12},{12,0},{1,5},{5,9},{9,13},{13,1},{2,6},{6,10},{... | collective-permute-start | bytes 589832 | tf_op jit(solution)/shard_map/ppermute | solution.py:89
  122.2 6.9 %collective-permute-start.17 = (bf16[256,384]{0,1:T(8,128)(2,1)S(1)}, bf16[256,384]{0,1:T(8,128)(2,1)S(1)}, u32[]{:S(2)}, u32[]{:S(2)}) collective-permute-start(bf16[256,384]{0,1:T(8,128)(2,1)S(1)} %add_convert_fusion), channel_id=1, source_target_pairs={{0,2},{2,0},{1,3},{3,1},{4,6},{6,4},{5,7},{7,5},{8,10},{10,8},{9,1... | collective-permute-start | bytes 589832 | tf_op jit(solution)/shard_map/ppermute | solution.py:339
  (23 other events, 35.8 us)
Sparse Core Ops, SparseCore 0:
  8.9 10.4 all-gather.3
  20.9 10.2 all-gather.5
  32.7 12.8 all-gather.7

commit v8 on v7

--- a/solution.py
+++ b/solution.py
@@ -89,6 +89,17 @@
         moved = lax.ppermute(piece, "cand", [(j, (j + k) % count) for j in range(count)])
         total = total + moved.astype(total_type)
     return total
+
+
+def gather_mp(block, axis):
+    if lax.axis_size("mp") != 2:
+        return lax.all_gather(block, "mp", axis=axis, tiled=True)
+    other = lax.ppermute(block, "mp", [(0, 1), (1, 0)])
+    return jnp.where(
+        lax.axis_index("mp") == 0,
+        jnp.concatenate([block, other], axis),
+        jnp.concatenate([other, block], axis),
+    )
 
 
 def sum_query(block):
@@ -123,9 +134,9 @@
     cross_valid = local_ids[:, None] != jnp.arange(cand_count)[None, :]
     head_shape = (lists, local_cands, seq_len, local_heads, HEAD_DIM)
     cls_shape = (lists, cand_count, local_heads, HEAD_DIM)
-    out_first_full = lax.all_gather(w_out_first, "mp", axis=0, tiled=True)
-    last_full = lax.all_gather(w_last, "mp", axis=2, tiled=True)
-    out_last_full = lax.all_gather(w_out_last, "mp", axis=0, tiled=True)
+    out_first_full = gather_mp(w_out_first, 0)
+    last_full = gather_mp(w_last, 2)
+    out_last_full = gather_mp(w_out_last, 0)
     cls_and_teacher = gather_cand(
         jnp.concatenate([tokens[:, :, 0].astype(jnp.float32), teacher[..., None]], -1), 1
     )

time: 139 us -> 116 us (0.83); the launches traced: 137 us -> 116 us
  between operations: 22 us -> 8.5 us
  other arithmetic: 18.3 us -> 13.9 us
  local copies, waits for them, and re-layouts: 11.3 us -> 7.62 us
  starting transfers between devices: 30.4 us -> 28.4 us
  matrix products: 19.1 us -> 20.8 us
    select_n x0 -> x1, other arithmetic: none -> 3.41 us  [gather_mp(): jnp.where(lax.axis_index('mp') == 0, jnp.concatenate([block, other], axis...]
    ppermute x6, waiting for transfers between devices: 14.9 us -> 17.9 us  [scatter_cand(): lax.ppermute(piece, 'cand', [(j, (j + k) % count) for j in range(count)])]
    unnamed x73 -> x45, local copies, waits for them, and re-layouts: 3.31 us -> 1.27 us
    dot_general x32, matrix products: 19.1 us -> 20.8 us  [mixed(): jnp.einsum(pattern, former, latter, preferred_element_type=jnp.float32)]
    unnamed x3 -> x0, waiting for transfers between devices: 1.42 us -> none
  transfers between devices with their start and end apart: 21 -> 21, of which waited for: 6 -> 8; matrix products, arithmetic and copies ran while one was open for 31% -> 33% of each run, Pallas kernels for 0% -> 0%
where the time goes in v8:
time: 116 us
  waiting for transfers between devices  30 us (26%)
  starting transfers between devices  28.4 us (24%)
  matrix products  20.8 us (18%)
  other arithmetic  13.9 us (12%)
  between operations  8.5 us (7%)
  local copies, waits for them, and re-layouts  7.62 us (7%)
  blocking collectives  6.37 us (5%)
    dot_general x32, matrix products, mixed(): jnp.einsum(pattern, former, latter, preferred_element_type=jnp.float32)  20.8 us
    ppermute x6, waiting for transfers between devices, scatter_cand(): lax.ppermute(piece, 'cand', [(j, (j + k) % count) for j in range(count)])  17.9 us
    ppermute x6, starting transfers between devices, scatter_cand(): lax.ppermute(piece, 'cand', [(j, (j + k) % count) for j in range(count)])  8.88 us
    ppermute x6, starting transfers between devices, gather_cand(): lax.ppermute(block, 'cand', [(j, (j + k) % count) for j in range(count)])  8.45 us
    ppermute x3, starting transfers between devices, sum_cand(): lax.ppermute(block, 'cand', [(j, (j + k) % count) for j in range(count)])  7.77 us
    ppermute x1, waiting for transfers between devices, local(): partner = lax.ppermute(reduced, 'query', swap)  5.94 us
    ppermute x1, waiting for transfers between devices, local(): lax.ppermute(jnp.concatenate([given_half.reshape(-1), cls_flat.reshape(-1...  5.04 us
    select_n x1, other arithmetic, gather_mp(): jnp.where(lax.axis_index('mp') == 0, jnp.concatenate([block, other], axis...  3.41 us
  transfers between devices with their start and end apart: 21, of which 8 were waited for; matrix products, arithmetic and copies ran while one was open for 33% of the time, Pallas kernels for 0%

profile of v8, /device:TPU:8, one launch (start us, length us, event | category | flops | bytes accessed | tf_op | source)
XLA Modules:
  0.0 115.7 jit_solution(6697066333852225620)
XLA Ops:
  1.4 1.6 %collective-permute-start = (f32[1,1,1025]{2,1,0:T(1,128)S(1)}, f32[1,1,1025]{2,1,0:T(1,128)S(1)}, u32[]{:S(2)}, u32[]{:S(2)}) collective-permute-start(f32[1,1,1025]{2,1,0:T(1,128)S(1)} %pad_maximum_fusion.4), channel_id=1, source_target_pairs={{0,4},{4,8},{8,12},{12,0},{1,5},{5,9},{9,13},{13,1},{2,6},{6,10},{... | collective-permute-start | bytes 12308 | tf_op jit(solution)/shard_map/ppermute | solution.py:60
  3.0 1.1 collective-permute-start.1
  4.1 1.9 %collective-permute-start.2 = (f32[1,1,1025]{2,1,0:T(1,128)S(1)}, f32[1,1,1025]{2,1,0:T(1,128)S(1)}, u32[]{:S(2)}, u32[]{:S(2)}) collective-permute-start(f32[1,1,1025]{2,1,0:T(1,128)S(1)} %pad_maximum_fusion.4), channel_id=1, source_target_pairs={{0,12},{4,0},{8,4},{12,8},{1,13},{5,1},{9,5},{13,9},{2,14},{6,2},{... | collective-permute-start | bytes 12308 | tf_op jit(solution)/shard_map/ppermute | solution.py:60
  6.6 2.2 %fusion.5 = bf16[3,1,1,256,256]{3,4,0,2,1:T(8,128)(2,1)S(1)} fusion(bf16[3,1024,256]{2,1,0:T(8,128)(2,1)} %param.13, bf16[1,1,256,1024]{3,2,1,0:T(8,128)(2,1)} %param.10), kind=kOutput, calls=%fused_computation.15 | convolution fusion | flops 402849792 | bytes 2490368 | tf_op jit(solution)/shard_map/qcsd,kdf->kqcsf/dot_general | solution.py:15
  15.1 1.3 %exponential_reduce_fusion = f32[]{:T(128)} fusion(f32[1,4,1025]{2,1,0:T(4,128)S(1)} %bitcast_select_fusion, f32[]{:T(128)} %slice_reduce_fusion.2), kind=kLoop, calls=%fused_computation.203 | loop fusion | flops 7 | bytes 24 | tf_op jit(solution)/shard_map/reduce_sum | solution.py:210
  18.9 2.1 %all_gather.9 = bf16[1,1,256,512]{2,3,1,0:T(8,128)(2,1)S(1)} all-gather(bf16[1,1,256,256]{2,3,1,0:T(8,128)(2,1)S(1)} %bitcast.364), channel_id=1, replica_groups=mesh['groups'=2,'cand'=4,'query'=2,'mp'=2] {'mp'}, dimensions={3}, use_global_device_ids=true | all-gather | bytes 393216 | tf_op jit(solution)/shard_map/all_gather | solution.py:172
  21.0 1.9 %fusion.141 = (f32[256]{0:T(256)S(1)}, f32[1,1,256,1024]{3,2,1,0:T(8,128)S(1)}) fusion(bf16[256,1024]{1,0:T(8,128)(2,1)} %collective-permute-done.3, bf16[256,1024]{1,0:T(8,128)(2,1)S(1)} %copy-done.2, pred[]{:T(512)S(6)} %eq.51, bf16[1,1,256,512]{2,3,1,0:T(8,128)(2,1)S(1)} %all_gather.9, bf16[1,1,256,1024]{3,2,1,0:T(8,128)(2,1)} %param.10), kind=kOutput, calls=%fused_computation.261 | convolution fusion | flops 273940224 | bytes 2884609 | tf_op jit(solution)/shard_map/qcsf,fd->qcsd/dot_general | solution.py:15
  23.5 1.7 %fusion.6 = bf16[2,1,1,256,256]{4,3,0,2,1:T(8,128)(2,1)S(1)} fusion(bf16[3,1024,256]{2,1,0:T(8,128)(2,1)} %param.16, bf16[1,1,256,1024]{3,2,1,0:T(8,128)(2,1)S(1)} %multiply_convert_fusion.1), kind=kOutput, calls=%fused_computation.20 | convolution fusion | flops 268566528 | bytes 1835008 | tf_op jit(solution)/shard_map/qcsd,kdf->kqcsf/dot_general | solution.py:15
  25.4 3.6 %collective-permute-start.5 = (bf16[1,1,512]{2,1,0:T(2,128)(2,1)S(1)}, bf16[1,1,512]{2,1,0:T(2,128)(2,1)S(1)}, u32[]{:S(2)}, u32[]{:S(2)}) collective-permute-start(bf16[1,1,512]{2,1,0:T(2,128)(2,1)S(1)} %pad_maximum_fusion.5), channel_id=1, source_target_pairs={{0,8},{4,12},{8,0},{12,4},{1,9},{5,13},{9,1},{13,5},{2,10},{6,14},... | collective-permute-start | bytes 3080 | tf_op jit(solution)/shard_map/ppermute | solution.py:60
  29.1 1.2 %fusion.39 = f32[1,256]{1,0:T(1,128)S(1)} fusion(bf16[3,1024,256]{2,1,0:T(8,128)(2,1)} %param.16, bf16[1,1,256,1024]{3,2,1,0:T(8,128)(2,1)S(1)} %multiply_convert_fusion.1), kind=kOutput, calls=%fused_computation.72 | convolution fusion | flops 524288 | bytes 529408 | tf_op jit(solution)/shard_map/qcd,df->qcf/dot_general | solution.py:15
  31.0 1.6 %collective-permute-start.16 = (bf16[256,1024]{1,0:T(8,128)(2,1)}, bf16[256,1024]{1,0:T(8,128)(2,1)}, u32[]{:S(2)}, u32[]{:S(2)}) collective-permute-start(bf16[256,1024]{1,0:T(8,128)(2,1)} %bitcast), channel_id=1, source_target_pairs={{0,2},{2,0},{1,3},{3,1},{4,6},{6,4},{5,7},{7,5},{8,10},{10,8},{9,1... | collective-permute-start | bytes 1572872 | tf_op jit(solution)/shard_map/ppermute | solution.py:149
  34.8 1.8 %all_gather.10 = bf16[1,1,512]{2,1,0:T(2,128)(2,1)S(1)} all-gather(bf16[1,1,256]{2,1,0:T(2,128)(2,1)S(1)} %convert_element_type.264), channel_id=1, replica_groups=mesh['groups'=2,'cand'=4,'query'=2,'mp'=2] {'mp'}, dimensions={2}, use_global_device_ids=true | all-gather | bytes 1536 | tf_op jit(solution)/shard_map/all_gather | solution.py:201
  36.5 1.6 %fusion.16 = f32[1,1024]{1,0:T(1,128)S(1)} fusion(bf16[256,1024]{1,0:T(8,128)(2,1)} %collective-permute-done.7, bf16[256,1024]{1,0:T(8,128)(2,1)S(1)} %copy-done.1, pred[]{:T(512)S(6)} %eq.51, bf16[1,1,512]{2,1,0:T(2,128)(2,1)S(1)} %all_gather.10), kind=kOutput, calls=%fused_computation.38 | convolution fusion | flops 5767168 | bytes 1053697 | tf_op jit(solution)/shard_map/qcf,fd->qcd/dot_general | solution.py:15
  41.8 3.3 %collective-permute-start.8 = (f32[1]{0:T(128)}, f32[1]{0:T(128)}, u32[]{:S(2)}, u32[]{:S(2)}) collective-permute-start(f32[1]{0:T(128)} %bitcast.72), channel_id=1, source_target_pairs={{0,4},{4,8},{8,12},{12,0},{1,5},{5,9},{9,13},{13,1},{2,6},{6,10},{... | collective-permute-start | bytes 20 | tf_op jit(solution)/shard_map/ppermute | solution.py:75
  45.1 3.1 %collective-permute-start.9 = (f32[1]{0:T(128)}, f32[1]{0:T(128)}, u32[]{:S(2)}, u32[]{:S(2)}) collective-permute-start(f32[1]{0:T(128)} %bitcast.72), channel_id=1, source_target_pairs={{0,8},{4,12},{8,0},{12,4},{1,9},{5,13},{9,1},{13,5},{2,10},{6,14},... | collective-permute-start | bytes 20 | tf_op jit(solution)/shard_map/ppermute | solution.py:75
  48.2 1.4 %collective-permute-start.10 = (f32[1]{0:T(128)}, f32[1]{0:T(128)}, u32[]{:S(2)}, u32[]{:S(2)}) collective-permute-start(f32[1]{0:T(128)} %bitcast.72), channel_id=1, source_target_pairs={{0,12},{4,0},{8,4},{12,8},{1,13},{5,1},{9,5},{13,9},{2,14},{6,2},{... | collective-permute-start | bytes 20 | tf_op jit(solution)/shard_map/ppermute | solution.py:75
  56.8 2.9 %collective-permute-start.12 = (f32[1,1,512]{2,1,0:T(1,128)S(1)}, f32[1,1,512]{2,1,0:T(1,128)S(1)}, u32[]{:S(2)}, u32[]{:S(2)}) collective-permute-start(f32[1,1,512]{2,1,0:T(1,128)S(1)} %get-tuple-element.36), channel_id=1, source_target_pairs={{0,8},{4,12},{8,0},{12,4},{1,9},{5,13},{9,1},{13,5},{2,10},{6,14},... | collective-permute-start | bytes 6152 | tf_op jit(solution)/shard_map/ppermute | solution.py:89
  59.7 1.1 collective-permute-start.13
  61.5 1.8 %collective-permute-done.13 = f32[1,1,512]{2,1,0:T(1,128)S(1)} collective-permute-done((f32[1,1,512]{2,1,0:T(1,128)S(1)}, f32[1,1,512]{2,1,0:T(1,128)S(1)}, u32[]{:S(2)}, u32[]{:S(2)}) %collective-permute-start.13) | collective-permute-done | bytes 2080 | tf_op jit(solution)/shard_map/ppermute | solution.py:89
  63.5 2.5 %all_gather.11 = bf16[1,1,513,512]{2,3,1,0:T(8,128)(2,1)S(1)} all-gather(bf16[1,1,513,256]{2,3,1,0:T(8,128)(2,1)S(1)} %pad_maximum_fusion.1), channel_id=1, replica_groups=mesh['groups'=2,'cand'=4,'query'=2,'mp'=2] {'mp'}, dimensions={3}, use_global_device_ids=true | all-gather | bytes 787968 | tf_op jit(solution)/shard_map/all_gather | solution.py:262
  66.1 3.4 %maximum_select_fusion = bf16[3,1024,512]{2,1,0:T(8,128)(2,1)S(1)} fusion(bf16[3,1024,256]{2,1,0:T(8,128)(2,1)} %collective-permute-done.14, bf16[3,1024,256]{2,1,0:T(8,128)(2,1)} %param.16, pred[]{:T(512)S(6)} %eq.51), kind=kLoop, calls=%fused_computation.2 | loop fusion | flops 14155776 | bytes 6291457 | tf_op jit(solution)/shard_map/jit(_where)/select_n | solution.py:98
  71.5 1.6 %convolution_convert_fusion.3 = bf16[256,256]{0,1:T(8,128)(2,1)S(1)} fusion(bf16[256,1024]{1,0:T(8,128)(2,1)} %param.14, f32[1,1,256,1024]{3,2,1,0:T(8,128)S(1)} %get-tuple-element.48, f32[256,1024]{1,0:T(8,128)S(1)} %get-tuple-element.50, f32[256]{0:T(256)S(1)} %broadcast_multiply_fusion.1, f32[256]{0:T(256)S(1)} %broadcast_multiply_fusion.2, ...), kind=kOutput, calls=%fused_computation.23 | convolution fusion | flops 136118272 | bytes 2756608 | tf_op jit(solution)/shard_map/qcsd,fd->qcsf/dot_general | solution.py:15
  74.2 1.3 %multiply_reduce_fusion = (f32[4,256]{1,0:T(4,128)S(1)}, f32[4,256,256]{1,2,0:T(8,128)S(1)}) fusion(f32[4,256]{1,0:T(4,128)} %copy-done.5, f32[4,256,256]{1,2,0:T(8,128)S(1)} %get-tuple-element.46, f32[4,256]{1,0:T(4,128)S(1)} %broadcast_select_fusion.2, bf16[256,4,64]{0,2,1:T(8,128)(2,1)S(1)} %bitcast.362, bf16[256,4,64]{0,2,1:T(8,128)(2,1)} %bitcast.366), kind=kOutput, calls=%fused_computation.50 | convolution fusion | flops 34601984 | bytes 2371584 | tf_op jit(solution)/shard_map/qcshe,qcthe->qchst/dot_general | solution.py:15
  79.0 1.6 %fusion.31 = f32[1024,384]{0,1:T(8,128)S(1)} fusion(bf16[4,1024]{1,0:T(4,128)(2,1)S(1)} %get-tuple-element.33, bf16[256,1024]{1,0:T(8,128)(2,1)} %bitcast, s32[]{:T(128)S(6)} %select_n.262, bf16[256,768]{0,1:T(8,128)(2,1)S(1)} %bitcast.346, bf16[4,768]{0,1:T(8,128)(2,1)S(1)} %copy.82), kind=kOutput, calls=%fused_computation.65 | convolution fusion | flops 205936640 | bytes 2504708 | tf_op jit(solution)/shard_map/rd,rf->df/dot_general | solution.py:15
  80.6 5.0 %collective-permute-done.15 = bf16[103936]{0:T(1024)(128)(2,1)S(1)} collective-permute-done((bf16[103936]{0:T(1024)(128)(2,1)S(1)}, bf16[103936]{0:T(1024)(128)(2,1)S(1)}, u32[]{:S(2)}, u32[]{:S(2)}) %collective-permute-start.15) | collective-permute-done | bytes 207904 | tf_op jit(solution)/shard_map/ppermute | solution.py:339
  85.9 1.4 %fusion.145 = f32[384,1024]{1,0:T(8,128)S(1)} fusion(bf16[256,384]{1,0:T(8,128)(2,1)S(1)} %slice.153, bf16[256,1024]{1,0:T(8,128)(2,1)} %collective-permute-done.16), kind=kOutput, calls=%fused_computation.265 | convolution fusion | flops 201326592 | bytes 2293760 | tf_op jit(solution)/shard_map/rd,rf->df/dot_general | solution.py:15
  88.4 2.9 %collective-permute-start.18 = (bf16[256,384]{0,1:T(8,128)(2,1)S(1)}, bf16[256,384]{0,1:T(8,128)(2,1)S(1)}, u32[]{:S(2)}, u32[]{:S(2)}) collective-permute-start(bf16[256,384]{0,1:T(8,128)(2,1)S(1)} %get-tuple-element.24), channel_id=1, source_target_pairs={{0,8},{4,12},{8,0},{12,4},{1,9},{5,13},{9,1},{13,5},{2,10},{6,14},... | collective-permute-start | bytes 589832 | tf_op jit(solution)/shard_map/ppermute | solution.py:89
  91.7 10.3 %collective-permute-done.17 = bf16[256,384]{0,1:T(8,128)(2,1)S(1)} collective-permute-done((bf16[256,384]{0,1:T(8,128)(2,1)S(1)}, bf16[256,384]{0,1:T(8,128)(2,1)S(1)}, u32[]{:S(2)}, u32[]{:S(2)}) %collective-permute-start.17) | collective-permute-done | bytes 196640 | tf_op jit(solution)/shard_map/ppermute | solution.py:89
  102.0 2.7 %collective-permute-done.18 = bf16[256,384]{0,1:T(8,128)(2,1)S(1)} collective-permute-done((bf16[256,384]{0,1:T(8,128)(2,1)S(1)}, bf16[256,384]{0,1:T(8,128)(2,1)S(1)}, u32[]{:S(2)}, u32[]{:S(2)}) %collective-permute-start.18) | collective-permute-done | bytes 196640 | tf_op jit(solution)/shard_map/ppermute | solution.py:89
  104.7 3.1 %collective-permute-done.19 = bf16[256,384]{0,1:T(8,128)(2,1)S(1)} collective-permute-done((bf16[256,384]{0,1:T(8,128)(2,1)S(1)}, bf16[256,384]{0,1:T(8,128)(2,1)S(1)}, u32[]{:S(2)}, u32[]{:S(2)}) %collective-permute-start.19) | collective-permute-done | bytes 196640 | tf_op jit(solution)/shard_map/ppermute | solution.py:89
  108.5 5.9 %collective-permute-done.20 = bf16[256,384]{0,1:T(8,128)(2,1)S(1)} collective-permute-done((bf16[256,384]{0,1:T(8,128)(2,1)S(1)}, bf16[256,384]{0,1:T(8,128)(2,1)S(1)}, u32[]{:S(2)}, u32[]{:S(2)}) %collective-permute-start.20) | collective-permute-done | bytes 196640 | tf_op jit(solution)/shard_map/ppermute | solution.py:350
  114.6 1.1 copy.84
  (227 shorter events, 27.0 us)
Async XLA Ops:
  1.4 10.0 %collective-permute-start = (f32[1,1,1025]{2,1,0:T(1,128)S(1)}, f32[1,1,1025]{2,1,0:T(1,128)S(1)}, u32[]{:S(2)}, u32[]{:S(2)}) collective-permute-start(f32[1,1,1025]{2,1,0:T(1,128)S(1)} %pad_maximum_fusion.4), channel_id=1, source_target_pairs={{0,4},{4,8},{8,12},{12,0},{1,5},{5,9},{9,13},{13,1},{2,6},{6,10},{... | collective-permute-start | bytes 12308 | tf_op jit(solution)/shard_map/ppermute | solution.py:60
  3.0 8.4 %collective-permute-start.1 = (f32[1,1,1025]{2,1,0:T(1,128)S(1)}, f32[1,1,1025]{2,1,0:T(1,128)S(1)}, u32[]{:S(2)}, u32[]{:S(2)}) collective-permute-start(f32[1,1,1025]{2,1,0:T(1,128)S(1)} %pad_maximum_fusion.4), channel_id=1, source_target_pairs={{0,8},{4,12},{8,0},{12,4},{1,9},{5,13},{9,1},{13,5},{2,10},{6,14},... | collective-permute-start | bytes 12308 | tf_op jit(solution)/shard_map/ppermute | solution.py:60
  4.1 7.3 %collective-permute-start.2 = (f32[1,1,1025]{2,1,0:T(1,128)S(1)}, f32[1,1,1025]{2,1,0:T(1,128)S(1)}, u32[]{:S(2)}, u32[]{:S(2)}) collective-permute-start(f32[1,1,1025]{2,1,0:T(1,128)S(1)} %pad_maximum_fusion.4), channel_id=1, source_target_pairs={{0,12},{4,0},{8,4},{12,8},{1,13},{5,1},{9,5},{13,9},{2,14},{6,2},{... | collective-permute-start | bytes 12308 | tf_op jit(solution)/shard_map/ppermute | solution.py:60
  6.1 15.0 %collective-permute-start.3 = (bf16[256,1024]{1,0:T(8,128)(2,1)}, bf16[256,1024]{1,0:T(8,128)(2,1)}, u32[]{:S(2)}, u32[]{:S(2)}) collective-permute-start(bf16[256,1024]{1,0:T(8,128)(2,1)} %param.14), channel_id=1, source_target_pairs={{0,1},{1,0},{2,3},{3,2},{4,5},{5,4},{6,7},{7,6},{8,9},{9,8},{10,11... | collective-permute-start | bytes 1572872 | tf_op jit(solution)/shard_map/ppermute | solution.py:97
  6.1 30.5 %collective-permute-start.7 = (bf16[256,1024]{1,0:T(8,128)(2,1)}, bf16[256,1024]{1,0:T(8,128)(2,1)}, u32[]{:S(2)}, u32[]{:S(2)}) collective-permute-start(bf16[256,1024]{1,0:T(8,128)(2,1)} %param.17), channel_id=1, source_target_pairs={{0,1},{1,0},{2,3},{3,2},{4,5},{5,4},{6,7},{7,6},{8,9},{9,8},{10,11... | collective-permute-start | bytes 1572872 | tf_op jit(solution)/shard_map/ppermute | solution.py:97
  6.6 5.4 %copy-start = (bf16[3,1024,256]{2,1,0:T(8,128)(2,1)S(1)}, bf16[3,1024,256]{2,1,0:T(8,128)(2,1)}, u32[]{:S(2)}) copy-start(bf16[3,1024,256]{2,1,0:T(8,128)(2,1)} %param.13) | copy-start | bytes 4718596
  8.9 14.0 %copy-start.3 = (bf16[1,1,1,256,256]{3,4,0,2,1:T(8,128)(2,1)}, bf16[1,1,1,256,256]{3,4,0,2,1:T(8,128)(2,1)S(1)}, u32[]{:S(2)}) copy-start(bf16[1,1,1,256,256]{3,4,0,2,1:T(8,128)(2,1)S(1)} %get-tuple-element.26) | copy-start | bytes 393220
  10.7 59.7 %copy-start.10 = (pred[256]{0:T(512)(128)(4,1)}, pred[256]{0:T(512)(128)(4,1)S(1)}, u32[]{:S(2)}) copy-start(pred[256]{0:T(512)(128)(4,1)S(1)} %iota_compare_fusion.1) | copy-start | bytes 772
  11.4 54.8 %collective-permute-start.14 = (bf16[3,1024,256]{2,1,0:T(8,128)(2,1)}, bf16[3,1024,256]{2,1,0:T(8,128)(2,1)}, u32[]{:S(2)}, u32[]{:S(2)}) collective-permute-start(bf16[3,1024,256]{2,1,0:T(8,128)(2,1)} %param.16), channel_id=1, source_target_pairs={{0,1},{1,0},{2,3},{3,2},{4,5},{5,4},{6,7},{7,6},{8,9},{9,8},{10,11... | collective-permute-start | bytes 4718600 | tf_op jit(solution)/shard_map/ppermute | solution.py:97
  12.4 2.5 %copy-start.16 = (bf16[4,4,64]{2,1,0:T(4,128)(2,1)}, bf16[4,4,64]{2,1,0:T(4,128)(2,1)S(1)}, u32[]{:S(2)}) copy-start(bf16[4,4,64]{2,1,0:T(4,128)(2,1)S(1)} %reshape.1066) | copy-start | bytes 6148
  14.2 9.2 %copy-start.5 = (f32[4,256]{1,0:T(4,128)}, f32[4,256]{1,0:T(4,128)S(1)}, u32[]{:S(2)}) copy-start(f32[4,256]{1,0:T(4,128)S(1)} %broadcast_select_fusion.1) | copy-start | bytes 12292
  15.1 3.8 %copy-start.18 = (bf16[4,4,64]{2,1,0:T(4,128)(2,1)}, bf16[4,4,64]{2,1,0:T(4,128)(2,1)S(1)}, u32[]{:S(2)}) copy-start(bf16[4,4,64]{2,1,0:T(4,128)(2,1)S(1)} %reshape.1069) | copy-start | bytes 6148
  22.9 47.5 %copy-start.9 = (f32[256]{0:T(256)}, f32[256]{0:T(256)S(1)}, u32[]{:S(2)}) copy-start(f32[256]{0:T(256)S(1)} %broadcast_multiply_fusion.3) | copy-start | bytes 3076
  23.2 47.2 %copy-start.12 = (f32[256]{0:T(256)}, f32[256]{0:T(256)S(1)}, u32[]{:S(2)}) copy-start(f32[256]{0:T(256)S(1)} %add_rsqrt_fusion) | copy-start | bytes 3076
  23.5 13.1 %copy-start.1 = (bf16[256,1024]{1,0:T(8,128)(2,1)S(1)}, bf16[256,1024]{1,0:T(8,128)(2,1)}, u32[]{:S(2)}) copy-start(bf16[256,1024]{1,0:T(8,128)(2,1)} %param.17) | copy-start | bytes 1572868
  25.3 5.7 %collective-permute-start.4 = (bf16[1,1,512]{2,1,0:T(2,128)(2,1)S(1)}, bf16[1,1,512]{2,1,0:T(2,128)(2,1)S(1)}, u32[]{:S(2)}, u32[]{:S(2)}) collective-permute-start(bf16[1,1,512]{2,1,0:T(2,128)(2,1)S(1)} %pad_maximum_fusion.5), channel_id=1, source_target_pairs={{0,4},{4,8},{8,12},{12,0},{1,5},{5,9},{9,13},{13,1},{2,6},{6,10},{... | collective-permute-start | bytes 3080 | tf_op jit(solution)/shard_map/ppermute | solution.py:60
  25.4 7.1 %collective-permute-start.5 = (bf16[1,1,512]{2,1,0:T(2,128)(2,1)S(1)}, bf16[1,1,512]{2,1,0:T(2,128)(2,1)S(1)}, u32[]{:S(2)}, u32[]{:S(2)}) collective-permute-start(bf16[1,1,512]{2,1,0:T(2,128)(2,1)S(1)} %pad_maximum_fusion.5), channel_id=1, source_target_pairs={{0,8},{4,12},{8,0},{12,4},{1,9},{5,13},{9,1},{13,5},{2,10},{6,14},... | collective-permute-start | bytes 3080 | tf_op jit(solution)/shard_map/ppermute | solution.py:60
  29.1 3.6 %collective-permute-start.6 = (bf16[1,1,512]{2,1,0:T(2,128)(2,1)S(1)}, bf16[1,1,512]{2,1,0:T(2,128)(2,1)S(1)}, u32[]{:S(2)}, u32[]{:S(2)}) collective-permute-start(bf16[1,1,512]{2,1,0:T(2,128)(2,1)S(1)} %pad_maximum_fusion.5), channel_id=1, source_target_pairs={{0,12},{4,0},{8,4},{12,8},{1,13},{5,1},{9,5},{13,9},{2,14},{6,2},{... | collective-permute-start | bytes 3080 | tf_op jit(solution)/shard_map/ppermute | solution.py:60
  31.0 54.9 %collective-permute-start.16 = (bf16[256,1024]{1,0:T(8,128)(2,1)}, bf16[256,1024]{1,0:T(8,128)(2,1)}, u32[]{:S(2)}, u32[]{:S(2)}) collective-permute-start(bf16[256,1024]{1,0:T(8,128)(2,1)} %bitcast), channel_id=1, source_target_pairs={{0,2},{2,0},{1,3},{3,1},{4,6},{6,4},{5,7},{7,5},{8,10},{10,8},{9,1... | collective-permute-start | bytes 1572872 | tf_op jit(solution)/shard_map/ppermute | solution.py:149
  34.5 6.1 %copy-start.7 = (f32[1024]{0:T(1024)S(1)}, f32[1024]{0:T(1024)}, u32[]{:S(2)}) copy-start(f32[1024]{0:T(1024)} %param.18) | copy-start | bytes 12292
  34.5 6.1 %copy-start.8 = (f32[1024]{0:T(1024)S(1)}, f32[1024]{0:T(1024)}, u32[]{:S(2)}) copy-start(f32[1024]{0:T(1024)} %param.19) | copy-start | bytes 12292
  41.8 7.8 %collective-permute-start.8 = (f32[1]{0:T(128)}, f32[1]{0:T(128)}, u32[]{:S(2)}, u32[]{:S(2)}) collective-permute-start(f32[1]{0:T(128)} %bitcast.72), channel_id=1, source_target_pairs={{0,4},{4,8},{8,12},{12,0},{1,5},{5,9},{9,13},{13,1},{2,6},{6,10},{... | collective-permute-start | bytes 20 | tf_op jit(solution)/shard_map/ppermute | solution.py:75
  45.1 5.1 %collective-permute-start.9 = (f32[1]{0:T(128)}, f32[1]{0:T(128)}, u32[]{:S(2)}, u32[]{:S(2)}) collective-permute-start(f32[1]{0:T(128)} %bitcast.72), channel_id=1, source_target_pairs={{0,8},{4,12},{8,0},{12,4},{1,9},{5,13},{9,1},{13,5},{2,10},{6,14},... | collective-permute-start | bytes 20 | tf_op jit(solution)/shard_map/ppermute | solution.py:75
  48.2 3.6 %collective-permute-start.10 = (f32[1]{0:T(128)}, f32[1]{0:T(128)}, u32[]{:S(2)}, u32[]{:S(2)}) collective-permute-start(f32[1]{0:T(128)} %bitcast.72), channel_id=1, source_target_pairs={{0,12},{4,0},{8,4},{12,8},{1,13},{5,1},{9,5},{13,9},{2,14},{6,2},{... | collective-permute-start | bytes 20 | tf_op jit(solution)/shard_map/ppermute | solution.py:75
  55.8 5.7 %collective-permute-start.11 = (f32[1,1,512]{2,1,0:T(1,128)S(1)}, f32[1,1,512]{2,1,0:T(1,128)S(1)}, u32[]{:S(2)}, u32[]{:S(2)}) collective-permute-start(f32[1,1,512]{2,1,0:T(1,128)S(1)} %get-tuple-element.34), channel_id=1, source_target_pairs={{0,4},{4,8},{8,12},{12,0},{1,5},{5,9},{9,13},{13,1},{2,6},{6,10},{... | collective-permute-start | bytes 6152 | tf_op jit(solution)/shard_map/ppermute | solution.py:89
  56.8 4.7 %collective-permute-start.12 = (f32[1,1,512]{2,1,0:T(1,128)S(1)}, f32[1,1,512]{2,1,0:T(1,128)S(1)}, u32[]{:S(2)}, u32[]{:S(2)}) collective-permute-start(f32[1,1,512]{2,1,0:T(1,128)S(1)} %get-tuple-element.36), channel_id=1, source_target_pairs={{0,8},{4,12},{8,0},{12,4},{1,9},{5,13},{9,1},{13,5},{2,10},{6,14},... | collective-permute-start | bytes 6152 | tf_op jit(solution)/shard_map/ppermute | solution.py:89
  59.7 3.6 %collective-permute-start.13 = (f32[1,1,512]{2,1,0:T(1,128)S(1)}, f32[1,1,512]{2,1,0:T(1,128)S(1)}, u32[]{:S(2)}, u32[]{:S(2)}) collective-permute-start(f32[1,1,512]{2,1,0:T(1,128)S(1)} %get-tuple-element.35), channel_id=1, source_target_pairs={{0,12},{4,0},{8,4},{12,8},{1,13},{5,1},{9,5},{13,9},{2,14},{6,2},{... | collective-permute-start | bytes 6152 | tf_op jit(solution)/shard_map/ppermute | solution.py:89
  78.4 7.3 %collective-permute-start.15 = (bf16[103936]{0:T(1024)(128)(2,1)S(1)}, bf16[103936]{0:T(1024)(128)(2,1)S(1)}, u32[]{:S(2)}, u32[]{:S(2)}) collective-permute-start(bf16[103936]{0:T(1024)(128)(2,1)S(1)} %pad_maximum_fusion.2), channel_id=1, source_target_pairs={{0,2},{2,0},{1,3},{3,1},{4,6},{6,4},{5,7},{7,5},{8,10},{10,8},{9,1... | collective-permute-start | bytes 623624 | tf_op jit(solution)/shard_map/ppermute | solution.py:339
  87.8 14.2 %collective-permute-start.17 = (bf16[256,384]{0,1:T(8,128)(2,1)S(1)}, bf16[256,384]{0,1:T(8,128)(2,1)S(1)}, u32[]{:S(2)}, u32[]{:S(2)}) collective-permute-start(bf16[256,384]{0,1:T(8,128)(2,1)S(1)} %get-tuple-element.22), channel_id=1, source_target_pairs={{0,4},{4,8},{8,12},{12,0},{1,5},{5,9},{9,13},{13,1},{2,6},{6,10},{... | collective-permute-start | bytes 589832 | tf_op jit(solution)/shard_map/ppermute | solution.py:89
  88.4 16.3 %collective-permute-start.18 = (bf16[256,384]{0,1:T(8,128)(2,1)S(1)}, bf16[256,384]{0,1:T(8,128)(2,1)S(1)}, u32[]{:S(2)}, u32[]{:S(2)}) collective-permute-start(bf16[256,384]{0,1:T(8,128)(2,1)S(1)} %get-tuple-element.24), channel_id=1, source_target_pairs={{0,8},{4,12},{8,0},{12,4},{1,9},{5,13},{9,1},{13,5},{2,10},{6,14},... | collective-permute-start | bytes 589832 | tf_op jit(solution)/shard_map/ppermute | solution.py:89
  91.3 16.5 %collective-permute-start.19 = (bf16[256,384]{0,1:T(8,128)(2,1)S(1)}, bf16[256,384]{0,1:T(8,128)(2,1)S(1)}, u32[]{:S(2)}, u32[]{:S(2)}) collective-permute-start(bf16[256,384]{0,1:T(8,128)(2,1)S(1)} %get-tuple-element.23), channel_id=1, source_target_pairs={{0,12},{4,0},{8,4},{12,8},{1,13},{5,1},{9,5},{13,9},{2,14},{6,2},{... | collective-permute-start | bytes 589832 | tf_op jit(solution)/shard_map/ppermute | solution.py:89
  107.9 6.6 %collective-permute-start.20 = (bf16[256,384]{0,1:T(8,128)(2,1)S(1)}, bf16[256,384]{0,1:T(8,128)(2,1)S(1)}, u32[]{:S(2)}, u32[]{:S(2)}) collective-permute-start(bf16[256,384]{0,1:T(8,128)(2,1)S(1)} %add_convert_fusion), channel_id=1, source_target_pairs={{0,2},{2,0},{1,3},{3,1},{4,6},{6,4},{5,7},{7,5},{8,10},{10,8},{9,1... | collective-permute-start | bytes 589832 | tf_op jit(solution)/shard_map/ppermute | solution.py:350
  (9 other events, 12.4 us)

commit v9 on v8

--- a/solution.py
+++ b/solution.py
@@ -178,10 +178,11 @@
     last_query = mixed("qcd,df->qcf", hidden[:, :, 0], w_last[0]).astype(jnp.bfloat16)
     last_kv = mixed("qcsd,kdf->kqcsf", hidden, w_last[1:]).astype(jnp.bfloat16)
     gathered_kv_last = gather_cand(
-        jnp.concatenate([last_kv[0][:, :, 0], last_kv[1][:, :, 0]], -1), 1
+        jnp.concatenate([last_kv[0][:, :, 0], last_kv[1][:, :, 0], last_query], -1), 1
     )
     gathered_keys_last = gathered_kv_last[..., :local_width]
-    gathered_vals_last = gathered_kv_last[..., local_width:]
+    gathered_vals_last = gathered_kv_last[..., local_width : 2 * local_width]
+    cls_queries_last = gathered_kv_last[..., 2 * local_width :].reshape(cls_shape)
     last_heads = last_query.reshape(lists, local_cands, local_heads, HEAD_DIM)
     last_keys = last_kv[0].reshape(head_shape)
     last_vals = last_kv[1].reshape(head_shape)
@@ -202,23 +203,46 @@
     residual_last = hidden[:, :, 0].astype(jnp.float32) + mixed(
         "qcf,fd->qcd", last_joined, out_last_full
     )
-    normed_last, unit_last, inverse_last = norm_forward(residual_last, gain_last)
-    scores = jnp.einsum("qcd,d->qc", normed_last, w_score, precision=lax.Precision.HIGHEST)
+    exact = lax.Precision.HIGHEST
+    mean_last = jnp.einsum(
+        "qcht,qcthe->qche", own_last_prob, last_vals.astype(jnp.float32), precision=exact
+    ) + jnp.einsum(
+        "qchd,qdhe->qche", cross_last_prob, cls_vals_last.astype(jnp.float32), precision=exact
+    )
+    shared_last = gather_cand(
+        jnp.concatenate(
+            [
+                residual_last,
+                mean_last.reshape(lists, local_cands, local_width),
+                cross_last_prob.reshape(lists, local_cands, local_heads * cand_count),
+            ],
+            -1,
+        ),
+        1,
+    )
+    all_residual = shared_last[..., :model_width]
+    all_mean = shared_last[..., model_width : model_width + local_width].reshape(cls_shape)
+    all_cross_prob = shared_last[..., model_width + local_width :].reshape(
+        lists, cand_count, local_heads, cand_count
+    )
+    normed_last, unit_last, inverse_last = norm_forward(all_residual, gain_last)
+    scores = jnp.einsum("qcd,d->qc", normed_last, w_score, precision=exact)
     score_exp = jnp.exp(scores)
     teacher_peak = jnp.max(teacher_all, 1)
-    teacher_exp = jnp.exp(teacher - teacher_peak[:, None])
-    teacher_totals = jnp.sum(jnp.exp(teacher_all - teacher_peak[:, None]), 1)
-    score_totals = sum_cand(jnp.sum(score_exp, 1))
-    student_prob = score_exp / score_totals[:, None]
-    teacher_prob = teacher_exp / teacher_totals[:, None]
+    teacher_exp = jnp.exp(teacher_all - teacher_peak[:, None])
+    student_prob = score_exp / jnp.sum(score_exp, 1)[:, None]
+    teacher_prob = teacher_exp / jnp.sum(teacher_exp, 1)[:, None]
     score_grad = LOSS_SCALE * (student_prob - teacher_prob) / query_count
-    grad_last = norm_backward(score_grad[..., None] * w_score, unit_last, inverse_last, gain_last)
-    grad_last_low = grad_last.astype(jnp.bfloat16)
-    grad_mixed_last = (
-        mixed("qcd,fd->qcf", grad_last_low, w_out_last)
+    grad_last_all = norm_backward(
+        score_grad[..., None] * w_score, unit_last, inverse_last, gain_last
+    )
+    grad_mixed_all = (
+        mixed("qcd,fd->qcf", grad_last_all.astype(jnp.bfloat16), w_out_last)
         .astype(jnp.bfloat16)
-        .reshape(lists, local_cands, local_heads, HEAD_DIM)
-    )
+        .reshape(cls_shape)
+    )
+    grad_last = jnp.take(grad_last_all, local_ids, axis=1)
+    grad_mixed_last = jnp.take(grad_mixed_all, local_ids, axis=1)
     own_dot = mixed("qche,qcthe->qcht", grad_mixed_last, last_vals)
     cross_dot = mixed("qche,qdhe->qchd", grad_mixed_last, cls_vals_last)
     centre = jnp.sum(own_last_prob * own_dot, -1, keepdims=True) + jnp.sum(
@@ -243,15 +267,17 @@
     own_val_grad = mixed("qcht,qche->qcthe", own_last_weight, grad_mixed_last).reshape(
         lists, local_cands, seq_len, local_width
     )
-    cls_key_terms = (mixed("qchd,qche->qdhe", cross_slope, last_heads) * score_scale).reshape(
-        lists, cand_count, local_width
-    )
-    cls_val_terms = mixed("qchd,qche->qdhe", cross_last_weight, grad_mixed_last).reshape(
-        lists, cand_count, local_width
-    )
-    back_terms = scatter_cand(jnp.concatenate([cls_key_terms, cls_val_terms], -1), 1)
-    back_keys = back_terms[..., :local_width]
-    back_vals = back_terms[..., local_width:]
+    own_cls_vals = last_vals[:, :, 0]
+    dot_in = mixed("qche,qdhe->qchd", grad_mixed_all, own_cls_vals)
+    centre_all = jnp.sum(grad_mixed_all.astype(jnp.float32) * all_mean, -1)
+    prob_in = jnp.take(all_cross_prob, local_ids, axis=3)
+    slope_in = (prob_in * (dot_in - centre_all[..., None])).astype(jnp.bfloat16)
+    back_keys = (
+        mixed("qchd,qche->qdhe", slope_in, cls_queries_last) * score_scale
+    ).reshape(lists, local_cands, local_width)
+    back_vals = mixed(
+        "qchd,qche->qdhe", prob_in.astype(jnp.bfloat16), grad_mixed_all
+    ).reshape(lists, local_cands, local_width)
     first_cols = first_mask[None, None, :, None]
     key_grad = jnp.where(first_cols, own_key_grad + back_keys[:, :, None], own_key_grad).astype(
         jnp.bfloat16

time: 116 us -> 119 us (1.026)
  the two profiles are of different devices: /device:TPU:8 before, /device:TPU:0 now
where the time goes in v9:
time: 119 us; the launch traced here: 118 us
  waiting for transfers between devices  31.1 us (26%)
  matrix products  23 us (19%)
  other arithmetic  20.1 us (17%)
  starting transfers between devices  19.9 us (17%)
  local copies, waits for them, and re-layouts  15.7 us (13%)
  blocking collectives  6.36 us (5%)
  between operations  2.12 us (2%)
    dot_general x35, matrix products, mixed(): jnp.einsum(pattern, former, latter, preferred_element_type=jnp.float32)  21.8 us
    ppermute x3, waiting for transfers between devices, scatter_cand(): lax.ppermute(piece, 'cand', [(j, (j + k) % count) for j in range(count)])  15 us
    ppermute x9, starting transfers between devices, gather_cand(): lax.ppermute(block, 'cand', [(j, (j + k) % count) for j in range(count)])  13.4 us
    ppermute x9, waiting for transfers between devices, gather_cand(): lax.ppermute(block, 'cand', [(j, (j + k) % count) for j in range(count)])  5.86 us
    ppermute x1, waiting for transfers between devices, local(): partner = lax.ppermute(reduced, 'query', swap)  5.14 us
    ppermute x1, waiting for transfers between devices, local(): lax.ppermute(jnp.concatenate([given_half.reshape(-1), cls_flat.reshape(-1...  5.05 us
    unnamed x77, local copies, waits for them, and re-layouts  3.82 us
    select_n x1, other arithmetic, gather_mp(): jnp.where(lax.axis_index('mp') == 0, jnp.concatenate([block, other], axis...  3.41 us
  transfers between devices with their start and end apart: 18, of which 8 were waited for; matrix products, arithmetic and copies ran while one was open for 45% of the time, Pallas kernels for 0%

profile of v9, /device:TPU:0, one launch (start us, length us, event | category | flops | bytes accessed | tf_op | source)
XLA Modules:
  0.0 118.2 jit_solution(15282473659483823681)
XLA Ops:
  1.4 5.1 %collective-permute-start.2 = (f32[1,1,1025]{2,1,0:T(1,128)S(1)}, f32[1,1,1025]{2,1,0:T(1,128)S(1)}, u32[]{:S(2)}, u32[]{:S(2)}) collective-permute-start(f32[1,1,1025]{2,1,0:T(1,128)S(1)} %pad_maximum_fusion.5), channel_id=1, source_target_pairs={{0,12},{4,0},{8,4},{12,8},{1,13},{5,1},{9,5},{13,9},{2,14},{6,2},{... | collective-permute-start | bytes 12308 | tf_op jit(solution)/shard_map/ppermute | solution.py:60
  6.5 1.0 collective-permute-start
  8.1 2.3 %fusion.5 = bf16[3,1,1,256,256]{3,4,0,2,1:T(8,128)(2,1)S(1)} fusion(bf16[3,1024,256]{2,1,0:T(8,128)(2,1)} %param.13, bf16[1,1,256,1024]{3,2,1,0:T(8,128)(2,1)} %param.10), kind=kOutput, calls=%fused_computation.16 | convolution fusion | flops 402849792 | bytes 2490368 | tf_op jit(solution)/shard_map/qcsd,kdf->kqcsf/dot_general | solution.py:15
  17.3 2.1 %all_gather.9 = bf16[1,1,256,512]{2,3,1,0:T(8,128)(2,1)S(1)} all-gather(bf16[1,1,256,256]{2,3,1,0:T(8,128)(2,1)S(1)} %bitcast.372), channel_id=1, replica_groups=mesh['groups'=2,'cand'=4,'query'=2,'mp'=2] {'mp'}, dimensions={3}, use_global_device_ids=true | all-gather | bytes 393216 | tf_op jit(solution)/shard_map/all_gather | solution.py:172
  20.0 1.2 %fusion.128 = f32[]{:T(128)} fusion(f32[1,4,1025]{2,1,0:T(4,128)S(1)} %bitcast_select_fusion.1, f32[]{:T(128)} %slice_reduce_fusion.5), kind=kLoop, calls=%fused_computation.245 | loop fusion | flops 7 | bytes 24 | tf_op jit(solution)/shard_map/reduce_sum | solution.py:234
  21.3 1.9 %divide_reduce_fusion = f32[4]{0:T(128)} fusion(f32[1,4,1025]{2,1,0:T(4,128)S(1)} %bitcast_select_fusion.1, f32[]{:T(128)} %fusion.128, f32[]{:T(128)} %slice_reduce_fusion.5), kind=kLoop, calls=%fused_computation.228 | loop fusion | flops 8 | bytes 40 | tf_op jit(solution)/shard_map/div | solution.py:234
  23.2 1.9 %fusion.159 = (f32[256]{0:T(256)S(1)}, f32[1,1,256,1024]{3,2,1,0:T(8,128)S(1)}) fusion(bf16[256,1024]{1,0:T(8,128)(2,1)} %collective-permute-done.3, bf16[256,1024]{1,0:T(8,128)(2,1)S(1)} %copy-done.4, pred[]{:T(512)S(6)} %eq.49, bf16[1,1,256,512]{2,3,1,0:T(8,128)(2,1)S(1)} %all_gather.9, bf16[1,1,256,1024]{3,2,1,0:T(8,128)(2,1)} %param.10), kind=kOutput, calls=%fused_computation.292 | convolution fusion | flops 273940224 | bytes 2884609 | tf_op jit(solution)/shard_map/qcsf,fd->qcsd/dot_general | solution.py:15
  25.6 1.2 %fusion.40 = f32[1,256]{1,0:T(1,128)S(1)} fusion(bf16[3,1024,256]{2,1,0:T(8,128)(2,1)} %param.16, bf16[1,1,256,1024]{3,2,1,0:T(8,128)(2,1)S(1)} %multiply_convert_fusion.1), kind=kOutput, calls=%fused_computation.76 | convolution fusion | flops 524288 | bytes 529408 | tf_op jit(solution)/shard_map/qcd,df->qcf/dot_general | solution.py:15
  26.9 2.5 %fusion.6 = bf16[2,1,1,256,256]{3,4,0,2,1:T(8,128)(2,1)} fusion(bf16[3,1024,256]{2,1,0:T(8,128)(2,1)} %param.16, bf16[1,1,256,1024]{3,2,1,0:T(8,128)(2,1)S(1)} %multiply_convert_fusion.1), kind=kOutput, calls=%fused_computation.21 | convolution fusion | flops 268566528 | bytes 1835008 | tf_op jit(solution)/shard_map/qcsd,kdf->kqcsf/dot_general | solution.py:15
  30.6 1.0 fusion.155
  33.0 1.2 %constant_dynamic-update-slice_fusion = bf16[1,1,768]{2,1,0:T(2,128)(2,1)} fusion(bf16[1,1,768]{2,1,0:T(2,128)(2,1)} %constant_dynamic-update-slice_fusion.1, bf16[256]{0:T(256)(128)(2,1)} %copy-done.33), kind=kLoop, calls=%fused_computation.137 | loop fusion | bytes 1536 | tf_op jit(solution)/shard_map/concatenate | solution.py:181
  34.2 2.8 %collective-permute-start.6 = (bf16[1,1,768]{2,1,0:T(2,128)(2,1)}, bf16[1,1,768]{2,1,0:T(2,128)(2,1)}, u32[]{:S(2)}, u32[]{:S(2)}) collective-permute-start(bf16[1,1,768]{2,1,0:T(2,128)(2,1)} %constant_dynamic-update-slice_fusion), channel_id=1, source_target_pairs={{0,12},{4,0},{8,4},{12,8},{1,13},{5,1},{9,5},{13,9},{2,14},{6,2},{... | collective-permute-start | bytes 4616 | tf_op jit(solution)/shard_map/ppermute | solution.py:60
  37.0 1.1 collective-permute-start.5
  41.1 1.6 %collective-permute-start.13 = (bf16[256,1024]{1,0:T(8,128)(2,1)}, bf16[256,1024]{1,0:T(8,128)(2,1)}, u32[]{:S(2)}, u32[]{:S(2)}) collective-permute-start(bf16[256,1024]{1,0:T(8,128)(2,1)} %bitcast), channel_id=1, source_target_pairs={{0,2},{2,0},{1,3},{3,1},{4,6},{6,4},{5,7},{7,5},{8,10},{10,8},{9,1... | collective-permute-start | bytes 1572872 | tf_op jit(solution)/shard_map/ppermute | solution.py:149
  42.6 1.2 collective-permute-done.4
  51.8 1.8 %all_gather.10 = bf16[1,1,512]{2,1,0:T(2,128)(2,1)S(1)} all-gather(bf16[1,1,256]{2,1,0:T(2,128)(2,1)S(1)} %convert_element_type.294), channel_id=1, replica_groups=mesh['groups'=2,'cand'=4,'query'=2,'mp'=2] {'mp'}, dimensions={2}, use_global_device_ids=true | all-gather | bytes 1536 | tf_op jit(solution)/shard_map/all_gather | solution.py:202
  53.6 1.6 %fusion.17 = f32[1,1024]{1,0:T(1,128)S(1)} fusion(bf16[256,1024]{1,0:T(8,128)(2,1)} %collective-permute-done.7, bf16[256,1024]{1,0:T(8,128)(2,1)S(1)} %copy-done.1, pred[]{:T(512)S(6)} %eq.49, bf16[1,1,512]{2,1,0:T(2,128)(2,1)S(1)} %all_gather.10), kind=kOutput, calls=%fused_computation.42 | convolution fusion | flops 5767168 | bytes 1053697 | tf_op jit(solution)/shard_map/qcf,fd->qcd/dot_general | solution.py:15
  55.3 2.7 %collective-permute-start.10 = (f32[1,1,1296]{2,1,0:T(1,128)S(1)}, f32[1,1,1296]{2,1,0:T(1,128)S(1)}, u32[]{:S(2)}, u32[]{:S(2)}) collective-permute-start(f32[1,1,1296]{2,1,0:T(1,128)S(1)} %pad_maximum_fusion.4), channel_id=1, source_target_pairs={{0,12},{4,0},{8,4},{12,8},{1,13},{5,1},{9,5},{13,9},{2,14},{6,2},{... | collective-permute-start | bytes 15560 | tf_op jit(solution)/shard_map/ppermute | solution.py:60
  59.3 3.2 %collective-permute-done.9 = f32[1,1,1296]{2,1,0:T(1,128)S(1)} collective-permute-done((f32[1,1,1296]{2,1,0:T(1,128)S(1)}, f32[1,1,1296]{2,1,0:T(1,128)S(1)}, u32[]{:S(2)}, u32[]{:S(2)}) %collective-permute-start.9) | collective-permute-done | bytes 5216 | tf_op jit(solution)/shard_map/ppermute | solution.py:60
  62.5 0.9 collective-permute-done.8
  64.6 0.9 fusion.160
  69.7 2.5 %all_gather.11 = bf16[1,1,513,512]{2,3,1,0:T(8,128)(2,1)S(1)} all-gather(bf16[1,1,513,256]{2,3,1,0:T(8,128)(2,1)S(1)} %pad_maximum_fusion.1), channel_id=1, replica_groups=mesh['groups'=2,'cand'=4,'query'=2,'mp'=2] {'mp'}, dimensions={3}, use_global_device_ids=true | all-gather | bytes 787968 | tf_op jit(solution)/shard_map/all_gather | solution.py:288
  72.4 3.4 %maximum_select_fusion = bf16[3,1024,512]{2,1,0:T(8,128)(2,1)S(1)} fusion(bf16[3,1024,256]{2,1,0:T(8,128)(2,1)} %collective-permute-done.11, bf16[3,1024,256]{2,1,0:T(8,128)(2,1)} %param.16, pred[]{:T(512)S(6)} %eq.49), kind=kLoop, calls=%fused_computation.3 | loop fusion | flops 14155776 | bytes 6291457 | tf_op jit(solution)/shard_map/jit(_where)/select_n | solution.py:98
  77.7 1.6 %convolution_convert_fusion.3 = bf16[256,256]{0,1:T(8,128)(2,1)S(1)} fusion(bf16[256,1024]{1,0:T(8,128)(2,1)} %param.14, f32[1,1,256,1024]{3,2,1,0:T(8,128)S(1)} %get-tuple-element.74, f32[256,1024]{1,0:T(8,128)S(1)} %get-tuple-element.78, f32[256]{0:T(256)S(1)} %broadcast_multiply_fusion.2, f32[256]{0:T(256)S(1)} %broadcast_multiply_fusion.3, ...), kind=kOutput, calls=%fused_computation.24 | convolution fusion | flops 136118272 | bytes 2756608 | tf_op jit(solution)/shard_map/qcsd,fd->qcsf/dot_general | solution.py:15
  84.1 1.6 %fusion.32 = f32[1024,384]{0,1:T(8,128)S(1)} fusion(bf16[4,1024]{1,0:T(4,128)(2,1)S(1)} %get-tuple-element.61, bf16[256,1024]{1,0:T(8,128)(2,1)} %bitcast, s32[]{:T(128)S(6)} %select_n.310, bf16[256,768]{0,1:T(8,128)(2,1)S(1)} %bitcast.352, bf16[4,768]{0,1:T(8,128)(2,1)S(1)} %copy.101), kind=kOutput, calls=%fused_computation.69 | convolution fusion | flops 205936640 | bytes 2504708 | tf_op jit(solution)/shard_map/rd,rf->df/dot_general | solution.py:15
  85.7 5.0 %collective-permute-done.12 = bf16[103936]{0:T(1024)(128)(2,1)S(1)} collective-permute-done((bf16[103936]{0:T(1024)(128)(2,1)S(1)}, bf16[103936]{0:T(1024)(128)(2,1)S(1)}, u32[]{:S(2)}, u32[]{:S(2)}) %collective-permute-start.12) | collective-permute-done | bytes 207904 | tf_op jit(solution)/shard_map/ppermute | solution.py:365
  91.0 1.4 %fusion.162 = f32[384,1024]{1,0:T(8,128)S(1)} fusion(bf16[256,384]{1,0:T(8,128)(2,1)S(1)} %slice.165, bf16[256,1024]{1,0:T(8,128)(2,1)} %collective-permute-done.13), kind=kOutput, calls=%fused_computation.295 | convolution fusion | flops 201326592 | bytes 2293760 | tf_op jit(solution)/shard_map/rd,rf->df/dot_general | solution.py:15
  94.2 1.9 %collective-permute-start.14 = (bf16[256,384]{0,1:T(8,128)(2,1)S(1)}, bf16[256,384]{0,1:T(8,128)(2,1)S(1)}, u32[]{:S(2)}, u32[]{:S(2)}) collective-permute-start(bf16[256,384]{0,1:T(8,128)(2,1)S(1)} %get-tuple-element.50), channel_id=1, source_target_pairs={{0,4},{4,8},{8,12},{12,0},{1,5},{5,9},{9,13},{13,1},{2,6},{6,10},{... | collective-permute-start | bytes 589832 | tf_op jit(solution)/shard_map/ppermute | solution.py:89
  96.1 3.9 %collective-permute-done.16 = bf16[256,384]{0,1:T(8,128)(2,1)S(1)} collective-permute-done((bf16[256,384]{0,1:T(8,128)(2,1)S(1)}, bf16[256,384]{0,1:T(8,128)(2,1)S(1)}, u32[]{:S(2)}, u32[]{:S(2)}) %collective-permute-start.16) | collective-permute-done | bytes 196640 | tf_op jit(solution)/shard_map/ppermute | solution.py:89
  100.1 11.1 %collective-permute-done.15 = bf16[256,384]{0,1:T(8,128)(2,1)S(1)} collective-permute-done((bf16[256,384]{0,1:T(8,128)(2,1)S(1)}, bf16[256,384]{0,1:T(8,128)(2,1)S(1)}, u32[]{:S(2)}, u32[]{:S(2)}) %collective-permute-start.15) | collective-permute-done | bytes 196640 | tf_op jit(solution)/shard_map/ppermute | solution.py:89
  111.8 5.1 %collective-permute-done.17 = bf16[256,384]{0,1:T(8,128)(2,1)S(1)} collective-permute-done((bf16[256,384]{0,1:T(8,128)(2,1)S(1)}, bf16[256,384]{0,1:T(8,128)(2,1)S(1)}, u32[]{:S(2)}, u32[]{:S(2)}) %collective-permute-start.17) | collective-permute-done | bytes 196640 | tf_op jit(solution)/shard_map/ppermute | solution.py:376
  117.1 1.1 copy.103
  (269 shorter events, 38.2 us)
Async XLA Ops:
  1.4 11.4 %collective-permute-start.2 = (f32[1,1,1025]{2,1,0:T(1,128)S(1)}, f32[1,1,1025]{2,1,0:T(1,128)S(1)}, u32[]{:S(2)}, u32[]{:S(2)}) collective-permute-start(f32[1,1,1025]{2,1,0:T(1,128)S(1)} %pad_maximum_fusion.5), channel_id=1, source_target_pairs={{0,12},{4,0},{8,4},{12,8},{1,13},{5,1},{9,5},{13,9},{2,14},{6,2},{... | collective-permute-start | bytes 12308 | tf_op jit(solution)/shard_map/ppermute | solution.py:60
  6.5 6.3 %collective-permute-start.1 = (f32[1,1,1025]{2,1,0:T(1,128)S(1)}, f32[1,1,1025]{2,1,0:T(1,128)S(1)}, u32[]{:S(2)}, u32[]{:S(2)}) collective-permute-start(f32[1,1,1025]{2,1,0:T(1,128)S(1)} %pad_maximum_fusion.5), channel_id=1, source_target_pairs={{0,8},{4,12},{8,0},{12,4},{1,9},{5,13},{9,1},{13,5},{2,10},{6,14},... | collective-permute-start | bytes 12308 | tf_op jit(solution)/shard_map/ppermute | solution.py:60
  6.5 6.3 %collective-permute-start = (f32[1,1,1025]{2,1,0:T(1,128)S(1)}, f32[1,1,1025]{2,1,0:T(1,128)S(1)}, u32[]{:S(2)}, u32[]{:S(2)}) collective-permute-start(f32[1,1,1025]{2,1,0:T(1,128)S(1)} %pad_maximum_fusion.5), channel_id=1, source_target_pairs={{0,4},{4,8},{8,12},{12,0},{1,5},{5,9},{9,13},{13,1},{2,6},{6,10},{... | collective-permute-start | bytes 12308 | tf_op jit(solution)/shard_map/ppermute | solution.py:60
  7.5 15.7 %collective-permute-start.3 = (bf16[256,1024]{1,0:T(8,128)(2,1)}, bf16[256,1024]{1,0:T(8,128)(2,1)}, u32[]{:S(2)}, u32[]{:S(2)}) collective-permute-start(bf16[256,1024]{1,0:T(8,128)(2,1)} %param.14), channel_id=1, source_target_pairs={{0,1},{1,0},{2,3},{3,2},{4,5},{5,4},{6,7},{7,6},{8,9},{9,8},{10,11... | collective-permute-start | bytes 1572872 | tf_op jit(solution)/shard_map/ppermute | solution.py:97
  7.5 46.1 %collective-permute-start.7 = (bf16[256,1024]{1,0:T(8,128)(2,1)}, bf16[256,1024]{1,0:T(8,128)(2,1)}, u32[]{:S(2)}, u32[]{:S(2)}) collective-permute-start(bf16[256,1024]{1,0:T(8,128)(2,1)} %param.17), channel_id=1, source_target_pairs={{0,1},{1,0},{2,3},{3,2},{4,5},{5,4},{6,7},{7,6},{8,9},{9,8},{10,11... | collective-permute-start | bytes 1572872 | tf_op jit(solution)/shard_map/ppermute | solution.py:97
  8.0 5.4 %copy-start.24 = (pred[4]{0:T(512)(128)(4,1)}, pred[4]{0:T(512)(128)(4,1)S(1)}, u32[]{:S(2)}) copy-start(pred[4]{0:T(512)(128)(4,1)S(1)} %get-tuple-element.81) | copy-start | bytes 16
  8.1 17.1 %copy-start.8 = (pred[4]{0:T(512)(128)(4,1)}, pred[4]{0:T(512)(128)(4,1)S(1)}, u32[]{:S(2)}) copy-start(pred[4]{0:T(512)(128)(4,1)S(1)} %get-tuple-element.82) | copy-start | bytes 16
  8.1 4.8 %copy-start.23 = (s32[1024]{0:T(1024)}, s32[1024]{0:T(1024)S(1)}, u32[]{:S(2)}) copy-start(s32[1024]{0:T(1024)S(1)} %pad_clamp_fusion) | copy-start | bytes 12292
  8.1 5.4 %copy-start = (bf16[3,1024,256]{2,1,0:T(8,128)(2,1)S(1)}, bf16[3,1024,256]{2,1,0:T(8,128)(2,1)}, u32[]{:S(2)}) copy-start(bf16[3,1024,256]{2,1,0:T(8,128)(2,1)} %param.13) | copy-start | bytes 4718596
  10.4 6.3 %copy-start.5 = (bf16[1,1,1,256,256]{3,4,0,2,1:T(8,128)(2,1)}, bf16[1,1,1,256,256]{3,4,0,2,1:T(8,128)(2,1)S(1)}, u32[]{:S(2)}) copy-start(bf16[1,1,1,256,256]{3,4,0,2,1:T(8,128)(2,1)S(1)} %get-tuple-element.54) | copy-start | bytes 393220
  12.8 59.5 %collective-permute-start.11 = (bf16[3,1024,256]{2,1,0:T(8,128)(2,1)}, bf16[3,1024,256]{2,1,0:T(8,128)(2,1)}, u32[]{:S(2)}, u32[]{:S(2)}) collective-permute-start(bf16[3,1024,256]{2,1,0:T(8,128)(2,1)} %param.16), channel_id=1, source_target_pairs={{0,1},{1,0},{2,3},{3,2},{4,5},{5,4},{6,7},{7,6},{8,9},{9,8},{10,11... | collective-permute-start | bytes 4718600 | tf_op jit(solution)/shard_map/ppermute | solution.py:97
  16.4 6.8 %copy-start.4 = (bf16[256,1024]{1,0:T(8,128)(2,1)S(1)}, bf16[256,1024]{1,0:T(8,128)(2,1)}, u32[]{:S(2)}) copy-start(bf16[256,1024]{1,0:T(8,128)(2,1)} %param.14) | copy-start | bytes 1572868
  26.9 26.7 %copy-start.1 = (bf16[256,1024]{1,0:T(8,128)(2,1)S(1)}, bf16[256,1024]{1,0:T(8,128)(2,1)}, u32[]{:S(2)}) copy-start(bf16[256,1024]{1,0:T(8,128)(2,1)} %param.17) | copy-start | bytes 1572868
  31.6 7.1 %copy-start.2 = (bf16[1,1,1,256,256]{3,4,0,2,1:T(8,128)(2,1)}, bf16[1,1,1,256,256]{3,4,0,2,1:T(8,128)(2,1)S(1)}, u32[]{:S(2)}) copy-start(bf16[1,1,1,256,256]{3,4,0,2,1:T(8,128)(2,1)S(1)} %get-tuple-element.59) | copy-start | bytes 393220
  34.2 6.9 %collective-permute-start.6 = (bf16[1,1,768]{2,1,0:T(2,128)(2,1)}, bf16[1,1,768]{2,1,0:T(2,128)(2,1)}, u32[]{:S(2)}, u32[]{:S(2)}) collective-permute-start(bf16[1,1,768]{2,1,0:T(2,128)(2,1)} %constant_dynamic-update-slice_fusion), channel_id=1, source_target_pairs={{0,12},{4,0},{8,4},{12,8},{1,13},{5,1},{9,5},{13,9},{2,14},{6,2},{... | collective-permute-start | bytes 4616 | tf_op jit(solution)/shard_map/ppermute | solution.py:60
  37.0 5.7 %collective-permute-start.5 = (bf16[1,1,768]{2,1,0:T(2,128)(2,1)}, bf16[1,1,768]{2,1,0:T(2,128)(2,1)}, u32[]{:S(2)}, u32[]{:S(2)}) collective-permute-start(bf16[1,1,768]{2,1,0:T(2,128)(2,1)} %constant_dynamic-update-slice_fusion), channel_id=1, source_target_pairs={{0,8},{4,12},{8,0},{12,4},{1,9},{5,13},{9,1},{13,5},{2,10},{6,14},... | collective-permute-start | bytes 4616 | tf_op jit(solution)/shard_map/ppermute | solution.py:60
  38.1 5.7 %collective-permute-start.4 = (bf16[1,1,768]{2,1,0:T(2,128)(2,1)}, bf16[1,1,768]{2,1,0:T(2,128)(2,1)}, u32[]{:S(2)}, u32[]{:S(2)}) collective-permute-start(bf16[1,1,768]{2,1,0:T(2,128)(2,1)} %constant_dynamic-update-slice_fusion), channel_id=1, source_target_pairs={{0,4},{4,8},{8,12},{12,0},{1,5},{5,9},{9,13},{13,1},{2,6},{6,10},{... | collective-permute-start | bytes 4616 | tf_op jit(solution)/shard_map/ppermute | solution.py:60
  41.1 49.9 %collective-permute-start.13 = (bf16[256,1024]{1,0:T(8,128)(2,1)}, bf16[256,1024]{1,0:T(8,128)(2,1)}, u32[]{:S(2)}, u32[]{:S(2)}) collective-permute-start(bf16[256,1024]{1,0:T(8,128)(2,1)} %bitcast), channel_id=1, source_target_pairs={{0,2},{2,0},{1,3},{3,1},{4,6},{6,4},{5,7},{7,5},{8,10},{10,8},{9,1... | collective-permute-start | bytes 1572872 | tf_op jit(solution)/shard_map/ppermute | solution.py:149
  53.6 10.6 %copy-start.25 = (pred[4]{0:T(512)(128)(4,1)S(1)}, pred[4]{0:T(512)(128)(4,1)}, u32[]{:S(2)}) copy-start(pred[4]{0:T(512)(128)(4,1)} %copy-done.24) | copy-start | bytes 16
  53.6 11.0 %copy-start.11 = (f32[1024]{0:T(1024)S(1)}, f32[1024]{0:T(1024)}, u32[]{:S(2)}) copy-start(f32[1024]{0:T(1024)} %param.19) | copy-start | bytes 12292
  53.6 11.0 %copy-start.12 = (f32[1024]{0:T(1024)S(1)}, f32[1024]{0:T(1024)}, u32[]{:S(2)}) copy-start(f32[1024]{0:T(1024)} %param.18) | copy-start | bytes 12292
  53.6 11.9 %copy-start.32 = (f32[4]{0:T(128)S(1)}, f32[4]{0:T(128)}, u32[]{:S(2)}) copy-start(f32[4]{0:T(128)} %divide_reduce_fusion) | copy-start | bytes 52
  53.6 13.9 %copy-start.3 = (bf16[1,1,1,256,256]{3,4,0,2,1:T(8,128)(2,1)S(1)}, bf16[1,1,1,256,256]{3,4,0,2,1:T(8,128)(2,1)}, u32[]{:S(2)}) copy-start(bf16[1,1,1,256,256]{3,4,0,2,1:T(8,128)(2,1)} %copy-done.2) | copy-start | bytes 393220
  55.2 14.3 %copy-start.16 = (pred[256]{0:T(512)(128)(4,1)S(1)}, pred[256]{0:T(512)(128)(4,1)}, u32[]{:S(2)}) copy-start(pred[256]{0:T(512)(128)(4,1)} %copy-done.15) | copy-start | bytes 772
  55.3 4.1 %collective-permute-start.10 = (f32[1,1,1296]{2,1,0:T(1,128)S(1)}, f32[1,1,1296]{2,1,0:T(1,128)S(1)}, u32[]{:S(2)}, u32[]{:S(2)}) collective-permute-start(f32[1,1,1296]{2,1,0:T(1,128)S(1)} %pad_maximum_fusion.4), channel_id=1, source_target_pairs={{0,12},{4,0},{8,4},{12,8},{1,13},{5,1},{9,5},{13,9},{2,14},{6,2},{... | collective-permute-start | bytes 15560 | tf_op jit(solution)/shard_map/ppermute | solution.py:60
  58.0 4.5 %collective-permute-start.9 = (f32[1,1,1296]{2,1,0:T(1,128)S(1)}, f32[1,1,1296]{2,1,0:T(1,128)S(1)}, u32[]{:S(2)}, u32[]{:S(2)}) collective-permute-start(f32[1,1,1296]{2,1,0:T(1,128)S(1)} %pad_maximum_fusion.4), channel_id=1, source_target_pairs={{0,8},{4,12},{8,0},{12,4},{1,9},{5,13},{9,1},{13,5},{2,10},{6,14},... | collective-permute-start | bytes 15560 | tf_op jit(solution)/shard_map/ppermute | solution.py:60
  58.0 5.4 %collective-permute-start.8 = (f32[1,1,1296]{2,1,0:T(1,128)S(1)}, f32[1,1,1296]{2,1,0:T(1,128)S(1)}, u32[]{:S(2)}, u32[]{:S(2)}) collective-permute-start(f32[1,1,1296]{2,1,0:T(1,128)S(1)} %pad_maximum_fusion.4), channel_id=1, source_target_pairs={{0,4},{4,8},{8,12},{12,0},{1,5},{5,9},{9,13},{13,1},{2,6},{6,10},{... | collective-permute-start | bytes 15560 | tf_op jit(solution)/shard_map/ppermute | solution.py:60
  83.5 7.3 %collective-permute-start.12 = (bf16[103936]{0:T(1024)(128)(2,1)S(1)}, bf16[103936]{0:T(1024)(128)(2,1)S(1)}, u32[]{:S(2)}, u32[]{:S(2)}) collective-permute-start(bf16[103936]{0:T(1024)(128)(2,1)S(1)} %pad_maximum_fusion.2), channel_id=1, source_target_pairs={{0,2},{2,0},{1,3},{3,1},{4,6},{6,4},{5,7},{7,5},{8,10},{10,8},{9,1... | collective-permute-start | bytes 623624 | tf_op jit(solution)/shard_map/ppermute | solution.py:365
  92.9 7.1 %collective-permute-start.16 = (bf16[256,384]{0,1:T(8,128)(2,1)S(1)}, bf16[256,384]{0,1:T(8,128)(2,1)S(1)}, u32[]{:S(2)}, u32[]{:S(2)}) collective-permute-start(bf16[256,384]{0,1:T(8,128)(2,1)S(1)} %get-tuple-element.51), channel_id=1, source_target_pairs={{0,12},{4,0},{8,4},{12,8},{1,13},{5,1},{9,5},{13,9},{2,14},{6,2},{... | collective-permute-start | bytes 589832 | tf_op jit(solution)/shard_map/ppermute | solution.py:89
  93.5 17.6 %collective-permute-start.15 = (bf16[256,384]{0,1:T(8,128)(2,1)S(1)}, bf16[256,384]{0,1:T(8,128)(2,1)S(1)}, u32[]{:S(2)}, u32[]{:S(2)}) collective-permute-start(bf16[256,384]{0,1:T(8,128)(2,1)S(1)} %get-tuple-element.52), channel_id=1, source_target_pairs={{0,8},{4,12},{8,0},{12,4},{1,9},{5,13},{9,1},{13,5},{2,10},{6,14},... | collective-permute-start | bytes 589832 | tf_op jit(solution)/shard_map/ppermute | solution.py:89
  94.2 16.9 %collective-permute-start.14 = (bf16[256,384]{0,1:T(8,128)(2,1)S(1)}, bf16[256,384]{0,1:T(8,128)(2,1)S(1)}, u32[]{:S(2)}, u32[]{:S(2)}) collective-permute-start(bf16[256,384]{0,1:T(8,128)(2,1)S(1)} %get-tuple-element.50), channel_id=1, source_target_pairs={{0,4},{4,8},{8,12},{12,0},{1,5},{5,9},{9,13},{13,1},{2,6},{6,10},{... | collective-permute-start | bytes 589832 | tf_op jit(solution)/shard_map/ppermute | solution.py:89
  111.2 5.7 %collective-permute-start.17 = (bf16[256,384]{0,1:T(8,128)(2,1)S(1)}, bf16[256,384]{0,1:T(8,128)(2,1)S(1)}, u32[]{:S(2)}, u32[]{:S(2)}) collective-permute-start(bf16[256,384]{0,1:T(8,128)(2,1)S(1)} %add_convert_fusion), channel_id=1, source_target_pairs={{0,2},{2,0},{1,3},{3,1},{4,6},{6,4},{5,7},{7,5},{8,10},{10,8},{9,1... | collective-permute-start | bytes 589832 | tf_op jit(solution)/shard_map/ppermute | solution.py:376
  (21 other events, 36.0 us)

commit v10 on v7

--- a/solution.py
+++ b/solution.py
@@ -89,6 +89,10 @@
         moved = lax.ppermute(piece, "cand", [(j, (j + k) % count) for j in range(count)])
         total = total + moved.astype(total_type)
     return total
+
+
+def swap_core(block):
+    return lax.ppermute(block, "mp", [(0, 1), (1, 0)])
 
 
 def sum_query(block):
@@ -123,9 +127,9 @@
     cross_valid = local_ids[:, None] != jnp.arange(cand_count)[None, :]
     head_shape = (lists, local_cands, seq_len, local_heads, HEAD_DIM)
     cls_shape = (lists, cand_count, local_heads, HEAD_DIM)
-    out_first_full = lax.all_gather(w_out_first, "mp", axis=0, tiled=True)
-    last_full = lax.all_gather(w_last, "mp", axis=2, tiled=True)
-    out_last_full = lax.all_gather(w_out_last, "mp", axis=0, tiled=True)
+    other_out_first = swap_core(w_out_first)
+    other_last = swap_core(w_last)
+    other_out_last = swap_core(w_out_last)
     cls_and_teacher = gather_cand(
         jnp.concatenate([tokens[:, :, 0].astype(jnp.float32), teacher[..., None]], -1), 1
     )
@@ -158,9 +162,10 @@
         first_mask[None, None, :, None, None], attended + attended_cls[:, :, None], attended
     )
     first_mixed = attended.reshape(lists, local_cands, seq_len, local_width).astype(jnp.bfloat16)
-    first_joined = lax.all_gather(first_mixed, "mp", axis=3, tiled=True)
-    residual_first = tokens.astype(jnp.float32) + mixed(
-        "qcsf,fd->qcsd", first_joined, out_first_full
+    residual_first = (
+        tokens.astype(jnp.float32)
+        + mixed("qcsf,fd->qcsd", first_mixed, w_out_first)
+        + mixed("qcsf,fd->qcsd", swap_core(first_mixed), other_out_first)
     )
     normed_first, unit_first, inverse_first = norm_forward(residual_first, gain_first)
     hidden = normed_first.astype(jnp.bfloat16)
@@ -187,9 +192,10 @@
         "qchd,qdhe->qche", cross_last_weight, cls_vals_last
     )
     last_mixed = attended_last.reshape(lists, local_cands, local_width).astype(jnp.bfloat16)
-    last_joined = lax.all_gather(last_mixed, "mp", axis=2, tiled=True)
-    residual_last = hidden[:, :, 0].astype(jnp.float32) + mixed(
-        "qcf,fd->qcd", last_joined, out_last_full
+    residual_last = (
+        hidden[:, :, 0].astype(jnp.float32)
+        + mixed("qcf,fd->qcd", last_mixed, w_out_last)
+        + mixed("qcf,fd->qcd", swap_core(last_mixed), other_out_last)
     )
     normed_last, unit_last, inverse_last = norm_forward(residual_last, gain_last)
     scores = jnp.einsum("qcd,d->qc", normed_last, w_score, precision=lax.Precision.HIGHEST)
@@ -248,19 +254,19 @@
     val_grad = jnp.where(first_cols, own_val_grad + back_vals[:, :, None], own_val_grad).astype(
         jnp.bfloat16
     )
-    joined = lax.all_gather(
-        jnp.concatenate([key_grad, val_grad, grad_query_last[:, :, None]], 2),
-        "mp",
-        axis=3,
-        tiled=True,
-    )
-    key_joined = joined[:, :, :seq_len]
-    val_joined = joined[:, :, seq_len : 2 * seq_len]
-    query_joined = joined[:, :, 2 * seq_len]
-    summed_term = mixed("qcsf,df->qcsd", key_joined, last_full[1]) + mixed(
-        "qcsf,df->qcsd", val_joined, last_full[2]
-    )
-    query_term = mixed("qcf,df->qcd", query_joined, last_full[0])
+    other = swap_core(jnp.concatenate([key_grad, val_grad, grad_query_last[:, :, None]], 2))
+    other_key = other[:, :, :seq_len]
+    other_val = other[:, :, seq_len : 2 * seq_len]
+    other_query = other[:, :, 2 * seq_len]
+    summed_term = (
+        mixed("qcsf,df->qcsd", key_grad, w_last[1])
+        + mixed("qcsf,df->qcsd", val_grad, w_last[2])
+        + mixed("qcsf,df->qcsd", other_key, other_last[1])
+        + mixed("qcsf,df->qcsd", other_val, other_last[2])
+    )
+    query_term = mixed("qcf,df->qcd", grad_query_last, w_last[0]) + mixed(
+        "qcf,df->qcd", other_query, other_last[0]
+    )
     summed_term = jnp.where(first_cols, summed_term + query_term[:, :, None], summed_term)
     grad_hidden = jnp.where(first_cols, summed_term + grad_last[:, :, None], summed_term)
     grad_first = norm_backward(grad_hidden, unit_first, inverse_first, gain_first).astype(

time: 139 us -> 117 us (0.84)
  between operations: 22 us -> 8.72 us
  matrix products: 19.1 us -> 28.4 us
  other arithmetic: 18.3 us -> 10.5 us
  blocking collectives: 6.23 us -> 0 us
  local copies, waits for them, and re-layouts: 11.3 us -> 8.47 us
  starting transfers between devices: 30.4 us -> 29 us
    dot_general x32 -> x37, matrix products: 19.1 us -> 28.4 us  [mixed(): jnp.einsum(pattern, former, latter, preferred_element_type=jnp.float32)]
    all_gather x3 -> x0, blocking collectives: 6.23 us -> none  [the longest x1 2.46 us: local(): lax.all_gather(jnp.concatenate([key_grad, val_grad, grad_query_last[:, :,...]
    ppermute x6, waiting for transfers between devices: 14.9 us -> 16.9 us  [scatter_cand(): lax.ppermute(piece, 'cand', [(j, (j + k) % count) for j in range(count)])]
    unnamed x3 -> x0, waiting for transfers between devices: 1.42 us -> none
    unnamed x73 -> x45, local copies, waits for them, and re-layouts: 3.31 us -> 1.95 us
  transfers between devices with their start and end apart: 21 -> 24, of which waited for: 6 -> 9; matrix products, arithmetic and copies ran while one was open for 31% -> 37% of each run, Pallas kernels for 0% -> 0%
where the time goes in v10:
time: 117 us; the launch traced here: 115 us
  waiting for transfers between devices  30.3 us (26%)
  starting transfers between devices  29 us (25%)
  matrix products  28.4 us (24%)
  other arithmetic  10.5 us (9%)
  between operations  8.72 us (7%)
  local copies, waits for them, and re-layouts  8.47 us (7%)
    dot_general x37, matrix products, mixed(): jnp.einsum(pattern, former, latter, preferred_element_type=jnp.float32)  28.4 us
    ppermute x6, waiting for transfers between devices, scatter_cand(): lax.ppermute(piece, 'cand', [(j, (j + k) % count) for j in range(count)])  16.9 us
    ppermute x6, starting transfers between devices, scatter_cand(): lax.ppermute(piece, 'cand', [(j, (j + k) % count) for j in range(count)])  8.88 us
    ppermute x6, starting transfers between devices, gather_cand(): lax.ppermute(block, 'cand', [(j, (j + k) % count) for j in range(count)])  8.43 us
    ppermute x3, starting transfers between devices, sum_cand(): lax.ppermute(block, 'cand', [(j, (j + k) % count) for j in range(count)])  7.77 us
    ppermute x1, waiting for transfers between devices, local(): partner = lax.ppermute(reduced, 'query', swap)  5.96 us
    ppermute x1, waiting for transfers between devices, local(): lax.ppermute(jnp.concatenate([given_half.reshape(-1), cls_flat.reshape(-1...  5.4 us
  transfers between devices with their start and end apart: 24, of which 9 were waited for; matrix products, arithmetic and copies ran while one was open for 37% of the time, Pallas kernels for 0%

profile of v10, /device:TPU:8, one launch (start us, length us, event | category | flops | bytes accessed | tf_op | source)
XLA Modules:
  0.0 115.5 jit_solution(14811923183899318427)
XLA Ops:
  1.4 1.6 %collective-permute-start = (f32[1,1,1025]{2,1,0:T(1,128)S(1)}, f32[1,1,1025]{2,1,0:T(1,128)S(1)}, u32[]{:S(2)}, u32[]{:S(2)}) collective-permute-start(f32[1,1,1025]{2,1,0:T(1,128)S(1)} %pad_maximum_fusion.4), channel_id=1, source_target_pairs={{0,4},{4,8},{8,12},{12,0},{1,5},{5,9},{9,13},{13,1},{2,6},{6,10},{... | collective-permute-start | bytes 12308 | tf_op jit(solution)/shard_map/ppermute | solution.py:60
  4.1 1.9 %collective-permute-start.2 = (f32[1,1,1025]{2,1,0:T(1,128)S(1)}, f32[1,1,1025]{2,1,0:T(1,128)S(1)}, u32[]{:S(2)}, u32[]{:S(2)}) collective-permute-start(f32[1,1,1025]{2,1,0:T(1,128)S(1)} %pad_maximum_fusion.4), channel_id=1, source_target_pairs={{0,12},{4,0},{8,4},{12,8},{1,13},{5,1},{9,5},{13,9},{2,14},{6,2},{... | collective-permute-start | bytes 12308 | tf_op jit(solution)/shard_map/ppermute | solution.py:60
  6.6 2.1 %fusion.7 = bf16[3,1,1,256,256]{3,4,0,2,1:T(8,128)(2,1)S(1)} fusion(bf16[3,1024,256]{2,1,0:T(8,128)(2,1)} %param.13, bf16[1,1,256,1024]{3,2,1,0:T(8,128)(2,1)} %param.10), kind=kOutput, calls=%fused_computation.18 | convolution fusion | flops 402849792 | bytes 2490368 | tf_op jit(solution)/shard_map/qcsd,kdf->kqcsf/dot_general | solution.py:15
  16.1 1.4 %fusion.5 = f32[1,1,256,1024]{3,2,1,0:T(8,128)S(1)} fusion(bf16[256,256]{0,1:T(8,128)(2,1)S(1)} %bitcast.399, bf16[256,1024]{1,0:T(8,128)(2,1)S(1)} %copy-done.1, bf16[1,1,256,1024]{3,2,1,0:T(8,128)(2,1)} %param.10), kind=kOutput, calls=%fused_computation.15 | convolution fusion | flops 134742016 | bytes 2228224 | tf_op jit(solution)/shard_map/qcsf,fd->qcsd/dot_general | solution.py:15
  19.4 1.3 %exponential_reduce_fusion = f32[]{:T(128)} fusion(f32[1,4,1025]{2,1,0:T(4,128)S(1)} %bitcast_select_fusion, f32[]{:T(128)} %slice_reduce_fusion.2), kind=kLoop, calls=%fused_computation.208 | loop fusion | flops 7 | bytes 24 | tf_op jit(solution)/shard_map/reduce_sum | solution.py:205
  21.5 1.4 %fusion.147 = (f32[256]{0:T(256)S(1)}, f32[1,1,256,1024]{3,2,1,0:T(8,128)S(1)}) fusion(f32[1,1,256,1024]{3,2,1,0:T(8,128)S(1)} %fusion.5, bf16[256,1024]{1,0:T(8,128)(2,1)} %collective-permute-done.4, bf16[1,1,256,256]{2,3,1,0:T(8,128)(2,1)S(1)} %collective-permute-done.3), kind=kOutput, calls=%fused_computation.266 | convolution fusion | flops 134741760 | bytes 2753536 | tf_op jit(solution)/shard_map/qcsf,fd->qcsd/dot_general | solution.py:15
  23.5 1.7 %fusion.8 = bf16[2,1,1,256,256]{4,3,0,2,1:T(8,128)(2,1)S(1)} fusion(bf16[3,1024,256]{2,1,0:T(8,128)(2,1)} %param.16, bf16[1,1,256,1024]{3,2,1,0:T(8,128)(2,1)S(1)} %multiply_convert_fusion.1), kind=kOutput, calls=%fused_computation.23 | convolution fusion | flops 268566528 | bytes 1835008 | tf_op jit(solution)/shard_map/qcsd,kdf->kqcsf/dot_general | solution.py:15
  25.4 3.6 %collective-permute-start.6 = (bf16[1,1,512]{2,1,0:T(2,128)(2,1)S(1)}, bf16[1,1,512]{2,1,0:T(2,128)(2,1)S(1)}, u32[]{:S(2)}, u32[]{:S(2)}) collective-permute-start(bf16[1,1,512]{2,1,0:T(2,128)(2,1)S(1)} %pad_maximum_fusion.5), channel_id=1, source_target_pairs={{0,8},{4,12},{8,0},{12,4},{1,9},{5,13},{9,1},{13,5},{2,10},{6,14},... | collective-permute-start | bytes 3080 | tf_op jit(solution)/shard_map/ppermute | solution.py:60
  29.0 1.2 %fusion.33 = f32[1,256]{1,0:T(1,128)S(1)} fusion(bf16[3,1024,256]{2,1,0:T(8,128)(2,1)} %param.16, bf16[1,1,256,1024]{3,2,1,0:T(8,128)(2,1)S(1)} %multiply_convert_fusion.1), kind=kOutput, calls=%fused_computation.65 | convolution fusion | flops 524288 | bytes 529408 | tf_op jit(solution)/shard_map/qcd,df->qcf/dot_general | solution.py:15
  30.9 1.6 %collective-permute-start.19 = (bf16[256,1024]{1,0:T(8,128)(2,1)}, bf16[256,1024]{1,0:T(8,128)(2,1)}, u32[]{:S(2)}, u32[]{:S(2)}) collective-permute-start(bf16[256,1024]{1,0:T(8,128)(2,1)} %bitcast), channel_id=1, source_target_pairs={{0,2},{2,0},{1,3},{3,1},{4,6},{6,4},{5,7},{7,5},{8,10},{10,8},{9,1... | collective-permute-start | bytes 1572872 | tf_op jit(solution)/shard_map/ppermute | solution.py:142
  35.9 1.2 %fusion.118 = f32[1,1024]{1,0:T(1,128)S(1)} fusion(bf16[256,1024]{1,0:T(8,128)(2,1)} %collective-permute-done.9, bf16[1,1,256]{2,1,0:T(2,128)(2,1)S(1)} %collective-permute-done.8), kind=kOutput, calls=%fused_computation.228 | convolution fusion | flops 524288 | bytes 528896 | tf_op jit(solution)/shard_map/qcf,fd->qcd/dot_general | solution.py:15
  40.8 3.3 %collective-permute-start.10 = (f32[1]{0:T(128)}, f32[1]{0:T(128)}, u32[]{:S(2)}, u32[]{:S(2)}) collective-permute-start(f32[1]{0:T(128)} %bitcast.75), channel_id=1, source_target_pairs={{0,4},{4,8},{8,12},{12,0},{1,5},{5,9},{9,13},{13,1},{2,6},{6,10},{... | collective-permute-start | bytes 20 | tf_op jit(solution)/shard_map/ppermute | solution.py:75
  44.1 3.1 %collective-permute-start.11 = (f32[1]{0:T(128)}, f32[1]{0:T(128)}, u32[]{:S(2)}, u32[]{:S(2)}) collective-permute-start(f32[1]{0:T(128)} %bitcast.75), channel_id=1, source_target_pairs={{0,8},{4,12},{8,0},{12,4},{1,9},{5,13},{9,1},{13,5},{2,10},{6,14},... | collective-permute-start | bytes 20 | tf_op jit(solution)/shard_map/ppermute | solution.py:75
  47.2 1.4 %collective-permute-start.12 = (f32[1]{0:T(128)}, f32[1]{0:T(128)}, u32[]{:S(2)}, u32[]{:S(2)}) collective-permute-start(f32[1]{0:T(128)} %bitcast.75), channel_id=1, source_target_pairs={{0,12},{4,0},{8,4},{12,8},{1,13},{5,1},{9,5},{13,9},{2,14},{6,2},{... | collective-permute-start | bytes 20 | tf_op jit(solution)/shard_map/ppermute | solution.py:75
  55.8 2.9 %collective-permute-start.14 = (f32[1,1,512]{2,1,0:T(1,128)S(1)}, f32[1,1,512]{2,1,0:T(1,128)S(1)}, u32[]{:S(2)}, u32[]{:S(2)}) collective-permute-start(f32[1,1,512]{2,1,0:T(1,128)S(1)} %get-tuple-element.38), channel_id=1, source_target_pairs={{0,8},{4,12},{8,0},{12,4},{1,9},{5,13},{9,1},{13,5},{2,10},{6,14},... | collective-permute-start | bytes 6152 | tf_op jit(solution)/shard_map/ppermute | solution.py:89
  58.7 1.1 collective-permute-start.15
  60.4 1.3 %fusion.31 = f32[1,1024]{1,0:T(1,128)S(1)} fusion(bf16[256,1]{0,1:T(2,128)(2,1)S(1)} %reshape.1372, bf16[3,1024,256]{2,1,0:T(8,128)(2,1)} %param.16), kind=kOutput, calls=%fused_computation.63 | convolution fusion | flops 524288 | bytes 528896 | tf_op jit(solution)/shard_map/qcf,df->qcd/dot_general | solution.py:15
  62.6 1.5 %fusion.29 = f32[256,1024]{1,0:T(8,128)S(1)} fusion(bf16[3,1024,256]{2,1,0:T(8,128)(2,1)} %param.16, f32[1,1,256,1,1,1,1,256]{2,7,6,5,4,3,1,0:T(8,128)S(1)} %bitcast.382, f32[256]{0:T(256)S(1)} %bitcast.414, pred[256]{0:T(512)(128)(4,1)S(1)} %iota_compare_fusion.1), kind=kOutput, calls=%fused_computation.61 | convolution fusion | flops 134414336 | bytes 1836288 | tf_op jit(solution)/shard_map/qcsf,df->qcsd/dot_general | solution.py:15
  64.0 1.5 %convolution_add_fusion.1 = f32[256,1024]{1,0:T(8,128)S(1)} fusion(f32[256,1024]{1,0:T(8,128)S(1)} %fusion.29, bf16[3,1024,256]{2,1,0:T(8,128)(2,1)} %param.16, f32[1,1,256,1,1,1,1,256]{2,7,6,5,4,3,1,0:T(8,128)S(1)} %bitcast.380, f32[256]{0:T(256)S(1)} %bitcast.412, pred[256]{0:T(512)(128)(4,1)S(1)} %iota_compare_fusion.1), kind=kOutput, calls=%fused_computation.10 | convolution fusion | flops 134676480 | bytes 2884864 | tf_op jit(solution)/shard_map/qcsf,df->qcsd/dot_general | solution.py:15
  65.7 1.3 %fusion.24 = f32[1,1024]{1,0:T(1,128)S(1)} fusion(bf16[256,1]{0,1:T(2,128)(2,1)S(1)} %reshape.1374, bf16[3,1024,256]{2,1,0:T(8,128)(2,1)} %collective-permute-done.17), kind=kOutput, calls=%fused_computation.54 | convolution fusion | flops 524288 | bytes 528896 | tf_op jit(solution)/shard_map/qcf,df->qcd/dot_general | solution.py:15
  66.9 1.4 %fusion.25 = f32[256,1024]{1,0:T(8,128)S(1)} fusion(bf16[3,1024,256]{2,1,0:T(8,128)(2,1)} %collective-permute-done.17, bf16[1,1,513,256]{2,3,1,0:T(8,128)(2,1)S(1)} %collective-permute-done.16), kind=kOutput, calls=%fused_computation.56 | convolution fusion | flops 134217728 | bytes 1703936 | tf_op jit(solution)/shard_map/qcsf,df->qcsd/dot_general | solution.py:15
  68.4 1.8 %fusion.11 = (f32[256]{0:T(256)S(1)}, f32[256,1024]{1,0:T(8,128)S(1)}) fusion(f32[1,1,256,1024]{3,2,1,0:T(8,128)S(1)} %get-tuple-element.50, f32[256]{0:T(256)S(1)} %add_rsqrt_fusion, f32[256]{0:T(256)S(1)} %broadcast_multiply_fusion.3, f32[1024]{0:T(1024)S(1)} %copy-done.8, f32[1024]{0:T(1024)S(1)} %get-tuple-element.20, f32[1024]{0:T(1024)S(1)} %add.353, ...), kind=kOutput, calls=%fused_computation.30 | convolution fusion | flops 137101056 | bytes 4865536 | tf_op jit(solution)/shard_map/qcsf,df->qcsd/dot_general | solution.py:15
  70.4 1.6 %convolution_convert_fusion.3 = bf16[256,256]{0,1:T(8,128)(2,1)S(1)} fusion(bf16[256,1024]{1,0:T(8,128)(2,1)} %param.14, f32[1,1,256,1024]{3,2,1,0:T(8,128)S(1)} %get-tuple-element.50, f32[256,1024]{1,0:T(8,128)S(1)} %get-tuple-element.52, f32[256]{0:T(256)S(1)} %broadcast_multiply_fusion.1, f32[256]{0:T(256)S(1)} %broadcast_multiply_fusion.2, ...), kind=kOutput, calls=%fused_computation.26 | convolution fusion | flops 136118272 | bytes 2756608 | tf_op jit(solution)/shard_map/qcsd,fd->qcsf/dot_general | solution.py:15
  73.1 1.3 %multiply_reduce_fusion = (f32[4,256]{1,0:T(4,128)S(1)}, f32[4,256,256]{1,2,0:T(8,128)S(1)}) fusion(f32[4,256]{1,0:T(4,128)} %copy-done.10, f32[4,256,256]{1,2,0:T(8,128)S(1)} %get-tuple-element.48, f32[4,256]{1,0:T(4,128)S(1)} %broadcast_select_fusion.2, bf16[256,4,64]{0,2,1:T(8,128)(2,1)S(1)} %bitcast.396, bf16[256,4,64]{0,2,1:T(8,128)(2,1)} %bitcast.401), kind=kOutput, calls=%fused_computation.35 | convolution fusion | flops 34601984 | bytes 2371584 | tf_op jit(solution)/shard_map/qcshe,qcthe->qchst/dot_general | solution.py:15
  78.0 1.6 %fusion.18 = f32[1024,384]{0,1:T(8,128)S(1)} fusion(bf16[4,1024]{1,0:T(4,128)(2,1)S(1)} %get-tuple-element.35, bf16[256,1024]{1,0:T(8,128)(2,1)} %bitcast, s32[]{:T(128)S(6)} %select_n.271, bf16[256,768]{0,1:T(8,128)(2,1)S(1)} %bitcast.378, bf16[4,768]{0,1:T(8,128)(2,1)S(1)} %copy.83), kind=kOutput, calls=%fused_computation.48 | convolution fusion | flops 205936640 | bytes 2504708 | tf_op jit(solution)/shard_map/rd,rf->df/dot_general | solution.py:15
  79.6 5.4 %collective-permute-done.18 = bf16[103936]{0:T(1024)(128)(2,1)S(1)} collective-permute-done((bf16[103936]{0:T(1024)(128)(2,1)S(1)}, bf16[103936]{0:T(1024)(128)(2,1)S(1)}, u32[]{:S(2)}, u32[]{:S(2)}) %collective-permute-start.18) | collective-permute-done | bytes 207904 | tf_op jit(solution)/shard_map/ppermute | solution.py:334
  85.2 1.4 %fusion.152 = f32[384,1024]{1,0:T(8,128)S(1)} fusion(bf16[256,384]{1,0:T(8,128)(2,1)S(1)} %slice.168, bf16[256,1024]{1,0:T(8,128)(2,1)} %collective-permute-done.19), kind=kOutput, calls=%fused_computation.271 | convolution fusion | flops 201326592 | bytes 2293760 | tf_op jit(solution)/shard_map/rd,rf->df/dot_general | solution.py:15
  87.8 2.8 %collective-permute-start.21 = (bf16[256,384]{0,1:T(8,128)(2,1)S(1)}, bf16[256,384]{0,1:T(8,128)(2,1)S(1)}, u32[]{:S(2)}, u32[]{:S(2)}) collective-permute-start(bf16[256,384]{0,1:T(8,128)(2,1)S(1)} %get-tuple-element.26), channel_id=1, source_target_pairs={{0,8},{4,12},{8,0},{12,4},{1,9},{5,13},{9,1},{13,5},{2,10},{6,14},... | collective-permute-start | bytes 589832 | tf_op jit(solution)/shard_map/ppermute | solution.py:89
  91.0 10.4 %collective-permute-done.20 = bf16[256,384]{0,1:T(8,128)(2,1)S(1)} collective-permute-done((bf16[256,384]{0,1:T(8,128)(2,1)S(1)}, bf16[256,384]{0,1:T(8,128)(2,1)S(1)}, u32[]{:S(2)}, u32[]{:S(2)}) %collective-permute-start.20) | collective-permute-done | bytes 196640 | tf_op jit(solution)/shard_map/ppermute | solution.py:89
  101.4 3.1 %collective-permute-done.21 = bf16[256,384]{0,1:T(8,128)(2,1)S(1)} collective-permute-done((bf16[256,384]{0,1:T(8,128)(2,1)S(1)}, bf16[256,384]{0,1:T(8,128)(2,1)S(1)}, u32[]{:S(2)}, u32[]{:S(2)}) %collective-permute-start.21) | collective-permute-done | bytes 196640 | tf_op jit(solution)/shard_map/ppermute | solution.py:89
  104.5 3.1 %collective-permute-done.22 = bf16[256,384]{0,1:T(8,128)(2,1)S(1)} collective-permute-done((bf16[256,384]{0,1:T(8,128)(2,1)S(1)}, bf16[256,384]{0,1:T(8,128)(2,1)S(1)}, u32[]{:S(2)}, u32[]{:S(2)}) %collective-permute-start.22) | collective-permute-done | bytes 196640 | tf_op jit(solution)/shard_map/ppermute | solution.py:89
  108.3 6.0 %collective-permute-done.23 = bf16[256,384]{0,1:T(8,128)(2,1)S(1)} collective-permute-done((bf16[256,384]{0,1:T(8,128)(2,1)S(1)}, bf16[256,384]{0,1:T(8,128)(2,1)S(1)}, u32[]{:S(2)}, u32[]{:S(2)}) %collective-permute-start.23) | collective-permute-done | bytes 196640 | tf_op jit(solution)/shard_map/ppermute | solution.py:345
  (237 shorter events, 30.4 us)
Async XLA Ops:
  1.4 10.0 %collective-permute-start = (f32[1,1,1025]{2,1,0:T(1,128)S(1)}, f32[1,1,1025]{2,1,0:T(1,128)S(1)}, u32[]{:S(2)}, u32[]{:S(2)}) collective-permute-start(f32[1,1,1025]{2,1,0:T(1,128)S(1)} %pad_maximum_fusion.4), channel_id=1, source_target_pairs={{0,4},{4,8},{8,12},{12,0},{1,5},{5,9},{9,13},{13,1},{2,6},{6,10},{... | collective-permute-start | bytes 12308 | tf_op jit(solution)/shard_map/ppermute | solution.py:60
  3.0 8.4 %collective-permute-start.1 = (f32[1,1,1025]{2,1,0:T(1,128)S(1)}, f32[1,1,1025]{2,1,0:T(1,128)S(1)}, u32[]{:S(2)}, u32[]{:S(2)}) collective-permute-start(f32[1,1,1025]{2,1,0:T(1,128)S(1)} %pad_maximum_fusion.4), channel_id=1, source_target_pairs={{0,8},{4,12},{8,0},{12,4},{1,9},{5,13},{9,1},{13,5},{2,10},{6,14},... | collective-permute-start | bytes 12308 | tf_op jit(solution)/shard_map/ppermute | solution.py:60
  4.1 7.3 %collective-permute-start.2 = (f32[1,1,1025]{2,1,0:T(1,128)S(1)}, f32[1,1,1025]{2,1,0:T(1,128)S(1)}, u32[]{:S(2)}, u32[]{:S(2)}) collective-permute-start(f32[1,1,1025]{2,1,0:T(1,128)S(1)} %pad_maximum_fusion.4), channel_id=1, source_target_pairs={{0,12},{4,0},{8,4},{12,8},{1,13},{5,1},{9,5},{13,9},{2,14},{6,2},{... | collective-permute-start | bytes 12308 | tf_op jit(solution)/shard_map/ppermute | solution.py:60
  6.1 15.4 %collective-permute-start.4 = (bf16[256,1024]{1,0:T(8,128)(2,1)}, bf16[256,1024]{1,0:T(8,128)(2,1)}, u32[]{:S(2)}, u32[]{:S(2)}) collective-permute-start(bf16[256,1024]{1,0:T(8,128)(2,1)} %param.14), channel_id=1, source_target_pairs={{0,1},{1,0},{2,3},{3,2},{4,5},{5,4},{6,7},{7,6},{8,9},{9,8},{10,11... | collective-permute-start | bytes 1572872 | tf_op jit(solution)/shard_map/ppermute | solution.py:95
  6.1 28.9 %collective-permute-start.9 = (bf16[256,1024]{1,0:T(8,128)(2,1)}, bf16[256,1024]{1,0:T(8,128)(2,1)}, u32[]{:S(2)}, u32[]{:S(2)}) collective-permute-start(bf16[256,1024]{1,0:T(8,128)(2,1)} %param.17), channel_id=1, source_target_pairs={{0,1},{1,0},{2,3},{3,2},{4,5},{5,4},{6,7},{7,6},{8,9},{9,8},{10,11... | collective-permute-start | bytes 1572872 | tf_op jit(solution)/shard_map/ppermute | solution.py:95
  8.8 3.3 %copy-start.2 = (bf16[3,1024,256]{2,1,0:T(8,128)(2,1)S(1)}, bf16[3,1024,256]{2,1,0:T(8,128)(2,1)}, u32[]{:S(2)}) copy-start(bf16[3,1024,256]{2,1,0:T(8,128)(2,1)} %param.13) | copy-start | bytes 4718596
  8.8 8.6 %copy-start.3 = (bf16[1,1,1,256,256]{3,4,0,2,1:T(8,128)(2,1)}, bf16[1,1,1,256,256]{3,4,0,2,1:T(8,128)(2,1)S(1)}, u32[]{:S(2)}) copy-start(bf16[1,1,1,256,256]{3,4,0,2,1:T(8,128)(2,1)S(1)} %get-tuple-element.28) | copy-start | bytes 393220
  10.7 57.6 %copy-start.5 = (pred[256]{0:T(512)(128)(4,1)}, pred[256]{0:T(512)(128)(4,1)S(1)}, u32[]{:S(2)}) copy-start(pred[256]{0:T(512)(128)(4,1)S(1)} %iota_compare_fusion.1) | copy-start | bytes 772
  11.4 54.3 %collective-permute-start.17 = (bf16[3,1024,256]{2,1,0:T(8,128)(2,1)}, bf16[3,1024,256]{2,1,0:T(8,128)(2,1)}, u32[]{:S(2)}, u32[]{:S(2)}) collective-permute-start(bf16[3,1024,256]{2,1,0:T(8,128)(2,1)} %param.16), channel_id=1, source_target_pairs={{0,1},{1,0},{2,3},{3,2},{4,5},{5,4},{6,7},{7,6},{8,9},{9,8},{10,11... | collective-permute-start | bytes 4718600 | tf_op jit(solution)/shard_map/ppermute | solution.py:95
  15.4 6.1 %collective-permute-start.3 = (bf16[1,1,256,256]{2,3,1,0:T(8,128)(2,1)S(1)}, bf16[1,1,256,256]{2,3,1,0:T(8,128)(2,1)S(1)}, u32[]{:S(2)}, u32[]{:S(2)}) collective-permute-start(bf16[1,1,256,256]{2,3,1,0:T(8,128)(2,1)S(1)} %bitcast.398), channel_id=1, source_target_pairs={{0,1},{1,0},{2,3},{3,2},{4,5},{5,4},{6,7},{7,6},{8,9},{9,8},{10,11... | collective-permute-start | bytes 393224 | tf_op jit(solution)/shard_map/ppermute | solution.py:95
  22.9 45.4 %copy-start.7 = (f32[256]{0:T(256)}, f32[256]{0:T(256)S(1)}, u32[]{:S(2)}) copy-start(f32[256]{0:T(256)S(1)} %broadcast_multiply_fusion.3) | copy-start | bytes 3076
  23.2 45.2 %copy-start.9 = (f32[256]{0:T(256)}, f32[256]{0:T(256)S(1)}, u32[]{:S(2)}) copy-start(f32[256]{0:T(256)S(1)} %add_rsqrt_fusion) | copy-start | bytes 3076
  25.1 9.7 %copy-start = (bf16[256,1024]{1,0:T(8,128)(2,1)S(1)}, bf16[256,1024]{1,0:T(8,128)(2,1)}, u32[]{:S(2)}) copy-start(bf16[256,1024]{1,0:T(8,128)(2,1)} %param.17) | copy-start | bytes 1572868
  25.1 14.5 %copy-start.12 = (f32[1024]{0:T(1024)S(1)}, f32[1024]{0:T(1024)}, u32[]{:S(2)}) copy-start(f32[1024]{0:T(1024)} %param.18) | copy-start | bytes 12292
  25.2 14.5 %copy-start.13 = (f32[1024]{0:T(1024)S(1)}, f32[1024]{0:T(1024)}, u32[]{:S(2)}) copy-start(f32[1024]{0:T(1024)} %param.19) | copy-start | bytes 12292
  25.2 5.7 %collective-permute-start.5 = (bf16[1,1,512]{2,1,0:T(2,128)(2,1)S(1)}, bf16[1,1,512]{2,1,0:T(2,128)(2,1)S(1)}, u32[]{:S(2)}, u32[]{:S(2)}) collective-permute-start(bf16[1,1,512]{2,1,0:T(2,128)(2,1)S(1)} %pad_maximum_fusion.5), channel_id=1, source_target_pairs={{0,4},{4,8},{8,12},{12,0},{1,5},{5,9},{9,13},{13,1},{2,6},{6,10},{... | collective-permute-start | bytes 3080 | tf_op jit(solution)/shard_map/ppermute | solution.py:60
  25.4 7.1 %collective-permute-start.6 = (bf16[1,1,512]{2,1,0:T(2,128)(2,1)S(1)}, bf16[1,1,512]{2,1,0:T(2,128)(2,1)S(1)}, u32[]{:S(2)}, u32[]{:S(2)}) collective-permute-start(bf16[1,1,512]{2,1,0:T(2,128)(2,1)S(1)} %pad_maximum_fusion.5), channel_id=1, source_target_pairs={{0,8},{4,12},{8,0},{12,4},{1,9},{5,13},{9,1},{13,5},{2,10},{6,14},... | collective-permute-start | bytes 3080 | tf_op jit(solution)/shard_map/ppermute | solution.py:60
  29.0 3.6 %collective-permute-start.7 = (bf16[1,1,512]{2,1,0:T(2,128)(2,1)S(1)}, bf16[1,1,512]{2,1,0:T(2,128)(2,1)S(1)}, u32[]{:S(2)}, u32[]{:S(2)}) collective-permute-start(bf16[1,1,512]{2,1,0:T(2,128)(2,1)S(1)} %pad_maximum_fusion.5), channel_id=1, source_target_pairs={{0,12},{4,0},{8,4},{12,8},{1,13},{5,1},{9,5},{13,9},{2,14},{6,2},{... | collective-permute-start | bytes 3080 | tf_op jit(solution)/shard_map/ppermute | solution.py:60
  30.9 54.3 %collective-permute-start.19 = (bf16[256,1024]{1,0:T(8,128)(2,1)}, bf16[256,1024]{1,0:T(8,128)(2,1)}, u32[]{:S(2)}, u32[]{:S(2)}) collective-permute-start(bf16[256,1024]{1,0:T(8,128)(2,1)} %bitcast), channel_id=1, source_target_pairs={{0,2},{2,0},{1,3},{3,1},{4,6},{6,4},{5,7},{7,5},{8,10},{10,8},{9,1... | collective-permute-start | bytes 1572872 | tf_op jit(solution)/shard_map/ppermute | solution.py:142
  34.8 1.2 %collective-permute-start.8 = (bf16[1,1,256]{2,1,0:T(2,128)(2,1)S(1)}, bf16[1,1,256]{2,1,0:T(2,128)(2,1)S(1)}, u32[]{:S(2)}, u32[]{:S(2)}) collective-permute-start(bf16[1,1,256]{2,1,0:T(2,128)(2,1)S(1)} %convert_element_type.310), channel_id=1, source_target_pairs={{0,1},{1,0},{2,3},{3,2},{4,5},{5,4},{6,7},{7,6},{8,9},{9,8},{10,11... | collective-permute-start | bytes 1544 | tf_op jit(solution)/shard_map/ppermute | solution.py:95
  40.8 7.8 %collective-permute-start.10 = (f32[1]{0:T(128)}, f32[1]{0:T(128)}, u32[]{:S(2)}, u32[]{:S(2)}) collective-permute-start(f32[1]{0:T(128)} %bitcast.75), channel_id=1, source_target_pairs={{0,4},{4,8},{8,12},{12,0},{1,5},{5,9},{9,13},{13,1},{2,6},{6,10},{... | collective-permute-start | bytes 20 | tf_op jit(solution)/shard_map/ppermute | solution.py:75
  44.1 5.1 %collective-permute-start.11 = (f32[1]{0:T(128)}, f32[1]{0:T(128)}, u32[]{:S(2)}, u32[]{:S(2)}) collective-permute-start(f32[1]{0:T(128)} %bitcast.75), channel_id=1, source_target_pairs={{0,8},{4,12},{8,0},{12,4},{1,9},{5,13},{9,1},{13,5},{2,10},{6,14},... | collective-permute-start | bytes 20 | tf_op jit(solution)/shard_map/ppermute | solution.py:75
  47.2 3.6 %collective-permute-start.12 = (f32[1]{0:T(128)}, f32[1]{0:T(128)}, u32[]{:S(2)}, u32[]{:S(2)}) collective-permute-start(f32[1]{0:T(128)} %bitcast.75), channel_id=1, source_target_pairs={{0,12},{4,0},{8,4},{12,8},{1,13},{5,1},{9,5},{13,9},{2,14},{6,2},{... | collective-permute-start | bytes 20 | tf_op jit(solution)/shard_map/ppermute | solution.py:75
  54.8 7.2 %collective-permute-start.13 = (f32[1,1,512]{2,1,0:T(1,128)S(1)}, f32[1,1,512]{2,1,0:T(1,128)S(1)}, u32[]{:S(2)}, u32[]{:S(2)}) collective-permute-start(f32[1,1,512]{2,1,0:T(1,128)S(1)} %get-tuple-element.36), channel_id=1, source_target_pairs={{0,4},{4,8},{8,12},{12,0},{1,5},{5,9},{9,13},{13,1},{2,6},{6,10},{... | collective-permute-start | bytes 6152 | tf_op jit(solution)/shard_map/ppermute | solution.py:89
  55.8 6.2 %collective-permute-start.14 = (f32[1,1,512]{2,1,0:T(1,128)S(1)}, f32[1,1,512]{2,1,0:T(1,128)S(1)}, u32[]{:S(2)}, u32[]{:S(2)}) collective-permute-start(f32[1,1,512]{2,1,0:T(1,128)S(1)} %get-tuple-element.38), channel_id=1, source_target_pairs={{0,8},{4,12},{8,0},{12,4},{1,9},{5,13},{9,1},{13,5},{2,10},{6,14},... | collective-permute-start | bytes 6152 | tf_op jit(solution)/shard_map/ppermute | solution.py:89
  58.7 3.6 %collective-permute-start.15 = (f32[1,1,512]{2,1,0:T(1,128)S(1)}, f32[1,1,512]{2,1,0:T(1,128)S(1)}, u32[]{:S(2)}, u32[]{:S(2)}) collective-permute-start(f32[1,1,512]{2,1,0:T(1,128)S(1)} %get-tuple-element.37), channel_id=1, source_target_pairs={{0,12},{4,0},{8,4},{12,8},{1,13},{5,1},{9,5},{13,9},{2,14},{6,2},{... | collective-permute-start | bytes 6152 | tf_op jit(solution)/shard_map/ppermute | solution.py:89
  62.5 3.0 %collective-permute-start.16 = (bf16[1,1,513,256]{2,3,1,0:T(8,128)(2,1)S(1)}, bf16[1,1,513,256]{2,3,1,0:T(8,128)(2,1)S(1)}, u32[]{:S(2)}, u32[]{:S(2)}) collective-permute-start(bf16[1,1,513,256]{2,3,1,0:T(8,128)(2,1)S(1)} %pad_maximum_fusion.1), channel_id=1, source_target_pairs={{0,1},{1,0},{2,3},{3,2},{4,5},{5,4},{6,7},{7,6},{8,9},{9,8},{10,11... | collective-permute-start | bytes 787976 | tf_op jit(solution)/shard_map/ppermute | solution.py:95
  77.4 7.6 %collective-permute-start.18 = (bf16[103936]{0:T(1024)(128)(2,1)S(1)}, bf16[103936]{0:T(1024)(128)(2,1)S(1)}, u32[]{:S(2)}, u32[]{:S(2)}) collective-permute-start(bf16[103936]{0:T(1024)(128)(2,1)S(1)} %pad_maximum_fusion.2), channel_id=1, source_target_pairs={{0,2},{2,0},{1,3},{3,1},{4,6},{6,4},{5,7},{7,5},{8,10},{10,8},{9,1... | collective-permute-start | bytes 623624 | tf_op jit(solution)/shard_map/ppermute | solution.py:334
  87.1 14.3 %collective-permute-start.20 = (bf16[256,384]{0,1:T(8,128)(2,1)S(1)}, bf16[256,384]{0,1:T(8,128)(2,1)S(1)}, u32[]{:S(2)}, u32[]{:S(2)}) collective-permute-start(bf16[256,384]{0,1:T(8,128)(2,1)S(1)} %get-tuple-element.24), channel_id=1, source_target_pairs={{0,4},{4,8},{8,12},{12,0},{1,5},{5,9},{9,13},{13,1},{2,6},{6,10},{... | collective-permute-start | bytes 589832 | tf_op jit(solution)/shard_map/ppermute | solution.py:89
  87.8 16.7 %collective-permute-start.21 = (bf16[256,384]{0,1:T(8,128)(2,1)S(1)}, bf16[256,384]{0,1:T(8,128)(2,1)S(1)}, u32[]{:S(2)}, u32[]{:S(2)}) collective-permute-start(bf16[256,384]{0,1:T(8,128)(2,1)S(1)} %get-tuple-element.26), channel_id=1, source_target_pairs={{0,8},{4,12},{8,0},{12,4},{1,9},{5,13},{9,1},{13,5},{2,10},{6,14},... | collective-permute-start | bytes 589832 | tf_op jit(solution)/shard_map/ppermute | solution.py:89
  90.7 16.9 %collective-permute-start.22 = (bf16[256,384]{0,1:T(8,128)(2,1)S(1)}, bf16[256,384]{0,1:T(8,128)(2,1)S(1)}, u32[]{:S(2)}, u32[]{:S(2)}) collective-permute-start(bf16[256,384]{0,1:T(8,128)(2,1)S(1)} %get-tuple-element.25), channel_id=1, source_target_pairs={{0,12},{4,0},{8,4},{12,8},{1,13},{5,1},{9,5},{13,9},{2,14},{6,2},{... | collective-permute-start | bytes 589832 | tf_op jit(solution)/shard_map/ppermute | solution.py:89
  107.7 6.6 %collective-permute-start.23 = (bf16[256,384]{0,1:T(8,128)(2,1)S(1)}, bf16[256,384]{0,1:T(8,128)(2,1)S(1)}, u32[]{:S(2)}, u32[]{:S(2)}) collective-permute-start(bf16[256,384]{0,1:T(8,128)(2,1)S(1)} %add_convert_fusion), channel_id=1, source_target_pairs={{0,2},{2,0},{1,3},{3,1},{4,6},{6,4},{5,7},{7,5},{8,10},{10,8},{9,1... | collective-permute-start | bytes 589832 | tf_op jit(solution)/shard_map/ppermute | solution.py:345
  (12 other events, 13.0 us)

commit v11 on v10

--- a/solution.py
+++ b/solution.py
@@ -130,9 +130,11 @@
     other_out_first = swap_core(w_out_first)
     other_last = swap_core(w_last)
     other_out_last = swap_core(w_out_last)
-    cls_and_teacher = gather_cand(
-        jnp.concatenate([tokens[:, :, 0].astype(jnp.float32), teacher[..., None]], -1), 1
-    )
+    projected = mixed("qcsd,kdf->kqcsf", tokens, w_first).astype(jnp.bfloat16)
+    cls_rows, projected = lax.optimization_barrier(
+        (jnp.concatenate([tokens[:, :, 0].astype(jnp.float32), teacher[..., None]], -1), projected)
+    )
+    cls_and_teacher = gather_cand(cls_rows, 1)
     cls_tokens = cls_and_teacher[..., :model_width].astype(jnp.bfloat16)
     teacher_all = cls_and_teacher[..., model_width]
     row_count = lists * local_cands * seq_len
@@ -140,7 +142,6 @@
     paired_lists = lax.axis_size("query") == 2
     if paired_lists:
         other_tokens = lax.ppermute(tokens.reshape(row_count, model_width), "query", swap)
-    projected = mixed("qcsd,kdf->kqcsf", tokens, w_first).astype(jnp.bfloat16)
     cls_projected = mixed("qcd,kdf->kqcf", cls_tokens, w_first[1:]).astype(jnp.bfloat16)
     gathered_keys = cls_projected[0]
     gathered_vals = cls_projected[1]

time: 117 us -> 127 us (1.085)
  other arithmetic: 10.5 us -> 18 us
  local copies, waits for them, and re-layouts: 8.47 us -> 11.1 us
    another operation x4 -> x3, other arithmetic: 0.06 us -> 1.42 us  [gather_cand(): jnp.stack(parts, 0)]
  transfers between devices with their start and end apart: 24 -> 24, of which waited for: 9 -> 8; matrix products, arithmetic and copies ran while one was open for 37% -> 40% of each run, Pallas kernels for 0% -> 0%
where the time goes in v11:
time: 127 us; the launch traced here: 126 us
  waiting for transfers between devices  30.5 us (24%)
  starting transfers between devices  29 us (23%)
  matrix products  28.6 us (23%)
  other arithmetic  18 us (14%)
  local copies, waits for them, and re-layouts  11.1 us (9%)
  between operations  8.81 us (7%)
    dot_general x37, matrix products, mixed(): jnp.einsum(pattern, former, latter, preferred_element_type=jnp.float32)  28.6 us
    ppermute x6, waiting for transfers between devices, scatter_cand(): lax.ppermute(piece, 'cand', [(j, (j + k) % count) for j in range(count)])  17.1 us
    ppermute x6, starting transfers between devices, scatter_cand(): lax.ppermute(piece, 'cand', [(j, (j + k) % count) for j in range(count)])  8.88 us
    ppermute x6, starting transfers between devices, gather_cand(): lax.ppermute(block, 'cand', [(j, (j + k) % count) for j in range(count)])  8.52 us
    ppermute x3, starting transfers between devices, sum_cand(): lax.ppermute(block, 'cand', [(j, (j + k) % count) for j in range(count)])  7.63 us
    ppermute x1, waiting for transfers between devices, local(): partner = lax.ppermute(reduced, 'query', swap)  6.18 us
    ppermute x1, waiting for transfers between devices, local(): lax.ppermute(jnp.concatenate([given_half.reshape(-1), cls_flat.reshape(-1...  5.4 us
    another operation x10, other arithmetic  2.72 us
  transfers between devices with their start and end apart: 24, of which 8 were waited for; matrix products, arithmetic and copies ran while one was open for 40% of the time, Pallas kernels for 0%

profile of v11, /device:TPU:8, one launch (start us, length us, event | category | flops | bytes accessed | tf_op | source)
XLA Modules:
  0.0 126.0 jit_solution(5369869232773384553)
XLA Ops:
  1.5 2.1 %fusion.7 = bf16[3,1,1,256,256]{3,4,0,2,1:T(8,128)(2,1)S(1)} fusion(bf16[3,1024,256]{2,1,0:T(8,128)(2,1)} %param.13, bf16[1,1,256,1024]{3,2,1,0:T(8,128)(2,1)} %param.10), kind=kOutput, calls=%fused_computation.18 | convolution fusion | flops 402849792 | bytes 2490368 | tf_op jit(solution)/shard_map/qcsd,kdf->kqcsf/dot_general | solution.py:15
  3.6 1.6 %collective-permute-start = (f32[1,1,1025]{2,1,0:T(1,128)S(1)}, f32[1,1,1025]{2,1,0:T(1,128)S(1)}, u32[]{:S(2)}, u32[]{:S(2)}) collective-permute-start(f32[1,1,1025]{2,1,0:T(1,128)S(1)} %pad_maximum_fusion.4), channel_id=1, source_target_pairs={{0,4},{4,8},{8,12},{12,0},{1,5},{5,9},{9,13},{13,1},{2,6},{6,10},{... | collective-permute-start | bytes 12308 | tf_op jit(solution)/shard_map/ppermute | solution.py:60
  6.3 1.9 %collective-permute-start.2 = (f32[1,1,1025]{2,1,0:T(1,128)S(1)}, f32[1,1,1025]{2,1,0:T(1,128)S(1)}, u32[]{:S(2)}, u32[]{:S(2)}) collective-permute-start(f32[1,1,1025]{2,1,0:T(1,128)S(1)} %pad_maximum_fusion.4), channel_id=1, source_target_pairs={{0,12},{4,0},{8,4},{12,8},{1,13},{5,1},{9,5},{13,9},{2,14},{6,2},{... | collective-permute-start | bytes 12308 | tf_op jit(solution)/shard_map/ppermute | solution.py:60
  12.0 1.5 %fusion.10 = bf16[2,1,4,256]{3,2,0,1:T(4,128)(2,1)S(1)} fusion(bf16[3,1024,256]{2,1,0:T(8,128)(2,1)} %param.13, f32[1,4,1025]{2,1,0:T(4,128)S(1)} %bitcast_select_fusion), kind=kOutput, calls=%fused_computation.28 | convolution fusion | flops 4196352 | bytes 1060864 | tf_op jit(solution)/shard_map/qcd,kdf->kqcf/dot_general | solution.py:15
  17.3 1.4 %fusion.5 = f32[1,1,256,1024]{3,2,1,0:T(8,128)S(1)} fusion(bf16[256,256]{0,1:T(8,128)(2,1)S(1)} %bitcast.397, bf16[256,1024]{1,0:T(8,128)(2,1)S(1)} %copy-done.1, bf16[1,1,256,1024]{3,2,1,0:T(8,128)(2,1)} %param.10), kind=kOutput, calls=%fused_computation.15 | convolution fusion | flops 134742016 | bytes 2228224 | tf_op jit(solution)/shard_map/qcsf,fd->qcsd/dot_general | solution.py:15
  20.5 1.2 exponential_reduce_fusion
  23.7 1.7 %fusion.8 = bf16[2,1,1,256,256]{4,3,0,2,1:T(8,128)(2,1)S(1)} fusion(bf16[3,1024,256]{2,1,0:T(8,128)(2,1)} %param.16, bf16[1,1,256,1024]{3,2,1,0:T(8,128)(2,1)S(1)} %multiply_convert_fusion.1), kind=kOutput, calls=%fused_computation.23 | convolution fusion | flops 268566528 | bytes 1835008 | tf_op jit(solution)/shard_map/qcsd,kdf->kqcsf/dot_general | solution.py:15
  26.7 3.6 %collective-permute-start.6 = (bf16[1,1,512]{2,1,0:T(2,128)(2,1)}, bf16[1,1,512]{2,1,0:T(2,128)(2,1)}, u32[]{:S(2)}, u32[]{:S(2)}) collective-permute-start(bf16[1,1,512]{2,1,0:T(2,128)(2,1)} %pad_maximum_fusion.5), channel_id=1, source_target_pairs={{0,8},{4,12},{8,0},{12,4},{1,9},{5,13},{9,1},{13,5},{2,10},{6,14},... | collective-permute-start | bytes 3080 | tf_op jit(solution)/shard_map/ppermute | solution.py:60
  35.2 1.6 %collective-permute-start.19 = (bf16[256,1024]{1,0:T(8,128)(2,1)}, bf16[256,1024]{1,0:T(8,128)(2,1)}, u32[]{:S(2)}, u32[]{:S(2)}) collective-permute-start(bf16[256,1024]{1,0:T(8,128)(2,1)} %bitcast), channel_id=1, source_target_pairs={{0,2},{2,0},{1,3},{3,1},{4,6},{6,4},{5,7},{7,5},{8,10},{10,8},{9,1... | collective-permute-start | bytes 1572872 | tf_op jit(solution)/shard_map/ppermute | solution.py:144
  44.6 1.2 fusion.118
  48.3 1.3 %multiply_reduce_fusion.2 = f32[]{:T(128)} fusion(f32[1024]{0:T(1024)} %param.19, f32[1024]{0:T(1024)} %param.18, f32[1024]{0:T(1024)S(1)} %get-tuple-element.27, f32[]{:T(128)S(6)} %rsqrt.13, f32[]{:T(128)S(6)} %div.79), kind=kLoop, calls=%fused_computation.138 | loop fusion | flops 5119 | bytes 12300 | tf_op jit(solution)/shard_map/qcd,d->qc/dot_general | solution.py:202
  50.4 3.2 %collective-permute-start.10 = (f32[1]{0:T(128)}, f32[1]{0:T(128)}, u32[]{:S(2)}, u32[]{:S(2)}) collective-permute-start(f32[1]{0:T(128)} %bitcast.74), channel_id=1, source_target_pairs={{0,4},{4,8},{8,12},{12,0},{1,5},{5,9},{9,13},{13,1},{2,6},{6,10},{... | collective-permute-start | bytes 20 | tf_op jit(solution)/shard_map/ppermute | solution.py:75
  53.6 3.1 %collective-permute-start.11 = (f32[1]{0:T(128)}, f32[1]{0:T(128)}, u32[]{:S(2)}, u32[]{:S(2)}) collective-permute-start(f32[1]{0:T(128)} %bitcast.74), channel_id=1, source_target_pairs={{0,8},{4,12},{8,0},{12,4},{1,9},{5,13},{9,1},{13,5},{2,10},{6,14},... | collective-permute-start | bytes 20 | tf_op jit(solution)/shard_map/ppermute | solution.py:75
  56.7 1.3 %collective-permute-start.12 = (f32[1]{0:T(128)}, f32[1]{0:T(128)}, u32[]{:S(2)}, u32[]{:S(2)}) collective-permute-start(f32[1]{0:T(128)} %bitcast.74), channel_id=1, source_target_pairs={{0,12},{4,0},{8,4},{12,8},{1,13},{5,1},{9,5},{13,9},{2,14},{6,2},{... | collective-permute-start | bytes 20 | tf_op jit(solution)/shard_map/ppermute | solution.py:75
  60.9 1.3 %fusion.129 = (f32[]{:T(128)}, f32[]{:T(128)}, f32[1024]{0:T(1024)S(1)}) fusion(f32[]{:T(128)S(6)} %rsqrt.13, f32[1024]{0:T(1024)S(1)} %get-tuple-element.27, f32[]{:T(128)S(6)} %div.79, f32[1024]{0:T(1024)} %param.18, f32[1024]{0:T(1024)} %param.19, f32[]{:T(128)} %bitcast.78), kind=kLoop, calls=%fused_computation.254 | loop fusion | flops 7166 | bytes 16404 | tf_op jit(solution)/shard_map/reduce_sum | solution.py:29
  66.0 2.9 %collective-permute-start.14 = (f32[1,1,512]{2,1,0:T(1,128)S(1)}, f32[1,1,512]{2,1,0:T(1,128)S(1)}, u32[]{:S(2)}, u32[]{:S(2)}) collective-permute-start(f32[1,1,512]{2,1,0:T(1,128)S(1)} %get-tuple-element.42), channel_id=1, source_target_pairs={{0,8},{4,12},{8,0},{12,4},{1,9},{5,13},{9,1},{13,5},{2,10},{6,14},... | collective-permute-start | bytes 6152 | tf_op jit(solution)/shard_map/ppermute | solution.py:89
  70.4 1.3 %fusion.31 = f32[1,1024]{1,0:T(1,128)S(1)} fusion(bf16[256,1]{0,1:T(2,128)(2,1)S(1)} %reshape.1372, bf16[3,1024,256]{2,1,0:T(8,128)(2,1)} %param.16), kind=kOutput, calls=%fused_computation.63 | convolution fusion | flops 524288 | bytes 528896 | tf_op jit(solution)/shard_map/qcf,df->qcd/dot_general | solution.py:15
  72.8 1.5 %fusion.29 = f32[256,1024]{1,0:T(8,128)S(1)} fusion(bf16[3,1024,256]{2,1,0:T(8,128)(2,1)} %param.16, f32[1,1,256,1,1,1,1,256]{2,7,6,5,4,3,1,0:T(8,128)S(1)} %bitcast.380, f32[256]{0:T(256)S(1)} %bitcast.413, pred[256]{0:T(512)(128)(4,1)S(1)} %copy-done.5), kind=kOutput, calls=%fused_computation.61 | convolution fusion | flops 134414336 | bytes 1836288 | tf_op jit(solution)/shard_map/qcsf,df->qcsd/dot_general | solution.py:15
  74.3 1.5 %convolution_add_fusion.1 = f32[256,1024]{1,0:T(8,128)S(1)} fusion(f32[256,1024]{1,0:T(8,128)S(1)} %fusion.29, bf16[3,1024,256]{2,1,0:T(8,128)(2,1)} %param.16, f32[1,1,256,1,1,1,1,256]{2,7,6,5,4,3,1,0:T(8,128)S(1)} %bitcast.378, f32[256]{0:T(256)S(1)} %bitcast.411, pred[256]{0:T(512)(128)(4,1)S(1)} %copy-done.5), kind=kOutput, calls=%fused_computation.10 | convolution fusion | flops 134676480 | bytes 2884864 | tf_op jit(solution)/shard_map/qcsf,df->qcsd/dot_general | solution.py:15
  76.0 1.3 %fusion.24 = f32[1,1024]{1,0:T(1,128)S(1)} fusion(bf16[256,1]{0,1:T(2,128)(2,1)S(1)} %reshape.1374, bf16[3,1024,256]{2,1,0:T(8,128)(2,1)} %collective-permute-done.17), kind=kOutput, calls=%fused_computation.54 | convolution fusion | flops 524288 | bytes 528896 | tf_op jit(solution)/shard_map/qcf,df->qcd/dot_general | solution.py:15
  77.3 1.4 %fusion.25 = f32[256,1024]{1,0:T(8,128)S(1)} fusion(bf16[3,1024,256]{2,1,0:T(8,128)(2,1)} %collective-permute-done.17, bf16[1,1,513,256]{2,3,1,0:T(8,128)(2,1)S(1)} %collective-permute-done.16), kind=kOutput, calls=%fused_computation.56 | convolution fusion | flops 134217728 | bytes 1703936 | tf_op jit(solution)/shard_map/qcsf,df->qcsd/dot_general | solution.py:15
  78.7 1.8 %fusion.11 = (f32[256]{0:T(256)S(1)}, f32[256,1024]{1,0:T(8,128)S(1)}) fusion(f32[1,1,256,1024]{3,2,1,0:T(8,128)S(1)} %get-tuple-element.54, f32[256]{0:T(256)S(1)} %copy-done.13, f32[256]{0:T(256)S(1)} %copy-done.8, f32[1024]{0:T(1024)S(1)} %copy-done.11, f32[1024]{0:T(1024)S(1)} %get-tuple-element.24, f32[1024]{0:T(1024)S(1)} %add.353, ...), kind=kOutput, calls=%fused_computation.30 | convolution fusion | flops 137101056 | bytes 4865536 | tf_op jit(solution)/shard_map/qcsf,df->qcsd/dot_general | solution.py:15
  80.7 1.6 %convolution_convert_fusion.3 = bf16[256,256]{0,1:T(8,128)(2,1)S(1)} fusion(bf16[256,1024]{1,0:T(8,128)(2,1)} %param.14, f32[1,1,256,1024]{3,2,1,0:T(8,128)S(1)} %get-tuple-element.54, f32[256,1024]{1,0:T(8,128)S(1)} %get-tuple-element.56, f32[256]{0:T(256)S(1)} %broadcast_multiply_fusion.1, f32[256]{0:T(256)S(1)} %broadcast_multiply_fusion.2, ...), kind=kOutput, calls=%fused_computation.26 | convolution fusion | flops 136118272 | bytes 2756608 | tf_op jit(solution)/shard_map/qcsd,fd->qcsf/dot_general | solution.py:15
  83.5 1.3 %multiply_reduce_fusion = (f32[4,256]{1,0:T(4,128)S(1)}, f32[4,256,256]{1,2,0:T(8,128)S(1)}) fusion(f32[4,256]{1,0:T(4,128)} %copy-done.14, f32[4,256,256]{1,2,0:T(8,128)S(1)} %get-tuple-element.52, f32[4,256]{1,0:T(4,128)S(1)} %broadcast_select_fusion.2, bf16[256,4,64]{0,2,1:T(8,128)(2,1)S(1)} %bitcast.394, bf16[256,4,64]{0,2,1:T(8,128)(2,1)} %bitcast.399), kind=kOutput, calls=%fused_computation.35 | convolution fusion | flops 34601984 | bytes 2371584 | tf_op jit(solution)/shard_map/qcshe,qcthe->qchst/dot_general | solution.py:15
  88.3 1.6 %fusion.18 = f32[1024,384]{0,1:T(8,128)S(1)} fusion(bf16[4,1024]{1,0:T(4,128)(2,1)S(1)} %get-tuple-element.39, bf16[256,1024]{1,0:T(8,128)(2,1)} %bitcast, s32[]{:T(128)S(6)} %select_n.271, bf16[256,768]{0,1:T(8,128)(2,1)S(1)} %bitcast.376, bf16[4,768]{0,1:T(8,128)(2,1)S(1)} %copy.83), kind=kOutput, calls=%fused_computation.48 | convolution fusion | flops 205936640 | bytes 2504708 | tf_op jit(solution)/shard_map/rd,rf->df/dot_general | solution.py:15
  89.9 5.4 %collective-permute-done.18 = bf16[103936]{0:T(1024)(128)(2,1)S(1)} collective-permute-done((bf16[103936]{0:T(1024)(128)(2,1)S(1)}, bf16[103936]{0:T(1024)(128)(2,1)S(1)}, u32[]{:S(2)}, u32[]{:S(2)}) %collective-permute-start.18) | collective-permute-done | bytes 207904 | tf_op jit(solution)/shard_map/ppermute | solution.py:335
  95.5 1.4 %fusion.152 = f32[384,1024]{1,0:T(8,128)S(1)} fusion(bf16[256,384]{1,0:T(8,128)(2,1)S(1)} %slice.168, bf16[256,1024]{1,0:T(8,128)(2,1)} %collective-permute-done.19), kind=kOutput, calls=%fused_computation.271 | convolution fusion | flops 201326592 | bytes 2293760 | tf_op jit(solution)/shard_map/rd,rf->df/dot_general | solution.py:15
  98.1 2.6 %collective-permute-start.21 = (bf16[256,384]{0,1:T(8,128)(2,1)S(1)}, bf16[256,384]{0,1:T(8,128)(2,1)S(1)}, u32[]{:S(2)}, u32[]{:S(2)}) collective-permute-start(bf16[256,384]{0,1:T(8,128)(2,1)S(1)} %get-tuple-element.30), channel_id=1, source_target_pairs={{0,8},{4,12},{8,0},{12,4},{1,9},{5,13},{9,1},{13,5},{2,10},{6,14},... | collective-permute-start | bytes 589832 | tf_op jit(solution)/shard_map/ppermute | solution.py:89
  101.3 10.4 %collective-permute-done.20 = bf16[256,384]{0,1:T(8,128)(2,1)S(1)} collective-permute-done((bf16[256,384]{0,1:T(8,128)(2,1)S(1)}, bf16[256,384]{0,1:T(8,128)(2,1)S(1)}, u32[]{:S(2)}, u32[]{:S(2)}) %collective-permute-start.20) | collective-permute-done | bytes 196640 | tf_op jit(solution)/shard_map/ppermute | solution.py:89
  111.8 3.1 %collective-permute-done.21 = bf16[256,384]{0,1:T(8,128)(2,1)S(1)} collective-permute-done((bf16[256,384]{0,1:T(8,128)(2,1)S(1)}, bf16[256,384]{0,1:T(8,128)(2,1)S(1)}, u32[]{:S(2)}, u32[]{:S(2)}) %collective-permute-start.21) | collective-permute-done | bytes 196640 | tf_op jit(solution)/shard_map/ppermute | solution.py:89
  114.8 3.1 %collective-permute-done.22 = bf16[256,384]{0,1:T(8,128)(2,1)S(1)} collective-permute-done((bf16[256,384]{0,1:T(8,128)(2,1)S(1)}, bf16[256,384]{0,1:T(8,128)(2,1)S(1)}, u32[]{:S(2)}, u32[]{:S(2)}) %collective-permute-start.22) | collective-permute-done | bytes 196640 | tf_op jit(solution)/shard_map/ppermute | solution.py:89
  118.6 6.2 %collective-permute-done.23 = bf16[256,384]{0,1:T(8,128)(2,1)S(1)} collective-permute-done((bf16[256,384]{0,1:T(8,128)(2,1)S(1)}, bf16[256,384]{0,1:T(8,128)(2,1)S(1)}, u32[]{:S(2)}, u32[]{:S(2)}) %collective-permute-start.23) | collective-permute-done | bytes 196640 | tf_op jit(solution)/shard_map/ppermute | solution.py:346
  (252 shorter events, 40.7 us)
Async XLA Ops:
  0.0 8.3 %copy-start.1 = (bf16[256,1024]{1,0:T(8,128)(2,1)S(1)}, bf16[256,1024]{1,0:T(8,128)(2,1)}, u32[]{:S(2)}) copy-start(bf16[256,1024]{1,0:T(8,128)(2,1)} %param.14) | copy-start | bytes 1572868
  0.0 8.3 %copy-start = (bf16[256,1024]{1,0:T(8,128)(2,1)S(1)}, bf16[256,1024]{1,0:T(8,128)(2,1)}, u32[]{:S(2)}) copy-start(bf16[256,1024]{1,0:T(8,128)(2,1)} %param.17) | copy-start | bytes 1572868
  3.6 7.6 %collective-permute-start = (f32[1,1,1025]{2,1,0:T(1,128)S(1)}, f32[1,1,1025]{2,1,0:T(1,128)S(1)}, u32[]{:S(2)}, u32[]{:S(2)}) collective-permute-start(f32[1,1,1025]{2,1,0:T(1,128)S(1)} %pad_maximum_fusion.4), channel_id=1, source_target_pairs={{0,4},{4,8},{8,12},{12,0},{1,5},{5,9},{9,13},{13,1},{2,6},{6,10},{... | collective-permute-start | bytes 12308 | tf_op jit(solution)/shard_map/ppermute | solution.py:60
  5.2 6.1 %collective-permute-start.1 = (f32[1,1,1025]{2,1,0:T(1,128)S(1)}, f32[1,1,1025]{2,1,0:T(1,128)S(1)}, u32[]{:S(2)}, u32[]{:S(2)}) collective-permute-start(f32[1,1,1025]{2,1,0:T(1,128)S(1)} %pad_maximum_fusion.4), channel_id=1, source_target_pairs={{0,8},{4,12},{8,0},{12,4},{1,9},{5,13},{9,1},{13,5},{2,10},{6,14},... | collective-permute-start | bytes 12308 | tf_op jit(solution)/shard_map/ppermute | solution.py:60
  6.3 5.0 %collective-permute-start.2 = (f32[1,1,1025]{2,1,0:T(1,128)S(1)}, f32[1,1,1025]{2,1,0:T(1,128)S(1)}, u32[]{:S(2)}, u32[]{:S(2)}) collective-permute-start(f32[1,1,1025]{2,1,0:T(1,128)S(1)} %pad_maximum_fusion.4), channel_id=1, source_target_pairs={{0,12},{4,0},{8,4},{12,8},{1,13},{5,1},{9,5},{13,9},{2,14},{6,2},{... | collective-permute-start | bytes 12308 | tf_op jit(solution)/shard_map/ppermute | solution.py:60
  8.3 14.2 %collective-permute-start.4 = (bf16[256,1024]{1,0:T(8,128)(2,1)S(1)}, bf16[256,1024]{1,0:T(8,128)(2,1)S(1)}, u32[]{:S(2)}, u32[]{:S(2)}) collective-permute-start(bf16[256,1024]{1,0:T(8,128)(2,1)S(1)} %copy-done.1), channel_id=1, source_target_pairs={{0,1},{1,0},{2,3},{3,2},{4,5},{5,4},{6,7},{7,6},{8,9},{9,8},{10,11... | collective-permute-start | bytes 1572872 | tf_op jit(solution)/shard_map/ppermute | solution.py:95
  8.3 35.3 %collective-permute-start.9 = (bf16[256,1024]{1,0:T(8,128)(2,1)S(1)}, bf16[256,1024]{1,0:T(8,128)(2,1)}, u32[]{:S(2)}, u32[]{:S(2)}) collective-permute-start(bf16[256,1024]{1,0:T(8,128)(2,1)S(1)} %copy-done), channel_id=1, source_target_pairs={{0,1},{1,0},{2,3},{3,2},{4,5},{5,4},{6,7},{7,6},{8,9},{9,8},{10,11... | collective-permute-start | bytes 1572872 | tf_op jit(solution)/shard_map/ppermute | solution.py:95
  8.8 6.1 %copy-start.9 = (pred[4]{0:T(512)(128)(4,1)}, pred[4]{0:T(512)(128)(4,1)S(1)}, u32[]{:S(2)}) copy-start(pred[4]{0:T(512)(128)(4,1)S(1)} %get-tuple-element.60) | copy-start | bytes 16
  8.9 7.1 %copy-start.2 = (bf16[1,1,1,256,256]{3,4,0,2,1:T(8,128)(2,1)}, bf16[1,1,1,256,256]{3,4,0,2,1:T(8,128)(2,1)S(1)}, u32[]{:S(2)}) copy-start(bf16[1,1,1,256,256]{3,4,0,2,1:T(8,128)(2,1)S(1)} %get-tuple-element.32) | copy-start | bytes 393220
  11.3 64.7 %collective-permute-start.17 = (bf16[3,1024,256]{2,1,0:T(8,128)(2,1)}, bf16[3,1024,256]{2,1,0:T(8,128)(2,1)}, u32[]{:S(2)}, u32[]{:S(2)}) collective-permute-start(bf16[3,1024,256]{2,1,0:T(8,128)(2,1)} %param.16), channel_id=1, source_target_pairs={{0,1},{1,0},{2,3},{3,2},{4,5},{5,4},{6,7},{7,6},{8,9},{9,8},{10,11... | collective-permute-start | bytes 4718600 | tf_op jit(solution)/shard_map/ppermute | solution.py:95
  16.8 5.7 %collective-permute-start.3 = (bf16[1,1,256,256]{2,3,1,0:T(8,128)(2,1)S(1)}, bf16[1,1,256,256]{2,3,1,0:T(8,128)(2,1)S(1)}, u32[]{:S(2)}, u32[]{:S(2)}) collective-permute-start(bf16[1,1,256,256]{2,3,1,0:T(8,128)(2,1)S(1)} %bitcast.396), channel_id=1, source_target_pairs={{0,1},{1,0},{2,3},{3,2},{4,5},{5,4},{6,7},{7,6},{8,9},{9,8},{10,11... | collective-permute-start | bytes 393224 | tf_op jit(solution)/shard_map/ppermute | solution.py:95
  26.1 6.3 %copy-start.16 = (bf16[1,1,256]{2,1,0:T(2,128)(2,1)}, bf16[1,1,256]{2,1,0:T(2,128)(2,1)S(1)}, u32[]{:S(2)}) copy-start(bf16[1,1,256]{2,1,0:T(2,128)(2,1)S(1)} %slice_bitcast_fusion.10) | copy-start | bytes 1540
  26.1 6.3 %copy-start.17 = (bf16[1,1,256]{2,1,0:T(2,128)(2,1)}, bf16[1,1,256]{2,1,0:T(2,128)(2,1)S(1)}, u32[]{:S(2)}) copy-start(bf16[1,1,256]{2,1,0:T(2,128)(2,1)S(1)} %slice_bitcast_fusion.11) | copy-start | bytes 1540
  26.7 8.5 %collective-permute-start.5 = (bf16[1,1,512]{2,1,0:T(2,128)(2,1)}, bf16[1,1,512]{2,1,0:T(2,128)(2,1)}, u32[]{:S(2)}, u32[]{:S(2)}) collective-permute-start(bf16[1,1,512]{2,1,0:T(2,128)(2,1)} %pad_maximum_fusion.5), channel_id=1, source_target_pairs={{0,4},{4,8},{8,12},{12,0},{1,5},{5,9},{9,13},{13,1},{2,6},{6,10},{... | collective-permute-start | bytes 3080 | tf_op jit(solution)/shard_map/ppermute | solution.py:60
  26.7 10.0 %collective-permute-start.6 = (bf16[1,1,512]{2,1,0:T(2,128)(2,1)}, bf16[1,1,512]{2,1,0:T(2,128)(2,1)}, u32[]{:S(2)}, u32[]{:S(2)}) collective-permute-start(bf16[1,1,512]{2,1,0:T(2,128)(2,1)} %pad_maximum_fusion.5), channel_id=1, source_target_pairs={{0,8},{4,12},{8,0},{12,4},{1,9},{5,13},{9,1},{13,5},{2,10},{6,14},... | collective-permute-start | bytes 3080 | tf_op jit(solution)/shard_map/ppermute | solution.py:60
  30.4 6.4 %collective-permute-start.7 = (bf16[1,1,512]{2,1,0:T(2,128)(2,1)}, bf16[1,1,512]{2,1,0:T(2,128)(2,1)}, u32[]{:S(2)}, u32[]{:S(2)}) collective-permute-start(bf16[1,1,512]{2,1,0:T(2,128)(2,1)} %pad_maximum_fusion.5), channel_id=1, source_target_pairs={{0,12},{4,0},{8,4},{12,8},{1,13},{5,1},{9,5},{13,9},{2,14},{6,2},{... | collective-permute-start | bytes 3080 | tf_op jit(solution)/shard_map/ppermute | solution.py:60
  32.4 13.4 %copy-start.21 = (bf16[1024]{0:T(1024)(128)(2,1)S(1)}, bf16[1024]{0:T(1024)(128)(2,1)}, u32[]{:S(2)}) copy-start(bf16[1024]{0:T(1024)(128)(2,1)} %slice_reduce_fusion.1) | copy-start | bytes 6148
  35.2 60.3 %collective-permute-start.19 = (bf16[256,1024]{1,0:T(8,128)(2,1)}, bf16[256,1024]{1,0:T(8,128)(2,1)}, u32[]{:S(2)}, u32[]{:S(2)}) collective-permute-start(bf16[256,1024]{1,0:T(8,128)(2,1)} %bitcast), channel_id=1, source_target_pairs={{0,2},{2,0},{1,3},{3,1},{4,6},{6,4},{5,7},{7,5},{8,10},{10,8},{9,1... | collective-permute-start | bytes 1572872 | tf_op jit(solution)/shard_map/ppermute | solution.py:144
  43.4 29.2 %copy-start.5 = (pred[256]{0:T(512)(128)(4,1)S(1)}, pred[256]{0:T(512)(128)(4,1)}, u32[]{:S(2)}) copy-start(pred[256]{0:T(512)(128)(4,1)} %copy-done.4) | copy-start | bytes 772
  43.4 1.2 collective-permute-start.8
  50.4 7.6 %collective-permute-start.10 = (f32[1]{0:T(128)}, f32[1]{0:T(128)}, u32[]{:S(2)}, u32[]{:S(2)}) collective-permute-start(f32[1]{0:T(128)} %bitcast.74), channel_id=1, source_target_pairs={{0,4},{4,8},{8,12},{12,0},{1,5},{5,9},{9,13},{13,1},{2,6},{6,10},{... | collective-permute-start | bytes 20 | tf_op jit(solution)/shard_map/ppermute | solution.py:75
  53.6 5.0 %collective-permute-start.11 = (f32[1]{0:T(128)}, f32[1]{0:T(128)}, u32[]{:S(2)}, u32[]{:S(2)}) collective-permute-start(f32[1]{0:T(128)} %bitcast.74), channel_id=1, source_target_pairs={{0,8},{4,12},{8,0},{12,4},{1,9},{5,13},{9,1},{13,5},{2,10},{6,14},... | collective-permute-start | bytes 20 | tf_op jit(solution)/shard_map/ppermute | solution.py:75
  56.7 3.5 %collective-permute-start.12 = (f32[1]{0:T(128)}, f32[1]{0:T(128)}, u32[]{:S(2)}, u32[]{:S(2)}) collective-permute-start(f32[1]{0:T(128)} %bitcast.74), channel_id=1, source_target_pairs={{0,12},{4,0},{8,4},{12,8},{1,13},{5,1},{9,5},{13,9},{2,14},{6,2},{... | collective-permute-start | bytes 20 | tf_op jit(solution)/shard_map/ppermute | solution.py:75
  64.9 7.2 %collective-permute-start.13 = (f32[1,1,512]{2,1,0:T(1,128)S(1)}, f32[1,1,512]{2,1,0:T(1,128)S(1)}, u32[]{:S(2)}, u32[]{:S(2)}) collective-permute-start(f32[1,1,512]{2,1,0:T(1,128)S(1)} %get-tuple-element.40), channel_id=1, source_target_pairs={{0,4},{4,8},{8,12},{12,0},{1,5},{5,9},{9,13},{13,1},{2,6},{6,10},{... | collective-permute-start | bytes 6152 | tf_op jit(solution)/shard_map/ppermute | solution.py:89
  66.0 6.0 %collective-permute-start.14 = (f32[1,1,512]{2,1,0:T(1,128)S(1)}, f32[1,1,512]{2,1,0:T(1,128)S(1)}, u32[]{:S(2)}, u32[]{:S(2)}) collective-permute-start(f32[1,1,512]{2,1,0:T(1,128)S(1)} %get-tuple-element.42), channel_id=1, source_target_pairs={{0,8},{4,12},{8,0},{12,4},{1,9},{5,13},{9,1},{13,5},{2,10},{6,14},... | collective-permute-start | bytes 6152 | tf_op jit(solution)/shard_map/ppermute | solution.py:89
  69.0 3.6 %collective-permute-start.15 = (f32[1,1,512]{2,1,0:T(1,128)S(1)}, f32[1,1,512]{2,1,0:T(1,128)S(1)}, u32[]{:S(2)}, u32[]{:S(2)}) collective-permute-start(f32[1,1,512]{2,1,0:T(1,128)S(1)} %get-tuple-element.41), channel_id=1, source_target_pairs={{0,12},{4,0},{8,4},{12,8},{1,13},{5,1},{9,5},{13,9},{2,14},{6,2},{... | collective-permute-start | bytes 6152 | tf_op jit(solution)/shard_map/ppermute | solution.py:89
  72.8 3.1 %collective-permute-start.16 = (bf16[1,1,513,256]{2,3,1,0:T(8,128)(2,1)S(1)}, bf16[1,1,513,256]{2,3,1,0:T(8,128)(2,1)S(1)}, u32[]{:S(2)}, u32[]{:S(2)}) collective-permute-start(bf16[1,1,513,256]{2,3,1,0:T(8,128)(2,1)S(1)} %pad_maximum_fusion.1), channel_id=1, source_target_pairs={{0,1},{1,0},{2,3},{3,2},{4,5},{5,4},{6,7},{7,6},{8,9},{9,8},{10,11... | collective-permute-start | bytes 787976 | tf_op jit(solution)/shard_map/ppermute | solution.py:95
  87.7 7.6 %collective-permute-start.18 = (bf16[103936]{0:T(1024)(128)(2,1)S(1)}, bf16[103936]{0:T(1024)(128)(2,1)S(1)}, u32[]{:S(2)}, u32[]{:S(2)}) collective-permute-start(bf16[103936]{0:T(1024)(128)(2,1)S(1)} %pad_maximum_fusion.2), channel_id=1, source_target_pairs={{0,2},{2,0},{1,3},{3,1},{4,6},{6,4},{5,7},{7,5},{8,10},{10,8},{9,1... | collective-permute-start | bytes 623624 | tf_op jit(solution)/shard_map/ppermute | solution.py:335
  97.5 14.3 %collective-permute-start.20 = (bf16[256,384]{0,1:T(8,128)(2,1)S(1)}, bf16[256,384]{0,1:T(8,128)(2,1)S(1)}, u32[]{:S(2)}, u32[]{:S(2)}) collective-permute-start(bf16[256,384]{0,1:T(8,128)(2,1)S(1)} %get-tuple-element.28), channel_id=1, source_target_pairs={{0,4},{4,8},{8,12},{12,0},{1,5},{5,9},{9,13},{13,1},{2,6},{6,10},{... | collective-permute-start | bytes 589832 | tf_op jit(solution)/shard_map/ppermute | solution.py:89
  98.1 16.7 %collective-permute-start.21 = (bf16[256,384]{0,1:T(8,128)(2,1)S(1)}, bf16[256,384]{0,1:T(8,128)(2,1)S(1)}, u32[]{:S(2)}, u32[]{:S(2)}) collective-permute-start(bf16[256,384]{0,1:T(8,128)(2,1)S(1)} %get-tuple-element.30), channel_id=1, source_target_pairs={{0,8},{4,12},{8,0},{12,4},{1,9},{5,13},{9,1},{13,5},{2,10},{6,14},... | collective-permute-start | bytes 589832 | tf_op jit(solution)/shard_map/ppermute | solution.py:89
  100.8 17.1 %collective-permute-start.22 = (bf16[256,384]{0,1:T(8,128)(2,1)S(1)}, bf16[256,384]{0,1:T(8,128)(2,1)S(1)}, u32[]{:S(2)}, u32[]{:S(2)}) collective-permute-start(bf16[256,384]{0,1:T(8,128)(2,1)S(1)} %get-tuple-element.29), channel_id=1, source_target_pairs={{0,12},{4,0},{8,4},{12,8},{1,13},{5,1},{9,5},{13,9},{2,14},{6,2},{... | collective-permute-start | bytes 589832 | tf_op jit(solution)/shard_map/ppermute | solution.py:89
  118.0 6.8 %collective-permute-start.23 = (bf16[256,384]{0,1:T(8,128)(2,1)S(1)}, bf16[256,384]{0,1:T(8,128)(2,1)S(1)}, u32[]{:S(2)}, u32[]{:S(2)}) collective-permute-start(bf16[256,384]{0,1:T(8,128)(2,1)S(1)} %add_convert_fusion), channel_id=1, source_target_pairs={{0,2},{2,0},{1,3},{3,1},{4,6},{6,4},{5,7},{7,5},{8,10},{10,8},{9,1... | collective-permute-start | bytes 589832 | tf_op jit(solution)/shard_map/ppermute | solution.py:346
  (20 other events, 35.9 us)

commit v12 on v10

--- a/solution.py
+++ b/solution.py
@@ -199,16 +199,18 @@
     )
     normed_last, unit_last, inverse_last = norm_forward(residual_last, gain_last)
     scores = jnp.einsum("qcd,d->qc", normed_last, w_score, precision=lax.Precision.HIGHEST)
-    score_exp = jnp.exp(scores)
+    score_exp_all = gather_cand(jnp.exp(scores), 1)
     teacher_peak = jnp.max(teacher_all, 1)
-    teacher_exp = jnp.exp(teacher - teacher_peak[:, None])
-    teacher_totals = jnp.sum(jnp.exp(teacher_all - teacher_peak[:, None]), 1)
-    score_totals = sum_cand(jnp.sum(score_exp, 1))
-    student_prob = score_exp / score_totals[:, None]
-    teacher_prob = teacher_exp / teacher_totals[:, None]
-    score_grad = LOSS_SCALE * (student_prob - teacher_prob) / query_count
-    grad_last = norm_backward(score_grad[..., None] * w_score, unit_last, inverse_last, gain_last)
-    grad_last_low = grad_last.astype(jnp.bfloat16)
+    teacher_exp = jnp.exp(teacher_all - teacher_peak[:, None])
+    student_prob = score_exp_all / jnp.sum(score_exp_all, 1)[:, None]
+    teacher_prob = teacher_exp / jnp.sum(teacher_exp, 1)[:, None]
+    score_grad_all = LOSS_SCALE * (student_prob - teacher_prob) / query_count
+    score_grad = jnp.take(score_grad_all, local_ids, axis=1)
+    unit_grad_last = norm_backward(
+        jnp.broadcast_to(w_score, normed_last.shape), unit_last, inverse_last, gain_last
+    )
+    grad_last = score_grad[..., None] * unit_grad_last
+    grad_last_low = unit_grad_last.astype(jnp.bfloat16)
     grad_mixed_last = (
         mixed("qcd,fd->qcf", grad_last_low, w_out_last)
         .astype(jnp.bfloat16)
@@ -221,6 +223,7 @@
     )
     own_slope = (own_last_prob * (own_dot - centre)).astype(jnp.bfloat16)
     cross_slope = (cross_last_prob * (cross_dot - centre)).astype(jnp.bfloat16)
+    own_scale = score_grad[:, :, None, None]
     grad_query_last = (
         (
             (
@@ -228,23 +231,38 @@
                 + mixed("qchd,qdhe->qche", cross_slope, cls_keys_last)
             )
             * score_scale
+            * own_scale
         )
         .astype(jnp.bfloat16)
         .reshape(lists, local_cands, local_width)
     )
-    own_key_grad = (mixed("qcht,qche->qcthe", own_slope, last_heads) * score_scale).reshape(
-        lists, local_cands, seq_len, local_width
-    )
-    own_val_grad = mixed("qcht,qche->qcthe", own_last_weight, grad_mixed_last).reshape(
-        lists, local_cands, seq_len, local_width
-    )
-    cls_key_terms = (mixed("qchd,qche->qdhe", cross_slope, last_heads) * score_scale).reshape(
-        lists, cand_count, local_width
-    )
-    cls_val_terms = mixed("qchd,qche->qdhe", cross_last_weight, grad_mixed_last).reshape(
-        lists, cand_count, local_width
-    )
-    back_terms = scatter_cand(jnp.concatenate([cls_key_terms, cls_val_terms], -1), 1)
+    own_key_grad = (
+        mixed("qcht,qche->qcthe", own_slope, last_heads) * score_scale * own_scale[..., None]
+    ).reshape(lists, local_cands, seq_len, local_width)
+    own_val_grad = (
+        mixed("qcht,qche->qcthe", own_last_weight, grad_mixed_last) * own_scale[..., None]
+    ).reshape(lists, local_cands, seq_len, local_width)
+    cls_key_terms = mixed("qchd,qche->qcdhe", cross_slope, last_heads) * score_scale
+    cls_val_terms = mixed("qchd,qche->qcdhe", cross_last_weight, grad_mixed_last)
+    cls_terms = jnp.concatenate(
+        [
+            cls_key_terms.reshape(lists, local_cands, cand_count, local_width),
+            cls_val_terms.reshape(lists, local_cands, cand_count, local_width),
+        ],
+        -1,
+    )
+    count = lax.axis_size("cand")
+    if count <= 8 and local_cands == 1:
+        me = lax.axis_index("cand")
+        block = cls_terms[:, 0]
+        back_terms = lax.dynamic_slice_in_dim(block, me, 1, 1) * score_grad[:, :, None]
+        for k in range(1, count):
+            piece = lax.dynamic_slice_in_dim(block, (me + k) % count, 1, 1)
+            moved = lax.ppermute(piece, "cand", [(j, (j + k) % count) for j in range(count)])
+            source = lax.dynamic_slice_in_dim(score_grad_all, (me - k) % count, 1, 1)
+            back_terms = back_terms + moved * source[:, :, None]
+    else:
+        back_terms = scatter_cand(jnp.sum(cls_terms * score_grad[:, :, None, None], 1), 1)
     back_keys = back_terms[..., :local_width]
     back_vals = back_terms[..., local_width:]
     first_cols = first_mask[None, None, :, None]

time: 117 us -> 121 us (1.034)
  other arithmetic: 10.5 us -> 16.4 us
  between operations: 8.72 us -> 6.08 us
    ppermute x6 -> x9, starting transfers between devices: 8.43 us -> 16.2 us  [gather_cand(): lax.ppermute(block, 'cand', [(j, (j + k) % count) for j in range(count)])]
    ppermute x6 -> x3, starting transfers between devices: 8.88 us -> 3.88 us  [scatter_cand(): lax.ppermute(piece, 'cand', [(j, (j + k) % count) for j in range(count)])]
    ppermute x3, starting transfers between devices: 7.77 us -> 5 us  [local(): lax.ppermute(piece, 'cand', [(j, (j + k) % count) for j in range(count)])]
    div x0 -> x2, other arithmetic: none -> 2.07 us  [the longest x1 1.43 us: local(): teacher_prob = teacher_exp / jnp.sum(teacher_exp, 1)[:, None]]
    another operation x4 -> x5, other arithmetic: 0.06 us -> 1.92 us  [gather_cand(): jnp.stack(parts, 0)]
    add x1, other arithmetic: 0.01 us -> 1.85 us  [local(): back_terms = back_terms + moved * source[:, :, None]]
    ppermute x6 -> x3, waiting for transfers between devices: 16.9 us -> 16.6 us  [scatter_cand(): lax.ppermute(piece, 'cand', [(j, (j + k) % count) for j in range(count)])]
  transfers between devices with their start and end apart: 24 -> 24, of which waited for: 9 -> 9; matrix products, arithmetic and copies ran while one was open for 37% -> 41% of each run, Pallas kernels for 0% -> 0%
where the time goes in v12:
time: 121 us; the launch traced here: 119 us
  waiting for transfers between devices  30.4 us (25%)
  starting transfers between devices  28.9 us (24%)
  matrix products  28.4 us (23%)
  other arithmetic  16.4 us (14%)
  local copies, waits for them, and re-layouts  9.26 us (8%)
  between operations  6.08 us (5%)
    dot_general x37, matrix products, mixed(): jnp.einsum(pattern, former, latter, preferred_element_type=jnp.float32)  28.4 us
    ppermute x3, waiting for transfers between devices, scatter_cand(): lax.ppermute(piece, 'cand', [(j, (j + k) % count) for j in range(count)])  16.6 us
    ppermute x9, starting transfers between devices, gather_cand(): lax.ppermute(block, 'cand', [(j, (j + k) % count) for j in range(count)])  16.2 us
    ppermute x1, waiting for transfers between devices, local(): partner = lax.ppermute(reduced, 'query', swap)  6.07 us
    ppermute x1, waiting for transfers between devices, local(): lax.ppermute(jnp.concatenate([given_half.reshape(-1), cls_flat.reshape(-1...  5.41 us
    ppermute x3, starting transfers between devices, local(): lax.ppermute(piece, 'cand', [(j, (j + k) % count) for j in range(count)])  5 us
    ppermute x3, starting transfers between devices, scatter_cand(): lax.ppermute(piece, 'cand', [(j, (j + k) % count) for j in range(count)])  3.88 us
  transfers between devices with their start and end apart: 24, of which 9 were waited for; matrix products, arithmetic and copies ran while one was open for 41% of the time, Pallas kernels for 0%

profile of v12, /device:TPU:8, one launch (start us, length us, event | category | flops | bytes accessed | tf_op | source)
XLA Modules:
  0.0 119.5 jit_solution(656091940557387761)
XLA Ops:
  1.4 1.6 %collective-permute-start = (f32[1,1,1025]{2,1,0:T(1,128)S(1)}, f32[1,1,1025]{2,1,0:T(1,128)S(1)}, u32[]{:S(2)}, u32[]{:S(2)}) collective-permute-start(f32[1,1,1025]{2,1,0:T(1,128)S(1)} %pad_maximum_fusion.4), channel_id=1, source_target_pairs={{0,4},{4,8},{8,12},{12,0},{1,5},{5,9},{9,13},{13,1},{2,6},{6,10},{... | collective-permute-start | bytes 12308 | tf_op jit(solution)/shard_map/ppermute | solution.py:60
  4.1 1.9 %collective-permute-start.2 = (f32[1,1,1025]{2,1,0:T(1,128)S(1)}, f32[1,1,1025]{2,1,0:T(1,128)S(1)}, u32[]{:S(2)}, u32[]{:S(2)}) collective-permute-start(f32[1,1,1025]{2,1,0:T(1,128)S(1)} %pad_maximum_fusion.4), channel_id=1, source_target_pairs={{0,12},{4,0},{8,4},{12,8},{1,13},{5,1},{9,5},{13,9},{2,14},{6,2},{... | collective-permute-start | bytes 12308 | tf_op jit(solution)/shard_map/ppermute | solution.py:60
  6.7 2.1 %fusion.7 = bf16[3,1,1,256,256]{3,4,0,2,1:T(8,128)(2,1)S(1)} fusion(bf16[3,1024,256]{2,1,0:T(8,128)(2,1)} %param.13, bf16[1,1,256,1024]{3,2,1,0:T(8,128)(2,1)} %param.10), kind=kOutput, calls=%fused_computation.19 | convolution fusion | flops 402849792 | bytes 2490368 | tf_op jit(solution)/shard_map/qcsd,kdf->kqcsf/dot_general | solution.py:15
  16.3 1.4 %fusion.5 = f32[1,1,256,1024]{3,2,1,0:T(8,128)S(1)} fusion(bf16[256,256]{0,1:T(8,128)(2,1)S(1)} %bitcast.437, bf16[256,1024]{1,0:T(8,128)(2,1)S(1)} %copy-done.1, bf16[1,1,256,1024]{3,2,1,0:T(8,128)(2,1)} %param.10), kind=kOutput, calls=%fused_computation.16 | convolution fusion | flops 134742016 | bytes 2228224 | tf_op jit(solution)/shard_map/qcsf,fd->qcsd/dot_general | solution.py:15
  17.7 1.3 %fusion.120 = f32[]{:T(128)} fusion(f32[1,4,1025]{2,1,0:T(4,128)S(1)} %bitcast_select_fusion, f32[]{:T(128)} %slice_reduce_fusion.2), kind=kLoop, calls=%fused_computation.240 | loop fusion | flops 7 | bytes 24 | tf_op jit(solution)/shard_map/reduce_sum | solution.py:206
  19.6 1.4 %divide_reduce_fusion = f32[4]{0:T(128)S(1)} fusion(f32[1,4,1025]{2,1,0:T(4,128)S(1)} %bitcast_select_fusion, f32[]{:T(128)} %fusion.120, f32[]{:T(128)} %slice_reduce_fusion.2), kind=kLoop, calls=%fused_computation.227 | loop fusion | flops 8 | bytes 40 | tf_op jit(solution)/shard_map/div | solution.py:206
  21.1 1.4 %fusion.154 = (f32[256]{0:T(256)S(1)}, f32[1,1,256,1024]{3,2,1,0:T(8,128)S(1)}) fusion(f32[1,1,256,1024]{3,2,1,0:T(8,128)S(1)} %fusion.5, bf16[256,1024]{1,0:T(8,128)(2,1)} %collective-permute-done.4, bf16[1,1,256,256]{2,3,1,0:T(8,128)(2,1)S(1)} %collective-permute-done.3), kind=kOutput, calls=%fused_computation.287 | convolution fusion | flops 134741760 | bytes 2753536 | tf_op jit(solution)/shard_map/qcsf,fd->qcsd/dot_general | solution.py:15
  23.0 1.7 %fusion.8 = bf16[2,1,1,256,256]{4,3,0,2,1:T(8,128)(2,1)S(1)} fusion(bf16[3,1024,256]{2,1,0:T(8,128)(2,1)} %param.16, bf16[1,1,256,1024]{3,2,1,0:T(8,128)(2,1)S(1)} %multiply_convert_fusion.1), kind=kOutput, calls=%fused_computation.24 | convolution fusion | flops 268566528 | bytes 1835008 | tf_op jit(solution)/shard_map/qcsd,kdf->kqcsf/dot_general | solution.py:15
  25.0 3.6 %collective-permute-start.6 = (bf16[1,1,512]{2,1,0:T(2,128)(2,1)S(1)}, bf16[1,1,512]{2,1,0:T(2,128)(2,1)S(1)}, u32[]{:S(2)}, u32[]{:S(2)}) collective-permute-start(bf16[1,1,512]{2,1,0:T(2,128)(2,1)S(1)} %pad_maximum_fusion.5), channel_id=1, source_target_pairs={{0,8},{4,12},{8,0},{12,4},{1,9},{5,13},{9,1},{13,5},{2,10},{6,14},... | collective-permute-start | bytes 3080 | tf_op jit(solution)/shard_map/ppermute | solution.py:60
  30.5 1.6 %collective-permute-start.19 = (bf16[256,1024]{1,0:T(8,128)(2,1)}, bf16[256,1024]{1,0:T(8,128)(2,1)}, u32[]{:S(2)}, u32[]{:S(2)}) collective-permute-start(bf16[256,1024]{1,0:T(8,128)(2,1)} %bitcast), channel_id=1, source_target_pairs={{0,2},{2,0},{1,3},{3,1},{4,6},{6,4},{5,7},{7,5},{8,10},{10,8},{9,1... | collective-permute-start | bytes 1572872 | tf_op jit(solution)/shard_map/ppermute | solution.py:142
  40.5 3.3 %collective-permute-start.10 = (f32[1,1]{1,0:T(1,128)}, f32[1,1]{1,0:T(1,128)}, u32[]{:S(2)}, u32[]{:S(2)}) collective-permute-start(f32[1,1]{1,0:T(1,128)} %bitcast.80), channel_id=1, source_target_pairs={{0,4},{4,8},{8,12},{12,0},{1,5},{5,9},{9,13},{13,1},{2,6},{6,10},{... | collective-permute-start | bytes 20 | tf_op jit(solution)/shard_map/ppermute | solution.py:60
  43.8 3.1 %collective-permute-start.11 = (f32[1,1]{1,0:T(1,128)}, f32[1,1]{1,0:T(1,128)}, u32[]{:S(2)}, u32[]{:S(2)}) collective-permute-start(f32[1,1]{1,0:T(1,128)} %bitcast.80), channel_id=1, source_target_pairs={{0,8},{4,12},{8,0},{12,4},{1,9},{5,13},{9,1},{13,5},{2,10},{6,14},... | collective-permute-start | bytes 20 | tf_op jit(solution)/shard_map/ppermute | solution.py:60
  46.9 1.4 %collective-permute-start.12 = (f32[1,1]{1,0:T(1,128)}, f32[1,1]{1,0:T(1,128)}, u32[]{:S(2)}, u32[]{:S(2)}) collective-permute-start(f32[1,1]{1,0:T(1,128)} %bitcast.80), channel_id=1, source_target_pairs={{0,12},{4,0},{8,4},{12,8},{1,13},{5,1},{9,5},{13,9},{2,14},{6,2},{... | collective-permute-start | bytes 20 | tf_op jit(solution)/shard_map/ppermute | solution.py:60
  50.5 1.9 %maximum_bitcast_fusion.2 = f32[4]{0:T(128)S(1)} fusion(f32[1,1,1]{0,2,1:T(1,128)} %bitcast.85, f32[1,1,1]{0,2,1:T(1,128)} %bitcast.84, f32[1,1,1]{0,2,1:T(1,128)} %bitcast.82, f32[1,1,1]{0,2,1:T(1,128)} %bitcast.79), kind=kLoop, calls=%fused_computation.260 | loop fusion | flops 12 | bytes 32 | tf_op jit(solution)/shard_map/stack | solution.py:63
  57.8 2.9 %collective-permute-start.14 = (f32[1,1,512]{2,1,0:T(1,128)S(1)}, f32[1,1,512]{2,1,0:T(1,128)S(1)}, u32[]{:S(2)}, u32[]{:S(2)}) collective-permute-start(f32[1,1,512]{2,1,0:T(1,128)S(1)} %get-tuple-element.50), channel_id=1, source_target_pairs={{0,8},{4,12},{8,0},{12,4},{1,9},{5,13},{9,1},{13,5},{2,10},{6,14},... | collective-permute-start | bytes 6152 | tf_op jit(solution)/shard_map/ppermute | solution.py:261
  62.4 1.3 %fusion.31 = f32[1,1024]{1,0:T(1,128)S(1)} fusion(bf16[256,1]{0,1:T(2,128)(2,1)S(1)} %reshape.1563, bf16[3,1024,256]{2,1,0:T(8,128)(2,1)} %param.16), kind=kOutput, calls=%fused_computation.64 | convolution fusion | flops 524288 | bytes 528896 | tf_op jit(solution)/shard_map/qcf,df->qcd/dot_general | solution.py:15
  64.4 1.8 %multiply_add_fusion = f32[1,1,512]{2,1,0:T(1,128)S(1)} fusion(f32[1,1,512]{2,1,0:T(1,128)S(1)} %collective-permute-done.15, f32[1,1,512]{2,1,0:T(1,128)S(1)} %collective-permute-done.14, f32[1,1,512]{2,1,0:T(1,128)S(1)} %collective-permute-done.13, f32[1,1,4,512]{3,2,1,0:T(4,128)S(1)} %constant_dynamic-update-slice_fusion, s32[]{:T(128)S(6)} %select_n.345, ...), kind=kLoop, calls=%fused_computation.220 | loop fusion | flops 3584 | bytes 10260 | tf_op jit(solution)/shard_map/add | solution.py:263
  66.5 1.5 %fusion.29 = f32[256,1024]{1,0:T(8,128)S(1)} fusion(bf16[3,1024,256]{2,1,0:T(8,128)(2,1)} %param.16, f32[1,1,256,1,1,1,1,256]{2,7,6,5,4,3,1,0:T(8,128)S(1)} %bitcast.420, f32[256]{0:T(256)S(1)} %bitcast.452, pred[256]{0:T(512)(128)(4,1)S(1)} %iota_compare_fusion.1), kind=kOutput, calls=%fused_computation.62 | convolution fusion | flops 134414336 | bytes 1836288 | tf_op jit(solution)/shard_map/qcsf,df->qcsd/dot_general | solution.py:15
  68.0 1.5 %convolution_add_fusion.1 = f32[256,1024]{1,0:T(8,128)S(1)} fusion(f32[256,1024]{1,0:T(8,128)S(1)} %fusion.29, bf16[3,1024,256]{2,1,0:T(8,128)(2,1)} %param.16, f32[1,1,256,1,1,1,1,256]{2,7,6,5,4,3,1,0:T(8,128)S(1)} %bitcast.418, f32[256]{0:T(256)S(1)} %bitcast.450, pred[256]{0:T(512)(128)(4,1)S(1)} %iota_compare_fusion.1), kind=kOutput, calls=%fused_computation.11 | convolution fusion | flops 134676480 | bytes 2884864 | tf_op jit(solution)/shard_map/qcsf,df->qcsd/dot_general | solution.py:15
  69.6 1.3 %fusion.24 = f32[1,1024]{1,0:T(1,128)S(1)} fusion(bf16[256,1]{0,1:T(2,128)(2,1)S(1)} %reshape.1565, bf16[3,1024,256]{2,1,0:T(8,128)(2,1)} %collective-permute-done.17), kind=kOutput, calls=%fused_computation.55 | convolution fusion | flops 524288 | bytes 528896 | tf_op jit(solution)/shard_map/qcf,df->qcd/dot_general | solution.py:15
  70.9 1.4 %fusion.25 = f32[256,1024]{1,0:T(8,128)S(1)} fusion(bf16[3,1024,256]{2,1,0:T(8,128)(2,1)} %collective-permute-done.17, bf16[1,1,513,256]{2,3,1,0:T(8,128)(2,1)S(1)} %collective-permute-done.16), kind=kOutput, calls=%fused_computation.57 | convolution fusion | flops 134217728 | bytes 1703936 | tf_op jit(solution)/shard_map/qcsf,df->qcsd/dot_general | solution.py:15
  72.3 1.8 %fusion.11 = (f32[256]{0:T(256)S(1)}, f32[256,1024]{1,0:T(8,128)S(1)}) fusion(f32[1,1,256,1024]{3,2,1,0:T(8,128)S(1)} %get-tuple-element.66, f32[256]{0:T(256)S(1)} %add_rsqrt_fusion, f32[256]{0:T(256)S(1)} %broadcast_multiply_fusion.3, f32[1024]{0:T(1024)S(1)} %copy-done.8, f32[1024]{0:T(1024)S(1)} %get-tuple-element.46, f32[1024]{0:T(1024)S(1)} %add.415, ...), kind=kOutput, calls=%fused_computation.31 | convolution fusion | flops 137101056 | bytes 4865536 | tf_op jit(solution)/shard_map/qcsf,df->qcsd/dot_general | solution.py:15
  74.3 1.6 %convolution_convert_fusion.3 = bf16[256,256]{0,1:T(8,128)(2,1)S(1)} fusion(bf16[256,1024]{1,0:T(8,128)(2,1)} %param.14, f32[1,1,256,1024]{3,2,1,0:T(8,128)S(1)} %get-tuple-element.66, f32[256,1024]{1,0:T(8,128)S(1)} %get-tuple-element.68, f32[256]{0:T(256)S(1)} %broadcast_multiply_fusion.1, f32[256]{0:T(256)S(1)} %broadcast_multiply_fusion.2, ...), kind=kOutput, calls=%fused_computation.27 | convolution fusion | flops 136118272 | bytes 2756608 | tf_op jit(solution)/shard_map/qcsd,fd->qcsf/dot_general | solution.py:15
  77.0 1.3 %multiply_reduce_fusion = (f32[4,256]{1,0:T(4,128)S(1)}, f32[4,256,256]{1,2,0:T(8,128)S(1)}) fusion(f32[4,256]{1,0:T(4,128)} %copy-done.10, f32[4,256,256]{1,2,0:T(8,128)S(1)} %get-tuple-element.64, f32[4,256]{1,0:T(4,128)S(1)} %broadcast_select_fusion.2, bf16[256,4,64]{0,2,1:T(8,128)(2,1)S(1)} %bitcast.434, bf16[256,4,64]{0,2,1:T(8,128)(2,1)} %bitcast.439), kind=kOutput, calls=%fused_computation.36 | convolution fusion | flops 34601984 | bytes 2371584 | tf_op jit(solution)/shard_map/qcshe,qcthe->qchst/dot_general | solution.py:15
  81.9 1.6 %fusion.18 = f32[1024,384]{0,1:T(8,128)S(1)} fusion(bf16[4,1024]{1,0:T(4,128)(2,1)S(1)} %get-tuple-element.45, bf16[256,1024]{1,0:T(8,128)(2,1)} %bitcast, s32[]{:T(128)S(6)} %select_n.366, bf16[256,768]{0,1:T(8,128)(2,1)S(1)} %bitcast.416, bf16[4,768]{0,1:T(8,128)(2,1)S(1)} %copy.97), kind=kOutput, calls=%fused_computation.49 | convolution fusion | flops 205936640 | bytes 2504708 | tf_op jit(solution)/shard_map/rd,rf->df/dot_general | solution.py:15
  83.5 5.4 %collective-permute-done.18 = bf16[103936]{0:T(1024)(128)(2,1)S(1)} collective-permute-done((bf16[103936]{0:T(1024)(128)(2,1)S(1)}, bf16[103936]{0:T(1024)(128)(2,1)S(1)}, u32[]{:S(2)}, u32[]{:S(2)}) %collective-permute-start.18) | collective-permute-done | bytes 207904 | tf_op jit(solution)/shard_map/ppermute | solution.py:352
  89.1 1.4 %fusion.159 = f32[384,1024]{1,0:T(8,128)S(1)} fusion(bf16[256,384]{1,0:T(8,128)(2,1)S(1)} %slice.168, bf16[256,1024]{1,0:T(8,128)(2,1)} %collective-permute-done.19), kind=kOutput, calls=%fused_computation.292 | convolution fusion | flops 201326592 | bytes 2293760 | tf_op jit(solution)/shard_map/rd,rf->df/dot_general | solution.py:15
  91.8 2.8 %collective-permute-start.21 = (bf16[256,384]{0,1:T(8,128)(2,1)S(1)}, bf16[256,384]{0,1:T(8,128)(2,1)S(1)}, u32[]{:S(2)}, u32[]{:S(2)}) collective-permute-start(bf16[256,384]{0,1:T(8,128)(2,1)S(1)} %get-tuple-element.36), channel_id=1, source_target_pairs={{0,8},{4,12},{8,0},{12,4},{1,9},{5,13},{9,1},{13,5},{2,10},{6,14},... | collective-permute-start | bytes 589832 | tf_op jit(solution)/shard_map/ppermute | solution.py:89
  94.9 10.4 %collective-permute-done.20 = bf16[256,384]{0,1:T(8,128)(2,1)S(1)} collective-permute-done((bf16[256,384]{0,1:T(8,128)(2,1)S(1)}, bf16[256,384]{0,1:T(8,128)(2,1)S(1)}, u32[]{:S(2)}, u32[]{:S(2)}) %collective-permute-start.20) | collective-permute-done | bytes 196640 | tf_op jit(solution)/shard_map/ppermute | solution.py:89
  105.4 3.1 %collective-permute-done.21 = bf16[256,384]{0,1:T(8,128)(2,1)S(1)} collective-permute-done((bf16[256,384]{0,1:T(8,128)(2,1)S(1)}, bf16[256,384]{0,1:T(8,128)(2,1)S(1)}, u32[]{:S(2)}, u32[]{:S(2)}) %collective-permute-start.21) | collective-permute-done | bytes 196640 | tf_op jit(solution)/shard_map/ppermute | solution.py:89
  108.4 3.1 %collective-permute-done.22 = bf16[256,384]{0,1:T(8,128)(2,1)S(1)} collective-permute-done((bf16[256,384]{0,1:T(8,128)(2,1)S(1)}, bf16[256,384]{0,1:T(8,128)(2,1)S(1)}, u32[]{:S(2)}, u32[]{:S(2)}) %collective-permute-start.22) | collective-permute-done | bytes 196640 | tf_op jit(solution)/shard_map/ppermute | solution.py:89
  112.2 6.1 %collective-permute-done.23 = bf16[256,384]{0,1:T(8,128)(2,1)S(1)} collective-permute-done((bf16[256,384]{0,1:T(8,128)(2,1)S(1)}, bf16[256,384]{0,1:T(8,128)(2,1)S(1)}, u32[]{:S(2)}, u32[]{:S(2)}) %collective-permute-start.23) | collective-permute-done | bytes 196640 | tf_op jit(solution)/shard_map/ppermute | solution.py:363
  (242 shorter events, 35.4 us)
Async XLA Ops:
  1.4 10.1 %collective-permute-start = (f32[1,1,1025]{2,1,0:T(1,128)S(1)}, f32[1,1,1025]{2,1,0:T(1,128)S(1)}, u32[]{:S(2)}, u32[]{:S(2)}) collective-permute-start(f32[1,1,1025]{2,1,0:T(1,128)S(1)} %pad_maximum_fusion.4), channel_id=1, source_target_pairs={{0,4},{4,8},{8,12},{12,0},{1,5},{5,9},{9,13},{13,1},{2,6},{6,10},{... | collective-permute-start | bytes 12308 | tf_op jit(solution)/shard_map/ppermute | solution.py:60
  3.0 8.5 %collective-permute-start.1 = (f32[1,1,1025]{2,1,0:T(1,128)S(1)}, f32[1,1,1025]{2,1,0:T(1,128)S(1)}, u32[]{:S(2)}, u32[]{:S(2)}) collective-permute-start(f32[1,1,1025]{2,1,0:T(1,128)S(1)} %pad_maximum_fusion.4), channel_id=1, source_target_pairs={{0,8},{4,12},{8,0},{12,4},{1,9},{5,13},{9,1},{13,5},{2,10},{6,14},... | collective-permute-start | bytes 12308 | tf_op jit(solution)/shard_map/ppermute | solution.py:60
  4.1 7.4 %collective-permute-start.2 = (f32[1,1,1025]{2,1,0:T(1,128)S(1)}, f32[1,1,1025]{2,1,0:T(1,128)S(1)}, u32[]{:S(2)}, u32[]{:S(2)}) collective-permute-start(f32[1,1,1025]{2,1,0:T(1,128)S(1)} %pad_maximum_fusion.4), channel_id=1, source_target_pairs={{0,12},{4,0},{8,4},{12,8},{1,13},{5,1},{9,5},{13,9},{2,14},{6,2},{... | collective-permute-start | bytes 12308 | tf_op jit(solution)/shard_map/ppermute | solution.py:60
  6.1 15.0 %collective-permute-start.4 = (bf16[256,1024]{1,0:T(8,128)(2,1)}, bf16[256,1024]{1,0:T(8,128)(2,1)}, u32[]{:S(2)}, u32[]{:S(2)}) collective-permute-start(bf16[256,1024]{1,0:T(8,128)(2,1)} %param.14), channel_id=1, source_target_pairs={{0,1},{1,0},{2,3},{3,2},{4,5},{5,4},{6,7},{7,6},{8,9},{9,8},{10,11... | collective-permute-start | bytes 1572872 | tf_op jit(solution)/shard_map/ppermute | solution.py:95
  6.1 28.5 %collective-permute-start.9 = (bf16[256,1024]{1,0:T(8,128)(2,1)}, bf16[256,1024]{1,0:T(8,128)(2,1)}, u32[]{:S(2)}, u32[]{:S(2)}) collective-permute-start(bf16[256,1024]{1,0:T(8,128)(2,1)} %param.17), channel_id=1, source_target_pairs={{0,1},{1,0},{2,3},{3,2},{4,5},{5,4},{6,7},{7,6},{8,9},{9,8},{10,11... | collective-permute-start | bytes 1572872 | tf_op jit(solution)/shard_map/ppermute | solution.py:95
  6.6 65.7 %copy-start.5 = (pred[256]{0:T(512)(128)(4,1)}, pred[256]{0:T(512)(128)(4,1)S(1)}, u32[]{:S(2)}) copy-start(pred[256]{0:T(512)(128)(4,1)S(1)} %iota_compare_fusion.1) | copy-start | bytes 772
  8.8 3.3 %copy-start.2 = (bf16[3,1024,256]{2,1,0:T(8,128)(2,1)S(1)}, bf16[3,1024,256]{2,1,0:T(8,128)(2,1)}, u32[]{:S(2)}) copy-start(bf16[3,1024,256]{2,1,0:T(8,128)(2,1)} %param.13) | copy-start | bytes 4718596
  8.9 8.8 %copy-start.3 = (bf16[1,1,1,256,256]{3,4,0,2,1:T(8,128)(2,1)}, bf16[1,1,1,256,256]{3,4,0,2,1:T(8,128)(2,1)S(1)}, u32[]{:S(2)}) copy-start(bf16[1,1,1,256,256]{3,4,0,2,1:T(8,128)(2,1)S(1)} %get-tuple-element.38) | copy-start | bytes 393220
  11.5 58.1 %collective-permute-start.17 = (bf16[3,1024,256]{2,1,0:T(8,128)(2,1)}, bf16[3,1024,256]{2,1,0:T(8,128)(2,1)}, u32[]{:S(2)}, u32[]{:S(2)}) collective-permute-start(bf16[3,1024,256]{2,1,0:T(8,128)(2,1)} %param.16), channel_id=1, source_target_pairs={{0,1},{1,0},{2,3},{3,2},{4,5},{5,4},{6,7},{7,6},{8,9},{9,8},{10,11... | collective-permute-start | bytes 4718600 | tf_op jit(solution)/shard_map/ppermute | solution.py:95
  15.8 5.2 %collective-permute-start.3 = (bf16[1,1,256,256]{2,3,1,0:T(8,128)(2,1)S(1)}, bf16[1,1,256,256]{2,3,1,0:T(8,128)(2,1)S(1)}, u32[]{:S(2)}, u32[]{:S(2)}) collective-permute-start(bf16[1,1,256,256]{2,3,1,0:T(8,128)(2,1)S(1)} %bitcast.436), channel_id=1, source_target_pairs={{0,1},{1,0},{2,3},{3,2},{4,5},{5,4},{6,7},{7,6},{8,9},{9,8},{10,11... | collective-permute-start | bytes 393224 | tf_op jit(solution)/shard_map/ppermute | solution.py:95
  22.5 49.8 %copy-start.7 = (f32[256]{0:T(256)}, f32[256]{0:T(256)S(1)}, u32[]{:S(2)}) copy-start(f32[256]{0:T(256)S(1)} %broadcast_multiply_fusion.3) | copy-start | bytes 3076
  22.8 49.5 %copy-start.9 = (f32[256]{0:T(256)}, f32[256]{0:T(256)S(1)}, u32[]{:S(2)}) copy-start(f32[256]{0:T(256)S(1)} %add_rsqrt_fusion) | copy-start | bytes 3076
  24.7 9.7 %copy-start = (bf16[256,1024]{1,0:T(8,128)(2,1)S(1)}, bf16[256,1024]{1,0:T(8,128)(2,1)}, u32[]{:S(2)}) copy-start(bf16[256,1024]{1,0:T(8,128)(2,1)} %param.17) | copy-start | bytes 1572868
  24.7 14.5 %copy-start.14 = (f32[1024]{0:T(1024)S(1)}, f32[1024]{0:T(1024)}, u32[]{:S(2)}) copy-start(f32[1024]{0:T(1024)} %param.19) | copy-start | bytes 12292
  24.7 14.5 %copy-start.15 = (f32[1024]{0:T(1024)S(1)}, f32[1024]{0:T(1024)}, u32[]{:S(2)}) copy-start(f32[1024]{0:T(1024)} %param.18) | copy-start | bytes 12292
  24.8 5.7 %collective-permute-start.5 = (bf16[1,1,512]{2,1,0:T(2,128)(2,1)S(1)}, bf16[1,1,512]{2,1,0:T(2,128)(2,1)S(1)}, u32[]{:S(2)}, u32[]{:S(2)}) collective-permute-start(bf16[1,1,512]{2,1,0:T(2,128)(2,1)S(1)} %pad_maximum_fusion.5), channel_id=1, source_target_pairs={{0,4},{4,8},{8,12},{12,0},{1,5},{5,9},{9,13},{13,1},{2,6},{6,10},{... | collective-permute-start | bytes 3080 | tf_op jit(solution)/shard_map/ppermute | solution.py:60
  25.0 7.1 %collective-permute-start.6 = (bf16[1,1,512]{2,1,0:T(2,128)(2,1)S(1)}, bf16[1,1,512]{2,1,0:T(2,128)(2,1)S(1)}, u32[]{:S(2)}, u32[]{:S(2)}) collective-permute-start(bf16[1,1,512]{2,1,0:T(2,128)(2,1)S(1)} %pad_maximum_fusion.5), channel_id=1, source_target_pairs={{0,8},{4,12},{8,0},{12,4},{1,9},{5,13},{9,1},{13,5},{2,10},{6,14},... | collective-permute-start | bytes 3080 | tf_op jit(solution)/shard_map/ppermute | solution.py:60
  28.6 3.6 %collective-permute-start.7 = (bf16[1,1,512]{2,1,0:T(2,128)(2,1)S(1)}, bf16[1,1,512]{2,1,0:T(2,128)(2,1)S(1)}, u32[]{:S(2)}, u32[]{:S(2)}) collective-permute-start(bf16[1,1,512]{2,1,0:T(2,128)(2,1)S(1)} %pad_maximum_fusion.5), channel_id=1, source_target_pairs={{0,12},{4,0},{8,4},{12,8},{1,13},{5,1},{9,5},{13,9},{2,14},{6,2},{... | collective-permute-start | bytes 3080 | tf_op jit(solution)/shard_map/ppermute | solution.py:60
  30.5 58.6 %collective-permute-start.19 = (bf16[256,1024]{1,0:T(8,128)(2,1)}, bf16[256,1024]{1,0:T(8,128)(2,1)}, u32[]{:S(2)}, u32[]{:S(2)}) collective-permute-start(bf16[256,1024]{1,0:T(8,128)(2,1)} %bitcast), channel_id=1, source_target_pairs={{0,2},{2,0},{1,3},{3,1},{4,6},{6,4},{5,7},{7,5},{8,10},{10,8},{9,1... | collective-permute-start | bytes 1572872 | tf_op jit(solution)/shard_map/ppermute | solution.py:142
  34.4 1.2 collective-permute-start.8
  40.5 9.0 %collective-permute-start.10 = (f32[1,1]{1,0:T(1,128)}, f32[1,1]{1,0:T(1,128)}, u32[]{:S(2)}, u32[]{:S(2)}) collective-permute-start(f32[1,1]{1,0:T(1,128)} %bitcast.80), channel_id=1, source_target_pairs={{0,4},{4,8},{8,12},{12,0},{1,5},{5,9},{9,13},{13,1},{2,6},{6,10},{... | collective-permute-start | bytes 20 | tf_op jit(solution)/shard_map/ppermute | solution.py:60
  43.8 5.7 %collective-permute-start.11 = (f32[1,1]{1,0:T(1,128)}, f32[1,1]{1,0:T(1,128)}, u32[]{:S(2)}, u32[]{:S(2)}) collective-permute-start(f32[1,1]{1,0:T(1,128)} %bitcast.80), channel_id=1, source_target_pairs={{0,8},{4,12},{8,0},{12,4},{1,9},{5,13},{9,1},{13,5},{2,10},{6,14},... | collective-permute-start | bytes 20 | tf_op jit(solution)/shard_map/ppermute | solution.py:60
  46.9 3.6 %collective-permute-start.12 = (f32[1,1]{1,0:T(1,128)}, f32[1,1]{1,0:T(1,128)}, u32[]{:S(2)}, u32[]{:S(2)}) collective-permute-start(f32[1,1]{1,0:T(1,128)} %bitcast.80), channel_id=1, source_target_pairs={{0,12},{4,0},{8,4},{12,8},{1,13},{5,1},{9,5},{13,9},{2,14},{6,2},{... | collective-permute-start | bytes 20 | tf_op jit(solution)/shard_map/ppermute | solution.py:60
  56.9 7.2 %collective-permute-start.13 = (f32[1,1,512]{2,1,0:T(1,128)S(1)}, f32[1,1,512]{2,1,0:T(1,128)S(1)}, u32[]{:S(2)}, u32[]{:S(2)}) collective-permute-start(f32[1,1,512]{2,1,0:T(1,128)S(1)} %get-tuple-element.48), channel_id=1, source_target_pairs={{0,4},{4,8},{8,12},{12,0},{1,5},{5,9},{9,13},{13,1},{2,6},{6,10},{... | collective-permute-start | bytes 6152 | tf_op jit(solution)/shard_map/ppermute | solution.py:261
  57.8 6.2 %collective-permute-start.14 = (f32[1,1,512]{2,1,0:T(1,128)S(1)}, f32[1,1,512]{2,1,0:T(1,128)S(1)}, u32[]{:S(2)}, u32[]{:S(2)}) collective-permute-start(f32[1,1,512]{2,1,0:T(1,128)S(1)} %get-tuple-element.50), channel_id=1, source_target_pairs={{0,8},{4,12},{8,0},{12,4},{1,9},{5,13},{9,1},{13,5},{2,10},{6,14},... | collective-permute-start | bytes 6152 | tf_op jit(solution)/shard_map/ppermute | solution.py:261
  60.8 3.6 %collective-permute-start.15 = (f32[1,1,512]{2,1,0:T(1,128)S(1)}, f32[1,1,512]{2,1,0:T(1,128)S(1)}, u32[]{:S(2)}, u32[]{:S(2)}) collective-permute-start(f32[1,1,512]{2,1,0:T(1,128)S(1)} %get-tuple-element.49), channel_id=1, source_target_pairs={{0,12},{4,0},{8,4},{12,8},{1,13},{5,1},{9,5},{13,9},{2,14},{6,2},{... | collective-permute-start | bytes 6152 | tf_op jit(solution)/shard_map/ppermute | solution.py:261
  66.4 3.0 %collective-permute-start.16 = (bf16[1,1,513,256]{2,3,1,0:T(8,128)(2,1)S(1)}, bf16[1,1,513,256]{2,3,1,0:T(8,128)(2,1)S(1)}, u32[]{:S(2)}, u32[]{:S(2)}) collective-permute-start(bf16[1,1,513,256]{2,3,1,0:T(8,128)(2,1)S(1)} %pad_maximum_fusion.1), channel_id=1, source_target_pairs={{0,1},{1,0},{2,3},{3,2},{4,5},{5,4},{6,7},{7,6},{8,9},{9,8},{10,11... | collective-permute-start | bytes 787976 | tf_op jit(solution)/shard_map/ppermute | solution.py:95
  81.3 7.6 %collective-permute-start.18 = (bf16[103936]{0:T(1024)(128)(2,1)S(1)}, bf16[103936]{0:T(1024)(128)(2,1)S(1)}, u32[]{:S(2)}, u32[]{:S(2)}) collective-permute-start(bf16[103936]{0:T(1024)(128)(2,1)S(1)} %pad_maximum_fusion.2), channel_id=1, source_target_pairs={{0,2},{2,0},{1,3},{3,1},{4,6},{6,4},{5,7},{7,5},{8,10},{10,8},{9,1... | collective-permute-start | bytes 623624 | tf_op jit(solution)/shard_map/ppermute | solution.py:352
  91.1 14.3 %collective-permute-start.20 = (bf16[256,384]{0,1:T(8,128)(2,1)S(1)}, bf16[256,384]{0,1:T(8,128)(2,1)S(1)}, u32[]{:S(2)}, u32[]{:S(2)}) collective-permute-start(bf16[256,384]{0,1:T(8,128)(2,1)S(1)} %get-tuple-element.34), channel_id=1, source_target_pairs={{0,4},{4,8},{8,12},{12,0},{1,5},{5,9},{9,13},{13,1},{2,6},{6,10},{... | collective-permute-start | bytes 589832 | tf_op jit(solution)/shard_map/ppermute | solution.py:89
  91.8 16.7 %collective-permute-start.21 = (bf16[256,384]{0,1:T(8,128)(2,1)S(1)}, bf16[256,384]{0,1:T(8,128)(2,1)S(1)}, u32[]{:S(2)}, u32[]{:S(2)}) collective-permute-start(bf16[256,384]{0,1:T(8,128)(2,1)S(1)} %get-tuple-element.36), channel_id=1, source_target_pairs={{0,8},{4,12},{8,0},{12,4},{1,9},{5,13},{9,1},{13,5},{2,10},{6,14},... | collective-permute-start | bytes 589832 | tf_op jit(solution)/shard_map/ppermute | solution.py:89
  94.6 16.9 %collective-permute-start.22 = (bf16[256,384]{0,1:T(8,128)(2,1)S(1)}, bf16[256,384]{0,1:T(8,128)(2,1)S(1)}, u32[]{:S(2)}, u32[]{:S(2)}) collective-permute-start(bf16[256,384]{0,1:T(8,128)(2,1)S(1)} %get-tuple-element.35), channel_id=1, source_target_pairs={{0,12},{4,0},{8,4},{12,8},{1,13},{5,1},{9,5},{13,9},{2,14},{6,2},{... | collective-permute-start | bytes 589832 | tf_op jit(solution)/shard_map/ppermute | solution.py:89
  111.6 6.7 %collective-permute-start.23 = (bf16[256,384]{0,1:T(8,128)(2,1)S(1)}, bf16[256,384]{0,1:T(8,128)(2,1)S(1)}, u32[]{:S(2)}, u32[]{:S(2)}) collective-permute-start(bf16[256,384]{0,1:T(8,128)(2,1)S(1)} %add_convert_fusion), channel_id=1, source_target_pairs={{0,2},{2,0},{1,3},{3,1},{4,6},{6,4},{5,7},{7,5},{8,10},{10,8},{9,1... | collective-permute-start | bytes 589832 | tf_op jit(solution)/shard_map/ppermute | solution.py:363
  (12 other events, 14.7 us)

commit v13 on v8

--- a/solution.py
+++ b/solution.py
@@ -169,7 +169,7 @@
         first_mask[None, None, :, None, None], attended + attended_cls[:, :, None], attended
     )
     first_mixed = attended.reshape(lists, local_cands, seq_len, local_width).astype(jnp.bfloat16)
-    first_joined = lax.all_gather(first_mixed, "mp", axis=3, tiled=True)
+    first_joined = gather_mp(first_mixed, 3)
     residual_first = tokens.astype(jnp.float32) + mixed(
         "qcsf,fd->qcsd", first_joined, out_first_full
     )
@@ -198,7 +198,7 @@
         "qchd,qdhe->qche", cross_last_weight, cls_vals_last
     )
     last_mixed = attended_last.reshape(lists, local_cands, local_width).astype(jnp.bfloat16)
-    last_joined = lax.all_gather(last_mixed, "mp", axis=2, tiled=True)
+    last_joined = gather_mp(last_mixed, 2)
     residual_last = hidden[:, :, 0].astype(jnp.float32) + mixed(
         "qcf,fd->qcd", last_joined, out_last_full
     )
@@ -259,12 +259,7 @@
     val_grad = jnp.where(first_cols, own_val_grad + back_vals[:, :, None], own_val_grad).astype(
         jnp.bfloat16
     )
-    joined = lax.all_gather(
-        jnp.concatenate([key_grad, val_grad, grad_query_last[:, :, None]], 2),
-        "mp",
-        axis=3,
-        tiled=True,
-    )
+    joined = gather_mp(jnp.concatenate([key_grad, val_grad, grad_query_last[:, :, None]], 2), 3)
     key_joined = joined[:, :, :seq_len]
     val_joined = joined[:, :, seq_len : 2 * seq_len]
     query_joined = joined[:, :, 2 * seq_len]

time: 116 us -> 136 us (1.17)
  local copies, waits for them, and re-layouts: 7.62 us -> 18.2 us
  other arithmetic: 13.9 us -> 23.2 us
  blocking collectives: 6.37 us -> 0 us
  matrix products: 20.8 us -> 24.2 us
  waiting for transfers between devices: 30 us -> 31.5 us
    all_gather x3 -> x0, blocking collectives: 6.37 us -> none  [the longest x1 2.46 us: local(): lax.all_gather(jnp.concatenate([key_grad, val_grad, grad_query_last[:, :,...]
    dot_general x32, matrix products: 20.8 us -> 24.2 us  [mixed(): jnp.einsum(pattern, former, latter, preferred_element_type=jnp.float32)]
    another operation x9, local copies, waits for them, and re-layouts: 0.69 us -> 3.19 us
    slice x2, local copies, waits for them, and re-layouts: 0.14 us -> 2.39 us  [local(): last_kv[1][:, :, 0]]
    another operation x4, other arithmetic: 0.06 us -> 1.99 us  [gather_cand(): jnp.stack(parts, 0)]
    another operation x10, other arithmetic: 1.52 us -> 3.34 us
    unnamed x45 -> x91, local copies, waits for them, and re-layouts: 1.27 us -> 2.96 us
    select_n x1 -> x3, other arithmetic: 3.41 us -> 4.56 us  [gather_mp(): jnp.where(lax.axis_index('mp') == 0, jnp.concatenate([block, other], axis...]
  transfers between devices with their start and end apart: 21 -> 24, of which waited for: 8 -> 8; matrix products, arithmetic and copies ran while one was open for 33% -> 45% of each run, Pallas kernels for 0% -> 0%
where the time goes in v13:
time: 136 us; the launch traced here: 135 us
  waiting for transfers between devices  31.5 us (23%)
  starting transfers between devices  28.8 us (21%)
  matrix products  24.2 us (18%)
  other arithmetic  23.2 us (17%)
  local copies, waits for them, and re-layouts  18.2 us (13%)
  between operations  8.96 us (7%)
    dot_general x32, matrix products, mixed(): jnp.einsum(pattern, former, latter, preferred_element_type=jnp.float32)  24.2 us
    ppermute x6, waiting for transfers between devices, scatter_cand(): lax.ppermute(piece, 'cand', [(j, (j + k) % count) for j in range(count)])  18.5 us
    ppermute x6, starting transfers between devices, scatter_cand(): lax.ppermute(piece, 'cand', [(j, (j + k) % count) for j in range(count)])  8.89 us
    ppermute x6, starting transfers between devices, gather_cand(): lax.ppermute(block, 'cand', [(j, (j + k) % count) for j in range(count)])  8.38 us
    ppermute x3, starting transfers between devices, sum_cand(): lax.ppermute(block, 'cand', [(j, (j + k) % count) for j in range(count)])  7.77 us
    ppermute x1, waiting for transfers between devices, local(): partner = lax.ppermute(reduced, 'query', swap)  6.25 us
    ppermute x1, waiting for transfers between devices, local(): lax.ppermute(jnp.concatenate([given_half.reshape(-1), cls_flat.reshape(-1...  5.41 us
    select_n x3, other arithmetic, gather_mp(): jnp.where(lax.axis_index('mp') == 0, jnp.concatenate([block, other], axis...  4.56 us
  transfers between devices with their start and end apart: 24, of which 8 were waited for; matrix products, arithmetic and copies ran while one was open for 45% of the time, Pallas kernels for 0%

profile of v13, /device:TPU:8, one launch (start us, length us, event | category | flops | bytes accessed | tf_op | source)
XLA Modules:
  0.0 134.9 jit_solution(9229954902235143708)
XLA Ops:
  1.4 1.6 %collective-permute-start = (f32[1,1,1025]{2,1,0:T(1,128)S(1)}, f32[1,1,1025]{2,1,0:T(1,128)S(1)}, u32[]{:S(2)}, u32[]{:S(2)}) collective-permute-start(f32[1,1,1025]{2,1,0:T(1,128)S(1)} %pad_maximum_fusion.4), channel_id=1, source_target_pairs={{0,4},{4,8},{8,12},{12,0},{1,5},{5,9},{9,13},{13,1},{2,6},{6,10},{... | collective-permute-start | bytes 12308 | tf_op jit(solution)/shard_map/ppermute | solution.py:60
  4.1 1.9 %collective-permute-start.2 = (f32[1,1,1025]{2,1,0:T(1,128)S(1)}, f32[1,1,1025]{2,1,0:T(1,128)S(1)}, u32[]{:S(2)}, u32[]{:S(2)}) collective-permute-start(f32[1,1,1025]{2,1,0:T(1,128)S(1)} %pad_maximum_fusion.4), channel_id=1, source_target_pairs={{0,12},{4,0},{8,4},{12,8},{1,13},{5,1},{9,5},{13,9},{2,14},{6,2},{... | collective-permute-start | bytes 12308 | tf_op jit(solution)/shard_map/ppermute | solution.py:60
  6.6 2.1 %fusion.5 = bf16[3,1,1,256,256]{3,4,0,2,1:T(8,128)(2,1)S(1)} fusion(bf16[3,1024,256]{2,1,0:T(8,128)(2,1)} %param.13, bf16[1,1,256,1024]{3,2,1,0:T(8,128)(2,1)} %param.10), kind=kOutput, calls=%fused_computation.15 | convolution fusion | flops 402849792 | bytes 2490368 | tf_op jit(solution)/shard_map/qcsd,kdf->kqcsf/dot_general | solution.py:15
  15.8 1.2 exponential_reduce_fusion
  17.8 2.0 %fusion.145 = (f32[256]{0:T(256)S(1)}, f32[1,1,256,1024]{3,2,1,0:T(8,128)S(1)}) fusion(bf16[256,1024]{1,0:T(8,128)(2,1)} %collective-permute-done.4, bf16[256,1024]{1,0:T(8,128)(2,1)S(1)} %copy-done.3, pred[]{:T(512)S(6)} %eq.54, bf16[256,256]{0,1:T(8,128)(2,1)S(1)} %bitcast.395, bf16[256,256]{0,1:T(8,128)(2,1)S(1)} %bitcast.394, ...), kind=kOutput, calls=%fused_computation.268 | convolution fusion | flops 275119872 | bytes 2884609 | tf_op jit(solution)/shard_map/qcsf,fd->qcsd/dot_general | solution.py:15
  20.3 1.7 %fusion.6 = bf16[2,1,1,256,256]{4,3,0,2,1:T(8,128)(2,1)S(1)} fusion(bf16[3,1024,256]{2,1,0:T(8,128)(2,1)} %param.16, bf16[1,1,256,1024]{3,2,1,0:T(8,128)(2,1)S(1)} %multiply_convert_fusion.1), kind=kOutput, calls=%fused_computation.20 | convolution fusion | flops 268566528 | bytes 1835008 | tf_op jit(solution)/shard_map/qcsd,kdf->kqcsf/dot_general | solution.py:15
  23.4 3.6 %collective-permute-start.6 = (bf16[1,1,512]{2,1,0:T(2,128)(2,1)}, bf16[1,1,512]{2,1,0:T(2,128)(2,1)}, u32[]{:S(2)}, u32[]{:S(2)}) collective-permute-start(bf16[1,1,512]{2,1,0:T(2,128)(2,1)} %pad_maximum_fusion.5), channel_id=1, source_target_pairs={{0,8},{4,12},{8,0},{12,4},{1,9},{5,13},{9,1},{13,5},{2,10},{6,14},... | collective-permute-start | bytes 3080 | tf_op jit(solution)/shard_map/ppermute | solution.py:60
  30.7 1.3 fusion.116
  32.0 1.3 fusion.182
  33.3 1.7 %copy.75 = bf16[1,1,1,256,256]{3,4,2,1,0:T(8,128)(2,1)} copy(bf16[1,1,1,256,256]{4,3,0,2,1:T(8,128)(2,1)} %get-tuple-element.28) | data formatting | bytes 262144 | tf_op jit(solution)/shard_map/slice | solution.py:181
  34.9 1.5 %collective-permute-start.19 = (bf16[256,1024]{1,0:T(8,128)(2,1)}, bf16[256,1024]{1,0:T(8,128)(2,1)}, u32[]{:S(2)}, u32[]{:S(2)}) collective-permute-start(bf16[256,1024]{1,0:T(8,128)(2,1)} %bitcast), channel_id=1, source_target_pairs={{0,2},{2,0},{1,3},{3,1},{4,6},{6,4},{5,7},{7,5},{8,10},{10,8},{9,1... | collective-permute-start | bytes 1572872 | tf_op jit(solution)/shard_map/ppermute | solution.py:149
  37.1 1.3 gather_fusion.1
  41.1 1.3 fusion.82
  45.5 1.3 convert_convert_fusion
  52.8 1.6 %fusion.16 = f32[1,1024]{1,0:T(1,128)S(1)} fusion(bf16[512,1]{0,1:T(2,128)(2,1)S(1)} %reshape.1233, bf16[256,1024]{1,0:T(8,128)(2,1)} %collective-permute-done.9, bf16[256,1024]{1,0:T(8,128)(2,1)S(1)} %copy-done.1, pred[]{:T(512)S(6)} %eq.54), kind=kOutput, calls=%fused_computation.38 | convolution fusion | flops 5767168 | bytes 1053697 | tf_op jit(solution)/shard_map/qcf,fd->qcd/dot_general | solution.py:15
  58.4 3.4 %collective-permute-start.10 = (f32[1]{0:T(128)}, f32[1]{0:T(128)}, u32[]{:S(2)}, u32[]{:S(2)}) collective-permute-start(f32[1]{0:T(128)} %bitcast.73), channel_id=1, source_target_pairs={{0,4},{4,8},{8,12},{12,0},{1,5},{5,9},{9,13},{13,1},{2,6},{6,10},{... | collective-permute-start | bytes 20 | tf_op jit(solution)/shard_map/ppermute | solution.py:75
  61.8 3.1 %collective-permute-start.11 = (f32[1]{0:T(128)}, f32[1]{0:T(128)}, u32[]{:S(2)}, u32[]{:S(2)}) collective-permute-start(f32[1]{0:T(128)} %bitcast.73), channel_id=1, source_target_pairs={{0,8},{4,12},{8,0},{12,4},{1,9},{5,13},{9,1},{13,5},{2,10},{6,14},... | collective-permute-start | bytes 20 | tf_op jit(solution)/shard_map/ppermute | solution.py:75
  64.9 1.3 collective-permute-start.12
  73.7 2.9 %collective-permute-start.14 = (f32[1,1,512]{2,1,0:T(1,128)S(1)}, f32[1,1,512]{2,1,0:T(1,128)S(1)}, u32[]{:S(2)}, u32[]{:S(2)}) collective-permute-start(f32[1,1,512]{2,1,0:T(1,128)S(1)} %get-tuple-element.36), channel_id=1, source_target_pairs={{0,8},{4,12},{8,0},{12,4},{1,9},{5,13},{9,1},{13,5},{2,10},{6,14},... | collective-permute-start | bytes 6152 | tf_op jit(solution)/shard_map/ppermute | solution.py:89
  78.2 1.9 %collective-permute-done.15 = f32[1,1,512]{2,1,0:T(1,128)S(1)} collective-permute-done((f32[1,1,512]{2,1,0:T(1,128)S(1)}, f32[1,1,512]{2,1,0:T(1,128)S(1)}, u32[]{:S(2)}, u32[]{:S(2)}) %collective-permute-start.15) | collective-permute-done | bytes 2080 | tf_op jit(solution)/shard_map/ppermute | solution.py:89
  82.9 1.3 maximum_select_fusion.5
  84.3 3.3 %maximum_select_fusion = bf16[3,1024,512]{2,1,0:T(8,128)(2,1)S(1)} fusion(bf16[3,1024,256]{2,1,0:T(8,128)(2,1)} %collective-permute-done.17, bf16[3,1024,256]{2,1,0:T(8,128)(2,1)} %param.16, pred[]{:T(512)S(6)} %eq.54), kind=kLoop, calls=%fused_computation.2 | loop fusion | flops 14155776 | bytes 6291457 | tf_op jit(solution)/shard_map/jit(_where)/select_n | solution.py:98
  89.6 1.6 %convolution_convert_fusion.3 = bf16[256,256]{0,1:T(8,128)(2,1)S(1)} fusion(bf16[256,1024]{1,0:T(8,128)(2,1)} %param.14, f32[1,1,256,1024]{3,2,1,0:T(8,128)S(1)} %get-tuple-element.48, f32[256,1024]{1,0:T(8,128)S(1)} %get-tuple-element.50, f32[256]{0:T(256)S(1)} %broadcast_multiply_fusion.1, f32[256]{0:T(256)S(1)} %broadcast_multiply_fusion.2, ...), kind=kOutput, calls=%fused_computation.23 | convolution fusion | flops 136118272 | bytes 2756608 | tf_op jit(solution)/shard_map/qcsd,fd->qcsf/dot_general | solution.py:15
  92.3 1.3 multiply_reduce_fusion
  97.2 1.6 %fusion.31 = f32[1024,384]{0,1:T(8,128)S(1)} fusion(bf16[4,1024]{1,0:T(4,128)(2,1)S(1)} %get-tuple-element.33, bf16[256,1024]{1,0:T(8,128)(2,1)} %bitcast, s32[]{:T(128)S(6)} %select_n.306, bf16[256,768]{0,1:T(8,128)(2,1)S(1)} %bitcast.341, bf16[4,768]{0,1:T(8,128)(2,1)S(1)} %copy.82), kind=kOutput, calls=%fused_computation.66 | convolution fusion | flops 205936640 | bytes 2504708 | tf_op jit(solution)/shard_map/rd,rf->df/dot_general | solution.py:15
  98.8 5.4 %collective-permute-done.18 = bf16[103936]{0:T(1024)(128)(2,1)S(1)} collective-permute-done((bf16[103936]{0:T(1024)(128)(2,1)S(1)}, bf16[103936]{0:T(1024)(128)(2,1)S(1)}, u32[]{:S(2)}, u32[]{:S(2)}) %collective-permute-start.18) | collective-permute-done | bytes 207904 | tf_op jit(solution)/shard_map/ppermute | solution.py:334
  104.4 1.4 %fusion.149 = f32[384,1024]{1,0:T(8,128)S(1)} fusion(bf16[256,384]{1,0:T(8,128)(2,1)S(1)} %slice.153, bf16[256,1024]{1,0:T(8,128)(2,1)} %collective-permute-done.19), kind=kOutput, calls=%fused_computation.272 | convolution fusion | flops 201326592 | bytes 2293760 | tf_op jit(solution)/shard_map/rd,rf->df/dot_general | solution.py:15
  106.8 2.9 %collective-permute-start.21 = (bf16[256,384]{0,1:T(8,128)(2,1)S(1)}, bf16[256,384]{0,1:T(8,128)(2,1)S(1)}, u32[]{:S(2)}, u32[]{:S(2)}) collective-permute-start(bf16[256,384]{0,1:T(8,128)(2,1)S(1)} %get-tuple-element.24), channel_id=1, source_target_pairs={{0,8},{4,12},{8,0},{12,4},{1,9},{5,13},{9,1},{13,5},{2,10},{6,14},... | collective-permute-start | bytes 589832 | tf_op jit(solution)/shard_map/ppermute | solution.py:89
  110.2 4.0 %collective-permute-done.20 = bf16[256,384]{0,1:T(8,128)(2,1)S(1)} collective-permute-done((bf16[256,384]{0,1:T(8,128)(2,1)S(1)}, bf16[256,384]{0,1:T(8,128)(2,1)S(1)}, u32[]{:S(2)}, u32[]{:S(2)}) %collective-permute-start.20) | collective-permute-done | bytes 196640 | tf_op jit(solution)/shard_map/ppermute | solution.py:89
  114.2 9.3 %collective-permute-done.21 = bf16[256,384]{0,1:T(8,128)(2,1)S(1)} collective-permute-done((bf16[256,384]{0,1:T(8,128)(2,1)S(1)}, bf16[256,384]{0,1:T(8,128)(2,1)S(1)}, u32[]{:S(2)}, u32[]{:S(2)}) %collective-permute-start.21) | collective-permute-done | bytes 196640 | tf_op jit(solution)/shard_map/ppermute | solution.py:89
  123.5 3.3 %collective-permute-done.22 = bf16[256,384]{0,1:T(8,128)(2,1)S(1)} collective-permute-done((bf16[256,384]{0,1:T(8,128)(2,1)S(1)}, bf16[256,384]{0,1:T(8,128)(2,1)S(1)}, u32[]{:S(2)}, u32[]{:S(2)}) %collective-permute-start.22) | collective-permute-done | bytes 196640 | tf_op jit(solution)/shard_map/ppermute | solution.py:89
  127.5 6.3 %collective-permute-done.23 = bf16[256,384]{0,1:T(8,128)(2,1)S(1)} collective-permute-done((bf16[256,384]{0,1:T(8,128)(2,1)S(1)}, bf16[256,384]{0,1:T(8,128)(2,1)S(1)}, u32[]{:S(2)}, u32[]{:S(2)}) %collective-permute-start.23) | collective-permute-done | bytes 196640 | tf_op jit(solution)/shard_map/ppermute | solution.py:345
  (281 shorter events, 46.3 us)
Async XLA Ops:
  1.4 8.9 %collective-permute-start = (f32[1,1,1025]{2,1,0:T(1,128)S(1)}, f32[1,1,1025]{2,1,0:T(1,128)S(1)}, u32[]{:S(2)}, u32[]{:S(2)}) collective-permute-start(f32[1,1,1025]{2,1,0:T(1,128)S(1)} %pad_maximum_fusion.4), channel_id=1, source_target_pairs={{0,4},{4,8},{8,12},{12,0},{1,5},{5,9},{9,13},{13,1},{2,6},{6,10},{... | collective-permute-start | bytes 12308 | tf_op jit(solution)/shard_map/ppermute | solution.py:60
  3.0 7.4 %collective-permute-start.1 = (f32[1,1,1025]{2,1,0:T(1,128)S(1)}, f32[1,1,1025]{2,1,0:T(1,128)S(1)}, u32[]{:S(2)}, u32[]{:S(2)}) collective-permute-start(f32[1,1,1025]{2,1,0:T(1,128)S(1)} %pad_maximum_fusion.4), channel_id=1, source_target_pairs={{0,8},{4,12},{8,0},{12,4},{1,9},{5,13},{9,1},{13,5},{2,10},{6,14},... | collective-permute-start | bytes 12308 | tf_op jit(solution)/shard_map/ppermute | solution.py:60
  4.1 6.3 %collective-permute-start.2 = (f32[1,1,1025]{2,1,0:T(1,128)S(1)}, f32[1,1,1025]{2,1,0:T(1,128)S(1)}, u32[]{:S(2)}, u32[]{:S(2)}) collective-permute-start(f32[1,1,1025]{2,1,0:T(1,128)S(1)} %pad_maximum_fusion.4), channel_id=1, source_target_pairs={{0,12},{4,0},{8,4},{12,8},{1,13},{5,1},{9,5},{13,9},{2,14},{6,2},{... | collective-permute-start | bytes 12308 | tf_op jit(solution)/shard_map/ppermute | solution.py:60
  6.1 11.7 %collective-permute-start.4 = (bf16[256,1024]{1,0:T(8,128)(2,1)}, bf16[256,1024]{1,0:T(8,128)(2,1)}, u32[]{:S(2)}, u32[]{:S(2)}) collective-permute-start(bf16[256,1024]{1,0:T(8,128)(2,1)} %param.14), channel_id=1, source_target_pairs={{0,1},{1,0},{2,3},{3,2},{4,5},{5,4},{6,7},{7,6},{8,9},{9,8},{10,11... | collective-permute-start | bytes 1572872 | tf_op jit(solution)/shard_map/ppermute | solution.py:97
  6.1 46.8 %collective-permute-start.9 = (bf16[256,1024]{1,0:T(8,128)(2,1)}, bf16[256,1024]{1,0:T(8,128)(2,1)}, u32[]{:S(2)}, u32[]{:S(2)}) collective-permute-start(bf16[256,1024]{1,0:T(8,128)(2,1)} %param.17), channel_id=1, source_target_pairs={{0,1},{1,0},{2,3},{3,2},{4,5},{5,4},{6,7},{7,6},{8,9},{9,8},{10,11... | collective-permute-start | bytes 1572872 | tf_op jit(solution)/shard_map/ppermute | solution.py:97
  10.3 74.0 %collective-permute-start.17 = (bf16[3,1024,256]{2,1,0:T(8,128)(2,1)}, bf16[3,1024,256]{2,1,0:T(8,128)(2,1)}, u32[]{:S(2)}, u32[]{:S(2)}) collective-permute-start(bf16[3,1024,256]{2,1,0:T(8,128)(2,1)} %param.16), channel_id=1, source_target_pairs={{0,1},{1,0},{2,3},{3,2},{4,5},{5,4},{6,7},{7,6},{8,9},{9,8},{10,11... | collective-permute-start | bytes 4718600 | tf_op jit(solution)/shard_map/ppermute | solution.py:97
  14.1 3.7 %collective-permute-start.3 = (bf16[1,1,256,256]{2,3,1,0:T(8,128)(2,1)S(1)}, bf16[1,1,256,256]{2,3,1,0:T(8,128)(2,1)S(1)}, u32[]{:S(2)}, u32[]{:S(2)}) collective-permute-start(bf16[1,1,256,256]{2,3,1,0:T(8,128)(2,1)S(1)} %bitcast.393), channel_id=1, source_target_pairs={{0,1},{1,0},{2,3},{3,2},{4,5},{5,4},{6,7},{7,6},{8,9},{9,8},{10,11... | collective-permute-start | bytes 393224 | tf_op jit(solution)/shard_map/ppermute | solution.py:97
  22.0 30.8 %copy-start.1 = (bf16[256,1024]{1,0:T(8,128)(2,1)S(1)}, bf16[256,1024]{1,0:T(8,128)(2,1)}, u32[]{:S(2)}) copy-start(bf16[256,1024]{1,0:T(8,128)(2,1)} %param.17) | copy-start | bytes 1572868
  23.4 11.6 %collective-permute-start.5 = (bf16[1,1,512]{2,1,0:T(2,128)(2,1)}, bf16[1,1,512]{2,1,0:T(2,128)(2,1)}, u32[]{:S(2)}, u32[]{:S(2)}) collective-permute-start(bf16[1,1,512]{2,1,0:T(2,128)(2,1)} %pad_maximum_fusion.5), channel_id=1, source_target_pairs={{0,4},{4,8},{8,12},{12,0},{1,5},{5,9},{9,13},{13,1},{2,6},{6,10},{... | collective-permute-start | bytes 3080 | tf_op jit(solution)/shard_map/ppermute | solution.py:60
  23.4 13.0 %collective-permute-start.6 = (bf16[1,1,512]{2,1,0:T(2,128)(2,1)}, bf16[1,1,512]{2,1,0:T(2,128)(2,1)}, u32[]{:S(2)}, u32[]{:S(2)}) collective-permute-start(bf16[1,1,512]{2,1,0:T(2,128)(2,1)} %pad_maximum_fusion.5), channel_id=1, source_target_pairs={{0,8},{4,12},{8,0},{12,4},{1,9},{5,13},{9,1},{13,5},{2,10},{6,14},... | collective-permute-start | bytes 3080 | tf_op jit(solution)/shard_map/ppermute | solution.py:60
  27.1 9.4 %collective-permute-start.7 = (bf16[1,1,512]{2,1,0:T(2,128)(2,1)}, bf16[1,1,512]{2,1,0:T(2,128)(2,1)}, u32[]{:S(2)}, u32[]{:S(2)}) collective-permute-start(bf16[1,1,512]{2,1,0:T(2,128)(2,1)} %pad_maximum_fusion.5), channel_id=1, source_target_pairs={{0,12},{4,0},{8,4},{12,8},{1,13},{5,1},{9,5},{13,9},{2,14},{6,2},{... | collective-permute-start | bytes 3080 | tf_op jit(solution)/shard_map/ppermute | solution.py:60
  34.9 69.5 %collective-permute-start.19 = (bf16[256,1024]{1,0:T(8,128)(2,1)}, bf16[256,1024]{1,0:T(8,128)(2,1)}, u32[]{:S(2)}, u32[]{:S(2)}) collective-permute-start(bf16[256,1024]{1,0:T(8,128)(2,1)} %bitcast), channel_id=1, source_target_pairs={{0,2},{2,0},{1,3},{3,1},{4,6},{6,4},{5,7},{7,5},{8,10},{10,8},{9,1... | collective-permute-start | bytes 1572872 | tf_op jit(solution)/shard_map/ppermute | solution.py:149
  50.8 1.2 collective-permute-start.8
  52.8 18.7 %copy-start.39 = (bf16[4,4,64]{2,1,0:T(4,128)(2,1)S(1)}, bf16[4,4,64]{2,1,0:T(4,128)(2,1)}, u32[]{:S(2)}) copy-start(bf16[4,4,64]{2,1,0:T(4,128)(2,1)} %copy-done.38) | copy-start | bytes 6148
  52.8 18.8 %copy-start.2 = (bf16[1,1,1,256,256]{3,4,2,1,0:T(8,128)(2,1)S(1)}, bf16[1,1,1,256,256]{3,4,2,1,0:T(8,128)(2,1)}, u32[]{:S(2)}) copy-start(bf16[1,1,1,256,256]{3,4,2,1,0:T(8,128)(2,1)} %copy.75) | copy-start | bytes 393220
  52.8 19.1 %copy-start.10 = (f32[4,4]{0,1:T(4,128)S(1)}, f32[4,4]{0,1:T(4,128)}, u32[]{:S(2)}) copy-start(f32[4,4]{0,1:T(4,128)} %copy-done.9) | copy-start | bytes 196
  52.8 19.3 %copy-start.11 = (f32[4,256]{1,0:T(4,128)S(1)}, f32[4,256]{1,0:T(4,128)}, u32[]{:S(2)}) copy-start(f32[4,256]{1,0:T(4,128)} %get-tuple-element.17) | copy-start | bytes 12292
  52.8 19.4 %copy-start.27 = (f32[4,4]{0,1:T(4,128)S(1)}, f32[4,4]{0,1:T(4,128)}, u32[]{:S(2)}) copy-start(f32[4,4]{0,1:T(4,128)} %get-tuple-element.13) | copy-start | bytes 196
  52.8 25.0 %copy-start.37 = (bf16[4,4,64]{2,1,0:T(4,128)(2,1)S(1)}, bf16[4,4,64]{2,1,0:T(4,128)(2,1)}, u32[]{:S(2)}) copy-start(bf16[4,4,64]{2,1,0:T(4,128)(2,1)} %copy-done.36) | copy-start | bytes 6148
  54.4 25.8 %copy-start.19 = (pred[256]{0:T(512)(128)(4,1)S(1)}, pred[256]{0:T(512)(128)(4,1)}, u32[]{:S(2)}) copy-start(pred[256]{0:T(512)(128)(4,1)} %copy-done.18) | copy-start | bytes 772
  58.4 7.8 %collective-permute-start.10 = (f32[1]{0:T(128)}, f32[1]{0:T(128)}, u32[]{:S(2)}, u32[]{:S(2)}) collective-permute-start(f32[1]{0:T(128)} %bitcast.73), channel_id=1, source_target_pairs={{0,4},{4,8},{8,12},{12,0},{1,5},{5,9},{9,13},{13,1},{2,6},{6,10},{... | collective-permute-start | bytes 20 | tf_op jit(solution)/shard_map/ppermute | solution.py:75
  61.8 5.1 %collective-permute-start.11 = (f32[1]{0:T(128)}, f32[1]{0:T(128)}, u32[]{:S(2)}, u32[]{:S(2)}) collective-permute-start(f32[1]{0:T(128)} %bitcast.73), channel_id=1, source_target_pairs={{0,8},{4,12},{8,0},{12,4},{1,9},{5,13},{9,1},{13,5},{2,10},{6,14},... | collective-permute-start | bytes 20 | tf_op jit(solution)/shard_map/ppermute | solution.py:75
  64.9 3.5 %collective-permute-start.12 = (f32[1]{0:T(128)}, f32[1]{0:T(128)}, u32[]{:S(2)}, u32[]{:S(2)}) collective-permute-start(f32[1]{0:T(128)} %bitcast.73), channel_id=1, source_target_pairs={{0,12},{4,0},{8,4},{12,8},{1,13},{5,1},{9,5},{13,9},{2,14},{6,2},{... | collective-permute-start | bytes 20 | tf_op jit(solution)/shard_map/ppermute | solution.py:75
  72.5 5.7 %collective-permute-start.13 = (f32[1,1,512]{2,1,0:T(1,128)S(1)}, f32[1,1,512]{2,1,0:T(1,128)S(1)}, u32[]{:S(2)}, u32[]{:S(2)}) collective-permute-start(f32[1,1,512]{2,1,0:T(1,128)S(1)} %get-tuple-element.34), channel_id=1, source_target_pairs={{0,4},{4,8},{8,12},{12,0},{1,5},{5,9},{9,13},{13,1},{2,6},{6,10},{... | collective-permute-start | bytes 6152 | tf_op jit(solution)/shard_map/ppermute | solution.py:89
  73.7 4.6 %collective-permute-start.14 = (f32[1,1,512]{2,1,0:T(1,128)S(1)}, f32[1,1,512]{2,1,0:T(1,128)S(1)}, u32[]{:S(2)}, u32[]{:S(2)}) collective-permute-start(f32[1,1,512]{2,1,0:T(1,128)S(1)} %get-tuple-element.36), channel_id=1, source_target_pairs={{0,8},{4,12},{8,0},{12,4},{1,9},{5,13},{9,1},{13,5},{2,10},{6,14},... | collective-permute-start | bytes 6152 | tf_op jit(solution)/shard_map/ppermute | solution.py:89
  76.6 3.6 %collective-permute-start.15 = (f32[1,1,512]{2,1,0:T(1,128)S(1)}, f32[1,1,512]{2,1,0:T(1,128)S(1)}, u32[]{:S(2)}, u32[]{:S(2)}) collective-permute-start(f32[1,1,512]{2,1,0:T(1,128)S(1)} %get-tuple-element.35), channel_id=1, source_target_pairs={{0,12},{4,0},{8,4},{12,8},{1,13},{5,1},{9,5},{13,9},{2,14},{6,2},{... | collective-permute-start | bytes 6152 | tf_op jit(solution)/shard_map/ppermute | solution.py:89
  80.4 2.5 %collective-permute-start.16 = (bf16[1,1,513,256]{2,3,1,0:T(8,128)(2,1)S(1)}, bf16[1,1,513,256]{2,3,1,0:T(8,128)(2,1)}, u32[]{:S(2)}, u32[]{:S(2)}) collective-permute-start(bf16[1,1,513,256]{2,3,1,0:T(8,128)(2,1)S(1)} %pad_maximum_fusion.1), channel_id=1, source_target_pairs={{0,1},{1,0},{2,3},{3,2},{4,5},{5,4},{6,7},{7,6},{8,9},{9,8},{10,11... | collective-permute-start | bytes 787976 | tf_op jit(solution)/shard_map/ppermute | solution.py:97
  96.6 7.6 %collective-permute-start.18 = (bf16[103936]{0:T(1024)(128)(2,1)S(1)}, bf16[103936]{0:T(1024)(128)(2,1)S(1)}, u32[]{:S(2)}, u32[]{:S(2)}) collective-permute-start(bf16[103936]{0:T(1024)(128)(2,1)S(1)} %pad_maximum_fusion.2), channel_id=1, source_target_pairs={{0,2},{2,0},{1,3},{3,1},{4,6},{6,4},{5,7},{7,5},{8,10},{10,8},{9,1... | collective-permute-start | bytes 623624 | tf_op jit(solution)/shard_map/ppermute | solution.py:334
  106.3 7.9 %collective-permute-start.20 = (bf16[256,384]{0,1:T(8,128)(2,1)S(1)}, bf16[256,384]{0,1:T(8,128)(2,1)S(1)}, u32[]{:S(2)}, u32[]{:S(2)}) collective-permute-start(bf16[256,384]{0,1:T(8,128)(2,1)S(1)} %get-tuple-element.22), channel_id=1, source_target_pairs={{0,4},{4,8},{8,12},{12,0},{1,5},{5,9},{9,13},{13,1},{2,6},{6,10},{... | collective-permute-start | bytes 589832 | tf_op jit(solution)/shard_map/ppermute | solution.py:89
  106.8 16.7 %collective-permute-start.21 = (bf16[256,384]{0,1:T(8,128)(2,1)S(1)}, bf16[256,384]{0,1:T(8,128)(2,1)S(1)}, u32[]{:S(2)}, u32[]{:S(2)}) collective-permute-start(bf16[256,384]{0,1:T(8,128)(2,1)S(1)} %get-tuple-element.24), channel_id=1, source_target_pairs={{0,8},{4,12},{8,0},{12,4},{1,9},{5,13},{9,1},{13,5},{2,10},{6,14},... | collective-permute-start | bytes 589832 | tf_op jit(solution)/shard_map/ppermute | solution.py:89
  109.7 17.1 %collective-permute-start.22 = (bf16[256,384]{0,1:T(8,128)(2,1)S(1)}, bf16[256,384]{0,1:T(8,128)(2,1)S(1)}, u32[]{:S(2)}, u32[]{:S(2)}) collective-permute-start(bf16[256,384]{0,1:T(8,128)(2,1)S(1)} %get-tuple-element.23), channel_id=1, source_target_pairs={{0,12},{4,0},{8,4},{12,8},{1,13},{5,1},{9,5},{13,9},{2,14},{6,2},{... | collective-permute-start | bytes 589832 | tf_op jit(solution)/shard_map/ppermute | solution.py:89
  126.9 6.8 %collective-permute-start.23 = (bf16[256,384]{0,1:T(8,128)(2,1)S(1)}, bf16[256,384]{0,1:T(8,128)(2,1)S(1)}, u32[]{:S(2)}, u32[]{:S(2)}) collective-permute-start(bf16[256,384]{0,1:T(8,128)(2,1)S(1)} %add_convert_fusion), channel_id=1, source_target_pairs={{0,2},{2,0},{1,3},{3,1},{4,6},{6,4},{5,7},{7,5},{8,10},{10,8},{9,1... | collective-permute-start | bytes 589832 | tf_op jit(solution)/shard_map/ppermute | solution.py:345
  (35 other events, 88.7 us)

commit v14 on v7

--- a/solution.py
+++ b/solution.py
@@ -89,6 +89,12 @@
         moved = lax.ppermute(piece, "cand", [(j, (j + k) % count) for j in range(count)])
         total = total + moved.astype(total_type)
     return total
+
+
+def sum_mp(block):
+    if lax.axis_size("mp") != 2:
+        return lax.psum(block, "mp")
+    return block + lax.ppermute(block, "mp", [(0, 1), (1, 0)])
 
 
 def sum_query(block):
@@ -123,9 +129,6 @@
     cross_valid = local_ids[:, None] != jnp.arange(cand_count)[None, :]
     head_shape = (lists, local_cands, seq_len, local_heads, HEAD_DIM)
     cls_shape = (lists, cand_count, local_heads, HEAD_DIM)
-    out_first_full = lax.all_gather(w_out_first, "mp", axis=0, tiled=True)
-    last_full = lax.all_gather(w_last, "mp", axis=2, tiled=True)
-    out_last_full = lax.all_gather(w_out_last, "mp", axis=0, tiled=True)
     cls_and_teacher = gather_cand(
         jnp.concatenate([tokens[:, :, 0].astype(jnp.float32), teacher[..., None]], -1), 1
     )
@@ -158,9 +161,8 @@
         first_mask[None, None, :, None, None], attended + attended_cls[:, :, None], attended
     )
     first_mixed = attended.reshape(lists, local_cands, seq_len, local_width).astype(jnp.bfloat16)
-    first_joined = lax.all_gather(first_mixed, "mp", axis=3, tiled=True)
-    residual_first = tokens.astype(jnp.float32) + mixed(
-        "qcsf,fd->qcsd", first_joined, out_first_full
+    residual_first = tokens.astype(jnp.float32) + sum_mp(
+        mixed("qcsf,fd->qcsd", first_mixed, w_out_first)
     )
     normed_first, unit_first, inverse_first = norm_forward(residual_first, gain_first)
     hidden = normed_first.astype(jnp.bfloat16)
@@ -187,9 +189,8 @@
         "qchd,qdhe->qche", cross_last_weight, cls_vals_last
     )
     last_mixed = attended_last.reshape(lists, local_cands, local_width).astype(jnp.bfloat16)
-    last_joined = lax.all_gather(last_mixed, "mp", axis=2, tiled=True)
-    residual_last = hidden[:, :, 0].astype(jnp.float32) + mixed(
-        "qcf,fd->qcd", last_joined, out_last_full
+    residual_last = hidden[:, :, 0].astype(jnp.float32) + sum_mp(
+        mixed("qcf,fd->qcd", last_mixed, w_out_last)
     )
     normed_last, unit_last, inverse_last = norm_forward(residual_last, gain_last)
     scores = jnp.einsum("qcd,d->qc", normed_last, w_score, precision=lax.Precision.HIGHEST)
@@ -248,20 +249,12 @@
     val_grad = jnp.where(first_cols, own_val_grad + back_vals[:, :, None], own_val_grad).astype(
         jnp.bfloat16
     )
-    joined = lax.all_gather(
-        jnp.concatenate([key_grad, val_grad, grad_query_last[:, :, None]], 2),
-        "mp",
-        axis=3,
-        tiled=True,
-    )
-    key_joined = joined[:, :, :seq_len]
-    val_joined = joined[:, :, seq_len : 2 * seq_len]
-    query_joined = joined[:, :, 2 * seq_len]
-    summed_term = mixed("qcsf,df->qcsd", key_joined, last_full[1]) + mixed(
-        "qcsf,df->qcsd", val_joined, last_full[2]
-    )
-    query_term = mixed("qcf,df->qcd", query_joined, last_full[0])
-    summed_term = jnp.where(first_cols, summed_term + query_term[:, :, None], summed_term)
+    partial_term = mixed("qcsf,df->qcsd", key_grad, w_last[1]) + mixed(
+        "qcsf,df->qcsd", val_grad, w_last[2]
+    )
+    query_term = mixed("qcf,df->qcd", grad_query_last, w_last[0])
+    partial_term = jnp.where(first_cols, partial_term + query_term[:, :, None], partial_term)
+    summed_term = sum_mp(partial_term)
     grad_hidden = jnp.where(first_cols, summed_term + grad_last[:, :, None], summed_term)
     grad_first = norm_backward(grad_hidden, unit_first, inverse_first, gain_first).astype(
         jnp.bfloat16

time: 139 us -> 168 us (1.21)
  the two profiles are of different devices: /device:TPU:8 before, /device:TPU:0 now
where the time goes in v14:
time: 168 us; the launch traced here: 166 us
  other arithmetic  41.6 us (25%)
  waiting for transfers between devices  30.4 us (18%)
  starting transfers between devices  29.7 us (18%)
  local copies, waits for them, and re-layouts  28.9 us (17%)
  matrix products  27.2 us (16%)
  between operations  8.64 us (5%)
    dot_general x32, matrix products, mixed(): jnp.einsum(pattern, former, latter, preferred_element_type=jnp.float32)  27.2 us
    ppermute x6, waiting for transfers between devices, scatter_cand(): lax.ppermute(piece, 'cand', [(j, (j + k) % count) for j in range(count)])  16.7 us
    ppermute x6, starting transfers between devices, gather_cand(): lax.ppermute(block, 'cand', [(j, (j + k) % count) for j in range(count)])  9.29 us
    ppermute x3, starting transfers between devices, sum_cand(): lax.ppermute(block, 'cand', [(j, (j + k) % count) for j in range(count)])  8.67 us
    ppermute x6, starting transfers between devices, scatter_cand(): lax.ppermute(piece, 'cand', [(j, (j + k) % count) for j in range(count)])  7.14 us
    another operation x10, other arithmetic  7.06 us
    another operation x9, local copies, waits for them, and re-layouts  6.29 us
    ppermute x1, waiting for transfers between devices, local(): lax.ppermute(jnp.concatenate([given_half.reshape(-1), cls_flat.reshape(-1...  5.34 us
  transfers between devices with their start and end apart: 21, of which 8 were waited for; matrix products, arithmetic and copies ran while one was open for 18% of the time, Pallas kernels for 0%

profile of v14, /device:TPU:0, one launch (start us, length us, event | category | flops | bytes accessed | tf_op | source)
XLA Modules:
  0.0 166.4 jit_solution(3539435866985032484)
XLA Ops:
  1.4 5.1 %collective-permute-start.2 = (f32[1,1,1025]{2,1,0:T(1,128)S(1)}, f32[1,1,1025]{2,1,0:T(1,128)S(1)}, u32[]{:S(2)}, u32[]{:S(2)}) collective-permute-start(f32[1,1,1025]{2,1,0:T(1,128)S(1)} %pad_maximum_fusion.3), channel_id=1, source_target_pairs={{0,12},{4,0},{8,4},{12,8},{1,13},{5,1},{9,5},{13,9},{2,14},{6,2},{... | collective-permute-start | bytes 12308 | tf_op jit(solution)/shard_map/ppermute | solution.py:60
  7.7 2.1 %fusion.4 = bf16[3,1,1,256,256]{3,4,0,2,1:T(8,128)(2,1)S(1)} fusion(bf16[3,1024,256]{2,1,0:T(8,128)(2,1)} %param.13, bf16[1,1,256,1024]{3,2,1,0:T(8,128)(2,1)} %param.10), kind=kOutput, calls=%fused_computation.13 | convolution fusion | flops 402849792 | bytes 2490368 | tf_op jit(solution)/shard_map/qcsd,kdf->kqcsf/dot_general | solution.py:15
  12.7 1.5 fusion.7
  19.1 1.9 %collective-permute-done.3 = f32[1,1,256,1024]{3,2,1,0:T(8,128)} collective-permute-done((f32[1,1,256,1024]{3,2,1,0:T(8,128)S(1)}, f32[1,1,256,1024]{3,2,1,0:T(8,128)}, u32[]{:S(2)}, u32[]{:S(2)}) %collective-permute-start.3) | collective-permute-done | bytes 1048608 | tf_op jit(solution)/shard_map/ppermute | solution.py:97
  21.0 1.8 %fusion.134 = (f32[256]{0:T(256)S(1)}, f32[1,1,256,1024]{3,2,1,0:T(8,128)S(1)}) fusion(f32[1,1,256,1024]{3,2,1,0:T(8,128)} %copy-done.1, f32[1,1,256,1024]{3,2,1,0:T(8,128)} %collective-permute-done.3, bf16[1,1,256,1024]{3,2,1,0:T(8,128)(2,1)S(1)} %copy-done.3), kind=kLoop, calls=%fused_computation.243 | loop fusion | flops 1048320 | bytes 3671040 | tf_op jit(solution)/shard_map/reduce_sum | solution.py:19
  26.1 2.0 %collective-permute-start.6 = (bf16[1,1,512]{2,1,0:T(2,128)(2,1)}, bf16[1,1,512]{2,1,0:T(2,128)(2,1)}, u32[]{:S(2)}, u32[]{:S(2)}) collective-permute-start(bf16[1,1,512]{2,1,0:T(2,128)(2,1)} %pad_maximum_fusion.4), channel_id=1, source_target_pairs={{0,12},{4,0},{8,4},{12,8},{1,13},{5,1},{9,5},{13,9},{2,14},{6,2},{... | collective-permute-start | bytes 3080 | tf_op jit(solution)/shard_map/ppermute | solution.py:60
  34.3 1.6 copy.85
  40.6 1.4 fusion.77
  52.7 1.9 %exponential_reduce_fusion = f32[]{:T(128)} fusion(f32[1,4,1025]{2,1,0:T(4,128)} %copy-done.7, f32[]{:T(128)} %slice_reduce_fusion), kind=kLoop, calls=%fused_computation.192 | loop fusion | flops 7 | bytes 24 | tf_op jit(solution)/shard_map/reduce_sum | solution.py:200
  58.4 1.4 fusion.133
  64.5 3.7 %collective-permute-start.8 = (f32[1]{0:T(128)}, f32[1]{0:T(128)}, u32[]{:S(2)}, u32[]{:S(2)}) collective-permute-start(f32[1]{0:T(128)} %bitcast.76), channel_id=1, source_target_pairs={{0,4},{4,8},{8,12},{12,0},{1,5},{5,9},{9,13},{13,1},{2,6},{6,10},{... | collective-permute-start | bytes 20 | tf_op jit(solution)/shard_map/ppermute | solution.py:75
  68.2 3.3 %collective-permute-start.9 = (f32[1]{0:T(128)}, f32[1]{0:T(128)}, u32[]{:S(2)}, u32[]{:S(2)}) collective-permute-start(f32[1]{0:T(128)} %bitcast.76), channel_id=1, source_target_pairs={{0,8},{4,12},{8,0},{12,4},{1,9},{5,13},{9,1},{13,5},{2,10},{6,14},... | collective-permute-start | bytes 20 | tf_op jit(solution)/shard_map/ppermute | solution.py:75
  71.5 1.6 collective-permute-start.10
  84.6 1.4 fusion.71
  92.5 1.5 multiply_multiply_fusion
  98.7 1.4 reshape.1132
  101.3 1.4 constant_dynamic-slice_fusion.5
  102.7 2.1 %collective-permute-start.13 = (f32[1,1,512]{2,1,0:T(1,128)}, f32[1,1,512]{2,1,0:T(1,128)}, u32[]{:S(2)}, u32[]{:S(2)}) collective-permute-start(f32[1,1,512]{2,1,0:T(1,128)} %get-tuple-element.39), channel_id=1, source_target_pairs={{0,12},{4,0},{8,4},{12,8},{1,13},{5,1},{9,5},{13,9},{2,14},{6,2},{... | collective-permute-start | bytes 6152 | tf_op jit(solution)/shard_map/ppermute | solution.py:89
  105.7 1.4 fusion.64
  112.2 1.6 fusion.22
  113.8 2.5 %fusion.2 = f32[1,1,256,1024]{3,2,1,0:T(8,128)} fusion(f32[256,1024]{1,0:T(8,128)S(1)} %fusion.22, f32[1024]{0:T(1024)S(1)} %bitcast.368, bf16[3,1024,256]{2,1,0:T(8,128)(2,1)} %param.16, pred[256]{0:T(512)(128)(4,1)S(1)} %copy-done.14, f32[1,1,256,1,1,1,1,256]{2,7,6,5,4,3,1,0:T(8,128)S(1)} %bitcast.347, f32[256]{0:T(256)S(1)} %bitcast.378), kind=kOutput, calls=%fused_computation.8 | convolution fusion | flops 135200768 | bytes 2889728 | tf_op jit(solution)/shard_map/qcsf,df->qcsd/dot_general | solution.py:15
  116.3 1.5 collective-permute-start.16
  119.3 2.1 %fusion.121 = (f32[256]{0:T(256)S(1)}, f32[256]{0:T(256)S(1)}, f32[1,1,256,1024]{3,2,1,0:T(8,128)S(1)}) fusion(f32[256]{0:T(256)S(1)} %copy-done.19, f32[1,1,256,1024]{3,2,1,0:T(8,128)S(1)} %get-tuple-element.25, f32[256]{0:T(256)S(1)} %copy-done.12, f32[1024]{0:T(1024)S(1)} %copy-done.17, f32[1024]{0:T(1024)S(1)} %bitcast.362, ...), kind=kLoop, calls=%fused_computation.237 | loop fusion | flops 2358784 | bytes 4206848 | tf_op jit(solution)/shard_map/reduce_sum | solution.py:29
  125.0 1.5 multiply_convert_fusion
  128.9 1.5 collective-permute-start.15
  130.9 5.3 %collective-permute-done.15 = bf16[103936]{0:T(1024)(128)(2,1)S(1)} collective-permute-done((bf16[103936]{0:T(1024)(128)(2,1)}, bf16[103936]{0:T(1024)(128)(2,1)S(1)}, u32[]{:S(2)}, u32[]{:S(2)}) %collective-permute-start.15) | collective-permute-done | bytes 207904 | tf_op jit(solution)/shard_map/ppermute | solution.py:321
  136.5 1.4 fusion.142
  138.4 3.3 %collective-permute-start.19 = (bf16[256,384]{0,1:T(8,128)(2,1)S(1)}, bf16[256,384]{0,1:T(8,128)(2,1)S(1)}, u32[]{:S(2)}, u32[]{:S(2)}) collective-permute-start(bf16[256,384]{0,1:T(8,128)(2,1)S(1)} %get-tuple-element.27), channel_id=1, source_target_pairs={{0,12},{4,0},{8,4},{12,8},{1,13},{5,1},{9,5},{13,9},{2,14},{6,2},{... | collective-permute-start | bytes 589832 | tf_op jit(solution)/shard_map/ppermute | solution.py:89
  142.6 4.5 %collective-permute-done.19 = bf16[256,384]{0,1:T(8,128)(2,1)S(1)} collective-permute-done((bf16[256,384]{0,1:T(8,128)(2,1)S(1)}, bf16[256,384]{0,1:T(8,128)(2,1)S(1)}, u32[]{:S(2)}, u32[]{:S(2)}) %collective-permute-start.19) | collective-permute-done | bytes 196640 | tf_op jit(solution)/shard_map/ppermute | solution.py:89
  147.2 12.2 %collective-permute-done.18 = bf16[256,384]{0,1:T(8,128)(2,1)S(1)} collective-permute-done((bf16[256,384]{0,1:T(8,128)(2,1)S(1)}, bf16[256,384]{0,1:T(8,128)(2,1)S(1)}, u32[]{:S(2)}, u32[]{:S(2)}) %collective-permute-start.18) | collective-permute-done | bytes 196640 | tf_op jit(solution)/shard_map/ppermute | solution.py:89
  159.4 1.6 collective-permute-start.20
  161.0 4.2 %collective-permute-done.20 = bf16[256,384]{0,1:T(8,128)(2,1)S(1)} collective-permute-done((bf16[256,384]{0,1:T(8,128)(2,1)S(1)}, bf16[256,384]{0,1:T(8,128)(2,1)S(1)}, u32[]{:S(2)}, u32[]{:S(2)}) %collective-permute-start.20) | collective-permute-done | bytes 196640 | tf_op jit(solution)/shard_map/ppermute | solution.py:332
  (255 shorter events, 76.1 us)
Async XLA Ops:
  0.0 17.8 %copy-start = (bf16[256,1024]{1,0:T(8,128)(2,1)S(1)}, bf16[256,1024]{1,0:T(8,128)(2,1)}, u32[]{:S(2)}) copy-start(bf16[256,1024]{1,0:T(8,128)(2,1)} %param.14) | copy-start | bytes 1572868
  1.4 9.7 %collective-permute-start.2 = (f32[1,1,1025]{2,1,0:T(1,128)S(1)}, f32[1,1,1025]{2,1,0:T(1,128)S(1)}, u32[]{:S(2)}, u32[]{:S(2)}) collective-permute-start(f32[1,1,1025]{2,1,0:T(1,128)S(1)} %pad_maximum_fusion.3), channel_id=1, source_target_pairs={{0,12},{4,0},{8,4},{12,8},{1,13},{5,1},{9,5},{13,9},{2,14},{6,2},{... | collective-permute-start | bytes 12308 | tf_op jit(solution)/shard_map/ppermute | solution.py:60
  6.5 4.6 %collective-permute-start.1 = (f32[1,1,1025]{2,1,0:T(1,128)S(1)}, f32[1,1,1025]{2,1,0:T(1,128)S(1)}, u32[]{:S(2)}, u32[]{:S(2)}) collective-permute-start(f32[1,1,1025]{2,1,0:T(1,128)S(1)} %pad_maximum_fusion.3), channel_id=1, source_target_pairs={{0,8},{4,12},{8,0},{12,4},{1,9},{5,13},{9,1},{13,5},{2,10},{6,14},... | collective-permute-start | bytes 12308 | tf_op jit(solution)/shard_map/ppermute | solution.py:60
  6.6 5.4 %collective-permute-start = (f32[1,1,1025]{2,1,0:T(1,128)S(1)}, f32[1,1,1025]{2,1,0:T(1,128)S(1)}, u32[]{:S(2)}, u32[]{:S(2)}) collective-permute-start(f32[1,1,1025]{2,1,0:T(1,128)S(1)} %pad_maximum_fusion.3), channel_id=1, source_target_pairs={{0,4},{4,8},{8,12},{12,0},{1,5},{5,9},{9,13},{13,1},{2,6},{6,10},{... | collective-permute-start | bytes 12308 | tf_op jit(solution)/shard_map/ppermute | solution.py:60
  7.6 36.7 %copy-start.15 = (pred[4]{0:T(512)(128)(4,1)}, pred[4]{0:T(512)(128)(4,1)S(1)}, u32[]{:S(2)}) copy-start(pred[4]{0:T(512)(128)(4,1)S(1)} %get-tuple-element.52) | copy-start | bytes 16
  9.8 7.1 %copy-start.5 = (bf16[1,1,1,256,256]{3,4,0,2,1:T(8,128)(2,1)}, bf16[1,1,1,256,256]{3,4,0,2,1:T(8,128)(2,1)S(1)}, u32[]{:S(2)}) copy-start(bf16[1,1,1,256,256]{3,4,0,2,1:T(8,128)(2,1)S(1)} %get-tuple-element.30) | copy-start | bytes 393220
  11.0 6.7 %copy-start.13 = (pred[256]{0:T(512)(128)(4,1)}, pred[256]{0:T(512)(128)(4,1)S(1)}, u32[]{:S(2)}) copy-start(pred[256]{0:T(512)(128)(4,1)S(1)} %iota_compare_fusion.1) | copy-start | bytes 772
  11.2 6.6 %copy-start.27 = (bf16[1,1,1,4,64]{4,3,2,1,0:T(4,128)(2,1)}, bf16[1,1,1,4,64]{4,3,2,1,0:T(4,128)(2,1)S(1)}, u32[]{:S(2)}) copy-start(bf16[1,1,1,4,64]{4,3,2,1,0:T(4,128)(2,1)S(1)} %copy.127) | copy-start | bytes 1540
  12.7 5.6 %copy-start.7 = (f32[1,4,1025]{2,1,0:T(4,128)}, f32[1,4,1025]{2,1,0:T(4,128)S(1)}, u32[]{:S(2)}) copy-start(f32[1,4,1025]{2,1,0:T(4,128)S(1)} %bitcast_select_fusion) | copy-start | bytes 49204
  18.1 2.9 %collective-permute-start.3 = (f32[1,1,256,1024]{3,2,1,0:T(8,128)S(1)}, f32[1,1,256,1024]{3,2,1,0:T(8,128)}, u32[]{:S(2)}, u32[]{:S(2)}) collective-permute-start(f32[1,1,256,1024]{3,2,1,0:T(8,128)S(1)} %convolution_bitcast_fusion), channel_id=1, source_target_pairs={{0,1},{1,0},{2,3},{3,2},{4,5},{5,4},{6,7},{7,6},{8,9},{9,8},{10,11... | collective-permute-start | bytes 3145736 | tf_op jit(solution)/shard_map/ppermute | solution.py:97
  26.1 9.8 %collective-permute-start.6 = (bf16[1,1,512]{2,1,0:T(2,128)(2,1)}, bf16[1,1,512]{2,1,0:T(2,128)(2,1)}, u32[]{:S(2)}, u32[]{:S(2)}) collective-permute-start(bf16[1,1,512]{2,1,0:T(2,128)(2,1)} %pad_maximum_fusion.4), channel_id=1, source_target_pairs={{0,12},{4,0},{8,4},{12,8},{1,13},{5,1},{9,5},{13,9},{2,14},{6,2},{... | collective-permute-start | bytes 3080 | tf_op jit(solution)/shard_map/ppermute | solution.py:60
  28.2 7.8 %collective-permute-start.5 = (bf16[1,1,512]{2,1,0:T(2,128)(2,1)}, bf16[1,1,512]{2,1,0:T(2,128)(2,1)}, u32[]{:S(2)}, u32[]{:S(2)}) collective-permute-start(bf16[1,1,512]{2,1,0:T(2,128)(2,1)} %pad_maximum_fusion.4), channel_id=1, source_target_pairs={{0,8},{4,12},{8,0},{12,4},{1,9},{5,13},{9,1},{13,5},{2,10},{6,14},... | collective-permute-start | bytes 3080 | tf_op jit(solution)/shard_map/ppermute | solution.py:60
  29.3 6.7 %collective-permute-start.4 = (bf16[1,1,512]{2,1,0:T(2,128)(2,1)}, bf16[1,1,512]{2,1,0:T(2,128)(2,1)}, u32[]{:S(2)}, u32[]{:S(2)}) collective-permute-start(bf16[1,1,512]{2,1,0:T(2,128)(2,1)} %pad_maximum_fusion.4), channel_id=1, source_target_pairs={{0,4},{4,8},{8,12},{12,0},{1,5},{5,9},{9,13},{13,1},{2,6},{6,10},{... | collective-permute-start | bytes 3080 | tf_op jit(solution)/shard_map/ppermute | solution.py:60
  47.0 28.9 %copy-start.10 = (f32[4,4]{0,1:T(4,128)}, f32[4,4]{0,1:T(4,128)S(1)}, u32[]{:S(2)}) copy-start(f32[4,4]{0,1:T(4,128)S(1)} %get-tuple-element.15) | copy-start | bytes 196
  52.7 5.8 %copy-start.22 = (f32[1,1,1024]{2,1,0:T(1,128)}, f32[1,1,1024]{2,1,0:T(1,128)S(1)}, u32[]{:S(2)}) copy-start(f32[1,1,1024]{2,1,0:T(1,128)S(1)} %convolution_bitcast_fusion.3) | copy-start | bytes 12292
  52.7 5.8 %collective-permute-start.7 = (f32[1,1,1024]{2,1,0:T(1,128)S(1)}, f32[1,1,1024]{2,1,0:T(1,128)}, u32[]{:S(2)}, u32[]{:S(2)}) collective-permute-start(f32[1,1,1024]{2,1,0:T(1,128)S(1)} %convolution_bitcast_fusion.3), channel_id=1, source_target_pairs={{0,1},{1,0},{2,3},{3,2},{4,5},{5,4},{6,7},{7,6},{8,9},{9,8},{10,11... | collective-permute-start | bytes 12296 | tf_op jit(solution)/shard_map/ppermute | solution.py:97
  64.5 8.7 %collective-permute-start.8 = (f32[1]{0:T(128)}, f32[1]{0:T(128)}, u32[]{:S(2)}, u32[]{:S(2)}) collective-permute-start(f32[1]{0:T(128)} %bitcast.76), channel_id=1, source_target_pairs={{0,4},{4,8},{8,12},{12,0},{1,5},{5,9},{9,13},{13,1},{2,6},{6,10},{... | collective-permute-start | bytes 20 | tf_op jit(solution)/shard_map/ppermute | solution.py:75
  68.2 5.5 %collective-permute-start.9 = (f32[1]{0:T(128)}, f32[1]{0:T(128)}, u32[]{:S(2)}, u32[]{:S(2)}) collective-permute-start(f32[1]{0:T(128)} %bitcast.76), channel_id=1, source_target_pairs={{0,8},{4,12},{8,0},{12,4},{1,9},{5,13},{9,1},{13,5},{2,10},{6,14},... | collective-permute-start | bytes 20 | tf_op jit(solution)/shard_map/ppermute | solution.py:75
  71.5 3.6 %collective-permute-start.10 = (f32[1]{0:T(128)}, f32[1]{0:T(128)}, u32[]{:S(2)}, u32[]{:S(2)}) collective-permute-start(f32[1]{0:T(128)} %bitcast.76), channel_id=1, source_target_pairs={{0,12},{4,0},{8,4},{12,8},{1,13},{5,1},{9,5},{13,9},{2,14},{6,2},{... | collective-permute-start | bytes 20 | tf_op jit(solution)/shard_map/ppermute | solution.py:75
  92.5 21.3 %copy-start.14 = (pred[256]{0:T(512)(128)(4,1)S(1)}, pred[256]{0:T(512)(128)(4,1)}, u32[]{:S(2)}) copy-start(pred[256]{0:T(512)(128)(4,1)} %copy-done.13) | copy-start | bytes 772
  102.7 8.7 %collective-permute-start.13 = (f32[1,1,512]{2,1,0:T(1,128)}, f32[1,1,512]{2,1,0:T(1,128)}, u32[]{:S(2)}, u32[]{:S(2)}) collective-permute-start(f32[1,1,512]{2,1,0:T(1,128)} %get-tuple-element.39), channel_id=1, source_target_pairs={{0,12},{4,0},{8,4},{12,8},{1,13},{5,1},{9,5},{13,9},{2,14},{6,2},{... | collective-permute-start | bytes 6152 | tf_op jit(solution)/shard_map/ppermute | solution.py:89
  104.9 6.6 %collective-permute-start.12 = (f32[1,1,512]{2,1,0:T(1,128)}, f32[1,1,512]{2,1,0:T(1,128)}, u32[]{:S(2)}, u32[]{:S(2)}) collective-permute-start(f32[1,1,512]{2,1,0:T(1,128)} %get-tuple-element.40), channel_id=1, source_target_pairs={{0,8},{4,12},{8,0},{12,4},{1,9},{5,13},{9,1},{13,5},{2,10},{6,14},... | collective-permute-start | bytes 6152 | tf_op jit(solution)/shard_map/ppermute | solution.py:89
  105.1 6.3 %collective-permute-start.11 = (f32[1,1,512]{2,1,0:T(1,128)}, f32[1,1,512]{2,1,0:T(1,128)}, u32[]{:S(2)}, u32[]{:S(2)}) collective-permute-start(f32[1,1,512]{2,1,0:T(1,128)} %get-tuple-element.38), channel_id=1, source_target_pairs={{0,4},{4,8},{8,12},{12,0},{1,5},{5,9},{9,13},{13,1},{2,6},{6,10},{... | collective-permute-start | bytes 6152 | tf_op jit(solution)/shard_map/ppermute | solution.py:89
  113.8 5.5 %copy-start.12 = (f32[256]{0:T(256)S(1)}, f32[256]{0:T(256)}, u32[]{:S(2)}) copy-start(f32[256]{0:T(256)} %copy-done.11) | copy-start | bytes 3076
  113.8 5.5 %copy-start.17 = (f32[1024]{0:T(1024)S(1)}, f32[1024]{0:T(1024)}, u32[]{:S(2)}) copy-start(f32[1024]{0:T(1024)} %param.15) | copy-start | bytes 12292
  116.3 3.0 %collective-permute-start.14 = (f32[1,1,256,1024]{3,2,1,0:T(8,128)}, f32[1,1,256,1024]{3,2,1,0:T(8,128)}, u32[]{:S(2)}, u32[]{:S(2)}) collective-permute-start(f32[1,1,256,1024]{3,2,1,0:T(8,128)} %fusion.2), channel_id=1, source_target_pairs={{0,1},{1,0},{2,3},{3,2},{4,5},{5,4},{6,7},{7,6},{8,9},{9,8},{10,11... | collective-permute-start | bytes 3145736 | tf_op jit(solution)/shard_map/ppermute | solution.py:97
  116.3 20.2 %collective-permute-start.16 = (bf16[256,1024]{1,0:T(8,128)(2,1)S(1)}, bf16[256,1024]{1,0:T(8,128)(2,1)}, u32[]{:S(2)}, u32[]{:S(2)}) collective-permute-start(bf16[256,1024]{1,0:T(8,128)(2,1)S(1)} %bitcast.339), channel_id=1, source_target_pairs={{0,2},{2,0},{1,3},{3,1},{4,6},{6,4},{5,7},{7,5},{8,10},{10,8},{9,1... | collective-permute-start | bytes 1572872 | tf_op jit(solution)/shard_map/ppermute | solution.py:141
  128.9 7.4 %collective-permute-start.15 = (bf16[103936]{0:T(1024)(128)(2,1)}, bf16[103936]{0:T(1024)(128)(2,1)S(1)}, u32[]{:S(2)}, u32[]{:S(2)}) collective-permute-start(bf16[103936]{0:T(1024)(128)(2,1)} %pad_maximum_fusion.1), channel_id=1, source_target_pairs={{0,2},{2,0},{1,3},{3,1},{4,6},{6,4},{5,7},{7,5},{8,10},{10,8},{9,1... | collective-permute-start | bytes 623624 | tf_op jit(solution)/shard_map/ppermute | solution.py:321
  138.4 8.7 %collective-permute-start.19 = (bf16[256,384]{0,1:T(8,128)(2,1)S(1)}, bf16[256,384]{0,1:T(8,128)(2,1)S(1)}, u32[]{:S(2)}, u32[]{:S(2)}) collective-permute-start(bf16[256,384]{0,1:T(8,128)(2,1)S(1)} %get-tuple-element.27), channel_id=1, source_target_pairs={{0,12},{4,0},{8,4},{12,8},{1,13},{5,1},{9,5},{13,9},{2,14},{6,2},{... | collective-permute-start | bytes 589832 | tf_op jit(solution)/shard_map/ppermute | solution.py:89
  141.8 17.6 %collective-permute-start.18 = (bf16[256,384]{0,1:T(8,128)(2,1)S(1)}, bf16[256,384]{0,1:T(8,128)(2,1)S(1)}, u32[]{:S(2)}, u32[]{:S(2)}) collective-permute-start(bf16[256,384]{0,1:T(8,128)(2,1)S(1)} %get-tuple-element.28), channel_id=1, source_target_pairs={{0,8},{4,12},{8,0},{12,4},{1,9},{5,13},{9,1},{13,5},{2,10},{6,14},... | collective-permute-start | bytes 589832 | tf_op jit(solution)/shard_map/ppermute | solution.py:89
  142.6 16.7 %collective-permute-start.17 = (bf16[256,384]{0,1:T(8,128)(2,1)S(1)}, bf16[256,384]{0,1:T(8,128)(2,1)S(1)}, u32[]{:S(2)}, u32[]{:S(2)}) collective-permute-start(bf16[256,384]{0,1:T(8,128)(2,1)S(1)} %get-tuple-element.26), channel_id=1, source_target_pairs={{0,4},{4,8},{8,12},{12,0},{1,5},{5,9},{9,13},{13,1},{2,6},{6,10},{... | collective-permute-start | bytes 589832 | tf_op jit(solution)/shard_map/ppermute | solution.py:89
  159.4 5.7 %collective-permute-start.20 = (bf16[256,384]{0,1:T(8,128)(2,1)S(1)}, bf16[256,384]{0,1:T(8,128)(2,1)S(1)}, u32[]{:S(2)}, u32[]{:S(2)}) collective-permute-start(bf16[256,384]{0,1:T(8,128)(2,1)S(1)} %add_convert_fusion), channel_id=1, source_target_pairs={{0,2},{2,0},{1,3},{3,1},{4,6},{6,4},{5,7},{7,5},{8,10},{10,8},{9,1... | collective-permute-start | bytes 589832 | tf_op jit(solution)/shard_map/ppermute | solution.py:332
  (26 other events, 53.4 us)

commit v15 on v8

--- a/solution.py
+++ b/solution.py
@@ -51,15 +51,20 @@
     return (own_exp / totals, cross_exp / totals)
 
 
+def shift_order(count):
+    return sorted(range(1, count), key=lambda k: min(k, count - k), reverse=True)
+
+
 def gather_cand(block, axis):
     count = lax.axis_size("cand")
     if count > 8:
         return lax.all_gather(block, "cand", axis=axis, tiled=True)
     me = lax.axis_index("cand")
-    parts = [block] + [
-        lax.ppermute(block, "cand", [(j, (j + k) % count) for j in range(count)])
-        for k in range(1, count)
-    ]
+    moved = {
+        k: lax.ppermute(block, "cand", [(j, (j + k) % count) for j in range(count)])
+        for k in shift_order(count)
+    }
+    parts = [block] + [moved[k] for k in range(1, count)]
     ordered = jnp.take(jnp.stack(parts, 0), (me - jnp.arange(count)) % count, axis=0)
     ordered = jnp.moveaxis(ordered, 0, axis)
     shape = block.shape[:axis] + (count * block.shape[axis],) + block.shape[axis + 1 :]
@@ -71,7 +76,7 @@
     if count > 8:
         return lax.psum(block, "cand")
     total = block
-    for k in range(1, count):
+    for k in shift_order(count):
         total = total + lax.ppermute(block, "cand", [(j, (j + k) % count) for j in range(count)])
     return total
 
@@ -84,7 +89,7 @@
     me = lax.axis_index("cand")
     width = block.shape[axis] // count
     total = lax.dynamic_slice_in_dim(block, me * width, width, axis).astype(total_type)
-    for k in range(1, count):
+    for k in shift_order(count):
         piece = lax.dynamic_slice_in_dim(block, ((me + k) % count) * width, width, axis)
         moved = lax.ppermute(piece, "cand", [(j, (j + k) % count) for j in range(count)])
         total = total + moved.astype(total_type)

time: 116 us -> 117 us (level)
  starting transfers between devices: 28.4 us -> 31.2 us
  waiting for transfers between devices: 30 us -> 27.5 us
    ppermute x6, starting transfers between devices: 8.88 us -> 11.7 us  [scatter_cand(): lax.ppermute(piece, 'cand', [(j, (j + k) % count) for j in range(count)])]
    ppermute x6, waiting for transfers between devices: 17.9 us -> 15.9 us  [scatter_cand(): lax.ppermute(piece, 'cand', [(j, (j + k) % count) for j in range(count)])]
where the time goes in v15:
time: 117 us; the launch traced here: 116 us
  starting transfers between devices  31.2 us (27%)
  waiting for transfers between devices  27.5 us (24%)
  matrix products  20.8 us (18%)
  other arithmetic  13.9 us (12%)
  between operations  8.49 us (7%)
  local copies, waits for them, and re-layouts  7.62 us (7%)
  blocking collectives  6.37 us (5%)
    dot_general x32, matrix products, mixed(): jnp.einsum(pattern, former, latter, preferred_element_type=jnp.float32)  20.8 us
    ppermute x6, waiting for transfers between devices, scatter_cand(): lax.ppermute(piece, 'cand', [(j, (j + k) % count) for j in range(count)])  15.9 us
    ppermute x6, starting transfers between devices, scatter_cand(): lax.ppermute(piece, 'cand', [(j, (j + k) % count) for j in range(count)])  11.7 us
    ppermute x6, starting transfers between devices, gather_cand(): lax.ppermute(block, 'cand', [(j, (j + k) % count) for j in range(count)])  8.45 us
    ppermute x3, starting transfers between devices, sum_cand(): lax.ppermute(block, 'cand', [(j, (j + k) % count) for j in range(count)])  7.78 us
    ppermute x1, waiting for transfers between devices, local(): partner = lax.ppermute(reduced, 'query', swap)  6.3 us
    ppermute x1, waiting for transfers between devices, local(): lax.ppermute(jnp.concatenate([given_half.reshape(-1), cls_flat.reshape(-1...  5.04 us
    select_n x1, other arithmetic, gather_mp(): jnp.where(lax.axis_index('mp') == 0, jnp.concatenate([block, other], axis...  3.41 us
  transfers between devices with their start and end apart: 21, of which 8 were waited for; matrix products, arithmetic and copies ran while one was open for 33% of the time, Pallas kernels for 0%

profile of v15, /device:TPU:8, one launch (start us, length us, event | category | flops | bytes accessed | tf_op | source)
XLA Modules:
  0.0 115.9 jit_solution(6285475584407185337)
XLA Ops:
  1.4 1.6 %collective-permute-start = (f32[1,1,1025]{2,1,0:T(1,128)S(1)}, f32[1,1,1025]{2,1,0:T(1,128)S(1)}, u32[]{:S(2)}, u32[]{:S(2)}) collective-permute-start(f32[1,1,1025]{2,1,0:T(1,128)S(1)} %pad_maximum_fusion.4), channel_id=1, source_target_pairs={{0,4},{4,8},{8,12},{12,0},{1,5},{5,9},{9,13},{13,1},{2,6},{6,10},{... | collective-permute-start | bytes 12308 | tf_op jit(solution)/shard_map/ppermute | solution.py:64
  3.0 1.1 collective-permute-start.1
  4.1 1.9 %collective-permute-start.2 = (f32[1,1,1025]{2,1,0:T(1,128)S(1)}, f32[1,1,1025]{2,1,0:T(1,128)S(1)}, u32[]{:S(2)}, u32[]{:S(2)}) collective-permute-start(f32[1,1,1025]{2,1,0:T(1,128)S(1)} %pad_maximum_fusion.4), channel_id=1, source_target_pairs={{0,12},{4,0},{8,4},{12,8},{1,13},{5,1},{9,5},{13,9},{2,14},{6,2},{... | collective-permute-start | bytes 12308 | tf_op jit(solution)/shard_map/ppermute | solution.py:64
  6.6 2.2 %fusion.5 = bf16[3,1,1,256,256]{3,4,0,2,1:T(8,128)(2,1)S(1)} fusion(bf16[3,1024,256]{2,1,0:T(8,128)(2,1)} %param.13, bf16[1,1,256,1024]{3,2,1,0:T(8,128)(2,1)} %param.10), kind=kOutput, calls=%fused_computation.15 | convolution fusion | flops 402849792 | bytes 2490368 | tf_op jit(solution)/shard_map/qcsd,kdf->kqcsf/dot_general | solution.py:15
  15.1 1.3 %exponential_reduce_fusion = f32[]{:T(128)} fusion(f32[1,4,1025]{2,1,0:T(4,128)S(1)} %bitcast_select_fusion, f32[]{:T(128)} %slice_reduce_fusion.2), kind=kLoop, calls=%fused_computation.203 | loop fusion | flops 7 | bytes 24 | tf_op jit(solution)/shard_map/reduce_sum | solution.py:215
  18.9 2.1 %all_gather.9 = bf16[1,1,256,512]{2,3,1,0:T(8,128)(2,1)S(1)} all-gather(bf16[1,1,256,256]{2,3,1,0:T(8,128)(2,1)S(1)} %bitcast.364), channel_id=1, replica_groups=mesh['groups'=2,'cand'=4,'query'=2,'mp'=2] {'mp'}, dimensions={3}, use_global_device_ids=true | all-gather | bytes 393216 | tf_op jit(solution)/shard_map/all_gather | solution.py:177
  21.0 1.9 %fusion.141 = (f32[256]{0:T(256)S(1)}, f32[1,1,256,1024]{3,2,1,0:T(8,128)S(1)}) fusion(bf16[256,1024]{1,0:T(8,128)(2,1)} %collective-permute-done.3, bf16[256,1024]{1,0:T(8,128)(2,1)S(1)} %copy-done.2, pred[]{:T(512)S(6)} %eq.51, bf16[1,1,256,512]{2,3,1,0:T(8,128)(2,1)S(1)} %all_gather.9, bf16[1,1,256,1024]{3,2,1,0:T(8,128)(2,1)} %param.10), kind=kOutput, calls=%fused_computation.261 | convolution fusion | flops 273940224 | bytes 2884609 | tf_op jit(solution)/shard_map/qcsf,fd->qcsd/dot_general | solution.py:15
  23.5 1.7 %fusion.6 = bf16[2,1,1,256,256]{4,3,0,2,1:T(8,128)(2,1)S(1)} fusion(bf16[3,1024,256]{2,1,0:T(8,128)(2,1)} %param.16, bf16[1,1,256,1024]{3,2,1,0:T(8,128)(2,1)S(1)} %multiply_convert_fusion.1), kind=kOutput, calls=%fused_computation.20 | convolution fusion | flops 268566528 | bytes 1835008 | tf_op jit(solution)/shard_map/qcsd,kdf->kqcsf/dot_general | solution.py:15
  25.4 3.6 %collective-permute-start.5 = (bf16[1,1,512]{2,1,0:T(2,128)(2,1)S(1)}, bf16[1,1,512]{2,1,0:T(2,128)(2,1)S(1)}, u32[]{:S(2)}, u32[]{:S(2)}) collective-permute-start(bf16[1,1,512]{2,1,0:T(2,128)(2,1)S(1)} %pad_maximum_fusion.5), channel_id=1, source_target_pairs={{0,8},{4,12},{8,0},{12,4},{1,9},{5,13},{9,1},{13,5},{2,10},{6,14},... | collective-permute-start | bytes 3080 | tf_op jit(solution)/shard_map/ppermute | solution.py:64
  29.1 1.2 %fusion.39 = f32[1,256]{1,0:T(1,128)S(1)} fusion(bf16[3,1024,256]{2,1,0:T(8,128)(2,1)} %param.16, bf16[1,1,256,1024]{3,2,1,0:T(8,128)(2,1)S(1)} %multiply_convert_fusion.1), kind=kOutput, calls=%fused_computation.72 | convolution fusion | flops 524288 | bytes 529408 | tf_op jit(solution)/shard_map/qcd,df->qcf/dot_general | solution.py:15
  31.0 1.6 %collective-permute-start.16 = (bf16[256,1024]{1,0:T(8,128)(2,1)}, bf16[256,1024]{1,0:T(8,128)(2,1)}, u32[]{:S(2)}, u32[]{:S(2)}) collective-permute-start(bf16[256,1024]{1,0:T(8,128)(2,1)} %bitcast), channel_id=1, source_target_pairs={{0,2},{2,0},{1,3},{3,1},{4,6},{6,4},{5,7},{7,5},{8,10},{10,8},{9,1... | collective-permute-start | bytes 1572872 | tf_op jit(solution)/shard_map/ppermute | solution.py:154
  34.8 1.8 %all_gather.10 = bf16[1,1,512]{2,1,0:T(2,128)(2,1)S(1)} all-gather(bf16[1,1,256]{2,1,0:T(2,128)(2,1)S(1)} %convert_element_type.264), channel_id=1, replica_groups=mesh['groups'=2,'cand'=4,'query'=2,'mp'=2] {'mp'}, dimensions={2}, use_global_device_ids=true | all-gather | bytes 1536 | tf_op jit(solution)/shard_map/all_gather | solution.py:206
  36.5 1.6 %fusion.16 = f32[1,1024]{1,0:T(1,128)S(1)} fusion(bf16[256,1024]{1,0:T(8,128)(2,1)} %collective-permute-done.7, bf16[256,1024]{1,0:T(8,128)(2,1)S(1)} %copy-done.1, pred[]{:T(512)S(6)} %eq.51, bf16[1,1,512]{2,1,0:T(2,128)(2,1)S(1)} %all_gather.10), kind=kOutput, calls=%fused_computation.38 | convolution fusion | flops 5767168 | bytes 1053697 | tf_op jit(solution)/shard_map/qcf,fd->qcd/dot_general | solution.py:15
  41.8 3.2 %collective-permute-start.8 = (f32[1]{0:T(128)}, f32[1]{0:T(128)}, u32[]{:S(2)}, u32[]{:S(2)}) collective-permute-start(f32[1]{0:T(128)} %bitcast.72), channel_id=1, source_target_pairs={{0,8},{4,12},{8,0},{12,4},{1,9},{5,13},{9,1},{13,5},{2,10},{6,14},... | collective-permute-start | bytes 20 | tf_op jit(solution)/shard_map/ppermute | solution.py:80
  45.0 2.3 %collective-permute-start.9 = (f32[1]{0:T(128)}, f32[1]{0:T(128)}, u32[]{:S(2)}, u32[]{:S(2)}) collective-permute-start(f32[1]{0:T(128)} %bitcast.72), channel_id=1, source_target_pairs={{0,4},{4,8},{8,12},{12,0},{1,5},{5,9},{9,13},{13,1},{2,6},{6,10},{... | collective-permute-start | bytes 20 | tf_op jit(solution)/shard_map/ppermute | solution.py:80
  47.3 2.3 %collective-permute-start.10 = (f32[1]{0:T(128)}, f32[1]{0:T(128)}, u32[]{:S(2)}, u32[]{:S(2)}) collective-permute-start(f32[1]{0:T(128)} %bitcast.72), channel_id=1, source_target_pairs={{0,12},{4,0},{8,4},{12,8},{1,13},{5,1},{9,5},{13,9},{2,14},{6,2},{... | collective-permute-start | bytes 20 | tf_op jit(solution)/shard_map/ppermute | solution.py:80
  55.0 4.8 %collective-permute-start.11 = (f32[1,1,512]{2,1,0:T(1,128)S(1)}, f32[1,1,512]{2,1,0:T(1,128)S(1)}, u32[]{:S(2)}, u32[]{:S(2)}) collective-permute-start(f32[1,1,512]{2,1,0:T(1,128)S(1)} %get-tuple-element.34), channel_id=1, source_target_pairs={{0,8},{4,12},{8,0},{12,4},{1,9},{5,13},{9,1},{13,5},{2,10},{6,14},... | collective-permute-start | bytes 6152 | tf_op jit(solution)/shard_map/ppermute | solution.py:94
  59.8 2.0 %collective-permute-start.13 = (f32[1,1,512]{2,1,0:T(1,128)S(1)}, f32[1,1,512]{2,1,0:T(1,128)S(1)}, u32[]{:S(2)}, u32[]{:S(2)}) collective-permute-start(f32[1,1,512]{2,1,0:T(1,128)S(1)} %get-tuple-element.35), channel_id=1, source_target_pairs={{0,12},{4,0},{8,4},{12,8},{1,13},{5,1},{9,5},{13,9},{2,14},{6,2},{... | collective-permute-start | bytes 6152 | tf_op jit(solution)/shard_map/ppermute | solution.py:94
  63.6 2.5 %all_gather.11 = bf16[1,1,513,512]{2,3,1,0:T(8,128)(2,1)S(1)} all-gather(bf16[1,1,513,256]{2,3,1,0:T(8,128)(2,1)S(1)} %pad_maximum_fusion.1), channel_id=1, replica_groups=mesh['groups'=2,'cand'=4,'query'=2,'mp'=2] {'mp'}, dimensions={3}, use_global_device_ids=true | all-gather | bytes 787968 | tf_op jit(solution)/shard_map/all_gather | solution.py:267
  66.2 3.4 %maximum_select_fusion = bf16[3,1024,512]{2,1,0:T(8,128)(2,1)S(1)} fusion(bf16[3,1024,256]{2,1,0:T(8,128)(2,1)} %collective-permute-done.14, bf16[3,1024,256]{2,1,0:T(8,128)(2,1)} %param.16, pred[]{:T(512)S(6)} %eq.51), kind=kLoop, calls=%fused_computation.2 | loop fusion | flops 14155776 | bytes 6291457 | tf_op jit(solution)/shard_map/jit(_where)/select_n | solution.py:103
  71.5 1.6 %convolution_convert_fusion.3 = bf16[256,256]{0,1:T(8,128)(2,1)S(1)} fusion(bf16[256,1024]{1,0:T(8,128)(2,1)} %param.14, f32[1,1,256,1024]{3,2,1,0:T(8,128)S(1)} %get-tuple-element.48, f32[256,1024]{1,0:T(8,128)S(1)} %get-tuple-element.50, f32[256]{0:T(256)S(1)} %broadcast_multiply_fusion.1, f32[256]{0:T(256)S(1)} %broadcast_multiply_fusion.2, ...), kind=kOutput, calls=%fused_computation.23 | convolution fusion | flops 136118272 | bytes 2756608 | tf_op jit(solution)/shard_map/qcsd,fd->qcsf/dot_general | solution.py:15
  74.2 1.3 %multiply_reduce_fusion = (f32[4,256]{1,0:T(4,128)S(1)}, f32[4,256,256]{1,2,0:T(8,128)S(1)}) fusion(f32[4,256]{1,0:T(4,128)} %copy-done.5, f32[4,256,256]{1,2,0:T(8,128)S(1)} %get-tuple-element.46, f32[4,256]{1,0:T(4,128)S(1)} %broadcast_select_fusion.2, bf16[256,4,64]{0,2,1:T(8,128)(2,1)S(1)} %bitcast.362, bf16[256,4,64]{0,2,1:T(8,128)(2,1)} %bitcast.366), kind=kOutput, calls=%fused_computation.50 | convolution fusion | flops 34601984 | bytes 2371584 | tf_op jit(solution)/shard_map/qcshe,qcthe->qchst/dot_general | solution.py:15
  79.0 1.6 %fusion.31 = f32[1024,384]{0,1:T(8,128)S(1)} fusion(bf16[4,1024]{1,0:T(4,128)(2,1)S(1)} %get-tuple-element.33, bf16[256,1024]{1,0:T(8,128)(2,1)} %bitcast, s32[]{:T(128)S(6)} %select_n.262, bf16[256,768]{0,1:T(8,128)(2,1)S(1)} %bitcast.346, bf16[4,768]{0,1:T(8,128)(2,1)S(1)} %copy.82), kind=kOutput, calls=%fused_computation.65 | convolution fusion | flops 205936640 | bytes 2504708 | tf_op jit(solution)/shard_map/rd,rf->df/dot_general | solution.py:15
  80.7 5.0 %collective-permute-done.15 = bf16[103936]{0:T(1024)(128)(2,1)S(1)} collective-permute-done((bf16[103936]{0:T(1024)(128)(2,1)S(1)}, bf16[103936]{0:T(1024)(128)(2,1)S(1)}, u32[]{:S(2)}, u32[]{:S(2)}) %collective-permute-start.15) | collective-permute-done | bytes 207904 | tf_op jit(solution)/shard_map/ppermute | solution.py:344
  85.9 1.4 %fusion.145 = f32[384,1024]{1,0:T(8,128)S(1)} fusion(bf16[256,384]{1,0:T(8,128)(2,1)S(1)} %slice.153, bf16[256,1024]{1,0:T(8,128)(2,1)} %collective-permute-done.16), kind=kOutput, calls=%fused_computation.265 | convolution fusion | flops 201326592 | bytes 2293760 | tf_op jit(solution)/shard_map/rd,rf->df/dot_general | solution.py:15
  87.8 2.8 %collective-permute-start.17 = (bf16[256,384]{0,1:T(8,128)(2,1)S(1)}, bf16[256,384]{0,1:T(8,128)(2,1)S(1)}, u32[]{:S(2)}, u32[]{:S(2)}) collective-permute-start(bf16[256,384]{0,1:T(8,128)(2,1)S(1)} %get-tuple-element.22), channel_id=1, source_target_pairs={{0,8},{4,12},{8,0},{12,4},{1,9},{5,13},{9,1},{13,5},{2,10},{6,14},... | collective-permute-start | bytes 589832 | tf_op jit(solution)/shard_map/ppermute | solution.py:94
  91.4 1.3 %collective-permute-start.19 = (bf16[256,384]{0,1:T(8,128)(2,1)S(1)}, bf16[256,384]{0,1:T(8,128)(2,1)S(1)}, u32[]{:S(2)}, u32[]{:S(2)}) collective-permute-start(bf16[256,384]{0,1:T(8,128)(2,1)S(1)} %get-tuple-element.23), channel_id=1, source_target_pairs={{0,12},{4,0},{8,4},{12,8},{1,13},{5,1},{9,5},{13,9},{2,14},{6,2},{... | collective-permute-start | bytes 589832 | tf_op jit(solution)/shard_map/ppermute | solution.py:94
  92.7 6.2 %collective-permute-done.17 = bf16[256,384]{0,1:T(8,128)(2,1)S(1)} collective-permute-done((bf16[256,384]{0,1:T(8,128)(2,1)S(1)}, bf16[256,384]{0,1:T(8,128)(2,1)S(1)}, u32[]{:S(2)}, u32[]{:S(2)}) %collective-permute-start.17) | collective-permute-done | bytes 196640 | tf_op jit(solution)/shard_map/ppermute | solution.py:94
  98.9 7.0 %collective-permute-done.18 = bf16[256,384]{0,1:T(8,128)(2,1)S(1)} collective-permute-done((bf16[256,384]{0,1:T(8,128)(2,1)S(1)}, bf16[256,384]{0,1:T(8,128)(2,1)S(1)}, u32[]{:S(2)}, u32[]{:S(2)}) %collective-permute-start.18) | collective-permute-done | bytes 196640 | tf_op jit(solution)/shard_map/ppermute | solution.py:94
  105.9 1.8 %collective-permute-done.19 = bf16[256,384]{0,1:T(8,128)(2,1)S(1)} collective-permute-done((bf16[256,384]{0,1:T(8,128)(2,1)S(1)}, bf16[256,384]{0,1:T(8,128)(2,1)S(1)}, u32[]{:S(2)}, u32[]{:S(2)}) %collective-permute-start.19) | collective-permute-done | bytes 196640 | tf_op jit(solution)/shard_map/ppermute | solution.py:94
  108.4 6.3 %collective-permute-done.20 = bf16[256,384]{0,1:T(8,128)(2,1)S(1)} collective-permute-done((bf16[256,384]{0,1:T(8,128)(2,1)S(1)}, bf16[256,384]{0,1:T(8,128)(2,1)S(1)}, u32[]{:S(2)}, u32[]{:S(2)}) %collective-permute-start.20) | collective-permute-done | bytes 196640 | tf_op jit(solution)/shard_map/ppermute | solution.py:355
  114.9 1.1 copy.84
  (227 shorter events, 25.8 us)
Async XLA Ops:
  1.4 10.0 %collective-permute-start = (f32[1,1,1025]{2,1,0:T(1,128)S(1)}, f32[1,1,1025]{2,1,0:T(1,128)S(1)}, u32[]{:S(2)}, u32[]{:S(2)}) collective-permute-start(f32[1,1,1025]{2,1,0:T(1,128)S(1)} %pad_maximum_fusion.4), channel_id=1, source_target_pairs={{0,4},{4,8},{8,12},{12,0},{1,5},{5,9},{9,13},{13,1},{2,6},{6,10},{... | collective-permute-start | bytes 12308 | tf_op jit(solution)/shard_map/ppermute | solution.py:64
  3.0 8.4 %collective-permute-start.1 = (f32[1,1,1025]{2,1,0:T(1,128)S(1)}, f32[1,1,1025]{2,1,0:T(1,128)S(1)}, u32[]{:S(2)}, u32[]{:S(2)}) collective-permute-start(f32[1,1,1025]{2,1,0:T(1,128)S(1)} %pad_maximum_fusion.4), channel_id=1, source_target_pairs={{0,8},{4,12},{8,0},{12,4},{1,9},{5,13},{9,1},{13,5},{2,10},{6,14},... | collective-permute-start | bytes 12308 | tf_op jit(solution)/shard_map/ppermute | solution.py:64
  4.1 7.3 %collective-permute-start.2 = (f32[1,1,1025]{2,1,0:T(1,128)S(1)}, f32[1,1,1025]{2,1,0:T(1,128)S(1)}, u32[]{:S(2)}, u32[]{:S(2)}) collective-permute-start(f32[1,1,1025]{2,1,0:T(1,128)S(1)} %pad_maximum_fusion.4), channel_id=1, source_target_pairs={{0,12},{4,0},{8,4},{12,8},{1,13},{5,1},{9,5},{13,9},{2,14},{6,2},{... | collective-permute-start | bytes 12308 | tf_op jit(solution)/shard_map/ppermute | solution.py:64
  6.1 15.0 %collective-permute-start.3 = (bf16[256,1024]{1,0:T(8,128)(2,1)}, bf16[256,1024]{1,0:T(8,128)(2,1)}, u32[]{:S(2)}, u32[]{:S(2)}) collective-permute-start(bf16[256,1024]{1,0:T(8,128)(2,1)} %param.14), channel_id=1, source_target_pairs={{0,1},{1,0},{2,3},{3,2},{4,5},{5,4},{6,7},{7,6},{8,9},{9,8},{10,11... | collective-permute-start | bytes 1572872 | tf_op jit(solution)/shard_map/ppermute | solution.py:102
  6.1 30.5 %collective-permute-start.7 = (bf16[256,1024]{1,0:T(8,128)(2,1)}, bf16[256,1024]{1,0:T(8,128)(2,1)}, u32[]{:S(2)}, u32[]{:S(2)}) collective-permute-start(bf16[256,1024]{1,0:T(8,128)(2,1)} %param.17), channel_id=1, source_target_pairs={{0,1},{1,0},{2,3},{3,2},{4,5},{5,4},{6,7},{7,6},{8,9},{9,8},{10,11... | collective-permute-start | bytes 1572872 | tf_op jit(solution)/shard_map/ppermute | solution.py:102
  6.6 5.4 %copy-start = (bf16[3,1024,256]{2,1,0:T(8,128)(2,1)S(1)}, bf16[3,1024,256]{2,1,0:T(8,128)(2,1)}, u32[]{:S(2)}) copy-start(bf16[3,1024,256]{2,1,0:T(8,128)(2,1)} %param.13) | copy-start | bytes 4718596
  8.9 14.0 %copy-start.3 = (bf16[1,1,1,256,256]{3,4,0,2,1:T(8,128)(2,1)}, bf16[1,1,1,256,256]{3,4,0,2,1:T(8,128)(2,1)S(1)}, u32[]{:S(2)}) copy-start(bf16[1,1,1,256,256]{3,4,0,2,1:T(8,128)(2,1)S(1)} %get-tuple-element.26) | copy-start | bytes 393220
  10.7 59.7 %copy-start.10 = (pred[256]{0:T(512)(128)(4,1)}, pred[256]{0:T(512)(128)(4,1)S(1)}, u32[]{:S(2)}) copy-start(pred[256]{0:T(512)(128)(4,1)S(1)} %iota_compare_fusion.1) | copy-start | bytes 772
  11.4 54.8 %collective-permute-start.14 = (bf16[3,1024,256]{2,1,0:T(8,128)(2,1)}, bf16[3,1024,256]{2,1,0:T(8,128)(2,1)}, u32[]{:S(2)}, u32[]{:S(2)}) collective-permute-start(bf16[3,1024,256]{2,1,0:T(8,128)(2,1)} %param.16), channel_id=1, source_target_pairs={{0,1},{1,0},{2,3},{3,2},{4,5},{5,4},{6,7},{7,6},{8,9},{9,8},{10,11... | collective-permute-start | bytes 4718600 | tf_op jit(solution)/shard_map/ppermute | solution.py:102
  12.4 2.5 %copy-start.16 = (bf16[4,4,64]{2,1,0:T(4,128)(2,1)}, bf16[4,4,64]{2,1,0:T(4,128)(2,1)S(1)}, u32[]{:S(2)}) copy-start(bf16[4,4,64]{2,1,0:T(4,128)(2,1)S(1)} %reshape.1066) | copy-start | bytes 6148
  14.2 9.2 %copy-start.5 = (f32[4,256]{1,0:T(4,128)}, f32[4,256]{1,0:T(4,128)S(1)}, u32[]{:S(2)}) copy-start(f32[4,256]{1,0:T(4,128)S(1)} %broadcast_select_fusion.1) | copy-start | bytes 12292
  15.1 3.8 %copy-start.18 = (bf16[4,4,64]{2,1,0:T(4,128)(2,1)}, bf16[4,4,64]{2,1,0:T(4,128)(2,1)S(1)}, u32[]{:S(2)}) copy-start(bf16[4,4,64]{2,1,0:T(4,128)(2,1)S(1)} %reshape.1069) | copy-start | bytes 6148
  22.9 47.5 %copy-start.9 = (f32[256]{0:T(256)}, f32[256]{0:T(256)S(1)}, u32[]{:S(2)}) copy-start(f32[256]{0:T(256)S(1)} %broadcast_multiply_fusion.3) | copy-start | bytes 3076
  23.2 47.2 %copy-start.12 = (f32[256]{0:T(256)}, f32[256]{0:T(256)S(1)}, u32[]{:S(2)}) copy-start(f32[256]{0:T(256)S(1)} %add_rsqrt_fusion) | copy-start | bytes 3076
  23.5 13.1 %copy-start.1 = (bf16[256,1024]{1,0:T(8,128)(2,1)S(1)}, bf16[256,1024]{1,0:T(8,128)(2,1)}, u32[]{:S(2)}) copy-start(bf16[256,1024]{1,0:T(8,128)(2,1)} %param.17) | copy-start | bytes 1572868
  25.3 5.7 %collective-permute-start.4 = (bf16[1,1,512]{2,1,0:T(2,128)(2,1)S(1)}, bf16[1,1,512]{2,1,0:T(2,128)(2,1)S(1)}, u32[]{:S(2)}, u32[]{:S(2)}) collective-permute-start(bf16[1,1,512]{2,1,0:T(2,128)(2,1)S(1)} %pad_maximum_fusion.5), channel_id=1, source_target_pairs={{0,4},{4,8},{8,12},{12,0},{1,5},{5,9},{9,13},{13,1},{2,6},{6,10},{... | collective-permute-start | bytes 3080 | tf_op jit(solution)/shard_map/ppermute | solution.py:64
  25.4 7.1 %collective-permute-start.5 = (bf16[1,1,512]{2,1,0:T(2,128)(2,1)S(1)}, bf16[1,1,512]{2,1,0:T(2,128)(2,1)S(1)}, u32[]{:S(2)}, u32[]{:S(2)}) collective-permute-start(bf16[1,1,512]{2,1,0:T(2,128)(2,1)S(1)} %pad_maximum_fusion.5), channel_id=1, source_target_pairs={{0,8},{4,12},{8,0},{12,4},{1,9},{5,13},{9,1},{13,5},{2,10},{6,14},... | collective-permute-start | bytes 3080 | tf_op jit(solution)/shard_map/ppermute | solution.py:64
  29.1 3.6 %collective-permute-start.6 = (bf16[1,1,512]{2,1,0:T(2,128)(2,1)S(1)}, bf16[1,1,512]{2,1,0:T(2,128)(2,1)S(1)}, u32[]{:S(2)}, u32[]{:S(2)}) collective-permute-start(bf16[1,1,512]{2,1,0:T(2,128)(2,1)S(1)} %pad_maximum_fusion.5), channel_id=1, source_target_pairs={{0,12},{4,0},{8,4},{12,8},{1,13},{5,1},{9,5},{13,9},{2,14},{6,2},{... | collective-permute-start | bytes 3080 | tf_op jit(solution)/shard_map/ppermute | solution.py:64
  31.0 54.9 %collective-permute-start.16 = (bf16[256,1024]{1,0:T(8,128)(2,1)}, bf16[256,1024]{1,0:T(8,128)(2,1)}, u32[]{:S(2)}, u32[]{:S(2)}) collective-permute-start(bf16[256,1024]{1,0:T(8,128)(2,1)} %bitcast), channel_id=1, source_target_pairs={{0,2},{2,0},{1,3},{3,1},{4,6},{6,4},{5,7},{7,5},{8,10},{10,8},{9,1... | collective-permute-start | bytes 1572872 | tf_op jit(solution)/shard_map/ppermute | solution.py:154
  34.5 6.1 %copy-start.7 = (f32[1024]{0:T(1024)S(1)}, f32[1024]{0:T(1024)}, u32[]{:S(2)}) copy-start(f32[1024]{0:T(1024)} %param.18) | copy-start | bytes 12292
  34.5 6.1 %copy-start.8 = (f32[1024]{0:T(1024)S(1)}, f32[1024]{0:T(1024)}, u32[]{:S(2)}) copy-start(f32[1024]{0:T(1024)} %param.19) | copy-start | bytes 12292
  41.8 7.8 %collective-permute-start.8 = (f32[1]{0:T(128)}, f32[1]{0:T(128)}, u32[]{:S(2)}, u32[]{:S(2)}) collective-permute-start(f32[1]{0:T(128)} %bitcast.72), channel_id=1, source_target_pairs={{0,8},{4,12},{8,0},{12,4},{1,9},{5,13},{9,1},{13,5},{2,10},{6,14},... | collective-permute-start | bytes 20 | tf_op jit(solution)/shard_map/ppermute | solution.py:80
  45.0 5.2 %collective-permute-start.9 = (f32[1]{0:T(128)}, f32[1]{0:T(128)}, u32[]{:S(2)}, u32[]{:S(2)}) collective-permute-start(f32[1]{0:T(128)} %bitcast.72), channel_id=1, source_target_pairs={{0,4},{4,8},{8,12},{12,0},{1,5},{5,9},{9,13},{13,1},{2,6},{6,10},{... | collective-permute-start | bytes 20 | tf_op jit(solution)/shard_map/ppermute | solution.py:80
  47.3 3.6 %collective-permute-start.10 = (f32[1]{0:T(128)}, f32[1]{0:T(128)}, u32[]{:S(2)}, u32[]{:S(2)}) collective-permute-start(f32[1]{0:T(128)} %bitcast.72), channel_id=1, source_target_pairs={{0,12},{4,0},{8,4},{12,8},{1,13},{5,1},{9,5},{13,9},{2,14},{6,2},{... | collective-permute-start | bytes 20 | tf_op jit(solution)/shard_map/ppermute | solution.py:80
  55.0 7.5 %collective-permute-start.11 = (f32[1,1,512]{2,1,0:T(1,128)S(1)}, f32[1,1,512]{2,1,0:T(1,128)S(1)}, u32[]{:S(2)}, u32[]{:S(2)}) collective-permute-start(f32[1,1,512]{2,1,0:T(1,128)S(1)} %get-tuple-element.34), channel_id=1, source_target_pairs={{0,8},{4,12},{8,0},{12,4},{1,9},{5,13},{9,1},{13,5},{2,10},{6,14},... | collective-permute-start | bytes 6152 | tf_op jit(solution)/shard_map/ppermute | solution.py:94
  59.7 3.6 %collective-permute-start.12 = (f32[1,1,512]{2,1,0:T(1,128)S(1)}, f32[1,1,512]{2,1,0:T(1,128)S(1)}, u32[]{:S(2)}, u32[]{:S(2)}) collective-permute-start(f32[1,1,512]{2,1,0:T(1,128)S(1)} %get-tuple-element.36), channel_id=1, source_target_pairs={{0,4},{4,8},{8,12},{12,0},{1,5},{5,9},{9,13},{13,1},{2,6},{6,10},{... | collective-permute-start | bytes 6152 | tf_op jit(solution)/shard_map/ppermute | solution.py:94
  59.8 3.6 %collective-permute-start.13 = (f32[1,1,512]{2,1,0:T(1,128)S(1)}, f32[1,1,512]{2,1,0:T(1,128)S(1)}, u32[]{:S(2)}, u32[]{:S(2)}) collective-permute-start(f32[1,1,512]{2,1,0:T(1,128)S(1)} %get-tuple-element.35), channel_id=1, source_target_pairs={{0,12},{4,0},{8,4},{12,8},{1,13},{5,1},{9,5},{13,9},{2,14},{6,2},{... | collective-permute-start | bytes 6152 | tf_op jit(solution)/shard_map/ppermute | solution.py:94
  78.4 7.3 %collective-permute-start.15 = (bf16[103936]{0:T(1024)(128)(2,1)S(1)}, bf16[103936]{0:T(1024)(128)(2,1)S(1)}, u32[]{:S(2)}, u32[]{:S(2)}) collective-permute-start(bf16[103936]{0:T(1024)(128)(2,1)S(1)} %pad_maximum_fusion.2), channel_id=1, source_target_pairs={{0,2},{2,0},{1,3},{3,1},{4,6},{6,4},{5,7},{7,5},{8,10},{10,8},{9,1... | collective-permute-start | bytes 623624 | tf_op jit(solution)/shard_map/ppermute | solution.py:344
  87.8 11.1 %collective-permute-start.17 = (bf16[256,384]{0,1:T(8,128)(2,1)S(1)}, bf16[256,384]{0,1:T(8,128)(2,1)S(1)}, u32[]{:S(2)}, u32[]{:S(2)}) collective-permute-start(bf16[256,384]{0,1:T(8,128)(2,1)S(1)} %get-tuple-element.22), channel_id=1, source_target_pairs={{0,8},{4,12},{8,0},{12,4},{1,9},{5,13},{9,1},{13,5},{2,10},{6,14},... | collective-permute-start | bytes 589832 | tf_op jit(solution)/shard_map/ppermute | solution.py:94
  90.7 15.3 %collective-permute-start.18 = (bf16[256,384]{0,1:T(8,128)(2,1)S(1)}, bf16[256,384]{0,1:T(8,128)(2,1)S(1)}, u32[]{:S(2)}, u32[]{:S(2)}) collective-permute-start(bf16[256,384]{0,1:T(8,128)(2,1)S(1)} %get-tuple-element.24), channel_id=1, source_target_pairs={{0,4},{4,8},{8,12},{12,0},{1,5},{5,9},{9,13},{13,1},{2,6},{6,10},{... | collective-permute-start | bytes 589832 | tf_op jit(solution)/shard_map/ppermute | solution.py:94
  91.4 16.4 %collective-permute-start.19 = (bf16[256,384]{0,1:T(8,128)(2,1)S(1)}, bf16[256,384]{0,1:T(8,128)(2,1)S(1)}, u32[]{:S(2)}, u32[]{:S(2)}) collective-permute-start(bf16[256,384]{0,1:T(8,128)(2,1)S(1)} %get-tuple-element.23), channel_id=1, source_target_pairs={{0,12},{4,0},{8,4},{12,8},{1,13},{5,1},{9,5},{13,9},{2,14},{6,2},{... | collective-permute-start | bytes 589832 | tf_op jit(solution)/shard_map/ppermute | solution.py:94
  107.8 6.9 %collective-permute-start.20 = (bf16[256,384]{0,1:T(8,128)(2,1)S(1)}, bf16[256,384]{0,1:T(8,128)(2,1)S(1)}, u32[]{:S(2)}, u32[]{:S(2)}) collective-permute-start(bf16[256,384]{0,1:T(8,128)(2,1)S(1)} %add_convert_fusion), channel_id=1, source_target_pairs={{0,2},{2,0},{1,3},{3,1},{4,6},{6,4},{5,7},{7,5},{8,10},{10,8},{9,1... | collective-permute-start | bytes 589832 | tf_op jit(solution)/shard_map/ppermute | solution.py:355
  (9 other events, 12.4 us)

commit v16 on v15

--- a/solution.py
+++ b/solution.py
@@ -351,7 +351,10 @@
         + mixed("rd,rf->df", other_tokens, other_half[:row_count])
         + mixed("rd,rf->df", other_cls, other_half[row_count:])
     )
-    reduced = scatter_cand(paired.astype(jnp.bfloat16), 0, jnp.float32).astype(jnp.bfloat16)
+    count = lax.axis_size("cand")
+    blocks = paired.astype(jnp.bfloat16).reshape(count, -1, half)
+    arrived = lax.all_to_all(blocks, "cand", 0, 0, tiled=False)
+    reduced = jnp.sum(arrived.astype(jnp.float32), 0).astype(jnp.bfloat16)
     partner = lax.ppermute(reduced, "query", swap)
     joined = jnp.where(
         side == 0,

time: 117 us -> 122 us (1.043)
  the two profiles are of different devices: /device:TPU:8 before, /device:TPU:0 now
where the time goes in v16:
time: 122 us; the launch traced here: 121 us
  blocking collectives  29.3 us (24%)
  starting transfers between devices  27.9 us (23%)
  matrix products  21.1 us (17%)
  other arithmetic  13.9 us (11%)
  waiting for transfers between devices  12.5 us (10%)
  between operations  8.5 us (7%)
  local copies, waits for them, and re-layouts  7.89 us (6%)
    all_to_all x1, blocking collectives, local(): arrived = lax.all_to_all(blocks, 'cand', 0, 0, tiled=False)  22.9 us
    dot_general x32, matrix products, mixed(): jnp.einsum(pattern, former, latter, preferred_element_type=jnp.float32)  21.1 us
    ppermute x6, starting transfers between devices, gather_cand(): lax.ppermute(block, 'cand', [(j, (j + k) % count) for j in range(count)])  10.9 us
    ppermute x3, starting transfers between devices, sum_cand(): lax.ppermute(block, 'cand', [(j, (j + k) % count) for j in range(count)])  9.8 us
    ppermute x1, waiting for transfers between devices, local(): partner = lax.ppermute(reduced, 'query', swap)  5.13 us
    ppermute x1, waiting for transfers between devices, local(): lax.ppermute(jnp.concatenate([given_half.reshape(-1), cls_flat.reshape(-1...  4.9 us
    ppermute x3, starting transfers between devices, scatter_cand(): lax.ppermute(piece, 'cand', [(j, (j + k) % count) for j in range(count)])  3.95 us
    select_n x1, other arithmetic, gather_mp(): jnp.where(lax.axis_index('mp') == 0, jnp.concatenate([block, other], axis...  3.41 us
  transfers between devices with their start and end apart: 18, of which 4 were waited for; matrix products, arithmetic and copies ran while one was open for 31% of the time, Pallas kernels for 0%

profile of v16, /device:TPU:0, one launch (start us, length us, event | category | flops | bytes accessed | tf_op | source)
XLA Modules:
  0.0 121.1 jit_solution(5987615206741228937)
XLA Ops:
  1.4 3.1 %collective-permute-start = (f32[1,1,1025]{2,1,0:T(1,128)S(1)}, f32[1,1,1025]{2,1,0:T(1,128)S(1)}, u32[]{:S(2)}, u32[]{:S(2)}) collective-permute-start(f32[1,1,1025]{2,1,0:T(1,128)S(1)} %pad_maximum_fusion.4), channel_id=1, source_target_pairs={{0,4},{4,8},{8,12},{12,0},{1,5},{5,9},{9,13},{13,1},{2,6},{6,10},{... | collective-permute-start | bytes 12308 | tf_op jit(solution)/shard_map/ppermute | solution.py:64
  4.5 2.6 %collective-permute-start.1 = (f32[1,1,1025]{2,1,0:T(1,128)S(1)}, f32[1,1,1025]{2,1,0:T(1,128)S(1)}, u32[]{:S(2)}, u32[]{:S(2)}) collective-permute-start(f32[1,1,1025]{2,1,0:T(1,128)S(1)} %pad_maximum_fusion.4), channel_id=1, source_target_pairs={{0,8},{4,12},{8,0},{12,4},{1,9},{5,13},{9,1},{13,5},{2,10},{6,14},... | collective-permute-start | bytes 12308 | tf_op jit(solution)/shard_map/ppermute | solution.py:64
  7.1 1.3 %collective-permute-start.2 = (f32[1,1,1025]{2,1,0:T(1,128)S(1)}, f32[1,1,1025]{2,1,0:T(1,128)S(1)}, u32[]{:S(2)}, u32[]{:S(2)}) collective-permute-start(f32[1,1,1025]{2,1,0:T(1,128)S(1)} %pad_maximum_fusion.4), channel_id=1, source_target_pairs={{0,12},{4,0},{8,4},{12,8},{1,13},{5,1},{9,5},{13,9},{2,14},{6,2},{... | collective-permute-start | bytes 12308 | tf_op jit(solution)/shard_map/ppermute | solution.py:64
  9.0 2.2 %fusion.5 = bf16[3,1,1,256,256]{3,4,0,2,1:T(8,128)(2,1)S(1)} fusion(bf16[3,1024,256]{2,1,0:T(8,128)(2,1)} %param.13, bf16[1,1,256,1024]{3,2,1,0:T(8,128)(2,1)} %param.10), kind=kOutput, calls=%fused_computation.15 | convolution fusion | flops 402849792 | bytes 2490368 | tf_op jit(solution)/shard_map/qcsd,kdf->kqcsf/dot_general | solution.py:15
  17.5 1.3 %exponential_reduce_fusion = f32[]{:T(128)} fusion(f32[1,4,1025]{2,1,0:T(4,128)S(1)} %bitcast_select_fusion, f32[]{:T(128)} %slice_reduce_fusion.2), kind=kLoop, calls=%fused_computation.193 | loop fusion | flops 7 | bytes 24 | tf_op jit(solution)/shard_map/reduce_sum | solution.py:215
  21.2 2.1 %all_gather.9 = bf16[1,1,256,512]{2,3,1,0:T(8,128)(2,1)S(1)} all-gather(bf16[1,1,256,256]{2,3,1,0:T(8,128)(2,1)S(1)} %bitcast.365), channel_id=1, replica_groups=mesh['groups'=2,'cand'=4,'query'=2,'mp'=2] {'mp'}, dimensions={3}, use_global_device_ids=true | all-gather | bytes 393216 | tf_op jit(solution)/shard_map/all_gather | solution.py:177
  23.4 1.9 %fusion.139 = (f32[256]{0:T(256)S(1)}, f32[1,1,256,1024]{3,2,1,0:T(8,128)S(1)}) fusion(bf16[256,1024]{1,0:T(8,128)(2,1)} %collective-permute-done.3, bf16[256,1024]{1,0:T(8,128)(2,1)S(1)} %copy-done.2, pred[]{:T(512)S(6)} %eq.48, bf16[1,1,256,512]{2,3,1,0:T(8,128)(2,1)S(1)} %all_gather.9, bf16[1,1,256,1024]{3,2,1,0:T(8,128)(2,1)} %param.10), kind=kOutput, calls=%fused_computation.255 | convolution fusion | flops 273940224 | bytes 2884609 | tf_op jit(solution)/shard_map/qcsf,fd->qcsd/dot_general | solution.py:15
  25.8 1.7 %fusion.6 = bf16[2,1,1,256,256]{4,3,0,2,1:T(8,128)(2,1)S(1)} fusion(bf16[3,1024,256]{2,1,0:T(8,128)(2,1)} %param.16, bf16[1,1,256,1024]{3,2,1,0:T(8,128)(2,1)S(1)} %multiply_convert_fusion.1), kind=kOutput, calls=%fused_computation.20 | convolution fusion | flops 268566528 | bytes 1835008 | tf_op jit(solution)/shard_map/qcsd,kdf->kqcsf/dot_general | solution.py:15
  27.6 0.7 collective-permute-start.4
  28.7 2.8 %collective-permute-start.6 = (bf16[1,1,512]{2,1,0:T(2,128)(2,1)S(1)}, bf16[1,1,512]{2,1,0:T(2,128)(2,1)S(1)}, u32[]{:S(2)}, u32[]{:S(2)}) collective-permute-start(bf16[1,1,512]{2,1,0:T(2,128)(2,1)S(1)} %pad_maximum_fusion.5), channel_id=1, source_target_pairs={{0,12},{4,0},{8,4},{12,8},{1,13},{5,1},{9,5},{13,9},{2,14},{6,2},{... | collective-permute-start | bytes 3080 | tf_op jit(solution)/shard_map/ppermute | solution.py:64
  31.5 1.2 %fusion.39 = f32[1,256]{1,0:T(1,128)S(1)} fusion(bf16[3,1024,256]{2,1,0:T(8,128)(2,1)} %param.16, bf16[1,1,256,1024]{3,2,1,0:T(8,128)(2,1)S(1)} %multiply_convert_fusion.1), kind=kOutput, calls=%fused_computation.72 | convolution fusion | flops 524288 | bytes 529408 | tf_op jit(solution)/shard_map/qcd,df->qcf/dot_general | solution.py:15
  33.4 1.6 %collective-permute-start.16 = (bf16[256,1024]{1,0:T(8,128)(2,1)}, bf16[256,1024]{1,0:T(8,128)(2,1)}, u32[]{:S(2)}, u32[]{:S(2)}) collective-permute-start(bf16[256,1024]{1,0:T(8,128)(2,1)} %bitcast), channel_id=1, source_target_pairs={{0,2},{2,0},{1,3},{3,1},{4,6},{6,4},{5,7},{7,5},{8,10},{10,8},{9,1... | collective-permute-start | bytes 1572872 | tf_op jit(solution)/shard_map/ppermute | solution.py:154
  37.1 1.8 %all_gather.10 = bf16[1,1,512]{2,1,0:T(2,128)(2,1)S(1)} all-gather(bf16[1,1,256]{2,1,0:T(2,128)(2,1)S(1)} %convert_element_type.251), channel_id=1, replica_groups=mesh['groups'=2,'cand'=4,'query'=2,'mp'=2] {'mp'}, dimensions={2}, use_global_device_ids=true | all-gather | bytes 1536 | tf_op jit(solution)/shard_map/all_gather | solution.py:206
  38.9 1.6 %fusion.16 = f32[1,1024]{1,0:T(1,128)S(1)} fusion(bf16[256,1024]{1,0:T(8,128)(2,1)} %collective-permute-done.7, bf16[256,1024]{1,0:T(8,128)(2,1)S(1)} %copy-done.1, pred[]{:T(512)S(6)} %eq.48, bf16[1,1,512]{2,1,0:T(2,128)(2,1)S(1)} %all_gather.10), kind=kOutput, calls=%fused_computation.38 | convolution fusion | flops 5767168 | bytes 1053697 | tf_op jit(solution)/shard_map/qcf,fd->qcd/dot_general | solution.py:15
  44.2 3.4 %collective-permute-start.8 = (f32[1]{0:T(128)}, f32[1]{0:T(128)}, u32[]{:S(2)}, u32[]{:S(2)}) collective-permute-start(f32[1]{0:T(128)} %bitcast.72), channel_id=1, source_target_pairs={{0,8},{4,12},{8,0},{12,4},{1,9},{5,13},{9,1},{13,5},{2,10},{6,14},... | collective-permute-start | bytes 20 | tf_op jit(solution)/shard_map/ppermute | solution.py:80
  47.5 1.7 %collective-permute-start.9 = (f32[1]{0:T(128)}, f32[1]{0:T(128)}, u32[]{:S(2)}, u32[]{:S(2)}) collective-permute-start(f32[1]{0:T(128)} %bitcast.72), channel_id=1, source_target_pairs={{0,4},{4,8},{8,12},{12,0},{1,5},{5,9},{9,13},{13,1},{2,6},{6,10},{... | collective-permute-start | bytes 20 | tf_op jit(solution)/shard_map/ppermute | solution.py:80
  49.3 4.7 %collective-permute-start.10 = (f32[1]{0:T(128)}, f32[1]{0:T(128)}, u32[]{:S(2)}, u32[]{:S(2)}) collective-permute-start(f32[1]{0:T(128)} %bitcast.72), channel_id=1, source_target_pairs={{0,12},{4,0},{8,4},{12,8},{1,13},{5,1},{9,5},{13,9},{2,14},{6,2},{... | collective-permute-start | bytes 20 | tf_op jit(solution)/shard_map/ppermute | solution.py:80
  59.3 3.5 %collective-permute-start.12 = (f32[1,1,512]{2,1,0:T(1,128)S(1)}, f32[1,1,512]{2,1,0:T(1,128)S(1)}, u32[]{:S(2)}, u32[]{:S(2)}) collective-permute-start(f32[1,1,512]{2,1,0:T(1,128)S(1)} %get-tuple-element.33), channel_id=1, source_target_pairs={{0,4},{4,8},{8,12},{12,0},{1,5},{5,9},{9,13},{13,1},{2,6},{6,10},{... | collective-permute-start | bytes 6152 | tf_op jit(solution)/shard_map/ppermute | solution.py:94
  63.9 0.9 collective-permute-done.12
  64.8 1.6 %collective-permute-done.13 = f32[1,1,512]{2,1,0:T(1,128)S(1)} collective-permute-done((f32[1,1,512]{2,1,0:T(1,128)S(1)}, f32[1,1,512]{2,1,0:T(1,128)S(1)}, u32[]{:S(2)}, u32[]{:S(2)}) %collective-permute-start.13) | collective-permute-done | bytes 2080 | tf_op jit(solution)/shard_map/ppermute | solution.py:94
  66.6 2.5 %all_gather.11 = bf16[1,1,513,512]{2,3,1,0:T(8,128)(2,1)S(1)} all-gather(bf16[1,1,513,256]{2,3,1,0:T(8,128)(2,1)S(1)} %pad_maximum_fusion.1), channel_id=1, replica_groups=mesh['groups'=2,'cand'=4,'query'=2,'mp'=2] {'mp'}, dimensions={3}, use_global_device_ids=true | all-gather | bytes 787968 | tf_op jit(solution)/shard_map/all_gather | solution.py:267
  69.2 3.4 %maximum_select_fusion = bf16[3,1024,512]{2,1,0:T(8,128)(2,1)S(1)} fusion(bf16[3,1024,256]{2,1,0:T(8,128)(2,1)} %collective-permute-done.14, bf16[3,1024,256]{2,1,0:T(8,128)(2,1)} %param.16, pred[]{:T(512)S(6)} %eq.48), kind=kLoop, calls=%fused_computation.2 | loop fusion | flops 14155776 | bytes 6291457 | tf_op jit(solution)/shard_map/jit(_where)/select_n | solution.py:103
  73.5 0.9 fusion.22
  74.5 1.6 %convolution_convert_fusion.3 = bf16[256,256]{0,1:T(8,128)(2,1)S(1)} fusion(bf16[256,1024]{1,0:T(8,128)(2,1)} %param.14, f32[1,1,256,1024]{3,2,1,0:T(8,128)S(1)} %get-tuple-element.45, f32[256,1024]{1,0:T(8,128)S(1)} %get-tuple-element.47, f32[256]{0:T(256)S(1)} %broadcast_multiply_fusion.1, f32[256]{0:T(256)S(1)} %broadcast_multiply_fusion.2, ...), kind=kOutput, calls=%fused_computation.23 | convolution fusion | flops 136118272 | bytes 2756608 | tf_op jit(solution)/shard_map/qcsd,fd->qcsf/dot_general | solution.py:15
  76.2 0.8 fusion.80
  77.2 1.3 %multiply_reduce_fusion = (f32[4,256]{1,0:T(4,128)S(1)}, f32[4,256,256]{1,2,0:T(8,128)S(1)}) fusion(f32[4,256]{1,0:T(4,128)} %copy-done.5, f32[4,256,256]{1,2,0:T(8,128)S(1)} %get-tuple-element.43, f32[4,256]{1,0:T(4,128)S(1)} %broadcast_select_fusion.2, bf16[256,4,64]{0,2,1:T(8,128)(2,1)S(1)} %bitcast.363, bf16[256,4,64]{0,2,1:T(8,128)(2,1)} %bitcast.367), kind=kOutput, calls=%fused_computation.50 | convolution fusion | flops 34601984 | bytes 2371584 | tf_op jit(solution)/shard_map/qcshe,qcthe->qchst/dot_general | solution.py:15
  82.0 1.8 %fusion.31 = f32[1024,384]{1,0:T(8,128)S(1)} fusion(bf16[4,1024]{1,0:T(4,128)(2,1)S(1)} %get-tuple-element.30, bf16[256,1024]{1,0:T(8,128)(2,1)} %bitcast, s32[]{:T(128)S(6)} %select_n.244, bf16[256,768]{0,1:T(8,128)(2,1)S(1)} %bitcast.346, bf16[4,768]{0,1:T(8,128)(2,1)S(1)} %copy.86), kind=kOutput, calls=%fused_computation.65 | convolution fusion | flops 205936640 | bytes 2504708 | tf_op jit(solution)/shard_map/rd,rf->df/dot_general | solution.py:15
  83.8 4.9 %collective-permute-done.15 = bf16[103936]{0:T(1024)(128)(2,1)S(1)} collective-permute-done((bf16[103936]{0:T(1024)(128)(2,1)S(1)}, bf16[103936]{0:T(1024)(128)(2,1)S(1)}, u32[]{:S(2)}, u32[]{:S(2)}) %collective-permute-start.15) | collective-permute-done | bytes 207904 | tf_op jit(solution)/shard_map/ppermute | solution.py:344
  88.9 1.5 %fusion.143 = f32[384,1024]{0,1:T(8,128)S(1)} fusion(bf16[256,384]{1,0:T(8,128)(2,1)S(1)} %slice.153, bf16[256,1024]{1,0:T(8,128)(2,1)} %collective-permute-done.16), kind=kOutput, calls=%fused_computation.259 | convolution fusion | flops 201326592 | bytes 2293760 | tf_op jit(solution)/shard_map/rd,rf->df/dot_general | solution.py:15
  90.8 22.9 %all_to_all.5 = bf16[4,256,384]{2,1,0:T(8,128)(2,1)S(1)} all-to-all(bf16[4,256,384]{2,1,0:T(8,128)(2,1)S(1)} %bitcast.348), channel_id=1, replica_groups=mesh['groups'=2,'cand'=4,'query'=2,'mp'=2] {'cand'}, dimensions={0} | all-to-all | bytes 1572864 | tf_op jit(solution)/shard_map/all_to_all | solution.py:356
  114.5 5.1 %collective-permute-done.17 = bf16[256,384]{1,0:T(8,128)(2,1)S(1)} collective-permute-done((bf16[256,384]{1,0:T(8,128)(2,1)S(1)}, bf16[256,384]{1,0:T(8,128)(2,1)S(1)}, u32[]{:S(2)}, u32[]{:S(2)}) %collective-permute-start.17) | collective-permute-done | bytes 196640 | tf_op jit(solution)/shard_map/ppermute | solution.py:358
  120.0 1.1 copy.90
  (222 shorter events, 23.1 us)
Async XLA Ops:
  1.4 12.3 %collective-permute-start = (f32[1,1,1025]{2,1,0:T(1,128)S(1)}, f32[1,1,1025]{2,1,0:T(1,128)S(1)}, u32[]{:S(2)}, u32[]{:S(2)}) collective-permute-start(f32[1,1,1025]{2,1,0:T(1,128)S(1)} %pad_maximum_fusion.4), channel_id=1, source_target_pairs={{0,4},{4,8},{8,12},{12,0},{1,5},{5,9},{9,13},{13,1},{2,6},{6,10},{... | collective-permute-start | bytes 12308 | tf_op jit(solution)/shard_map/ppermute | solution.py:64
  4.5 9.2 %collective-permute-start.1 = (f32[1,1,1025]{2,1,0:T(1,128)S(1)}, f32[1,1,1025]{2,1,0:T(1,128)S(1)}, u32[]{:S(2)}, u32[]{:S(2)}) collective-permute-start(f32[1,1,1025]{2,1,0:T(1,128)S(1)} %pad_maximum_fusion.4), channel_id=1, source_target_pairs={{0,8},{4,12},{8,0},{12,4},{1,9},{5,13},{9,1},{13,5},{2,10},{6,14},... | collective-permute-start | bytes 12308 | tf_op jit(solution)/shard_map/ppermute | solution.py:64
  7.1 6.7 %collective-permute-start.2 = (f32[1,1,1025]{2,1,0:T(1,128)S(1)}, f32[1,1,1025]{2,1,0:T(1,128)S(1)}, u32[]{:S(2)}, u32[]{:S(2)}) collective-permute-start(f32[1,1,1025]{2,1,0:T(1,128)S(1)} %pad_maximum_fusion.4), channel_id=1, source_target_pairs={{0,12},{4,0},{8,4},{12,8},{1,13},{5,1},{9,5},{13,9},{2,14},{6,2},{... | collective-permute-start | bytes 12308 | tf_op jit(solution)/shard_map/ppermute | solution.py:64
  8.4 15.0 %collective-permute-start.3 = (bf16[256,1024]{1,0:T(8,128)(2,1)}, bf16[256,1024]{1,0:T(8,128)(2,1)}, u32[]{:S(2)}, u32[]{:S(2)}) collective-permute-start(bf16[256,1024]{1,0:T(8,128)(2,1)} %param.14), channel_id=1, source_target_pairs={{0,1},{1,0},{2,3},{3,2},{4,5},{5,4},{6,7},{7,6},{8,9},{9,8},{10,11... | collective-permute-start | bytes 1572872 | tf_op jit(solution)/shard_map/ppermute | solution.py:102
  8.4 30.5 %collective-permute-start.7 = (bf16[256,1024]{1,0:T(8,128)(2,1)}, bf16[256,1024]{1,0:T(8,128)(2,1)}, u32[]{:S(2)}, u32[]{:S(2)}) collective-permute-start(bf16[256,1024]{1,0:T(8,128)(2,1)} %param.17), channel_id=1, source_target_pairs={{0,1},{1,0},{2,3},{3,2},{4,5},{5,4},{6,7},{7,6},{8,9},{9,8},{10,11... | collective-permute-start | bytes 1572872 | tf_op jit(solution)/shard_map/ppermute | solution.py:102
  9.0 5.4 %copy-start = (bf16[3,1024,256]{2,1,0:T(8,128)(2,1)S(1)}, bf16[3,1024,256]{2,1,0:T(8,128)(2,1)}, u32[]{:S(2)}) copy-start(bf16[3,1024,256]{2,1,0:T(8,128)(2,1)} %param.13) | copy-start | bytes 4718596
  11.3 14.0 %copy-start.3 = (bf16[1,1,1,256,256]{3,4,0,2,1:T(8,128)(2,1)}, bf16[1,1,1,256,256]{3,4,0,2,1:T(8,128)(2,1)S(1)}, u32[]{:S(2)}) copy-start(bf16[1,1,1,256,256]{3,4,0,2,1:T(8,128)(2,1)S(1)} %get-tuple-element.23) | copy-start | bytes 393220
  13.1 60.4 %copy-start.10 = (pred[256]{0:T(512)(128)(4,1)}, pred[256]{0:T(512)(128)(4,1)S(1)}, u32[]{:S(2)}) copy-start(pred[256]{0:T(512)(128)(4,1)S(1)} %iota_compare_fusion.1) | copy-start | bytes 772
  13.7 55.4 %collective-permute-start.14 = (bf16[3,1024,256]{2,1,0:T(8,128)(2,1)}, bf16[3,1024,256]{2,1,0:T(8,128)(2,1)}, u32[]{:S(2)}, u32[]{:S(2)}) collective-permute-start(bf16[3,1024,256]{2,1,0:T(8,128)(2,1)} %param.16), channel_id=1, source_target_pairs={{0,1},{1,0},{2,3},{3,2},{4,5},{5,4},{6,7},{7,6},{8,9},{9,8},{10,11... | collective-permute-start | bytes 4718600 | tf_op jit(solution)/shard_map/ppermute | solution.py:102
  14.7 2.5 %copy-start.16 = (bf16[4,4,64]{2,1,0:T(4,128)(2,1)}, bf16[4,4,64]{2,1,0:T(4,128)(2,1)S(1)}, u32[]{:S(2)}) copy-start(bf16[4,4,64]{2,1,0:T(4,128)(2,1)S(1)} %reshape.1069) | copy-start | bytes 6148
  16.6 9.2 %copy-start.5 = (f32[4,256]{1,0:T(4,128)}, f32[4,256]{1,0:T(4,128)S(1)}, u32[]{:S(2)}) copy-start(f32[4,256]{1,0:T(4,128)S(1)} %broadcast_select_fusion.1) | copy-start | bytes 12292
  17.4 3.8 %copy-start.18 = (bf16[4,4,64]{2,1,0:T(4,128)(2,1)}, bf16[4,4,64]{2,1,0:T(4,128)(2,1)S(1)}, u32[]{:S(2)}) copy-start(bf16[4,4,64]{2,1,0:T(4,128)(2,1)S(1)} %reshape.1072) | copy-start | bytes 6148
  20.9 2.5 %copy-start.2 = (bf16[256,1024]{1,0:T(8,128)(2,1)S(1)}, bf16[256,1024]{1,0:T(8,128)(2,1)}, u32[]{:S(2)}) copy-start(bf16[256,1024]{1,0:T(8,128)(2,1)} %param.14) | copy-start | bytes 1572868
  23.3 2.2 %copy-start.15 = (f32[1024]{0:T(1024)S(1)}, f32[1024]{0:T(1024)}, u32[]{:S(2)}) copy-start(f32[1024]{0:T(1024)} %param.15) | copy-start | bytes 12292
  25.3 48.1 %copy-start.9 = (f32[256]{0:T(256)}, f32[256]{0:T(256)S(1)}, u32[]{:S(2)}) copy-start(f32[256]{0:T(256)S(1)} %broadcast_multiply_fusion.3) | copy-start | bytes 3076
  25.6 47.9 %copy-start.12 = (f32[256]{0:T(256)}, f32[256]{0:T(256)S(1)}, u32[]{:S(2)}) copy-start(f32[256]{0:T(256)S(1)} %add_rsqrt_fusion) | copy-start | bytes 3076
  25.8 13.1 %copy-start.1 = (bf16[256,1024]{1,0:T(8,128)(2,1)S(1)}, bf16[256,1024]{1,0:T(8,128)(2,1)}, u32[]{:S(2)}) copy-start(bf16[256,1024]{1,0:T(8,128)(2,1)} %param.17) | copy-start | bytes 1572868
  27.6 5.8 %collective-permute-start.4 = (bf16[1,1,512]{2,1,0:T(2,128)(2,1)S(1)}, bf16[1,1,512]{2,1,0:T(2,128)(2,1)S(1)}, u32[]{:S(2)}, u32[]{:S(2)}) collective-permute-start(bf16[1,1,512]{2,1,0:T(2,128)(2,1)S(1)} %pad_maximum_fusion.5), channel_id=1, source_target_pairs={{0,4},{4,8},{8,12},{12,0},{1,5},{5,9},{9,13},{13,1},{2,6},{6,10},{... | collective-permute-start | bytes 3080 | tf_op jit(solution)/shard_map/ppermute | solution.py:64
  28.4 6.6 %collective-permute-start.5 = (bf16[1,1,512]{2,1,0:T(2,128)(2,1)S(1)}, bf16[1,1,512]{2,1,0:T(2,128)(2,1)S(1)}, u32[]{:S(2)}, u32[]{:S(2)}) collective-permute-start(bf16[1,1,512]{2,1,0:T(2,128)(2,1)S(1)} %pad_maximum_fusion.5), channel_id=1, source_target_pairs={{0,8},{4,12},{8,0},{12,4},{1,9},{5,13},{9,1},{13,5},{2,10},{6,14},... | collective-permute-start | bytes 3080 | tf_op jit(solution)/shard_map/ppermute | solution.py:64
  28.7 6.3 %collective-permute-start.6 = (bf16[1,1,512]{2,1,0:T(2,128)(2,1)S(1)}, bf16[1,1,512]{2,1,0:T(2,128)(2,1)S(1)}, u32[]{:S(2)}, u32[]{:S(2)}) collective-permute-start(bf16[1,1,512]{2,1,0:T(2,128)(2,1)S(1)} %pad_maximum_fusion.5), channel_id=1, source_target_pairs={{0,12},{4,0},{8,4},{12,8},{1,13},{5,1},{9,5},{13,9},{2,14},{6,2},{... | collective-permute-start | bytes 3080 | tf_op jit(solution)/shard_map/ppermute | solution.py:64
  33.4 55.4 %collective-permute-start.16 = (bf16[256,1024]{1,0:T(8,128)(2,1)}, bf16[256,1024]{1,0:T(8,128)(2,1)}, u32[]{:S(2)}, u32[]{:S(2)}) collective-permute-start(bf16[256,1024]{1,0:T(8,128)(2,1)} %bitcast), channel_id=1, source_target_pairs={{0,2},{2,0},{1,3},{3,1},{4,6},{6,4},{5,7},{7,5},{8,10},{10,8},{9,1... | collective-permute-start | bytes 1572872 | tf_op jit(solution)/shard_map/ppermute | solution.py:154
  36.9 6.1 %copy-start.7 = (f32[1024]{0:T(1024)S(1)}, f32[1024]{0:T(1024)}, u32[]{:S(2)}) copy-start(f32[1024]{0:T(1024)} %param.18) | copy-start | bytes 12292
  36.9 6.1 %copy-start.8 = (f32[1024]{0:T(1024)S(1)}, f32[1024]{0:T(1024)}, u32[]{:S(2)}) copy-start(f32[1024]{0:T(1024)} %param.19) | copy-start | bytes 12292
  44.2 9.8 %collective-permute-start.8 = (f32[1]{0:T(128)}, f32[1]{0:T(128)}, u32[]{:S(2)}, u32[]{:S(2)}) collective-permute-start(f32[1]{0:T(128)} %bitcast.72), channel_id=1, source_target_pairs={{0,8},{4,12},{8,0},{12,4},{1,9},{5,13},{9,1},{13,5},{2,10},{6,14},... | collective-permute-start | bytes 20 | tf_op jit(solution)/shard_map/ppermute | solution.py:80
  47.5 7.0 %collective-permute-start.9 = (f32[1]{0:T(128)}, f32[1]{0:T(128)}, u32[]{:S(2)}, u32[]{:S(2)}) collective-permute-start(f32[1]{0:T(128)} %bitcast.72), channel_id=1, source_target_pairs={{0,4},{4,8},{8,12},{12,0},{1,5},{5,9},{9,13},{13,1},{2,6},{6,10},{... | collective-permute-start | bytes 20 | tf_op jit(solution)/shard_map/ppermute | solution.py:80
  49.3 5.9 %collective-permute-start.10 = (f32[1]{0:T(128)}, f32[1]{0:T(128)}, u32[]{:S(2)}, u32[]{:S(2)}) collective-permute-start(f32[1]{0:T(128)} %bitcast.72), channel_id=1, source_target_pairs={{0,12},{4,0},{8,4},{12,8},{1,13},{5,1},{9,5},{13,9},{2,14},{6,2},{... | collective-permute-start | bytes 20 | tf_op jit(solution)/shard_map/ppermute | solution.py:80
  59.2 4.6 %collective-permute-start.11 = (f32[1,1,512]{2,1,0:T(1,128)S(1)}, f32[1,1,512]{2,1,0:T(1,128)S(1)}, u32[]{:S(2)}, u32[]{:S(2)}) collective-permute-start(f32[1,1,512]{2,1,0:T(1,128)S(1)} %get-tuple-element.31), channel_id=1, source_target_pairs={{0,8},{4,12},{8,0},{12,4},{1,9},{5,13},{9,1},{13,5},{2,10},{6,14},... | collective-permute-start | bytes 6152 | tf_op jit(solution)/shard_map/ppermute | solution.py:94
  59.3 5.4 %collective-permute-start.12 = (f32[1,1,512]{2,1,0:T(1,128)S(1)}, f32[1,1,512]{2,1,0:T(1,128)S(1)}, u32[]{:S(2)}, u32[]{:S(2)}) collective-permute-start(f32[1,1,512]{2,1,0:T(1,128)S(1)} %get-tuple-element.33), channel_id=1, source_target_pairs={{0,4},{4,8},{8,12},{12,0},{1,5},{5,9},{9,13},{13,1},{2,6},{6,10},{... | collective-permute-start | bytes 6152 | tf_op jit(solution)/shard_map/ppermute | solution.py:94
  62.8 3.6 %collective-permute-start.13 = (f32[1,1,512]{2,1,0:T(1,128)S(1)}, f32[1,1,512]{2,1,0:T(1,128)S(1)}, u32[]{:S(2)}, u32[]{:S(2)}) collective-permute-start(f32[1,1,512]{2,1,0:T(1,128)S(1)} %get-tuple-element.32), channel_id=1, source_target_pairs={{0,12},{4,0},{8,4},{12,8},{1,13},{5,1},{9,5},{13,9},{2,14},{6,2},{... | collective-permute-start | bytes 6152 | tf_op jit(solution)/shard_map/ppermute | solution.py:94
  77.2 1.5 %copy-start.6 = (f32[4,256]{1,0:T(4,128)S(1)}, f32[4,256]{1,0:T(4,128)}, u32[]{:S(2)}) copy-start(f32[4,256]{1,0:T(4,128)} %copy-done.5) | copy-start | bytes 12292
  81.4 7.3 %collective-permute-start.15 = (bf16[103936]{0:T(1024)(128)(2,1)S(1)}, bf16[103936]{0:T(1024)(128)(2,1)S(1)}, u32[]{:S(2)}, u32[]{:S(2)}) collective-permute-start(bf16[103936]{0:T(1024)(128)(2,1)S(1)} %pad_maximum_fusion.2), channel_id=1, source_target_pairs={{0,2},{2,0},{1,3},{3,1},{4,6},{6,4},{5,7},{7,5},{8,10},{10,8},{9,1... | collective-permute-start | bytes 623624 | tf_op jit(solution)/shard_map/ppermute | solution.py:344
  113.9 5.7 %collective-permute-start.17 = (bf16[256,384]{1,0:T(8,128)(2,1)S(1)}, bf16[256,384]{1,0:T(8,128)(2,1)S(1)}, u32[]{:S(2)}, u32[]{:S(2)}) collective-permute-start(bf16[256,384]{1,0:T(8,128)(2,1)S(1)} %reduce_sum.201), channel_id=1, source_target_pairs={{0,2},{2,0},{1,3},{3,1},{4,6},{6,4},{5,7},{7,5},{8,10},{10,8},{9,1... | collective-permute-start | bytes 589832 | tf_op jit(solution)/shard_map/ppermute | solution.py:358
  (6 other events, 6.2 us)

commit v17 on v8

--- a/solution.py
+++ b/solution.py
@@ -49,6 +49,32 @@
     cross_exp = jnp.exp(cross_scores - peak)
     totals = (jnp.sum(own_exp, -1) + jnp.sum(cross_exp, -1))[..., None]
     return (own_exp / totals, cross_exp / totals)
+
+
+def slotted(block, axis):
+    return lax.axis_size("cand") <= 8 and block.shape[axis] == 1
+
+
+def gather_slots(block, axis):
+    if not slotted(block, axis):
+        return lax.all_gather(block, "cand", axis=axis, tiled=True)
+    count = lax.axis_size("cand")
+    parts = [block] + [
+        lax.ppermute(block, "cand", [(j, (j + k) % count) for j in range(count)])
+        for k in range(1, count)
+    ]
+    return jnp.concatenate(parts, axis)
+
+
+def scatter_slots(block, axis):
+    count = lax.axis_size("cand")
+    if count > 8 or block.shape[axis] != count:
+        return lax.psum_scatter(block, "cand", scatter_dimension=axis, tiled=True)
+    total = lax.slice_in_dim(block, 0, 1, axis=axis)
+    for k in range(1, count):
+        piece = lax.slice_in_dim(block, count - k, count - k + 1, axis=axis)
+        total = total + lax.ppermute(piece, "cand", [(j, (j + k) % count) for j in range(count)])
+    return total
 
 
 def gather_cand(block, axis):
@@ -131,13 +157,17 @@
     first_mask = positions == 0
     own_valid = positions[None, None, :] < lengths[:, :, None]
     local_ids = lax.axis_index("cand") * local_cands + jnp.arange(local_cands)
-    cross_valid = local_ids[:, None] != jnp.arange(cand_count)[None, :]
+    if local_cands == 1 and lax.axis_size("cand") <= 8:
+        slot_ids = (lax.axis_index("cand") - jnp.arange(cand_count)) % cand_count
+    else:
+        slot_ids = jnp.arange(cand_count)
+    cross_valid = local_ids[:, None] != slot_ids[None, :]
     head_shape = (lists, local_cands, seq_len, local_heads, HEAD_DIM)
     cls_shape = (lists, cand_count, local_heads, HEAD_DIM)
     out_first_full = gather_mp(w_out_first, 0)
     last_full = gather_mp(w_last, 2)
     out_last_full = gather_mp(w_out_last, 0)
-    cls_and_teacher = gather_cand(
+    cls_and_teacher = gather_slots(
         jnp.concatenate([tokens[:, :, 0].astype(jnp.float32), teacher[..., None]], -1), 1
     )
     cls_tokens = cls_and_teacher[..., :model_width].astype(jnp.bfloat16)
@@ -177,7 +207,7 @@
     hidden = normed_first.astype(jnp.bfloat16)
     last_query = mixed("qcd,df->qcf", hidden[:, :, 0], w_last[0]).astype(jnp.bfloat16)
     last_kv = mixed("qcsd,kdf->kqcsf", hidden, w_last[1:]).astype(jnp.bfloat16)
-    gathered_kv_last = gather_cand(
+    gathered_kv_last = gather_slots(
         jnp.concatenate([last_kv[0][:, :, 0], last_kv[1][:, :, 0]], -1), 1
     )
     gathered_keys_last = gathered_kv_last[..., :local_width]
@@ -249,7 +279,7 @@
     cls_val_terms = mixed("qchd,qche->qdhe", cross_last_weight, grad_mixed_last).reshape(
         lists, cand_count, local_width
     )
-    back_terms = scatter_cand(jnp.concatenate([cls_key_terms, cls_val_terms], -1), 1)
+    back_terms = scatter_slots(jnp.concatenate([cls_key_terms, cls_val_terms], -1), 1)
     back_keys = back_terms[..., :local_width]
     back_vals = back_terms[..., local_width:]
     first_cols = first_mask[None, None, :, None]

time: 116 us -> 125 us (1.078)
  other arithmetic: 13.9 us -> 19.8 us
  local copies, waits for them, and re-layouts: 7.62 us -> 9 us
    ppermute x6 -> x3, starting transfers between devices: 8.88 us -> 3.89 us  [scatter_cand(): lax.ppermute(piece, 'cand', [(j, (j + k) % count) for j in range(count)])]
    ppermute x6 -> x9, starting transfers between devices: 8.45 us -> 13.4 us  [the longest x6 8.4 us: gather_slots(): lax.ppermute(block, 'cand', [(j, (j + k) % count) for j in range(count)])]
    ppermute x6 -> x3, waiting for transfers between devices: 17.9 us -> 16.1 us  [scatter_cand(): lax.ppermute(piece, 'cand', [(j, (j + k) % count) for j in range(count)])]
    ppermute x6 -> x9, waiting for transfers between devices: 0.12 us -> 1.75 us  [the longest x3 1.73 us: scatter_slots(): lax.ppermute(piece, 'cand', [(j, (j + k) % count) for j in range(count)])]
    another operation x14 -> x10, other arithmetic: 1.58 us -> 2.72 us
  transfers between devices with their start and end apart: 21 -> 21, of which waited for: 8 -> 7; matrix products, arithmetic and copies ran while one was open for 33% -> 37% of each run, Pallas kernels for 0% -> 0%
where the time goes in v17:
time: 125 us; the launch traced here: 124 us
  waiting for transfers between devices  30 us (24%)
  starting transfers between devices  28.3 us (23%)
  matrix products  21.8 us (17%)
  other arithmetic  19.8 us (16%)
  local copies, waits for them, and re-layouts  9 us (7%)
  between operations  8.47 us (7%)
  blocking collectives  6.37 us (5%)
    dot_general x32, matrix products, mixed(): jnp.einsum(pattern, former, latter, preferred_element_type=jnp.float32)  21.8 us
    ppermute x3, waiting for transfers between devices, scatter_cand(): lax.ppermute(piece, 'cand', [(j, (j + k) % count) for j in range(count)])  16.1 us
    ppermute x6, starting transfers between devices, gather_slots(): lax.ppermute(block, 'cand', [(j, (j + k) % count) for j in range(count)])  8.4 us
    ppermute x3, starting transfers between devices, sum_cand(): lax.ppermute(block, 'cand', [(j, (j + k) % count) for j in range(count)])  7.77 us
    ppermute x1, waiting for transfers between devices, local(): partner = lax.ppermute(reduced, 'query', swap)  5.88 us
    ppermute x1, waiting for transfers between devices, local(): lax.ppermute(jnp.concatenate([given_half.reshape(-1), cls_flat.reshape(-1...  5.03 us
    ppermute x3, starting transfers between devices, scatter_slots(): lax.ppermute(piece, 'cand', [(j, (j + k) % count) for j in range(count)])  5 us
    ppermute x3, starting transfers between devices, scatter_cand(): lax.ppermute(piece, 'cand', [(j, (j + k) % count) for j in range(count)])  3.89 us
  transfers between devices with their start and end apart: 21, of which 7 were waited for; matrix products, arithmetic and copies ran while one was open for 37% of the time, Pallas kernels for 0%

profile of v17, /device:TPU:8, one launch (start us, length us, event | category | flops | bytes accessed | tf_op | source)
XLA Modules:
  0.0 123.8 jit_solution(5195319578393276482)
XLA Ops:
  1.4 1.6 %collective-permute-start = (f32[1,1,1025]{2,1,0:T(1,128)S(1)}, f32[1,1,1025]{2,1,0:T(1,128)S(1)}, u32[]{:S(2)}, u32[]{:S(2)}) collective-permute-start(f32[1,1,1025]{2,1,0:T(1,128)S(1)} %pad_maximum_fusion.5), channel_id=1, source_target_pairs={{0,4},{4,8},{8,12},{12,0},{1,5},{5,9},{9,13},{13,1},{2,6},{6,10},{... | collective-permute-start | bytes 12308 | tf_op jit(solution)/shard_map/ppermute | solution.py:63
  4.1 1.9 %collective-permute-start.2 = (f32[1,1,1025]{2,1,0:T(1,128)S(1)}, f32[1,1,1025]{2,1,0:T(1,128)S(1)}, u32[]{:S(2)}, u32[]{:S(2)}) collective-permute-start(f32[1,1,1025]{2,1,0:T(1,128)S(1)} %pad_maximum_fusion.5), channel_id=1, source_target_pairs={{0,12},{4,0},{8,4},{12,8},{1,13},{5,1},{9,5},{13,9},{2,14},{6,2},{... | collective-permute-start | bytes 12308 | tf_op jit(solution)/shard_map/ppermute | solution.py:63
  6.6 2.3 %fusion.5 = bf16[3,1,1,256,256]{3,4,0,2,1:T(8,128)(2,1)S(1)} fusion(bf16[3,1024,256]{2,1,0:T(8,128)(2,1)} %param.13, bf16[1,1,256,1024]{3,2,1,0:T(8,128)(2,1)} %param.10), kind=kOutput, calls=%fused_computation.13 | convolution fusion | flops 402849792 | bytes 2490368 | tf_op jit(solution)/shard_map/qcsd,kdf->kqcsf/dot_general | solution.py:15
  15.0 1.3 %exponential_reduce_fusion = f32[]{:T(128)} fusion(f32[1,4,1]{2,1,0:T(4,128)S(1)} %get-tuple-element.23, f32[]{:T(128)} %get-tuple-element.22), kind=kLoop, calls=%fused_computation.187 | loop fusion | flops 7 | bytes 24 | tf_op jit(solution)/shard_map/reduce_sum | solution.py:240
  18.7 2.1 %all_gather.9 = bf16[1,1,256,512]{2,3,1,0:T(8,128)(2,1)S(1)} all-gather(bf16[1,1,256,256]{2,3,1,0:T(8,128)(2,1)S(1)} %bitcast.345), channel_id=1, replica_groups=mesh['groups'=2,'cand'=4,'query'=2,'mp'=2] {'mp'}, dimensions={3}, use_global_device_ids=true | all-gather | bytes 393216 | tf_op jit(solution)/shard_map/all_gather | solution.py:202
  20.9 1.9 %fusion.141 = (f32[256]{0:T(256)S(1)}, f32[1,1,256,1024]{3,2,1,0:T(8,128)S(1)}) fusion(bf16[256,1024]{1,0:T(8,128)(2,1)} %collective-permute-done.3, bf16[256,1024]{1,0:T(8,128)(2,1)S(1)} %copy-done.2, pred[]{:T(512)S(6)} %eq.47, bf16[1,1,256,512]{2,3,1,0:T(8,128)(2,1)S(1)} %all_gather.9, bf16[1,1,256,1024]{3,2,1,0:T(8,128)(2,1)} %param.10), kind=kOutput, calls=%fused_computation.246 | convolution fusion | flops 273940224 | bytes 2884609 | tf_op jit(solution)/shard_map/qcsf,fd->qcsd/dot_general | solution.py:15
  23.6 1.7 %fusion.6 = bf16[2,1,1,256,256]{4,3,0,2,1:T(8,128)(2,1)S(1)} fusion(bf16[3,1024,256]{2,1,0:T(8,128)(2,1)} %param.16, bf16[1,1,256,1024]{3,2,1,0:T(8,128)(2,1)S(1)} %multiply_convert_fusion.1), kind=kOutput, calls=%fused_computation.18 | convolution fusion | flops 268566528 | bytes 1835008 | tf_op jit(solution)/shard_map/qcsd,kdf->kqcsf/dot_general | solution.py:15
  26.8 3.6 %collective-permute-start.5 = (bf16[1,1,512]{2,1,0:T(2,128)(2,1)}, bf16[1,1,512]{2,1,0:T(2,128)(2,1)}, u32[]{:S(2)}, u32[]{:S(2)}) collective-permute-start(bf16[1,1,512]{2,1,0:T(2,128)(2,1)} %pad_maximum_fusion.8), channel_id=1, source_target_pairs={{0,8},{4,12},{8,0},{12,4},{1,9},{5,13},{9,1},{13,5},{2,10},{6,14},... | collective-permute-start | bytes 3080 | tf_op jit(solution)/shard_map/ppermute | solution.py:63
  30.4 1.2 fusion.39
  33.8 1.6 %collective-permute-start.16 = (bf16[256,1024]{1,0:T(8,128)(2,1)}, bf16[256,1024]{1,0:T(8,128)(2,1)}, u32[]{:S(2)}, u32[]{:S(2)}) collective-permute-start(bf16[256,1024]{1,0:T(8,128)(2,1)} %bitcast), channel_id=1, source_target_pairs={{0,2},{2,0},{1,3},{3,1},{4,6},{6,4},{5,7},{7,5},{8,10},{10,8},{9,1... | collective-permute-start | bytes 1572872 | tf_op jit(solution)/shard_map/ppermute | solution.py:179
  40.5 1.8 %all_gather.10 = bf16[1,1,512]{2,1,0:T(2,128)(2,1)S(1)} all-gather(bf16[1,1,256]{2,1,0:T(2,128)(2,1)S(1)} %convert_element_type.264), channel_id=1, replica_groups=mesh['groups'=2,'cand'=4,'query'=2,'mp'=2] {'mp'}, dimensions={2}, use_global_device_ids=true | all-gather | bytes 1536 | tf_op jit(solution)/shard_map/all_gather | solution.py:231
  42.3 1.6 %fusion.16 = f32[1,1024]{1,0:T(1,128)S(1)} fusion(bf16[256,1024]{1,0:T(8,128)(2,1)} %collective-permute-done.7, bf16[256,1024]{1,0:T(8,128)(2,1)S(1)} %copy-done.1, pred[]{:T(512)S(6)} %eq.47, bf16[1,1,512]{2,1,0:T(2,128)(2,1)S(1)} %all_gather.10), kind=kOutput, calls=%fused_computation.36 | convolution fusion | flops 5767168 | bytes 1053697 | tf_op jit(solution)/shard_map/qcf,fd->qcd/dot_general | solution.py:15
  47.8 3.4 %collective-permute-start.8 = (f32[1]{0:T(128)}, f32[1]{0:T(128)}, u32[]{:S(2)}, u32[]{:S(2)}) collective-permute-start(f32[1]{0:T(128)} %bitcast.59), channel_id=1, source_target_pairs={{0,4},{4,8},{8,12},{12,0},{1,5},{5,9},{9,13},{13,1},{2,6},{6,10},{... | collective-permute-start | bytes 20 | tf_op jit(solution)/shard_map/ppermute | solution.py:101
  51.2 3.1 %collective-permute-start.9 = (f32[1]{0:T(128)}, f32[1]{0:T(128)}, u32[]{:S(2)}, u32[]{:S(2)}) collective-permute-start(f32[1]{0:T(128)} %bitcast.59), channel_id=1, source_target_pairs={{0,8},{4,12},{8,0},{12,4},{1,9},{5,13},{9,1},{13,5},{2,10},{6,14},... | collective-permute-start | bytes 20 | tf_op jit(solution)/shard_map/ppermute | solution.py:101
  54.3 1.3 %collective-permute-start.10 = (f32[1]{0:T(128)}, f32[1]{0:T(128)}, u32[]{:S(2)}, u32[]{:S(2)}) collective-permute-start(f32[1]{0:T(128)} %bitcast.59), channel_id=1, source_target_pairs={{0,12},{4,0},{8,4},{12,8},{1,13},{5,1},{9,5},{13,9},{2,14},{6,2},{... | collective-permute-start | bytes 20 | tf_op jit(solution)/shard_map/ppermute | solution.py:101
  56.7 1.2 collective-permute-done.10
  62.8 2.9 %collective-permute-start.12 = (f32[1,1,512]{2,1,0:T(1,128)S(1)}, f32[1,1,512]{2,1,0:T(1,128)S(1)}, u32[]{:S(2)}, u32[]{:S(2)}) collective-permute-start(f32[1,1,512]{2,1,0:T(1,128)S(1)} %get-tuple-element.38), channel_id=1, source_target_pairs={{0,8},{4,12},{8,0},{12,4},{1,9},{5,13},{9,1},{13,5},{2,10},{6,14},... | collective-permute-start | bytes 6152 | tf_op jit(solution)/shard_map/ppermute | solution.py:76
  65.7 1.2 collective-permute-start.13
  67.6 1.7 %collective-permute-done.13 = f32[1,1,512]{2,1,0:T(1,128)S(1)} collective-permute-done((f32[1,1,512]{2,1,0:T(1,128)S(1)}, f32[1,1,512]{2,1,0:T(1,128)S(1)}, u32[]{:S(2)}, u32[]{:S(2)}) %collective-permute-start.13) | collective-permute-done | bytes 2080 | tf_op jit(solution)/shard_map/ppermute | solution.py:76
  69.5 2.5 %all_gather.11 = bf16[1,1,513,512]{2,3,1,0:T(8,128)(2,1)S(1)} all-gather(bf16[1,1,513,256]{2,3,1,0:T(8,128)(2,1)S(1)} %pad_maximum_fusion.1), channel_id=1, replica_groups=mesh['groups'=2,'cand'=4,'query'=2,'mp'=2] {'mp'}, dimensions={3}, use_global_device_ids=true | all-gather | bytes 787968 | tf_op jit(solution)/shard_map/all_gather | solution.py:292
  72.1 3.4 %maximum_select_fusion = bf16[3,1024,512]{2,1,0:T(8,128)(2,1)S(1)} fusion(bf16[3,1024,256]{2,1,0:T(8,128)(2,1)} %collective-permute-done.14, bf16[3,1024,256]{2,1,0:T(8,128)(2,1)} %param.16, pred[]{:T(512)S(6)} %eq.47), kind=kLoop, calls=%fused_computation | loop fusion | flops 14155776 | bytes 6291457 | tf_op jit(solution)/shard_map/jit(_where)/select_n | solution.py:124
  77.5 1.6 %convolution_convert_fusion.3 = bf16[256,256]{0,1:T(8,128)(2,1)S(1)} fusion(bf16[256,1024]{1,0:T(8,128)(2,1)} %param.14, f32[1,1,256,1024]{3,2,1,0:T(8,128)S(1)} %get-tuple-element.50, f32[256,1024]{1,0:T(8,128)S(1)} %get-tuple-element.52, f32[256]{0:T(256)S(1)} %broadcast_multiply_fusion.1, f32[256]{0:T(256)S(1)} %broadcast_multiply_fusion.2, ...), kind=kOutput, calls=%fused_computation.21 | convolution fusion | flops 136118272 | bytes 2756608 | tf_op jit(solution)/shard_map/qcsd,fd->qcsf/dot_general | solution.py:15
  80.2 2.3 %multiply_reduce_fusion = (f32[4,256]{1,0:T(4,128)S(1)}, f32[4,256,256]{1,2,0:T(8,128)}) fusion(f32[4,256]{1,0:T(4,128)} %copy-done.8, f32[4,256,256]{1,2,0:T(8,128)S(1)} %get-tuple-element.48, f32[4,256]{1,0:T(4,128)S(1)} %broadcast_select_fusion.2, bf16[256,4,64]{0,2,1:T(8,128)(2,1)S(1)} %bitcast.343, bf16[256,4,64]{0,2,1:T(8,128)(2,1)} %bitcast.347), kind=kOutput, calls=%fused_computation.48 | convolution fusion | flops 34601984 | bytes 2371584 | tf_op jit(solution)/shard_map/qcshe,qcthe->qchst/dot_general | solution.py:15
  84.2 1.5 %multiply_convert_fusion = bf16[4,256,256]{1,2,0:T(8,128)(2,1)S(1)} fusion(f32[4,256,256]{1,2,0:T(8,128)} %get-tuple-element.54, f32[4,256]{1,0:T(4,128)S(1)} %broadcast_select_fusion, f32[4,256]{1,0:T(4,128)S(1)} %copy-done.9, f32[4,256,256]{1,2,0:T(8,128)S(1)} %get-tuple-element.48, f32[4,256]{1,0:T(4,128)S(1)} %broadcast_select_fusion.2), kind=kLoop, calls=%fused_computation.47 | loop fusion | flops 1310720 | bytes 2633728 | tf_op jit(solution)/shard_map/convert_element_type | solution.py:318
  87.2 1.6 %fusion.31 = f32[1024,384]{0,1:T(8,128)S(1)} fusion(bf16[4,1024]{1,0:T(4,128)(2,1)S(1)} %get-tuple-element.35, bf16[256,1024]{1,0:T(8,128)(2,1)} %bitcast, s32[]{:T(128)S(6)} %select_n.180, bf16[256,768]{0,1:T(8,128)(2,1)S(1)} %bitcast.327, bf16[4,768]{0,1:T(8,128)(2,1)S(1)} %copy.82), kind=kOutput, calls=%fused_computation.63 | convolution fusion | flops 205936640 | bytes 2504708 | tf_op jit(solution)/shard_map/rd,rf->df/dot_general | solution.py:15
  88.8 5.0 %collective-permute-done.15 = bf16[103936]{0:T(1024)(128)(2,1)S(1)} collective-permute-done((bf16[103936]{0:T(1024)(128)(2,1)S(1)}, bf16[103936]{0:T(1024)(128)(2,1)S(1)}, u32[]{:S(2)}, u32[]{:S(2)}) %collective-permute-start.15) | collective-permute-done | bytes 207904 | tf_op jit(solution)/shard_map/ppermute | solution.py:369
  94.1 1.4 %fusion.145 = f32[384,1024]{1,0:T(8,128)S(1)} fusion(bf16[256,384]{1,0:T(8,128)(2,1)S(1)} %slice.169, bf16[256,1024]{1,0:T(8,128)(2,1)} %collective-permute-done.16), kind=kOutput, calls=%fused_computation.250 | convolution fusion | flops 201326592 | bytes 2293760 | tf_op jit(solution)/shard_map/rd,rf->df/dot_general | solution.py:15
  96.7 2.9 %collective-permute-start.18 = (bf16[256,384]{0,1:T(8,128)(2,1)S(1)}, bf16[256,384]{0,1:T(8,128)(2,1)S(1)}, u32[]{:S(2)}, u32[]{:S(2)}) collective-permute-start(bf16[256,384]{0,1:T(8,128)(2,1)S(1)} %get-tuple-element.26), channel_id=1, source_target_pairs={{0,8},{4,12},{8,0},{12,4},{1,9},{5,13},{9,1},{13,5},{2,10},{6,14},... | collective-permute-start | bytes 589832 | tf_op jit(solution)/shard_map/ppermute | solution.py:115
  99.9 10.3 %collective-permute-done.17 = bf16[256,384]{0,1:T(8,128)(2,1)S(1)} collective-permute-done((bf16[256,384]{0,1:T(8,128)(2,1)S(1)}, bf16[256,384]{0,1:T(8,128)(2,1)S(1)}, u32[]{:S(2)}, u32[]{:S(2)}) %collective-permute-start.17) | collective-permute-done | bytes 196640 | tf_op jit(solution)/shard_map/ppermute | solution.py:115
  110.2 2.8 %collective-permute-done.18 = bf16[256,384]{0,1:T(8,128)(2,1)S(1)} collective-permute-done((bf16[256,384]{0,1:T(8,128)(2,1)S(1)}, bf16[256,384]{0,1:T(8,128)(2,1)S(1)}, u32[]{:S(2)}, u32[]{:S(2)}) %collective-permute-start.18) | collective-permute-done | bytes 196640 | tf_op jit(solution)/shard_map/ppermute | solution.py:115
  112.9 3.1 %collective-permute-done.19 = bf16[256,384]{0,1:T(8,128)(2,1)S(1)} collective-permute-done((bf16[256,384]{0,1:T(8,128)(2,1)S(1)}, bf16[256,384]{0,1:T(8,128)(2,1)S(1)}, u32[]{:S(2)}, u32[]{:S(2)}) %collective-permute-start.19) | collective-permute-done | bytes 196640 | tf_op jit(solution)/shard_map/ppermute | solution.py:115
  116.7 5.9 %collective-permute-done.20 = bf16[256,384]{0,1:T(8,128)(2,1)S(1)} collective-permute-done((bf16[256,384]{0,1:T(8,128)(2,1)S(1)}, bf16[256,384]{0,1:T(8,128)(2,1)S(1)}, u32[]{:S(2)}, u32[]{:S(2)}) %collective-permute-start.20) | collective-permute-done | bytes 196640 | tf_op jit(solution)/shard_map/ppermute | solution.py:380
  (238 shorter events, 33.8 us)
Async XLA Ops:
  1.4 9.9 %collective-permute-start = (f32[1,1,1025]{2,1,0:T(1,128)S(1)}, f32[1,1,1025]{2,1,0:T(1,128)S(1)}, u32[]{:S(2)}, u32[]{:S(2)}) collective-permute-start(f32[1,1,1025]{2,1,0:T(1,128)S(1)} %pad_maximum_fusion.5), channel_id=1, source_target_pairs={{0,4},{4,8},{8,12},{12,0},{1,5},{5,9},{9,13},{13,1},{2,6},{6,10},{... | collective-permute-start | bytes 12308 | tf_op jit(solution)/shard_map/ppermute | solution.py:63
  3.0 8.3 %collective-permute-start.1 = (f32[1,1,1025]{2,1,0:T(1,128)S(1)}, f32[1,1,1025]{2,1,0:T(1,128)S(1)}, u32[]{:S(2)}, u32[]{:S(2)}) collective-permute-start(f32[1,1,1025]{2,1,0:T(1,128)S(1)} %pad_maximum_fusion.5), channel_id=1, source_target_pairs={{0,8},{4,12},{8,0},{12,4},{1,9},{5,13},{9,1},{13,5},{2,10},{6,14},... | collective-permute-start | bytes 12308 | tf_op jit(solution)/shard_map/ppermute | solution.py:63
  4.1 7.2 %collective-permute-start.2 = (f32[1,1,1025]{2,1,0:T(1,128)S(1)}, f32[1,1,1025]{2,1,0:T(1,128)S(1)}, u32[]{:S(2)}, u32[]{:S(2)}) collective-permute-start(f32[1,1,1025]{2,1,0:T(1,128)S(1)} %pad_maximum_fusion.5), channel_id=1, source_target_pairs={{0,12},{4,0},{8,4},{12,8},{1,13},{5,1},{9,5},{13,9},{2,14},{6,2},{... | collective-permute-start | bytes 12308 | tf_op jit(solution)/shard_map/ppermute | solution.py:63
  6.1 14.8 %collective-permute-start.3 = (bf16[256,1024]{1,0:T(8,128)(2,1)}, bf16[256,1024]{1,0:T(8,128)(2,1)}, u32[]{:S(2)}, u32[]{:S(2)}) collective-permute-start(bf16[256,1024]{1,0:T(8,128)(2,1)} %param.14), channel_id=1, source_target_pairs={{0,1},{1,0},{2,3},{3,2},{4,5},{5,4},{6,7},{7,6},{8,9},{9,8},{10,11... | collective-permute-start | bytes 1572872 | tf_op jit(solution)/shard_map/ppermute | solution.py:123
  6.1 36.3 %collective-permute-start.7 = (bf16[256,1024]{1,0:T(8,128)(2,1)}, bf16[256,1024]{1,0:T(8,128)(2,1)}, u32[]{:S(2)}, u32[]{:S(2)}) collective-permute-start(bf16[256,1024]{1,0:T(8,128)(2,1)} %param.17), channel_id=1, source_target_pairs={{0,1},{1,0},{2,3},{3,2},{4,5},{5,4},{6,7},{7,6},{8,9},{9,8},{10,11... | collective-permute-start | bytes 1572872 | tf_op jit(solution)/shard_map/ppermute | solution.py:123
  6.6 11.8 %copy-start.14 = (pred[256]{0:T(512)(128)(4,1)}, pred[256]{0:T(512)(128)(4,1)S(1)}, u32[]{:S(2)}) copy-start(pred[256]{0:T(512)(128)(4,1)S(1)} %iota_compare_fusion.1) | copy-start | bytes 772
  6.6 4.8 %copy-start = (bf16[3,1024,256]{2,1,0:T(8,128)(2,1)S(1)}, bf16[3,1024,256]{2,1,0:T(8,128)(2,1)}, u32[]{:S(2)}) copy-start(bf16[3,1024,256]{2,1,0:T(8,128)(2,1)} %param.13) | copy-start | bytes 4718596
  8.9 13.9 %copy-start.3 = (bf16[1,1,1,256,256]{3,4,0,2,1:T(8,128)(2,1)}, bf16[1,1,1,256,256]{3,4,0,2,1:T(8,128)(2,1)S(1)}, u32[]{:S(2)}) copy-start(bf16[1,1,1,256,256]{3,4,0,2,1:T(8,128)(2,1)S(1)} %get-tuple-element.28) | copy-start | bytes 393220
  10.7 8.0 %copy-start.7 = (pred[4]{0:T(512)(128)(4,1)}, pred[4]{0:T(512)(128)(4,1)S(1)}, u32[]{:S(2)}) copy-start(pred[4]{0:T(512)(128)(4,1)S(1)} %fusion.112) | copy-start | bytes 16
  11.3 60.8 %collective-permute-start.14 = (bf16[3,1024,256]{2,1,0:T(8,128)(2,1)}, bf16[3,1024,256]{2,1,0:T(8,128)(2,1)}, u32[]{:S(2)}, u32[]{:S(2)}) collective-permute-start(bf16[3,1024,256]{2,1,0:T(8,128)(2,1)} %param.16), channel_id=1, source_target_pairs={{0,1},{1,0},{2,3},{3,2},{4,5},{5,4},{6,7},{7,6},{8,9},{9,8},{10,11... | collective-permute-start | bytes 4718600 | tf_op jit(solution)/shard_map/ppermute | solution.py:123
  14.0 4.7 %copy-start.5 = (f32[4,4]{0,1:T(4,128)}, f32[4,4]{0,1:T(4,128)S(1)}, u32[]{:S(2)}) copy-start(f32[4,4]{0,1:T(4,128)S(1)} %get-tuple-element.10) | copy-start | bytes 196
  14.1 4.6 %copy-start.8 = (f32[4,256]{1,0:T(4,128)}, f32[4,256]{1,0:T(4,128)S(1)}, u32[]{:S(2)}) copy-start(f32[4,256]{1,0:T(4,128)S(1)} %broadcast_select_fusion.1) | copy-start | bytes 12292
  23.6 18.7 %copy-start.1 = (bf16[256,1024]{1,0:T(8,128)(2,1)S(1)}, bf16[256,1024]{1,0:T(8,128)(2,1)}, u32[]{:S(2)}) copy-start(bf16[256,1024]{1,0:T(8,128)(2,1)} %param.17) | copy-start | bytes 1572868
  26.1 5.6 %copy-start.20 = (bf16[1,1,256]{2,1,0:T(2,128)(2,1)}, bf16[1,1,256]{2,1,0:T(2,128)(2,1)S(1)}, u32[]{:S(2)}) copy-start(bf16[1,1,256]{2,1,0:T(2,128)(2,1)S(1)} %get-tuple-element.56) | copy-start | bytes 1540
  26.7 7.2 %collective-permute-start.4 = (bf16[1,1,512]{2,1,0:T(2,128)(2,1)}, bf16[1,1,512]{2,1,0:T(2,128)(2,1)}, u32[]{:S(2)}, u32[]{:S(2)}) collective-permute-start(bf16[1,1,512]{2,1,0:T(2,128)(2,1)} %pad_maximum_fusion.8), channel_id=1, source_target_pairs={{0,4},{4,8},{8,12},{12,0},{1,5},{5,9},{9,13},{13,1},{2,6},{6,10},{... | collective-permute-start | bytes 3080 | tf_op jit(solution)/shard_map/ppermute | solution.py:63
  26.8 8.6 %collective-permute-start.5 = (bf16[1,1,512]{2,1,0:T(2,128)(2,1)}, bf16[1,1,512]{2,1,0:T(2,128)(2,1)}, u32[]{:S(2)}, u32[]{:S(2)}) collective-permute-start(bf16[1,1,512]{2,1,0:T(2,128)(2,1)} %pad_maximum_fusion.8), channel_id=1, source_target_pairs={{0,8},{4,12},{8,0},{12,4},{1,9},{5,13},{9,1},{13,5},{2,10},{6,14},... | collective-permute-start | bytes 3080 | tf_op jit(solution)/shard_map/ppermute | solution.py:63
  30.4 5.0 %collective-permute-start.6 = (bf16[1,1,512]{2,1,0:T(2,128)(2,1)}, bf16[1,1,512]{2,1,0:T(2,128)(2,1)}, u32[]{:S(2)}, u32[]{:S(2)}) collective-permute-start(bf16[1,1,512]{2,1,0:T(2,128)(2,1)} %pad_maximum_fusion.8), channel_id=1, source_target_pairs={{0,12},{4,0},{8,4},{12,8},{1,13},{5,1},{9,5},{13,9},{2,14},{6,2},{... | collective-permute-start | bytes 3080 | tf_op jit(solution)/shard_map/ppermute | solution.py:63
  33.8 60.2 %collective-permute-start.16 = (bf16[256,1024]{1,0:T(8,128)(2,1)}, bf16[256,1024]{1,0:T(8,128)(2,1)}, u32[]{:S(2)}, u32[]{:S(2)}) collective-permute-start(bf16[256,1024]{1,0:T(8,128)(2,1)} %bitcast), channel_id=1, source_target_pairs={{0,2},{2,0},{1,3},{3,1},{4,6},{6,4},{5,7},{7,5},{8,10},{10,8},{9,1... | collective-permute-start | bytes 1572872 | tf_op jit(solution)/shard_map/ppermute | solution.py:179
  40.3 6.2 %copy-start.10 = (f32[1024]{0:T(1024)S(1)}, f32[1024]{0:T(1024)}, u32[]{:S(2)}) copy-start(f32[1024]{0:T(1024)} %param.18) | copy-start | bytes 12292
  40.3 6.2 %copy-start.11 = (f32[1024]{0:T(1024)S(1)}, f32[1024]{0:T(1024)}, u32[]{:S(2)}) copy-start(f32[1024]{0:T(1024)} %param.19) | copy-start | bytes 12292
  42.3 27.0 %copy-start.15 = (pred[256]{0:T(512)(128)(4,1)S(1)}, pred[256]{0:T(512)(128)(4,1)}, u32[]{:S(2)}) copy-start(pred[256]{0:T(512)(128)(4,1)} %copy-done.14) | copy-start | bytes 772
  47.8 7.8 %collective-permute-start.8 = (f32[1]{0:T(128)}, f32[1]{0:T(128)}, u32[]{:S(2)}, u32[]{:S(2)}) collective-permute-start(f32[1]{0:T(128)} %bitcast.59), channel_id=1, source_target_pairs={{0,4},{4,8},{8,12},{12,0},{1,5},{5,9},{9,13},{13,1},{2,6},{6,10},{... | collective-permute-start | bytes 20 | tf_op jit(solution)/shard_map/ppermute | solution.py:101
  51.2 5.0 %collective-permute-start.9 = (f32[1]{0:T(128)}, f32[1]{0:T(128)}, u32[]{:S(2)}, u32[]{:S(2)}) collective-permute-start(f32[1]{0:T(128)} %bitcast.59), channel_id=1, source_target_pairs={{0,8},{4,12},{8,0},{12,4},{1,9},{5,13},{9,1},{13,5},{2,10},{6,14},... | collective-permute-start | bytes 20 | tf_op jit(solution)/shard_map/ppermute | solution.py:101
  54.3 3.6 %collective-permute-start.10 = (f32[1]{0:T(128)}, f32[1]{0:T(128)}, u32[]{:S(2)}, u32[]{:S(2)}) collective-permute-start(f32[1]{0:T(128)} %bitcast.59), channel_id=1, source_target_pairs={{0,12},{4,0},{8,4},{12,8},{1,13},{5,1},{9,5},{13,9},{2,14},{6,2},{... | collective-permute-start | bytes 20 | tf_op jit(solution)/shard_map/ppermute | solution.py:101
  61.9 5.7 %collective-permute-start.11 = (f32[1,1,512]{2,1,0:T(1,128)S(1)}, f32[1,1,512]{2,1,0:T(1,128)S(1)}, u32[]{:S(2)}, u32[]{:S(2)}) collective-permute-start(f32[1,1,512]{2,1,0:T(1,128)S(1)} %get-tuple-element.36), channel_id=1, source_target_pairs={{0,4},{4,8},{8,12},{12,0},{1,5},{5,9},{9,13},{13,1},{2,6},{6,10},{... | collective-permute-start | bytes 6152 | tf_op jit(solution)/shard_map/ppermute | solution.py:76
  62.8 4.8 %collective-permute-start.12 = (f32[1,1,512]{2,1,0:T(1,128)S(1)}, f32[1,1,512]{2,1,0:T(1,128)S(1)}, u32[]{:S(2)}, u32[]{:S(2)}) collective-permute-start(f32[1,1,512]{2,1,0:T(1,128)S(1)} %get-tuple-element.38), channel_id=1, source_target_pairs={{0,8},{4,12},{8,0},{12,4},{1,9},{5,13},{9,1},{13,5},{2,10},{6,14},... | collective-permute-start | bytes 6152 | tf_op jit(solution)/shard_map/ppermute | solution.py:76
  65.7 3.6 %collective-permute-start.13 = (f32[1,1,512]{2,1,0:T(1,128)S(1)}, f32[1,1,512]{2,1,0:T(1,128)S(1)}, u32[]{:S(2)}, u32[]{:S(2)}) collective-permute-start(f32[1,1,512]{2,1,0:T(1,128)S(1)} %get-tuple-element.37), channel_id=1, source_target_pairs={{0,12},{4,0},{8,4},{12,8},{1,13},{5,1},{9,5},{13,9},{2,14},{6,2},{... | collective-permute-start | bytes 6152 | tf_op jit(solution)/shard_map/ppermute | solution.py:76
  86.6 7.3 %collective-permute-start.15 = (bf16[103936]{0:T(1024)(128)(2,1)S(1)}, bf16[103936]{0:T(1024)(128)(2,1)S(1)}, u32[]{:S(2)}, u32[]{:S(2)}) collective-permute-start(bf16[103936]{0:T(1024)(128)(2,1)S(1)} %pad_maximum_fusion.2), channel_id=1, source_target_pairs={{0,2},{2,0},{1,3},{3,1},{4,6},{6,4},{5,7},{7,5},{8,10},{10,8},{9,1... | collective-permute-start | bytes 623624 | tf_op jit(solution)/shard_map/ppermute | solution.py:369
  96.0 14.2 %collective-permute-start.17 = (bf16[256,384]{0,1:T(8,128)(2,1)S(1)}, bf16[256,384]{0,1:T(8,128)(2,1)S(1)}, u32[]{:S(2)}, u32[]{:S(2)}) collective-permute-start(bf16[256,384]{0,1:T(8,128)(2,1)S(1)} %get-tuple-element.24), channel_id=1, source_target_pairs={{0,4},{4,8},{8,12},{12,0},{1,5},{5,9},{9,13},{13,1},{2,6},{6,10},{... | collective-permute-start | bytes 589832 | tf_op jit(solution)/shard_map/ppermute | solution.py:115
  96.7 16.3 %collective-permute-start.18 = (bf16[256,384]{0,1:T(8,128)(2,1)S(1)}, bf16[256,384]{0,1:T(8,128)(2,1)S(1)}, u32[]{:S(2)}, u32[]{:S(2)}) collective-permute-start(bf16[256,384]{0,1:T(8,128)(2,1)S(1)} %get-tuple-element.26), channel_id=1, source_target_pairs={{0,8},{4,12},{8,0},{12,4},{1,9},{5,13},{9,1},{13,5},{2,10},{6,14},... | collective-permute-start | bytes 589832 | tf_op jit(solution)/shard_map/ppermute | solution.py:115
  99.6 16.4 %collective-permute-start.19 = (bf16[256,384]{0,1:T(8,128)(2,1)S(1)}, bf16[256,384]{0,1:T(8,128)(2,1)S(1)}, u32[]{:S(2)}, u32[]{:S(2)}) collective-permute-start(bf16[256,384]{0,1:T(8,128)(2,1)S(1)} %get-tuple-element.25), channel_id=1, source_target_pairs={{0,12},{4,0},{8,4},{12,8},{1,13},{5,1},{9,5},{13,9},{2,14},{6,2},{... | collective-permute-start | bytes 589832 | tf_op jit(solution)/shard_map/ppermute | solution.py:115
  116.1 6.5 %collective-permute-start.20 = (bf16[256,384]{0,1:T(8,128)(2,1)S(1)}, bf16[256,384]{0,1:T(8,128)(2,1)S(1)}, u32[]{:S(2)}, u32[]{:S(2)}) collective-permute-start(bf16[256,384]{0,1:T(8,128)(2,1)S(1)} %add_convert_fusion), channel_id=1, source_target_pairs={{0,2},{2,0},{1,3},{3,1},{4,6},{6,4},{5,7},{7,5},{8,10},{10,8},{9,1... | collective-permute-start | bytes 589832 | tf_op jit(solution)/shard_map/ppermute | solution.py:380
  (19 other events, 31.9 us)

commit v18 on v13

--- a/solution.py
+++ b/solution.py
@@ -92,14 +92,8 @@
 
 
 def gather_mp(block, axis):
-    if lax.axis_size("mp") != 2:
-        return lax.all_gather(block, "mp", axis=axis, tiled=True)
     other = lax.ppermute(block, "mp", [(0, 1), (1, 0)])
-    return jnp.where(
-        lax.axis_index("mp") == 0,
-        jnp.concatenate([block, other], axis),
-        jnp.concatenate([other, block], axis),
-    )
+    return jnp.concatenate([block, other], axis)
 
 
 def sum_query(block):

time: 136 us -> 140 us (1.029)
  the two profiles are of different devices: /device:TPU:8 before, /device:TPU:0 now
where the time goes in v18:
time: 140 us; the launch traced here: 139 us
  waiting for transfers between devices  32.1 us (23%)
  starting transfers between devices  28.4 us (20%)
  matrix products  25.9 us (18%)
  local copies, waits for them, and re-layouts  23.1 us (16%)
  other arithmetic  20.8 us (15%)
  between operations  8.85 us (6%)
    dot_general x32, matrix products, mixed(): jnp.einsum(pattern, former, latter, preferred_element_type=jnp.float32)  25.9 us
    ppermute x6, waiting for transfers between devices, scatter_cand(): lax.ppermute(piece, 'cand', [(j, (j + k) % count) for j in range(count)])  19.8 us
    ppermute x6, starting transfers between devices, gather_cand(): lax.ppermute(block, 'cand', [(j, (j + k) % count) for j in range(count)])  10 us
    ppermute x3, starting transfers between devices, sum_cand(): lax.ppermute(block, 'cand', [(j, (j + k) % count) for j in range(count)])  8.67 us
    ppermute x6, starting transfers between devices, scatter_cand(): lax.ppermute(piece, 'cand', [(j, (j + k) % count) for j in range(count)])  5.96 us
    unnamed x84, local copies, waits for them, and re-layouts  5.83 us
    ppermute x1, waiting for transfers between devices, local(): partner = lax.ppermute(reduced, 'query', swap)  5.47 us
    ppermute x1, waiting for transfers between devices, local(): lax.ppermute(jnp.concatenate([given_half.reshape(-1), cls_flat.reshape(-1...  5.42 us
  transfers between devices with their start and end apart: 24, of which 9 were waited for; matrix products, arithmetic and copies ran while one was open for 46% of the time, Pallas kernels for 0%

profile of v18, /device:TPU:0, one launch (start us, length us, event | category | flops | bytes accessed | tf_op | source)
XLA Modules:
  0.0 139.1 jit_solution(10061251186344486343)
XLA Ops:
  1.4 5.1 %collective-permute-start.2 = (f32[1,1,1025]{2,1,0:T(1,128)S(1)}, f32[1,1,1025]{2,1,0:T(1,128)S(1)}, u32[]{:S(2)}, u32[]{:S(2)}) collective-permute-start(f32[1,1,1025]{2,1,0:T(1,128)S(1)} %pad_maximum_fusion.5), channel_id=1, source_target_pairs={{0,12},{4,0},{8,4},{12,8},{1,13},{5,1},{9,5},{13,9},{2,14},{6,2},{... | collective-permute-start | bytes 12308 | tf_op jit(solution)/shard_map/ppermute | solution.py:60
  8.1 2.1 %fusion.5 = bf16[3,1,1,256,256]{3,4,0,2,1:T(8,128)(2,1)S(1)} fusion(bf16[3,1024,256]{2,1,0:T(8,128)(2,1)} %param.13, bf16[1,1,256,1024]{3,2,1,0:T(8,128)(2,1)} %param.10), kind=kOutput, calls=%fused_computation.14 | convolution fusion | flops 402849792 | bytes 2490368 | tf_op jit(solution)/shard_map/qcsd,kdf->kqcsf/dot_general | solution.py:15
  18.5 1.3 exponential_reduce_fusion
  20.5 1.7 %fusion.137 = (f32[256]{0:T(256)S(1)}, f32[1,1,256,1024]{3,2,1,0:T(8,128)S(1)}) fusion(bf16[256,1024]{1,0:T(8,128)(2,1)} %collective-permute-done.4, bf16[256,1024]{1,0:T(8,128)(2,1)S(1)} %copy-done.3, bf16[1,1,256,256]{2,3,1,0:T(8,128)(2,1)S(1)} %collective-permute-done.3, bf16[1,1,256,256]{2,3,1,0:T(8,128)(2,1)S(1)} %bitcast.399, ...), kind=kOutput, calls=%fused_computation.259 | convolution fusion | flops 271843072 | bytes 2884608 | tf_op jit(solution)/shard_map/qcsf,fd->qcsd/dot_general | solution.py:15
  22.8 1.7 %fusion.6 = bf16[2,1,1,256,256]{4,3,0,2,1:T(8,128)(2,1)S(1)} fusion(bf16[3,1024,256]{2,1,0:T(8,128)(2,1)} %param.16, bf16[1,1,256,1024]{3,2,1,0:T(8,128)(2,1)S(1)} %multiply_convert_fusion.1), kind=kOutput, calls=%fused_computation.19 | convolution fusion | flops 268566528 | bytes 1835008 | tf_op jit(solution)/shard_map/qcsd,kdf->kqcsf/dot_general | solution.py:15
  24.5 1.3 fusion.33
  27.1 2.8 %collective-permute-start.7 = (bf16[1,1,512]{2,1,0:T(2,128)(2,1)}, bf16[1,1,512]{2,1,0:T(2,128)(2,1)}, u32[]{:S(2)}, u32[]{:S(2)}) collective-permute-start(bf16[1,1,512]{2,1,0:T(2,128)(2,1)} %pad_maximum_fusion.6), channel_id=1, source_target_pairs={{0,12},{4,0},{8,4},{12,8},{1,13},{5,1},{9,5},{13,9},{2,14},{6,2},{... | collective-permute-start | bytes 3080 | tf_op jit(solution)/shard_map/ppermute | solution.py:60
  36.0 1.7 %copy.75 = bf16[1,1,1,256,256]{3,4,2,1,0:T(8,128)(2,1)} copy(bf16[1,1,1,256,256]{4,3,0,2,1:T(8,128)(2,1)} %get-tuple-element.28) | data formatting | bytes 262144 | tf_op jit(solution)/shard_map/slice | solution.py:175
  37.7 1.5 %collective-permute-start.19 = (bf16[256,1024]{1,0:T(8,128)(2,1)}, bf16[256,1024]{1,0:T(8,128)(2,1)}, u32[]{:S(2)}, u32[]{:S(2)}) collective-permute-start(bf16[256,1024]{1,0:T(8,128)(2,1)} %bitcast), channel_id=1, source_target_pairs={{0,2},{2,0},{1,3},{3,1},{4,6},{6,4},{5,7},{7,5},{8,10},{10,8},{9,1... | collective-permute-start | bytes 1572872 | tf_op jit(solution)/shard_map/ppermute | solution.py:143
  39.9 1.3 gather_fusion.1
  43.9 1.4 fusion.72
  47.6 1.3 convert_convert_fusion
  56.2 1.3 fusion.14
  60.0 1.4 multiply_reduce_fusion.2
  62.1 3.7 %collective-permute-start.10 = (f32[1]{0:T(128)}, f32[1]{0:T(128)}, u32[]{:S(2)}, u32[]{:S(2)}) collective-permute-start(f32[1]{0:T(128)} %bitcast.72), channel_id=1, source_target_pairs={{0,4},{4,8},{8,12},{12,0},{1,5},{5,9},{9,13},{13,1},{2,6},{6,10},{... | collective-permute-start | bytes 20 | tf_op jit(solution)/shard_map/ppermute | solution.py:75
  65.8 3.3 %collective-permute-start.11 = (f32[1]{0:T(128)}, f32[1]{0:T(128)}, u32[]{:S(2)}, u32[]{:S(2)}) collective-permute-start(f32[1]{0:T(128)} %bitcast.72), channel_id=1, source_target_pairs={{0,8},{4,12},{8,0},{12,4},{1,9},{5,13},{9,1},{13,5},{2,10},{6,14},... | collective-permute-start | bytes 20 | tf_op jit(solution)/shard_map/ppermute | solution.py:75
  69.1 1.6 %collective-permute-start.12 = (f32[1]{0:T(128)}, f32[1]{0:T(128)}, u32[]{:S(2)}, u32[]{:S(2)}) collective-permute-start(f32[1]{0:T(128)} %bitcast.72), channel_id=1, source_target_pairs={{0,12},{4,0},{8,4},{12,8},{1,13},{5,1},{9,5},{13,9},{2,14},{6,2},{... | collective-permute-start | bytes 20 | tf_op jit(solution)/shard_map/ppermute | solution.py:75
  77.1 2.2 %collective-permute-start.15 = (f32[1,1,512]{2,1,0:T(1,128)S(1)}, f32[1,1,512]{2,1,0:T(1,128)S(1)}, u32[]{:S(2)}, u32[]{:S(2)}) collective-permute-start(f32[1,1,512]{2,1,0:T(1,128)S(1)} %get-tuple-element.35), channel_id=1, source_target_pairs={{0,12},{4,0},{8,4},{12,8},{1,13},{5,1},{9,5},{13,9},{2,14},{6,2},{... | collective-permute-start | bytes 6152 | tf_op jit(solution)/shard_map/ppermute | solution.py:89
  80.8 3.0 %collective-permute-done.14 = f32[1,1,512]{2,1,0:T(1,128)S(1)} collective-permute-done((f32[1,1,512]{2,1,0:T(1,128)S(1)}, f32[1,1,512]{2,1,0:T(1,128)S(1)}, u32[]{:S(2)}, u32[]{:S(2)}) %collective-permute-start.14) | collective-permute-done | bytes 2080 | tf_op jit(solution)/shard_map/ppermute | solution.py:89
  85.9 2.7 %constant_dynamic-update-slice_fusion.3 = bf16[3,1024,512]{2,1,0:T(8,128)(2,1)} fusion(bf16[3,1024,256]{2,1,0:T(8,128)(2,1)} %param.16), kind=kLoop, calls=%fused_computation.104 | loop fusion | bytes 3145728
  89.5 2.7 %constant_dynamic-update-slice_fusion.2 = bf16[3,1024,512]{2,1,0:T(8,128)(2,1)} fusion(bf16[3,1024,512]{2,1,0:T(8,128)(2,1)} %constant_dynamic-update-slice_fusion.3, bf16[3,1024,256]{2,1,0:T(8,128)(2,1)} %collective-permute-done.17), kind=kLoop, calls=%fused_computation.103 | loop fusion | bytes 3145728 | tf_op jit(solution)/shard_map/concatenate | solution.py:96
  92.2 1.6 %fusion.9 = f32[1,1024]{1,0:T(1,128)S(1)} fusion(bf16[512,1]{0,1:T(2,128)(2,1)S(1)} %reshape.1155, bf16[3,1024,512]{2,1,0:T(8,128)(2,1)} %constant_dynamic-update-slice_fusion.2), kind=kOutput, calls=%fused_computation.26 | convolution fusion | flops 1048576 | bytes 1053696 | tf_op jit(solution)/shard_map/qcf,df->qcd/dot_general | solution.py:15
  93.8 1.7 %fusion.10 = f32[256,1024]{1,0:T(8,128)S(1)} fusion(bf16[3,1024,512]{2,1,0:T(8,128)(2,1)} %constant_dynamic-update-slice_fusion.2, bf16[1,1,513,512]{2,3,1,0:T(8,128)(2,1)S(1)} %pad_maximum_fusion), kind=kOutput, calls=%fused_computation.28 | convolution fusion | flops 268435456 | bytes 2359296 | tf_op jit(solution)/shard_map/qcsf,df->qcsd/dot_general | solution.py:15
  95.6 2.1 %fusion.18 = (f32[256]{0:T(256)S(1)}, f32[256,1024]{1,0:T(8,128)S(1)}) fusion(f32[1,1,256,1024]{3,2,1,0:T(8,128)S(1)} %get-tuple-element.48, f32[256]{0:T(256)S(1)} %copy-done.20, f32[256]{0:T(256)S(1)} %copy-done.16, f32[1024]{0:T(1024)S(1)} %copy-done.28, f32[1024]{0:T(1024)S(1)} %get-tuple-element.20, f32[1024]{0:T(1024)S(1)} %bitcast.380, ...), kind=kOutput, calls=%fused_computation.38 | convolution fusion | flops 271056640 | bytes 4472320 | tf_op jit(solution)/shard_map/qcsf,df->qcsd/dot_general | solution.py:15
  97.8 1.6 %convolution_convert_fusion.3 = bf16[256,256]{0,1:T(8,128)(2,1)S(1)} fusion(bf16[256,1024]{1,0:T(8,128)(2,1)} %param.14, f32[1,1,256,1024]{3,2,1,0:T(8,128)S(1)} %get-tuple-element.48, f32[256,1024]{1,0:T(8,128)S(1)} %get-tuple-element.50, f32[256]{0:T(256)S(1)} %broadcast_multiply_fusion.1, f32[256]{0:T(256)S(1)} %broadcast_multiply_fusion.2, ...), kind=kOutput, calls=%fused_computation.22 | convolution fusion | flops 136118272 | bytes 2756608 | tf_op jit(solution)/shard_map/qcsd,fd->qcsf/dot_general | solution.py:15
  104.2 1.6 %fusion.25 = f32[1024,384]{0,1:T(8,128)S(1)} fusion(bf16[4,1024]{1,0:T(4,128)(2,1)S(1)} %get-tuple-element.33, bf16[256,1024]{1,0:T(8,128)(2,1)} %bitcast, s32[]{:T(128)S(6)} %select_n.237, bf16[256,768]{0,1:T(8,128)(2,1)S(1)} %bitcast.346, bf16[4,768]{0,1:T(8,128)(2,1)S(1)} %copy.82), kind=kOutput, calls=%fused_computation.57 | convolution fusion | flops 205936640 | bytes 2504708 | tf_op jit(solution)/shard_map/rd,rf->df/dot_general | solution.py:15
  105.8 5.4 %collective-permute-done.18 = bf16[103936]{0:T(1024)(128)(2,1)S(1)} collective-permute-done((bf16[103936]{0:T(1024)(128)(2,1)S(1)}, bf16[103936]{0:T(1024)(128)(2,1)S(1)}, u32[]{:S(2)}, u32[]{:S(2)}) %collective-permute-start.18) | collective-permute-done | bytes 207904 | tf_op jit(solution)/shard_map/ppermute | solution.py:328
  111.4 1.4 %fusion.141 = f32[384,1024]{1,0:T(8,128)S(1)} fusion(bf16[256,384]{1,0:T(8,128)(2,1)S(1)} %slice.153, bf16[256,1024]{1,0:T(8,128)(2,1)} %collective-permute-done.19), kind=kOutput, calls=%fused_computation.263 | convolution fusion | flops 201326592 | bytes 2293760 | tf_op jit(solution)/shard_map/rd,rf->df/dot_general | solution.py:15
  114.4 1.9 %collective-permute-start.20 = (bf16[256,384]{0,1:T(8,128)(2,1)S(1)}, bf16[256,384]{0,1:T(8,128)(2,1)S(1)}, u32[]{:S(2)}, u32[]{:S(2)}) collective-permute-start(bf16[256,384]{0,1:T(8,128)(2,1)S(1)} %get-tuple-element.22), channel_id=1, source_target_pairs={{0,4},{4,8},{8,12},{12,0},{1,5},{5,9},{9,13},{13,1},{2,6},{6,10},{... | collective-permute-start | bytes 589832 | tf_op jit(solution)/shard_map/ppermute | solution.py:89
  116.3 4.5 %collective-permute-done.22 = bf16[256,384]{0,1:T(8,128)(2,1)S(1)} collective-permute-done((bf16[256,384]{0,1:T(8,128)(2,1)S(1)}, bf16[256,384]{0,1:T(8,128)(2,1)S(1)}, u32[]{:S(2)}, u32[]{:S(2)}) %collective-permute-start.22) | collective-permute-done | bytes 196640 | tf_op jit(solution)/shard_map/ppermute | solution.py:89
  120.8 10.9 %collective-permute-done.21 = bf16[256,384]{0,1:T(8,128)(2,1)S(1)} collective-permute-done((bf16[256,384]{0,1:T(8,128)(2,1)S(1)}, bf16[256,384]{0,1:T(8,128)(2,1)S(1)}, u32[]{:S(2)}, u32[]{:S(2)}) %collective-permute-start.21) | collective-permute-done | bytes 196640 | tf_op jit(solution)/shard_map/ppermute | solution.py:89
  132.4 5.5 %collective-permute-done.23 = bf16[256,384]{0,1:T(8,128)(2,1)S(1)} collective-permute-done((bf16[256,384]{0,1:T(8,128)(2,1)S(1)}, bf16[256,384]{0,1:T(8,128)(2,1)S(1)}, u32[]{:S(2)}, u32[]{:S(2)}) %collective-permute-start.23) | collective-permute-done | bytes 196640 | tf_op jit(solution)/shard_map/ppermute | solution.py:339
  (270 shorter events, 46.9 us)
Async XLA Ops:
  1.4 10.9 %collective-permute-start.2 = (f32[1,1,1025]{2,1,0:T(1,128)S(1)}, f32[1,1,1025]{2,1,0:T(1,128)S(1)}, u32[]{:S(2)}, u32[]{:S(2)}) collective-permute-start(f32[1,1,1025]{2,1,0:T(1,128)S(1)} %pad_maximum_fusion.5), channel_id=1, source_target_pairs={{0,12},{4,0},{8,4},{12,8},{1,13},{5,1},{9,5},{13,9},{2,14},{6,2},{... | collective-permute-start | bytes 12308 | tf_op jit(solution)/shard_map/ppermute | solution.py:60
  6.5 5.9 %collective-permute-start.1 = (f32[1,1,1025]{2,1,0:T(1,128)S(1)}, f32[1,1,1025]{2,1,0:T(1,128)S(1)}, u32[]{:S(2)}, u32[]{:S(2)}) collective-permute-start(f32[1,1,1025]{2,1,0:T(1,128)S(1)} %pad_maximum_fusion.5), channel_id=1, source_target_pairs={{0,8},{4,12},{8,0},{12,4},{1,9},{5,13},{9,1},{13,5},{2,10},{6,14},... | collective-permute-start | bytes 12308 | tf_op jit(solution)/shard_map/ppermute | solution.py:60
  6.5 5.9 %collective-permute-start = (f32[1,1,1025]{2,1,0:T(1,128)S(1)}, f32[1,1,1025]{2,1,0:T(1,128)S(1)}, u32[]{:S(2)}, u32[]{:S(2)}) collective-permute-start(f32[1,1,1025]{2,1,0:T(1,128)S(1)} %pad_maximum_fusion.5), channel_id=1, source_target_pairs={{0,4},{4,8},{8,12},{12,0},{1,5},{5,9},{9,13},{13,1},{2,6},{6,10},{... | collective-permute-start | bytes 12308 | tf_op jit(solution)/shard_map/ppermute | solution.py:60
  7.5 13.0 %collective-permute-start.4 = (bf16[256,1024]{1,0:T(8,128)(2,1)}, bf16[256,1024]{1,0:T(8,128)(2,1)}, u32[]{:S(2)}, u32[]{:S(2)}) collective-permute-start(bf16[256,1024]{1,0:T(8,128)(2,1)} %param.14), channel_id=1, source_target_pairs={{0,1},{1,0},{2,3},{3,2},{4,5},{5,4},{6,7},{7,6},{8,9},{9,8},{10,11... | collective-permute-start | bytes 1572872 | tf_op jit(solution)/shard_map/ppermute | solution.py:95
  7.5 48.1 %collective-permute-start.9 = (bf16[256,1024]{1,0:T(8,128)(2,1)}, bf16[256,1024]{1,0:T(8,128)(2,1)}, u32[]{:S(2)}, u32[]{:S(2)}) collective-permute-start(bf16[256,1024]{1,0:T(8,128)(2,1)} %param.17), channel_id=1, source_target_pairs={{0,1},{1,0},{2,3},{3,2},{4,5},{5,4},{6,7},{7,6},{8,9},{9,8},{10,11... | collective-permute-start | bytes 1572872 | tf_op jit(solution)/shard_map/ppermute | solution.py:95
  8.1 39.5 %copy-start.9 = (pred[4]{0:T(512)(128)(4,1)}, pred[4]{0:T(512)(128)(4,1)S(1)}, u32[]{:S(2)}) copy-start(pred[4]{0:T(512)(128)(4,1)S(1)} %get-tuple-element.54) | copy-start | bytes 16
  12.3 77.2 %collective-permute-start.17 = (bf16[3,1024,256]{2,1,0:T(8,128)(2,1)}, bf16[3,1024,256]{2,1,0:T(8,128)(2,1)}, u32[]{:S(2)}, u32[]{:S(2)}) collective-permute-start(bf16[3,1024,256]{2,1,0:T(8,128)(2,1)} %param.16), channel_id=1, source_target_pairs={{0,1},{1,0},{2,3},{3,2},{4,5},{5,4},{6,7},{7,6},{8,9},{9,8},{10,11... | collective-permute-start | bytes 4718600 | tf_op jit(solution)/shard_map/ppermute | solution.py:95
  16.6 3.8 %collective-permute-start.3 = (bf16[1,1,256,256]{2,3,1,0:T(8,128)(2,1)S(1)}, bf16[1,1,256,256]{2,3,1,0:T(8,128)(2,1)S(1)}, u32[]{:S(2)}, u32[]{:S(2)}) collective-permute-start(bf16[1,1,256,256]{2,3,1,0:T(8,128)(2,1)S(1)} %bitcast.398), channel_id=1, source_target_pairs={{0,1},{1,0},{2,3},{3,2},{4,5},{5,4},{6,7},{7,6},{8,9},{9,8},{10,11... | collective-permute-start | bytes 393224 | tf_op jit(solution)/shard_map/ppermute | solution.py:95
  24.5 31.8 %copy-start.1 = (bf16[256,1024]{1,0:T(8,128)(2,1)S(1)}, bf16[256,1024]{1,0:T(8,128)(2,1)}, u32[]{:S(2)}) copy-start(bf16[256,1024]{1,0:T(8,128)(2,1)} %param.17) | copy-start | bytes 1572868
  27.1 10.6 %collective-permute-start.7 = (bf16[1,1,512]{2,1,0:T(2,128)(2,1)}, bf16[1,1,512]{2,1,0:T(2,128)(2,1)}, u32[]{:S(2)}, u32[]{:S(2)}) collective-permute-start(bf16[1,1,512]{2,1,0:T(2,128)(2,1)} %pad_maximum_fusion.6), channel_id=1, source_target_pairs={{0,12},{4,0},{8,4},{12,8},{1,13},{5,1},{9,5},{13,9},{2,14},{6,2},{... | collective-permute-start | bytes 3080 | tf_op jit(solution)/shard_map/ppermute | solution.py:60
  29.9 9.3 %collective-permute-start.6 = (bf16[1,1,512]{2,1,0:T(2,128)(2,1)}, bf16[1,1,512]{2,1,0:T(2,128)(2,1)}, u32[]{:S(2)}, u32[]{:S(2)}) collective-permute-start(bf16[1,1,512]{2,1,0:T(2,128)(2,1)} %pad_maximum_fusion.6), channel_id=1, source_target_pairs={{0,8},{4,12},{8,0},{12,4},{1,9},{5,13},{9,1},{13,5},{2,10},{6,14},... | collective-permute-start | bytes 3080 | tf_op jit(solution)/shard_map/ppermute | solution.py:60
  31.0 8.2 %collective-permute-start.5 = (bf16[1,1,512]{2,1,0:T(2,128)(2,1)}, bf16[1,1,512]{2,1,0:T(2,128)(2,1)}, u32[]{:S(2)}, u32[]{:S(2)}) collective-permute-start(bf16[1,1,512]{2,1,0:T(2,128)(2,1)} %pad_maximum_fusion.6), channel_id=1, source_target_pairs={{0,4},{4,8},{8,12},{12,0},{1,5},{5,9},{9,13},{13,1},{2,6},{6,10},{... | collective-permute-start | bytes 3080 | tf_op jit(solution)/shard_map/ppermute | solution.py:60
  37.7 73.7 %collective-permute-start.19 = (bf16[256,1024]{1,0:T(8,128)(2,1)}, bf16[256,1024]{1,0:T(8,128)(2,1)}, u32[]{:S(2)}, u32[]{:S(2)}) collective-permute-start(bf16[256,1024]{1,0:T(8,128)(2,1)} %bitcast), channel_id=1, source_target_pairs={{0,2},{2,0},{1,3},{3,1},{4,6},{6,4},{5,7},{7,5},{8,10},{10,8},{9,1... | collective-permute-start | bytes 1572872 | tf_op jit(solution)/shard_map/ppermute | solution.py:143
  54.7 1.5 %collective-permute-start.8 = (bf16[1,1,256]{2,1,0:T(2,128)(2,1)}, bf16[1,1,256]{2,1,0:T(2,128)(2,1)}, u32[]{:S(2)}, u32[]{:S(2)}) collective-permute-start(bf16[1,1,256]{2,1,0:T(2,128)(2,1)} %convert_element_type.264), channel_id=1, source_target_pairs={{0,1},{1,0},{2,3},{3,2},{4,5},{5,4},{6,7},{7,6},{8,9},{9,8},{10,11... | collective-permute-start | bytes 1544 | tf_op jit(solution)/shard_map/ppermute | solution.py:95
  54.8 20.9 %copy-start.2 = (bf16[1,1,1,256,256]{3,4,2,1,0:T(8,128)(2,1)S(1)}, bf16[1,1,1,256,256]{3,4,2,1,0:T(8,128)(2,1)}, u32[]{:S(2)}) copy-start(bf16[1,1,1,256,256]{3,4,2,1,0:T(8,128)(2,1)} %copy.75) | copy-start | bytes 393220
  54.8 21.1 %copy-start.36 = (bf16[4,4,64]{2,1,0:T(4,128)(2,1)S(1)}, bf16[4,4,64]{2,1,0:T(4,128)(2,1)}, u32[]{:S(2)}) copy-start(bf16[4,4,64]{2,1,0:T(4,128)(2,1)} %copy-done.35) | copy-start | bytes 6148
  54.8 22.1 %copy-start.25 = (f32[4,4]{0,1:T(4,128)S(1)}, f32[4,4]{0,1:T(4,128)}, u32[]{:S(2)}) copy-start(f32[4,4]{0,1:T(4,128)} %get-tuple-element.13) | copy-start | bytes 196
  54.8 25.3 %copy-start.10 = (f32[4,256]{1,0:T(4,128)S(1)}, f32[4,256]{1,0:T(4,128)}, u32[]{:S(2)}) copy-start(f32[4,256]{1,0:T(4,128)} %get-tuple-element.17) | copy-start | bytes 12292
  55.6 24.6 %copy-start.34 = (bf16[4,4,64]{2,1,0:T(4,128)(2,1)S(1)}, bf16[4,4,64]{2,1,0:T(4,128)(2,1)}, u32[]{:S(2)}) copy-start(bf16[4,4,64]{2,1,0:T(4,128)(2,1)} %copy-done.33) | copy-start | bytes 6148
  55.6 29.3 %copy-start.18 = (pred[256]{0:T(512)(128)(4,1)S(1)}, pred[256]{0:T(512)(128)(4,1)}, u32[]{:S(2)}) copy-start(pred[256]{0:T(512)(128)(4,1)} %copy-done.17) | copy-start | bytes 772
  62.1 8.7 %collective-permute-start.10 = (f32[1]{0:T(128)}, f32[1]{0:T(128)}, u32[]{:S(2)}, u32[]{:S(2)}) collective-permute-start(f32[1]{0:T(128)} %bitcast.72), channel_id=1, source_target_pairs={{0,4},{4,8},{8,12},{12,0},{1,5},{5,9},{9,13},{13,1},{2,6},{6,10},{... | collective-permute-start | bytes 20 | tf_op jit(solution)/shard_map/ppermute | solution.py:75
  65.8 5.6 %collective-permute-start.11 = (f32[1]{0:T(128)}, f32[1]{0:T(128)}, u32[]{:S(2)}, u32[]{:S(2)}) collective-permute-start(f32[1]{0:T(128)} %bitcast.72), channel_id=1, source_target_pairs={{0,8},{4,12},{8,0},{12,4},{1,9},{5,13},{9,1},{13,5},{2,10},{6,14},... | collective-permute-start | bytes 20 | tf_op jit(solution)/shard_map/ppermute | solution.py:75
  69.1 3.6 %collective-permute-start.12 = (f32[1]{0:T(128)}, f32[1]{0:T(128)}, u32[]{:S(2)}, u32[]{:S(2)}) collective-permute-start(f32[1]{0:T(128)} %bitcast.72), channel_id=1, source_target_pairs={{0,12},{4,0},{8,4},{12,8},{1,13},{5,1},{9,5},{13,9},{2,14},{6,2},{... | collective-permute-start | bytes 20 | tf_op jit(solution)/shard_map/ppermute | solution.py:75
  77.1 3.6 %collective-permute-start.15 = (f32[1,1,512]{2,1,0:T(1,128)S(1)}, f32[1,1,512]{2,1,0:T(1,128)S(1)}, u32[]{:S(2)}, u32[]{:S(2)}) collective-permute-start(f32[1,1,512]{2,1,0:T(1,128)S(1)} %get-tuple-element.35), channel_id=1, source_target_pairs={{0,12},{4,0},{8,4},{12,8},{1,13},{5,1},{9,5},{13,9},{2,14},{6,2},{... | collective-permute-start | bytes 6152 | tf_op jit(solution)/shard_map/ppermute | solution.py:89
  79.3 4.5 %collective-permute-start.14 = (f32[1,1,512]{2,1,0:T(1,128)S(1)}, f32[1,1,512]{2,1,0:T(1,128)S(1)}, u32[]{:S(2)}, u32[]{:S(2)}) collective-permute-start(f32[1,1,512]{2,1,0:T(1,128)S(1)} %get-tuple-element.36), channel_id=1, source_target_pairs={{0,8},{4,12},{8,0},{12,4},{1,9},{5,13},{9,1},{13,5},{2,10},{6,14},... | collective-permute-start | bytes 6152 | tf_op jit(solution)/shard_map/ppermute | solution.py:89
  79.6 5.4 %collective-permute-start.13 = (f32[1,1,512]{2,1,0:T(1,128)S(1)}, f32[1,1,512]{2,1,0:T(1,128)S(1)}, u32[]{:S(2)}, u32[]{:S(2)}) collective-permute-start(f32[1,1,512]{2,1,0:T(1,128)S(1)} %get-tuple-element.34), channel_id=1, source_target_pairs={{0,4},{4,8},{8,12},{12,0},{1,5},{5,9},{9,13},{13,1},{2,6},{6,10},{... | collective-permute-start | bytes 6152 | tf_op jit(solution)/shard_map/ppermute | solution.py:89
  85.9 3.4 %collective-permute-start.16 = (bf16[1,1,513,256]{2,3,1,0:T(8,128)(2,1)}, bf16[1,1,513,256]{2,3,1,0:T(8,128)(2,1)S(1)}, u32[]{:S(2)}, u32[]{:S(2)}) collective-permute-start(bf16[1,1,513,256]{2,3,1,0:T(8,128)(2,1)} %pad_maximum_fusion.2), channel_id=1, source_target_pairs={{0,1},{1,0},{2,3},{3,2},{4,5},{5,4},{6,7},{7,6},{8,9},{9,8},{10,11... | collective-permute-start | bytes 787976 | tf_op jit(solution)/shard_map/ppermute | solution.py:95
  103.6 7.6 %collective-permute-start.18 = (bf16[103936]{0:T(1024)(128)(2,1)S(1)}, bf16[103936]{0:T(1024)(128)(2,1)S(1)}, u32[]{:S(2)}, u32[]{:S(2)}) collective-permute-start(bf16[103936]{0:T(1024)(128)(2,1)S(1)} %pad_maximum_fusion.3), channel_id=1, source_target_pairs={{0,2},{2,0},{1,3},{3,1},{4,6},{6,4},{5,7},{7,5},{8,10},{10,8},{9,1... | collective-permute-start | bytes 623624 | tf_op jit(solution)/shard_map/ppermute | solution.py:328
  113.3 7.5 %collective-permute-start.22 = (bf16[256,384]{0,1:T(8,128)(2,1)S(1)}, bf16[256,384]{0,1:T(8,128)(2,1)S(1)}, u32[]{:S(2)}, u32[]{:S(2)}) collective-permute-start(bf16[256,384]{0,1:T(8,128)(2,1)S(1)} %get-tuple-element.23), channel_id=1, source_target_pairs={{0,12},{4,0},{8,4},{12,8},{1,13},{5,1},{9,5},{13,9},{2,14},{6,2},{... | collective-permute-start | bytes 589832 | tf_op jit(solution)/shard_map/ppermute | solution.py:89
  113.7 18.0 %collective-permute-start.21 = (bf16[256,384]{0,1:T(8,128)(2,1)S(1)}, bf16[256,384]{0,1:T(8,128)(2,1)S(1)}, u32[]{:S(2)}, u32[]{:S(2)}) collective-permute-start(bf16[256,384]{0,1:T(8,128)(2,1)S(1)} %get-tuple-element.24), channel_id=1, source_target_pairs={{0,8},{4,12},{8,0},{12,4},{1,9},{5,13},{9,1},{13,5},{2,10},{6,14},... | collective-permute-start | bytes 589832 | tf_op jit(solution)/shard_map/ppermute | solution.py:89
  114.4 17.4 %collective-permute-start.20 = (bf16[256,384]{0,1:T(8,128)(2,1)S(1)}, bf16[256,384]{0,1:T(8,128)(2,1)S(1)}, u32[]{:S(2)}, u32[]{:S(2)}) collective-permute-start(bf16[256,384]{0,1:T(8,128)(2,1)S(1)} %get-tuple-element.22), channel_id=1, source_target_pairs={{0,4},{4,8},{8,12},{12,0},{1,5},{5,9},{9,13},{13,1},{2,6},{6,10},{... | collective-permute-start | bytes 589832 | tf_op jit(solution)/shard_map/ppermute | solution.py:89
  131.9 6.0 %collective-permute-start.23 = (bf16[256,384]{0,1:T(8,128)(2,1)S(1)}, bf16[256,384]{0,1:T(8,128)(2,1)S(1)}, u32[]{:S(2)}, u32[]{:S(2)}) collective-permute-start(bf16[256,384]{0,1:T(8,128)(2,1)S(1)} %add_convert_fusion), channel_id=1, source_target_pairs={{0,2},{2,0},{1,3},{3,1},{4,6},{6,4},{5,7},{7,5},{8,10},{10,8},{9,1... | collective-permute-start | bytes 589832 | tf_op jit(solution)/shard_map/ppermute | solution.py:339
  (31 other events, 105.6 us)

commit v19 on v8

--- a/solution.py
+++ b/solution.py
@@ -135,7 +135,7 @@
     head_shape = (lists, local_cands, seq_len, local_heads, HEAD_DIM)
     cls_shape = (lists, cand_count, local_heads, HEAD_DIM)
     out_first_full = gather_mp(w_out_first, 0)
-    last_full = gather_mp(w_last, 2)
+    other_last = lax.ppermute(w_last, "mp", [(0, 1), (1, 0)])
     out_last_full = gather_mp(w_out_last, 0)
     cls_and_teacher = gather_cand(
         jnp.concatenate([tokens[:, :, 0].astype(jnp.float32), teacher[..., None]], -1), 1
@@ -265,13 +265,18 @@
         axis=3,
         tiled=True,
     )
-    key_joined = joined[:, :, :seq_len]
-    val_joined = joined[:, :, seq_len : 2 * seq_len]
-    query_joined = joined[:, :, 2 * seq_len]
-    summed_term = mixed("qcsf,df->qcsd", key_joined, last_full[1]) + mixed(
-        "qcsf,df->qcsd", val_joined, last_full[2]
-    )
-    query_term = mixed("qcf,df->qcd", query_joined, last_full[0])
+    partner = lax.dynamic_slice_in_dim(
+        joined, (1 - lax.axis_index("mp")) * local_width, local_width, 3
+    )
+    summed_term = (
+        mixed("qcsf,df->qcsd", key_grad, w_last[1])
+        + mixed("qcsf,df->qcsd", val_grad, w_last[2])
+        + mixed("qcsf,df->qcsd", partner[:, :, :seq_len], other_last[1])
+        + mixed("qcsf,df->qcsd", partner[:, :, seq_len : 2 * seq_len], other_last[2])
+    )
+    query_term = mixed("qcf,df->qcd", grad_query_last, w_last[0]) + mixed(
+        "qcf,df->qcd", partner[:, :, 2 * seq_len], other_last[0]
+    )
     summed_term = jnp.where(first_cols, summed_term + query_term[:, :, None], summed_term)
     grad_hidden = jnp.where(first_cols, summed_term + grad_last[:, :, None], summed_term)
     grad_first = norm_backward(grad_hidden, unit_first, inverse_first, gain_first).astype(

time: 116 us -> 119 us (1.026)
  matrix products: 20.8 us -> 27.7 us
  other arithmetic: 13.9 us -> 10.5 us
  waiting for transfers between devices: 30 us -> 28.6 us
    dot_general x32 -> x35, matrix products: 20.8 us -> 27.7 us  [mixed(): jnp.einsum(pattern, former, latter, preferred_element_type=jnp.float32)]
    select_n x1 -> x0, other arithmetic: 3.41 us -> none  [gather_mp(): jnp.where(lax.axis_index('mp') == 0, jnp.concatenate([block, other], axis...]
    ppermute x6, waiting for transfers between devices: 17.9 us -> 16.5 us  [scatter_cand(): lax.ppermute(piece, 'cand', [(j, (j + k) % count) for j in range(count)])]
  transfers between devices with their start and end apart: 21 -> 21, of which waited for: 8 -> 8; matrix products, arithmetic and copies ran while one was open for 33% -> 35% of each run, Pallas kernels for 0% -> 0%
where the time goes in v19:
time: 119 us; the launch traced here: 118 us
  waiting for transfers between devices  28.6 us (24%)
  starting transfers between devices  28.3 us (24%)
  matrix products  27.7 us (23%)
  other arithmetic  10.5 us (9%)
  between operations  8.66 us (7%)
  local copies, waits for them, and re-layouts  7.77 us (7%)
  blocking collectives  6.37 us (5%)
    dot_general x35, matrix products, mixed(): jnp.einsum(pattern, former, latter, preferred_element_type=jnp.float32)  27.7 us
    ppermute x6, waiting for transfers between devices, scatter_cand(): lax.ppermute(piece, 'cand', [(j, (j + k) % count) for j in range(count)])  16.5 us
    ppermute x6, starting transfers between devices, scatter_cand(): lax.ppermute(piece, 'cand', [(j, (j + k) % count) for j in range(count)])  8.88 us
    ppermute x6, starting transfers between devices, gather_cand(): lax.ppermute(block, 'cand', [(j, (j + k) % count) for j in range(count)])  8.45 us
    ppermute x3, starting transfers between devices, sum_cand(): lax.ppermute(block, 'cand', [(j, (j + k) % count) for j in range(count)])  7.77 us
    ppermute x1, waiting for transfers between devices, local(): partner = lax.ppermute(reduced, 'query', swap)  5.97 us
    ppermute x1, waiting for transfers between devices, local(): lax.ppermute(jnp.concatenate([given_half.reshape(-1), cls_flat.reshape(-1...  5.05 us
    all_gather x1, blocking collectives, local(): lax.all_gather(jnp.concatenate([key_grad, val_grad, grad_query_last[:, :,...  2.46 us
  transfers between devices with their start and end apart: 21, of which 8 were waited for; matrix products, arithmetic and copies ran while one was open for 35% of the time, Pallas kernels for 0%

profile of v19, /device:TPU:8, one launch (start us, length us, event | category | flops | bytes accessed | tf_op | source)
XLA Modules:
  0.0 118.0 jit_solution(945010540695949987)
XLA Ops:
  1.4 1.6 %collective-permute-start = (f32[1,1,1025]{2,1,0:T(1,128)S(1)}, f32[1,1,1025]{2,1,0:T(1,128)S(1)}, u32[]{:S(2)}, u32[]{:S(2)}) collective-permute-start(f32[1,1,1025]{2,1,0:T(1,128)S(1)} %pad_maximum_fusion.4), channel_id=1, source_target_pairs={{0,4},{4,8},{8,12},{12,0},{1,5},{5,9},{9,13},{13,1},{2,6},{6,10},{... | collective-permute-start | bytes 12308 | tf_op jit(solution)/shard_map/ppermute | solution.py:60
  4.1 1.9 %collective-permute-start.2 = (f32[1,1,1025]{2,1,0:T(1,128)S(1)}, f32[1,1,1025]{2,1,0:T(1,128)S(1)}, u32[]{:S(2)}, u32[]{:S(2)}) collective-permute-start(f32[1,1,1025]{2,1,0:T(1,128)S(1)} %pad_maximum_fusion.4), channel_id=1, source_target_pairs={{0,12},{4,0},{8,4},{12,8},{1,13},{5,1},{9,5},{13,9},{2,14},{6,2},{... | collective-permute-start | bytes 12308 | tf_op jit(solution)/shard_map/ppermute | solution.py:60
  6.6 2.1 %fusion.6 = bf16[3,1,1,256,256]{3,4,0,2,1:T(8,128)(2,1)S(1)} fusion(bf16[3,1024,256]{2,1,0:T(8,128)(2,1)} %param.13, bf16[1,1,256,1024]{3,2,1,0:T(8,128)(2,1)} %param.10), kind=kOutput, calls=%fused_computation.16 | convolution fusion | flops 402849792 | bytes 2490368 | tf_op jit(solution)/shard_map/qcsd,kdf->kqcsf/dot_general | solution.py:15
  15.1 1.3 %exponential_reduce_fusion = f32[]{:T(128)} fusion(f32[1,4,1025]{2,1,0:T(4,128)S(1)} %bitcast_select_fusion, f32[]{:T(128)} %slice_reduce_fusion.1), kind=kLoop, calls=%fused_computation.224 | loop fusion | flops 7 | bytes 24 | tf_op jit(solution)/shard_map/reduce_sum | solution.py:210
  18.9 2.1 %all_gather.9 = bf16[1,1,256,512]{2,3,1,0:T(8,128)(2,1)S(1)} all-gather(bf16[1,1,256,256]{2,3,1,0:T(8,128)(2,1)S(1)} %bitcast.386), channel_id=1, replica_groups=mesh['groups'=2,'cand'=4,'query'=2,'mp'=2] {'mp'}, dimensions={3}, use_global_device_ids=true | all-gather | bytes 393216 | tf_op jit(solution)/shard_map/all_gather | solution.py:172
  21.1 1.9 %fusion.162 = (f32[256]{0:T(256)S(1)}, f32[1,1,256,1024]{3,2,1,0:T(8,128)S(1)}) fusion(bf16[256,1024]{1,0:T(8,128)(2,1)} %collective-permute-done.3, bf16[256,1024]{1,0:T(8,128)(2,1)S(1)} %copy-done.2, pred[]{:T(512)S(6)} %eq.54, bf16[1,1,256,512]{2,3,1,0:T(8,128)(2,1)S(1)} %all_gather.9, bf16[1,1,256,1024]{3,2,1,0:T(8,128)(2,1)} %param.10), kind=kOutput, calls=%fused_computation.282 | convolution fusion | flops 273940224 | bytes 2884609 | tf_op jit(solution)/shard_map/qcsf,fd->qcsd/dot_general | solution.py:15
  23.5 1.7 %fusion.7 = bf16[2,1,1,256,256]{4,3,0,2,1:T(8,128)(2,1)S(1)} fusion(bf16[3,1024,256]{2,1,0:T(8,128)(2,1)} %param.16, bf16[1,1,256,1024]{3,2,1,0:T(8,128)(2,1)S(1)} %multiply_convert_fusion.1), kind=kOutput, calls=%fused_computation.21 | convolution fusion | flops 268566528 | bytes 1835008 | tf_op jit(solution)/shard_map/qcsd,kdf->kqcsf/dot_general | solution.py:15
  25.4 3.6 %collective-permute-start.5 = (bf16[1,1,512]{2,1,0:T(2,128)(2,1)S(1)}, bf16[1,1,512]{2,1,0:T(2,128)(2,1)S(1)}, u32[]{:S(2)}, u32[]{:S(2)}) collective-permute-start(bf16[1,1,512]{2,1,0:T(2,128)(2,1)S(1)} %pad_maximum_fusion.5), channel_id=1, source_target_pairs={{0,8},{4,12},{8,0},{12,4},{1,9},{5,13},{9,1},{13,5},{2,10},{6,14},... | collective-permute-start | bytes 3080 | tf_op jit(solution)/shard_map/ppermute | solution.py:60
  31.0 1.6 %collective-permute-start.16 = (bf16[256,1024]{1,0:T(8,128)(2,1)}, bf16[256,1024]{1,0:T(8,128)(2,1)}, u32[]{:S(2)}, u32[]{:S(2)}) collective-permute-start(bf16[256,1024]{1,0:T(8,128)(2,1)} %bitcast), channel_id=1, source_target_pairs={{0,2},{2,0},{1,3},{3,1},{4,6},{6,4},{5,7},{7,5},{8,10},{10,8},{9,1... | collective-permute-start | bytes 1572872 | tf_op jit(solution)/shard_map/ppermute | solution.py:149
  34.7 1.8 %all_gather.10 = bf16[1,1,512]{2,1,0:T(2,128)(2,1)S(1)} all-gather(bf16[1,1,256]{2,1,0:T(2,128)(2,1)S(1)} %convert_element_type.300), channel_id=1, replica_groups=mesh['groups'=2,'cand'=4,'query'=2,'mp'=2] {'mp'}, dimensions={2}, use_global_device_ids=true | all-gather | bytes 1536 | tf_op jit(solution)/shard_map/all_gather | solution.py:201
  36.5 1.6 %fusion.15 = f32[1,1024]{1,0:T(1,128)S(1)} fusion(bf16[256,1024]{1,0:T(8,128)(2,1)} %collective-permute-done.7, bf16[256,1024]{1,0:T(8,128)(2,1)S(1)} %copy-done.1, pred[]{:T(512)S(6)} %eq.54, bf16[1,1,512]{2,1,0:T(2,128)(2,1)S(1)} %all_gather.10), kind=kOutput, calls=%fused_computation.34 | convolution fusion | flops 5767168 | bytes 1053697 | tf_op jit(solution)/shard_map/qcf,fd->qcd/dot_general | solution.py:15
  41.8 3.3 %collective-permute-start.8 = (f32[1]{0:T(128)}, f32[1]{0:T(128)}, u32[]{:S(2)}, u32[]{:S(2)}) collective-permute-start(f32[1]{0:T(128)} %bitcast.72), channel_id=1, source_target_pairs={{0,4},{4,8},{8,12},{12,0},{1,5},{5,9},{9,13},{13,1},{2,6},{6,10},{... | collective-permute-start | bytes 20 | tf_op jit(solution)/shard_map/ppermute | solution.py:75
  45.1 3.1 %collective-permute-start.9 = (f32[1]{0:T(128)}, f32[1]{0:T(128)}, u32[]{:S(2)}, u32[]{:S(2)}) collective-permute-start(f32[1]{0:T(128)} %bitcast.72), channel_id=1, source_target_pairs={{0,8},{4,12},{8,0},{12,4},{1,9},{5,13},{9,1},{13,5},{2,10},{6,14},... | collective-permute-start | bytes 20 | tf_op jit(solution)/shard_map/ppermute | solution.py:75
  48.2 1.4 %collective-permute-start.10 = (f32[1]{0:T(128)}, f32[1]{0:T(128)}, u32[]{:S(2)}, u32[]{:S(2)}) collective-permute-start(f32[1]{0:T(128)} %bitcast.72), channel_id=1, source_target_pairs={{0,12},{4,0},{8,4},{12,8},{1,13},{5,1},{9,5},{13,9},{2,14},{6,2},{... | collective-permute-start | bytes 20 | tf_op jit(solution)/shard_map/ppermute | solution.py:75
  56.7 2.9 %collective-permute-start.12 = (f32[1,1,512]{2,1,0:T(1,128)S(1)}, f32[1,1,512]{2,1,0:T(1,128)S(1)}, u32[]{:S(2)}, u32[]{:S(2)}) collective-permute-start(f32[1,1,512]{2,1,0:T(1,128)S(1)} %get-tuple-element.36), channel_id=1, source_target_pairs={{0,8},{4,12},{8,0},{12,4},{1,9},{5,13},{9,1},{13,5},{2,10},{6,14},... | collective-permute-start | bytes 6152 | tf_op jit(solution)/shard_map/ppermute | solution.py:89
  61.3 1.3 %fusion.43 = f32[1,1024]{1,0:T(1,128)S(1)} fusion(bf16[256,1]{0,1:T(2,128)(2,1)S(1)} %reshape.1360, bf16[3,1024,256]{2,1,0:T(8,128)(2,1)} %param.16), kind=kOutput, calls=%fused_computation.76 | convolution fusion | flops 524288 | bytes 528896 | tf_op jit(solution)/shard_map/qcf,df->qcd/dot_general | solution.py:15
  63.4 2.5 %all_gather.11 = bf16[1,1,513,512]{2,3,1,0:T(8,128)(2,1)S(1)} all-gather(bf16[1,1,513,256]{2,3,1,0:T(8,128)(2,1)S(1)} %pad_maximum_fusion.1), channel_id=1, replica_groups=mesh['groups'=2,'cand'=4,'query'=2,'mp'=2] {'mp'}, dimensions={3}, use_global_device_ids=true | all-gather | bytes 787968 | tf_op jit(solution)/shard_map/all_gather | solution.py:262
  66.0 1.5 %fusion.41 = f32[256,1024]{1,0:T(8,128)S(1)} fusion(bf16[3,1024,256]{2,1,0:T(8,128)(2,1)} %param.16, f32[1,1,256,1,1,1,1,256]{2,7,6,5,4,3,1,0:T(8,128)S(1)} %bitcast.370, f32[256]{0:T(256)S(1)} %bitcast.404, pred[256]{0:T(512)(128)(4,1)S(1)} %iota_compare_fusion.1), kind=kOutput, calls=%fused_computation.74 | convolution fusion | flops 134414336 | bytes 1836288 | tf_op jit(solution)/shard_map/qcsf,df->qcsd/dot_general | solution.py:15
  67.5 1.5 %convolution_add_fusion.1 = f32[256,1024]{1,0:T(8,128)S(1)} fusion(f32[256,1024]{1,0:T(8,128)S(1)} %fusion.41, bf16[3,1024,256]{2,1,0:T(8,128)(2,1)} %param.16, f32[1,1,256,1,1,1,1,256]{2,7,6,5,4,3,1,0:T(8,128)S(1)} %bitcast.368, f32[256]{0:T(256)S(1)} %bitcast.402, pred[256]{0:T(512)(128)(4,1)S(1)} %iota_compare_fusion.1), kind=kOutput, calls=%fused_computation.10 | convolution fusion | flops 134676480 | bytes 2884864 | tf_op jit(solution)/shard_map/qcsf,df->qcsd/dot_general | solution.py:15
  69.0 1.3 %fusion.36 = f32[1,1024]{1,0:T(1,128)S(1)} fusion(bf16[256,1]{0,1:T(2,128)(2,1)S(1)} %reshape.1362, bf16[3,1024,256]{2,1,0:T(8,128)(2,1)} %collective-permute-done.14), kind=kOutput, calls=%fused_computation.67 | convolution fusion | flops 524288 | bytes 528896 | tf_op jit(solution)/shard_map/qcf,df->qcd/dot_general | solution.py:15
  70.3 1.4 %fusion.37 = f32[256,1024]{1,0:T(8,128)S(1)} fusion(bf16[3,1024,256]{2,1,0:T(8,128)(2,1)} %collective-permute-done.14, bf16[1,1,513,512]{2,3,1,0:T(8,128)(2,1)S(1)} %all_gather.11, s32[]{:T(128)S(6)} %add.373, s32[]{:T(128)S(6)} %select_n.285), kind=kOutput, calls=%fused_computation.69 | convolution fusion | flops 134217728 | bytes 1703944 | tf_op jit(solution)/shard_map/qcsf,df->qcsd/dot_general | solution.py:15
  71.7 1.8 %fusion.21 = (f32[256]{0:T(256)S(1)}, f32[256,1024]{1,0:T(8,128)S(1)}) fusion(f32[1,1,256,1024]{3,2,1,0:T(8,128)S(1)} %get-tuple-element.48, f32[256]{0:T(256)S(1)} %add_rsqrt_fusion, f32[256]{0:T(256)S(1)} %broadcast_multiply_fusion.3, f32[1024]{0:T(1024)S(1)} %copy-done.8, f32[1024]{0:T(1024)S(1)} %get-tuple-element.20, f32[1024]{0:T(1024)S(1)} %add.348, ...), kind=kOutput, calls=%fused_computation.41 | convolution fusion | flops 137101056 | bytes 4865540 | tf_op jit(solution)/shard_map/qcsf,df->qcsd/dot_general | solution.py:15
  73.7 1.6 %convolution_convert_fusion.3 = bf16[256,256]{0,1:T(8,128)(2,1)S(1)} fusion(bf16[256,1024]{1,0:T(8,128)(2,1)} %param.14, f32[1,1,256,1024]{3,2,1,0:T(8,128)S(1)} %get-tuple-element.48, f32[256,1024]{1,0:T(8,128)S(1)} %get-tuple-element.50, f32[256]{0:T(256)S(1)} %broadcast_multiply_fusion.1, f32[256]{0:T(256)S(1)} %broadcast_multiply_fusion.2, ...), kind=kOutput, calls=%fused_computation.24 | convolution fusion | flops 136118272 | bytes 2756608 | tf_op jit(solution)/shard_map/qcsd,fd->qcsf/dot_general | solution.py:15
  76.5 1.3 %multiply_reduce_fusion = (f32[4,256]{1,0:T(4,128)S(1)}, f32[4,256,256]{1,2,0:T(8,128)S(1)}) fusion(f32[4,256]{1,0:T(4,128)} %copy-done.10, f32[4,256,256]{1,2,0:T(8,128)S(1)} %get-tuple-element.46, f32[4,256]{1,0:T(4,128)S(1)} %broadcast_select_fusion.2, bf16[256,4,64]{0,2,1:T(8,128)(2,1)S(1)} %bitcast.384, bf16[256,4,64]{0,2,1:T(8,128)(2,1)} %bitcast.388), kind=kOutput, calls=%fused_computation.46 | convolution fusion | flops 34601984 | bytes 2371584 | tf_op jit(solution)/shard_map/qcshe,qcthe->qchst/dot_general | solution.py:15
  81.3 1.6 %fusion.30 = f32[1024,384]{0,1:T(8,128)S(1)} fusion(bf16[4,1024]{1,0:T(4,128)(2,1)S(1)} %get-tuple-element.33, bf16[256,1024]{1,0:T(8,128)(2,1)} %bitcast, s32[]{:T(128)S(6)} %select_n.290, bf16[256,768]{0,1:T(8,128)(2,1)S(1)} %bitcast.366, bf16[4,768]{0,1:T(8,128)(2,1)S(1)} %copy.83), kind=kOutput, calls=%fused_computation.61 | convolution fusion | flops 205936640 | bytes 2504708 | tf_op jit(solution)/shard_map/rd,rf->df/dot_general | solution.py:15
  82.9 5.0 %collective-permute-done.15 = bf16[103936]{0:T(1024)(128)(2,1)S(1)} collective-permute-done((bf16[103936]{0:T(1024)(128)(2,1)S(1)}, bf16[103936]{0:T(1024)(128)(2,1)S(1)}, u32[]{:S(2)}, u32[]{:S(2)}) %collective-permute-start.15) | collective-permute-done | bytes 207904 | tf_op jit(solution)/shard_map/ppermute | solution.py:344
  88.2 1.4 %fusion.166 = f32[384,1024]{1,0:T(8,128)S(1)} fusion(bf16[256,384]{1,0:T(8,128)(2,1)S(1)} %slice.168, bf16[256,1024]{1,0:T(8,128)(2,1)} %collective-permute-done.16), kind=kOutput, calls=%fused_computation.286 | convolution fusion | flops 201326592 | bytes 2293760 | tf_op jit(solution)/shard_map/rd,rf->df/dot_general | solution.py:15
  90.8 2.8 %collective-permute-start.18 = (bf16[256,384]{0,1:T(8,128)(2,1)S(1)}, bf16[256,384]{0,1:T(8,128)(2,1)S(1)}, u32[]{:S(2)}, u32[]{:S(2)}) collective-permute-start(bf16[256,384]{0,1:T(8,128)(2,1)S(1)} %get-tuple-element.24), channel_id=1, source_target_pairs={{0,8},{4,12},{8,0},{12,4},{1,9},{5,13},{9,1},{13,5},{2,10},{6,14},... | collective-permute-start | bytes 589832 | tf_op jit(solution)/shard_map/ppermute | solution.py:89
  94.0 10.4 %collective-permute-done.17 = bf16[256,384]{0,1:T(8,128)(2,1)S(1)} collective-permute-done((bf16[256,384]{0,1:T(8,128)(2,1)S(1)}, bf16[256,384]{0,1:T(8,128)(2,1)S(1)}, u32[]{:S(2)}, u32[]{:S(2)}) %collective-permute-start.17) | collective-permute-done | bytes 196640 | tf_op jit(solution)/shard_map/ppermute | solution.py:89
  104.4 2.7 %collective-permute-done.18 = bf16[256,384]{0,1:T(8,128)(2,1)S(1)} collective-permute-done((bf16[256,384]{0,1:T(8,128)(2,1)S(1)}, bf16[256,384]{0,1:T(8,128)(2,1)S(1)}, u32[]{:S(2)}, u32[]{:S(2)}) %collective-permute-start.18) | collective-permute-done | bytes 196640 | tf_op jit(solution)/shard_map/ppermute | solution.py:89
  107.1 3.1 %collective-permute-done.19 = bf16[256,384]{0,1:T(8,128)(2,1)S(1)} collective-permute-done((bf16[256,384]{0,1:T(8,128)(2,1)S(1)}, bf16[256,384]{0,1:T(8,128)(2,1)S(1)}, u32[]{:S(2)}, u32[]{:S(2)}) %collective-permute-start.19) | collective-permute-done | bytes 196640 | tf_op jit(solution)/shard_map/ppermute | solution.py:89
  110.9 6.0 %collective-permute-done.20 = bf16[256,384]{0,1:T(8,128)(2,1)S(1)} collective-permute-done((bf16[256,384]{0,1:T(8,128)(2,1)S(1)}, bf16[256,384]{0,1:T(8,128)(2,1)S(1)}, u32[]{:S(2)}, u32[]{:S(2)}) %collective-permute-start.20) | collective-permute-done | bytes 196640 | tf_op jit(solution)/shard_map/ppermute | solution.py:355
  (231 shorter events, 30.3 us)
Async XLA Ops:
  1.4 10.0 %collective-permute-start = (f32[1,1,1025]{2,1,0:T(1,128)S(1)}, f32[1,1,1025]{2,1,0:T(1,128)S(1)}, u32[]{:S(2)}, u32[]{:S(2)}) collective-permute-start(f32[1,1,1025]{2,1,0:T(1,128)S(1)} %pad_maximum_fusion.4), channel_id=1, source_target_pairs={{0,4},{4,8},{8,12},{12,0},{1,5},{5,9},{9,13},{13,1},{2,6},{6,10},{... | collective-permute-start | bytes 12308 | tf_op jit(solution)/shard_map/ppermute | solution.py:60
  3.0 8.4 %collective-permute-start.1 = (f32[1,1,1025]{2,1,0:T(1,128)S(1)}, f32[1,1,1025]{2,1,0:T(1,128)S(1)}, u32[]{:S(2)}, u32[]{:S(2)}) collective-permute-start(f32[1,1,1025]{2,1,0:T(1,128)S(1)} %pad_maximum_fusion.4), channel_id=1, source_target_pairs={{0,8},{4,12},{8,0},{12,4},{1,9},{5,13},{9,1},{13,5},{2,10},{6,14},... | collective-permute-start | bytes 12308 | tf_op jit(solution)/shard_map/ppermute | solution.py:60
  4.1 7.3 %collective-permute-start.2 = (f32[1,1,1025]{2,1,0:T(1,128)S(1)}, f32[1,1,1025]{2,1,0:T(1,128)S(1)}, u32[]{:S(2)}, u32[]{:S(2)}) collective-permute-start(f32[1,1,1025]{2,1,0:T(1,128)S(1)} %pad_maximum_fusion.4), channel_id=1, source_target_pairs={{0,12},{4,0},{8,4},{12,8},{1,13},{5,1},{9,5},{13,9},{2,14},{6,2},{... | collective-permute-start | bytes 12308 | tf_op jit(solution)/shard_map/ppermute | solution.py:60
  6.1 15.0 %collective-permute-start.3 = (bf16[256,1024]{1,0:T(8,128)(2,1)}, bf16[256,1024]{1,0:T(8,128)(2,1)}, u32[]{:S(2)}, u32[]{:S(2)}) collective-permute-start(bf16[256,1024]{1,0:T(8,128)(2,1)} %param.14), channel_id=1, source_target_pairs={{0,1},{1,0},{2,3},{3,2},{4,5},{5,4},{6,7},{7,6},{8,9},{9,8},{10,11... | collective-permute-start | bytes 1572872 | tf_op jit(solution)/shard_map/ppermute | solution.py:97
  6.1 30.5 %collective-permute-start.7 = (bf16[256,1024]{1,0:T(8,128)(2,1)}, bf16[256,1024]{1,0:T(8,128)(2,1)}, u32[]{:S(2)}, u32[]{:S(2)}) collective-permute-start(bf16[256,1024]{1,0:T(8,128)(2,1)} %param.17), channel_id=1, source_target_pairs={{0,1},{1,0},{2,3},{3,2},{4,5},{5,4},{6,7},{7,6},{8,9},{9,8},{10,11... | collective-permute-start | bytes 1572872 | tf_op jit(solution)/shard_map/ppermute | solution.py:97
  8.8 3.3 %copy-start = (bf16[3,1024,256]{2,1,0:T(8,128)(2,1)S(1)}, bf16[3,1024,256]{2,1,0:T(8,128)(2,1)}, u32[]{:S(2)}) copy-start(bf16[3,1024,256]{2,1,0:T(8,128)(2,1)} %param.13) | copy-start | bytes 4718596
  8.8 14.2 %copy-start.3 = (bf16[1,1,1,256,256]{3,4,0,2,1:T(8,128)(2,1)}, bf16[1,1,1,256,256]{3,4,0,2,1:T(8,128)(2,1)S(1)}, u32[]{:S(2)}) copy-start(bf16[1,1,1,256,256]{3,4,0,2,1:T(8,128)(2,1)S(1)} %get-tuple-element.26) | copy-start | bytes 393220
  10.7 61.0 %copy-start.5 = (pred[256]{0:T(512)(128)(4,1)}, pred[256]{0:T(512)(128)(4,1)S(1)}, u32[]{:S(2)}) copy-start(pred[256]{0:T(512)(128)(4,1)S(1)} %iota_compare_fusion.1) | copy-start | bytes 772
  11.4 57.6 %collective-permute-start.14 = (bf16[3,1024,256]{2,1,0:T(8,128)(2,1)}, bf16[3,1024,256]{2,1,0:T(8,128)(2,1)}, u32[]{:S(2)}, u32[]{:S(2)}) collective-permute-start(bf16[3,1024,256]{2,1,0:T(8,128)(2,1)} %param.16), channel_id=1, source_target_pairs={{0,1},{1,0},{2,3},{3,2},{4,5},{5,4},{6,7},{7,6},{8,9},{9,8},{10,11... | collective-permute-start | bytes 4718600 | tf_op jit(solution)/shard_map/ppermute | solution.py:138
  12.4 2.5 %copy-start.16 = (bf16[4,4,64]{2,1,0:T(4,128)(2,1)}, bf16[4,4,64]{2,1,0:T(4,128)(2,1)S(1)}, u32[]{:S(2)}) copy-start(bf16[4,4,64]{2,1,0:T(4,128)(2,1)S(1)} %reshape.1268) | copy-start | bytes 6148
  14.3 4.7 %copy-start.10 = (f32[4,256]{1,0:T(4,128)}, f32[4,256]{1,0:T(4,128)S(1)}, u32[]{:S(2)}) copy-start(f32[4,256]{1,0:T(4,128)S(1)} %broadcast_select_fusion.1) | copy-start | bytes 12292
  15.1 3.8 %copy-start.18 = (bf16[4,4,64]{2,1,0:T(4,128)(2,1)}, bf16[4,4,64]{2,1,0:T(4,128)(2,1)S(1)}, u32[]{:S(2)}) copy-start(bf16[4,4,64]{2,1,0:T(4,128)(2,1)S(1)} %reshape.1271) | copy-start | bytes 6148
  23.0 48.7 %copy-start.7 = (f32[256]{0:T(256)}, f32[256]{0:T(256)S(1)}, u32[]{:S(2)}) copy-start(f32[256]{0:T(256)S(1)} %broadcast_multiply_fusion.3) | copy-start | bytes 3076
  23.3 48.4 %copy-start.9 = (f32[256]{0:T(256)}, f32[256]{0:T(256)S(1)}, u32[]{:S(2)}) copy-start(f32[256]{0:T(256)S(1)} %add_rsqrt_fusion) | copy-start | bytes 3076
  25.2 11.4 %copy-start.1 = (bf16[256,1024]{1,0:T(8,128)(2,1)S(1)}, bf16[256,1024]{1,0:T(8,128)(2,1)}, u32[]{:S(2)}) copy-start(bf16[256,1024]{1,0:T(8,128)(2,1)} %param.17) | copy-start | bytes 1572868
  25.3 5.7 %collective-permute-start.4 = (bf16[1,1,512]{2,1,0:T(2,128)(2,1)S(1)}, bf16[1,1,512]{2,1,0:T(2,128)(2,1)S(1)}, u32[]{:S(2)}, u32[]{:S(2)}) collective-permute-start(bf16[1,1,512]{2,1,0:T(2,128)(2,1)S(1)} %pad_maximum_fusion.5), channel_id=1, source_target_pairs={{0,4},{4,8},{8,12},{12,0},{1,5},{5,9},{9,13},{13,1},{2,6},{6,10},{... | collective-permute-start | bytes 3080 | tf_op jit(solution)/shard_map/ppermute | solution.py:60
  25.4 7.1 %collective-permute-start.5 = (bf16[1,1,512]{2,1,0:T(2,128)(2,1)S(1)}, bf16[1,1,512]{2,1,0:T(2,128)(2,1)S(1)}, u32[]{:S(2)}, u32[]{:S(2)}) collective-permute-start(bf16[1,1,512]{2,1,0:T(2,128)(2,1)S(1)} %pad_maximum_fusion.5), channel_id=1, source_target_pairs={{0,8},{4,12},{8,0},{12,4},{1,9},{5,13},{9,1},{13,5},{2,10},{6,14},... | collective-permute-start | bytes 3080 | tf_op jit(solution)/shard_map/ppermute | solution.py:60
  29.1 3.6 %collective-permute-start.6 = (bf16[1,1,512]{2,1,0:T(2,128)(2,1)S(1)}, bf16[1,1,512]{2,1,0:T(2,128)(2,1)S(1)}, u32[]{:S(2)}, u32[]{:S(2)}) collective-permute-start(bf16[1,1,512]{2,1,0:T(2,128)(2,1)S(1)} %pad_maximum_fusion.5), channel_id=1, source_target_pairs={{0,12},{4,0},{8,4},{12,8},{1,13},{5,1},{9,5},{13,9},{2,14},{6,2},{... | collective-permute-start | bytes 3080 | tf_op jit(solution)/shard_map/ppermute | solution.py:60
  31.0 57.2 %collective-permute-start.16 = (bf16[256,1024]{1,0:T(8,128)(2,1)}, bf16[256,1024]{1,0:T(8,128)(2,1)}, u32[]{:S(2)}, u32[]{:S(2)}) collective-permute-start(bf16[256,1024]{1,0:T(8,128)(2,1)} %bitcast), channel_id=1, source_target_pairs={{0,2},{2,0},{1,3},{3,1},{4,6},{6,4},{5,7},{7,5},{8,10},{10,8},{9,1... | collective-permute-start | bytes 1572872 | tf_op jit(solution)/shard_map/ppermute | solution.py:149
  36.5 4.1 %copy-start.12 = (f32[1024]{0:T(1024)S(1)}, f32[1024]{0:T(1024)}, u32[]{:S(2)}) copy-start(f32[1024]{0:T(1024)} %param.18) | copy-start | bytes 12292
  36.5 4.1 %copy-start.13 = (f32[1024]{0:T(1024)S(1)}, f32[1024]{0:T(1024)}, u32[]{:S(2)}) copy-start(f32[1024]{0:T(1024)} %param.19) | copy-start | bytes 12292
  41.8 7.8 %collective-permute-start.8 = (f32[1]{0:T(128)}, f32[1]{0:T(128)}, u32[]{:S(2)}, u32[]{:S(2)}) collective-permute-start(f32[1]{0:T(128)} %bitcast.72), channel_id=1, source_target_pairs={{0,4},{4,8},{8,12},{12,0},{1,5},{5,9},{9,13},{13,1},{2,6},{6,10},{... | collective-permute-start | bytes 20 | tf_op jit(solution)/shard_map/ppermute | solution.py:75
  45.1 5.1 %collective-permute-start.9 = (f32[1]{0:T(128)}, f32[1]{0:T(128)}, u32[]{:S(2)}, u32[]{:S(2)}) collective-permute-start(f32[1]{0:T(128)} %bitcast.72), channel_id=1, source_target_pairs={{0,8},{4,12},{8,0},{12,4},{1,9},{5,13},{9,1},{13,5},{2,10},{6,14},... | collective-permute-start | bytes 20 | tf_op jit(solution)/shard_map/ppermute | solution.py:75
  48.2 3.6 %collective-permute-start.10 = (f32[1]{0:T(128)}, f32[1]{0:T(128)}, u32[]{:S(2)}, u32[]{:S(2)}) collective-permute-start(f32[1]{0:T(128)} %bitcast.72), channel_id=1, source_target_pairs={{0,12},{4,0},{8,4},{12,8},{1,13},{5,1},{9,5},{13,9},{2,14},{6,2},{... | collective-permute-start | bytes 20 | tf_op jit(solution)/shard_map/ppermute | solution.py:75
  55.7 7.2 %collective-permute-start.11 = (f32[1,1,512]{2,1,0:T(1,128)S(1)}, f32[1,1,512]{2,1,0:T(1,128)S(1)}, u32[]{:S(2)}, u32[]{:S(2)}) collective-permute-start(f32[1,1,512]{2,1,0:T(1,128)S(1)} %get-tuple-element.34), channel_id=1, source_target_pairs={{0,4},{4,8},{8,12},{12,0},{1,5},{5,9},{9,13},{13,1},{2,6},{6,10},{... | collective-permute-start | bytes 6152 | tf_op jit(solution)/shard_map/ppermute | solution.py:89
  56.7 6.2 %collective-permute-start.12 = (f32[1,1,512]{2,1,0:T(1,128)S(1)}, f32[1,1,512]{2,1,0:T(1,128)S(1)}, u32[]{:S(2)}, u32[]{:S(2)}) collective-permute-start(f32[1,1,512]{2,1,0:T(1,128)S(1)} %get-tuple-element.36), channel_id=1, source_target_pairs={{0,8},{4,12},{8,0},{12,4},{1,9},{5,13},{9,1},{13,5},{2,10},{6,14},... | collective-permute-start | bytes 6152 | tf_op jit(solution)/shard_map/ppermute | solution.py:89
  59.6 3.6 %collective-permute-start.13 = (f32[1,1,512]{2,1,0:T(1,128)S(1)}, f32[1,1,512]{2,1,0:T(1,128)S(1)}, u32[]{:S(2)}, u32[]{:S(2)}) collective-permute-start(f32[1,1,512]{2,1,0:T(1,128)S(1)} %get-tuple-element.35), channel_id=1, source_target_pairs={{0,12},{4,0},{8,4},{12,8},{1,13},{5,1},{9,5},{13,9},{2,14},{6,2},{... | collective-permute-start | bytes 6152 | tf_op jit(solution)/shard_map/ppermute | solution.py:89
  80.7 7.3 %collective-permute-start.15 = (bf16[103936]{0:T(1024)(128)(2,1)S(1)}, bf16[103936]{0:T(1024)(128)(2,1)S(1)}, u32[]{:S(2)}, u32[]{:S(2)}) collective-permute-start(bf16[103936]{0:T(1024)(128)(2,1)S(1)} %pad_maximum_fusion.2), channel_id=1, source_target_pairs={{0,2},{2,0},{1,3},{3,1},{4,6},{6,4},{5,7},{7,5},{8,10},{10,8},{9,1... | collective-permute-start | bytes 623624 | tf_op jit(solution)/shard_map/ppermute | solution.py:344
  90.1 14.3 %collective-permute-start.17 = (bf16[256,384]{0,1:T(8,128)(2,1)S(1)}, bf16[256,384]{0,1:T(8,128)(2,1)S(1)}, u32[]{:S(2)}, u32[]{:S(2)}) collective-permute-start(bf16[256,384]{0,1:T(8,128)(2,1)S(1)} %get-tuple-element.22), channel_id=1, source_target_pairs={{0,4},{4,8},{8,12},{12,0},{1,5},{5,9},{9,13},{13,1},{2,6},{6,10},{... | collective-permute-start | bytes 589832 | tf_op jit(solution)/shard_map/ppermute | solution.py:89
  90.8 16.3 %collective-permute-start.18 = (bf16[256,384]{0,1:T(8,128)(2,1)S(1)}, bf16[256,384]{0,1:T(8,128)(2,1)S(1)}, u32[]{:S(2)}, u32[]{:S(2)}) collective-permute-start(bf16[256,384]{0,1:T(8,128)(2,1)S(1)} %get-tuple-element.24), channel_id=1, source_target_pairs={{0,8},{4,12},{8,0},{12,4},{1,9},{5,13},{9,1},{13,5},{2,10},{6,14},... | collective-permute-start | bytes 589832 | tf_op jit(solution)/shard_map/ppermute | solution.py:89
  93.6 16.5 %collective-permute-start.19 = (bf16[256,384]{0,1:T(8,128)(2,1)S(1)}, bf16[256,384]{0,1:T(8,128)(2,1)S(1)}, u32[]{:S(2)}, u32[]{:S(2)}) collective-permute-start(bf16[256,384]{0,1:T(8,128)(2,1)S(1)} %get-tuple-element.23), channel_id=1, source_target_pairs={{0,12},{4,0},{8,4},{12,8},{1,13},{5,1},{9,5},{13,9},{2,14},{6,2},{... | collective-permute-start | bytes 589832 | tf_op jit(solution)/shard_map/ppermute | solution.py:89
  110.3 6.6 %collective-permute-start.20 = (bf16[256,384]{0,1:T(8,128)(2,1)S(1)}, bf16[256,384]{0,1:T(8,128)(2,1)S(1)}, u32[]{:S(2)}, u32[]{:S(2)}) collective-permute-start(bf16[256,384]{0,1:T(8,128)(2,1)S(1)} %add_convert_fusion), channel_id=1, source_target_pairs={{0,2},{2,0},{1,3},{3,1},{4,6},{6,4},{5,7},{7,5},{8,10},{10,8},{9,1... | collective-permute-start | bytes 589832 | tf_op jit(solution)/shard_map/ppermute | solution.py:355
  (9 other events, 12.2 us)

commit v20 on v8

--- a/solution.py
+++ b/solution.py
@@ -134,9 +134,11 @@
     cross_valid = local_ids[:, None] != jnp.arange(cand_count)[None, :]
     head_shape = (lists, local_cands, seq_len, local_heads, HEAD_DIM)
     cls_shape = (lists, cand_count, local_heads, HEAD_DIM)
-    out_first_full = gather_mp(w_out_first, 0)
+    swap = [(0, 1), (1, 0)]
+    other_out_first = lax.ppermute(w_out_first, "mp", swap)
     last_full = gather_mp(w_last, 2)
-    out_last_full = gather_mp(w_out_last, 0)
+    other_out_last = lax.ppermute(w_out_last, "mp", swap)
+    partner_at = (1 - lax.axis_index("mp")) * local_width
     cls_and_teacher = gather_cand(
         jnp.concatenate([tokens[:, :, 0].astype(jnp.float32), teacher[..., None]], -1), 1
     )
@@ -170,8 +172,14 @@
     )
     first_mixed = attended.reshape(lists, local_cands, seq_len, local_width).astype(jnp.bfloat16)
     first_joined = lax.all_gather(first_mixed, "mp", axis=3, tiled=True)
-    residual_first = tokens.astype(jnp.float32) + mixed(
-        "qcsf,fd->qcsd", first_joined, out_first_full
+    residual_first = (
+        tokens.astype(jnp.float32)
+        + mixed("qcsf,fd->qcsd", first_mixed, w_out_first)
+        + mixed(
+            "qcsf,fd->qcsd",
+            lax.dynamic_slice_in_dim(first_joined, partner_at, local_width, 3),
+            other_out_first,
+        )
     )
     normed_first, unit_first, inverse_first = norm_forward(residual_first, gain_first)
     hidden = normed_first.astype(jnp.bfloat16)
@@ -199,8 +207,14 @@
     )
     last_mixed = attended_last.reshape(lists, local_cands, local_width).astype(jnp.bfloat16)
     last_joined = lax.all_gather(last_mixed, "mp", axis=2, tiled=True)
-    residual_last = hidden[:, :, 0].astype(jnp.float32) + mixed(
-        "qcf,fd->qcd", last_joined, out_last_full
+    residual_last = (
+        hidden[:, :, 0].astype(jnp.float32)
+        + mixed("qcf,fd->qcd", last_mixed, w_out_last)
+        + mixed(
+            "qcf,fd->qcd",
+            lax.dynamic_slice_in_dim(last_joined, partner_at, local_width, 2),
+            other_out_last,
+        )
     )
     normed_last, unit_last, inverse_last = norm_forward(residual_last, gain_last)
     scores = jnp.einsum("qcd,d->qc", normed_last, w_score, precision=lax.Precision.HIGHEST)

time: 116 us -> 118 us (1.017)
    dot_general x32 -> x34, matrix products: 20.8 us -> 21.3 us  [mixed(): jnp.einsum(pattern, former, latter, preferred_element_type=jnp.float32)]
  transfers between devices with their start and end apart: 21 -> 21, of which waited for: 8 -> 8; matrix products, arithmetic and copies ran while one was open for 33% -> 34% of each run, Pallas kernels for 0% -> 0%
where the time goes in v20:
time: 118 us; the launch traced here: 117 us
  waiting for transfers between devices  30 us (25%)
  starting transfers between devices  28.4 us (24%)
  matrix products  21.3 us (18%)
  other arithmetic  13.9 us (12%)
  between operations  8.5 us (7%)
  local copies, waits for them, and re-layouts  8.44 us (7%)
  blocking collectives  6.37 us (5%)
    dot_general x34, matrix products, mixed(): jnp.einsum(pattern, former, latter, preferred_element_type=jnp.float32)  21.3 us
    ppermute x6, waiting for transfers between devices, scatter_cand(): lax.ppermute(piece, 'cand', [(j, (j + k) % count) for j in range(count)])  17.9 us
    ppermute x6, starting transfers between devices, scatter_cand(): lax.ppermute(piece, 'cand', [(j, (j + k) % count) for j in range(count)])  8.88 us
    ppermute x6, starting transfers between devices, gather_cand(): lax.ppermute(block, 'cand', [(j, (j + k) % count) for j in range(count)])  8.45 us
    ppermute x3, starting transfers between devices, sum_cand(): lax.ppermute(block, 'cand', [(j, (j + k) % count) for j in range(count)])  7.77 us
    ppermute x1, waiting for transfers between devices, local(): partner = lax.ppermute(reduced, 'query', swap)  5.94 us
    ppermute x1, waiting for transfers between devices, local(): lax.ppermute(jnp.concatenate([given_half.reshape(-1), cls_flat.reshape(-1...  5.04 us
    select_n x1, other arithmetic, gather_mp(): jnp.where(lax.axis_index('mp') == 0, jnp.concatenate([block, other], axis...  3.41 us
  transfers between devices with their start and end apart: 21, of which 8 were waited for; matrix products, arithmetic and copies ran while one was open for 34% of the time, Pallas kernels for 0%

profile of v20, /device:TPU:8, one launch (start us, length us, event | category | flops | bytes accessed | tf_op | source)
XLA Modules:
  0.0 117.0 jit_solution(7122660813030779007)
XLA Ops:
  1.4 1.6 %collective-permute-start = (f32[1,1,1025]{2,1,0:T(1,128)S(1)}, f32[1,1,1025]{2,1,0:T(1,128)S(1)}, u32[]{:S(2)}, u32[]{:S(2)}) collective-permute-start(f32[1,1,1025]{2,1,0:T(1,128)S(1)} %pad_maximum_fusion.4), channel_id=1, source_target_pairs={{0,4},{4,8},{8,12},{12,0},{1,5},{5,9},{9,13},{13,1},{2,6},{6,10},{... | collective-permute-start | bytes 12308 | tf_op jit(solution)/shard_map/ppermute | solution.py:60
  3.0 1.1 collective-permute-start.1
  4.1 1.9 %collective-permute-start.2 = (f32[1,1,1025]{2,1,0:T(1,128)S(1)}, f32[1,1,1025]{2,1,0:T(1,128)S(1)}, u32[]{:S(2)}, u32[]{:S(2)}) collective-permute-start(f32[1,1,1025]{2,1,0:T(1,128)S(1)} %pad_maximum_fusion.4), channel_id=1, source_target_pairs={{0,12},{4,0},{8,4},{12,8},{1,13},{5,1},{9,5},{13,9},{2,14},{6,2},{... | collective-permute-start | bytes 12308 | tf_op jit(solution)/shard_map/ppermute | solution.py:60
  6.6 2.1 %fusion.6 = bf16[3,1,1,256,256]{3,4,0,2,1:T(8,128)(2,1)S(1)} fusion(bf16[3,1024,256]{2,1,0:T(8,128)(2,1)} %param.13, bf16[1,1,256,1024]{3,2,1,0:T(8,128)(2,1)} %param.10), kind=kOutput, calls=%fused_computation.17 | convolution fusion | flops 402849792 | bytes 2490368 | tf_op jit(solution)/shard_map/qcsd,kdf->kqcsf/dot_general | solution.py:15
  15.6 1.3 %exponential_reduce_fusion = f32[]{:T(128)} fusion(f32[1,4,1025]{2,1,0:T(4,128)S(1)} %bitcast_select_fusion, f32[]{:T(128)} %slice_reduce_fusion.2), kind=kLoop, calls=%fused_computation.192 | loop fusion | flops 7 | bytes 24 | tf_op jit(solution)/shard_map/reduce_sum | solution.py:224
  19.1 1.3 %fusion.36 = bf16[1,1,256,4,64]{2,4,3,1,0:T(8,128)(2,1)S(1)} fusion(bf16[256,4,64]{0,2,1:T(8,128)(2,1)} %bitcast.378, f32[4,64]{1,0:T(4,128)S(1)} %bitcast.412, pred[256]{0:T(512)(128)(4,1)S(1)} %iota_compare_fusion.1, f32[4,256,256]{1,2,0:T(8,128)S(1)} %get-tuple-element.48, f32[4,256]{1,0:T(4,128)S(1)} %broadcast_select_fusion.1, ...), kind=kOutput, calls=%fused_computation.75 | convolution fusion | flops 34537472 | bytes 1320192 | tf_op jit(solution)/shard_map/qchst,qcthe->qcshe/dot_general | solution.py:15
  20.4 2.1 %all_gather.9 = bf16[1,1,256,512]{2,3,1,0:T(8,128)(2,1)S(1)} all-gather(bf16[1,1,256,256]{2,3,1,0:T(8,128)(2,1)S(1)} %bitcast.367), channel_id=1, replica_groups=mesh['groups'=2,'cand'=4,'query'=2,'mp'=2] {'mp'}, dimensions={3}, use_global_device_ids=true | all-gather | bytes 393216 | tf_op jit(solution)/shard_map/all_gather | solution.py:174
  22.5 1.4 %fusion.4 = f32[1,1,256,1024]{3,2,1,0:T(8,128)S(1)} fusion(bf16[256,256]{0,1:T(8,128)(2,1)S(1)} %bitcast.368, bf16[256,1024]{1,0:T(8,128)(2,1)S(1)} %copy-done.1, bf16[1,1,256,1024]{3,2,1,0:T(8,128)(2,1)} %param.10), kind=kOutput, calls=%fused_computation.14 | convolution fusion | flops 134742016 | bytes 2228224 | tf_op jit(solution)/shard_map/qcsf,fd->qcsd/dot_general | solution.py:15
  24.8 1.7 %fusion.7 = bf16[2,1,1,256,256]{4,3,0,2,1:T(8,128)(2,1)S(1)} fusion(bf16[3,1024,256]{2,1,0:T(8,128)(2,1)} %param.16, bf16[1,1,256,1024]{3,2,1,0:T(8,128)(2,1)S(1)} %multiply_convert_fusion.1), kind=kOutput, calls=%fused_computation.22 | convolution fusion | flops 268566528 | bytes 1835008 | tf_op jit(solution)/shard_map/qcsd,kdf->kqcsf/dot_general | solution.py:15
  26.8 3.6 %collective-permute-start.5 = (bf16[1,1,512]{2,1,0:T(2,128)(2,1)S(1)}, bf16[1,1,512]{2,1,0:T(2,128)(2,1)S(1)}, u32[]{:S(2)}, u32[]{:S(2)}) collective-permute-start(bf16[1,1,512]{2,1,0:T(2,128)(2,1)S(1)} %pad_maximum_fusion.5), channel_id=1, source_target_pairs={{0,8},{4,12},{8,0},{12,4},{1,9},{5,13},{9,1},{13,5},{2,10},{6,14},... | collective-permute-start | bytes 3080 | tf_op jit(solution)/shard_map/ppermute | solution.py:60
  30.4 1.2 %fusion.27 = f32[1,256]{1,0:T(1,128)S(1)} fusion(bf16[3,1024,256]{2,1,0:T(8,128)(2,1)} %param.16, bf16[1,1,256,1024]{3,2,1,0:T(8,128)(2,1)S(1)} %multiply_convert_fusion.1), kind=kOutput, calls=%fused_computation.59 | convolution fusion | flops 524288 | bytes 529408 | tf_op jit(solution)/shard_map/qcd,df->qcf/dot_general | solution.py:15
  32.3 1.6 %collective-permute-start.16 = (bf16[256,1024]{1,0:T(8,128)(2,1)}, bf16[256,1024]{1,0:T(8,128)(2,1)}, u32[]{:S(2)}, u32[]{:S(2)}) collective-permute-start(bf16[256,1024]{1,0:T(8,128)(2,1)} %bitcast), channel_id=1, source_target_pairs={{0,2},{2,0},{1,3},{3,1},{4,6},{6,4},{5,7},{7,5},{8,10},{10,8},{9,1... | collective-permute-start | bytes 1572872 | tf_op jit(solution)/shard_map/ppermute | solution.py:151
  36.2 1.8 %all_gather.10 = bf16[1,1,512]{2,1,0:T(2,128)(2,1)S(1)} all-gather(bf16[1,1,256]{2,1,0:T(2,128)(2,1)S(1)} %convert_element_type.274), channel_id=1, replica_groups=mesh['groups'=2,'cand'=4,'query'=2,'mp'=2] {'mp'}, dimensions={2}, use_global_device_ids=true | all-gather | bytes 1536 | tf_op jit(solution)/shard_map/all_gather | solution.py:209
  38.1 1.2 %fusion.102 = f32[1,1024]{1,0:T(1,128)S(1)} fusion(bf16[256,1024]{1,0:T(8,128)(2,1)} %collective-permute-done.7, bf16[1,1,512]{2,1,0:T(2,128)(2,1)S(1)} %all_gather.10, s32[]{:T(128)S(6)} %select_n.233), kind=kOutput, calls=%fused_computation.211 | convolution fusion | flops 524288 | bytes 529412 | tf_op jit(solution)/shard_map/qcf,fd->qcd/dot_general | solution.py:15
  43.1 3.3 %collective-permute-start.8 = (f32[1]{0:T(128)}, f32[1]{0:T(128)}, u32[]{:S(2)}, u32[]{:S(2)}) collective-permute-start(f32[1]{0:T(128)} %bitcast.75), channel_id=1, source_target_pairs={{0,4},{4,8},{8,12},{12,0},{1,5},{5,9},{9,13},{13,1},{2,6},{6,10},{... | collective-permute-start | bytes 20 | tf_op jit(solution)/shard_map/ppermute | solution.py:75
  46.3 3.1 %collective-permute-start.9 = (f32[1]{0:T(128)}, f32[1]{0:T(128)}, u32[]{:S(2)}, u32[]{:S(2)}) collective-permute-start(f32[1]{0:T(128)} %bitcast.75), channel_id=1, source_target_pairs={{0,8},{4,12},{8,0},{12,4},{1,9},{5,13},{9,1},{13,5},{2,10},{6,14},... | collective-permute-start | bytes 20 | tf_op jit(solution)/shard_map/ppermute | solution.py:75
  49.4 1.4 %collective-permute-start.10 = (f32[1]{0:T(128)}, f32[1]{0:T(128)}, u32[]{:S(2)}, u32[]{:S(2)}) collective-permute-start(f32[1]{0:T(128)} %bitcast.75), channel_id=1, source_target_pairs={{0,12},{4,0},{8,4},{12,8},{1,13},{5,1},{9,5},{13,9},{2,14},{6,2},{... | collective-permute-start | bytes 20 | tf_op jit(solution)/shard_map/ppermute | solution.py:75
  58.1 2.9 %collective-permute-start.12 = (f32[1,1,512]{2,1,0:T(1,128)S(1)}, f32[1,1,512]{2,1,0:T(1,128)S(1)}, u32[]{:S(2)}, u32[]{:S(2)}) collective-permute-start(f32[1,1,512]{2,1,0:T(1,128)S(1)} %get-tuple-element.38), channel_id=1, source_target_pairs={{0,8},{4,12},{8,0},{12,4},{1,9},{5,13},{9,1},{13,5},{2,10},{6,14},... | collective-permute-start | bytes 6152 | tf_op jit(solution)/shard_map/ppermute | solution.py:89
  61.0 1.1 collective-permute-start.13
  62.8 1.8 %collective-permute-done.13 = f32[1,1,512]{2,1,0:T(1,128)S(1)} collective-permute-done((f32[1,1,512]{2,1,0:T(1,128)S(1)}, f32[1,1,512]{2,1,0:T(1,128)S(1)}, u32[]{:S(2)}, u32[]{:S(2)}) %collective-permute-start.13) | collective-permute-done | bytes 2080 | tf_op jit(solution)/shard_map/ppermute | solution.py:89
  64.8 2.5 %all_gather.11 = bf16[1,1,513,512]{2,3,1,0:T(8,128)(2,1)S(1)} all-gather(bf16[1,1,513,256]{2,3,1,0:T(8,128)(2,1)S(1)} %pad_maximum_fusion.1), channel_id=1, replica_groups=mesh['groups'=2,'cand'=4,'query'=2,'mp'=2] {'mp'}, dimensions={3}, use_global_device_ids=true | all-gather | bytes 787968 | tf_op jit(solution)/shard_map/all_gather | solution.py:276
  67.4 3.4 %maximum_select_fusion = bf16[3,1024,512]{2,1,0:T(8,128)(2,1)S(1)} fusion(bf16[3,1024,256]{2,1,0:T(8,128)(2,1)} %collective-permute-done.14, bf16[3,1024,256]{2,1,0:T(8,128)(2,1)} %param.16, pred[]{:T(512)S(6)} %eq.49), kind=kLoop, calls=%fused_computation.2 | loop fusion | flops 14155776 | bytes 6291457 | tf_op jit(solution)/shard_map/jit(_where)/select_n | solution.py:98
  72.7 1.6 %convolution_convert_fusion.3 = bf16[256,256]{0,1:T(8,128)(2,1)S(1)} fusion(bf16[256,1024]{1,0:T(8,128)(2,1)} %param.14, f32[1,1,256,1024]{3,2,1,0:T(8,128)S(1)} %get-tuple-element.50, f32[256,1024]{1,0:T(8,128)S(1)} %get-tuple-element.52, f32[256]{0:T(256)S(1)} %broadcast_multiply_fusion.1, f32[256]{0:T(256)S(1)} %broadcast_multiply_fusion.2, ...), kind=kOutput, calls=%fused_computation.25 | convolution fusion | flops 136118272 | bytes 2756608 | tf_op jit(solution)/shard_map/qcsd,fd->qcsf/dot_general | solution.py:15
  75.4 1.3 %multiply_reduce_fusion = (f32[4,256]{1,0:T(4,128)S(1)}, f32[4,256,256]{1,2,0:T(8,128)S(1)}) fusion(f32[4,256]{1,0:T(4,128)} %copy-done.4, f32[4,256,256]{1,2,0:T(8,128)S(1)} %get-tuple-element.48, f32[4,256]{1,0:T(4,128)S(1)} %broadcast_select_fusion.2, bf16[256,4,64]{0,2,1:T(8,128)(2,1)S(1)} %bitcast.376, bf16[256,4,64]{0,2,1:T(8,128)(2,1)} %bitcast.379), kind=kOutput, calls=%fused_computation.39 | convolution fusion | flops 34601984 | bytes 2371584 | tf_op jit(solution)/shard_map/qcshe,qcthe->qchst/dot_general | solution.py:15
  80.3 1.6 %fusion.19 = f32[1024,384]{0,1:T(8,128)S(1)} fusion(bf16[4,1024]{1,0:T(4,128)(2,1)S(1)} %get-tuple-element.35, bf16[256,1024]{1,0:T(8,128)(2,1)} %bitcast, s32[]{:T(128)S(6)} %select_n.252, bf16[256,768]{0,1:T(8,128)(2,1)S(1)} %bitcast.358, bf16[4,768]{0,1:T(8,128)(2,1)S(1)} %copy.82), kind=kOutput, calls=%fused_computation.52 | convolution fusion | flops 205936640 | bytes 2504708 | tf_op jit(solution)/shard_map/rd,rf->df/dot_general | solution.py:15
  81.9 5.0 %collective-permute-done.15 = bf16[103936]{0:T(1024)(128)(2,1)S(1)} collective-permute-done((bf16[103936]{0:T(1024)(128)(2,1)S(1)}, bf16[103936]{0:T(1024)(128)(2,1)S(1)}, u32[]{:S(2)}, u32[]{:S(2)}) %collective-permute-start.15) | collective-permute-done | bytes 207904 | tf_op jit(solution)/shard_map/ppermute | solution.py:353
  87.2 1.4 %fusion.136 = f32[384,1024]{1,0:T(8,128)S(1)} fusion(bf16[256,384]{1,0:T(8,128)(2,1)S(1)} %slice.153, bf16[256,1024]{1,0:T(8,128)(2,1)} %collective-permute-done.16), kind=kOutput, calls=%fused_computation.255 | convolution fusion | flops 201326592 | bytes 2293760 | tf_op jit(solution)/shard_map/rd,rf->df/dot_general | solution.py:15
  89.7 2.9 %collective-permute-start.18 = (bf16[256,384]{0,1:T(8,128)(2,1)S(1)}, bf16[256,384]{0,1:T(8,128)(2,1)S(1)}, u32[]{:S(2)}, u32[]{:S(2)}) collective-permute-start(bf16[256,384]{0,1:T(8,128)(2,1)S(1)} %get-tuple-element.26), channel_id=1, source_target_pairs={{0,8},{4,12},{8,0},{12,4},{1,9},{5,13},{9,1},{13,5},{2,10},{6,14},... | collective-permute-start | bytes 589832 | tf_op jit(solution)/shard_map/ppermute | solution.py:89
  93.0 10.2 %collective-permute-done.17 = bf16[256,384]{0,1:T(8,128)(2,1)S(1)} collective-permute-done((bf16[256,384]{0,1:T(8,128)(2,1)S(1)}, bf16[256,384]{0,1:T(8,128)(2,1)S(1)}, u32[]{:S(2)}, u32[]{:S(2)}) %collective-permute-start.17) | collective-permute-done | bytes 196640 | tf_op jit(solution)/shard_map/ppermute | solution.py:89
  103.2 2.8 %collective-permute-done.18 = bf16[256,384]{0,1:T(8,128)(2,1)S(1)} collective-permute-done((bf16[256,384]{0,1:T(8,128)(2,1)S(1)}, bf16[256,384]{0,1:T(8,128)(2,1)S(1)}, u32[]{:S(2)}, u32[]{:S(2)}) %collective-permute-start.18) | collective-permute-done | bytes 196640 | tf_op jit(solution)/shard_map/ppermute | solution.py:89
  106.0 3.1 %collective-permute-done.19 = bf16[256,384]{0,1:T(8,128)(2,1)S(1)} collective-permute-done((bf16[256,384]{0,1:T(8,128)(2,1)S(1)}, bf16[256,384]{0,1:T(8,128)(2,1)S(1)}, u32[]{:S(2)}, u32[]{:S(2)}) %collective-permute-start.19) | collective-permute-done | bytes 196640 | tf_op jit(solution)/shard_map/ppermute | solution.py:89
  109.9 5.9 %collective-permute-done.20 = bf16[256,384]{0,1:T(8,128)(2,1)S(1)} collective-permute-done((bf16[256,384]{0,1:T(8,128)(2,1)S(1)}, bf16[256,384]{0,1:T(8,128)(2,1)S(1)}, u32[]{:S(2)}, u32[]{:S(2)}) %collective-permute-start.20) | collective-permute-done | bytes 196640 | tf_op jit(solution)/shard_map/ppermute | solution.py:364
  (228 shorter events, 29.2 us)
Async XLA Ops:
  1.4 10.5 %collective-permute-start = (f32[1,1,1025]{2,1,0:T(1,128)S(1)}, f32[1,1,1025]{2,1,0:T(1,128)S(1)}, u32[]{:S(2)}, u32[]{:S(2)}) collective-permute-start(f32[1,1,1025]{2,1,0:T(1,128)S(1)} %pad_maximum_fusion.4), channel_id=1, source_target_pairs={{0,4},{4,8},{8,12},{12,0},{1,5},{5,9},{9,13},{13,1},{2,6},{6,10},{... | collective-permute-start | bytes 12308 | tf_op jit(solution)/shard_map/ppermute | solution.py:60
  3.0 8.9 %collective-permute-start.1 = (f32[1,1,1025]{2,1,0:T(1,128)S(1)}, f32[1,1,1025]{2,1,0:T(1,128)S(1)}, u32[]{:S(2)}, u32[]{:S(2)}) collective-permute-start(f32[1,1,1025]{2,1,0:T(1,128)S(1)} %pad_maximum_fusion.4), channel_id=1, source_target_pairs={{0,8},{4,12},{8,0},{12,4},{1,9},{5,13},{9,1},{13,5},{2,10},{6,14},... | collective-permute-start | bytes 12308 | tf_op jit(solution)/shard_map/ppermute | solution.py:60
  4.1 7.8 %collective-permute-start.2 = (f32[1,1,1025]{2,1,0:T(1,128)S(1)}, f32[1,1,1025]{2,1,0:T(1,128)S(1)}, u32[]{:S(2)}, u32[]{:S(2)}) collective-permute-start(f32[1,1,1025]{2,1,0:T(1,128)S(1)} %pad_maximum_fusion.4), channel_id=1, source_target_pairs={{0,12},{4,0},{8,4},{12,8},{1,13},{5,1},{9,5},{13,9},{2,14},{6,2},{... | collective-permute-start | bytes 12308 | tf_op jit(solution)/shard_map/ppermute | solution.py:60
  6.1 17.8 %collective-permute-start.3 = (bf16[256,1024]{1,0:T(8,128)(2,1)}, bf16[256,1024]{1,0:T(8,128)(2,1)S(1)}, u32[]{:S(2)}, u32[]{:S(2)}) collective-permute-start(bf16[256,1024]{1,0:T(8,128)(2,1)} %param.14), channel_id=1, source_target_pairs={{0,1},{1,0},{2,3},{3,2},{4,5},{5,4},{6,7},{7,6},{8,9},{9,8},{10,11... | collective-permute-start | bytes 1572872 | tf_op jit(solution)/shard_map/ppermute | solution.py:138
  6.1 32.1 %collective-permute-start.7 = (bf16[256,1024]{1,0:T(8,128)(2,1)}, bf16[256,1024]{1,0:T(8,128)(2,1)}, u32[]{:S(2)}, u32[]{:S(2)}) collective-permute-start(bf16[256,1024]{1,0:T(8,128)(2,1)} %param.17), channel_id=1, source_target_pairs={{0,1},{1,0},{2,3},{3,2},{4,5},{5,4},{6,7},{7,6},{8,9},{9,8},{10,11... | collective-permute-start | bytes 1572872 | tf_op jit(solution)/shard_map/ppermute | solution.py:140
  8.8 3.8 %copy-start.2 = (bf16[3,1024,256]{2,1,0:T(8,128)(2,1)S(1)}, bf16[3,1024,256]{2,1,0:T(8,128)(2,1)}, u32[]{:S(2)}) copy-start(bf16[3,1024,256]{2,1,0:T(8,128)(2,1)} %param.13) | copy-start | bytes 4718596
  11.2 60.4 %copy-start.9 = (pred[256]{0:T(512)(128)(4,1)}, pred[256]{0:T(512)(128)(4,1)S(1)}, u32[]{:S(2)}) copy-start(pred[256]{0:T(512)(128)(4,1)S(1)} %iota_compare_fusion.1) | copy-start | bytes 772
  11.9 55.5 %collective-permute-start.14 = (bf16[3,1024,256]{2,1,0:T(8,128)(2,1)}, bf16[3,1024,256]{2,1,0:T(8,128)(2,1)}, u32[]{:S(2)}, u32[]{:S(2)}) collective-permute-start(bf16[3,1024,256]{2,1,0:T(8,128)(2,1)} %param.16), channel_id=1, source_target_pairs={{0,1},{1,0},{2,3},{3,2},{4,5},{5,4},{6,7},{7,6},{8,9},{9,8},{10,11... | collective-permute-start | bytes 4718600 | tf_op jit(solution)/shard_map/ppermute | solution.py:97
  12.9 7.4 %copy-start.15 = (bf16[4,4,64]{2,1,0:T(4,128)(2,1)}, bf16[4,4,64]{2,1,0:T(4,128)(2,1)S(1)}, u32[]{:S(2)}) copy-start(bf16[4,4,64]{2,1,0:T(4,128)(2,1)S(1)} %reshape.1076) | copy-start | bytes 6148
  14.7 5.6 %copy-start.4 = (f32[4,256]{1,0:T(4,128)}, f32[4,256]{1,0:T(4,128)S(1)}, u32[]{:S(2)}) copy-start(f32[4,256]{1,0:T(4,128)S(1)} %broadcast_select_fusion.1) | copy-start | bytes 12292
  15.6 4.8 %copy-start.17 = (bf16[4,4,64]{2,1,0:T(4,128)(2,1)}, bf16[4,4,64]{2,1,0:T(4,128)(2,1)S(1)}, u32[]{:S(2)}) copy-start(bf16[4,4,64]{2,1,0:T(4,128)(2,1)S(1)} %reshape.1079) | copy-start | bytes 6148
  19.1 3.4 %copy-start.1 = (bf16[256,1024]{1,0:T(8,128)(2,1)S(1)}, bf16[256,1024]{1,0:T(8,128)(2,1)}, u32[]{:S(2)}) copy-start(bf16[256,1024]{1,0:T(8,128)(2,1)} %param.14) | copy-start | bytes 1572868
  24.3 47.3 %copy-start.8 = (f32[256]{0:T(256)}, f32[256]{0:T(256)S(1)}, u32[]{:S(2)}) copy-start(f32[256]{0:T(256)S(1)} %broadcast_multiply_fusion.3) | copy-start | bytes 3076
  24.6 47.1 %copy-start.11 = (f32[256]{0:T(256)}, f32[256]{0:T(256)S(1)}, u32[]{:S(2)}) copy-start(f32[256]{0:T(256)S(1)} %add_rsqrt_fusion) | copy-start | bytes 3076
  26.5 11.5 %copy-start = (bf16[256,1024]{1,0:T(8,128)(2,1)S(1)}, bf16[256,1024]{1,0:T(8,128)(2,1)}, u32[]{:S(2)}) copy-start(bf16[256,1024]{1,0:T(8,128)(2,1)} %param.17) | copy-start | bytes 1572868
  26.5 15.4 %copy-start.6 = (f32[1024]{0:T(1024)S(1)}, f32[1024]{0:T(1024)}, u32[]{:S(2)}) copy-start(f32[1024]{0:T(1024)} %param.18) | copy-start | bytes 12292
  26.5 15.4 %copy-start.7 = (f32[1024]{0:T(1024)S(1)}, f32[1024]{0:T(1024)}, u32[]{:S(2)}) copy-start(f32[1024]{0:T(1024)} %param.19) | copy-start | bytes 12292
  26.6 5.7 %collective-permute-start.4 = (bf16[1,1,512]{2,1,0:T(2,128)(2,1)S(1)}, bf16[1,1,512]{2,1,0:T(2,128)(2,1)S(1)}, u32[]{:S(2)}, u32[]{:S(2)}) collective-permute-start(bf16[1,1,512]{2,1,0:T(2,128)(2,1)S(1)} %pad_maximum_fusion.5), channel_id=1, source_target_pairs={{0,4},{4,8},{8,12},{12,0},{1,5},{5,9},{9,13},{13,1},{2,6},{6,10},{... | collective-permute-start | bytes 3080 | tf_op jit(solution)/shard_map/ppermute | solution.py:60
  26.8 7.1 %collective-permute-start.5 = (bf16[1,1,512]{2,1,0:T(2,128)(2,1)S(1)}, bf16[1,1,512]{2,1,0:T(2,128)(2,1)S(1)}, u32[]{:S(2)}, u32[]{:S(2)}) collective-permute-start(bf16[1,1,512]{2,1,0:T(2,128)(2,1)S(1)} %pad_maximum_fusion.5), channel_id=1, source_target_pairs={{0,8},{4,12},{8,0},{12,4},{1,9},{5,13},{9,1},{13,5},{2,10},{6,14},... | collective-permute-start | bytes 3080 | tf_op jit(solution)/shard_map/ppermute | solution.py:60
  30.4 3.6 %collective-permute-start.6 = (bf16[1,1,512]{2,1,0:T(2,128)(2,1)S(1)}, bf16[1,1,512]{2,1,0:T(2,128)(2,1)S(1)}, u32[]{:S(2)}, u32[]{:S(2)}) collective-permute-start(bf16[1,1,512]{2,1,0:T(2,128)(2,1)S(1)} %pad_maximum_fusion.5), channel_id=1, source_target_pairs={{0,12},{4,0},{8,4},{12,8},{1,13},{5,1},{9,5},{13,9},{2,14},{6,2},{... | collective-permute-start | bytes 3080 | tf_op jit(solution)/shard_map/ppermute | solution.py:60
  32.3 54.8 %collective-permute-start.16 = (bf16[256,1024]{1,0:T(8,128)(2,1)}, bf16[256,1024]{1,0:T(8,128)(2,1)}, u32[]{:S(2)}, u32[]{:S(2)}) collective-permute-start(bf16[256,1024]{1,0:T(8,128)(2,1)} %bitcast), channel_id=1, source_target_pairs={{0,2},{2,0},{1,3},{3,1},{4,6},{6,4},{5,7},{7,5},{8,10},{10,8},{9,1... | collective-permute-start | bytes 1572872 | tf_op jit(solution)/shard_map/ppermute | solution.py:151
  43.1 7.8 %collective-permute-start.8 = (f32[1]{0:T(128)}, f32[1]{0:T(128)}, u32[]{:S(2)}, u32[]{:S(2)}) collective-permute-start(f32[1]{0:T(128)} %bitcast.75), channel_id=1, source_target_pairs={{0,4},{4,8},{8,12},{12,0},{1,5},{5,9},{9,13},{13,1},{2,6},{6,10},{... | collective-permute-start | bytes 20 | tf_op jit(solution)/shard_map/ppermute | solution.py:75
  46.3 5.1 %collective-permute-start.9 = (f32[1]{0:T(128)}, f32[1]{0:T(128)}, u32[]{:S(2)}, u32[]{:S(2)}) collective-permute-start(f32[1]{0:T(128)} %bitcast.75), channel_id=1, source_target_pairs={{0,8},{4,12},{8,0},{12,4},{1,9},{5,13},{9,1},{13,5},{2,10},{6,14},... | collective-permute-start | bytes 20 | tf_op jit(solution)/shard_map/ppermute | solution.py:75
  49.4 3.6 %collective-permute-start.10 = (f32[1]{0:T(128)}, f32[1]{0:T(128)}, u32[]{:S(2)}, u32[]{:S(2)}) collective-permute-start(f32[1]{0:T(128)} %bitcast.75), channel_id=1, source_target_pairs={{0,12},{4,0},{8,4},{12,8},{1,13},{5,1},{9,5},{13,9},{2,14},{6,2},{... | collective-permute-start | bytes 20 | tf_op jit(solution)/shard_map/ppermute | solution.py:75
  57.1 5.7 %collective-permute-start.11 = (f32[1,1,512]{2,1,0:T(1,128)S(1)}, f32[1,1,512]{2,1,0:T(1,128)S(1)}, u32[]{:S(2)}, u32[]{:S(2)}) collective-permute-start(f32[1,1,512]{2,1,0:T(1,128)S(1)} %get-tuple-element.36), channel_id=1, source_target_pairs={{0,4},{4,8},{8,12},{12,0},{1,5},{5,9},{9,13},{13,1},{2,6},{6,10},{... | collective-permute-start | bytes 6152 | tf_op jit(solution)/shard_map/ppermute | solution.py:89
  58.1 4.7 %collective-permute-start.12 = (f32[1,1,512]{2,1,0:T(1,128)S(1)}, f32[1,1,512]{2,1,0:T(1,128)S(1)}, u32[]{:S(2)}, u32[]{:S(2)}) collective-permute-start(f32[1,1,512]{2,1,0:T(1,128)S(1)} %get-tuple-element.38), channel_id=1, source_target_pairs={{0,8},{4,12},{8,0},{12,4},{1,9},{5,13},{9,1},{13,5},{2,10},{6,14},... | collective-permute-start | bytes 6152 | tf_op jit(solution)/shard_map/ppermute | solution.py:89
  61.0 3.6 %collective-permute-start.13 = (f32[1,1,512]{2,1,0:T(1,128)S(1)}, f32[1,1,512]{2,1,0:T(1,128)S(1)}, u32[]{:S(2)}, u32[]{:S(2)}) collective-permute-start(f32[1,1,512]{2,1,0:T(1,128)S(1)} %get-tuple-element.37), channel_id=1, source_target_pairs={{0,12},{4,0},{8,4},{12,8},{1,13},{5,1},{9,5},{13,9},{2,14},{6,2},{... | collective-permute-start | bytes 6152 | tf_op jit(solution)/shard_map/ppermute | solution.py:89
  79.7 7.3 %collective-permute-start.15 = (bf16[103936]{0:T(1024)(128)(2,1)S(1)}, bf16[103936]{0:T(1024)(128)(2,1)S(1)}, u32[]{:S(2)}, u32[]{:S(2)}) collective-permute-start(bf16[103936]{0:T(1024)(128)(2,1)S(1)} %pad_maximum_fusion.2), channel_id=1, source_target_pairs={{0,2},{2,0},{1,3},{3,1},{4,6},{6,4},{5,7},{7,5},{8,10},{10,8},{9,1... | collective-permute-start | bytes 623624 | tf_op jit(solution)/shard_map/ppermute | solution.py:353
  89.1 14.1 %collective-permute-start.17 = (bf16[256,384]{0,1:T(8,128)(2,1)S(1)}, bf16[256,384]{0,1:T(8,128)(2,1)S(1)}, u32[]{:S(2)}, u32[]{:S(2)}) collective-permute-start(bf16[256,384]{0,1:T(8,128)(2,1)S(1)} %get-tuple-element.24), channel_id=1, source_target_pairs={{0,4},{4,8},{8,12},{12,0},{1,5},{5,9},{9,13},{13,1},{2,6},{6,10},{... | collective-permute-start | bytes 589832 | tf_op jit(solution)/shard_map/ppermute | solution.py:89
  89.7 16.3 %collective-permute-start.18 = (bf16[256,384]{0,1:T(8,128)(2,1)S(1)}, bf16[256,384]{0,1:T(8,128)(2,1)S(1)}, u32[]{:S(2)}, u32[]{:S(2)}) collective-permute-start(bf16[256,384]{0,1:T(8,128)(2,1)S(1)} %get-tuple-element.26), channel_id=1, source_target_pairs={{0,8},{4,12},{8,0},{12,4},{1,9},{5,13},{9,1},{13,5},{2,10},{6,14},... | collective-permute-start | bytes 589832 | tf_op jit(solution)/shard_map/ppermute | solution.py:89
  92.6 16.5 %collective-permute-start.19 = (bf16[256,384]{0,1:T(8,128)(2,1)S(1)}, bf16[256,384]{0,1:T(8,128)(2,1)S(1)}, u32[]{:S(2)}, u32[]{:S(2)}) collective-permute-start(bf16[256,384]{0,1:T(8,128)(2,1)S(1)} %get-tuple-element.25), channel_id=1, source_target_pairs={{0,12},{4,0},{8,4},{12,8},{1,13},{5,1},{9,5},{13,9},{2,14},{6,2},{... | collective-permute-start | bytes 589832 | tf_op jit(solution)/shard_map/ppermute | solution.py:89
  109.2 6.6 %collective-permute-start.20 = (bf16[256,384]{0,1:T(8,128)(2,1)S(1)}, bf16[256,384]{0,1:T(8,128)(2,1)S(1)}, u32[]{:S(2)}, u32[]{:S(2)}) collective-permute-start(bf16[256,384]{0,1:T(8,128)(2,1)S(1)} %add_convert_fusion), channel_id=1, source_target_pairs={{0,2},{2,0},{1,3},{3,1},{4,6},{6,4},{5,7},{7,5},{8,10},{10,8},{9,1... | collective-permute-start | bytes 589832 | tf_op jit(solution)/shard_map/ppermute | solution.py:364
  (8 other events, 8.2 us)

commit v21 on v8

--- a/solution.py
+++ b/solution.py
@@ -341,12 +341,44 @@
     )
     other_half = sent[: given_half.size].reshape(given_half.shape)
     other_cls = sent[given_half.size :].reshape(cls_flat.shape)
-    paired = (
-        mixed("rd,rf->df", all_tokens, own_half)
-        + mixed("rd,rf->df", other_tokens, other_half[:row_count])
-        + mixed("rd,rf->df", other_cls, other_half[row_count:])
-    )
-    reduced = scatter_cand(paired.astype(jnp.bfloat16), 0, jnp.float32).astype(jnp.bfloat16)
+    count = lax.axis_size("cand")
+    width = model_width // count
+
+    def block_for(member):
+        start = member * width
+        return (
+            mixed("rd,rf->df", lax.dynamic_slice_in_dim(all_tokens, start, width, 1), own_half)
+            + mixed(
+                "rd,rf->df",
+                lax.dynamic_slice_in_dim(other_tokens, start, width, 1),
+                other_half[:row_count],
+            )
+            + mixed(
+                "rd,rf->df",
+                lax.dynamic_slice_in_dim(other_cls, start, width, 1),
+                other_half[row_count:],
+            )
+        )
+
+    if count > 8:
+        paired = block_for(0) if count == 1 else jnp.concatenate(
+            [block_for(b) for b in range(count)], 0
+        )
+        reduced = scatter_cand(paired.astype(jnp.bfloat16), 0, jnp.float32).astype(jnp.bfloat16)
+    else:
+        me = lax.axis_index("cand")
+        moved = [
+            lax.ppermute(
+                block_for((me + k) % count).astype(jnp.bfloat16),
+                "cand",
+                [(j, (j + k) % count) for j in range(count)],
+            )
+            for k in range(1, count)
+        ]
+        total = block_for(me)
+        for piece in moved:
+            total = total + piece.astype(jnp.float32)
+        reduced = total.astype(jnp.bfloat16)
     partner = lax.ppermute(reduced, "query", swap)
     joined = jnp.where(
         side == 0,

time: 116 us -> 162 us (1.40)
  other arithmetic: 13.9 us -> 37.7 us
  local copies, waits for them, and re-layouts: 7.62 us -> 21.5 us
  matrix products: 20.8 us -> 31.2 us
  waiting for transfers between devices: 30 us -> 26.2 us
    ppermute x6 -> x3, waiting for transfers between devices: 17.9 us -> 0.03 us  [scatter_cand(): lax.ppermute(piece, 'cand', [(j, (j + k) % count) for j in range(count)])]
    ppermute x0 -> x3, waiting for transfers between devices: none -> 13.6 us  [local(): lax.ppermute(block_for((me + k) % count).astype(jnp.bfloat16), 'cand', [(...]
    dot_general x32 -> x41, matrix products: 20.8 us -> 31.2 us  [mixed(): jnp.einsum(pattern, former, latter, preferred_element_type=jnp.float32)]
    another operation x10, other arithmetic: 1.52 us -> 6.57 us
    ppermute x0 -> x3, starting transfers between devices: none -> 3.98 us  [local(): lax.ppermute(block_for((me + k) % count).astype(jnp.bfloat16), 'cand', [(...]
    ppermute x6 -> x3, starting transfers between devices: 8.88 us -> 4.95 us  [scatter_cand(): lax.ppermute(piece, 'cand', [(j, (j + k) % count) for j in range(count)])]
    another operation x9, local copies, waits for them, and re-layouts: 0.69 us -> 4.45 us
    reduce_sum x2, other arithmetic: 0.77 us -> 3.34 us  [norm_backward(): jnp.mean(scaled, -1, keepdims=True)]
  transfers between devices with their start and end apart: 21 -> 21, of which waited for: 8 -> 6; matrix products, arithmetic and copies ran while one was open for 33% -> 53% of each run, Pallas kernels for 0% -> 0%
where the time goes in v21:
time: 162 us; the launch traced here: 160 us
  other arithmetic  37.7 us (23%)
  matrix products  31.2 us (19%)
  starting transfers between devices  28.3 us (17%)
  waiting for transfers between devices  26.2 us (16%)
  local copies, waits for them, and re-layouts  21.5 us (13%)
  between operations  8.76 us (5%)
  blocking collectives  6.57 us (4%)
    dot_general x41, matrix products, mixed(): jnp.einsum(pattern, former, latter, preferred_element_type=jnp.float32)  31.2 us
    ppermute x3, waiting for transfers between devices, local(): lax.ppermute(block_for((me + k) % count).astype(jnp.bfloat16), 'cand', [(...  13.6 us
    ppermute x6, starting transfers between devices, gather_cand(): lax.ppermute(block, 'cand', [(j, (j + k) % count) for j in range(count)])  8.4 us
    ppermute x3, starting transfers between devices, sum_cand(): lax.ppermute(block, 'cand', [(j, (j + k) % count) for j in range(count)])  7.77 us
    another operation x10, other arithmetic  6.57 us
    ppermute x1, waiting for transfers between devices, local(): partner = lax.ppermute(reduced, 'query', swap)  6.28 us
    ppermute x1, waiting for transfers between devices, local(): lax.ppermute(jnp.concatenate([given_half.reshape(-1), cls_flat.reshape(-1...  5.3 us
    ppermute x3, starting transfers between devices, scatter_cand(): lax.ppermute(piece, 'cand', [(j, (j + k) % count) for j in range(count)])  4.95 us
  transfers between devices with their start and end apart: 21, of which 6 were waited for; matrix products, arithmetic and copies ran while one was open for 53% of the time, Pallas kernels for 0%

profile of v21, /device:TPU:8, one launch (start us, length us, event | category | flops | bytes accessed | tf_op | source)
XLA Modules:
  0.0 160.2 jit_solution(3199849357501447565)
XLA Ops:
  1.4 1.6 %collective-permute-start = (f32[1,1,1025]{2,1,0:T(1,128)S(1)}, f32[1,1,1025]{2,1,0:T(1,128)S(1)}, u32[]{:S(2)}, u32[]{:S(2)}) collective-permute-start(f32[1,1,1025]{2,1,0:T(1,128)S(1)} %pad_maximum_fusion.4), channel_id=1, source_target_pairs={{0,4},{4,8},{8,12},{12,0},{1,5},{5,9},{9,13},{13,1},{2,6},{6,10},{... | collective-permute-start | bytes 12308 | tf_op jit(solution)/shard_map/ppermute | solution.py:60
  4.1 1.9 %collective-permute-start.2 = (f32[1,1,1025]{2,1,0:T(1,128)S(1)}, f32[1,1,1025]{2,1,0:T(1,128)S(1)}, u32[]{:S(2)}, u32[]{:S(2)}) collective-permute-start(f32[1,1,1025]{2,1,0:T(1,128)S(1)} %pad_maximum_fusion.4), channel_id=1, source_target_pairs={{0,12},{4,0},{8,4},{12,8},{1,13},{5,1},{9,5},{13,9},{2,14},{6,2},{... | collective-permute-start | bytes 12308 | tf_op jit(solution)/shard_map/ppermute | solution.py:60
  6.7 2.2 %fusion.3 = bf16[3,1,1,256,256]{3,4,0,2,1:T(8,128)(2,1)S(1)} fusion(bf16[3,1024,256]{2,1,0:T(8,128)(2,1)} %param.13, bf16[1,1,256,1024]{3,2,1,0:T(8,128)(2,1)} %param.10), kind=kOutput, calls=%fused_computation.12 | convolution fusion | flops 402849792 | bytes 2490368 | tf_op jit(solution)/shard_map/qcsd,kdf->kqcsf/dot_general | solution.py:15
  18.8 2.1 %all_gather.9 = bf16[1,1,256,512]{2,3,1,0:T(8,128)(2,1)S(1)} all-gather(bf16[1,1,256,256]{2,3,1,0:T(8,128)(2,1)S(1)} %bitcast.369), channel_id=1, replica_groups=mesh['groups'=2,'cand'=4,'query'=2,'mp'=2] {'mp'}, dimensions={3}, use_global_device_ids=true | all-gather | bytes 393216 | tf_op jit(solution)/shard_map/all_gather | solution.py:172
  20.9 1.8 %fusion.176 = (f32[256]{0:T(256)S(1)}, f32[1,1,256,1024]{3,2,1,0:T(8,128)S(1)}) fusion(bf16[256,1024]{1,0:T(8,128)(2,1)} %collective-permute-done.3, bf16[256,1024]{1,0:T(8,128)(2,1)S(1)} %copy-done.3, pred[]{:T(512)S(6)} %eq.51, bf16[1,1,256,512]{2,3,1,0:T(8,128)(2,1)S(1)} %all_gather.9, bf16[1,1,256,1024]{3,2,1,0:T(8,128)(2,1)S(1)} %copy-done), kind=kOutput, calls=%fused_computation.304 | convolution fusion | flops 273940224 | bytes 2884609 | tf_op jit(solution)/shard_map/qcsf,fd->qcsd/dot_general | solution.py:15
  23.6 1.7 %fusion.15 = bf16[2,1,1,256,256]{4,3,0,2,1:T(8,128)(2,1)S(1)} fusion(bf16[3,1024,256]{2,1,0:T(8,128)(2,1)} %param.16, bf16[1,1,256,1024]{3,2,1,0:T(8,128)(2,1)S(1)} %multiply_convert_fusion.1), kind=kOutput, calls=%fused_computation.32 | convolution fusion | flops 268566528 | bytes 1835008 | tf_op jit(solution)/shard_map/qcsd,kdf->kqcsf/dot_general | solution.py:15
  26.7 3.6 %collective-permute-start.5 = (bf16[1,1,512]{2,1,0:T(2,128)(2,1)}, bf16[1,1,512]{2,1,0:T(2,128)(2,1)}, u32[]{:S(2)}, u32[]{:S(2)}) collective-permute-start(bf16[1,1,512]{2,1,0:T(2,128)(2,1)} %pad_maximum_fusion.5), channel_id=1, source_target_pairs={{0,8},{4,12},{8,0},{12,4},{1,9},{5,13},{9,1},{13,5},{2,10},{6,14},... | collective-permute-start | bytes 3080 | tf_op jit(solution)/shard_map/ppermute | solution.py:60
  36.7 1.3 reshape.1068
  38.0 1.7 %copy.78 = bf16[1,1,1,256,256]{3,4,2,1,0:T(8,128)(2,1)} copy(bf16[1,1,1,256,256]{4,3,0,2,1:T(8,128)(2,1)} %get-tuple-element.27) | data formatting | bytes 262144 | tf_op jit(solution)/shard_map/slice | solution.py:181
  40.9 1.5 collective-permute-start.15
  47.1 1.4 fusion.106
  52.3 1.3 convert_convert_fusion.1
  53.6 1.3 convert_convert_fusion
  56.9 1.3 reshape.1073
  62.0 2.0 %all_gather.10 = bf16[1,1,512]{2,1,0:T(2,128)(2,1)S(1)} all-gather(bf16[1,1,256]{2,1,0:T(2,128)(2,1)} %convert_element_type.267), channel_id=1, replica_groups=mesh['groups'=2,'cand'=4,'query'=2,'mp'=2] {'mp'}, dimensions={2}, use_global_device_ids=true | all-gather | bytes 1536 | tf_op jit(solution)/shard_map/all_gather | solution.py:201
  64.0 1.6 fusion.25
  68.3 1.3 multiply_reduce_fusion.2
  70.3 3.4 %collective-permute-start.8 = (f32[1]{0:T(128)}, f32[1]{0:T(128)}, u32[]{:S(2)}, u32[]{:S(2)}) collective-permute-start(f32[1]{0:T(128)} %bitcast.72), channel_id=1, source_target_pairs={{0,4},{4,8},{8,12},{12,0},{1,5},{5,9},{9,13},{13,1},{2,6},{6,10},{... | collective-permute-start | bytes 20 | tf_op jit(solution)/shard_map/ppermute | solution.py:75
  73.7 3.1 %collective-permute-start.9 = (f32[1]{0:T(128)}, f32[1]{0:T(128)}, u32[]{:S(2)}, u32[]{:S(2)}) collective-permute-start(f32[1]{0:T(128)} %bitcast.72), channel_id=1, source_target_pairs={{0,8},{4,12},{8,0},{12,4},{1,9},{5,13},{9,1},{13,5},{2,10},{6,14},... | collective-permute-start | bytes 20 | tf_op jit(solution)/shard_map/ppermute | solution.py:75
  81.0 2.0 %fusion.159 = (f32[]{:T(128)}, f32[]{:T(128)}, f32[1024]{0:T(1024)}) fusion(f32[]{:T(128)S(6)} %rsqrt.13, f32[]{:T(128)S(6)} %div.79, f32[1024]{0:T(1024)S(1)} %bitcast.376, bf16[1024]{0:T(1024)(128)(2,1)S(1)} %slice_reduce_fusion.1, f32[1024]{0:T(1024)} %param.18, f32[1024]{0:T(1024)} %param.19, f32[]{:T(128)} %bitcast.76), kind=kLoop, calls=%fused_computation.293 | loop fusion | flops 9214 | bytes 18452 | tf_op jit(solution)/shard_map/reduce_sum | solution.py:29
  94.9 2.9 %collective-permute-start.12 = (f32[1,1,512]{2,1,0:T(1,128)}, f32[1,1,512]{2,1,0:T(1,128)}, u32[]{:S(2)}, u32[]{:S(2)}) collective-permute-start(f32[1,1,512]{2,1,0:T(1,128)} %get-tuple-element.35), channel_id=1, source_target_pairs={{0,8},{4,12},{8,0},{12,4},{1,9},{5,13},{9,1},{13,5},{2,10},{6,14},... | collective-permute-start | bytes 6152 | tf_op jit(solution)/shard_map/ppermute | solution.py:89
  103.8 2.5 %all_gather.11 = bf16[1,1,513,512]{2,3,1,0:T(8,128)(2,1)S(1)} all-gather(bf16[1,1,513,256]{2,3,1,0:T(8,128)(2,1)S(1)} %pad_maximum_fusion.1), channel_id=1, replica_groups=mesh['groups'=2,'cand'=4,'query'=2,'mp'=2] {'mp'}, dimensions={3}, use_global_device_ids=true | all-gather | bytes 787968 | tf_op jit(solution)/shard_map/all_gather | solution.py:262
  106.4 3.3 %maximum_select_fusion = bf16[3,1024,512]{2,1,0:T(8,128)(2,1)S(1)} fusion(bf16[3,1024,256]{2,1,0:T(8,128)(2,1)} %collective-permute-done.14, bf16[3,1024,256]{2,1,0:T(8,128)(2,1)} %param.16, pred[]{:T(512)S(6)} %eq.51), kind=kLoop, calls=%fused_computation.2 | loop fusion | flops 14155776 | bytes 6291457 | tf_op jit(solution)/shard_map/jit(_where)/select_n | solution.py:98
  110.7 1.8 %fusion.31 = (f32[256]{0:T(256)S(1)}, f32[256,1024]{1,0:T(8,128)}) fusion(f32[1,1,256,1024]{3,2,1,0:T(8,128)S(1)} %get-tuple-element.47, f32[256]{0:T(256)S(1)} %copy-done.24, f32[256]{0:T(256)S(1)} %copy-done.19, f32[1024]{0:T(1024)S(1)} %copy-done.32, f32[1024]{0:T(1024)S(1)} %copy-done.37, f32[1024]{0:T(1024)S(1)} %bitcast.386, ...), kind=kOutput, calls=%fused_computation.61 | convolution fusion | flops 271056640 | bytes 4472320 | tf_op jit(solution)/shard_map/qcsf,df->qcsd/dot_general | solution.py:15
  112.4 1.4 reduce_sum.183
  113.8 1.8 %convolution_convert_fusion.3 = bf16[256,256]{0,1:T(8,128)(2,1)S(1)} fusion(bf16[256,1024]{1,0:T(8,128)(2,1)S(1)} %copy-done.4, f32[1,1,256,1024]{3,2,1,0:T(8,128)S(1)} %get-tuple-element.47, f32[256,1024]{1,0:T(8,128)} %get-tuple-element.49, f32[256]{0:T(256)S(1)} %broadcast_multiply_fusion.1, f32[256]{0:T(256)S(1)} %broadcast_multiply_fusion.2, ...), kind=kOutput, calls=%fused_computation.35 | convolution fusion | flops 136118272 | bytes 2756608 | tf_op jit(solution)/shard_map/qcsd,fd->qcsf/dot_general | solution.py:15
  122.9 5.3 %collective-permute-done.16 = bf16[103936]{0:T(1024)(128)(2,1)S(1)} collective-permute-done((bf16[103936]{0:T(1024)(128)(2,1)S(1)}, bf16[103936]{0:T(1024)(128)(2,1)S(1)}, u32[]{:S(2)}, u32[]{:S(2)}) %collective-permute-start.16) | collective-permute-done | bytes 207904 | tf_op jit(solution)/shard_map/ppermute | solution.py:339
  132.6 2.4 %collective-permute-start.18 = (bf16[256,384]{1,0:T(8,128)(2,1)S(1)}, bf16[256,384]{1,0:T(8,128)(2,1)S(1)}, u32[]{:S(2)}, u32[]{:S(2)}) collective-permute-start(bf16[256,384]{1,0:T(8,128)(2,1)S(1)} %fusion.13), channel_id=1, source_target_pairs={{0,8},{4,12},{8,0},{12,4},{1,9},{5,13},{9,1},{13,5},{2,10},{6,14},... | collective-permute-start | bytes 589832 | tf_op jit(solution)/shard_map/ppermute | solution.py:371
  137.0 7.4 %collective-permute-done.17 = bf16[256,384]{1,0:T(8,128)(2,1)S(1)} collective-permute-done((bf16[256,384]{1,0:T(8,128)(2,1)S(1)}, bf16[256,384]{1,0:T(8,128)(2,1)S(1)}, u32[]{:S(2)}, u32[]{:S(2)}) %collective-permute-start.17) | collective-permute-done | bytes 196640 | tf_op jit(solution)/shard_map/ppermute | solution.py:371
  144.3 3.4 %collective-permute-done.18 = bf16[256,384]{1,0:T(8,128)(2,1)S(1)} collective-permute-done((bf16[256,384]{1,0:T(8,128)(2,1)S(1)}, bf16[256,384]{1,0:T(8,128)(2,1)S(1)}, u32[]{:S(2)}, u32[]{:S(2)}) %collective-permute-start.18) | collective-permute-done | bytes 196640 | tf_op jit(solution)/shard_map/ppermute | solution.py:371
  147.8 2.8 %collective-permute-done.19 = bf16[256,384]{1,0:T(8,128)(2,1)S(1)} collective-permute-done((bf16[256,384]{1,0:T(8,128)(2,1)S(1)}, bf16[256,384]{1,0:T(8,128)(2,1)S(1)}, u32[]{:S(2)}, u32[]{:S(2)}) %collective-permute-start.19) | collective-permute-done | bytes 196640 | tf_op jit(solution)/shard_map/ppermute | solution.py:371
  152.4 6.3 %collective-permute-done.20 = bf16[256,384]{1,0:T(8,128)(2,1)S(1)} collective-permute-done((bf16[256,384]{1,0:T(8,128)(2,1)S(1)}, bf16[256,384]{1,0:T(8,128)(2,1)S(1)}, u32[]{:S(2)}, u32[]{:S(2)}) %collective-permute-start.20) | collective-permute-done | bytes 196640 | tf_op jit(solution)/shard_map/ppermute | solution.py:382
  (277 shorter events, 72.0 us)
Async XLA Ops:
  1.4 10.0 %collective-permute-start = (f32[1,1,1025]{2,1,0:T(1,128)S(1)}, f32[1,1,1025]{2,1,0:T(1,128)S(1)}, u32[]{:S(2)}, u32[]{:S(2)}) collective-permute-start(f32[1,1,1025]{2,1,0:T(1,128)S(1)} %pad_maximum_fusion.4), channel_id=1, source_target_pairs={{0,4},{4,8},{8,12},{12,0},{1,5},{5,9},{9,13},{13,1},{2,6},{6,10},{... | collective-permute-start | bytes 12308 | tf_op jit(solution)/shard_map/ppermute | solution.py:60
  3.0 8.4 %collective-permute-start.1 = (f32[1,1,1025]{2,1,0:T(1,128)S(1)}, f32[1,1,1025]{2,1,0:T(1,128)S(1)}, u32[]{:S(2)}, u32[]{:S(2)}) collective-permute-start(f32[1,1,1025]{2,1,0:T(1,128)S(1)} %pad_maximum_fusion.4), channel_id=1, source_target_pairs={{0,8},{4,12},{8,0},{12,4},{1,9},{5,13},{9,1},{13,5},{2,10},{6,14},... | collective-permute-start | bytes 12308 | tf_op jit(solution)/shard_map/ppermute | solution.py:60
  4.1 7.3 %collective-permute-start.2 = (f32[1,1,1025]{2,1,0:T(1,128)S(1)}, f32[1,1,1025]{2,1,0:T(1,128)S(1)}, u32[]{:S(2)}, u32[]{:S(2)}) collective-permute-start(f32[1,1,1025]{2,1,0:T(1,128)S(1)} %pad_maximum_fusion.4), channel_id=1, source_target_pairs={{0,12},{4,0},{8,4},{12,8},{1,13},{5,1},{9,5},{13,9},{2,14},{6,2},{... | collective-permute-start | bytes 12308 | tf_op jit(solution)/shard_map/ppermute | solution.py:60
  6.1 14.9 %collective-permute-start.3 = (bf16[256,1024]{1,0:T(8,128)(2,1)}, bf16[256,1024]{1,0:T(8,128)(2,1)}, u32[]{:S(2)}, u32[]{:S(2)}) collective-permute-start(bf16[256,1024]{1,0:T(8,128)(2,1)} %param.14), channel_id=1, source_target_pairs={{0,1},{1,0},{2,3},{3,2},{4,5},{5,4},{6,7},{7,6},{8,9},{9,8},{10,11... | collective-permute-start | bytes 1572872 | tf_op jit(solution)/shard_map/ppermute | solution.py:97
  6.1 57.9 %collective-permute-start.7 = (bf16[256,1024]{1,0:T(8,128)(2,1)}, bf16[256,1024]{1,0:T(8,128)(2,1)}, u32[]{:S(2)}, u32[]{:S(2)}) collective-permute-start(bf16[256,1024]{1,0:T(8,128)(2,1)} %param.17), channel_id=1, source_target_pairs={{0,1},{1,0},{2,3},{3,2},{4,5},{5,4},{6,7},{7,6},{8,9},{9,8},{10,11... | collective-permute-start | bytes 1572872 | tf_op jit(solution)/shard_map/ppermute | solution.py:97
  6.6 6.9 %copy-start.15 = (pred[4]{0:T(512)(128)(4,1)}, pred[4]{0:T(512)(128)(4,1)S(1)}, u32[]{:S(2)}) copy-start(pred[4]{0:T(512)(128)(4,1)S(1)} %get-tuple-element.53) | copy-start | bytes 16
  6.6 11.8 %copy-start.20 = (pred[256]{0:T(512)(128)(4,1)}, pred[256]{0:T(512)(128)(4,1)S(1)}, u32[]{:S(2)}) copy-start(pred[256]{0:T(512)(128)(4,1)S(1)} %iota_compare_fusion.1) | copy-start | bytes 772
  9.0 9.4 %copy-start.5 = (bf16[1,1,1,256,256]{3,4,0,2,1:T(8,128)(2,1)}, bf16[1,1,1,256,256]{3,4,0,2,1:T(8,128)(2,1)S(1)}, u32[]{:S(2)}) copy-start(bf16[1,1,1,256,256]{3,4,0,2,1:T(8,128)(2,1)S(1)} %get-tuple-element.25) | copy-start | bytes 393220
  11.4 95.0 %collective-permute-start.14 = (bf16[3,1024,256]{2,1,0:T(8,128)(2,1)}, bf16[3,1024,256]{2,1,0:T(8,128)(2,1)}, u32[]{:S(2)}, u32[]{:S(2)}) collective-permute-start(bf16[3,1024,256]{2,1,0:T(8,128)(2,1)} %param.16), channel_id=1, source_target_pairs={{0,1},{1,0},{2,3},{3,2},{4,5},{5,4},{6,7},{7,6},{8,9},{9,8},{10,11... | collective-permute-start | bytes 4718600 | tf_op jit(solution)/shard_map/ppermute | solution.py:97
  12.4 6.0 %copy-start.33 = (bf16[4,4,64]{2,1,0:T(4,128)(2,1)}, bf16[4,4,64]{2,1,0:T(4,128)(2,1)S(1)}, u32[]{:S(2)}) copy-start(bf16[4,4,64]{2,1,0:T(4,128)(2,1)S(1)} %reshape.1062) | copy-start | bytes 6148
  13.2 5.6 %copy-start.8 = (f32[4,256]{1,0:T(4,128)}, f32[4,256]{1,0:T(4,128)S(1)}, u32[]{:S(2)}) copy-start(f32[4,256]{1,0:T(4,128)S(1)} %broadcast_select_fusion.2) | copy-start | bytes 12292
  23.6 40.4 %copy-start.2 = (bf16[256,1024]{1,0:T(8,128)(2,1)S(1)}, bf16[256,1024]{1,0:T(8,128)(2,1)}, u32[]{:S(2)}) copy-start(bf16[256,1024]{1,0:T(8,128)(2,1)} %param.17) | copy-start | bytes 1572868
  26.0 7.3 %copy-start.25 = (bf16[1,1,256]{2,1,0:T(2,128)(2,1)}, bf16[1,1,256]{2,1,0:T(2,128)(2,1)S(1)}, u32[]{:S(2)}) copy-start(bf16[1,1,256]{2,1,0:T(2,128)(2,1)S(1)} %slice_bitcast_fusion.10) | copy-start | bytes 1540
  26.1 5.6 %copy-start.26 = (bf16[1,1,256]{2,1,0:T(2,128)(2,1)}, bf16[1,1,256]{2,1,0:T(2,128)(2,1)S(1)}, u32[]{:S(2)}) copy-start(bf16[1,1,256]{2,1,0:T(2,128)(2,1)S(1)} %slice_bitcast_fusion.11) | copy-start | bytes 1540
  26.7 14.3 %collective-permute-start.4 = (bf16[1,1,512]{2,1,0:T(2,128)(2,1)}, bf16[1,1,512]{2,1,0:T(2,128)(2,1)}, u32[]{:S(2)}, u32[]{:S(2)}) collective-permute-start(bf16[1,1,512]{2,1,0:T(2,128)(2,1)} %pad_maximum_fusion.5), channel_id=1, source_target_pairs={{0,4},{4,8},{8,12},{12,0},{1,5},{5,9},{9,13},{13,1},{2,6},{6,10},{... | collective-permute-start | bytes 3080 | tf_op jit(solution)/shard_map/ppermute | solution.py:60
  26.7 15.7 %collective-permute-start.5 = (bf16[1,1,512]{2,1,0:T(2,128)(2,1)}, bf16[1,1,512]{2,1,0:T(2,128)(2,1)}, u32[]{:S(2)}, u32[]{:S(2)}) collective-permute-start(bf16[1,1,512]{2,1,0:T(2,128)(2,1)} %pad_maximum_fusion.5), channel_id=1, source_target_pairs={{0,8},{4,12},{8,0},{12,4},{1,9},{5,13},{9,1},{13,5},{2,10},{6,14},... | collective-permute-start | bytes 3080 | tf_op jit(solution)/shard_map/ppermute | solution.py:60
  30.4 12.0 %collective-permute-start.6 = (bf16[1,1,512]{2,1,0:T(2,128)(2,1)}, bf16[1,1,512]{2,1,0:T(2,128)(2,1)}, u32[]{:S(2)}, u32[]{:S(2)}) collective-permute-start(bf16[1,1,512]{2,1,0:T(2,128)(2,1)} %pad_maximum_fusion.5), channel_id=1, source_target_pairs={{0,12},{4,0},{8,4},{12,8},{1,13},{5,1},{9,5},{13,9},{2,14},{6,2},{... | collective-permute-start | bytes 3080 | tf_op jit(solution)/shard_map/ppermute | solution.py:60
  34.1 8.3 %copy-start.6 = (f32[4,1,256]{2,1,0:T(1,128)}, f32[4,1,256]{2,1,0:T(1,128)S(1)}, u32[]{:S(2)}) copy-start(f32[4,1,256]{2,1,0:T(1,128)S(1)} %fusion.177) | copy-start | bytes 12292
  40.9 88.3 %collective-permute-start.15 = (bf16[256,1024]{1,0:T(8,128)(2,1)S(1)}, bf16[256,1024]{1,0:T(8,128)(2,1)}, u32[]{:S(2)}, u32[]{:S(2)}) collective-permute-start(bf16[256,1024]{1,0:T(8,128)(2,1)S(1)} %bitcast.346), channel_id=1, source_target_pairs={{0,2},{2,0},{1,3},{3,1},{4,6},{6,4},{5,7},{7,5},{8,10},{10,8},{9,1... | collective-permute-start | bytes 1572872 | tf_op jit(solution)/shard_map/ppermute | solution.py:149
  54.9 9.0 %copy-start.7 = (f32[4,256]{1,0:T(4,128)}, f32[4,256]{1,0:T(4,128)S(1)}, u32[]{:S(2)}) copy-start(f32[4,256]{1,0:T(4,128)S(1)} %get-tuple-element.18) | copy-start | bytes 12292
  70.3 7.8 %collective-permute-start.8 = (f32[1]{0:T(128)}, f32[1]{0:T(128)}, u32[]{:S(2)}, u32[]{:S(2)}) collective-permute-start(f32[1]{0:T(128)} %bitcast.72), channel_id=1, source_target_pairs={{0,4},{4,8},{8,12},{12,0},{1,5},{5,9},{9,13},{13,1},{2,6},{6,10},{... | collective-permute-start | bytes 20 | tf_op jit(solution)/shard_map/ppermute | solution.py:75
  73.7 5.0 %collective-permute-start.9 = (f32[1]{0:T(128)}, f32[1]{0:T(128)}, u32[]{:S(2)}, u32[]{:S(2)}) collective-permute-start(f32[1]{0:T(128)} %bitcast.72), channel_id=1, source_target_pairs={{0,8},{4,12},{8,0},{12,4},{1,9},{5,13},{9,1},{13,5},{2,10},{6,14},... | collective-permute-start | bytes 20 | tf_op jit(solution)/shard_map/ppermute | solution.py:75
  76.8 3.5 %collective-permute-start.10 = (f32[1]{0:T(128)}, f32[1]{0:T(128)}, u32[]{:S(2)}, u32[]{:S(2)}) collective-permute-start(f32[1]{0:T(128)} %bitcast.72), channel_id=1, source_target_pairs={{0,12},{4,0},{8,4},{12,8},{1,13},{5,1},{9,5},{13,9},{2,14},{6,2},{... | collective-permute-start | bytes 20 | tf_op jit(solution)/shard_map/ppermute | solution.py:75
  93.3 6.6 %copy-start.14 = (f32[1,4,512]{2,1,0:T(4,128)}, f32[1,4,512]{2,1,0:T(4,128)S(1)}, u32[]{:S(2)}) copy-start(f32[1,4,512]{2,1,0:T(4,128)S(1)} %constant_dynamic-update-slice_fusion) | copy-start | bytes 24580
  93.9 7.6 %collective-permute-start.11 = (f32[1,1,512]{2,1,0:T(1,128)}, f32[1,1,512]{2,1,0:T(1,128)}, u32[]{:S(2)}, u32[]{:S(2)}) collective-permute-start(f32[1,1,512]{2,1,0:T(1,128)} %get-tuple-element.33), channel_id=1, source_target_pairs={{0,4},{4,8},{8,12},{12,0},{1,5},{5,9},{9,13},{13,1},{2,6},{6,10},{... | collective-permute-start | bytes 6152 | tf_op jit(solution)/shard_map/ppermute | solution.py:89
  94.9 6.6 %collective-permute-start.12 = (f32[1,1,512]{2,1,0:T(1,128)}, f32[1,1,512]{2,1,0:T(1,128)}, u32[]{:S(2)}, u32[]{:S(2)}) collective-permute-start(f32[1,1,512]{2,1,0:T(1,128)} %get-tuple-element.35), channel_id=1, source_target_pairs={{0,8},{4,12},{8,0},{12,4},{1,9},{5,13},{9,1},{13,5},{2,10},{6,14},... | collective-permute-start | bytes 6152 | tf_op jit(solution)/shard_map/ppermute | solution.py:89
  97.8 3.7 %collective-permute-start.13 = (f32[1,1,512]{2,1,0:T(1,128)S(1)}, f32[1,1,512]{2,1,0:T(1,128)}, u32[]{:S(2)}, u32[]{:S(2)}) collective-permute-start(f32[1,1,512]{2,1,0:T(1,128)S(1)} %get-tuple-element.34), channel_id=1, source_target_pairs={{0,12},{4,0},{8,4},{12,8},{1,13},{5,1},{9,5},{13,9},{2,14},{6,2},{... | collective-permute-start | bytes 6152 | tf_op jit(solution)/shard_map/ppermute | solution.py:89
  120.9 7.3 %collective-permute-start.16 = (bf16[103936]{0:T(1024)(128)(2,1)S(1)}, bf16[103936]{0:T(1024)(128)(2,1)S(1)}, u32[]{:S(2)}, u32[]{:S(2)}) collective-permute-start(bf16[103936]{0:T(1024)(128)(2,1)S(1)} %pad_maximum_fusion.2), channel_id=1, source_target_pairs={{0,2},{2,0},{1,3},{3,1},{4,6},{6,4},{5,7},{7,5},{8,10},{10,8},{9,1... | collective-permute-start | bytes 623624 | tf_op jit(solution)/shard_map/ppermute | solution.py:339
  130.4 13.9 %collective-permute-start.17 = (bf16[256,384]{1,0:T(8,128)(2,1)S(1)}, bf16[256,384]{1,0:T(8,128)(2,1)S(1)}, u32[]{:S(2)}, u32[]{:S(2)}) collective-permute-start(bf16[256,384]{1,0:T(8,128)(2,1)S(1)} %fusion.14), channel_id=1, source_target_pairs={{0,4},{4,8},{8,12},{12,0},{1,5},{5,9},{9,13},{13,1},{2,6},{6,10},{... | collective-permute-start | bytes 589832 | tf_op jit(solution)/shard_map/ppermute | solution.py:371
  132.6 15.1 %collective-permute-start.18 = (bf16[256,384]{1,0:T(8,128)(2,1)S(1)}, bf16[256,384]{1,0:T(8,128)(2,1)S(1)}, u32[]{:S(2)}, u32[]{:S(2)}) collective-permute-start(bf16[256,384]{1,0:T(8,128)(2,1)S(1)} %fusion.13), channel_id=1, source_target_pairs={{0,8},{4,12},{8,0},{12,4},{1,9},{5,13},{9,1},{13,5},{2,10},{6,14},... | collective-permute-start | bytes 589832 | tf_op jit(solution)/shard_map/ppermute | solution.py:371
  136.2 14.4 %collective-permute-start.19 = (bf16[256,384]{1,0:T(8,128)(2,1)S(1)}, bf16[256,384]{1,0:T(8,128)(2,1)S(1)}, u32[]{:S(2)}, u32[]{:S(2)}) collective-permute-start(bf16[256,384]{1,0:T(8,128)(2,1)S(1)} %fusion.12), channel_id=1, source_target_pairs={{0,12},{4,0},{8,4},{12,8},{1,13},{5,1},{9,5},{13,9},{2,14},{6,2},{... | collective-permute-start | bytes 589832 | tf_op jit(solution)/shard_map/ppermute | solution.py:371
  151.8 6.9 %collective-permute-start.20 = (bf16[256,384]{1,0:T(8,128)(2,1)S(1)}, bf16[256,384]{1,0:T(8,128)(2,1)S(1)}, u32[]{:S(2)}, u32[]{:S(2)}) collective-permute-start(bf16[256,384]{1,0:T(8,128)(2,1)S(1)} %fusion.11), channel_id=1, source_target_pairs={{0,2},{2,0},{1,3},{3,1},{4,6},{6,4},{5,7},{7,5},{8,10},{10,8},{9,1... | collective-permute-start | bytes 589832 | tf_op jit(solution)/shard_map/ppermute | solution.py:382
  (30 other events, 63.9 us)

commit v22 on v8

--- a/solution.py
+++ b/solution.py
@@ -348,12 +348,12 @@
     )
     reduced = scatter_cand(paired.astype(jnp.bfloat16), 0, jnp.float32).astype(jnp.bfloat16)
     partner = lax.ppermute(reduced, "query", swap)
-    joined = jnp.where(
-        side == 0,
-        jnp.concatenate([reduced, partner], 1),
-        jnp.concatenate([partner, reduced], 1),
-    )
-    return joined.reshape(joined.shape[0], 3, local_width).astype(jnp.float32)
+    joined = jnp.zeros((reduced.shape[0], 2 * half), jnp.float32)
+    joined = lax.dynamic_update_slice_in_dim(joined, reduced.astype(jnp.float32), side * half, 1)
+    joined = lax.dynamic_update_slice_in_dim(
+        joined, partner.astype(jnp.float32), (1 - side) * half, 1
+    )
+    return joined.reshape(joined.shape[0], 3, local_width)
 
 
 def solution(mesh):

time: 116 us -> 116 us (level)
  no operation moved by 1% of the time
where the time goes in v22:
time: 116 us
  waiting for transfers between devices  30 us (26%)
  starting transfers between devices  28.4 us (24%)
  matrix products  20.8 us (18%)
  other arithmetic  13.8 us (12%)
  between operations  8.51 us (7%)
  local copies, waits for them, and re-layouts  7.77 us (7%)
  blocking collectives  6.37 us (5%)
    dot_general x32, matrix products, mixed(): jnp.einsum(pattern, former, latter, preferred_element_type=jnp.float32)  20.8 us
    ppermute x6, waiting for transfers between devices, scatter_cand(): lax.ppermute(piece, 'cand', [(j, (j + k) % count) for j in range(count)])  17.9 us
    ppermute x6, starting transfers between devices, scatter_cand(): lax.ppermute(piece, 'cand', [(j, (j + k) % count) for j in range(count)])  8.88 us
    ppermute x6, starting transfers between devices, gather_cand(): lax.ppermute(block, 'cand', [(j, (j + k) % count) for j in range(count)])  8.45 us
    ppermute x3, starting transfers between devices, sum_cand(): lax.ppermute(block, 'cand', [(j, (j + k) % count) for j in range(count)])  7.77 us
    ppermute x1, waiting for transfers between devices, local(): partner = lax.ppermute(reduced, 'query', swap)  5.94 us
    ppermute x1, waiting for transfers between devices, local(): lax.ppermute(jnp.concatenate([given_half.reshape(-1), cls_flat.reshape(-1...  5.04 us
    select_n x1, other arithmetic, gather_mp(): jnp.where(lax.axis_index('mp') == 0, jnp.concatenate([block, other], axis...  3.41 us
  transfers between devices with their start and end apart: 21, of which 8 were waited for; matrix products, arithmetic and copies ran while one was open for 33% of the time, Pallas kernels for 0%

profile of v22, /device:TPU:8, one launch (start us, length us, event | category | flops | bytes accessed | tf_op | source)
XLA Modules:
  0.0 115.7 jit_solution(4891520948152273838)
XLA Ops:
  1.4 1.6 %collective-permute-start = (f32[1,1,1025]{2,1,0:T(1,128)S(1)}, f32[1,1,1025]{2,1,0:T(1,128)S(1)}, u32[]{:S(2)}, u32[]{:S(2)}) collective-permute-start(f32[1,1,1025]{2,1,0:T(1,128)S(1)} %pad_maximum_fusion.4), channel_id=1, source_target_pairs={{0,4},{4,8},{8,12},{12,0},{1,5},{5,9},{9,13},{13,1},{2,6},{6,10},{... | collective-permute-start | bytes 12308 | tf_op jit(solution)/shard_map/ppermute | solution.py:60
  3.0 1.1 collective-permute-start.1
  4.1 1.9 %collective-permute-start.2 = (f32[1,1,1025]{2,1,0:T(1,128)S(1)}, f32[1,1,1025]{2,1,0:T(1,128)S(1)}, u32[]{:S(2)}, u32[]{:S(2)}) collective-permute-start(f32[1,1,1025]{2,1,0:T(1,128)S(1)} %pad_maximum_fusion.4), channel_id=1, source_target_pairs={{0,12},{4,0},{8,4},{12,8},{1,13},{5,1},{9,5},{13,9},{2,14},{6,2},{... | collective-permute-start | bytes 12308 | tf_op jit(solution)/shard_map/ppermute | solution.py:60
  6.6 2.2 %fusion.5 = bf16[3,1,1,256,256]{3,4,0,2,1:T(8,128)(2,1)S(1)} fusion(bf16[3,1024,256]{2,1,0:T(8,128)(2,1)} %param.13, bf16[1,1,256,1024]{3,2,1,0:T(8,128)(2,1)} %param.10), kind=kOutput, calls=%fused_computation.15 | convolution fusion | flops 402849792 | bytes 2490368 | tf_op jit(solution)/shard_map/qcsd,kdf->kqcsf/dot_general | solution.py:15
  15.1 1.3 %exponential_reduce_fusion = f32[]{:T(128)} fusion(f32[1,4,1025]{2,1,0:T(4,128)S(1)} %bitcast_select_fusion, f32[]{:T(128)} %slice_reduce_fusion.2), kind=kLoop, calls=%fused_computation.204 | loop fusion | flops 7 | bytes 24 | tf_op jit(solution)/shard_map/reduce_sum | solution.py:210
  18.9 2.1 %all_gather.9 = bf16[1,1,256,512]{2,3,1,0:T(8,128)(2,1)S(1)} all-gather(bf16[1,1,256,256]{2,3,1,0:T(8,128)(2,1)S(1)} %bitcast.363), channel_id=1, replica_groups=mesh['groups'=2,'cand'=4,'query'=2,'mp'=2] {'mp'}, dimensions={3}, use_global_device_ids=true | all-gather | bytes 393216 | tf_op jit(solution)/shard_map/all_gather | solution.py:172
  21.0 1.9 %fusion.141 = (f32[256]{0:T(256)S(1)}, f32[1,1,256,1024]{3,2,1,0:T(8,128)S(1)}) fusion(bf16[256,1024]{1,0:T(8,128)(2,1)} %collective-permute-done.3, bf16[256,1024]{1,0:T(8,128)(2,1)S(1)} %copy-done.2, pred[]{:T(512)S(6)} %eq.47, bf16[1,1,256,512]{2,3,1,0:T(8,128)(2,1)S(1)} %all_gather.9, bf16[1,1,256,1024]{3,2,1,0:T(8,128)(2,1)} %param.10), kind=kOutput, calls=%fused_computation.262 | convolution fusion | flops 273940224 | bytes 2884609 | tf_op jit(solution)/shard_map/qcsf,fd->qcsd/dot_general | solution.py:15
  23.5 1.7 %fusion.6 = bf16[2,1,1,256,256]{4,3,0,2,1:T(8,128)(2,1)S(1)} fusion(bf16[3,1024,256]{2,1,0:T(8,128)(2,1)} %param.16, bf16[1,1,256,1024]{3,2,1,0:T(8,128)(2,1)S(1)} %multiply_convert_fusion.1), kind=kOutput, calls=%fused_computation.20 | convolution fusion | flops 268566528 | bytes 1835008 | tf_op jit(solution)/shard_map/qcsd,kdf->kqcsf/dot_general | solution.py:15
  25.4 3.6 %collective-permute-start.5 = (bf16[1,1,512]{2,1,0:T(2,128)(2,1)S(1)}, bf16[1,1,512]{2,1,0:T(2,128)(2,1)S(1)}, u32[]{:S(2)}, u32[]{:S(2)}) collective-permute-start(bf16[1,1,512]{2,1,0:T(2,128)(2,1)S(1)} %pad_maximum_fusion.5), channel_id=1, source_target_pairs={{0,8},{4,12},{8,0},{12,4},{1,9},{5,13},{9,1},{13,5},{2,10},{6,14},... | collective-permute-start | bytes 3080 | tf_op jit(solution)/shard_map/ppermute | solution.py:60
  29.1 1.2 %fusion.39 = f32[1,256]{1,0:T(1,128)S(1)} fusion(bf16[3,1024,256]{2,1,0:T(8,128)(2,1)} %param.16, bf16[1,1,256,1024]{3,2,1,0:T(8,128)(2,1)S(1)} %multiply_convert_fusion.1), kind=kOutput, calls=%fused_computation.72 | convolution fusion | flops 524288 | bytes 529408 | tf_op jit(solution)/shard_map/qcd,df->qcf/dot_general | solution.py:15
  31.0 1.6 %collective-permute-start.16 = (bf16[256,1024]{1,0:T(8,128)(2,1)}, bf16[256,1024]{1,0:T(8,128)(2,1)}, u32[]{:S(2)}, u32[]{:S(2)}) collective-permute-start(bf16[256,1024]{1,0:T(8,128)(2,1)} %bitcast), channel_id=1, source_target_pairs={{0,2},{2,0},{1,3},{3,1},{4,6},{6,4},{5,7},{7,5},{8,10},{10,8},{9,1... | collective-permute-start | bytes 1572872 | tf_op jit(solution)/shard_map/ppermute | solution.py:149
  34.8 1.8 %all_gather.10 = bf16[1,1,512]{2,1,0:T(2,128)(2,1)S(1)} all-gather(bf16[1,1,256]{2,1,0:T(2,128)(2,1)S(1)} %convert_element_type.264), channel_id=1, replica_groups=mesh['groups'=2,'cand'=4,'query'=2,'mp'=2] {'mp'}, dimensions={2}, use_global_device_ids=true | all-gather | bytes 1536 | tf_op jit(solution)/shard_map/all_gather | solution.py:201
  36.5 1.6 %fusion.16 = f32[1,1024]{1,0:T(1,128)S(1)} fusion(bf16[256,1024]{1,0:T(8,128)(2,1)} %collective-permute-done.7, bf16[256,1024]{1,0:T(8,128)(2,1)S(1)} %copy-done.1, pred[]{:T(512)S(6)} %eq.47, bf16[1,1,512]{2,1,0:T(2,128)(2,1)S(1)} %all_gather.10), kind=kOutput, calls=%fused_computation.38 | convolution fusion | flops 5767168 | bytes 1053697 | tf_op jit(solution)/shard_map/qcf,fd->qcd/dot_general | solution.py:15
  41.8 3.3 %collective-permute-start.8 = (f32[1]{0:T(128)}, f32[1]{0:T(128)}, u32[]{:S(2)}, u32[]{:S(2)}) collective-permute-start(f32[1]{0:T(128)} %bitcast.72), channel_id=1, source_target_pairs={{0,4},{4,8},{8,12},{12,0},{1,5},{5,9},{9,13},{13,1},{2,6},{6,10},{... | collective-permute-start | bytes 20 | tf_op jit(solution)/shard_map/ppermute | solution.py:75
  45.1 3.1 %collective-permute-start.9 = (f32[1]{0:T(128)}, f32[1]{0:T(128)}, u32[]{:S(2)}, u32[]{:S(2)}) collective-permute-start(f32[1]{0:T(128)} %bitcast.72), channel_id=1, source_target_pairs={{0,8},{4,12},{8,0},{12,4},{1,9},{5,13},{9,1},{13,5},{2,10},{6,14},... | collective-permute-start | bytes 20 | tf_op jit(solution)/shard_map/ppermute | solution.py:75
  48.2 1.4 %collective-permute-start.10 = (f32[1]{0:T(128)}, f32[1]{0:T(128)}, u32[]{:S(2)}, u32[]{:S(2)}) collective-permute-start(f32[1]{0:T(128)} %bitcast.72), channel_id=1, source_target_pairs={{0,12},{4,0},{8,4},{12,8},{1,13},{5,1},{9,5},{13,9},{2,14},{6,2},{... | collective-permute-start | bytes 20 | tf_op jit(solution)/shard_map/ppermute | solution.py:75
  56.8 2.9 %collective-permute-start.12 = (f32[1,1,512]{2,1,0:T(1,128)S(1)}, f32[1,1,512]{2,1,0:T(1,128)S(1)}, u32[]{:S(2)}, u32[]{:S(2)}) collective-permute-start(f32[1,1,512]{2,1,0:T(1,128)S(1)} %get-tuple-element.38), channel_id=1, source_target_pairs={{0,8},{4,12},{8,0},{12,4},{1,9},{5,13},{9,1},{13,5},{2,10},{6,14},... | collective-permute-start | bytes 6152 | tf_op jit(solution)/shard_map/ppermute | solution.py:89
  59.7 1.1 collective-permute-start.13
  61.5 1.8 %collective-permute-done.13 = f32[1,1,512]{2,1,0:T(1,128)S(1)} collective-permute-done((f32[1,1,512]{2,1,0:T(1,128)S(1)}, f32[1,1,512]{2,1,0:T(1,128)S(1)}, u32[]{:S(2)}, u32[]{:S(2)}) %collective-permute-start.13) | collective-permute-done | bytes 2080 | tf_op jit(solution)/shard_map/ppermute | solution.py:89
  63.5 2.5 %all_gather.11 = bf16[1,1,513,512]{2,3,1,0:T(8,128)(2,1)S(1)} all-gather(bf16[1,1,513,256]{2,3,1,0:T(8,128)(2,1)S(1)} %pad_maximum_fusion.1), channel_id=1, replica_groups=mesh['groups'=2,'cand'=4,'query'=2,'mp'=2] {'mp'}, dimensions={3}, use_global_device_ids=true | all-gather | bytes 787968 | tf_op jit(solution)/shard_map/all_gather | solution.py:262
  66.1 3.4 %maximum_select_fusion = bf16[3,1024,512]{2,1,0:T(8,128)(2,1)S(1)} fusion(bf16[3,1024,256]{2,1,0:T(8,128)(2,1)} %collective-permute-done.14, bf16[3,1024,256]{2,1,0:T(8,128)(2,1)} %param.16, pred[]{:T(512)S(6)} %eq.47), kind=kLoop, calls=%fused_computation.2 | loop fusion | flops 14155776 | bytes 6291457 | tf_op jit(solution)/shard_map/jit(_where)/select_n | solution.py:98
  71.5 1.6 %convolution_convert_fusion.3 = bf16[256,256]{0,1:T(8,128)(2,1)S(1)} fusion(bf16[256,1024]{1,0:T(8,128)(2,1)} %param.14, f32[1,1,256,1024]{3,2,1,0:T(8,128)S(1)} %get-tuple-element.50, f32[256,1024]{1,0:T(8,128)S(1)} %get-tuple-element.52, f32[256]{0:T(256)S(1)} %broadcast_multiply_fusion.1, f32[256]{0:T(256)S(1)} %broadcast_multiply_fusion.2, ...), kind=kOutput, calls=%fused_computation.23 | convolution fusion | flops 136118272 | bytes 2756608 | tf_op jit(solution)/shard_map/qcsd,fd->qcsf/dot_general | solution.py:15
  74.2 1.3 %multiply_reduce_fusion = (f32[4,256]{1,0:T(4,128)S(1)}, f32[4,256,256]{1,2,0:T(8,128)S(1)}) fusion(f32[4,256]{1,0:T(4,128)} %copy-done.5, f32[4,256,256]{1,2,0:T(8,128)S(1)} %get-tuple-element.48, f32[4,256]{1,0:T(4,128)S(1)} %broadcast_select_fusion.2, bf16[256,4,64]{0,2,1:T(8,128)(2,1)S(1)} %bitcast.361, bf16[256,4,64]{0,2,1:T(8,128)(2,1)} %bitcast.365), kind=kOutput, calls=%fused_computation.50 | convolution fusion | flops 34601984 | bytes 2371584 | tf_op jit(solution)/shard_map/qcshe,qcthe->qchst/dot_general | solution.py:15
  79.0 1.6 %fusion.31 = f32[1024,384]{0,1:T(8,128)S(1)} fusion(bf16[4,1024]{1,0:T(4,128)(2,1)S(1)} %get-tuple-element.35, bf16[256,1024]{1,0:T(8,128)(2,1)} %bitcast, s32[]{:T(128)S(6)} %select_n.253, bf16[256,768]{0,1:T(8,128)(2,1)S(1)} %bitcast.345, bf16[4,768]{0,1:T(8,128)(2,1)S(1)} %copy.81), kind=kOutput, calls=%fused_computation.65 | convolution fusion | flops 205936640 | bytes 2504708 | tf_op jit(solution)/shard_map/rd,rf->df/dot_general | solution.py:15
  80.6 5.0 %collective-permute-done.15 = bf16[103936]{0:T(1024)(128)(2,1)S(1)} collective-permute-done((bf16[103936]{0:T(1024)(128)(2,1)S(1)}, bf16[103936]{0:T(1024)(128)(2,1)S(1)}, u32[]{:S(2)}, u32[]{:S(2)}) %collective-permute-start.15) | collective-permute-done | bytes 207904 | tf_op jit(solution)/shard_map/ppermute | solution.py:339
  85.9 1.4 %fusion.145 = f32[384,1024]{1,0:T(8,128)S(1)} fusion(bf16[256,384]{1,0:T(8,128)(2,1)S(1)} %slice.153, bf16[256,1024]{1,0:T(8,128)(2,1)} %collective-permute-done.16), kind=kOutput, calls=%fused_computation.266 | convolution fusion | flops 201326592 | bytes 2293760 | tf_op jit(solution)/shard_map/rd,rf->df/dot_general | solution.py:15
  88.4 2.9 %collective-permute-start.18 = (bf16[256,384]{0,1:T(8,128)(2,1)S(1)}, bf16[256,384]{0,1:T(8,128)(2,1)S(1)}, u32[]{:S(2)}, u32[]{:S(2)}) collective-permute-start(bf16[256,384]{0,1:T(8,128)(2,1)S(1)} %get-tuple-element.26), channel_id=1, source_target_pairs={{0,8},{4,12},{8,0},{12,4},{1,9},{5,13},{9,1},{13,5},{2,10},{6,14},... | collective-permute-start | bytes 589832 | tf_op jit(solution)/shard_map/ppermute | solution.py:89
  91.7 10.3 %collective-permute-done.17 = bf16[256,384]{0,1:T(8,128)(2,1)S(1)} collective-permute-done((bf16[256,384]{0,1:T(8,128)(2,1)S(1)}, bf16[256,384]{0,1:T(8,128)(2,1)S(1)}, u32[]{:S(2)}, u32[]{:S(2)}) %collective-permute-start.17) | collective-permute-done | bytes 196640 | tf_op jit(solution)/shard_map/ppermute | solution.py:89
  102.0 2.7 %collective-permute-done.18 = bf16[256,384]{0,1:T(8,128)(2,1)S(1)} collective-permute-done((bf16[256,384]{0,1:T(8,128)(2,1)S(1)}, bf16[256,384]{0,1:T(8,128)(2,1)S(1)}, u32[]{:S(2)}, u32[]{:S(2)}) %collective-permute-start.18) | collective-permute-done | bytes 196640 | tf_op jit(solution)/shard_map/ppermute | solution.py:89
  104.7 3.1 %collective-permute-done.19 = bf16[256,384]{0,1:T(8,128)(2,1)S(1)} collective-permute-done((bf16[256,384]{0,1:T(8,128)(2,1)S(1)}, bf16[256,384]{0,1:T(8,128)(2,1)S(1)}, u32[]{:S(2)}, u32[]{:S(2)}) %collective-permute-start.19) | collective-permute-done | bytes 196640 | tf_op jit(solution)/shard_map/ppermute | solution.py:89
  108.6 5.9 %collective-permute-done.20 = bf16[256,384]{0,1:T(8,128)(2,1)S(1)} collective-permute-done((bf16[256,384]{0,1:T(8,128)(2,1)S(1)}, bf16[256,384]{0,1:T(8,128)(2,1)S(1)}, u32[]{:S(2)}, u32[]{:S(2)}) %collective-permute-start.20) | collective-permute-done | bytes 196640 | tf_op jit(solution)/shard_map/ppermute | solution.py:350
  114.6 1.1 copy.83
  (228 shorter events, 27.0 us)
Async XLA Ops:
  1.4 10.0 %collective-permute-start = (f32[1,1,1025]{2,1,0:T(1,128)S(1)}, f32[1,1,1025]{2,1,0:T(1,128)S(1)}, u32[]{:S(2)}, u32[]{:S(2)}) collective-permute-start(f32[1,1,1025]{2,1,0:T(1,128)S(1)} %pad_maximum_fusion.4), channel_id=1, source_target_pairs={{0,4},{4,8},{8,12},{12,0},{1,5},{5,9},{9,13},{13,1},{2,6},{6,10},{... | collective-permute-start | bytes 12308 | tf_op jit(solution)/shard_map/ppermute | solution.py:60
  3.0 8.4 %collective-permute-start.1 = (f32[1,1,1025]{2,1,0:T(1,128)S(1)}, f32[1,1,1025]{2,1,0:T(1,128)S(1)}, u32[]{:S(2)}, u32[]{:S(2)}) collective-permute-start(f32[1,1,1025]{2,1,0:T(1,128)S(1)} %pad_maximum_fusion.4), channel_id=1, source_target_pairs={{0,8},{4,12},{8,0},{12,4},{1,9},{5,13},{9,1},{13,5},{2,10},{6,14},... | collective-permute-start | bytes 12308 | tf_op jit(solution)/shard_map/ppermute | solution.py:60
  4.1 7.3 %collective-permute-start.2 = (f32[1,1,1025]{2,1,0:T(1,128)S(1)}, f32[1,1,1025]{2,1,0:T(1,128)S(1)}, u32[]{:S(2)}, u32[]{:S(2)}) collective-permute-start(f32[1,1,1025]{2,1,0:T(1,128)S(1)} %pad_maximum_fusion.4), channel_id=1, source_target_pairs={{0,12},{4,0},{8,4},{12,8},{1,13},{5,1},{9,5},{13,9},{2,14},{6,2},{... | collective-permute-start | bytes 12308 | tf_op jit(solution)/shard_map/ppermute | solution.py:60
  6.1 15.0 %collective-permute-start.3 = (bf16[256,1024]{1,0:T(8,128)(2,1)}, bf16[256,1024]{1,0:T(8,128)(2,1)}, u32[]{:S(2)}, u32[]{:S(2)}) collective-permute-start(bf16[256,1024]{1,0:T(8,128)(2,1)} %param.14), channel_id=1, source_target_pairs={{0,1},{1,0},{2,3},{3,2},{4,5},{5,4},{6,7},{7,6},{8,9},{9,8},{10,11... | collective-permute-start | bytes 1572872 | tf_op jit(solution)/shard_map/ppermute | solution.py:97
  6.1 30.5 %collective-permute-start.7 = (bf16[256,1024]{1,0:T(8,128)(2,1)}, bf16[256,1024]{1,0:T(8,128)(2,1)}, u32[]{:S(2)}, u32[]{:S(2)}) collective-permute-start(bf16[256,1024]{1,0:T(8,128)(2,1)} %param.17), channel_id=1, source_target_pairs={{0,1},{1,0},{2,3},{3,2},{4,5},{5,4},{6,7},{7,6},{8,9},{9,8},{10,11... | collective-permute-start | bytes 1572872 | tf_op jit(solution)/shard_map/ppermute | solution.py:97
  6.6 5.4 %copy-start = (bf16[3,1024,256]{2,1,0:T(8,128)(2,1)S(1)}, bf16[3,1024,256]{2,1,0:T(8,128)(2,1)}, u32[]{:S(2)}) copy-start(bf16[3,1024,256]{2,1,0:T(8,128)(2,1)} %param.13) | copy-start | bytes 4718596
  8.9 14.0 %copy-start.3 = (bf16[1,1,1,256,256]{3,4,0,2,1:T(8,128)(2,1)}, bf16[1,1,1,256,256]{3,4,0,2,1:T(8,128)(2,1)S(1)}, u32[]{:S(2)}) copy-start(bf16[1,1,1,256,256]{3,4,0,2,1:T(8,128)(2,1)S(1)} %get-tuple-element.28) | copy-start | bytes 393220
  10.7 59.7 %copy-start.10 = (pred[256]{0:T(512)(128)(4,1)}, pred[256]{0:T(512)(128)(4,1)S(1)}, u32[]{:S(2)}) copy-start(pred[256]{0:T(512)(128)(4,1)S(1)} %iota_compare_fusion.1) | copy-start | bytes 772
  11.4 54.8 %collective-permute-start.14 = (bf16[3,1024,256]{2,1,0:T(8,128)(2,1)}, bf16[3,1024,256]{2,1,0:T(8,128)(2,1)}, u32[]{:S(2)}, u32[]{:S(2)}) collective-permute-start(bf16[3,1024,256]{2,1,0:T(8,128)(2,1)} %param.16), channel_id=1, source_target_pairs={{0,1},{1,0},{2,3},{3,2},{4,5},{5,4},{6,7},{7,6},{8,9},{9,8},{10,11... | collective-permute-start | bytes 4718600 | tf_op jit(solution)/shard_map/ppermute | solution.py:97
  12.4 2.5 %copy-start.16 = (bf16[4,4,64]{2,1,0:T(4,128)(2,1)}, bf16[4,4,64]{2,1,0:T(4,128)(2,1)S(1)}, u32[]{:S(2)}) copy-start(bf16[4,4,64]{2,1,0:T(4,128)(2,1)S(1)} %reshape.1062) | copy-start | bytes 6148
  14.2 9.2 %copy-start.5 = (f32[4,256]{1,0:T(4,128)}, f32[4,256]{1,0:T(4,128)S(1)}, u32[]{:S(2)}) copy-start(f32[4,256]{1,0:T(4,128)S(1)} %broadcast_select_fusion.1) | copy-start | bytes 12292
  15.1 3.8 %copy-start.18 = (bf16[4,4,64]{2,1,0:T(4,128)(2,1)}, bf16[4,4,64]{2,1,0:T(4,128)(2,1)S(1)}, u32[]{:S(2)}) copy-start(bf16[4,4,64]{2,1,0:T(4,128)(2,1)S(1)} %reshape.1065) | copy-start | bytes 6148
  22.9 47.5 %copy-start.9 = (f32[256]{0:T(256)}, f32[256]{0:T(256)S(1)}, u32[]{:S(2)}) copy-start(f32[256]{0:T(256)S(1)} %broadcast_multiply_fusion.3) | copy-start | bytes 3076
  23.2 47.2 %copy-start.12 = (f32[256]{0:T(256)}, f32[256]{0:T(256)S(1)}, u32[]{:S(2)}) copy-start(f32[256]{0:T(256)S(1)} %add_rsqrt_fusion) | copy-start | bytes 3076
  23.5 13.1 %copy-start.1 = (bf16[256,1024]{1,0:T(8,128)(2,1)S(1)}, bf16[256,1024]{1,0:T(8,128)(2,1)}, u32[]{:S(2)}) copy-start(bf16[256,1024]{1,0:T(8,128)(2,1)} %param.17) | copy-start | bytes 1572868
  25.3 5.7 %collective-permute-start.4 = (bf16[1,1,512]{2,1,0:T(2,128)(2,1)S(1)}, bf16[1,1,512]{2,1,0:T(2,128)(2,1)S(1)}, u32[]{:S(2)}, u32[]{:S(2)}) collective-permute-start(bf16[1,1,512]{2,1,0:T(2,128)(2,1)S(1)} %pad_maximum_fusion.5), channel_id=1, source_target_pairs={{0,4},{4,8},{8,12},{12,0},{1,5},{5,9},{9,13},{13,1},{2,6},{6,10},{... | collective-permute-start | bytes 3080 | tf_op jit(solution)/shard_map/ppermute | solution.py:60
  25.4 7.1 %collective-permute-start.5 = (bf16[1,1,512]{2,1,0:T(2,128)(2,1)S(1)}, bf16[1,1,512]{2,1,0:T(2,128)(2,1)S(1)}, u32[]{:S(2)}, u32[]{:S(2)}) collective-permute-start(bf16[1,1,512]{2,1,0:T(2,128)(2,1)S(1)} %pad_maximum_fusion.5), channel_id=1, source_target_pairs={{0,8},{4,12},{8,0},{12,4},{1,9},{5,13},{9,1},{13,5},{2,10},{6,14},... | collective-permute-start | bytes 3080 | tf_op jit(solution)/shard_map/ppermute | solution.py:60
  29.1 3.6 %collective-permute-start.6 = (bf16[1,1,512]{2,1,0:T(2,128)(2,1)S(1)}, bf16[1,1,512]{2,1,0:T(2,128)(2,1)S(1)}, u32[]{:S(2)}, u32[]{:S(2)}) collective-permute-start(bf16[1,1,512]{2,1,0:T(2,128)(2,1)S(1)} %pad_maximum_fusion.5), channel_id=1, source_target_pairs={{0,12},{4,0},{8,4},{12,8},{1,13},{5,1},{9,5},{13,9},{2,14},{6,2},{... | collective-permute-start | bytes 3080 | tf_op jit(solution)/shard_map/ppermute | solution.py:60
  31.0 54.9 %collective-permute-start.16 = (bf16[256,1024]{1,0:T(8,128)(2,1)}, bf16[256,1024]{1,0:T(8,128)(2,1)}, u32[]{:S(2)}, u32[]{:S(2)}) collective-permute-start(bf16[256,1024]{1,0:T(8,128)(2,1)} %bitcast), channel_id=1, source_target_pairs={{0,2},{2,0},{1,3},{3,1},{4,6},{6,4},{5,7},{7,5},{8,10},{10,8},{9,1... | collective-permute-start | bytes 1572872 | tf_op jit(solution)/shard_map/ppermute | solution.py:149
  34.5 6.1 %copy-start.7 = (f32[1024]{0:T(1024)S(1)}, f32[1024]{0:T(1024)}, u32[]{:S(2)}) copy-start(f32[1024]{0:T(1024)} %param.18) | copy-start | bytes 12292
  34.5 6.1 %copy-start.8 = (f32[1024]{0:T(1024)S(1)}, f32[1024]{0:T(1024)}, u32[]{:S(2)}) copy-start(f32[1024]{0:T(1024)} %param.19) | copy-start | bytes 12292
  41.8 7.8 %collective-permute-start.8 = (f32[1]{0:T(128)}, f32[1]{0:T(128)}, u32[]{:S(2)}, u32[]{:S(2)}) collective-permute-start(f32[1]{0:T(128)} %bitcast.72), channel_id=1, source_target_pairs={{0,4},{4,8},{8,12},{12,0},{1,5},{5,9},{9,13},{13,1},{2,6},{6,10},{... | collective-permute-start | bytes 20 | tf_op jit(solution)/shard_map/ppermute | solution.py:75
  45.1 5.1 %collective-permute-start.9 = (f32[1]{0:T(128)}, f32[1]{0:T(128)}, u32[]{:S(2)}, u32[]{:S(2)}) collective-permute-start(f32[1]{0:T(128)} %bitcast.72), channel_id=1, source_target_pairs={{0,8},{4,12},{8,0},{12,4},{1,9},{5,13},{9,1},{13,5},{2,10},{6,14},... | collective-permute-start | bytes 20 | tf_op jit(solution)/shard_map/ppermute | solution.py:75
  48.2 3.6 %collective-permute-start.10 = (f32[1]{0:T(128)}, f32[1]{0:T(128)}, u32[]{:S(2)}, u32[]{:S(2)}) collective-permute-start(f32[1]{0:T(128)} %bitcast.72), channel_id=1, source_target_pairs={{0,12},{4,0},{8,4},{12,8},{1,13},{5,1},{9,5},{13,9},{2,14},{6,2},{... | collective-permute-start | bytes 20 | tf_op jit(solution)/shard_map/ppermute | solution.py:75
  55.8 5.7 %collective-permute-start.11 = (f32[1,1,512]{2,1,0:T(1,128)S(1)}, f32[1,1,512]{2,1,0:T(1,128)S(1)}, u32[]{:S(2)}, u32[]{:S(2)}) collective-permute-start(f32[1,1,512]{2,1,0:T(1,128)S(1)} %get-tuple-element.36), channel_id=1, source_target_pairs={{0,4},{4,8},{8,12},{12,0},{1,5},{5,9},{9,13},{13,1},{2,6},{6,10},{... | collective-permute-start | bytes 6152 | tf_op jit(solution)/shard_map/ppermute | solution.py:89
  56.8 4.7 %collective-permute-start.12 = (f32[1,1,512]{2,1,0:T(1,128)S(1)}, f32[1,1,512]{2,1,0:T(1,128)S(1)}, u32[]{:S(2)}, u32[]{:S(2)}) collective-permute-start(f32[1,1,512]{2,1,0:T(1,128)S(1)} %get-tuple-element.38), channel_id=1, source_target_pairs={{0,8},{4,12},{8,0},{12,4},{1,9},{5,13},{9,1},{13,5},{2,10},{6,14},... | collective-permute-start | bytes 6152 | tf_op jit(solution)/shard_map/ppermute | solution.py:89
  59.7 3.6 %collective-permute-start.13 = (f32[1,1,512]{2,1,0:T(1,128)S(1)}, f32[1,1,512]{2,1,0:T(1,128)S(1)}, u32[]{:S(2)}, u32[]{:S(2)}) collective-permute-start(f32[1,1,512]{2,1,0:T(1,128)S(1)} %get-tuple-element.37), channel_id=1, source_target_pairs={{0,12},{4,0},{8,4},{12,8},{1,13},{5,1},{9,5},{13,9},{2,14},{6,2},{... | collective-permute-start | bytes 6152 | tf_op jit(solution)/shard_map/ppermute | solution.py:89
  78.4 7.3 %collective-permute-start.15 = (bf16[103936]{0:T(1024)(128)(2,1)S(1)}, bf16[103936]{0:T(1024)(128)(2,1)S(1)}, u32[]{:S(2)}, u32[]{:S(2)}) collective-permute-start(bf16[103936]{0:T(1024)(128)(2,1)S(1)} %pad_maximum_fusion.2), channel_id=1, source_target_pairs={{0,2},{2,0},{1,3},{3,1},{4,6},{6,4},{5,7},{7,5},{8,10},{10,8},{9,1... | collective-permute-start | bytes 623624 | tf_op jit(solution)/shard_map/ppermute | solution.py:339
  87.8 14.2 %collective-permute-start.17 = (bf16[256,384]{0,1:T(8,128)(2,1)S(1)}, bf16[256,384]{0,1:T(8,128)(2,1)S(1)}, u32[]{:S(2)}, u32[]{:S(2)}) collective-permute-start(bf16[256,384]{0,1:T(8,128)(2,1)S(1)} %get-tuple-element.24), channel_id=1, source_target_pairs={{0,4},{4,8},{8,12},{12,0},{1,5},{5,9},{9,13},{13,1},{2,6},{6,10},{... | collective-permute-start | bytes 589832 | tf_op jit(solution)/shard_map/ppermute | solution.py:89
  88.4 16.3 %collective-permute-start.18 = (bf16[256,384]{0,1:T(8,128)(2,1)S(1)}, bf16[256,384]{0,1:T(8,128)(2,1)S(1)}, u32[]{:S(2)}, u32[]{:S(2)}) collective-permute-start(bf16[256,384]{0,1:T(8,128)(2,1)S(1)} %get-tuple-element.26), channel_id=1, source_target_pairs={{0,8},{4,12},{8,0},{12,4},{1,9},{5,13},{9,1},{13,5},{2,10},{6,14},... | collective-permute-start | bytes 589832 | tf_op jit(solution)/shard_map/ppermute | solution.py:89
  91.3 16.5 %collective-permute-start.19 = (bf16[256,384]{0,1:T(8,128)(2,1)S(1)}, bf16[256,384]{0,1:T(8,128)(2,1)S(1)}, u32[]{:S(2)}, u32[]{:S(2)}) collective-permute-start(bf16[256,384]{0,1:T(8,128)(2,1)S(1)} %get-tuple-element.25), channel_id=1, source_target_pairs={{0,12},{4,0},{8,4},{12,8},{1,13},{5,1},{9,5},{13,9},{2,14},{6,2},{... | collective-permute-start | bytes 589832 | tf_op jit(solution)/shard_map/ppermute | solution.py:89
  108.0 6.6 %collective-permute-start.20 = (bf16[256,384]{0,1:T(8,128)(2,1)S(1)}, bf16[256,384]{0,1:T(8,128)(2,1)S(1)}, u32[]{:S(2)}, u32[]{:S(2)}) collective-permute-start(bf16[256,384]{0,1:T(8,128)(2,1)S(1)} %get-tuple-element.8), channel_id=1, source_target_pairs={{0,2},{2,0},{1,3},{3,1},{4,6},{6,4},{5,7},{7,5},{8,10},{10,8},{9,1... | collective-permute-start | bytes 589832 | tf_op jit(solution)/shard_map/ppermute | solution.py:350
  (9 other events, 12.4 us)
